TPU v7x, 32 devices: a whole 2x2x4 slice. The times are simulated.
32 devices in a mesh: sub: 8 (over z, x), coarse: 4 (over y, core).
Axes of the slice: x: 2, y: 2, z: 4, core: 2. Of those that a mesh axis runs over, the one named last changes fastest.
Arguments:
- residual: bfloat16 [128, 512, 256], P(('sub', 'coarse')), may hold values from -6 to 6
- margin: int32 [128, 4], P(('sub', 'coarse')), may hold values from 0 to 5, as said below
- inverse_blocks: bfloat16 [128, 4, 256, 256], P(('sub', 'coarse')), may hold values from -0.1875 to 0.1875
- interface: int32 [128, 2], P(('sub', 'coarse')), may hold values from 0 to 11, as said below
- basis: bfloat16 [128, 2, 256, 128], P(('sub', 'coarse')), may hold values from -0.375 to 0.375
- coarse_pattern: int32 [12, 4], P('coarse'), may hold values from 0 to 11, as said below
- coarse_inverse: bfloat16 [12, 4, 128, 128], P('coarse'), may hold values from -0.0546875 to 0.0546875
Outputs:
- correction: bfloat16 [128, 512, 256], P(('sub', 'coarse'))
Inputs may be any that keep to these rules, and one draw needn't show every extreme that they name: margin[j, 0] is j's own slot j % 4 + 1; the first block of each subdomain has slot 0 in entry 1 and the last has slot 5 in entry 2. interface[j, 0] = j % 12. coarse_pattern[n, 0] = n.
All inputs are finite; a program needn't handle non-finite values.
Results may differ from a plain program's by a relative error of at most 0.0051.
Values may be sent and summed in bfloat16 or wider, within the bound.
No kernel may reach another device: no remote copies, remote signals or barrier semaphores. Data moves between devices by JAX's collectives and lax.ppermute only.
A program may use at most 64 MiB of HBM per device.

v0:
```python
import jax
import jax.numpy as jnp
from jax import lax
from jax.sharding import PartitionSpec as P


def with_halo(cells, sides, width):
    for axis, dim in sides:
        count = lax.axis_size(axis)
        ends = count - 1
        head = lax.slice_in_dim(cells, 0, width, axis=dim)
        tail = lax.slice_in_dim(cells, cells.shape[dim] - width, cells.shape[dim], axis=dim)
        cells = jnp.concatenate(
            [
                lax.ppermute(tail, axis, [(i, (i + 1) % count) for i in range(ends)]),
                cells,
                lax.ppermute(head, axis, [((i + 1) % count, i) for i in range(ends)]),
            ],
            axis=dim,
        )
    return cells


def coarse_rows(inputs, coarse_pattern, coarse_inverse):
    chosen = jnp.take(inputs, coarse_pattern, axis=0)
    return jnp.einsum(
        "nerc,necd->nrd", chosen, coarse_inverse, preferred_element_type=jnp.float32
    ).astype(jnp.bfloat16)


def per_device(residual, margin, inverse_blocks, interface, basis, coarse_pattern, coarse_inverse):
    extended = with_halo(residual, ((("sub", "coarse"), 0),), 1)
    terms = jnp.einsum("jrb,jqbc->jqrc", residual, basis, preferred_element_type=jnp.float32)
    total_blocks = coarse_pattern.shape[0] * lax.axis_size("coarse")
    labels = jnp.arange(total_blocks, dtype=jnp.int32)
    onehot = (interface[:, :, None] == labels[None, None, :]).astype(jnp.float32)
    restricted = jnp.einsum("jqn,jqrc->nrc", onehot, terms, precision=lax.Precision.HIGHEST)
    picked = jnp.take(extended, margin, axis=0)
    local = jnp.einsum("jerb,jebc->jrc", picked, inverse_blocks, preferred_element_type=jnp.float32)
    shares = lax.psum_scatter(restricted, "coarse", scatter_dimension=0, tiled=True)
    shares = lax.psum(shares, "sub")
    inputs = lax.all_gather(shares.astype(jnp.bfloat16), "coarse", axis=0, tiled=True)
    owned = coarse_rows(inputs, coarse_pattern, coarse_inverse)
    coarse_out = lax.all_gather(owned, "coarse", axis=0, tiled=True)
    lifted = jnp.take(coarse_out, interface, axis=0)
    spread = jnp.einsum("jqrc,jqbc->jrb", lifted, basis, preferred_element_type=jnp.float32)
    return (local + spread).astype(jnp.bfloat16)


def solution(mesh):
    in_specs = (
        P(("sub", "coarse"), None, None),
        P(("sub", "coarse"), None),
        P(("sub", "coarse"), None, None, None),
        P(("sub", "coarse"), None),
        P(("sub", "coarse"), None, None, None),
        P("coarse", None),
        P("coarse", None, None, None),
    )
    out_specs = P(("sub", "coarse"), None, None)
    return jax.shard_map(
        per_device, mesh=mesh, in_specs=in_specs, out_specs=out_specs, check_vma=False
    )
```

profile of v0, /device:TPU:6, one launch (start us, length us, event | category | flops | bytes accessed | tf_op | source)
XLA Modules:
  0.0 169.5 jit_solution(14236015216186397533)
XLA Ops:
  6.5 0.0 copy-start
  6.5 0.0 reduce-scatter.2.cloned.1.call-start
  6.5 3.4 %convolution_bitcast_fusion.1 = f32[4,2,512,128]{2,3,1,0:T(8,128)} fusion(bf16[4,2,256,128]{3,2,1,0:T(8,128)(2,1)} %param.11, bf16[4,512,256]{2,1,0:T(8,128)(2,1)} %param.7), kind=kOutput, calls=%fused_computation.10 | convolution fusion | flops 268435456 | bytes 3670016 | tf_op jit(solution)/shard_map/jrb,jqbc->jqrc/dot_general | solution.py:33
  9.9 2.9 %copy.16 = f32[4,2,512,128]{3,0,1,2:T(4,128)} copy(f32[4,2,512,128]{2,3,1,0:T(8,128)} %convolution_bitcast_fusion.1) | data formatting | bytes 4194304 | tf_op jit(solution)/shard_map/jrb,jqbc->jqrc/transpose | solution.py:33
  12.8 4.1 %convolution_bitcast_fusion = f32[12,512,128]{2,0,1:T(8,128)S(1)} fusion(f32[4,2,512,128]{3,0,1,2:T(4,128)} %copy.16, s32[4,2]{0,1:T(2,128)S(1)} %copy-done.4), kind=kOutput, calls=%fused_computation.6 | convolution fusion | flops 75497568 | bytes 5242912 | tf_op jit(solution)/shard_map/jqn,jqrc->nrc/dot_general | solution.py:37
  17.0 2.6 %copy.17 = f32[12,512,128]{2,1,0:T(8,128)} copy(f32[12,512,128]{2,0,1:T(8,128)S(1)} %convolution_bitcast_fusion) | data formatting | bytes 6291456 | tf_op jit(solution)/shard_map/jqn,jqrc->nrc/dot_general | solution.py:37
  19.6 0.0 reduce-scatter.2.cloned.1.call-update
  19.6 0.0 all-gather.3.cloned.1.call-start
  19.6 38.3 %reduce-scatter.2.cloned.1.call-done = f32[3,512,128]{2,1,0:T(8,128)} async-done(((f32[12,512,128]{2,1,0:T(8,128)}), f32[3,512,128]{2,1,0:T(8,128)}) %reduce-scatter.2.cloned.1.call-update) | async-done | bytes 786448 | tf_op jit(solution)/shard_map/reduce_scatter | solution.py:40
  58.0 44.8 %all-reduce.1 = bf16[3,512,128]{2,1,0:T(8,128)(2,1)} all-reduce(f32[3,512,128]{2,1,0:T(8,128)} %reduce-scatter.2.cloned.1.call-done), channel_id=1, replica_groups=mesh['sub'=8,'coarse'=4] {'sub'}, use_global_device_ids=true, to_apply=%region_1.2 | all-reduce | flops 196608 | bytes 1179648 | tf_op jit(solution)/shard_map/psum | solution.py:41
  102.7 0.0 all-gather.3.cloned.1.call-update
  102.8 0.0 all-gather.5.cloned.1.call-start
  102.8 0.1 reshape.26
  102.9 19.7 %all-gather.3.cloned.1.call-done = bf16[12,512,128]{2,1,0:T(8,128)(2,1)} async-done(((bf16[3,512,128]{2,1,0:T(8,128)(2,1)}), bf16[12,512,128]{2,1,0:T(8,128)(2,1)}) %all-gather.3.cloned.1.call-update) | async-done | bytes 1572880 | tf_op jit(solution)/shard_map/all_gather | solution.py:42
  122.6 3.4 %gather_fusion.1 = bf16[12,512,128]{2,1,0:T(8,128)(2,1)} fusion(bf16[12,512,128]{2,1,0:T(8,128)(2,1)} %all-gather.3.cloned.1.call-done, s32[1024]{0:T(1024)S(1)} %pad_clamp_fusion.1), kind=kCustom, calls=%fused_computation.1 | custom fusion | bytes 3145776 | tf_op jit(solution)/shard_map/jit(_take)/gather | solution.py:25
  126.0 2.9 %fusion.13 = bf16[3,512,128]{2,1,0:T(8,128)(2,1)} fusion(bf16[3,4,128,128]{3,2,1,0:T(8,128)(2,1)} %param.13, bf16[3,4,512,128]{3,2,1,0:T(8,128)(2,1)} %bitcast.36, pred[3,4]{1,0:T(4,128)(4,1)S(1)} %compare_and_fusion), kind=kOutput, calls=%fused_computation.16 | convolution fusion | flops 202309632 | bytes 2359308 | tf_op jit(solution)/shard_map/nerc,necd->nrd/dot_general | solution.py:26
  128.9 0.0 all-gather.5.cloned.1.call-update
  128.9 0.8 fusion.28
  129.8 3.2 %collective-permute-start.1 = (bf16[1,512,256]{2,1,0:T(8,128)(2,1)}, bf16[1,512,256]{2,1,0:T(8,128)(2,1)S(1)}, u32[]{:S(2)}, u32[]{:S(2)}) collective-permute-start(bf16[1,512,256]{2,1,0:T(8,128)(2,1)} %get-tuple-element.6), channel_id=1, source_target_pairs={{1,0},{2,1},{3,2},{4,3},{5,4},{6,5},{7,6},{8,7},{9,8},{10,9},{11,1... | collective-permute-start | bytes 786440 | tf_op jit(solution)/shard_map/ppermute | solution.py:17
  133.0 1.9 %collective-permute-start = (bf16[1,512,256]{2,1,0:T(8,128)(2,1)}, bf16[1,512,256]{2,1,0:T(8,128)(2,1)}, u32[]{:S(2)}, u32[]{:S(2)}) collective-permute-start(bf16[1,512,256]{2,1,0:T(8,128)(2,1)} %get-tuple-element.5), channel_id=1, source_target_pairs={{0,1},{1,2},{2,3},{3,4},{4,5},{5,6},{6,7},{7,8},{8,9},{9,10},{10,1... | collective-permute-start | bytes 786440 | tf_op jit(solution)/shard_map/ppermute | solution.py:15
  134.9 0.1 copy.18
  135.0 0.1 reshape.34
  135.1 0.1 reshape.18
  135.2 0.1 copy.14
  135.4 1.9 %collective-permute-done.1 = bf16[1,512,256]{2,1,0:T(8,128)(2,1)S(1)} collective-permute-done((bf16[1,512,256]{2,1,0:T(8,128)(2,1)}, bf16[1,512,256]{2,1,0:T(8,128)(2,1)S(1)}, u32[]{:S(2)}, u32[]{:S(2)}) %collective-permute-start.1) | collective-permute-done | bytes 262176 | tf_op jit(solution)/shard_map/ppermute | solution.py:17
  137.2 11.0 %collective-permute-done = bf16[1,512,256]{2,1,0:T(8,128)(2,1)} collective-permute-done((bf16[1,512,256]{2,1,0:T(8,128)(2,1)}, bf16[1,512,256]{2,1,0:T(8,128)(2,1)}, u32[]{:S(2)}, u32[]{:S(2)}) %collective-permute-start) | collective-permute-done | bytes 262176 | tf_op jit(solution)/shard_map/ppermute | solution.py:15
  148.3 2.3 %pad_maximum_fusion = bf16[6,512,256]{2,1,0:T(8,128)(2,1)} fusion(bf16[1,512,256]{2,1,0:T(8,128)(2,1)S(1)} %collective-permute-done.1, bf16[4,512,256]{2,1,0:T(8,128)(2,1)S(1)} %copy-done.1, bf16[1,512,256]{2,1,0:T(8,128)(2,1)} %collective-permute-done), kind=kLoop, calls=%fused_computation.11 | loop fusion | flops 1572864 | bytes 3145728 | tf_op jit(solution)/shard_map/concatenate | solution.py:13
  150.6 4.2 %gather_fusion = bf16[16,512,256]{2,1,0:T(8,128)(2,1)} fusion(bf16[6,512,256]{2,1,0:T(8,128)(2,1)} %pad_maximum_fusion, s32[1024]{0:T(1024)S(1)} %pad_clamp_fusion.2), kind=kCustom, calls=%fused_computation | custom fusion | bytes 8388672 | tf_op jit(solution)/shard_map/jit(_take)/gather | solution.py:38
  154.8 2.2 %gather_fusion.2 = bf16[8,512,128]{2,1,0:T(8,128)(2,1)S(1)} fusion(bf16[12,512,128]{2,1,0:T(8,128)(2,1)} %all-gather.5.cloned.1.call-done, s32[1024]{0:T(1024)S(1)} %pad_clamp_fusion), kind=kCustom, calls=%fused_computation.2 | custom fusion | bytes 2097184 | tf_op jit(solution)/shard_map/jit(_take)/gather | solution.py:45
  156.9 1.5 fusion.17
  158.4 0.0 copy-done
  158.5 4.5 %fusion.3 = bf16[4,512,256]{2,1,0:T(8,128)(2,1)} fusion(f32[4,512,256,1]{2,1,3,0:T(8,128)S(1)} %fusion.17, bf16[4,4,256,256]{3,2,1,0:T(8,128)(2,1)S(1)} %copy-done, bf16[4,4,512,256]{3,2,1,0:T(8,128)(2,1)} %bitcast.34, pred[4,4]{1,0:T(4,128)(4,1)S(1)} %compare_and_fusion.2), kind=kOutput, calls=%fused_computation.8 | convolution fusion | flops 1076887552 | bytes 9437200 | tf_op jit(solution)/shard_map/jerb,jebc->jrc/dot_general | solution.py:39
  (18 shorter events, 0.1 us)
Async XLA Ops:
  6.5 151.9 %copy-start = (bf16[4,4,256,256]{3,2,1,0:T(8,128)(2,1)S(1)}, bf16[4,4,256,256]{3,2,1,0:T(8,128)(2,1)}, u32[]{:S(2)}) copy-start(bf16[4,4,256,256]{3,2,1,0:T(8,128)(2,1)} %param.9) | copy-start | bytes 6291460
  6.5 51.4 %reduce-scatter.2.cloned.1.call-start = ((), (), s32[]{:S(2)}) async-start(), calls=%async_computation.1 | async-start | bytes 3932160 | tf_op jit(solution)/shard_map/reduce_scatter | solution.py:40
  9.9 2.9 %copy-start.4 = (s32[4,2]{0,1:T(2,128)S(1)}, s32[4,2]{0,1:T(2,128)}, u32[]{:S(2)}) copy-start(s32[4,2]{0,1:T(2,128)} %param.10) | copy-start | bytes 100
  19.6 83.3 %copy-start.2 = (s32[3,4]{1,0:T(4,128)S(1)}, s32[3,4]{1,0:T(4,128)}, u32[]{:S(2)}) copy-start(s32[3,4]{1,0:T(4,128)} %param.12) | copy-start | bytes 148
  19.6 103.0 %all-gather.3.cloned.1.call-start = ((), (), s32[]{:S(2)}) async-start(), calls=%async_computation.2 | async-start | bytes 1966080 | tf_op jit(solution)/shard_map/all_gather | solution.py:42
  102.8 52.0 %all-gather.5.cloned.1.call-start = ((), (), s32[]{:S(2)}) async-start(), calls=%async_computation.3 | async-start | bytes 1966080 | tf_op jit(solution)/shard_map/all_gather | solution.py:44
  126.0 3.0 %copy-start.1 = (bf16[4,512,256]{2,1,0:T(8,128)(2,1)S(1)}, bf16[4,512,256]{2,1,0:T(8,128)(2,1)}, u32[]{:S(2)}) copy-start(bf16[4,512,256]{2,1,0:T(8,128)(2,1)} %param.7) | copy-start | bytes 3145732
  126.0 9.2 %copy-start.3 = (s32[4,4]{1,0:T(4,128)S(1)}, s32[4,4]{1,0:T(4,128)}, u32[]{:S(2)}) copy-start(s32[4,4]{1,0:T(4,128)} %param.8) | copy-start | bytes 196
  129.8 7.4 %collective-permute-start.1 = (bf16[1,512,256]{2,1,0:T(8,128)(2,1)}, bf16[1,512,256]{2,1,0:T(8,128)(2,1)S(1)}, u32[]{:S(2)}, u32[]{:S(2)}) collective-permute-start(bf16[1,512,256]{2,1,0:T(8,128)(2,1)} %get-tuple-element.6), channel_id=1, source_target_pairs={{1,0},{2,1},{3,2},{4,3},{5,4},{6,5},{7,6},{8,7},{9,8},{10,9},{11,1... | collective-permute-start | bytes 786440 | tf_op jit(solution)/shard_map/ppermute | solution.py:17
  133.0 15.3 %collective-permute-start = (bf16[1,512,256]{2,1,0:T(8,128)(2,1)}, bf16[1,512,256]{2,1,0:T(8,128)(2,1)}, u32[]{:S(2)}, u32[]{:S(2)}) collective-permute-start(bf16[1,512,256]{2,1,0:T(8,128)(2,1)} %get-tuple-element.5), channel_id=1, source_target_pairs={{0,1},{1,2},{2,3},{3,4},{4,5},{5,6},{6,7},{7,8},{8,9},{9,10},{10,1... | collective-permute-start | bytes 786440 | tf_op jit(solution)/shard_map/ppermute | solution.py:15
Sparse Core Ops, SparseCore 0:
  19.7 38.1 reduce-scatter.1
  102.9 19.6 all-gather.2
  129.0 23.5 all-gather.4
where the time goes:
time: 170 us; the launch traced here: 169 us
  waiting for transfers between devices  71 us (42%)
  blocking collectives  44.8 us (26%)
  local copies, waits for them, and re-layouts  16.5 us (10%)
  matrix products  16.4 us (10%)
  between operations  13.2 us (8%)
  starting transfers between devices  5.22 us (3%)
  other arithmetic  2.37 us (1%)
    psum x1, blocking collectives, per_device(): shares = lax.psum(shares, 'sub')  44.8 us
    reduce_scatter x1, waiting for transfers between devices, per_device(): lax.psum_scatter(restricted, 'coarse', scatter_dimension=0, tiled=True)  38.3 us
    all_gather x1, waiting for transfers between devices, per_device(): lax.all_gather(shares.astype(jnp.bfloat16), 'coarse', axis=0, tiled=True)  19.7 us
    ppermute x1, waiting for transfers between devices, with_halo(): lax.ppermute(tail, axis, [(i, (i + 1) % count) for i in range(ends)])  11 us
    dot_general x1, matrix products, per_device(): jnp.einsum('jerb,jebc->jrc', picked, inverse_blocks, preferred_element_ty...  4.48 us
    gather x1, local copies, waits for them, and re-layouts, per_device(): picked = jnp.take(extended, margin, axis=0)  4.18 us
    dot_general x1, matrix products, per_device(): jnp.einsum('jqn,jqrc->nrc', onehot, terms, precision=lax.Precision.HIGHEST)  4.12 us
  transfers between devices with their start and end apart: 5, of which 4 were waited for; matrix products, arithmetic and copies ran while one was open for 5% of the time, Pallas kernels for 0%

commit v1 on v0

--- a/solution.py
+++ b/solution.py
@@ -29,19 +29,21 @@
 
 
 def per_device(residual, margin, inverse_blocks, interface, basis, coarse_pattern, coarse_inverse):
+    pattern_all = lax.all_gather(coarse_pattern, "coarse", axis=0, tiled=True)
+    inverse_all = lax.all_gather(coarse_inverse, "coarse", axis=0, tiled=True)
     extended = with_halo(residual, ((("sub", "coarse"), 0),), 1)
     terms = jnp.einsum("jrb,jqbc->jqrc", residual, basis, preferred_element_type=jnp.float32)
-    total_blocks = coarse_pattern.shape[0] * lax.axis_size("coarse")
+    total_blocks = pattern_all.shape[0]
     labels = jnp.arange(total_blocks, dtype=jnp.int32)
     onehot = (interface[:, :, None] == labels[None, None, :]).astype(jnp.float32)
     restricted = jnp.einsum("jqn,jqrc->nrc", onehot, terms, precision=lax.Precision.HIGHEST)
     picked = jnp.take(extended, margin, axis=0)
     local = jnp.einsum("jerb,jebc->jrc", picked, inverse_blocks, preferred_element_type=jnp.float32)
-    shares = lax.psum_scatter(restricted, "coarse", scatter_dimension=0, tiled=True)
-    shares = lax.psum(shares, "sub")
-    inputs = lax.all_gather(shares.astype(jnp.bfloat16), "coarse", axis=0, tiled=True)
-    owned = coarse_rows(inputs, coarse_pattern, coarse_inverse)
-    coarse_out = lax.all_gather(owned, "coarse", axis=0, tiled=True)
+    pattern_all, inverse_all, restricted = lax.optimization_barrier((pattern_all, inverse_all, restricted))
+    flat = restricted.reshape(-1, restricted.shape[-1])
+    share = lax.psum_scatter(flat, ("sub", "coarse"), scatter_dimension=0, tiled=True)
+    coarse_in = lax.all_gather(share.astype(jnp.bfloat16), ("sub", "coarse"), axis=0, tiled=True)
+    coarse_out = coarse_rows(coarse_in.reshape(restricted.shape), pattern_all, inverse_all)
     lifted = jnp.take(coarse_out, interface, axis=0)
     spread = jnp.einsum("jqrc,jqbc->jrb", lifted, basis, preferred_element_type=jnp.float32)
     return (local + spread).astype(jnp.bfloat16)

time: 170 us -> 223 us (1.31)
  the two profiles are of different devices: /device:TPU:6 before, /device:TPU:0 now
where the time goes in v1:
time: 223 us
  waiting for transfers between devices  151 us (68%)
  local copies, waits for them, and re-layouts  22.2 us (10%)
  matrix products  20.5 us (9%)
  between operations  13.2 us (6%)
  blocking collectives  6.3 us (3%)
  starting transfers between devices  5.11 us (2%)
  other arithmetic  3.85 us (2%)
    reduce_scatter x1, waiting for transfers between devices, per_device(): lax.psum_scatter(flat, ('sub', 'coarse'), scatter_dimension=0, tiled=True)  102 us
    all_gather x1, waiting for transfers between devices, per_device(): lax.all_gather(share.astype(jnp.bfloat16), ('sub', 'coarse'), axis=0, til...  41.9 us
    all_gather x1, waiting for transfers between devices, per_device(): inverse_all = lax.all_gather(coarse_inverse, 'coarse', axis=0, tiled=True)  6.36 us
    gather x1, local copies, waits for them, and re-layouts, coarse_rows(): chosen = jnp.take(inputs, coarse_pattern, axis=0)  6.35 us
    dot_general x1, matrix products, coarse_rows(): jnp.einsum('nerc,necd->nrd', chosen, coarse_inverse, preferred_element_ty...  6.3 us
    all_gather x1, blocking collectives, per_device(): pattern_all = lax.all_gather(coarse_pattern, 'coarse', axis=0, tiled=True)  6.3 us
    dot_general x1, matrix products, per_device(): jnp.einsum('jqn,jqrc->nrc', onehot, terms, precision=lax.Precision.HIGHEST)  5.03 us
    optimization_barrier x2, local copies, waits for them, and re-layouts, per_device(): lax.optimization_barrier((pattern_all, inverse_all, restricted))  4.97 us
  transfers between devices with their start and end apart: 5, of which 4 were waited for; matrix products, arithmetic and copies ran while one was open for 9% of the time, Pallas kernels for 0%

profile of v1, /device:TPU:0, one launch (start us, length us, event | category | flops | bytes accessed | tf_op | source)
XLA Modules:
  0.0 222.6 jit_solution(6677805996948392814)
XLA Ops:
  6.5 0.7 all-gather.4.cloned.1.call-update
  7.3 0.0 reduce-scatter.2.cloned.1.call-start
  7.3 6.3 %all-gather = s32[4,3,4]{2,1,0:T(4,128)S(1)} all-gather(s32[1,3,4]{2,1,0:T(4,128)} %bitcast.40), channel_id=1, replica_groups=mesh['sub'=8,'coarse'=4] {'coarse'}, dimensions={0}, use_global_device_ids=true | all-gather | bytes 240 | tf_op jit(solution)/shard_map/all_gather | solution.py:32
  13.6 0.1 copy.33
  13.7 3.2 %convolution_bitcast_fusion.1 = f32[4,2,512,128]{2,3,1,0:T(8,128)} fusion(bf16[4,2,256,128]{3,2,1,0:T(8,128)(2,1)} %param.11, bf16[4,512,256]{2,1,0:T(8,128)(2,1)} %param.7), kind=kOutput, calls=%fused_computation.15 | convolution fusion | flops 268435456 | bytes 3670016 | tf_op jit(solution)/shard_map/jrb,jqbc->jqrc/dot_general | solution.py:35
  16.9 3.0 %copy.22 = f32[4,2,512,128]{3,0,1,2:T(4,128)} copy(f32[4,2,512,128]{2,3,1,0:T(8,128)} %convolution_bitcast_fusion.1) | data formatting | bytes 4194304 | tf_op jit(solution)/shard_map/jrb,jqbc->jqrc/transpose | solution.py:35
  19.9 5.0 %convolution_bitcast_fusion = f32[12,512,128]{2,0,1:T(8,128)} fusion(f32[4,2,512,128]{3,0,1,2:T(4,128)} %copy.22, s32[4,2]{0,1:T(2,128)S(1)} %copy-done.3), kind=kOutput, calls=%fused_computation.11 | convolution fusion | flops 75497568 | bytes 5242912 | tf_op jit(solution)/shard_map/jqn,jqrc->nrc/dot_general | solution.py:39
  25.0 6.4 %all-gather.4.cloned.1.call-done = bf16[12,4,128,128]{3,2,1,0:T(8,128)(2,1)} async-done(((bf16[3,4,128,128]{3,2,1,0:T(8,128)(2,1)}), bf16[12,4,128,128]{3,2,1,0:T(8,128)(2,1)}) %all-gather.4.cloned.1.call-update) | async-done | bytes 1572880 | tf_op jit(solution)/shard_map/all_gather | solution.py:33
  31.3 4.9 %copy.24 = f32[12,512,128]{2,1,0:T(8,128)} copy(f32[12,512,128]{2,0,1:T(8,128)} %convolution_bitcast_fusion) | data formatting | bytes 6291456 | tf_op jit(solution)/shard_map/optimization_barrier | solution.py:42
  36.2 0.0 reduce-scatter.2.cloned.1.call-update
  36.2 0.0 all-gather.6.cloned.1.call-start
  36.3 102.0 %reduce-scatter.2.cloned.1.call-done = f32[192,128]{1,0:T(8,128)} async-done(((f32[6144,128]{1,0:T(8,128)}), f32[192,128]{1,0:T(8,128)}) %reduce-scatter.2.cloned.1.call-update) | async-done | bytes 98320 | tf_op jit(solution)/shard_map/reduce_scatter | solution.py:44
  138.3 1.5 convert_element_type.10
  139.8 0.8 fusion.24
  140.7 1.3 collective-permute-start.1
  141.9 3.7 %collective-permute-start = (bf16[1,512,256]{2,1,0:T(8,128)(2,1)}, bf16[1,512,256]{2,1,0:T(8,128)(2,1)}, u32[]{:S(2)}, u32[]{:S(2)}) collective-permute-start(bf16[1,512,256]{2,1,0:T(8,128)(2,1)} %get-tuple-element.11), channel_id=1, source_target_pairs={{0,1},{1,2},{2,3},{3,4},{4,5},{5,6},{6,7},{7,8},{8,9},{9,10},{10,1... | collective-permute-start | bytes 786440 | tf_op jit(solution)/shard_map/ppermute | solution.py:15
  145.7 0.1 copy.26
  145.8 0.1 reshape.42
  145.9 0.1 reshape.26
  146.0 0.1 copy.19
  146.1 0.4 collective-permute-done
  146.5 2.3 %pad_maximum_fusion = bf16[6,512,256]{2,1,0:T(8,128)(2,1)} fusion(bf16[1,512,256]{2,1,0:T(8,128)(2,1)S(1)} %collective-permute-done.1, bf16[4,512,256]{2,1,0:T(8,128)(2,1)S(1)} %copy-done.1, bf16[1,512,256]{2,1,0:T(8,128)(2,1)} %collective-permute-done), kind=kLoop, calls=%fused_computation.16 | loop fusion | flops 1572864 | bytes 3145728 | tf_op jit(solution)/shard_map/concatenate | solution.py:13
  148.8 4.3 %gather_fusion = bf16[16,512,256]{2,1,0:T(8,128)(2,1)} fusion(bf16[6,512,256]{2,1,0:T(8,128)(2,1)} %pad_maximum_fusion, s32[1024]{0:T(1024)S(1)} %pad_clamp_fusion.2), kind=kCustom, calls=%fused_computation | custom fusion | bytes 8388672 | tf_op jit(solution)/shard_map/jit(_take)/gather | solution.py:40
  153.0 0.1 copy.25
  153.1 0.1 reshape.34
  153.2 0.1 copy.23
  153.3 41.9 %all-gather.6.cloned.1.call-done = bf16[6144,128]{1,0:T(8,128)(2,1)} async-done(((bf16[192,128]{1,0:T(8,128)(2,1)}), bf16[6144,128]{1,0:T(8,128)(2,1)}) %all-gather.6.cloned.1.call-update) | async-done | bytes 1572880 | tf_op jit(solution)/shard_map/all_gather | solution.py:45
  195.2 6.3 %gather_fusion.1 = bf16[48,512,128]{2,1,0:T(8,128)(2,1)} fusion(bf16[12,512,128]{2,1,0:T(8,128)(2,1)} %bitcast.35, s32[1024]{0:T(1024)S(1)} %pad_clamp_fusion.1), kind=kCustom, calls=%fused_computation.1 | custom fusion | bytes 12583104 | tf_op jit(solution)/shard_map/jit(_take)/gather | solution.py:25
  201.6 6.3 %bitcast_convert_fusion = bf16[12,512,128]{2,1,0:T(8,128)(2,1)} fusion(bf16[12,4,128,128]{3,2,1,0:T(8,128)(2,1)} %all-gather.4.cloned.1.call-done, bf16[12,4,512,128]{3,2,1,0:T(8,128)(2,1)} %bitcast.37, pred[12,4]{1,0:T(8,128)(4,1)S(1)} %copy.23), kind=kOutput, calls=%fused_computation.9 | convolution fusion | flops 809238528 | bytes 9437232 | tf_op jit(solution)/shard_map/nerc,necd->nrd/dot_general | solution.py:26
  207.9 2.2 gather_fusion.2
  210.1 1.5 fusion.14
  211.6 4.5 %fusion.7 = bf16[4,512,256]{2,1,0:T(8,128)(2,1)} fusion(f32[4,512,256,1]{2,1,3,0:T(8,128)S(1)} %fusion.14, bf16[4,4,256,256]{3,2,1,0:T(8,128)(2,1)S(1)} %copy-done, bf16[4,4,512,256]{3,2,1,0:T(8,128)(2,1)} %bitcast.38, pred[4,4]{1,0:T(4,128)(4,1)S(1)} %compare_and_fusion.2), kind=kOutput, calls=%fused_computation.13 | convolution fusion | flops 1076887552 | bytes 9437200 | tf_op jit(solution)/shard_map/jerb,jebc->jrc/dot_general | solution.py:41
  (21 shorter events, 0.1 us)
Async XLA Ops:
  6.5 205.1 %copy-start = (bf16[4,4,256,256]{3,2,1,0:T(8,128)(2,1)S(1)}, bf16[4,4,256,256]{3,2,1,0:T(8,128)(2,1)}, u32[]{:S(2)}) copy-start(bf16[4,4,256,256]{3,2,1,0:T(8,128)(2,1)} %param.9) | copy-start | bytes 6291460
  6.5 24.8 %all-gather.4.cloned.1.call-start = ((), (), s32[]{:S(2)}) async-start(), calls=%async_computation.1 | async-start | bytes 1966080 | tf_op jit(solution)/shard_map/all_gather | solution.py:33
  7.3 131.0 %reduce-scatter.2.cloned.1.call-start = ((), (), s32[]{:S(2)}) async-start(), calls=%async_computation.2 | async-start | bytes 3244032 | tf_op jit(solution)/shard_map/reduce_scatter | solution.py:44
  16.9 3.0 %copy-start.3 = (s32[4,2]{0,1:T(2,128)S(1)}, s32[4,2]{0,1:T(2,128)}, u32[]{:S(2)}) copy-start(s32[4,2]{0,1:T(2,128)} %param.10) | copy-start | bytes 100
  36.2 103.6 %copy-start.1 = (bf16[4,512,256]{2,1,0:T(8,128)(2,1)S(1)}, bf16[4,512,256]{2,1,0:T(8,128)(2,1)}, u32[]{:S(2)}) copy-start(bf16[4,512,256]{2,1,0:T(8,128)(2,1)} %param.7) | copy-start | bytes 3145732
  36.2 109.7 %copy-start.2 = (s32[4,4]{1,0:T(4,128)S(1)}, s32[4,4]{1,0:T(4,128)}, u32[]{:S(2)}) copy-start(s32[4,4]{1,0:T(4,128)} %param.8) | copy-start | bytes 196
  36.2 159.0 %all-gather.6.cloned.1.call-start = ((), (), s32[]{:S(2)}) async-start(), calls=%async_computation.3 | async-start | bytes 1622016 | tf_op jit(solution)/shard_map/all_gather | solution.py:45
  140.7 5.5 %collective-permute-start.1 = (bf16[1,512,256]{2,1,0:T(8,128)(2,1)}, bf16[1,512,256]{2,1,0:T(8,128)(2,1)S(1)}, u32[]{:S(2)}, u32[]{:S(2)}) collective-permute-start(bf16[1,512,256]{2,1,0:T(8,128)(2,1)} %get-tuple-element.12), channel_id=1, source_target_pairs={{1,0},{2,1},{3,2},{4,3},{5,4},{6,5},{7,6},{8,7},{9,8},{10,9},{11,1... | collective-permute-start | bytes 786440 | tf_op jit(solution)/shard_map/ppermute | solution.py:17
  141.9 4.5 %collective-permute-start = (bf16[1,512,256]{2,1,0:T(8,128)(2,1)}, bf16[1,512,256]{2,1,0:T(8,128)(2,1)}, u32[]{:S(2)}, u32[]{:S(2)}) collective-permute-start(bf16[1,512,256]{2,1,0:T(8,128)(2,1)} %get-tuple-element.11), channel_id=1, source_target_pairs={{0,1},{1,2},{2,3},{3,4},{4,5},{5,6},{6,7},{7,8},{8,9},{9,10},{10,1... | collective-permute-start | bytes 786440 | tf_op jit(solution)/shard_map/ppermute | solution.py:15
Sparse Core Ops, SparseCore 0:
  8.9 22.3 all-gather.3
  36.7 101.5 reduce-scatter.1
  141.2 54.0 all-gather.5

commit v2 on v1

--- a/solution.py
+++ b/solution.py
@@ -21,31 +21,87 @@
     return cells
 
 
-def coarse_rows(inputs, coarse_pattern, coarse_inverse):
-    chosen = jnp.take(inputs, coarse_pattern, axis=0)
-    return jnp.einsum(
-        "nerc,necd->nrd", chosen, coarse_inverse, preferred_element_type=jnp.float32
-    ).astype(jnp.bfloat16)
+def device_bits():
+    bits = []
+    for axis in ("coarse", "sub"):
+        size = lax.axis_size(axis)
+        mask = 1
+        while mask < size:
+            bits.append((axis, mask))
+            mask *= 2
+        assert mask == size
+    return bits
+
+
+def bit_of(axis, mask):
+    return (lax.axis_index(axis) // mask) % 2
+
+
+def pairs(axis, mask):
+    return [(i, i ^ mask) for i in range(lax.axis_size(axis))]
+
+
+def halve(x, dim, axis, mask):
+    v = bit_of(axis, mask)
+    keep = lax.dynamic_index_in_dim(x, v, axis=dim, keepdims=True)
+    send = lax.dynamic_index_in_dim(x, 1 - v, axis=dim, keepdims=True)
+    return keep + lax.ppermute(send, axis, pairs(axis, mask))
+
+
+def double(y, dim, axis, mask):
+    v = bit_of(axis, mask)
+    recv = lax.ppermute(y, axis, pairs(axis, mask))
+    return jnp.where(v == 0, jnp.concatenate([y, recv], axis=dim), jnp.concatenate([recv, y], axis=dim))
+
+
+def stream_orders(nbits, streams):
+    rest = list(range(1, nbits))
+    orders = []
+    for s in range(streams):
+        k = (s * len(rest)) // streams
+        orders.append([0] + rest[k:] + rest[:k])
+    return orders
 
 
 def per_device(residual, margin, inverse_blocks, interface, basis, coarse_pattern, coarse_inverse):
     pattern_all = lax.all_gather(coarse_pattern, "coarse", axis=0, tiled=True)
     inverse_all = lax.all_gather(coarse_inverse, "coarse", axis=0, tiled=True)
     extended = with_halo(residual, ((("sub", "coarse"), 0),), 1)
+    rhs = residual.shape[1]
+    width = basis.shape[-1]
+    total_blocks = pattern_all.shape[0]
     terms = jnp.einsum("jrb,jqbc->jqrc", residual, basis, preferred_element_type=jnp.float32)
-    total_blocks = pattern_all.shape[0]
     labels = jnp.arange(total_blocks, dtype=jnp.int32)
     onehot = (interface[:, :, None] == labels[None, None, :]).astype(jnp.float32)
-    restricted = jnp.einsum("jqn,jqrc->nrc", onehot, terms, precision=lax.Precision.HIGHEST)
+    restricted = jnp.einsum("jqn,jqrc->rnc", onehot, terms, precision=lax.Precision.HIGHEST)
+
+    bits = device_bits()
+    nb = len(bits)
+    inner = rhs >> nb
+    assert inner << nb == rhs
+    streams = 3 if total_blocks % 3 == 0 else 1
+    per = total_blocks // streams
+    orders = stream_orders(nb, streams)
+    split = restricted.reshape((2,) * nb + (inner, total_blocks, width))
+    parts = [lax.slice_in_dim(split, s * per, (s + 1) * per, axis=nb + 1) for s in range(streams)]
+    for step in range(nb):
+        parts = [halve(x, orders[s][step], *bits[orders[s][step]]) for s, x in enumerate(parts)]
+    mine = jnp.concatenate(parts, axis=nb + 1).reshape(inner, total_blocks, width)
+    coarse_in = mine.astype(jnp.bfloat16)
+    chosen = jnp.take(coarse_in, pattern_all, axis=1)
+    solved = jnp.einsum(
+        "rnec,necd->rnd", chosen, inverse_all, preferred_element_type=jnp.float32
+    ).astype(jnp.bfloat16)
+    solved = solved.reshape((1,) * nb + (inner, total_blocks, width))
+    outs = [lax.slice_in_dim(solved, s * per, (s + 1) * per, axis=nb + 1) for s in range(streams)]
+    for step in reversed(range(nb)):
+        outs = [double(y, orders[s][step], *bits[orders[s][step]]) for s, y in enumerate(outs)]
+    coarse_out = jnp.concatenate(outs, axis=nb + 1).reshape(rhs, total_blocks, width)
+
     picked = jnp.take(extended, margin, axis=0)
     local = jnp.einsum("jerb,jebc->jrc", picked, inverse_blocks, preferred_element_type=jnp.float32)
-    pattern_all, inverse_all, restricted = lax.optimization_barrier((pattern_all, inverse_all, restricted))
-    flat = restricted.reshape(-1, restricted.shape[-1])
-    share = lax.psum_scatter(flat, ("sub", "coarse"), scatter_dimension=0, tiled=True)
-    coarse_in = lax.all_gather(share.astype(jnp.bfloat16), ("sub", "coarse"), axis=0, tiled=True)
-    coarse_out = coarse_rows(coarse_in.reshape(restricted.shape), pattern_all, inverse_all)
-    lifted = jnp.take(coarse_out, interface, axis=0)
-    spread = jnp.einsum("jqrc,jqbc->jrb", lifted, basis, preferred_element_type=jnp.float32)
+    lifted = jnp.take(coarse_out, interface, axis=1)
+    spread = jnp.einsum("rjqc,jqbc->jrb", lifted, basis, preferred_element_type=jnp.float32)
     return (local + spread).astype(jnp.bfloat16)
 
 

time: 223 us -> 133 us (0.60)
  waiting for transfers between devices: 151 us -> 12.7 us
  starting transfers between devices: 5.11 us -> 45.2 us
  other arithmetic: 3.85 us -> 13.1 us
  blocking collectives: 6.3 us -> 11.9 us
  matrix products: 20.5 us -> 15.1 us
    reduce_scatter x1 -> x0, waiting for transfers between devices: 102 us -> none  [per_device(): lax.psum_scatter(flat, ('sub', 'coarse'), scatter_dimension=0, tiled=True)]
    all_gather x1 -> x0, waiting for transfers between devices: 41.9 us -> none  [per_device(): lax.all_gather(share.astype(jnp.bfloat16), ('sub', 'coarse'), axis=0, til...]
    ppermute x0 -> x30, starting transfers between devices: none -> 41.2 us  [the longest x15 23 us: halve(): return keep + lax.ppermute(send, axis, pairs(axis, mask))]
    ppermute x0 -> x30, waiting for transfers between devices: none -> 12.6 us  [the longest x15 7.86 us: halve(): return keep + lax.ppermute(send, axis, pairs(axis, mask))]
    all_gather x1, waiting for transfers between devices: 6.36 us -> 0.02 us  [per_device(): inverse_all = lax.all_gather(coarse_inverse, 'coarse', axis=0, tiled=True)]
    gather x2, local copies, waits for them, and re-layouts: 8.5 us -> 2.77 us  [the longest x1 2.15 us: per_device(): lifted = jnp.take(coarse_out, interface, axis=1)]
    dot_general x3, matrix products: 12.9 us -> 7.23 us  [the longest x1 3.93 us: per_device(): jnp.einsum('jqn,jqrc->rnc', onehot, terms, precision=lax.Precision.HIGHEST)]
    all_gather x1, blocking collectives: 6.3 us -> 11.9 us  [per_device(): pattern_all = lax.all_gather(coarse_pattern, 'coarse', axis=0, tiled=True)]
  transfers between devices with their start and end apart: 5 -> 33, of which waited for: 4 -> 12; matrix products, arithmetic and copies ran while one was open for 9% -> 17% of each run, Pallas kernels for 0% -> 0%
where the time goes in v2:
time: 133 us; the launch traced here: 132 us
  starting transfers between devices  45.2 us (34%)
  local copies, waits for them, and re-layouts  20 us (15%)
  matrix products  15.1 us (11%)
  between operations  14 us (11%)
  other arithmetic  13.1 us (10%)
  waiting for transfers between devices  12.7 us (10%)
  blocking collectives  11.9 us (9%)
    ppermute x15, starting transfers between devices, halve(): return keep + lax.ppermute(send, axis, pairs(axis, mask))  23 us
    ppermute x15, starting transfers between devices, double(): recv = lax.ppermute(y, axis, pairs(axis, mask))  18.2 us
    all_gather x1, blocking collectives, per_device(): pattern_all = lax.all_gather(coarse_pattern, 'coarse', axis=0, tiled=True)  11.9 us
    ppermute x15, waiting for transfers between devices, halve(): return keep + lax.ppermute(send, axis, pairs(axis, mask))  7.86 us
    select_n x15, other arithmetic, double(): jnp.where(v == 0, jnp.concatenate([y, recv], axis=dim), jnp.concatenate([...  5.32 us
    ppermute x15, waiting for transfers between devices, double(): recv = lax.ppermute(y, axis, pairs(axis, mask))  4.79 us
    dot_general x1, matrix products, per_device(): jnp.einsum('jerb,jebc->jrc', picked, inverse_blocks, preferred_element_ty...  4.48 us
    gather x1, local copies, waits for them, and re-layouts, per_device(): picked = jnp.take(extended, margin, axis=0)  4.2 us
  transfers between devices with their start and end apart: 33, of which 12 were waited for; matrix products, arithmetic and copies ran while one was open for 17% of the time, Pallas kernels for 0%

profile of v2, /device:TPU:0, one launch (start us, length us, event | category | flops | bytes accessed | tf_op | source)
XLA Modules:
  0.0 132.0 jit_solution(1379038838364969100)
XLA Ops:
  6.5 3.4 %convolution_bitcast_fusion = f32[4,2,512,128]{2,3,1,0:T(8,128)} fusion(bf16[4,2,256,128]{3,2,1,0:T(8,128)(2,1)} %param.11, bf16[4,512,256]{2,1,0:T(8,128)(2,1)} %param.7), kind=kOutput, calls=%fused_computation.9 | convolution fusion | flops 268435456 | bytes 3670016 | tf_op jit(solution)/shard_map/jrb,jqbc->jqrc/dot_general | solution.py:73
  9.9 2.9 %copy.47 = f32[4,2,512,128]{3,0,1,2:T(4,128)} copy(f32[4,2,512,128]{2,3,1,0:T(8,128)} %convolution_bitcast_fusion) | data formatting | bytes 4194304 | tf_op jit(solution)/shard_map/jrb,jqbc->jqrc/transpose | solution.py:73
  12.8 3.9 %fusion.32 = f32[512,128,12,1]{1,2,3,0:T(8,128)S(1)} fusion(f32[4,2,512,128]{3,0,1,2:T(4,128)} %copy.47, s32[4,2]{0,1:T(2,128)S(1)} %copy-done.6), kind=kOutput, calls=%fused_computation.104 | convolution fusion | flops 75497568 | bytes 5242912 | tf_op jit(solution)/shard_map/jqn,jqrc->rnc/dot_general | solution.py:76
  16.8 2.2 %fusion.44 = (f32[2,2,2,2,2,16,4,128]{7,6,5,4,3,2,1,0:T(4,128)}, f32[2,2,2,2,2,16,4,128]{7,6,5,4,3,2,1,0:T(4,128)S(1)}, f32[2,2,2,2,2,16,4,128]{7,6,5,4,3,2,1,0:T(4,128)}) fusion(f32[2,2,2,2,2,16,12,128]{7,6,5,4,3,2,1,0:T(8,128)S(1)} %bitcast.114), kind=kLoop, calls=%fused_computation.122 | loop fusion | bytes 6291456 | tf_op jit(solution)/shard_map/slice | solution.py:86
  19.0 2.2 %constant_dynamic-slice_fusion.17 = (f32[1,2,2,2,2,16,4,128]{7,6,5,4,3,2,1,0:T(4,128)}, f32[1,2,2,2,2,16,4,128]{7,6,5,4,3,2,1,0:T(4,128)S(1)}) fusion(f32[2,2,2,2,2,16,4,128]{7,6,5,4,3,2,1,0:T(4,128)} %get-tuple-element.5, s32[]{:T(128)S(6)} %select_n.676, s32[]{:T(128)S(6)} %select_n.677), kind=kLoop, calls=%fused_computation.92 | loop fusion | bytes 2097160 | tf_op jit(solution)/shard_map/jit(dynamic_index_in_dim)/dynamic_slice | solution.py:46
  26.7 2.7 %collective-permute-start = (bf16[1,512,256]{2,1,0:T(8,128)(2,1)}, bf16[1,512,256]{2,1,0:T(8,128)(2,1)}, u32[]{:S(2)}, u32[]{:S(2)}) collective-permute-start(bf16[1,512,256]{2,1,0:T(8,128)(2,1)} %get-tuple-element.8), channel_id=1, source_target_pairs={{0,1},{1,2},{2,3},{3,4},{4,5},{5,6},{6,7},{7,8},{8,9},{9,10},{10,1... | collective-permute-start | bytes 786440 | tf_op jit(solution)/shard_map/ppermute | solution.py:15
  30.7 11.9 %all-gather = s32[4,3,4]{2,1,0:T(4,128)S(1)} all-gather(s32[1,3,4]{2,1,0:T(4,128)S(1)} %bitcast.132), channel_id=1, replica_groups=mesh['sub'=8,'coarse'=4] {'coarse'}, dimensions={0}, use_global_device_ids=true | all-gather | bytes 240 | tf_op jit(solution)/shard_map/all_gather | solution.py:67
  46.2 1.5 %collective-permute-start.8 = (f32[1,2,1,2,2,16,4,128]{7,5,6,4,3,2,1,0:T(8,128)S(1)}, f32[1,2,1,2,2,16,4,128]{7,5,6,4,3,2,1,0:T(8,128)S(1)}, u32[]{:S(2)}, u32[]{:S(2)}) collective-permute-start(f32[1,2,1,2,2,16,4,128]{7,5,6,4,3,2,1,0:T(8,128)S(1)} %constant_dynamic-slice_fusion.9), channel_id=1, source_target_pairs={{0,4},{4,0},{8,12},{12,8},{16,20},{20,16},{24,28},{28,24},{1,5},{5... | collective-permute-start | bytes 786440 | tf_op jit(solution)/shard_map/ppermute | solution.py:48
  48.9 2.9 %collective-permute-start.13 = (f32[1,2,2,1,2,16,4,128]{7,5,6,4,3,2,1,0:T(8,128)S(1)}, f32[1,2,2,1,2,16,4,128]{7,5,6,4,3,2,1,0:T(8,128)S(1)}, u32[]{:S(2)}, u32[]{:S(2)}) collective-permute-start(f32[1,2,2,1,2,16,4,128]{7,5,6,4,3,2,1,0:T(8,128)S(1)} %constant_dynamic-slice_fusion.3), channel_id=1, source_target_pairs={{0,8},{4,12},{8,0},{12,4},{16,24},{20,28},{24,16},{28,20},{1,9},{5... | collective-permute-start | bytes 786440 | tf_op jit(solution)/shard_map/ppermute | solution.py:48
  51.8 1.6 %collective-permute-done.3 = f32[1,1,2,2,2,16,4,128]{7,5,6,4,3,2,1,0:T(8,128)S(1)} collective-permute-done((f32[1,1,2,2,2,16,4,128]{7,5,6,4,3,2,1,0:T(8,128)S(1)}, f32[1,1,2,2,2,16,4,128]{7,5,6,4,3,2,1,0:T(8,128)S(1)}, u32[]{:S(2)}, u32[]{:S(2)}) %collective-permute-start.3) | collective-permute-done | bytes 262176 | tf_op jit(solution)/shard_map/ppermute | solution.py:48
  53.5 1.6 %collective-permute-start.4 = (f32[1,1,1,2,2,16,4,128]{7,5,6,4,3,2,1,0:T(8,128)S(1)}, f32[1,1,1,2,2,16,4,128]{7,5,6,4,3,2,1,0:T(8,128)S(1)}, u32[]{:S(2)}, u32[]{:S(2)}) collective-permute-start(f32[1,1,1,2,2,16,4,128]{7,5,6,4,3,2,1,0:T(8,128)S(1)} %constant_dynamic-slice_fusion.14), channel_id=1, source_target_pairs={{0,4},{4,0},{8,12},{12,8},{16,20},{20,16},{24,28},{28,24},{1,5},{5... | collective-permute-start | bytes 393224 | tf_op jit(solution)/shard_map/ppermute | solution.py:48
  55.2 4.0 %collective-permute-start.9 = (f32[1,2,1,1,2,16,4,128]{7,5,6,4,3,2,1,0:T(8,128)S(1)}, f32[1,2,1,1,2,16,4,128]{7,5,6,4,3,2,1,0:T(8,128)S(1)}, u32[]{:S(2)}, u32[]{:S(2)}) collective-permute-start(f32[1,2,1,1,2,16,4,128]{7,5,6,4,3,2,1,0:T(8,128)S(1)} %constant_dynamic-slice_fusion.8), channel_id=1, source_target_pairs={{0,8},{4,12},{8,0},{12,4},{16,24},{20,28},{24,16},{28,20},{1,9},{5... | collective-permute-start | bytes 393224 | tf_op jit(solution)/shard_map/ppermute | solution.py:48
  59.3 3.1 %collective-permute-start.14 = (f32[1,2,2,1,1,16,4,128]{7,5,6,4,3,2,1,0:T(8,128)S(1)}, f32[1,2,2,1,1,16,4,128]{7,5,6,4,3,2,1,0:T(8,128)S(1)}, u32[]{:S(2)}, u32[]{:S(2)}) collective-permute-start(f32[1,2,2,1,1,16,4,128]{7,5,6,4,3,2,1,0:T(8,128)S(1)} %constant_dynamic-slice_fusion.2), channel_id=1, source_target_pairs={{0,16},{4,20},{8,24},{12,28},{16,0},{20,4},{24,8},{28,12},{1,17},{... | collective-permute-start | bytes 393224 | tf_op jit(solution)/shard_map/ppermute | solution.py:48
  63.6 3.4 %collective-permute-start.10 = (f32[1,2,1,1,1,16,4,128]{7,5,6,4,3,2,1,0:T(8,128)S(1)}, f32[1,2,1,1,1,16,4,128]{7,5,6,4,3,2,1,0:T(8,128)S(1)}, u32[]{:S(2)}, u32[]{:S(2)}) collective-permute-start(f32[1,2,1,1,1,16,4,128]{7,5,6,4,3,2,1,0:T(8,128)S(1)} %constant_dynamic-slice_fusion.7), channel_id=1, source_target_pairs={{0,16},{4,20},{8,24},{12,28},{16,0},{20,4},{24,8},{28,12},{1,17},{... | collective-permute-start | bytes 196616 | tf_op jit(solution)/shard_map/ppermute | solution.py:48
  67.0 2.2 %collective-permute-done.14 = f32[1,2,2,1,1,16,4,128]{7,5,6,4,3,2,1,0:T(8,128)S(1)} collective-permute-done((f32[1,2,2,1,1,16,4,128]{7,5,6,4,3,2,1,0:T(8,128)S(1)}, f32[1,2,2,1,1,16,4,128]{7,5,6,4,3,2,1,0:T(8,128)S(1)}, u32[]{:S(2)}, u32[]{:S(2)}) %collective-permute-start.14) | collective-permute-done | bytes 131104 | tf_op jit(solution)/shard_map/ppermute | solution.py:48
  69.2 1.6 %collective-permute-start.15 = (f32[1,1,2,1,1,16,4,128]{7,5,6,4,3,2,1,0:T(8,128)S(1)}, f32[1,1,2,1,1,16,4,128]{7,5,6,4,3,2,1,0:T(8,128)S(1)}, u32[]{:S(2)}, u32[]{:S(2)}) collective-permute-start(f32[1,1,2,1,1,16,4,128]{7,5,6,4,3,2,1,0:T(8,128)S(1)} %constant_dynamic-slice_fusion.1), channel_id=1, source_target_pairs={{0,2},{1,3},{2,0},{3,1},{4,6},{5,7},{6,4},{7,5},{8,10},{9,11},{10,... | collective-permute-start | bytes 196616 | tf_op jit(solution)/shard_map/ppermute | solution.py:48
  72.0 1.5 %collective-permute-done.15 = f32[1,1,2,1,1,16,4,128]{7,5,6,4,3,2,1,0:T(8,128)S(1)} collective-permute-done((f32[1,1,2,1,1,16,4,128]{7,5,6,4,3,2,1,0:T(8,128)S(1)}, f32[1,1,2,1,1,16,4,128]{7,5,6,4,3,2,1,0:T(8,128)S(1)}, u32[]{:S(2)}, u32[]{:S(2)}) %collective-permute-start.15) | collective-permute-done | bytes 65568 | tf_op jit(solution)/shard_map/ppermute | solution.py:48
  75.7 1.8 %collective-permute-done.16 = f32[1,1,1,1,1,16,4,128]{7,5,6,4,3,2,1,0:T(8,128)S(1)} collective-permute-done((f32[1,1,1,1,1,16,4,128]{7,5,6,4,3,2,1,0:T(8,128)S(1)}, f32[1,1,1,1,1,16,4,128]{7,5,6,4,3,2,1,0:T(8,128)S(1)}, u32[]{:S(2)}, u32[]{:S(2)}) %collective-permute-start.16) | collective-permute-done | bytes 32800 | tf_op jit(solution)/shard_map/ppermute | solution.py:48
  78.2 1.8 %fusion.8 = bf16[1,1,1,1,1,16,12,128]{7,5,6,4,3,2,1,0:T(8,128)(2,1)S(1)} fusion(bf16[12,4,128,128]{3,2,1,0:T(8,128)(2,1)} %all-gather.3.cloned.1.call-done, bf16[12,4,16,128]{3,2,1,0:T(8,128)(2,1)S(1)} %bitcast.120, pred[12,4]{1,0:T(8,128)(4,1)S(1)} %copy.45), kind=kOutput, calls=%fused_computation.14 | convolution fusion | flops 25288704 | bytes 1818672 | tf_op jit(solution)/shard_map/rnec,necd->rnd/dot_general | solution.py:92
  81.1 1.5 %collective-permute-start.22 = (bf16[1,1,1,1,1,16,4,128]{7,5,6,4,3,2,1,0:T(8,128)(2,1)S(1)}, bf16[1,1,1,1,1,16,4,128]{7,5,6,4,3,2,1,0:T(8,128)(2,1)S(1)}, u32[]{:S(2)}, u32[]{:S(2)}) collective-permute-start(bf16[1,1,1,1,1,16,4,128]{7,5,6,4,3,2,1,0:T(8,128)(2,1)S(1)} %get-tuple-element.27), channel_id=1, source_target_pairs={{0,2},{1,3},{2,0},{3,1},{4,6},{5,7},{6,4},{7,5},{8,10},{9,11},{10,... | collective-permute-start | bytes 49160 | tf_op jit(solution)/shard_map/ppermute | solution.py:53
  84.8 3.5 %collective-permute-start.18 = (bf16[1,1,1,1,2,16,4,128]{7,5,6,4,3,2,1,0:T(8,128)(2,1)S(1)}, bf16[1,1,1,1,2,16,4,128]{7,5,6,4,3,2,1,0:T(8,128)(2,1)S(1)}, u32[]{:S(2)}, u32[]{:S(2)}) collective-permute-start(bf16[1,1,1,1,2,16,4,128]{7,5,6,4,3,2,1,0:T(8,128)(2,1)S(1)} %maximum_select_fusion.18), channel_id=1, source_target_pairs={{0,8},{4,12},{8,0},{12,4},{16,24},{20,28},{24,16},{28,20},{1,9},{5... | collective-permute-start | bytes 98312 | tf_op jit(solution)/shard_map/ppermute | solution.py:53
  88.3 1.6 %collective-permute-start.23 = (bf16[1,2,1,1,1,16,4,128]{7,5,6,1,4,3,2,0:T(8,128)(2,1)S(1)}, bf16[1,2,1,1,1,16,4,128]{7,5,6,1,4,3,2,0:T(8,128)(2,1)S(1)}, u32[]{:S(2)}, u32[]{:S(2)}) collective-permute-start(bf16[1,2,1,1,1,16,4,128]{7,5,6,1,4,3,2,0:T(8,128)(2,1)S(1)} %fusion.22), channel_id=1, source_target_pairs={{0,16},{4,20},{8,24},{12,28},{16,0},{20,4},{24,8},{28,12},{1,17},{... | collective-permute-start | bytes 98312 | tf_op jit(solution)/shard_map/ppermute | solution.py:53
  89.8 1.9 %collective-permute-start.28 = (bf16[1,1,2,1,1,16,4,128]{7,5,6,4,3,2,1,0:T(8,128)(2,1)S(1)}, bf16[1,1,2,1,1,16,4,128]{7,5,6,4,3,2,1,0:T(8,128)(2,1)S(1)}, u32[]{:S(2)}, u32[]{:S(2)}) collective-permute-start(bf16[1,1,2,1,1,16,4,128]{7,5,6,4,3,2,1,0:T(8,128)(2,1)S(1)} %maximum_select_fusion.22), channel_id=1, source_target_pairs={{0,2},{1,3},{2,0},{3,1},{4,6},{5,7},{6,4},{7,5},{8,10},{9,11},{10,... | collective-permute-start | bytes 98312 | tf_op jit(solution)/shard_map/ppermute | solution.py:53
  94.0 1.5 %collective-permute-start.29 = (bf16[1,2,2,1,1,16,4,128]{7,5,6,4,3,2,1,0:T(8,128)(2,1)S(1)}, bf16[1,2,2,1,1,16,4,128]{7,5,6,4,3,2,1,0:T(8,128)(2,1)S(1)}, u32[]{:S(2)}, u32[]{:S(2)}) collective-permute-start(bf16[1,2,2,1,1,16,4,128]{7,5,6,4,3,2,1,0:T(8,128)(2,1)S(1)} %fusion.21), channel_id=1, source_target_pairs={{0,16},{4,20},{8,24},{12,28},{16,0},{20,4},{24,8},{28,12},{1,17},{... | collective-permute-start | bytes 196616 | tf_op jit(solution)/shard_map/ppermute | solution.py:53
  96.2 1.7 %collective-permute-start.20 = (bf16[1,1,2,2,2,16,4,128]{7,5,6,4,3,2,1,0:T(8,128)(2,1)S(1)}, bf16[1,1,2,2,2,16,4,128]{7,5,6,4,3,2,1,0:T(8,128)(2,1)S(1)}, u32[]{:S(2)}, u32[]{:S(2)}) collective-permute-start(bf16[1,1,2,2,2,16,4,128]{7,5,6,4,3,2,1,0:T(8,128)(2,1)S(1)} %maximum_select_fusion.7), channel_id=1, source_target_pairs={{0,2},{1,3},{2,0},{3,1},{4,6},{5,7},{6,4},{7,5},{8,10},{9,11},{10,... | collective-permute-start | bytes 393224 | tf_op jit(solution)/shard_map/ppermute | solution.py:53
  99.3 1.7 %collective-permute-start.30 = (bf16[1,2,2,1,2,16,4,128]{7,5,6,4,3,2,1,0:T(8,128)(2,1)S(1)}, bf16[1,2,2,1,2,16,4,128]{7,5,6,4,3,2,1,0:T(8,128)(2,1)S(1)}, u32[]{:S(2)}, u32[]{:S(2)}) collective-permute-start(bf16[1,2,2,1,2,16,4,128]{7,5,6,4,3,2,1,0:T(8,128)(2,1)S(1)} %maximum_select_fusion.11), channel_id=1, source_target_pairs={{0,8},{4,12},{8,0},{12,4},{16,24},{20,28},{24,16},{28,20},{1,9},{5... | collective-permute-start | bytes 393224 | tf_op jit(solution)/shard_map/ppermute | solution.py:53
  101.3 1.6 %collective-permute-done.25 = bf16[1,2,1,2,2,16,4,128]{7,5,6,4,3,2,1,0:T(8,128)(2,1)S(1)} collective-permute-done((bf16[1,2,1,2,2,16,4,128]{7,5,6,4,3,2,1,0:T(8,128)(2,1)S(1)}, bf16[1,2,1,2,2,16,4,128]{7,5,6,4,3,2,1,0:T(8,128)(2,1)S(1)}, u32[]{:S(2)}, u32[]{:S(2)}) %collective-permute-start.25) | collective-permute-done | bytes 131104 | tf_op jit(solution)/shard_map/ppermute | solution.py:53
  105.0 2.4 %pad_maximum_fusion = bf16[6,512,256]{2,1,0:T(8,128)(2,1)} fusion(bf16[1,512,256]{2,1,0:T(8,128)(2,1)} %collective-permute-done.1, bf16[4,512,256]{2,1,0:T(8,128)(2,1)S(1)} %copy-done.1, bf16[1,512,256]{2,1,0:T(8,128)(2,1)} %collective-permute-done), kind=kLoop, calls=%fused_computation.10 | loop fusion | flops 1572864 | bytes 3145728 | tf_op jit(solution)/shard_map/concatenate | solution.py:13
  107.4 4.2 %gather_fusion = bf16[16,512,256]{2,1,0:T(8,128)(2,1)} fusion(bf16[6,512,256]{2,1,0:T(8,128)(2,1)} %pad_maximum_fusion, s32[1024]{0:T(1024)S(1)} %pad_clamp_fusion.2), kind=kCustom, calls=%fused_computation | custom fusion | bytes 8388672 | tf_op jit(solution)/shard_map/jit(_take)/gather | solution.py:101
  116.9 2.2 %gather_fusion.2 = bf16[8,512,128]{2,1,0:T(8,128)(2,1)S(1)} fusion(bf16[512,12,128]{2,0,1:T(8,128)(2,1)} %pad_maximum_fusion.1, s32[1024]{0:T(1024)S(1)} %pad_clamp_fusion), kind=kCustom, calls=%fused_computation.2 | custom fusion | bytes 2097184 | tf_op jit(solution)/shard_map/jit(_take)/gather | solution.py:103
  119.1 1.5 %fusion.10 = f32[4,512,256,1]{2,1,3,0:T(8,128)S(1)} fusion(bf16[4,2,256,128]{3,2,1,0:T(8,128)(2,1)} %param.11, bf16[4,2,512,128]{3,2,1,0:T(8,128)(2,1)S(1)} %bitcast.116, pred[4,2]{1,0:T(4,128)(4,1)S(1)} %copy.43), kind=kOutput, calls=%fused_computation.16 | convolution fusion | flops 268959744 | bytes 3670024 | tf_op jit(solution)/shard_map/rjqc,jqbc->jrb/dot_general | solution.py:104
  120.6 4.5 %fusion.3 = bf16[4,512,256]{2,1,0:T(8,128)(2,1)} fusion(f32[4,512,256,1]{2,1,3,0:T(8,128)S(1)} %fusion.10, bf16[4,4,256,256]{3,2,1,0:T(8,128)(2,1)S(1)} %copy-done, bf16[4,4,512,256]{3,2,1,0:T(8,128)(2,1)} %bitcast.115, pred[4,4]{1,0:T(4,128)(4,1)S(1)} %compare_and_fusion.2), kind=kOutput, calls=%fused_computation.7 | convolution fusion | flops 1076887552 | bytes 9437200 | tf_op jit(solution)/shard_map/jerb,jebc->jrc/dot_general | solution.py:102
  (145 shorter events, 32.0 us)
Async XLA Ops:
  6.5 71.7 %all-gather.3.cloned.1.call-start = ((), (), s32[]{:S(2)}) async-start(), calls=%async_computation | async-start | bytes 1966080 | tf_op jit(solution)/shard_map/all_gather | solution.py:68
  22.0 21.4 %collective-permute-start.2 = (f32[1,2,2,2,2,16,4,128]{7,5,6,4,3,2,1,0:T(8,128)}, f32[1,2,2,2,2,16,4,128]{7,5,6,4,3,2,1,0:T(8,128)}, u32[]{:S(2)}, u32[]{:S(2)}) collective-permute-start(f32[1,2,2,2,2,16,4,128]{7,5,6,4,3,2,1,0:T(8,128)} %copy.74), channel_id=1, source_target_pairs={{0,1},{1,0},{2,3},{3,2},{4,5},{5,4},{6,7},{7,6},{8,9},{9,8},{10,11... | collective-permute-start | bytes 1572872 | tf_op jit(solution)/shard_map/ppermute | solution.py:48
  24.5 20.6 %collective-permute-start.7 = (f32[1,2,2,2,2,16,4,128]{7,5,6,4,3,2,1,0:T(8,128)}, f32[1,2,2,2,2,16,4,128]{7,5,6,4,3,2,1,0:T(8,128)}, u32[]{:S(2)}, u32[]{:S(2)}) collective-permute-start(f32[1,2,2,2,2,16,4,128]{7,5,6,4,3,2,1,0:T(8,128)} %copy.77), channel_id=1, source_target_pairs={{0,1},{1,0},{2,3},{3,2},{4,5},{5,4},{6,7},{7,6},{8,9},{9,8},{10,11... | collective-permute-start | bytes 1572872 | tf_op jit(solution)/shard_map/ppermute | solution.py:48
  25.4 22.4 %collective-permute-start.12 = (f32[1,2,2,2,2,16,4,128]{7,5,6,4,3,2,1,0:T(8,128)}, f32[1,2,2,2,2,16,4,128]{7,5,6,4,3,2,1,0:T(8,128)}, u32[]{:S(2)}, u32[]{:S(2)}) collective-permute-start(f32[1,2,2,2,2,16,4,128]{7,5,6,4,3,2,1,0:T(8,128)} %copy.80), channel_id=1, source_target_pairs={{0,1},{1,0},{2,3},{3,2},{4,5},{5,4},{6,7},{7,6},{8,9},{9,8},{10,11... | collective-permute-start | bytes 1572872 | tf_op jit(solution)/shard_map/ppermute | solution.py:48
  26.7 78.3 %collective-permute-start = (bf16[1,512,256]{2,1,0:T(8,128)(2,1)}, bf16[1,512,256]{2,1,0:T(8,128)(2,1)}, u32[]{:S(2)}, u32[]{:S(2)}) collective-permute-start(bf16[1,512,256]{2,1,0:T(8,128)(2,1)} %get-tuple-element.8), channel_id=1, source_target_pairs={{0,1},{1,2},{2,3},{3,4},{4,5},{5,6},{6,7},{7,8},{8,9},{9,10},{10,1... | collective-permute-start | bytes 786440 | tf_op jit(solution)/shard_map/ppermute | solution.py:15
  29.4 75.6 %collective-permute-start.1 = (bf16[1,512,256]{2,1,0:T(8,128)(2,1)}, bf16[1,512,256]{2,1,0:T(8,128)(2,1)}, u32[]{:S(2)}, u32[]{:S(2)}) collective-permute-start(bf16[1,512,256]{2,1,0:T(8,128)(2,1)} %get-tuple-element.9), channel_id=1, source_target_pairs={{1,0},{2,1},{3,2},{4,3},{5,4},{6,5},{7,6},{8,7},{9,8},{10,9},{11,1... | collective-permute-start | bytes 786440 | tf_op jit(solution)/shard_map/ppermute | solution.py:17
  44.9 8.6 %collective-permute-start.3 = (f32[1,1,2,2,2,16,4,128]{7,5,6,4,3,2,1,0:T(8,128)S(1)}, f32[1,1,2,2,2,16,4,128]{7,5,6,4,3,2,1,0:T(8,128)S(1)}, u32[]{:S(2)}, u32[]{:S(2)}) collective-permute-start(f32[1,1,2,2,2,16,4,128]{7,5,6,4,3,2,1,0:T(8,128)S(1)} %constant_dynamic-slice_fusion.15), channel_id=1, source_target_pairs={{0,2},{1,3},{2,0},{3,1},{4,6},{5,7},{6,4},{7,5},{8,10},{9,11},{10,... | collective-permute-start | bytes 786440 | tf_op jit(solution)/shard_map/ppermute | solution.py:48
  46.2 8.9 %collective-permute-start.8 = (f32[1,2,1,2,2,16,4,128]{7,5,6,4,3,2,1,0:T(8,128)S(1)}, f32[1,2,1,2,2,16,4,128]{7,5,6,4,3,2,1,0:T(8,128)S(1)}, u32[]{:S(2)}, u32[]{:S(2)}) collective-permute-start(f32[1,2,1,2,2,16,4,128]{7,5,6,4,3,2,1,0:T(8,128)S(1)} %constant_dynamic-slice_fusion.9), channel_id=1, source_target_pairs={{0,4},{4,0},{8,12},{12,8},{16,20},{20,16},{24,28},{28,24},{1,5},{5... | collective-permute-start | bytes 786440 | tf_op jit(solution)/shard_map/ppermute | solution.py:48
  48.9 10.3 %collective-permute-start.13 = (f32[1,2,2,1,2,16,4,128]{7,5,6,4,3,2,1,0:T(8,128)S(1)}, f32[1,2,2,1,2,16,4,128]{7,5,6,4,3,2,1,0:T(8,128)S(1)}, u32[]{:S(2)}, u32[]{:S(2)}) collective-permute-start(f32[1,2,2,1,2,16,4,128]{7,5,6,4,3,2,1,0:T(8,128)S(1)} %constant_dynamic-slice_fusion.3), channel_id=1, source_target_pairs={{0,8},{4,12},{8,0},{12,4},{16,24},{20,28},{24,16},{28,20},{1,9},{5... | collective-permute-start | bytes 786440 | tf_op jit(solution)/shard_map/ppermute | solution.py:48
  53.5 8.8 %collective-permute-start.4 = (f32[1,1,1,2,2,16,4,128]{7,5,6,4,3,2,1,0:T(8,128)S(1)}, f32[1,1,1,2,2,16,4,128]{7,5,6,4,3,2,1,0:T(8,128)S(1)}, u32[]{:S(2)}, u32[]{:S(2)}) collective-permute-start(f32[1,1,1,2,2,16,4,128]{7,5,6,4,3,2,1,0:T(8,128)S(1)} %constant_dynamic-slice_fusion.14), channel_id=1, source_target_pairs={{0,4},{4,0},{8,12},{12,8},{16,20},{20,16},{24,28},{28,24},{1,5},{5... | collective-permute-start | bytes 393224 | tf_op jit(solution)/shard_map/ppermute | solution.py:48
  55.2 8.4 %collective-permute-start.9 = (f32[1,2,1,1,2,16,4,128]{7,5,6,4,3,2,1,0:T(8,128)S(1)}, f32[1,2,1,1,2,16,4,128]{7,5,6,4,3,2,1,0:T(8,128)S(1)}, u32[]{:S(2)}, u32[]{:S(2)}) collective-permute-start(f32[1,2,1,1,2,16,4,128]{7,5,6,4,3,2,1,0:T(8,128)S(1)} %constant_dynamic-slice_fusion.8), channel_id=1, source_target_pairs={{0,8},{4,12},{8,0},{12,4},{16,24},{20,28},{24,16},{28,20},{1,9},{5... | collective-permute-start | bytes 393224 | tf_op jit(solution)/shard_map/ppermute | solution.py:48
  59.3 9.9 %collective-permute-start.14 = (f32[1,2,2,1,1,16,4,128]{7,5,6,4,3,2,1,0:T(8,128)S(1)}, f32[1,2,2,1,1,16,4,128]{7,5,6,4,3,2,1,0:T(8,128)S(1)}, u32[]{:S(2)}, u32[]{:S(2)}) collective-permute-start(f32[1,2,2,1,1,16,4,128]{7,5,6,4,3,2,1,0:T(8,128)S(1)} %constant_dynamic-slice_fusion.2), channel_id=1, source_target_pairs={{0,16},{4,20},{8,24},{12,28},{16,0},{20,4},{24,8},{28,12},{1,17},{... | collective-permute-start | bytes 393224 | tf_op jit(solution)/shard_map/ppermute | solution.py:48
  62.4 8.4 %collective-permute-start.5 = (f32[1,1,1,1,2,16,4,128]{7,5,6,4,3,2,1,0:T(8,128)S(1)}, f32[1,1,1,1,2,16,4,128]{7,5,6,4,3,2,1,0:T(8,128)S(1)}, u32[]{:S(2)}, u32[]{:S(2)}) collective-permute-start(f32[1,1,1,1,2,16,4,128]{7,5,6,4,3,2,1,0:T(8,128)S(1)} %constant_dynamic-slice_fusion.13), channel_id=1, source_target_pairs={{0,8},{4,12},{8,0},{12,4},{16,24},{20,28},{24,16},{28,20},{1,9},{5... | collective-permute-start | bytes 196616 | tf_op jit(solution)/shard_map/ppermute | solution.py:48
  63.6 7.7 %collective-permute-start.10 = (f32[1,2,1,1,1,16,4,128]{7,5,6,4,3,2,1,0:T(8,128)S(1)}, f32[1,2,1,1,1,16,4,128]{7,5,6,4,3,2,1,0:T(8,128)S(1)}, u32[]{:S(2)}, u32[]{:S(2)}) collective-permute-start(f32[1,2,1,1,1,16,4,128]{7,5,6,4,3,2,1,0:T(8,128)S(1)} %constant_dynamic-slice_fusion.7), channel_id=1, source_target_pairs={{0,16},{4,20},{8,24},{12,28},{16,0},{20,4},{24,8},{28,12},{1,17},{... | collective-permute-start | bytes 196616 | tf_op jit(solution)/shard_map/ppermute | solution.py:48
  69.2 4.3 %collective-permute-start.15 = (f32[1,1,2,1,1,16,4,128]{7,5,6,4,3,2,1,0:T(8,128)S(1)}, f32[1,1,2,1,1,16,4,128]{7,5,6,4,3,2,1,0:T(8,128)S(1)}, u32[]{:S(2)}, u32[]{:S(2)}) collective-permute-start(f32[1,1,2,1,1,16,4,128]{7,5,6,4,3,2,1,0:T(8,128)S(1)} %constant_dynamic-slice_fusion.1), channel_id=1, source_target_pairs={{0,2},{1,3},{2,0},{3,1},{4,6},{5,7},{6,4},{7,5},{8,10},{9,11},{10,... | collective-permute-start | bytes 196616 | tf_op jit(solution)/shard_map/ppermute | solution.py:48
  70.8 4.9 %collective-permute-start.6 = (f32[1,1,1,1,1,16,4,128]{7,5,6,4,3,2,1,0:T(8,128)S(1)}, f32[1,1,1,1,1,16,4,128]{7,5,6,4,3,2,1,0:T(8,128)S(1)}, u32[]{:S(2)}, u32[]{:S(2)}) collective-permute-start(f32[1,1,1,1,1,16,4,128]{7,5,6,4,3,2,1,0:T(8,128)S(1)} %constant_dynamic-slice_fusion.12), channel_id=1, source_target_pairs={{0,16},{4,20},{8,24},{12,28},{16,0},{20,4},{24,8},{28,12},{1,17},{... | collective-permute-start | bytes 98312 | tf_op jit(solution)/shard_map/ppermute | solution.py:48
  71.3 4.4 %collective-permute-start.11 = (f32[1,1,1,1,1,16,4,128]{7,5,6,4,3,2,1,0:T(8,128)S(1)}, f32[1,1,1,1,1,16,4,128]{7,5,6,4,3,2,1,0:T(8,128)S(1)}, u32[]{:S(2)}, u32[]{:S(2)}) collective-permute-start(f32[1,1,1,1,1,16,4,128]{7,5,6,4,3,2,1,0:T(8,128)S(1)} %constant_dynamic-slice_fusion.6), channel_id=1, source_target_pairs={{0,2},{1,3},{2,0},{3,1},{4,6},{5,7},{6,4},{7,5},{8,10},{9,11},{10,... | collective-permute-start | bytes 98312 | tf_op jit(solution)/shard_map/ppermute | solution.py:48
  80.0 4.7 %collective-permute-start.17 = (bf16[1,1,1,1,1,16,4,128]{7,5,6,4,3,2,1,0:T(8,128)(2,1)S(1)}, bf16[1,1,1,1,1,16,4,128]{7,5,6,4,3,2,1,0:T(8,128)(2,1)S(1)}, u32[]{:S(2)}, u32[]{:S(2)}) collective-permute-start(bf16[1,1,1,1,1,16,4,128]{7,5,6,4,3,2,1,0:T(8,128)(2,1)S(1)} %get-tuple-element.28), channel_id=1, source_target_pairs={{0,16},{4,20},{8,24},{12,28},{16,0},{20,4},{24,8},{28,12},{1,17},{... | collective-permute-start | bytes 49160 | tf_op jit(solution)/shard_map/ppermute | solution.py:53
  81.1 7.1 %collective-permute-start.22 = (bf16[1,1,1,1,1,16,4,128]{7,5,6,4,3,2,1,0:T(8,128)(2,1)S(1)}, bf16[1,1,1,1,1,16,4,128]{7,5,6,4,3,2,1,0:T(8,128)(2,1)S(1)}, u32[]{:S(2)}, u32[]{:S(2)}) collective-permute-start(bf16[1,1,1,1,1,16,4,128]{7,5,6,4,3,2,1,0:T(8,128)(2,1)S(1)} %get-tuple-element.27), channel_id=1, source_target_pairs={{0,2},{1,3},{2,0},{3,1},{4,6},{5,7},{6,4},{7,5},{8,10},{9,11},{10,... | collective-permute-start | bytes 49160 | tf_op jit(solution)/shard_map/ppermute | solution.py:53
  82.6 7.2 %collective-permute-start.27 = (bf16[1,1,1,1,1,16,4,128]{7,5,6,4,3,2,1,0:T(8,128)(2,1)S(1)}, bf16[1,1,1,1,1,16,4,128]{7,5,6,4,3,2,1,0:T(8,128)(2,1)S(1)}, u32[]{:S(2)}, u32[]{:S(2)}) collective-permute-start(bf16[1,1,1,1,1,16,4,128]{7,5,6,4,3,2,1,0:T(8,128)(2,1)S(1)} %get-tuple-element.26), channel_id=1, source_target_pairs={{0,4},{4,0},{8,12},{12,8},{16,20},{20,16},{24,28},{28,24},{1,5},{5... | collective-permute-start | bytes 49160 | tf_op jit(solution)/shard_map/ppermute | solution.py:53
  84.8 7.0 %collective-permute-start.18 = (bf16[1,1,1,1,2,16,4,128]{7,5,6,4,3,2,1,0:T(8,128)(2,1)S(1)}, bf16[1,1,1,1,2,16,4,128]{7,5,6,4,3,2,1,0:T(8,128)(2,1)S(1)}, u32[]{:S(2)}, u32[]{:S(2)}) collective-permute-start(bf16[1,1,1,1,2,16,4,128]{7,5,6,4,3,2,1,0:T(8,128)(2,1)S(1)} %maximum_select_fusion.18), channel_id=1, source_target_pairs={{0,8},{4,12},{8,0},{12,4},{16,24},{20,28},{24,16},{28,20},{1,9},{5... | collective-permute-start | bytes 98312 | tf_op jit(solution)/shard_map/ppermute | solution.py:53
  88.3 5.2 %collective-permute-start.23 = (bf16[1,2,1,1,1,16,4,128]{7,5,6,1,4,3,2,0:T(8,128)(2,1)S(1)}, bf16[1,2,1,1,1,16,4,128]{7,5,6,1,4,3,2,0:T(8,128)(2,1)S(1)}, u32[]{:S(2)}, u32[]{:S(2)}) collective-permute-start(bf16[1,2,1,1,1,16,4,128]{7,5,6,1,4,3,2,0:T(8,128)(2,1)S(1)} %fusion.22), channel_id=1, source_target_pairs={{0,16},{4,20},{8,24},{12,28},{16,0},{20,4},{24,8},{28,12},{1,17},{... | collective-permute-start | bytes 98312 | tf_op jit(solution)/shard_map/ppermute | solution.py:53
  89.8 4.1 %collective-permute-start.28 = (bf16[1,1,2,1,1,16,4,128]{7,5,6,4,3,2,1,0:T(8,128)(2,1)S(1)}, bf16[1,1,2,1,1,16,4,128]{7,5,6,4,3,2,1,0:T(8,128)(2,1)S(1)}, u32[]{:S(2)}, u32[]{:S(2)}) collective-permute-start(bf16[1,1,2,1,1,16,4,128]{7,5,6,4,3,2,1,0:T(8,128)(2,1)S(1)} %maximum_select_fusion.22), channel_id=1, source_target_pairs={{0,2},{1,3},{2,0},{3,1},{4,6},{5,7},{6,4},{7,5},{8,10},{9,11},{10,... | collective-permute-start | bytes 98312 | tf_op jit(solution)/shard_map/ppermute | solution.py:53
  91.8 4.3 %collective-permute-start.19 = (bf16[1,1,1,2,2,16,4,128]{7,5,6,4,3,2,1,0:T(8,128)(2,1)S(1)}, bf16[1,1,1,2,2,16,4,128]{7,5,6,4,3,2,1,0:T(8,128)(2,1)S(1)}, u32[]{:S(2)}, u32[]{:S(2)}) collective-permute-start(bf16[1,1,1,2,2,16,4,128]{7,5,6,4,3,2,1,0:T(8,128)(2,1)S(1)} %maximum_select_fusion.13), channel_id=1, source_target_pairs={{0,4},{4,0},{8,12},{12,8},{16,20},{20,16},{24,28},{28,24},{1,5},{5... | collective-permute-start | bytes 196616 | tf_op jit(solution)/shard_map/ppermute | solution.py:53
  93.5 4.4 %collective-permute-start.24 = (bf16[1,2,1,1,2,16,4,128]{7,5,6,4,3,2,1,0:T(8,128)(2,1)S(1)}, bf16[1,2,1,1,2,16,4,128]{7,5,6,4,3,2,1,0:T(8,128)(2,1)S(1)}, u32[]{:S(2)}, u32[]{:S(2)}) collective-permute-start(bf16[1,2,1,1,2,16,4,128]{7,5,6,4,3,2,1,0:T(8,128)(2,1)S(1)} %copy.54), channel_id=1, source_target_pairs={{0,8},{4,12},{8,0},{12,4},{16,24},{20,28},{24,16},{28,20},{1,9},{5... | collective-permute-start | bytes 196616 | tf_op jit(solution)/shard_map/ppermute | solution.py:53
  94.0 5.2 %collective-permute-start.29 = (bf16[1,2,2,1,1,16,4,128]{7,5,6,4,3,2,1,0:T(8,128)(2,1)S(1)}, bf16[1,2,2,1,1,16,4,128]{7,5,6,4,3,2,1,0:T(8,128)(2,1)S(1)}, u32[]{:S(2)}, u32[]{:S(2)}) collective-permute-start(bf16[1,2,2,1,1,16,4,128]{7,5,6,4,3,2,1,0:T(8,128)(2,1)S(1)} %fusion.21), channel_id=1, source_target_pairs={{0,16},{4,20},{8,24},{12,28},{16,0},{20,4},{24,8},{28,12},{1,17},{... | collective-permute-start | bytes 196616 | tf_op jit(solution)/shard_map/ppermute | solution.py:53
  96.2 5.0 %collective-permute-start.20 = (bf16[1,1,2,2,2,16,4,128]{7,5,6,4,3,2,1,0:T(8,128)(2,1)S(1)}, bf16[1,1,2,2,2,16,4,128]{7,5,6,4,3,2,1,0:T(8,128)(2,1)S(1)}, u32[]{:S(2)}, u32[]{:S(2)}) collective-permute-start(bf16[1,1,2,2,2,16,4,128]{7,5,6,4,3,2,1,0:T(8,128)(2,1)S(1)} %maximum_select_fusion.7), channel_id=1, source_target_pairs={{0,2},{1,3},{2,0},{3,1},{4,6},{5,7},{6,4},{7,5},{8,10},{9,11},{10,... | collective-permute-start | bytes 393224 | tf_op jit(solution)/shard_map/ppermute | solution.py:53
  97.9 5.0 %collective-permute-start.25 = (bf16[1,2,1,2,2,16,4,128]{7,5,6,4,3,2,1,0:T(8,128)(2,1)S(1)}, bf16[1,2,1,2,2,16,4,128]{7,5,6,4,3,2,1,0:T(8,128)(2,1)S(1)}, u32[]{:S(2)}, u32[]{:S(2)}) collective-permute-start(bf16[1,2,1,2,2,16,4,128]{7,5,6,4,3,2,1,0:T(8,128)(2,1)S(1)} %maximum_select_fusion.9), channel_id=1, source_target_pairs={{0,4},{4,0},{8,12},{12,8},{16,20},{20,16},{24,28},{28,24},{1,5},{5... | collective-permute-start | bytes 393224 | tf_op jit(solution)/shard_map/ppermute | solution.py:53
  99.3 5.0 %collective-permute-start.30 = (bf16[1,2,2,1,2,16,4,128]{7,5,6,4,3,2,1,0:T(8,128)(2,1)S(1)}, bf16[1,2,2,1,2,16,4,128]{7,5,6,4,3,2,1,0:T(8,128)(2,1)S(1)}, u32[]{:S(2)}, u32[]{:S(2)}) collective-permute-start(bf16[1,2,2,1,2,16,4,128]{7,5,6,4,3,2,1,0:T(8,128)(2,1)S(1)} %maximum_select_fusion.11), channel_id=1, source_target_pairs={{0,8},{4,12},{8,0},{12,4},{16,24},{20,28},{24,16},{28,20},{1,9},{5... | collective-permute-start | bytes 393224 | tf_op jit(solution)/shard_map/ppermute | solution.py:53
  101.2 10.4 %collective-permute-start.21 = (bf16[1,2,2,2,2,16,4,128]{7,5,6,4,3,2,1,0:T(8,128)(2,1)S(1)}, bf16[1,2,2,2,2,16,4,128]{7,5,6,4,3,2,1,0:T(8,128)(2,1)}, u32[]{:S(2)}, u32[]{:S(2)}) collective-permute-start(bf16[1,2,2,2,2,16,4,128]{7,5,6,4,3,2,1,0:T(8,128)(2,1)S(1)} %maximum_select_fusion.3), channel_id=1, source_target_pairs={{0,1},{1,0},{2,3},{3,2},{4,5},{5,4},{6,7},{7,6},{8,9},{9,8},{10,11... | collective-permute-start | bytes 786440 | tf_op jit(solution)/shard_map/ppermute | solution.py:53
  103.6 9.2 %collective-permute-start.26 = (bf16[1,2,2,2,2,16,4,128]{7,5,6,4,3,2,1,0:T(8,128)(2,1)}, bf16[1,2,2,2,2,16,4,128]{7,5,6,4,3,2,1,0:T(8,128)(2,1)}, u32[]{:S(2)}, u32[]{:S(2)}) collective-permute-start(bf16[1,2,2,2,2,16,4,128]{7,5,6,4,3,2,1,0:T(8,128)(2,1)} %maximum_select_fusion.4), channel_id=1, source_target_pairs={{0,1},{1,0},{2,3},{3,2},{4,5},{5,4},{6,7},{7,6},{8,9},{9,8},{10,11... | collective-permute-start | bytes 786440 | tf_op jit(solution)/shard_map/ppermute | solution.py:53
  105.0 9.2 %collective-permute-start.31 = (bf16[1,2,2,2,2,16,4,128]{7,5,6,4,3,2,1,0:T(8,128)(2,1)}, bf16[1,2,2,2,2,16,4,128]{7,5,6,4,3,2,1,0:T(8,128)(2,1)}, u32[]{:S(2)}, u32[]{:S(2)}) collective-permute-start(bf16[1,2,2,2,2,16,4,128]{7,5,6,4,3,2,1,0:T(8,128)(2,1)} %maximum_select_fusion.5), channel_id=1, source_target_pairs={{0,1},{1,0},{2,3},{3,2},{4,5},{5,4},{6,7},{7,6},{8,9},{9,8},{10,11... | collective-permute-start | bytes 786440 | tf_op jit(solution)/shard_map/ppermute | solution.py:53
  (9 other events, 158.7 us)
Sparse Core Ops, SparseCore 0:
  26.0 23.2 all-gather.2

commit v3 on v2

--- a/solution.py
+++ b/solution.py
@@ -64,8 +64,11 @@
 
 
 def per_device(residual, margin, inverse_blocks, interface, basis, coarse_pattern, coarse_inverse):
-    pattern_all = lax.all_gather(coarse_pattern, "coarse", axis=0, tiled=True)
-    inverse_all = lax.all_gather(coarse_inverse, "coarse", axis=0, tiled=True)
+    rows, cols = coarse_inverse.shape[-2:]
+    tags = jnp.broadcast_to(coarse_pattern.astype(jnp.bfloat16)[:, :, None, None], coarse_pattern.shape + (8, cols))
+    packed = lax.all_gather(jnp.concatenate([coarse_inverse, tags], axis=2), "coarse", axis=0, tiled=True)
+    inverse_all = packed[:, :, :rows, :]
+    pattern_all = packed[:, :, rows, 0].astype(jnp.int32)
     extended = with_halo(residual, ((("sub", "coarse"), 0),), 1)
     rhs = residual.shape[1]
     width = basis.shape[-1]
@@ -84,8 +87,12 @@
     orders = stream_orders(nb, streams)
     split = restricted.reshape((2,) * nb + (inner, total_blocks, width))
     parts = [lax.slice_in_dim(split, s * per, (s + 1) * per, axis=nb + 1) for s in range(streams)]
+    picked = jnp.take(extended, margin, axis=0)
+    local = jnp.einsum("jerb,jebc->jrc", picked, inverse_blocks, preferred_element_type=jnp.float32)
     for step in range(nb):
         parts = [halve(x, orders[s][step], *bits[orders[s][step]]) for s, x in enumerate(parts)]
+        if step == 0:
+            local, parts = lax.optimization_barrier((local, parts))
     mine = jnp.concatenate(parts, axis=nb + 1).reshape(inner, total_blocks, width)
     coarse_in = mine.astype(jnp.bfloat16)
     chosen = jnp.take(coarse_in, pattern_all, axis=1)
@@ -98,8 +105,6 @@
         outs = [double(y, orders[s][step], *bits[orders[s][step]]) for s, y in enumerate(outs)]
     coarse_out = jnp.concatenate(outs, axis=nb + 1).reshape(rhs, total_blocks, width)
 
-    picked = jnp.take(extended, margin, axis=0)
-    local = jnp.einsum("jerb,jebc->jrc", picked, inverse_blocks, preferred_element_type=jnp.float32)
     lifted = jnp.take(coarse_out, interface, axis=1)
     spread = jnp.einsum("rjqc,jqbc->jrb", lifted, basis, preferred_element_type=jnp.float32)
     return (local + spread).astype(jnp.bfloat16)

time: 133 us -> 130 us (0.977)
  blocking collectives: 11.9 us -> 0 us
  waiting for transfers between devices: 12.7 us -> 20 us
  local copies, waits for them, and re-layouts: 20 us -> 21.9 us
    all_gather x1 -> x0, blocking collectives: 11.9 us -> none  [per_device(): pattern_all = lax.all_gather(coarse_pattern, 'coarse', axis=0, tiled=True)]
    ppermute x15, waiting for transfers between devices: 4.79 us -> 8.78 us  [double(): recv = lax.ppermute(y, axis, pairs(axis, mask))]
    select_n x15, other arithmetic: 5.32 us -> 1.46 us  [double(): jnp.where(v == 0, jnp.concatenate([y, recv], axis=dim), jnp.concatenate([...]
    ppermute x1, waiting for transfers between devices: 0.01 us -> 3.45 us  [with_halo(): lax.ppermute(head, axis, [((i + 1) % count, i) for i in range(ends)])]
    ppermute x15, starting transfers between devices: 23 us -> 26 us  [halve(): return keep + lax.ppermute(send, axis, pairs(axis, mask))]
    ppermute x15, starting transfers between devices: 18.2 us -> 16.2 us  [double(): recv = lax.ppermute(y, axis, pairs(axis, mask))]
    unnamed x21 -> x28, local copies, waits for them, and re-layouts: 2.68 us -> 3.55 us
  transfers between devices with their start and end apart: 33 -> 33, of which waited for: 12 -> 15; matrix products, arithmetic and copies ran while one was open for 17% -> 17% of each run, Pallas kernels for 0% -> 0%
where the time goes in v3:
time: 130 us; the launch traced here: 129 us
  starting transfers between devices  45.4 us (35%)
  local copies, waits for them, and re-layouts  21.9 us (17%)
  waiting for transfers between devices  20 us (15%)
  matrix products  15.9 us (12%)
  between operations  14 us (11%)
  other arithmetic  12 us (9%)
    ppermute x15, starting transfers between devices, halve(): return keep + lax.ppermute(send, axis, pairs(axis, mask))  26 us
    ppermute x15, starting transfers between devices, double(): recv = lax.ppermute(y, axis, pairs(axis, mask))  16.2 us
    ppermute x15, waiting for transfers between devices, double(): recv = lax.ppermute(y, axis, pairs(axis, mask))  8.78 us
    ppermute x15, waiting for transfers between devices, halve(): return keep + lax.ppermute(send, axis, pairs(axis, mask))  7.73 us
    dot_general x1, matrix products, per_device(): jnp.einsum('jerb,jebc->jrc', picked, inverse_blocks, preferred_element_ty...  5.12 us
    add x12, other arithmetic, halve(): return keep + lax.ppermute(send, axis, pairs(axis, mask))  4.61 us
    gather x1, local copies, waits for them, and re-layouts, per_device(): picked = jnp.take(extended, margin, axis=0)  4.21 us
    dot_general x1, matrix products, per_device(): jnp.einsum('jqn,jqrc->rnc', onehot, terms, precision=lax.Precision.HIGHEST)  3.93 us
  transfers between devices with their start and end apart: 33, of which 15 were waited for; matrix products, arithmetic and copies ran while one was open for 17% of the time, Pallas kernels for 0%

profile of v3, /device:TPU:0, one launch (start us, length us, event | category | flops | bytes accessed | tf_op | source)
XLA Modules:
  0.0 129.2 jit_solution(12197924771348945667)
XLA Ops:
  6.5 3.4 %convolution_bitcast_fusion = f32[4,2,512,128]{2,3,1,0:T(8,128)} fusion(bf16[4,2,256,128]{3,2,1,0:T(8,128)(2,1)} %param.11, bf16[4,512,256]{2,1,0:T(8,128)(2,1)} %param.7), kind=kOutput, calls=%fused_computation.10 | convolution fusion | flops 268435456 | bytes 3670016 | tf_op jit(solution)/shard_map/jrb,jqbc->jqrc/dot_general | solution.py:76
  9.9 2.9 %copy.69 = f32[4,2,512,128]{3,0,1,2:T(4,128)} copy(f32[4,2,512,128]{2,3,1,0:T(8,128)} %convolution_bitcast_fusion) | data formatting | bytes 4194304 | tf_op jit(solution)/shard_map/jrb,jqbc->jqrc/transpose | solution.py:76
  12.9 3.9 %fusion.42 = f32[512,128,12,1]{1,2,3,0:T(8,128)S(1)} fusion(f32[4,2,512,128]{3,0,1,2:T(4,128)} %copy.69, s32[4,2]{0,1:T(2,128)S(1)} %copy-done.10), kind=kOutput, calls=%fused_computation.109 | convolution fusion | flops 75497568 | bytes 5242912 | tf_op jit(solution)/shard_map/jqn,jqrc->rnc/dot_general | solution.py:79
  16.8 2.2 %fusion.54 = (f32[2,2,2,2,2,16,4,128]{7,6,5,4,3,2,1,0:T(4,128)S(1)}, f32[2,2,2,2,2,16,4,128]{7,6,5,4,3,2,1,0:T(4,128)}, f32[2,2,2,2,2,16,4,128]{7,6,5,4,3,2,1,0:T(4,128)}) fusion(f32[2,2,2,2,2,16,12,128]{7,6,5,4,3,2,1,0:T(8,128)S(1)} %bitcast.124), kind=kLoop, calls=%fused_computation.129 | loop fusion | bytes 6291456 | tf_op jit(solution)/shard_map/slice | solution.py:89
  19.0 2.4 %constant_dynamic-slice_fusion.13 = (f32[1,2,2,2,2,16,4,128]{7,6,5,4,3,2,1,0:T(4,128)}, f32[1,2,2,2,2,16,4,128]{7,6,5,4,3,2,1,0:T(4,128)S(1)}, f32[1,2,2,2,2,16,...) fusion(f32[2,2,2,2,2,16,4,128]{7,6,5,4,3,2,1,0:T(4,128)S(1)} %get-tuple-element.13, s32[]{:T(128)S(6)} %select_n.673, ...), kind=kLoop, calls=%fused_computation.92 | loop fusion | bytes 4194312 | tf_op jit(solution)/shard_map/jit(dynamic_index_in_dim)/dynamic_slice | solution.py:46
  26.7 2.0 %collective-permute-start = (bf16[1,512,256]{2,1,0:T(8,128)(2,1)}, bf16[1,512,256]{2,1,0:T(8,128)(2,1)S(1)}, u32[]{:S(2)}, u32[]{:S(2)}) collective-permute-start(bf16[1,512,256]{2,1,0:T(8,128)(2,1)} %get-tuple-element.22), channel_id=1, source_target_pairs={{0,1},{1,2},{2,3},{3,4},{4,5},{5,6},{6,7},{7,8},{8,9},{9,10},{10,1... | collective-permute-start | bytes 786440 | tf_op jit(solution)/shard_map/ppermute | solution.py:15
  31.1 3.4 %collective-permute-done.1 = bf16[1,512,256]{2,1,0:T(8,128)(2,1)} collective-permute-done((bf16[1,512,256]{2,1,0:T(8,128)(2,1)}, bf16[1,512,256]{2,1,0:T(8,128)(2,1)}, u32[]{:S(2)}, u32[]{:S(2)}) %collective-permute-start.1) | collective-permute-done | bytes 262176 | tf_op jit(solution)/shard_map/ppermute | solution.py:17
  34.6 2.3 %pad_maximum_fusion = bf16[6,512,256]{2,1,0:T(8,128)(2,1)} fusion(bf16[1,512,256]{2,1,0:T(8,128)(2,1)} %collective-permute-done.1, bf16[4,512,256]{2,1,0:T(8,128)(2,1)S(1)} %copy-done.1, bf16[1,512,256]{2,1,0:T(8,128)(2,1)S(1)} %collective-permute-done), kind=kLoop, calls=%fused_computation.13 | loop fusion | flops 1572864 | bytes 3145728 | tf_op jit(solution)/shard_map/concatenate | solution.py:13
  36.9 4.2 %gather_fusion = bf16[16,512,256]{2,1,0:T(8,128)(2,1)} fusion(bf16[6,512,256]{2,1,0:T(8,128)(2,1)} %pad_maximum_fusion, s32[1024]{0:T(1024)S(1)} %pad_clamp_fusion.2), kind=kCustom, calls=%fused_computation | custom fusion | bytes 8388672 | tf_op jit(solution)/shard_map/jit(_take)/gather | solution.py:90
  41.1 5.1 %fusion.5 = f32[4,512,256]{2,1,0:T(8,128)} fusion(bf16[4,4,256,256]{3,2,1,0:T(8,128)(2,1)S(1)} %copy-done, bf16[4,4,512,256]{3,2,1,0:T(8,128)(2,1)} %bitcast.125, pred[4,4]{1,0:T(4,128)(4,1)S(1)} %compare_and_fusion.2), kind=kOutput, calls=%fused_computation.9 | convolution fusion | flops 1075838976 | bytes 8388624 | tf_op jit(solution)/shard_map/jerb,jebc->jrc/dot_general | solution.py:91
  50.5 4.4 %collective-permute-start.5 = (f32[1,1,2,2,2,16,4,128]{7,5,6,4,3,2,1,0:T(8,128)S(1)}, f32[1,1,2,2,2,16,4,128]{7,5,6,4,3,2,1,0:T(8,128)}, u32[]{:S(2)}, u32[]{:S(2)}) collective-permute-start(f32[1,1,2,2,2,16,4,128]{7,5,6,4,3,2,1,0:T(8,128)S(1)} %constant_dynamic-slice_fusion.11), channel_id=1, source_target_pairs={{0,2},{1,3},{2,0},{3,1},{4,6},{5,7},{6,4},{7,5},{8,10},{9,11},{10,... | collective-permute-start | bytes 786440 | tf_op jit(solution)/shard_map/ppermute | solution.py:48
  54.9 1.5 %collective-permute-start.9 = (f32[1,2,1,2,2,16,4,128]{7,5,6,4,3,2,1,0:T(8,128)S(1)}, f32[1,2,1,2,2,16,4,128]{7,5,6,4,3,2,1,0:T(8,128)S(1)}, u32[]{:S(2)}, u32[]{:S(2)}) collective-permute-start(f32[1,2,1,2,2,16,4,128]{7,5,6,4,3,2,1,0:T(8,128)S(1)} %constant_dynamic-slice_fusion.7), channel_id=1, source_target_pairs={{0,4},{4,0},{8,12},{12,8},{16,20},{20,16},{24,28},{28,24},{1,5},{5... | collective-permute-start | bytes 786440 | tf_op jit(solution)/shard_map/ppermute | solution.py:48
  56.4 1.6 %collective-permute-start.13 = (f32[1,2,2,1,2,16,4,128]{7,5,6,4,3,2,1,0:T(8,128)S(1)}, f32[1,2,2,1,2,16,4,128]{7,5,6,4,3,2,1,0:T(8,128)S(1)}, u32[]{:S(2)}, u32[]{:S(2)}) collective-permute-start(f32[1,2,2,1,2,16,4,128]{7,5,6,4,3,2,1,0:T(8,128)S(1)} %constant_dynamic-slice_fusion.3), channel_id=1, source_target_pairs={{0,8},{4,12},{8,0},{12,4},{16,24},{20,28},{24,16},{28,20},{1,9},{5... | collective-permute-start | bytes 786440 | tf_op jit(solution)/shard_map/ppermute | solution.py:48
  58.1 2.0 %collective-permute-done.5 = f32[1,1,2,2,2,16,4,128]{7,5,6,4,3,2,1,0:T(8,128)} collective-permute-done((f32[1,1,2,2,2,16,4,128]{7,5,6,4,3,2,1,0:T(8,128)S(1)}, f32[1,1,2,2,2,16,4,128]{7,5,6,4,3,2,1,0:T(8,128)}, u32[]{:S(2)}, u32[]{:S(2)}) %collective-permute-start.5) | collective-permute-done | bytes 262176 | tf_op jit(solution)/shard_map/ppermute | solution.py:48
  61.2 3.3 %collective-permute-start.6 = (f32[1,1,1,2,2,16,4,128]{7,5,6,4,3,2,1,0:T(8,128)S(1)}, f32[1,1,1,2,2,16,4,128]{7,5,6,4,3,2,1,0:T(8,128)S(1)}, u32[]{:S(2)}, u32[]{:S(2)}) collective-permute-start(f32[1,1,1,2,2,16,4,128]{7,5,6,4,3,2,1,0:T(8,128)S(1)} %constant_dynamic-slice_fusion.10), channel_id=1, source_target_pairs={{0,4},{4,0},{8,12},{12,8},{16,20},{20,16},{24,28},{28,24},{1,5},{5... | collective-permute-start | bytes 393224 | tf_op jit(solution)/shard_map/ppermute | solution.py:48
  64.6 2.7 %collective-permute-start.10 = (f32[1,2,1,1,2,16,4,128]{7,5,6,4,3,2,1,0:T(8,128)S(1)}, f32[1,2,1,1,2,16,4,128]{7,5,6,4,3,2,1,0:T(8,128)S(1)}, u32[]{:S(2)}, u32[]{:S(2)}) collective-permute-start(f32[1,2,1,1,2,16,4,128]{7,5,6,4,3,2,1,0:T(8,128)S(1)} %constant_dynamic-slice_fusion.6), channel_id=1, source_target_pairs={{0,8},{4,12},{8,0},{12,4},{16,24},{20,28},{24,16},{28,20},{1,9},{5... | collective-permute-start | bytes 393224 | tf_op jit(solution)/shard_map/ppermute | solution.py:48
  67.4 3.3 %collective-permute-start.14 = (f32[1,2,2,1,1,16,4,128]{7,5,6,4,3,2,1,0:T(8,128)S(1)}, f32[1,2,2,1,1,16,4,128]{7,5,6,4,3,2,1,0:T(8,128)S(1)}, u32[]{:S(2)}, u32[]{:S(2)}) collective-permute-start(f32[1,2,2,1,1,16,4,128]{7,5,6,4,3,2,1,0:T(8,128)S(1)} %constant_dynamic-slice_fusion.2), channel_id=1, source_target_pairs={{0,16},{4,20},{8,24},{12,28},{16,0},{20,4},{24,8},{28,12},{1,17},{... | collective-permute-start | bytes 393224 | tf_op jit(solution)/shard_map/ppermute | solution.py:48
  70.7 1.9 %collective-permute-start.7 = (f32[1,1,1,1,2,16,4,128]{7,5,6,4,3,2,1,0:T(8,128)S(1)}, f32[1,1,1,1,2,16,4,128]{7,5,6,4,3,2,1,0:T(8,128)S(1)}, u32[]{:S(2)}, u32[]{:S(2)}) collective-permute-start(f32[1,1,1,1,2,16,4,128]{7,5,6,4,3,2,1,0:T(8,128)S(1)} %constant_dynamic-slice_fusion.9), channel_id=1, source_target_pairs={{0,8},{4,12},{8,0},{12,4},{16,24},{20,28},{24,16},{28,20},{1,9},{5... | collective-permute-start | bytes 196616 | tf_op jit(solution)/shard_map/ppermute | solution.py:48
  77.1 2.1 %collective-permute-start.8 = (f32[1,1,1,1,1,16,4,128]{7,5,6,4,3,2,1,0:T(8,128)S(1)}, f32[1,1,1,1,1,16,4,128]{7,5,6,4,3,2,1,0:T(8,128)S(1)}, u32[]{:S(2)}, u32[]{:S(2)}) collective-permute-start(f32[1,1,1,1,1,16,4,128]{7,5,6,4,3,2,1,0:T(8,128)S(1)} %constant_dynamic-slice_fusion.8), channel_id=1, source_target_pairs={{0,16},{4,20},{8,24},{12,28},{16,0},{20,4},{24,8},{28,12},{1,17},{... | collective-permute-start | bytes 98312 | tf_op jit(solution)/shard_map/ppermute | solution.py:48
  79.2 1.4 %collective-permute-done.11 = f32[1,2,1,1,1,16,4,128]{7,5,6,4,3,2,1,0:T(8,128)S(1)} collective-permute-done((f32[1,2,1,1,1,16,4,128]{7,5,6,4,3,2,1,0:T(8,128)S(1)}, f32[1,2,1,1,1,16,4,128]{7,5,6,4,3,2,1,0:T(8,128)S(1)}, u32[]{:S(2)}, u32[]{:S(2)}) %collective-permute-start.11) | collective-permute-done | bytes 65568 | tf_op jit(solution)/shard_map/ppermute | solution.py:48
  80.8 2.0 %collective-permute-start.16 = (f32[1,1,1,1,1,16,4,128]{7,5,6,4,3,2,1,0:T(8,128)S(1)}, f32[1,1,1,1,1,16,4,128]{7,5,6,4,3,2,1,0:T(8,128)S(1)}, u32[]{:S(2)}, u32[]{:S(2)}) collective-permute-start(f32[1,1,1,1,1,16,4,128]{7,5,6,4,3,2,1,0:T(8,128)S(1)} %constant_dynamic-slice_fusion), channel_id=1, source_target_pairs={{0,4},{4,0},{8,12},{12,8},{16,20},{20,16},{24,28},{28,24},{1,5},{5... | collective-permute-start | bytes 98312 | tf_op jit(solution)/shard_map/ppermute | solution.py:48
  82.9 1.7 %collective-permute-done.12 = f32[1,1,1,1,1,16,4,128]{7,5,6,4,3,2,1,0:T(8,128)S(1)} collective-permute-done((f32[1,1,1,1,1,16,4,128]{7,5,6,4,3,2,1,0:T(8,128)S(1)}, f32[1,1,1,1,1,16,4,128]{7,5,6,4,3,2,1,0:T(8,128)S(1)}, u32[]{:S(2)}, u32[]{:S(2)}) %collective-permute-start.12) | collective-permute-done | bytes 32800 | tf_op jit(solution)/shard_map/ppermute | solution.py:48
  86.8 1.8 %fusion.16 = bf16[1,1,1,1,1,16,12,128]{7,5,6,4,3,2,1,0:T(8,128)(2,1)S(1)} fusion(bf16[12,4,136,128]{3,2,1,0:T(8,128)(2,1)} %all-gather.2.cloned.1.call-done, bf16[12,4,16,128]{3,2,1,0:T(8,128)(2,1)S(1)} %bitcast.136, pred[12,4]{1,0:T(8,128)(4,1)S(1)} %copy.75), kind=kOutput, calls=%fused_computation.17 | convolution fusion | flops 25288704 | bytes 1818672 | tf_op jit(solution)/shard_map/rnec,necd->rnd/dot_general | solution.py:99
  88.6 1.5 %collective-permute-start.17 = (bf16[1,1,1,1,1,16,4,128]{7,5,6,4,3,2,1,0:T(8,128)(2,1)S(1)}, bf16[1,1,1,1,1,16,4,128]{7,5,6,4,3,2,1,0:T(8,128)(2,1)S(1)}, u32[]{:S(2)}, u32[]{:S(2)}) collective-permute-start(bf16[1,1,1,1,1,16,4,128]{7,5,6,4,3,2,1,0:T(8,128)(2,1)S(1)} %get-tuple-element.36), channel_id=1, source_target_pairs={{0,16},{4,20},{8,24},{12,28},{16,0},{20,4},{24,8},{28,12},{1,17},{... | collective-permute-start | bytes 49160 | tf_op jit(solution)/shard_map/ppermute | solution.py:53
  93.3 2.4 %collective-permute-start.18 = (bf16[1,1,1,1,2,16,4,128]{7,5,6,4,3,2,1,0:T(8,128)(2,1)S(1)}, bf16[1,1,1,1,2,16,4,128]{7,5,6,4,3,2,1,0:T(8,128)(2,1)S(1)}, u32[]{:S(2)}, u32[]{:S(2)}) collective-permute-start(bf16[1,1,1,1,2,16,4,128]{7,5,6,4,3,2,1,0:T(8,128)(2,1)S(1)} %maximum_select_fusion.18), channel_id=1, source_target_pairs={{0,8},{4,12},{8,0},{12,4},{16,24},{20,28},{24,16},{28,20},{1,9},{5... | collective-permute-start | bytes 98312 | tf_op jit(solution)/shard_map/ppermute | solution.py:53
  95.7 2.1 %collective-permute-start.23 = (bf16[1,2,1,1,1,16,4,128]{7,5,6,1,4,3,2,0:T(8,128)(2,1)S(1)}, bf16[1,2,1,1,1,16,4,128]{7,5,6,1,4,3,2,0:T(8,128)(2,1)S(1)}, u32[]{:S(2)}, u32[]{:S(2)}) collective-permute-start(bf16[1,2,1,1,1,16,4,128]{7,5,6,1,4,3,2,0:T(8,128)(2,1)S(1)} %fusion.32), channel_id=1, source_target_pairs={{0,16},{4,20},{8,24},{12,28},{16,0},{20,4},{24,8},{28,12},{1,17},{... | collective-permute-start | bytes 98312 | tf_op jit(solution)/shard_map/ppermute | solution.py:53
  99.1 1.5 %collective-permute-start.19 = (bf16[1,1,1,2,2,16,4,128]{7,5,6,4,3,2,1,0:T(8,128)(2,1)S(1)}, bf16[1,1,1,2,2,16,4,128]{7,5,6,4,3,2,1,0:T(8,128)(2,1)S(1)}, u32[]{:S(2)}, u32[]{:S(2)}) collective-permute-start(bf16[1,1,1,2,2,16,4,128]{7,5,6,4,3,2,1,0:T(8,128)(2,1)S(1)} %maximum_select_fusion.13), channel_id=1, source_target_pairs={{0,4},{4,0},{8,12},{12,8},{16,20},{20,16},{24,28},{28,24},{1,5},{5... | collective-permute-start | bytes 196616 | tf_op jit(solution)/shard_map/ppermute | solution.py:53
  101.9 1.6 %collective-permute-start.29 = (bf16[1,2,2,1,1,16,4,128]{7,5,6,4,3,2,1,0:T(8,128)(2,1)S(1)}, bf16[1,2,2,1,1,16,4,128]{7,5,6,4,3,2,1,0:T(8,128)(2,1)S(1)}, u32[]{:S(2)}, u32[]{:S(2)}) collective-permute-start(bf16[1,2,2,1,1,16,4,128]{7,5,6,4,3,2,1,0:T(8,128)(2,1)S(1)} %fusion.31), channel_id=1, source_target_pairs={{0,16},{4,20},{8,24},{12,28},{16,0},{20,4},{24,8},{28,12},{1,17},{... | collective-permute-start | bytes 196616 | tf_op jit(solution)/shard_map/ppermute | solution.py:53
  108.8 1.6 %collective-permute-done.25 = bf16[1,2,1,2,2,16,4,128]{7,5,6,4,3,2,1,0:T(8,128)(2,1)S(1)} collective-permute-done((bf16[1,2,1,2,2,16,4,128]{7,5,6,4,3,2,1,0:T(8,128)(2,1)S(1)}, bf16[1,2,1,2,2,16,4,128]{7,5,6,4,3,2,1,0:T(8,128)(2,1)S(1)}, u32[]{:S(2)}, u32[]{:S(2)}) %collective-permute-start.25) | collective-permute-done | bytes 131104 | tf_op jit(solution)/shard_map/ppermute | solution.py:53
  110.4 2.5 %collective-permute-done.30 = bf16[1,2,2,1,2,16,4,128]{7,5,6,4,3,2,1,0:T(8,128)(2,1)S(1)} collective-permute-done((bf16[1,2,2,1,2,16,4,128]{7,5,6,4,3,2,1,0:T(8,128)(2,1)S(1)}, bf16[1,2,2,1,2,16,4,128]{7,5,6,4,3,2,1,0:T(8,128)(2,1)S(1)}, u32[]{:S(2)}, u32[]{:S(2)}) %collective-permute-start.30) | collective-permute-done | bytes 131104 | tf_op jit(solution)/shard_map/ppermute | solution.py:53
  117.2 2.2 %gather_fusion.2 = bf16[8,512,128]{2,1,0:T(8,128)(2,1)S(1)} fusion(bf16[512,12,128]{2,0,1:T(8,128)(2,1)} %pad_maximum_fusion.1, s32[1024]{0:T(1024)S(1)} %pad_clamp_fusion), kind=kCustom, calls=%fused_computation.2 | custom fusion | bytes 2097184 | tf_op jit(solution)/shard_map/jit(_take)/gather | solution.py:108
  119.4 1.7 %fusion.20 = f32[4,512,256,1]{2,1,3,0:T(8,128)S(1)} fusion(bf16[4,2,256,128]{3,2,1,0:T(8,128)(2,1)} %param.11, bf16[4,2,512,128]{3,2,1,0:T(8,128)(2,1)S(1)} %bitcast.126, pred[4,2]{1,0:T(4,128)(4,1)S(1)} %copy.73), kind=kOutput, calls=%fused_computation.19 | convolution fusion | flops 268959744 | bytes 3670024 | tf_op jit(solution)/shard_map/rjqc,jqbc->jrb/dot_general | solution.py:109
  (156 shorter events, 36.4 us)
Async XLA Ops:
  6.5 78.3 %all-gather.2.cloned.1.call-start = ((), (), s32[]{:S(2)}) async-start(), calls=%async_computation | async-start | bytes 2088960 | tf_op jit(solution)/shard_map/all_gather | solution.py:69
  22.3 23.9 %collective-permute-start.4 = (f32[1,2,2,2,2,16,4,128]{7,5,6,4,3,2,1,0:T(8,128)}, f32[1,2,2,2,2,16,4,128]{7,5,6,4,3,2,1,0:T(8,128)}, u32[]{:S(2)}, u32[]{:S(2)}) collective-permute-start(f32[1,2,2,2,2,16,4,128]{7,5,6,4,3,2,1,0:T(8,128)} %copy.104), channel_id=1, source_target_pairs={{0,1},{1,0},{2,3},{3,2},{4,5},{5,4},{6,7},{7,6},{8,9},{9,8},{10,11... | collective-permute-start | bytes 1572872 | tf_op jit(solution)/shard_map/ppermute | solution.py:48
  23.6 23.8 %collective-permute-start.3 = (f32[1,2,2,2,2,16,4,128]{7,5,6,4,3,2,1,0:T(8,128)}, f32[1,2,2,2,2,16,4,128]{7,5,6,4,3,2,1,0:T(8,128)}, u32[]{:S(2)}, u32[]{:S(2)}) collective-permute-start(f32[1,2,2,2,2,16,4,128]{7,5,6,4,3,2,1,0:T(8,128)} %copy.101), channel_id=1, source_target_pairs={{0,1},{1,0},{2,3},{3,2},{4,5},{5,4},{6,7},{7,6},{8,9},{9,8},{10,11... | collective-permute-start | bytes 1572872 | tf_op jit(solution)/shard_map/ppermute | solution.py:48
  25.4 23.1 %collective-permute-start.2 = (f32[1,2,2,2,2,16,4,128]{7,5,6,4,3,2,1,0:T(8,128)}, f32[1,2,2,2,2,16,4,128]{7,5,6,4,3,2,1,0:T(8,128)}, u32[]{:S(2)}, u32[]{:S(2)}) collective-permute-start(f32[1,2,2,2,2,16,4,128]{7,5,6,4,3,2,1,0:T(8,128)} %copy.98), channel_id=1, source_target_pairs={{0,1},{1,0},{2,3},{3,2},{4,5},{5,4},{6,7},{7,6},{8,9},{9,8},{10,11... | collective-permute-start | bytes 1572872 | tf_op jit(solution)/shard_map/ppermute | solution.py:48
  26.7 4.4 %collective-permute-start = (bf16[1,512,256]{2,1,0:T(8,128)(2,1)}, bf16[1,512,256]{2,1,0:T(8,128)(2,1)S(1)}, u32[]{:S(2)}, u32[]{:S(2)}) collective-permute-start(bf16[1,512,256]{2,1,0:T(8,128)(2,1)} %get-tuple-element.22), channel_id=1, source_target_pairs={{0,1},{1,2},{2,3},{3,4},{4,5},{5,6},{6,7},{7,8},{8,9},{9,10},{10,1... | collective-permute-start | bytes 786440 | tf_op jit(solution)/shard_map/ppermute | solution.py:15
  28.7 5.9 %collective-permute-start.1 = (bf16[1,512,256]{2,1,0:T(8,128)(2,1)}, bf16[1,512,256]{2,1,0:T(8,128)(2,1)}, u32[]{:S(2)}, u32[]{:S(2)}) collective-permute-start(bf16[1,512,256]{2,1,0:T(8,128)(2,1)} %get-tuple-element.23), channel_id=1, source_target_pairs={{1,0},{2,1},{3,2},{4,3},{5,4},{6,5},{7,6},{8,7},{9,8},{10,9},{11,1... | collective-permute-start | bytes 786440 | tf_op jit(solution)/shard_map/ppermute | solution.py:17
  50.5 9.6 %collective-permute-start.5 = (f32[1,1,2,2,2,16,4,128]{7,5,6,4,3,2,1,0:T(8,128)S(1)}, f32[1,1,2,2,2,16,4,128]{7,5,6,4,3,2,1,0:T(8,128)}, u32[]{:S(2)}, u32[]{:S(2)}) collective-permute-start(f32[1,1,2,2,2,16,4,128]{7,5,6,4,3,2,1,0:T(8,128)S(1)} %constant_dynamic-slice_fusion.11), channel_id=1, source_target_pairs={{0,2},{1,3},{2,0},{3,1},{4,6},{5,7},{6,4},{7,5},{8,10},{9,11},{10,... | collective-permute-start | bytes 786440 | tf_op jit(solution)/shard_map/ppermute | solution.py:48
  54.9 9.6 %collective-permute-start.9 = (f32[1,2,1,2,2,16,4,128]{7,5,6,4,3,2,1,0:T(8,128)S(1)}, f32[1,2,1,2,2,16,4,128]{7,5,6,4,3,2,1,0:T(8,128)S(1)}, u32[]{:S(2)}, u32[]{:S(2)}) collective-permute-start(f32[1,2,1,2,2,16,4,128]{7,5,6,4,3,2,1,0:T(8,128)S(1)} %constant_dynamic-slice_fusion.7), channel_id=1, source_target_pairs={{0,4},{4,0},{8,12},{12,8},{16,20},{20,16},{24,28},{28,24},{1,5},{5... | collective-permute-start | bytes 786440 | tf_op jit(solution)/shard_map/ppermute | solution.py:48
  56.4 10.9 %collective-permute-start.13 = (f32[1,2,2,1,2,16,4,128]{7,5,6,4,3,2,1,0:T(8,128)S(1)}, f32[1,2,2,1,2,16,4,128]{7,5,6,4,3,2,1,0:T(8,128)S(1)}, u32[]{:S(2)}, u32[]{:S(2)}) collective-permute-start(f32[1,2,2,1,2,16,4,128]{7,5,6,4,3,2,1,0:T(8,128)S(1)} %constant_dynamic-slice_fusion.3), channel_id=1, source_target_pairs={{0,8},{4,12},{8,0},{12,4},{16,24},{20,28},{24,16},{28,20},{1,9},{5... | collective-permute-start | bytes 786440 | tf_op jit(solution)/shard_map/ppermute | solution.py:48
  61.2 9.5 %collective-permute-start.6 = (f32[1,1,1,2,2,16,4,128]{7,5,6,4,3,2,1,0:T(8,128)S(1)}, f32[1,1,1,2,2,16,4,128]{7,5,6,4,3,2,1,0:T(8,128)S(1)}, u32[]{:S(2)}, u32[]{:S(2)}) collective-permute-start(f32[1,1,1,2,2,16,4,128]{7,5,6,4,3,2,1,0:T(8,128)S(1)} %constant_dynamic-slice_fusion.10), channel_id=1, source_target_pairs={{0,4},{4,0},{8,12},{12,8},{16,20},{20,16},{24,28},{28,24},{1,5},{5... | collective-permute-start | bytes 393224 | tf_op jit(solution)/shard_map/ppermute | solution.py:48
  64.6 9.3 %collective-permute-start.10 = (f32[1,2,1,1,2,16,4,128]{7,5,6,4,3,2,1,0:T(8,128)S(1)}, f32[1,2,1,1,2,16,4,128]{7,5,6,4,3,2,1,0:T(8,128)S(1)}, u32[]{:S(2)}, u32[]{:S(2)}) collective-permute-start(f32[1,2,1,1,2,16,4,128]{7,5,6,4,3,2,1,0:T(8,128)S(1)} %constant_dynamic-slice_fusion.6), channel_id=1, source_target_pairs={{0,8},{4,12},{8,0},{12,4},{16,24},{20,28},{24,16},{28,20},{1,9},{5... | collective-permute-start | bytes 393224 | tf_op jit(solution)/shard_map/ppermute | solution.py:48
  67.4 8.9 %collective-permute-start.14 = (f32[1,2,2,1,1,16,4,128]{7,5,6,4,3,2,1,0:T(8,128)S(1)}, f32[1,2,2,1,1,16,4,128]{7,5,6,4,3,2,1,0:T(8,128)S(1)}, u32[]{:S(2)}, u32[]{:S(2)}) collective-permute-start(f32[1,2,2,1,1,16,4,128]{7,5,6,4,3,2,1,0:T(8,128)S(1)} %constant_dynamic-slice_fusion.2), channel_id=1, source_target_pairs={{0,16},{4,20},{8,24},{12,28},{16,0},{20,4},{24,8},{28,12},{1,17},{... | collective-permute-start | bytes 393224 | tf_op jit(solution)/shard_map/ppermute | solution.py:48
  70.7 6.3 %collective-permute-start.7 = (f32[1,1,1,1,2,16,4,128]{7,5,6,4,3,2,1,0:T(8,128)S(1)}, f32[1,1,1,1,2,16,4,128]{7,5,6,4,3,2,1,0:T(8,128)S(1)}, u32[]{:S(2)}, u32[]{:S(2)}) collective-permute-start(f32[1,1,1,1,2,16,4,128]{7,5,6,4,3,2,1,0:T(8,128)S(1)} %constant_dynamic-slice_fusion.9), channel_id=1, source_target_pairs={{0,8},{4,12},{8,0},{12,4},{16,24},{20,28},{24,16},{28,20},{1,9},{5... | collective-permute-start | bytes 196616 | tf_op jit(solution)/shard_map/ppermute | solution.py:48
  74.0 6.6 %collective-permute-start.11 = (f32[1,2,1,1,1,16,4,128]{7,5,6,4,3,2,1,0:T(8,128)S(1)}, f32[1,2,1,1,1,16,4,128]{7,5,6,4,3,2,1,0:T(8,128)S(1)}, u32[]{:S(2)}, u32[]{:S(2)}) collective-permute-start(f32[1,2,1,1,1,16,4,128]{7,5,6,4,3,2,1,0:T(8,128)S(1)} %constant_dynamic-slice_fusion.5), channel_id=1, source_target_pairs={{0,16},{4,20},{8,24},{12,28},{16,0},{20,4},{24,8},{28,12},{1,17},{... | collective-permute-start | bytes 196616 | tf_op jit(solution)/shard_map/ppermute | solution.py:48
  76.3 4.5 %collective-permute-start.15 = (f32[1,1,2,1,1,16,4,128]{7,5,6,4,3,2,1,0:T(8,128)S(1)}, f32[1,1,2,1,1,16,4,128]{7,5,6,4,3,2,1,0:T(8,128)S(1)}, u32[]{:S(2)}, u32[]{:S(2)}) collective-permute-start(f32[1,1,2,1,1,16,4,128]{7,5,6,4,3,2,1,0:T(8,128)S(1)} %constant_dynamic-slice_fusion.1), channel_id=1, source_target_pairs={{0,2},{1,3},{2,0},{3,1},{4,6},{5,7},{6,4},{7,5},{8,10},{9,11},{10,... | collective-permute-start | bytes 196616 | tf_op jit(solution)/shard_map/ppermute | solution.py:48
  77.1 5.8 %collective-permute-start.8 = (f32[1,1,1,1,1,16,4,128]{7,5,6,4,3,2,1,0:T(8,128)S(1)}, f32[1,1,1,1,1,16,4,128]{7,5,6,4,3,2,1,0:T(8,128)S(1)}, u32[]{:S(2)}, u32[]{:S(2)}) collective-permute-start(f32[1,1,1,1,1,16,4,128]{7,5,6,4,3,2,1,0:T(8,128)S(1)} %constant_dynamic-slice_fusion.8), channel_id=1, source_target_pairs={{0,16},{4,20},{8,24},{12,28},{16,0},{20,4},{24,8},{28,12},{1,17},{... | collective-permute-start | bytes 98312 | tf_op jit(solution)/shard_map/ppermute | solution.py:48
  80.6 4.0 %collective-permute-start.12 = (f32[1,1,1,1,1,16,4,128]{7,5,6,4,3,2,1,0:T(8,128)S(1)}, f32[1,1,1,1,1,16,4,128]{7,5,6,4,3,2,1,0:T(8,128)S(1)}, u32[]{:S(2)}, u32[]{:S(2)}) collective-permute-start(f32[1,1,1,1,1,16,4,128]{7,5,6,4,3,2,1,0:T(8,128)S(1)} %constant_dynamic-slice_fusion.4), channel_id=1, source_target_pairs={{0,2},{1,3},{2,0},{3,1},{4,6},{5,7},{6,4},{7,5},{8,10},{9,11},{10,... | collective-permute-start | bytes 98312 | tf_op jit(solution)/shard_map/ppermute | solution.py:48
  80.8 4.0 %collective-permute-start.16 = (f32[1,1,1,1,1,16,4,128]{7,5,6,4,3,2,1,0:T(8,128)S(1)}, f32[1,1,1,1,1,16,4,128]{7,5,6,4,3,2,1,0:T(8,128)S(1)}, u32[]{:S(2)}, u32[]{:S(2)}) collective-permute-start(f32[1,1,1,1,1,16,4,128]{7,5,6,4,3,2,1,0:T(8,128)S(1)} %constant_dynamic-slice_fusion), channel_id=1, source_target_pairs={{0,4},{4,0},{8,12},{12,8},{16,20},{20,16},{24,28},{28,24},{1,5},{5... | collective-permute-start | bytes 98312 | tf_op jit(solution)/shard_map/ppermute | solution.py:48
  88.6 4.7 %collective-permute-start.17 = (bf16[1,1,1,1,1,16,4,128]{7,5,6,4,3,2,1,0:T(8,128)(2,1)S(1)}, bf16[1,1,1,1,1,16,4,128]{7,5,6,4,3,2,1,0:T(8,128)(2,1)S(1)}, u32[]{:S(2)}, u32[]{:S(2)}) collective-permute-start(bf16[1,1,1,1,1,16,4,128]{7,5,6,4,3,2,1,0:T(8,128)(2,1)S(1)} %get-tuple-element.36), channel_id=1, source_target_pairs={{0,16},{4,20},{8,24},{12,28},{16,0},{20,4},{24,8},{28,12},{1,17},{... | collective-permute-start | bytes 49160 | tf_op jit(solution)/shard_map/ppermute | solution.py:53
  90.4 5.4 %collective-permute-start.22 = (bf16[1,1,1,1,1,16,4,128]{7,5,6,4,3,2,1,0:T(8,128)(2,1)S(1)}, bf16[1,1,1,1,1,16,4,128]{7,5,6,4,3,2,1,0:T(8,128)(2,1)S(1)}, u32[]{:S(2)}, u32[]{:S(2)}) collective-permute-start(bf16[1,1,1,1,1,16,4,128]{7,5,6,4,3,2,1,0:T(8,128)(2,1)S(1)} %get-tuple-element.35), channel_id=1, source_target_pairs={{0,2},{1,3},{2,0},{3,1},{4,6},{5,7},{6,4},{7,5},{8,10},{9,11},{10,... | collective-permute-start | bytes 49160 | tf_op jit(solution)/shard_map/ppermute | solution.py:53
  90.9 6.9 %collective-permute-start.27 = (bf16[1,1,1,1,1,16,4,128]{7,5,6,4,3,2,1,0:T(8,128)(2,1)S(1)}, bf16[1,1,1,1,1,16,4,128]{7,5,6,4,3,2,1,0:T(8,128)(2,1)S(1)}, u32[]{:S(2)}, u32[]{:S(2)}) collective-permute-start(bf16[1,1,1,1,1,16,4,128]{7,5,6,4,3,2,1,0:T(8,128)(2,1)S(1)} %get-tuple-element.34), channel_id=1, source_target_pairs={{0,4},{4,0},{8,12},{12,8},{16,20},{20,16},{24,28},{28,24},{1,5},{5... | collective-permute-start | bytes 49160 | tf_op jit(solution)/shard_map/ppermute | solution.py:53
  93.3 5.7 %collective-permute-start.18 = (bf16[1,1,1,1,2,16,4,128]{7,5,6,4,3,2,1,0:T(8,128)(2,1)S(1)}, bf16[1,1,1,1,2,16,4,128]{7,5,6,4,3,2,1,0:T(8,128)(2,1)S(1)}, u32[]{:S(2)}, u32[]{:S(2)}) collective-permute-start(bf16[1,1,1,1,2,16,4,128]{7,5,6,4,3,2,1,0:T(8,128)(2,1)S(1)} %maximum_select_fusion.18), channel_id=1, source_target_pairs={{0,8},{4,12},{8,0},{12,4},{16,24},{20,28},{24,16},{28,20},{1,9},{5... | collective-permute-start | bytes 98312 | tf_op jit(solution)/shard_map/ppermute | solution.py:53
  95.7 5.2 %collective-permute-start.23 = (bf16[1,2,1,1,1,16,4,128]{7,5,6,1,4,3,2,0:T(8,128)(2,1)S(1)}, bf16[1,2,1,1,1,16,4,128]{7,5,6,1,4,3,2,0:T(8,128)(2,1)S(1)}, u32[]{:S(2)}, u32[]{:S(2)}) collective-permute-start(bf16[1,2,1,1,1,16,4,128]{7,5,6,1,4,3,2,0:T(8,128)(2,1)S(1)} %fusion.32), channel_id=1, source_target_pairs={{0,16},{4,20},{8,24},{12,28},{16,0},{20,4},{24,8},{28,12},{1,17},{... | collective-permute-start | bytes 98312 | tf_op jit(solution)/shard_map/ppermute | solution.py:53
  97.8 4.1 %collective-permute-start.28 = (bf16[1,1,2,1,1,16,4,128]{7,5,6,4,3,2,1,0:T(8,128)(2,1)S(1)}, bf16[1,1,2,1,1,16,4,128]{7,5,6,4,3,2,1,0:T(8,128)(2,1)S(1)}, u32[]{:S(2)}, u32[]{:S(2)}) collective-permute-start(bf16[1,1,2,1,1,16,4,128]{7,5,6,4,3,2,1,0:T(8,128)(2,1)S(1)} %maximum_select_fusion.22), channel_id=1, source_target_pairs={{0,2},{1,3},{2,0},{3,1},{4,6},{5,7},{6,4},{7,5},{8,10},{9,11},{10,... | collective-permute-start | bytes 98312 | tf_op jit(solution)/shard_map/ppermute | solution.py:53
  99.1 4.5 %collective-permute-start.19 = (bf16[1,1,1,2,2,16,4,128]{7,5,6,4,3,2,1,0:T(8,128)(2,1)S(1)}, bf16[1,1,1,2,2,16,4,128]{7,5,6,4,3,2,1,0:T(8,128)(2,1)S(1)}, u32[]{:S(2)}, u32[]{:S(2)}) collective-permute-start(bf16[1,1,1,2,2,16,4,128]{7,5,6,4,3,2,1,0:T(8,128)(2,1)S(1)} %maximum_select_fusion.13), channel_id=1, source_target_pairs={{0,4},{4,0},{8,12},{12,8},{16,20},{20,16},{24,28},{28,24},{1,5},{5... | collective-permute-start | bytes 196616 | tf_op jit(solution)/shard_map/ppermute | solution.py:53
  100.9 4.3 %collective-permute-start.24 = (bf16[1,2,1,1,2,16,4,128]{7,5,6,4,3,2,1,0:T(8,128)(2,1)S(1)}, bf16[1,2,1,1,2,16,4,128]{7,5,6,4,3,2,1,0:T(8,128)(2,1)S(1)}, u32[]{:S(2)}, u32[]{:S(2)}) collective-permute-start(bf16[1,2,1,1,2,16,4,128]{7,5,6,4,3,2,1,0:T(8,128)(2,1)S(1)} %copy.79), channel_id=1, source_target_pairs={{0,8},{4,12},{8,0},{12,4},{16,24},{20,28},{24,16},{28,20},{1,9},{5... | collective-permute-start | bytes 196616 | tf_op jit(solution)/shard_map/ppermute | solution.py:53
  101.9 5.9 %collective-permute-start.29 = (bf16[1,2,2,1,1,16,4,128]{7,5,6,4,3,2,1,0:T(8,128)(2,1)S(1)}, bf16[1,2,2,1,1,16,4,128]{7,5,6,4,3,2,1,0:T(8,128)(2,1)S(1)}, u32[]{:S(2)}, u32[]{:S(2)}) collective-permute-start(bf16[1,2,2,1,1,16,4,128]{7,5,6,4,3,2,1,0:T(8,128)(2,1)S(1)} %fusion.31), channel_id=1, source_target_pairs={{0,16},{4,20},{8,24},{12,28},{16,0},{20,4},{24,8},{28,12},{1,17},{... | collective-permute-start | bytes 196616 | tf_op jit(solution)/shard_map/ppermute | solution.py:53
  103.6 5.0 %collective-permute-start.20 = (bf16[1,1,2,2,2,16,4,128]{7,5,6,4,3,2,1,0:T(8,128)(2,1)S(1)}, bf16[1,1,2,2,2,16,4,128]{7,5,6,4,3,2,1,0:T(8,128)(2,1)S(1)}, u32[]{:S(2)}, u32[]{:S(2)}) collective-permute-start(bf16[1,1,2,2,2,16,4,128]{7,5,6,4,3,2,1,0:T(8,128)(2,1)S(1)} %maximum_select_fusion.7), channel_id=1, source_target_pairs={{0,2},{1,3},{2,0},{3,1},{4,6},{5,7},{6,4},{7,5},{8,10},{9,11},{10,... | collective-permute-start | bytes 393224 | tf_op jit(solution)/shard_map/ppermute | solution.py:53
  105.3 5.0 %collective-permute-start.25 = (bf16[1,2,1,2,2,16,4,128]{7,5,6,4,3,2,1,0:T(8,128)(2,1)S(1)}, bf16[1,2,1,2,2,16,4,128]{7,5,6,4,3,2,1,0:T(8,128)(2,1)S(1)}, u32[]{:S(2)}, u32[]{:S(2)}) collective-permute-start(bf16[1,2,1,2,2,16,4,128]{7,5,6,4,3,2,1,0:T(8,128)(2,1)S(1)} %maximum_select_fusion.9), channel_id=1, source_target_pairs={{0,4},{4,0},{8,12},{12,8},{16,20},{20,16},{24,28},{28,24},{1,5},{5... | collective-permute-start | bytes 393224 | tf_op jit(solution)/shard_map/ppermute | solution.py:53
  107.9 5.0 %collective-permute-start.30 = (bf16[1,2,2,1,2,16,4,128]{7,5,6,4,3,2,1,0:T(8,128)(2,1)S(1)}, bf16[1,2,2,1,2,16,4,128]{7,5,6,4,3,2,1,0:T(8,128)(2,1)S(1)}, u32[]{:S(2)}, u32[]{:S(2)}) collective-permute-start(bf16[1,2,2,1,2,16,4,128]{7,5,6,4,3,2,1,0:T(8,128)(2,1)S(1)} %maximum_select_fusion.11), channel_id=1, source_target_pairs={{0,8},{4,12},{8,0},{12,4},{16,24},{20,28},{24,16},{28,20},{1,9},{5... | collective-permute-start | bytes 393224 | tf_op jit(solution)/shard_map/ppermute | solution.py:53
  108.7 4.5 %collective-permute-start.21 = (bf16[1,2,2,2,2,16,4,128]{7,5,6,4,3,2,1,0:T(8,128)(2,1)S(1)}, bf16[1,2,2,2,2,16,4,128]{7,5,6,4,3,2,1,0:T(8,128)(2,1)S(1)}, u32[]{:S(2)}, u32[]{:S(2)}) collective-permute-start(bf16[1,2,2,2,2,16,4,128]{7,5,6,4,3,2,1,0:T(8,128)(2,1)S(1)} %maximum_select_fusion.3), channel_id=1, source_target_pairs={{0,1},{1,0},{2,3},{3,2},{4,5},{5,4},{6,7},{7,6},{8,9},{9,8},{10,11... | collective-permute-start | bytes 786440 | tf_op jit(solution)/shard_map/ppermute | solution.py:53
  110.3 3.0 %collective-permute-start.26 = (bf16[1,2,2,2,2,16,4,128]{7,5,6,4,3,2,1,0:T(8,128)(2,1)S(1)}, bf16[1,2,2,2,2,16,4,128]{7,5,6,4,3,2,1,0:T(8,128)(2,1)S(1)}, u32[]{:S(2)}, u32[]{:S(2)}) collective-permute-start(bf16[1,2,2,2,2,16,4,128]{7,5,6,4,3,2,1,0:T(8,128)(2,1)S(1)} %maximum_select_fusion.4), channel_id=1, source_target_pairs={{0,1},{1,0},{2,3},{3,2},{4,5},{5,4},{6,7},{7,6},{8,9},{9,8},{10,11... | collective-permute-start | bytes 786440 | tf_op jit(solution)/shard_map/ppermute | solution.py:53
  (13 other events, 80.1 us)
Sparse Core Ops, SparseCore 0:
  31.1 24.7 all-gather.1

commit v4 on v3

--- a/solution.py
+++ b/solution.py
@@ -82,7 +82,7 @@
     nb = len(bits)
     inner = rhs >> nb
     assert inner << nb == rhs
-    streams = 3 if total_blocks % 3 == 0 else 1
+    streams = 2 if total_blocks % 2 == 0 else 1
     per = total_blocks // streams
     orders = stream_orders(nb, streams)
     split = restricted.reshape((2,) * nb + (inner, total_blocks, width))

time: 130 us -> 136 us (1.046)
  waiting for transfers between devices: 20 us -> 29.4 us
  starting transfers between devices: 45.4 us -> 39.4 us
  local copies, waits for them, and re-layouts: 21.9 us -> 24.3 us
    ppermute x15 -> x10, waiting for transfers between devices: 7.73 us -> 13.3 us  [halve(): return keep + lax.ppermute(send, axis, pairs(axis, mask))]
    ppermute x15 -> x10, starting transfers between devices: 16.2 us -> 12.2 us  [double(): recv = lax.ppermute(y, axis, pairs(axis, mask))]
    ppermute x15 -> x10, waiting for transfers between devices: 8.78 us -> 11.6 us  [double(): recv = lax.ppermute(y, axis, pairs(axis, mask))]
    ppermute x15 -> x10, starting transfers between devices: 26 us -> 23.5 us  [halve(): return keep + lax.ppermute(send, axis, pairs(axis, mask))]
    dynamic_slice x12 -> x8, local copies, waits for them, and re-layouts: 0.18 us -> 1.68 us  [halve(): send = lax.dynamic_index_in_dim(x, 1 - v, axis=dim, keepdims=True)]
    dynamic_slice x2 -> x1, local copies, waits for them, and re-layouts: 3.36 us -> 3.89 us  [halve(): keep = lax.dynamic_index_in_dim(x, v, axis=dim, keepdims=True)]
    add x12 -> x8, other arithmetic: 4.61 us -> 5.08 us  [halve(): return keep + lax.ppermute(send, axis, pairs(axis, mask))]
    unnamed x28 -> x23, local copies, waits for them, and re-layouts: 3.55 us -> 3.27 us
  transfers between devices with their start and end apart: 33 -> 23, of which waited for: 15 -> 14; matrix products, arithmetic and copies ran while one was open for 17% -> 15% of each run, Pallas kernels for 0% -> 0%
where the time goes in v4:
time: 136 us; the launch traced here: 135 us
  starting transfers between devices  39.4 us (29%)
  waiting for transfers between devices  29.4 us (22%)
  local copies, waits for them, and re-layouts  24.3 us (18%)
  matrix products  15.7 us (12%)
  between operations  13.9 us (10%)
  other arithmetic  12.6 us (9%)
    ppermute x10, starting transfers between devices, halve(): return keep + lax.ppermute(send, axis, pairs(axis, mask))  23.5 us
    ppermute x10, waiting for transfers between devices, halve(): return keep + lax.ppermute(send, axis, pairs(axis, mask))  13.3 us
    ppermute x10, starting transfers between devices, double(): recv = lax.ppermute(y, axis, pairs(axis, mask))  12.2 us
    ppermute x10, waiting for transfers between devices, double(): recv = lax.ppermute(y, axis, pairs(axis, mask))  11.6 us
    add x8, other arithmetic, halve(): return keep + lax.ppermute(send, axis, pairs(axis, mask))  5.08 us
    dot_general x1, matrix products, per_device(): jnp.einsum('jerb,jebc->jrc', picked, inverse_blocks, preferred_element_ty...  4.94 us
    ppermute x1, waiting for transfers between devices, with_halo(): lax.ppermute(head, axis, [((i + 1) % count, i) for i in range(ends)])  4.42 us
    gather x1, local copies, waits for them, and re-layouts, per_device(): picked = jnp.take(extended, margin, axis=0)  4.21 us
  transfers between devices with their start and end apart: 23, of which 14 were waited for; matrix products, arithmetic and copies ran while one was open for 15% of the time, Pallas kernels for 0%

profile of v4, /device:TPU:0, one launch (start us, length us, event | category | flops | bytes accessed | tf_op | source)
XLA Modules:
  0.0 135.3 jit_solution(7773284898128737613)
XLA Ops:
  6.5 3.4 %convolution_bitcast_fusion = f32[4,2,512,128]{2,3,1,0:T(8,128)} fusion(bf16[4,2,256,128]{3,2,1,0:T(8,128)(2,1)} %param.11, bf16[4,512,256]{2,1,0:T(8,128)(2,1)} %param.7), kind=kOutput, calls=%fused_computation.10 | convolution fusion | flops 268435456 | bytes 3670016 | tf_op jit(solution)/shard_map/jrb,jqbc->jqrc/dot_general | solution.py:76
  9.9 2.9 %copy.56 = f32[4,2,512,128]{3,0,1,2:T(4,128)} copy(f32[4,2,512,128]{2,3,1,0:T(8,128)} %convolution_bitcast_fusion) | data formatting | bytes 4194304 | tf_op jit(solution)/shard_map/jrb,jqbc->jqrc/transpose | solution.py:76
  12.9 3.9 %fusion.37 = f32[512,128,12,1]{1,2,3,0:T(8,128)S(1)} fusion(f32[4,2,512,128]{3,0,1,2:T(4,128)} %copy.56, s32[4,2]{0,1:T(2,128)S(1)} %copy-done.8), kind=kOutput, calls=%fused_computation.84 | convolution fusion | flops 75497568 | bytes 5242912 | tf_op jit(solution)/shard_map/jqn,jqrc->rnc/dot_general | solution.py:79
  16.8 2.6 %fusion.49 = (f32[2,2,2,2,2,16,6,128]{7,6,5,4,3,2,1,0:T(8,128)}, f32[2,2,2,2,2,16,6,128]{7,6,5,4,3,2,1,0:T(8,128)}) fusion(f32[2,2,2,2,2,16,12,128]{7,6,5,4,3,2,1,0:T(8,128)S(1)} %bitcast.106), kind=kLoop, calls=%fused_computation.103 | loop fusion | bytes 6291456 | tf_op jit(solution)/shard_map/slice | solution.py:89
  19.4 3.9 %constant_dynamic-slice_fusion.9 = (f32[1,2,2,2,2,16,6,128]{7,6,5,4,3,2,1,0:T(8,128)}, f32[1,2,2,2,2,16,6,128]{7,6,5,4,3,2,1,0:T(8,128)S(1)}, f32[1,2,2,2,2,16,6...) fusion(f32[2,2,2,2,2,16,6,128]{7,6,5,4,3,2,1,0:T(8,128)} %get-tuple-element.11, s32[]{:T(128)S(6)} %select_n.478, ...), kind=kLoop, calls=%fused_computation.76 | loop fusion | bytes 6291464 | tf_op jit(solution)/shard_map/jit(dynamic_index_in_dim)/dynamic_slice | solution.py:46
  26.9 2.4 %collective-permute-start = (bf16[1,512,256]{2,1,0:T(8,128)(2,1)}, bf16[1,512,256]{2,1,0:T(8,128)(2,1)S(1)}, u32[]{:S(2)}, u32[]{:S(2)}) collective-permute-start(bf16[1,512,256]{2,1,0:T(8,128)(2,1)} %get-tuple-element.17), channel_id=1, source_target_pairs={{0,1},{1,2},{2,3},{3,4},{4,5},{5,6},{6,7},{7,8},{8,9},{9,10},{10,1... | collective-permute-start | bytes 786440 | tf_op jit(solution)/shard_map/ppermute | solution.py:15
  30.7 4.4 %collective-permute-done.1 = bf16[1,512,256]{2,1,0:T(8,128)(2,1)} collective-permute-done((bf16[1,512,256]{2,1,0:T(8,128)(2,1)}, bf16[1,512,256]{2,1,0:T(8,128)(2,1)}, u32[]{:S(2)}, u32[]{:S(2)}) %collective-permute-start.1) | collective-permute-done | bytes 262176 | tf_op jit(solution)/shard_map/ppermute | solution.py:17
  35.1 2.3 %pad_maximum_fusion = bf16[6,512,256]{2,1,0:T(8,128)(2,1)} fusion(bf16[1,512,256]{2,1,0:T(8,128)(2,1)} %collective-permute-done.1, bf16[4,512,256]{2,1,0:T(8,128)(2,1)S(1)} %copy-done.1, bf16[1,512,256]{2,1,0:T(8,128)(2,1)S(1)} %collective-permute-done), kind=kLoop, calls=%fused_computation.13 | loop fusion | flops 1572864 | bytes 3145728 | tf_op jit(solution)/shard_map/concatenate | solution.py:13
  37.4 4.2 %gather_fusion = bf16[16,512,256]{2,1,0:T(8,128)(2,1)} fusion(bf16[6,512,256]{2,1,0:T(8,128)(2,1)} %pad_maximum_fusion, s32[1024]{0:T(1024)S(1)} %pad_clamp_fusion.2), kind=kCustom, calls=%fused_computation | custom fusion | bytes 8388672 | tf_op jit(solution)/shard_map/jit(_take)/gather | solution.py:90
  41.6 4.9 %fusion.5 = f32[4,512,256]{2,1,0:T(8,128)} fusion(bf16[4,4,256,256]{3,2,1,0:T(8,128)(2,1)S(1)} %copy-done, bf16[4,4,512,256]{3,2,1,0:T(8,128)(2,1)} %bitcast.107, pred[4,4]{1,0:T(4,128)(4,1)S(1)} %compare_and_fusion.2), kind=kOutput, calls=%fused_computation.9 | convolution fusion | flops 1075838976 | bytes 8388624 | tf_op jit(solution)/shard_map/jerb,jebc->jrc/dot_general | solution.py:91
  51.1 4.5 %collective-permute-start.4 = (f32[1,1,2,2,2,16,6,128]{7,5,6,4,3,2,1,0:T(8,128)}, f32[1,1,2,2,2,16,6,128]{7,5,6,4,3,2,1,0:T(8,128)}, u32[]{:S(2)}, u32[]{:S(2)}) collective-permute-start(f32[1,1,2,2,2,16,6,128]{7,5,6,4,3,2,1,0:T(8,128)} %constant_dynamic-slice_fusion.7), channel_id=1, source_target_pairs={{0,2},{1,3},{2,0},{3,1},{4,6},{5,7},{6,4},{7,5},{8,10},{9,11},{10,... | collective-permute-start | bytes 1179656 | tf_op jit(solution)/shard_map/ppermute | solution.py:48
  56.3 2.5 %collective-permute-start.8 = (f32[1,2,2,1,2,16,6,128]{7,5,6,4,3,2,1,0:T(8,128)}, f32[1,2,2,1,2,16,6,128]{7,5,6,4,3,2,1,0:T(8,128)}, u32[]{:S(2)}, u32[]{:S(2)}) collective-permute-start(f32[1,2,2,1,2,16,6,128]{7,5,6,4,3,2,1,0:T(8,128)} %constant_dynamic-slice_fusion.3), channel_id=1, source_target_pairs={{0,8},{4,12},{8,0},{12,4},{16,24},{20,28},{24,16},{28,20},{1,9},{5... | collective-permute-start | bytes 1179656 | tf_op jit(solution)/shard_map/ppermute | solution.py:48
  59.8 4.1 %collective-permute-done.4 = f32[1,1,2,2,2,16,6,128]{7,5,6,4,3,2,1,0:T(8,128)} collective-permute-done((f32[1,1,2,2,2,16,6,128]{7,5,6,4,3,2,1,0:T(8,128)}, f32[1,1,2,2,2,16,6,128]{7,5,6,4,3,2,1,0:T(8,128)}, u32[]{:S(2)}, u32[]{:S(2)}) %collective-permute-start.4) | collective-permute-done | bytes 393248 | tf_op jit(solution)/shard_map/ppermute | solution.py:48
  65.0 3.4 %collective-permute-start.5 = (f32[1,1,1,2,2,16,6,128]{7,5,6,4,3,2,1,0:T(8,128)S(1)}, f32[1,1,1,2,2,16,6,128]{7,5,6,4,3,2,1,0:T(8,128)S(1)}, u32[]{:S(2)}, u32[]{:S(2)}) collective-permute-start(f32[1,1,1,2,2,16,6,128]{7,5,6,4,3,2,1,0:T(8,128)S(1)} %constant_dynamic-slice_fusion.6), channel_id=1, source_target_pairs={{0,4},{4,0},{8,12},{12,8},{16,20},{20,16},{24,28},{28,24},{1,5},{5... | collective-permute-start | bytes 589832 | tf_op jit(solution)/shard_map/ppermute | solution.py:48
  69.5 3.7 %collective-permute-start.9 = (f32[1,2,2,1,1,16,6,128]{7,5,6,4,3,2,1,0:T(8,128)S(1)}, f32[1,2,2,1,1,16,6,128]{7,5,6,4,3,2,1,0:T(8,128)S(1)}, u32[]{:S(2)}, u32[]{:S(2)}) collective-permute-start(f32[1,2,2,1,1,16,6,128]{7,5,6,4,3,2,1,0:T(8,128)S(1)} %constant_dynamic-slice_fusion.2), channel_id=1, source_target_pairs={{0,16},{4,20},{8,24},{12,28},{16,0},{20,4},{24,8},{28,12},{1,17},{... | collective-permute-start | bytes 589832 | tf_op jit(solution)/shard_map/ppermute | solution.py:48
  73.6 4.2 %collective-permute-start.6 = (f32[1,1,1,1,2,16,6,128]{7,5,6,4,3,2,1,0:T(8,128)S(1)}, f32[1,1,1,1,2,16,6,128]{7,5,6,4,3,2,1,0:T(8,128)S(1)}, u32[]{:S(2)}, u32[]{:S(2)}) collective-permute-start(f32[1,1,1,1,2,16,6,128]{7,5,6,4,3,2,1,0:T(8,128)S(1)} %constant_dynamic-slice_fusion.5), channel_id=1, source_target_pairs={{0,8},{4,12},{8,0},{12,4},{16,24},{20,28},{24,16},{28,20},{1,9},{5... | collective-permute-start | bytes 294920 | tf_op jit(solution)/shard_map/ppermute | solution.py:48
  77.8 4.9 %collective-permute-done.9 = f32[1,2,2,1,1,16,6,128]{7,5,6,4,3,2,1,0:T(8,128)S(1)} collective-permute-done((f32[1,2,2,1,1,16,6,128]{7,5,6,4,3,2,1,0:T(8,128)S(1)}, f32[1,2,2,1,1,16,6,128]{7,5,6,4,3,2,1,0:T(8,128)S(1)}, u32[]{:S(2)}, u32[]{:S(2)}) %collective-permute-start.9) | collective-permute-done | bytes 196640 | tf_op jit(solution)/shard_map/ppermute | solution.py:48
  83.8 2.2 %collective-permute-start.7 = (f32[1,1,1,1,1,16,6,128]{7,5,6,4,3,2,1,0:T(8,128)S(1)}, f32[1,1,1,1,1,16,6,128]{7,5,6,4,3,2,1,0:T(8,128)S(1)}, u32[]{:S(2)}, u32[]{:S(2)}) collective-permute-start(f32[1,1,1,1,1,16,6,128]{7,5,6,4,3,2,1,0:T(8,128)S(1)} %constant_dynamic-slice_fusion.4), channel_id=1, source_target_pairs={{0,16},{4,20},{8,24},{12,28},{16,0},{20,4},{24,8},{28,12},{1,17},{... | collective-permute-start | bytes 147464 | tf_op jit(solution)/shard_map/ppermute | solution.py:48
  86.1 1.4 %collective-permute-done.10 = f32[1,1,2,1,1,16,6,128]{7,5,6,4,3,2,1,0:T(8,128)S(1)} collective-permute-done((f32[1,1,2,1,1,16,6,128]{7,5,6,4,3,2,1,0:T(8,128)S(1)}, f32[1,1,2,1,1,16,6,128]{7,5,6,4,3,2,1,0:T(8,128)S(1)}, u32[]{:S(2)}, u32[]{:S(2)}) %collective-permute-start.10) | collective-permute-done | bytes 98336 | tf_op jit(solution)/shard_map/ppermute | solution.py:48
  87.5 1.5 %collective-permute-start.11 = (f32[1,1,1,1,1,16,6,128]{7,5,6,4,3,2,1,0:T(8,128)S(1)}, f32[1,1,1,1,1,16,6,128]{7,5,6,4,3,2,1,0:T(8,128)S(1)}, u32[]{:S(2)}, u32[]{:S(2)}) collective-permute-start(f32[1,1,1,1,1,16,6,128]{7,5,6,4,3,2,1,0:T(8,128)S(1)} %constant_dynamic-slice_fusion), channel_id=1, source_target_pairs={{0,4},{4,0},{8,12},{12,8},{16,20},{20,16},{24,28},{28,24},{1,5},{5... | collective-permute-start | bytes 147464 | tf_op jit(solution)/shard_map/ppermute | solution.py:48
  89.4 2.3 %collective-permute-done.11 = f32[1,1,1,1,1,16,6,128]{7,5,6,4,3,2,1,0:T(8,128)S(1)} collective-permute-done((f32[1,1,1,1,1,16,6,128]{7,5,6,4,3,2,1,0:T(8,128)S(1)}, f32[1,1,1,1,1,16,6,128]{7,5,6,4,3,2,1,0:T(8,128)S(1)}, u32[]{:S(2)}, u32[]{:S(2)}) %collective-permute-start.11) | collective-permute-done | bytes 49184 | tf_op jit(solution)/shard_map/ppermute | solution.py:48
  93.7 1.8 %fusion.16 = bf16[1,1,1,1,1,16,12,128]{7,5,6,4,3,2,1,0:T(8,128)(2,1)S(1)} fusion(bf16[12,4,136,128]{3,2,1,0:T(8,128)(2,1)} %all-gather.2.cloned.1.call-done, bf16[12,4,16,128]{3,2,1,0:T(8,128)(2,1)S(1)} %bitcast.116, pred[12,4]{1,0:T(8,128)(4,1)S(1)} %copy.61), kind=kOutput, calls=%fused_computation.17 | convolution fusion | flops 25288704 | bytes 1818672 | tf_op jit(solution)/shard_map/rnec,necd->rnd/dot_general | solution.py:99
  95.8 1.5 %collective-permute-start.17 = (bf16[1,1,1,1,1,16,6,128]{7,5,6,4,3,2,1,0:T(8,128)(2,1)S(1)}, bf16[1,1,1,1,1,16,6,128]{7,5,6,4,3,2,1,0:T(8,128)(2,1)S(1)}, u32[]{:S(2)}, u32[]{:S(2)}) collective-permute-start(bf16[1,1,1,1,1,16,6,128]{7,5,6,4,3,2,1,0:T(8,128)(2,1)S(1)} %get-tuple-element.28), channel_id=1, source_target_pairs={{0,4},{4,0},{8,12},{12,8},{16,20},{20,16},{24,28},{28,24},{1,5},{5... | collective-permute-start | bytes 73736 | tf_op jit(solution)/shard_map/ppermute | solution.py:53
  97.3 3.1 %collective-permute-done.12 = bf16[1,1,1,1,1,16,6,128]{7,5,6,4,3,2,1,0:T(8,128)(2,1)S(1)} collective-permute-done((bf16[1,1,1,1,1,16,6,128]{7,5,6,4,3,2,1,0:T(8,128)(2,1)S(1)}, bf16[1,1,1,1,1,16,6,128]{7,5,6,4,3,2,1,0:T(8,128)(2,1)S(1)}, u32[]{:S(2)}, u32[]{:S(2)}) %collective-permute-start.12) | collective-permute-done | bytes 24608 | tf_op jit(solution)/shard_map/ppermute | solution.py:53
  102.8 1.7 %collective-permute-done.13 = bf16[1,1,1,1,2,16,6,128]{7,5,6,4,3,2,1,0:T(8,128)(2,1)S(1)} collective-permute-done((bf16[1,1,1,1,2,16,6,128]{7,5,6,4,3,2,1,0:T(8,128)(2,1)S(1)}, bf16[1,1,1,1,2,16,6,128]{7,5,6,4,3,2,1,0:T(8,128)(2,1)S(1)}, u32[]{:S(2)}, u32[]{:S(2)}) %collective-permute-start.13) | collective-permute-done | bytes 49184 | tf_op jit(solution)/shard_map/ppermute | solution.py:53
  104.6 1.5 %collective-permute-start.14 = (bf16[1,1,1,2,2,16,6,128]{7,5,6,4,3,2,1,0:T(8,128)(2,1)S(1)}, bf16[1,1,1,2,2,16,6,128]{7,5,6,4,3,2,1,0:T(8,128)(2,1)S(1)}, u32[]{:S(2)}, u32[]{:S(2)}) collective-permute-start(bf16[1,1,1,2,2,16,6,128]{7,5,6,4,3,2,1,0:T(8,128)(2,1)S(1)} %maximum_select_fusion.9), channel_id=1, source_target_pairs={{0,4},{4,0},{8,12},{12,8},{16,20},{20,16},{24,28},{28,24},{1,5},{5... | collective-permute-start | bytes 294920 | tf_op jit(solution)/shard_map/ppermute | solution.py:53
  106.1 2.8 %collective-permute-start.19 = (bf16[1,2,2,1,1,16,6,128]{7,5,6,4,3,2,1,0:T(8,128)(2,1)S(1)}, bf16[1,2,2,1,1,16,6,128]{7,5,6,4,3,2,1,0:T(8,128)(2,1)S(1)}, u32[]{:S(2)}, u32[]{:S(2)}) collective-permute-start(bf16[1,2,2,1,1,16,6,128]{7,5,6,4,3,2,1,0:T(8,128)(2,1)S(1)} %fusion.30), channel_id=1, source_target_pairs={{0,16},{4,20},{8,24},{12,28},{16,0},{20,4},{24,8},{28,12},{1,17},{... | collective-permute-start | bytes 294920 | tf_op jit(solution)/shard_map/ppermute | solution.py:53
  110.2 1.6 %collective-permute-done.19 = bf16[1,2,2,1,1,16,6,128]{7,5,6,4,3,2,1,0:T(8,128)(2,1)S(1)} collective-permute-done((bf16[1,2,2,1,1,16,6,128]{7,5,6,4,3,2,1,0:T(8,128)(2,1)S(1)}, bf16[1,2,2,1,1,16,6,128]{7,5,6,4,3,2,1,0:T(8,128)(2,1)S(1)}, u32[]{:S(2)}, u32[]{:S(2)}) %collective-permute-start.19) | collective-permute-done | bytes 98336 | tf_op jit(solution)/shard_map/ppermute | solution.py:53
  111.8 3.0 %collective-permute-start.20 = (bf16[1,2,2,1,2,16,6,128]{7,5,6,4,3,2,1,0:T(8,128)(2,1)S(1)}, bf16[1,2,2,1,2,16,6,128]{7,5,6,4,3,2,1,0:T(8,128)(2,1)S(1)}, u32[]{:S(2)}, u32[]{:S(2)}) collective-permute-start(bf16[1,2,2,1,2,16,6,128]{7,5,6,4,3,2,1,0:T(8,128)(2,1)S(1)} %maximum_select_fusion.7), channel_id=1, source_target_pairs={{0,8},{4,12},{8,0},{12,4},{16,24},{20,28},{24,16},{28,20},{1,9},{5... | collective-permute-start | bytes 589832 | tf_op jit(solution)/shard_map/ppermute | solution.py:53
  115.2 3.3 %collective-permute-done.20 = bf16[1,2,2,1,2,16,6,128]{7,5,6,4,3,2,1,0:T(8,128)(2,1)S(1)} collective-permute-done((bf16[1,2,2,1,2,16,6,128]{7,5,6,4,3,2,1,0:T(8,128)(2,1)S(1)}, bf16[1,2,2,1,2,16,6,128]{7,5,6,4,3,2,1,0:T(8,128)(2,1)S(1)}, u32[]{:S(2)}, u32[]{:S(2)}) %collective-permute-start.20) | collective-permute-done | bytes 196640 | tf_op jit(solution)/shard_map/ppermute | solution.py:53
  123.3 2.2 %gather_fusion.2 = bf16[8,512,128]{2,1,0:T(8,128)(2,1)S(1)} fusion(bf16[512,12,128]{2,0,1:T(8,128)(2,1)} %pad_maximum_fusion.1, s32[1024]{0:T(1024)S(1)} %pad_clamp_fusion), kind=kCustom, calls=%fused_computation.2 | custom fusion | bytes 2097184 | tf_op jit(solution)/shard_map/jit(_take)/gather | solution.py:108
  125.5 1.7 %fusion.20 = f32[4,512,256,1]{2,1,3,0:T(8,128)S(1)} fusion(bf16[4,2,256,128]{3,2,1,0:T(8,128)(2,1)} %param.11, bf16[4,2,512,128]{3,2,1,0:T(8,128)(2,1)S(1)} %bitcast.108, pred[4,2]{1,0:T(4,128)(4,1)S(1)} %copy.59), kind=kOutput, calls=%fused_computation.19 | convolution fusion | flops 268959744 | bytes 3670024 | tf_op jit(solution)/shard_map/rjqc,jqbc->jrb/dot_general | solution.py:109
  (111 shorter events, 27.5 us)
Async XLA Ops:
  6.5 35.1 %copy-start = (bf16[4,4,256,256]{3,2,1,0:T(8,128)(2,1)S(1)}, bf16[4,4,256,256]{3,2,1,0:T(8,128)(2,1)}, u32[]{:S(2)}) copy-start(bf16[4,4,256,256]{3,2,1,0:T(8,128)(2,1)} %param.9) | copy-start | bytes 6291460
  6.5 85.2 %all-gather.2.cloned.1.call-start = ((), (), s32[]{:S(2)}) async-start(), calls=%async_computation | async-start | bytes 2088960 | tf_op jit(solution)/shard_map/all_gather | solution.py:69
  9.9 2.9 %copy-start.8 = (s32[4,2]{0,1:T(2,128)S(1)}, s32[4,2]{0,1:T(2,128)}, u32[]{:S(2)}) copy-start(s32[4,2]{0,1:T(2,128)} %param.10) | copy-start | bytes 100
  23.3 2.7 %copy-start.1 = (bf16[4,512,256]{2,1,0:T(8,128)(2,1)S(1)}, bf16[4,512,256]{2,1,0:T(8,128)(2,1)}, u32[]{:S(2)}) copy-start(bf16[4,512,256]{2,1,0:T(8,128)(2,1)} %param.7) | copy-start | bytes 3145732
  23.3 7.2 %copy-start.7 = (s32[4,4]{1,0:T(4,128)S(1)}, s32[4,4]{1,0:T(4,128)}, u32[]{:S(2)}) copy-start(s32[4,4]{1,0:T(4,128)} %param.8) | copy-start | bytes 196
  24.5 22.1 %collective-permute-start.3 = (f32[1,2,2,2,2,16,6,128]{7,5,6,4,3,2,1,0:T(8,128)}, f32[1,2,2,2,2,16,6,128]{7,5,6,4,3,2,1,0:T(8,128)}, u32[]{:S(2)}, u32[]{:S(2)}) collective-permute-start(f32[1,2,2,2,2,16,6,128]{7,5,6,4,3,2,1,0:T(8,128)} %copy.83), channel_id=1, source_target_pairs={{0,1},{1,0},{2,3},{3,2},{4,5},{5,4},{6,7},{7,6},{8,9},{9,8},{10,11... | collective-permute-start | bytes 2359304 | tf_op jit(solution)/shard_map/ppermute | solution.py:48
  26.0 22.1 %collective-permute-start.2 = (f32[1,2,2,2,2,16,6,128]{7,5,6,4,3,2,1,0:T(8,128)}, f32[1,2,2,2,2,16,6,128]{7,5,6,4,3,2,1,0:T(8,128)}, u32[]{:S(2)}, u32[]{:S(2)}) collective-permute-start(f32[1,2,2,2,2,16,6,128]{7,5,6,4,3,2,1,0:T(8,128)} %copy.80), channel_id=1, source_target_pairs={{0,1},{1,0},{2,3},{3,2},{4,5},{5,4},{6,7},{7,6},{8,9},{9,8},{10,11... | collective-permute-start | bytes 2359304 | tf_op jit(solution)/shard_map/ppermute | solution.py:48
  26.9 3.8 %collective-permute-start = (bf16[1,512,256]{2,1,0:T(8,128)(2,1)}, bf16[1,512,256]{2,1,0:T(8,128)(2,1)S(1)}, u32[]{:S(2)}, u32[]{:S(2)}) collective-permute-start(bf16[1,512,256]{2,1,0:T(8,128)(2,1)} %get-tuple-element.17), channel_id=1, source_target_pairs={{0,1},{1,2},{2,3},{3,4},{4,5},{5,6},{6,7},{7,8},{8,9},{9,10},{10,1... | collective-permute-start | bytes 786440 | tf_op jit(solution)/shard_map/ppermute | solution.py:15
  29.2 5.9 %collective-permute-start.1 = (bf16[1,512,256]{2,1,0:T(8,128)(2,1)}, bf16[1,512,256]{2,1,0:T(8,128)(2,1)}, u32[]{:S(2)}, u32[]{:S(2)}) collective-permute-start(bf16[1,512,256]{2,1,0:T(8,128)(2,1)} %get-tuple-element.18), channel_id=1, source_target_pairs={{1,0},{2,1},{3,2},{4,3},{5,4},{6,5},{7,6},{8,7},{9,8},{10,9},{11,1... | collective-permute-start | bytes 786440 | tf_op jit(solution)/shard_map/ppermute | solution.py:17
  41.6 5.0 %copy-start.3 = (f32[1,2,2,2,2,16,6,128]{7,6,5,4,3,2,1,0:T(8,128)S(1)}, f32[1,2,2,2,2,16,6,128]{7,6,5,4,3,2,1,0:T(8,128)}, u32[]{:S(2)}) copy-start(f32[1,2,2,2,2,16,6,128]{7,6,5,4,3,2,1,0:T(8,128)} %get-tuple-element.13) | copy-start | bytes 2359300
  46.6 1.5 %copy-start.2 = (f32[1,2,2,2,2,16,6,128]{7,6,5,4,3,2,1,0:T(8,128)S(1)}, f32[1,2,2,2,2,16,6,128]{7,6,5,4,3,2,1,0:T(8,128)}, u32[]{:S(2)}) copy-start(f32[1,2,2,2,2,16,6,128]{7,6,5,4,3,2,1,0:T(8,128)} %get-tuple-element.34) | copy-start | bytes 2359300
  48.0 7.5 %copy-start.9 = (s32[3,4]{1,0:T(4,128)S(1)}, s32[3,4]{1,0:T(4,128)}, u32[]{:S(2)}) copy-start(s32[3,4]{1,0:T(4,128)} %param.12) | copy-start | bytes 148
  48.0 10.8 %copy-start.6 = (bf16[3,4,128,128]{3,2,1,0:T(8,128)(2,1)S(1)}, bf16[3,4,128,128]{3,2,1,0:T(8,128)(2,1)}, u32[]{:S(2)}) copy-start(bf16[3,4,128,128]{3,2,1,0:T(8,128)(2,1)} %param.13) | copy-start | bytes 1179652
  51.1 12.8 %collective-permute-start.4 = (f32[1,1,2,2,2,16,6,128]{7,5,6,4,3,2,1,0:T(8,128)}, f32[1,1,2,2,2,16,6,128]{7,5,6,4,3,2,1,0:T(8,128)}, u32[]{:S(2)}, u32[]{:S(2)}) collective-permute-start(f32[1,1,2,2,2,16,6,128]{7,5,6,4,3,2,1,0:T(8,128)} %constant_dynamic-slice_fusion.7), channel_id=1, source_target_pairs={{0,2},{1,3},{2,0},{3,1},{4,6},{5,7},{6,4},{7,5},{8,10},{9,11},{10,... | collective-permute-start | bytes 1179656 | tf_op jit(solution)/shard_map/ppermute | solution.py:48
  56.3 12.1 %collective-permute-start.8 = (f32[1,2,2,1,2,16,6,128]{7,5,6,4,3,2,1,0:T(8,128)}, f32[1,2,2,1,2,16,6,128]{7,5,6,4,3,2,1,0:T(8,128)}, u32[]{:S(2)}, u32[]{:S(2)}) collective-permute-start(f32[1,2,2,1,2,16,6,128]{7,5,6,4,3,2,1,0:T(8,128)} %constant_dynamic-slice_fusion.3), channel_id=1, source_target_pairs={{0,8},{4,12},{8,0},{12,4},{16,24},{20,28},{24,16},{28,20},{1,9},{5... | collective-permute-start | bytes 1179656 | tf_op jit(solution)/shard_map/ppermute | solution.py:48
  65.0 8.5 %collective-permute-start.5 = (f32[1,1,1,2,2,16,6,128]{7,5,6,4,3,2,1,0:T(8,128)S(1)}, f32[1,1,1,2,2,16,6,128]{7,5,6,4,3,2,1,0:T(8,128)S(1)}, u32[]{:S(2)}, u32[]{:S(2)}) collective-permute-start(f32[1,1,1,2,2,16,6,128]{7,5,6,4,3,2,1,0:T(8,128)S(1)} %constant_dynamic-slice_fusion.6), channel_id=1, source_target_pairs={{0,4},{4,0},{8,12},{12,8},{16,20},{20,16},{24,28},{28,24},{1,5},{5... | collective-permute-start | bytes 589832 | tf_op jit(solution)/shard_map/ppermute | solution.py:48
  69.5 13.2 %collective-permute-start.9 = (f32[1,2,2,1,1,16,6,128]{7,5,6,4,3,2,1,0:T(8,128)S(1)}, f32[1,2,2,1,1,16,6,128]{7,5,6,4,3,2,1,0:T(8,128)S(1)}, u32[]{:S(2)}, u32[]{:S(2)}) collective-permute-start(f32[1,2,2,1,1,16,6,128]{7,5,6,4,3,2,1,0:T(8,128)S(1)} %constant_dynamic-slice_fusion.2), channel_id=1, source_target_pairs={{0,16},{4,20},{8,24},{12,28},{16,0},{20,4},{24,8},{28,12},{1,17},{... | collective-permute-start | bytes 589832 | tf_op jit(solution)/shard_map/ppermute | solution.py:48
  73.6 10.2 %collective-permute-start.6 = (f32[1,1,1,1,2,16,6,128]{7,5,6,4,3,2,1,0:T(8,128)S(1)}, f32[1,1,1,1,2,16,6,128]{7,5,6,4,3,2,1,0:T(8,128)S(1)}, u32[]{:S(2)}, u32[]{:S(2)}) collective-permute-start(f32[1,1,1,1,2,16,6,128]{7,5,6,4,3,2,1,0:T(8,128)S(1)} %constant_dynamic-slice_fusion.5), channel_id=1, source_target_pairs={{0,8},{4,12},{8,0},{12,4},{16,24},{20,28},{24,16},{28,20},{1,9},{5... | collective-permute-start | bytes 294920 | tf_op jit(solution)/shard_map/ppermute | solution.py:48
  82.8 4.7 %collective-permute-start.10 = (f32[1,1,2,1,1,16,6,128]{7,5,6,4,3,2,1,0:T(8,128)S(1)}, f32[1,1,2,1,1,16,6,128]{7,5,6,4,3,2,1,0:T(8,128)S(1)}, u32[]{:S(2)}, u32[]{:S(2)}) collective-permute-start(f32[1,1,2,1,1,16,6,128]{7,5,6,4,3,2,1,0:T(8,128)S(1)} %constant_dynamic-slice_fusion.1), channel_id=1, source_target_pairs={{0,2},{1,3},{2,0},{3,1},{4,6},{5,7},{6,4},{7,5},{8,10},{9,11},{10,... | collective-permute-start | bytes 294920 | tf_op jit(solution)/shard_map/ppermute | solution.py:48
  83.8 5.6 %collective-permute-start.7 = (f32[1,1,1,1,1,16,6,128]{7,5,6,4,3,2,1,0:T(8,128)S(1)}, f32[1,1,1,1,1,16,6,128]{7,5,6,4,3,2,1,0:T(8,128)S(1)}, u32[]{:S(2)}, u32[]{:S(2)}) collective-permute-start(f32[1,1,1,1,1,16,6,128]{7,5,6,4,3,2,1,0:T(8,128)S(1)} %constant_dynamic-slice_fusion.4), channel_id=1, source_target_pairs={{0,16},{4,20},{8,24},{12,28},{16,0},{20,4},{24,8},{28,12},{1,17},{... | collective-permute-start | bytes 147464 | tf_op jit(solution)/shard_map/ppermute | solution.py:48
  87.5 4.2 %collective-permute-start.11 = (f32[1,1,1,1,1,16,6,128]{7,5,6,4,3,2,1,0:T(8,128)S(1)}, f32[1,1,1,1,1,16,6,128]{7,5,6,4,3,2,1,0:T(8,128)S(1)}, u32[]{:S(2)}, u32[]{:S(2)}) collective-permute-start(f32[1,1,1,1,1,16,6,128]{7,5,6,4,3,2,1,0:T(8,128)S(1)} %constant_dynamic-slice_fusion), channel_id=1, source_target_pairs={{0,4},{4,0},{8,12},{12,8},{16,20},{20,16},{24,28},{28,24},{1,5},{5... | collective-permute-start | bytes 147464 | tf_op jit(solution)/shard_map/ppermute | solution.py:48
  95.5 4.9 %collective-permute-start.12 = (bf16[1,1,1,1,1,16,6,128]{7,5,6,4,3,2,1,0:T(8,128)(2,1)S(1)}, bf16[1,1,1,1,1,16,6,128]{7,5,6,4,3,2,1,0:T(8,128)(2,1)S(1)}, u32[]{:S(2)}, u32[]{:S(2)}) collective-permute-start(bf16[1,1,1,1,1,16,6,128]{7,5,6,4,3,2,1,0:T(8,128)(2,1)S(1)} %get-tuple-element.29), channel_id=1, source_target_pairs={{0,16},{4,20},{8,24},{12,28},{16,0},{20,4},{24,8},{28,12},{1,17},{... | collective-permute-start | bytes 73736 | tf_op jit(solution)/shard_map/ppermute | solution.py:53
  95.8 5.8 %collective-permute-start.17 = (bf16[1,1,1,1,1,16,6,128]{7,5,6,4,3,2,1,0:T(8,128)(2,1)S(1)}, bf16[1,1,1,1,1,16,6,128]{7,5,6,4,3,2,1,0:T(8,128)(2,1)S(1)}, u32[]{:S(2)}, u32[]{:S(2)}) collective-permute-start(bf16[1,1,1,1,1,16,6,128]{7,5,6,4,3,2,1,0:T(8,128)(2,1)S(1)} %get-tuple-element.28), channel_id=1, source_target_pairs={{0,4},{4,0},{8,12},{12,8},{16,20},{20,16},{24,28},{28,24},{1,5},{5... | collective-permute-start | bytes 73736 | tf_op jit(solution)/shard_map/ppermute | solution.py:53
  100.4 4.2 %collective-permute-start.13 = (bf16[1,1,1,1,2,16,6,128]{7,5,6,4,3,2,1,0:T(8,128)(2,1)S(1)}, bf16[1,1,1,1,2,16,6,128]{7,5,6,4,3,2,1,0:T(8,128)(2,1)S(1)}, u32[]{:S(2)}, u32[]{:S(2)}) collective-permute-start(bf16[1,1,1,1,2,16,6,128]{7,5,6,4,3,2,1,0:T(8,128)(2,1)S(1)} %maximum_select_fusion.12), channel_id=1, source_target_pairs={{0,8},{4,12},{8,0},{12,4},{16,24},{20,28},{24,16},{28,20},{1,9},{5... | collective-permute-start | bytes 147464 | tf_op jit(solution)/shard_map/ppermute | solution.py:53
  101.6 4.5 %collective-permute-start.18 = (bf16[1,1,2,1,1,16,6,128]{7,5,6,4,3,2,1,0:T(8,128)(2,1)S(1)}, bf16[1,1,2,1,1,16,6,128]{7,5,6,4,3,2,1,0:T(8,128)(2,1)S(1)}, u32[]{:S(2)}, u32[]{:S(2)}) collective-permute-start(bf16[1,1,2,1,1,16,6,128]{7,5,6,4,3,2,1,0:T(8,128)(2,1)S(1)} %maximum_select_fusion.14), channel_id=1, source_target_pairs={{0,2},{1,3},{2,0},{3,1},{4,6},{5,7},{6,4},{7,5},{8,10},{9,11},{10,... | collective-permute-start | bytes 147464 | tf_op jit(solution)/shard_map/ppermute | solution.py:53
  104.6 4.7 %collective-permute-start.14 = (bf16[1,1,1,2,2,16,6,128]{7,5,6,4,3,2,1,0:T(8,128)(2,1)S(1)}, bf16[1,1,1,2,2,16,6,128]{7,5,6,4,3,2,1,0:T(8,128)(2,1)S(1)}, u32[]{:S(2)}, u32[]{:S(2)}) collective-permute-start(bf16[1,1,1,2,2,16,6,128]{7,5,6,4,3,2,1,0:T(8,128)(2,1)S(1)} %maximum_select_fusion.9), channel_id=1, source_target_pairs={{0,4},{4,0},{8,12},{12,8},{16,20},{20,16},{24,28},{28,24},{1,5},{5... | collective-permute-start | bytes 294920 | tf_op jit(solution)/shard_map/ppermute | solution.py:53
  106.1 5.7 %collective-permute-start.19 = (bf16[1,2,2,1,1,16,6,128]{7,5,6,4,3,2,1,0:T(8,128)(2,1)S(1)}, bf16[1,2,2,1,1,16,6,128]{7,5,6,4,3,2,1,0:T(8,128)(2,1)S(1)}, u32[]{:S(2)}, u32[]{:S(2)}) collective-permute-start(bf16[1,2,2,1,1,16,6,128]{7,5,6,4,3,2,1,0:T(8,128)(2,1)S(1)} %fusion.30), channel_id=1, source_target_pairs={{0,16},{4,20},{8,24},{12,28},{16,0},{20,4},{24,8},{28,12},{1,17},{... | collective-permute-start | bytes 294920 | tf_op jit(solution)/shard_map/ppermute | solution.py:53
  109.3 5.7 %collective-permute-start.15 = (bf16[1,1,2,2,2,16,6,128]{7,5,6,4,3,2,1,0:T(8,128)(2,1)S(1)}, bf16[1,1,2,2,2,16,6,128]{7,5,6,4,3,2,1,0:T(8,128)(2,1)S(1)}, u32[]{:S(2)}, u32[]{:S(2)}) collective-permute-start(bf16[1,1,2,2,2,16,6,128]{7,5,6,4,3,2,1,0:T(8,128)(2,1)S(1)} %maximum_select_fusion.5), channel_id=1, source_target_pairs={{0,2},{1,3},{2,0},{3,1},{4,6},{5,7},{6,4},{7,5},{8,10},{9,11},{10,... | collective-permute-start | bytes 589832 | tf_op jit(solution)/shard_map/ppermute | solution.py:53
  111.8 6.7 %collective-permute-start.20 = (bf16[1,2,2,1,2,16,6,128]{7,5,6,4,3,2,1,0:T(8,128)(2,1)S(1)}, bf16[1,2,2,1,2,16,6,128]{7,5,6,4,3,2,1,0:T(8,128)(2,1)S(1)}, u32[]{:S(2)}, u32[]{:S(2)}) collective-permute-start(bf16[1,2,2,1,2,16,6,128]{7,5,6,4,3,2,1,0:T(8,128)(2,1)S(1)} %maximum_select_fusion.7), channel_id=1, source_target_pairs={{0,8},{4,12},{8,0},{12,4},{16,24},{20,28},{24,16},{28,20},{1,9},{5... | collective-permute-start | bytes 589832 | tf_op jit(solution)/shard_map/ppermute | solution.py:53
  115.1 3.7 %collective-permute-start.16 = (bf16[1,2,2,2,2,16,6,128]{7,5,6,4,3,2,1,0:T(8,128)(2,1)S(1)}, bf16[1,2,2,2,2,16,6,128]{7,5,6,4,3,2,1,0:T(8,128)(2,1)S(1)}, u32[]{:S(2)}, u32[]{:S(2)}) collective-permute-start(bf16[1,2,2,2,2,16,6,128]{7,5,6,4,3,2,1,0:T(8,128)(2,1)S(1)} %maximum_select_fusion.2), channel_id=1, source_target_pairs={{0,1},{1,0},{2,3},{3,2},{4,5},{5,4},{6,7},{7,6},{8,9},{9,8},{10,11... | collective-permute-start | bytes 1179656 | tf_op jit(solution)/shard_map/ppermute | solution.py:53
  118.5 1.9 %collective-permute-start.21 = (bf16[1,2,2,2,2,16,6,128]{7,5,6,4,3,2,1,0:T(8,128)(2,1)S(1)}, bf16[1,2,2,2,2,16,6,128]{7,5,6,4,3,2,1,0:T(8,128)(2,1)}, u32[]{:S(2)}, u32[]{:S(2)}) collective-permute-start(bf16[1,2,2,2,2,16,6,128]{7,5,6,4,3,2,1,0:T(8,128)(2,1)S(1)} %maximum_select_fusion.3), channel_id=1, source_target_pairs={{0,1},{1,0},{2,3},{3,2},{4,5},{5,4},{6,7},{7,6},{8,9},{9,8},{10,11... | collective-permute-start | bytes 1179656 | tf_op jit(solution)/shard_map/ppermute | solution.py:53
  125.5 1.7 %copy-start.5 = (f32[4,512,256]{2,1,0:T(8,128)S(1)}, f32[4,512,256]{2,1,0:T(8,128)}, u32[]{:S(2)}) copy-start(f32[4,512,256]{2,1,0:T(8,128)} %fusion.5) | copy-start | bytes 6291460
  (1 other events, 0.9 us)
Sparse Core Ops, SparseCore 0:
  59.8 21.1 all-gather.1

commit v5 on v3

--- a/solution.py
+++ b/solution.py
@@ -41,11 +41,11 @@
     return [(i, i ^ mask) for i in range(lax.axis_size(axis))]
 
 
-def halve(x, dim, axis, mask):
+def halve(x, dim, axis, mask, wire):
     v = bit_of(axis, mask)
     keep = lax.dynamic_index_in_dim(x, v, axis=dim, keepdims=True)
     send = lax.dynamic_index_in_dim(x, 1 - v, axis=dim, keepdims=True)
-    return keep + lax.ppermute(send, axis, pairs(axis, mask))
+    return keep + lax.ppermute(send.astype(wire), axis, pairs(axis, mask)).astype(x.dtype)
 
 
 def double(y, dim, axis, mask):
@@ -76,7 +76,7 @@
     terms = jnp.einsum("jrb,jqbc->jqrc", residual, basis, preferred_element_type=jnp.float32)
     labels = jnp.arange(total_blocks, dtype=jnp.int32)
     onehot = (interface[:, :, None] == labels[None, None, :]).astype(jnp.float32)
-    restricted = jnp.einsum("jqn,jqrc->rnc", onehot, terms, precision=lax.Precision.HIGHEST)
+    restricted = jnp.einsum("jqn,jqrc->nrc", onehot, terms, precision=lax.Precision.HIGHEST)
 
     bits = device_bits()
     nb = len(bits)
@@ -85,28 +85,29 @@
     streams = 3 if total_blocks % 3 == 0 else 1
     per = total_blocks // streams
     orders = stream_orders(nb, streams)
-    split = restricted.reshape((2,) * nb + (inner, total_blocks, width))
-    parts = [lax.slice_in_dim(split, s * per, (s + 1) * per, axis=nb + 1) for s in range(streams)]
+    split = restricted.reshape((total_blocks,) + (2,) * nb + (inner, width))
+    parts = [lax.slice_in_dim(split, s * per, (s + 1) * per, axis=0) for s in range(streams)]
     picked = jnp.take(extended, margin, axis=0)
     local = jnp.einsum("jerb,jebc->jrc", picked, inverse_blocks, preferred_element_type=jnp.float32)
     for step in range(nb):
-        parts = [halve(x, orders[s][step], *bits[orders[s][step]]) for s, x in enumerate(parts)]
+        wire = jnp.float32 if step == 0 else jnp.bfloat16
+        parts = [halve(x, 1 + orders[s][step], *bits[orders[s][step]], wire) for s, x in enumerate(parts)]
         if step == 0:
             local, parts = lax.optimization_barrier((local, parts))
-    mine = jnp.concatenate(parts, axis=nb + 1).reshape(inner, total_blocks, width)
+    mine = jnp.concatenate(parts, axis=0).reshape(total_blocks, inner, width)
     coarse_in = mine.astype(jnp.bfloat16)
-    chosen = jnp.take(coarse_in, pattern_all, axis=1)
+    chosen = jnp.take(coarse_in, pattern_all, axis=0)
     solved = jnp.einsum(
-        "rnec,necd->rnd", chosen, inverse_all, preferred_element_type=jnp.float32
+        "nerc,necd->nrd", chosen, inverse_all, preferred_element_type=jnp.float32
     ).astype(jnp.bfloat16)
-    solved = solved.reshape((1,) * nb + (inner, total_blocks, width))
-    outs = [lax.slice_in_dim(solved, s * per, (s + 1) * per, axis=nb + 1) for s in range(streams)]
+    solved = solved.reshape((total_blocks,) + (1,) * nb + (inner, width))
+    outs = [lax.slice_in_dim(solved, s * per, (s + 1) * per, axis=0) for s in range(streams)]
     for step in reversed(range(nb)):
-        outs = [double(y, orders[s][step], *bits[orders[s][step]]) for s, y in enumerate(outs)]
-    coarse_out = jnp.concatenate(outs, axis=nb + 1).reshape(rhs, total_blocks, width)
+        outs = [double(y, 1 + orders[s][step], *bits[orders[s][step]]) for s, y in enumerate(outs)]
+    coarse_out = jnp.concatenate(outs, axis=0).reshape(total_blocks, rhs, width)
 
-    lifted = jnp.take(coarse_out, interface, axis=1)
-    spread = jnp.einsum("rjqc,jqbc->jrb", lifted, basis, preferred_element_type=jnp.float32)
+    lifted = jnp.take(coarse_out, interface, axis=0)
+    spread = jnp.einsum("jqrc,jqbc->jrb", lifted, basis, preferred_element_type=jnp.float32)
     return (local + spread).astype(jnp.bfloat16)
 
 

time: 130 us -> 122 us (0.938)
  waiting for transfers between devices: 20 us -> 12.9 us
    ppermute x15, waiting for transfers between devices: 7.73 us -> 2.39 us  [halve(): lax.ppermute(send.astype(wire), axis, pairs(axis, mask)).astype(x.dtype)]
    ppermute x15, waiting for transfers between devices: 8.78 us -> 7.19 us  [double(): recv = lax.ppermute(y, axis, pairs(axis, mask))]
    unnamed x28 -> x26, local copies, waits for them, and re-layouts: 3.55 us -> 2.77 us
  transfers between devices with their start and end apart: 33 -> 33, of which waited for: 15 -> 11; matrix products, arithmetic and copies ran while one was open for 17% -> 17% of each run, Pallas kernels for 0% -> 0%
where the time goes in v5:
time: 122 us; the launch traced here: 121 us
  starting transfers between devices  46.2 us (38%)
  local copies, waits for them, and re-layouts  20.7 us (17%)
  matrix products  16.1 us (13%)
  between operations  14.1 us (12%)
  waiting for transfers between devices  12.9 us (11%)
  other arithmetic  11 us (9%)
    ppermute x15, starting transfers between devices, halve(): lax.ppermute(send.astype(wire), axis, pairs(axis, mask)).astype(x.dtype)  25.7 us
    ppermute x15, starting transfers between devices, double(): recv = lax.ppermute(y, axis, pairs(axis, mask))  17.2 us
    ppermute x15, waiting for transfers between devices, double(): recv = lax.ppermute(y, axis, pairs(axis, mask))  7.19 us
    dot_general x1, matrix products, per_device(): jnp.einsum('jerb,jebc->jrc', picked, inverse_blocks, preferred_element_ty...  5.13 us
    gather x1, local copies, waits for them, and re-layouts, per_device(): picked = jnp.take(extended, margin, axis=0)  4.2 us
    dot_general x1, matrix products, per_device(): jnp.einsum('jqn,jqrc->nrc', onehot, terms, precision=lax.Precision.HIGHEST)  4.18 us
    add x12, other arithmetic, halve(): keep + lax.ppermute(send.astype(wire), axis, pairs(axis, mask)).astype(x....  3.54 us
    dot_general x1, matrix products, per_device(): jnp.einsum('jrb,jqbc->jqrc', residual, basis, preferred_element_type=jnp....  3.38 us
  transfers between devices with their start and end apart: 33, of which 11 were waited for; matrix products, arithmetic and copies ran while one was open for 17% of the time, Pallas kernels for 0%

profile of v5, /device:TPU:0, one launch (start us, length us, event | category | flops | bytes accessed | tf_op | source)
XLA Modules:
  0.0 121.1 jit_solution(4497084803645879448)
XLA Ops:
  6.5 3.4 %convolution_bitcast_fusion.1 = f32[4,2,512,128]{2,3,1,0:T(8,128)} fusion(bf16[4,2,256,128]{3,2,1,0:T(8,128)(2,1)} %param.11, bf16[4,512,256]{2,1,0:T(8,128)(2,1)} %param.7), kind=kOutput, calls=%fused_computation.11 | convolution fusion | flops 268435456 | bytes 3670016 | tf_op jit(solution)/shard_map/jrb,jqbc->jqrc/dot_general | solution.py:76
  9.9 2.9 %copy.75 = f32[4,2,512,128]{3,0,1,2:T(4,128)} copy(f32[4,2,512,128]{2,3,1,0:T(8,128)} %convolution_bitcast_fusion.1) | data formatting | bytes 4194304 | tf_op jit(solution)/shard_map/jrb,jqbc->jqrc/transpose | solution.py:76
  12.9 4.2 %convolution_bitcast_fusion = f32[12,512,128]{2,0,1:T(8,128)S(1)} fusion(f32[4,2,512,128]{3,0,1,2:T(4,128)} %copy.75, s32[4,2]{0,1:T(2,128)S(1)} %copy-done.9), kind=kOutput, calls=%fused_computation.6 | convolution fusion | flops 75497568 | bytes 5242912 | tf_op jit(solution)/shard_map/jqn,jqrc->nrc/dot_general | solution.py:79
  17.0 1.8 %fusion.48 = (f32[4,512,128]{2,0,1:T(4,128)S(1)}, f32[4,512,128]{2,0,1:T(4,128)}, f32[4,512,128]{2,0,1:T(4,128)}) fusion(f32[12,512,128]{2,0,1:T(8,128)S(1)} %convolution_bitcast_fusion), kind=kLoop, calls=%fused_computation.129 | loop fusion | bytes 6291456 | tf_op jit(solution)/shard_map/slice | solution.py:89
  18.8 2.5 %constant_dynamic-slice_fusion.1 = (f32[4,1,2,2,2,2,16,128]{7,0,6,5,4,3,2,1:T(4,128)}, f32[4,1,2,2,2,2,16,128]{7,0,6,5,4,3,2,1:T(4,128)S(1)}, f32[4,1,2,2,2,2,16...) fusion(f32[4,2,2,2,2,2,16,128]{7,0,6,5,4,3,2,1:T(4,128)S(1)} %bitcast.119, s32[]{:T(128)S(6)} %select_n.673, ...), kind=kLoop, calls=%fused_computation.96 | loop fusion | bytes 4194312 | tf_op jit(solution)/shard_map/jit(dynamic_index_in_dim)/dynamic_slice | solution.py:46
  26.6 2.0 %collective-permute-start = (bf16[1,512,256]{2,1,0:T(8,128)(2,1)}, bf16[1,512,256]{2,1,0:T(8,128)(2,1)S(1)}, u32[]{:S(2)}, u32[]{:S(2)}) collective-permute-start(bf16[1,512,256]{2,1,0:T(8,128)(2,1)} %get-tuple-element.22), channel_id=1, source_target_pairs={{0,1},{1,2},{2,3},{3,4},{4,5},{5,6},{6,7},{7,8},{8,9},{9,10},{10,1... | collective-permute-start | bytes 786440 | tf_op jit(solution)/shard_map/ppermute | solution.py:15
  31.1 3.3 %collective-permute-done.1 = bf16[1,512,256]{2,1,0:T(8,128)(2,1)} collective-permute-done((bf16[1,512,256]{2,1,0:T(8,128)(2,1)}, bf16[1,512,256]{2,1,0:T(8,128)(2,1)}, u32[]{:S(2)}, u32[]{:S(2)}) %collective-permute-start.1) | collective-permute-done | bytes 262176 | tf_op jit(solution)/shard_map/ppermute | solution.py:17
  34.4 2.3 %pad_maximum_fusion = bf16[6,512,256]{2,1,0:T(8,128)(2,1)} fusion(bf16[1,512,256]{2,1,0:T(8,128)(2,1)} %collective-permute-done.1, bf16[4,512,256]{2,1,0:T(8,128)(2,1)S(1)} %copy-done.1, bf16[1,512,256]{2,1,0:T(8,128)(2,1)S(1)} %collective-permute-done), kind=kLoop, calls=%fused_computation.14 | loop fusion | flops 1572864 | bytes 3145728 | tf_op jit(solution)/shard_map/concatenate | solution.py:13
  36.7 4.2 %gather_fusion = bf16[16,512,256]{2,1,0:T(8,128)(2,1)} fusion(bf16[6,512,256]{2,1,0:T(8,128)(2,1)} %pad_maximum_fusion, s32[1024]{0:T(1024)S(1)} %pad_clamp_fusion.2), kind=kCustom, calls=%fused_computation | custom fusion | bytes 8388672 | tf_op jit(solution)/shard_map/jit(_take)/gather | solution.py:90
  40.9 5.1 %fusion.5 = f32[4,512,256]{2,1,0:T(8,128)} fusion(bf16[4,4,256,256]{3,2,1,0:T(8,128)(2,1)S(1)} %copy-done, bf16[4,4,512,256]{3,2,1,0:T(8,128)(2,1)} %bitcast.118, pred[4,4]{1,0:T(4,128)(4,1)S(1)} %compare_and_fusion.2), kind=kOutput, calls=%fused_computation.10 | convolution fusion | flops 1075838976 | bytes 8388624 | tf_op jit(solution)/shard_map/jerb,jebc->jrc/dot_general | solution.py:91
  49.6 4.4 %collective-permute-start.5 = (bf16[4,1,1,2,2,2,16,128]{7,6,0,5,4,3,2,1:T(8,128)(2,1)S(1)}, bf16[4,1,1,2,2,2,16,128]{7,6,0,5,4,3,2,1:T(8,128)(2,1)S(1)}, u32[]{:S(2)}, u32[]{:S(2)}) collective-permute-start(bf16[4,1,1,2,2,2,16,128]{7,6,0,5,4,3,2,1:T(8,128)(2,1)S(1)} %dynamic-slice_convert_fusion.2), channel_id=1, source_target_pairs={{0,2},{1,3},{2,0},{3,1},{4,6},{5,7},{6,4},{7,5},{8,10},{9,11},{10,... | collective-permute-start | bytes 393224 | tf_op jit(solution)/shard_map/ppermute | solution.py:48
  53.9 1.5 %collective-permute-start.9 = (bf16[4,1,2,1,2,2,16,128]{7,6,0,5,4,3,2,1:T(8,128)(2,1)S(1)}, bf16[4,1,2,1,2,2,16,128]{7,6,0,5,4,3,2,1:T(8,128)(2,1)S(1)}, u32[]{:S(2)}, u32[]{:S(2)}) collective-permute-start(bf16[4,1,2,1,2,2,16,128]{7,6,0,5,4,3,2,1:T(8,128)(2,1)S(1)} %dynamic-slice_convert_fusion.1), channel_id=1, source_target_pairs={{0,4},{4,0},{8,12},{12,8},{16,20},{20,16},{24,28},{28,24},{1,5},{5... | collective-permute-start | bytes 393224 | tf_op jit(solution)/shard_map/ppermute | solution.py:48
  55.5 1.6 %collective-permute-start.13 = (bf16[4,1,2,2,1,2,16,128]{7,6,0,5,4,3,2,1:T(8,128)(2,1)S(1)}, bf16[4,1,2,2,1,2,16,128]{7,6,0,5,4,3,2,1:T(8,128)(2,1)S(1)}, u32[]{:S(2)}, u32[]{:S(2)}) collective-permute-start(bf16[4,1,2,2,1,2,16,128]{7,6,0,5,4,3,2,1:T(8,128)(2,1)S(1)} %dynamic-slice_convert_fusion), channel_id=1, source_target_pairs={{0,8},{4,12},{8,0},{12,4},{16,24},{20,28},{24,16},{28,20},{1,9},{5... | collective-permute-start | bytes 393224 | tf_op jit(solution)/shard_map/ppermute | solution.py:48
  57.2 2.7 %collective-permute-start.6 = (bf16[4,1,1,1,2,2,16,128]{7,6,0,5,4,3,2,1:T(8,128)(2,1)S(1)}, bf16[4,1,1,1,2,2,16,128]{7,6,0,5,4,3,2,1:T(8,128)(2,1)S(1)}, u32[]{:S(2)}, u32[]{:S(2)}) collective-permute-start(bf16[4,1,1,1,2,2,16,128]{7,6,0,5,4,3,2,1:T(8,128)(2,1)S(1)} %dynamic-slice_convert_fusion.5), channel_id=1, source_target_pairs={{0,4},{4,0},{8,12},{12,8},{16,20},{20,16},{24,28},{28,24},{1,5},{5... | collective-permute-start | bytes 196616 | tf_op jit(solution)/shard_map/ppermute | solution.py:48
  60.0 2.4 %collective-permute-start.10 = (bf16[4,1,2,1,1,2,16,128]{7,6,0,5,4,3,2,1:T(8,128)(2,1)S(1)}, bf16[4,1,2,1,1,2,16,128]{7,6,0,5,4,3,2,1:T(8,128)(2,1)S(1)}, u32[]{:S(2)}, u32[]{:S(2)}) collective-permute-start(bf16[4,1,2,1,1,2,16,128]{7,6,0,5,4,3,2,1:T(8,128)(2,1)S(1)} %dynamic-slice_convert_fusion.4), channel_id=1, source_target_pairs={{0,8},{4,12},{8,0},{12,4},{16,24},{20,28},{24,16},{28,20},{1,9},{5... | collective-permute-start | bytes 196616 | tf_op jit(solution)/shard_map/ppermute | solution.py:48
  62.4 3.3 %collective-permute-start.14 = (bf16[4,1,2,2,1,1,16,128]{7,6,0,5,4,3,2,1:T(8,128)(2,1)S(1)}, bf16[4,1,2,2,1,1,16,128]{7,6,0,5,4,3,2,1:T(8,128)(2,1)S(1)}, u32[]{:S(2)}, u32[]{:S(2)}) collective-permute-start(bf16[4,1,2,2,1,1,16,128]{7,6,0,5,4,3,2,1:T(8,128)(2,1)S(1)} %dynamic-slice_convert_fusion.3), channel_id=1, source_target_pairs={{0,16},{4,20},{8,24},{12,28},{16,0},{20,4},{24,8},{28,12},{1,17},{... | collective-permute-start | bytes 196616 | tf_op jit(solution)/shard_map/ppermute | solution.py:48
  66.6 2.6 %collective-permute-start.11 = (bf16[4,1,2,1,1,1,16,128]{7,6,0,5,4,3,2,1:T(8,128)(2,1)S(1)}, bf16[4,1,2,1,1,1,16,128]{7,6,0,5,4,3,2,1:T(8,128)(2,1)S(1)}, u32[]{:S(2)}, u32[]{:S(2)}) collective-permute-start(bf16[4,1,2,1,1,1,16,128]{7,6,0,5,4,3,2,1:T(8,128)(2,1)S(1)} %dynamic-slice_convert_fusion.7), channel_id=1, source_target_pairs={{0,16},{4,20},{8,24},{12,28},{16,0},{20,4},{24,8},{28,12},{1,17},{... | collective-permute-start | bytes 98312 | tf_op jit(solution)/shard_map/ppermute | solution.py:48
  69.3 1.7 %collective-permute-start.15 = (bf16[4,1,1,2,1,1,16,128]{7,6,0,5,4,3,2,1:T(8,128)(2,1)S(1)}, bf16[4,1,1,2,1,1,16,128]{7,6,0,5,4,3,2,1:T(8,128)(2,1)S(1)}, u32[]{:S(2)}, u32[]{:S(2)}) collective-permute-start(bf16[4,1,1,2,1,1,16,128]{7,6,0,5,4,3,2,1:T(8,128)(2,1)S(1)} %dynamic-slice_convert_fusion.6), channel_id=1, source_target_pairs={{0,2},{1,3},{2,0},{3,1},{4,6},{5,7},{6,4},{7,5},{8,10},{9,11},{10,... | collective-permute-start | bytes 98312 | tf_op jit(solution)/shard_map/ppermute | solution.py:48
  73.4 1.5 %collective-permute-start.16 = (bf16[4,1,1,1,1,1,16,128]{7,6,0,5,4,3,2,1:T(8,128)(2,1)S(1)}, bf16[4,1,1,1,1,1,16,128]{7,6,0,5,4,3,2,1:T(8,128)(2,1)S(1)}, u32[]{:S(2)}, u32[]{:S(2)}) collective-permute-start(bf16[4,1,1,1,1,1,16,128]{7,6,0,5,4,3,2,1:T(8,128)(2,1)S(1)} %dynamic-slice_convert_fusion.9), channel_id=1, source_target_pairs={{0,4},{4,0},{8,12},{12,8},{16,20},{20,16},{24,28},{28,24},{1,5},{5... | collective-permute-start | bytes 49160 | tf_op jit(solution)/shard_map/ppermute | solution.py:48
  79.2 1.8 %fusion.13 = bf16[12,16,128]{2,1,0:T(8,128)(2,1)S(1)} fusion(bf16[12,4,136,128]{3,2,1,0:T(8,128)(2,1)} %all-gather.2.cloned.1.call-done, bf16[12,4,16,128]{3,2,1,0:T(8,128)(2,1)S(1)} %bitcast.132, pred[12,4]{1,0:T(8,128)(4,1)S(1)} %copy.84), kind=kOutput, calls=%fused_computation.17 | convolution fusion | flops 25288704 | bytes 1818672 | tf_op jit(solution)/shard_map/nerc,necd->nrd/dot_general | solution.py:100
  81.0 2.1 %collective-permute-start.17 = (bf16[4,1,1,1,1,1,16,128]{7,6,0,5,4,3,2,1:T(8,128)(2,1)S(1)}, bf16[4,1,1,1,1,1,16,128]{7,6,0,5,4,3,2,1:T(8,128)(2,1)S(1)}, u32[]{:S(2)}, u32[]{:S(2)}) collective-permute-start(bf16[4,1,1,1,1,1,16,128]{7,6,0,5,4,3,2,1:T(8,128)(2,1)S(1)} %get-tuple-element.32), channel_id=1, source_target_pairs={{0,16},{4,20},{8,24},{12,28},{16,0},{20,4},{24,8},{28,12},{1,17},{... | collective-permute-start | bytes 49160 | tf_op jit(solution)/shard_map/ppermute | solution.py:53
  85.7 1.7 %collective-permute-start.18 = (bf16[4,1,1,1,1,2,16,128]{7,6,0,5,4,3,2,1:T(8,128)(2,1)S(1)}, bf16[4,1,1,1,1,2,16,128]{7,6,0,5,4,3,2,1:T(8,128)(2,1)S(1)}, u32[]{:S(2)}, u32[]{:S(2)}) collective-permute-start(bf16[4,1,1,1,1,2,16,128]{7,6,0,5,4,3,2,1:T(8,128)(2,1)S(1)} %maximum_select_fusion.18), channel_id=1, source_target_pairs={{0,8},{4,12},{8,0},{12,4},{16,24},{20,28},{24,16},{28,20},{1,9},{5... | collective-permute-start | bytes 98312 | tf_op jit(solution)/shard_map/ppermute | solution.py:53
  87.4 1.5 %collective-permute-start.23 = (bf16[4,1,2,1,1,1,16,128]{7,6,0,2,5,4,3,1:T(8,128)(2,1)S(1)}, bf16[4,1,2,1,1,1,16,128]{7,6,0,2,5,4,3,1:T(8,128)(2,1)S(1)}, u32[]{:S(2)}, u32[]{:S(2)}) collective-permute-start(bf16[4,1,2,1,1,1,16,128]{7,6,0,2,5,4,3,1:T(8,128)(2,1)S(1)} %fusion.27), channel_id=1, source_target_pairs={{0,16},{4,20},{8,24},{12,28},{16,0},{20,4},{24,8},{28,12},{1,17},{... | collective-permute-start | bytes 98312 | tf_op jit(solution)/shard_map/ppermute | solution.py:53
  89.0 1.9 %collective-permute-start.28 = (bf16[4,1,1,2,1,1,16,128]{7,6,0,5,4,3,2,1:T(8,128)(2,1)S(1)}, bf16[4,1,1,2,1,1,16,128]{7,6,0,5,4,3,2,1:T(8,128)(2,1)S(1)}, u32[]{:S(2)}, u32[]{:S(2)}) collective-permute-start(bf16[4,1,1,2,1,1,16,128]{7,6,0,5,4,3,2,1:T(8,128)(2,1)S(1)} %maximum_select_fusion.22), channel_id=1, source_target_pairs={{0,2},{1,3},{2,0},{3,1},{4,6},{5,7},{6,4},{7,5},{8,10},{9,11},{10,... | collective-permute-start | bytes 98312 | tf_op jit(solution)/shard_map/ppermute | solution.py:53
  91.5 1.9 %collective-permute-done.23 = bf16[4,1,2,1,1,1,16,128]{7,6,0,2,5,4,3,1:T(8,128)(2,1)S(1)} collective-permute-done((bf16[4,1,2,1,1,1,16,128]{7,6,0,2,5,4,3,1:T(8,128)(2,1)S(1)}, bf16[4,1,2,1,1,1,16,128]{7,6,0,2,5,4,3,1:T(8,128)(2,1)S(1)}, u32[]{:S(2)}, u32[]{:S(2)}) %collective-permute-start.23) | collective-permute-done | bytes 32800 | tf_op jit(solution)/shard_map/ppermute | solution.py:53
  93.5 2.7 %collective-permute-start.29 = (bf16[4,1,2,2,1,1,16,128]{7,6,0,5,4,3,2,1:T(8,128)(2,1)S(1)}, bf16[4,1,2,2,1,1,16,128]{7,6,0,5,4,3,2,1:T(8,128)(2,1)S(1)}, u32[]{:S(2)}, u32[]{:S(2)}) collective-permute-start(bf16[4,1,2,2,1,1,16,128]{7,6,0,5,4,3,2,1:T(8,128)(2,1)S(1)} %fusion.26), channel_id=1, source_target_pairs={{0,16},{4,20},{8,24},{12,28},{16,0},{20,4},{24,8},{28,12},{1,17},{... | collective-permute-start | bytes 196616 | tf_op jit(solution)/shard_map/ppermute | solution.py:53
  96.4 1.4 %collective-permute-start.20 = (bf16[4,1,1,2,2,2,16,128]{7,6,0,5,4,3,2,1:T(8,128)(2,1)S(1)}, bf16[4,1,1,2,2,2,16,128]{7,6,0,5,4,3,2,1:T(8,128)(2,1)S(1)}, u32[]{:S(2)}, u32[]{:S(2)}) collective-permute-start(bf16[4,1,1,2,2,2,16,128]{7,6,0,5,4,3,2,1:T(8,128)(2,1)S(1)} %maximum_select_fusion.7), channel_id=1, source_target_pairs={{0,2},{1,3},{2,0},{3,1},{4,6},{5,7},{6,4},{7,5},{8,10},{9,11},{10,... | collective-permute-start | bytes 393224 | tf_op jit(solution)/shard_map/ppermute | solution.py:53
  97.8 1.9 %collective-permute-start.25 = (bf16[4,1,2,1,2,2,16,128]{7,6,0,5,4,3,2,1:T(8,128)(2,1)S(1)}, bf16[4,1,2,1,2,2,16,128]{7,6,0,5,4,3,2,1:T(8,128)(2,1)S(1)}, u32[]{:S(2)}, u32[]{:S(2)}) collective-permute-start(bf16[4,1,2,1,2,2,16,128]{7,6,0,5,4,3,2,1:T(8,128)(2,1)S(1)} %maximum_select_fusion.9), channel_id=1, source_target_pairs={{0,4},{4,0},{8,12},{12,8},{16,20},{20,16},{24,28},{28,24},{1,5},{5... | collective-permute-start | bytes 393224 | tf_op jit(solution)/shard_map/ppermute | solution.py:53
  102.9 1.9 %collective-permute-done.30 = bf16[4,1,2,2,1,2,16,128]{7,6,0,5,4,3,2,1:T(8,128)(2,1)S(1)} collective-permute-done((bf16[4,1,2,2,1,2,16,128]{7,6,0,5,4,3,2,1:T(8,128)(2,1)S(1)}, bf16[4,1,2,2,1,2,16,128]{7,6,0,5,4,3,2,1:T(8,128)(2,1)S(1)}, u32[]{:S(2)}, u32[]{:S(2)}) %collective-permute-start.30) | collective-permute-done | bytes 131104 | tf_op jit(solution)/shard_map/ppermute | solution.py:53
  107.7 1.4 %pad_maximum_fusion.1 = bf16[12,512,128]{2,1,0:T(8,128)(2,1)} fusion(bf16[4,512,128]{2,1,0:T(8,128)(2,1)S(1)} %bitcast.125, bf16[4,512,128]{2,1,0:T(8,128)(2,1)S(1)} %bitcast.124, bf16[4,512,128]{2,1,0:T(8,128)(2,1)S(1)} %bitcast.123), kind=kLoop, calls=%fused_computation.15 | loop fusion | flops 1572864 | bytes 3145728 | tf_op jit(solution)/shard_map/concatenate | solution.py:107
  109.1 2.2 %gather_fusion.2 = bf16[8,512,128]{2,1,0:T(8,128)(2,1)S(1)} fusion(bf16[12,512,128]{2,1,0:T(8,128)(2,1)} %pad_maximum_fusion.1, s32[1024]{0:T(1024)S(1)} %pad_clamp_fusion), kind=kCustom, calls=%fused_computation.2 | custom fusion | bytes 2097184 | tf_op jit(solution)/shard_map/jit(_take)/gather | solution.py:109
  111.3 1.7 %fusion.17 = f32[4,512,256,1]{2,1,3,0:T(8,128)S(1)} fusion(bf16[4,2,256,128]{3,2,1,0:T(8,128)(2,1)} %param.11, bf16[4,2,512,128]{3,2,1,0:T(8,128)(2,1)S(1)} %bitcast.121, pred[4,2]{1,0:T(4,128)(4,1)S(1)} %copy.82), kind=kOutput, calls=%fused_computation.19 | convolution fusion | flops 268959744 | bytes 3670024 | tf_op jit(solution)/shard_map/jqrc,jqbc->jrb/dot_general | solution.py:110
  (154 shorter events, 29.4 us)
Async XLA Ops:
  6.5 70.7 %all-gather.2.cloned.1.call-start = ((), (), s32[]{:S(2)}) async-start(), calls=%async_computation | async-start | bytes 2088960 | tf_op jit(solution)/shard_map/all_gather | solution.py:69
  22.1 23.9 %collective-permute-start.4 = (f32[4,1,2,2,2,2,16,128]{7,6,0,5,4,3,2,1:T(8,128)}, f32[4,1,2,2,2,2,16,128]{7,6,0,5,4,3,2,1:T(8,128)}, u32[]{:S(2)}, u32[]{:S(2)}) collective-permute-start(f32[4,1,2,2,2,2,16,128]{7,6,0,5,4,3,2,1:T(8,128)} %copy.110), channel_id=1, source_target_pairs={{0,1},{1,0},{2,3},{3,2},{4,5},{5,4},{6,7},{7,6},{8,9},{9,8},{10,11... | collective-permute-start | bytes 1572872 | tf_op jit(solution)/shard_map/ppermute | solution.py:48
  23.4 23.8 %collective-permute-start.3 = (f32[4,1,2,2,2,2,16,128]{7,6,0,5,4,3,2,1:T(8,128)}, f32[4,1,2,2,2,2,16,128]{7,6,0,5,4,3,2,1:T(8,128)}, u32[]{:S(2)}, u32[]{:S(2)}) collective-permute-start(f32[4,1,2,2,2,2,16,128]{7,6,0,5,4,3,2,1:T(8,128)} %copy.108), channel_id=1, source_target_pairs={{0,1},{1,0},{2,3},{3,2},{4,5},{5,4},{6,7},{7,6},{8,9},{9,8},{10,11... | collective-permute-start | bytes 1572872 | tf_op jit(solution)/shard_map/ppermute | solution.py:48
  25.3 23.1 %collective-permute-start.2 = (f32[4,1,2,2,2,2,16,128]{7,6,0,5,4,3,2,1:T(8,128)}, f32[4,1,2,2,2,2,16,128]{7,6,0,5,4,3,2,1:T(8,128)}, u32[]{:S(2)}, u32[]{:S(2)}) collective-permute-start(f32[4,1,2,2,2,2,16,128]{7,6,0,5,4,3,2,1:T(8,128)} %copy.106), channel_id=1, source_target_pairs={{0,1},{1,0},{2,3},{3,2},{4,5},{5,4},{6,7},{7,6},{8,9},{9,8},{10,11... | collective-permute-start | bytes 1572872 | tf_op jit(solution)/shard_map/ppermute | solution.py:48
  26.6 4.5 %collective-permute-start = (bf16[1,512,256]{2,1,0:T(8,128)(2,1)}, bf16[1,512,256]{2,1,0:T(8,128)(2,1)S(1)}, u32[]{:S(2)}, u32[]{:S(2)}) collective-permute-start(bf16[1,512,256]{2,1,0:T(8,128)(2,1)} %get-tuple-element.22), channel_id=1, source_target_pairs={{0,1},{1,2},{2,3},{3,4},{4,5},{5,6},{6,7},{7,8},{8,9},{9,10},{10,1... | collective-permute-start | bytes 786440 | tf_op jit(solution)/shard_map/ppermute | solution.py:15
  28.6 5.9 %collective-permute-start.1 = (bf16[1,512,256]{2,1,0:T(8,128)(2,1)}, bf16[1,512,256]{2,1,0:T(8,128)(2,1)}, u32[]{:S(2)}, u32[]{:S(2)}) collective-permute-start(bf16[1,512,256]{2,1,0:T(8,128)(2,1)} %get-tuple-element.23), channel_id=1, source_target_pairs={{1,0},{2,1},{3,2},{4,3},{5,4},{6,5},{7,6},{8,7},{9,8},{10,9},{11,1... | collective-permute-start | bytes 786440 | tf_op jit(solution)/shard_map/ppermute | solution.py:17
  49.6 7.6 %collective-permute-start.5 = (bf16[4,1,1,2,2,2,16,128]{7,6,0,5,4,3,2,1:T(8,128)(2,1)S(1)}, bf16[4,1,1,2,2,2,16,128]{7,6,0,5,4,3,2,1:T(8,128)(2,1)S(1)}, u32[]{:S(2)}, u32[]{:S(2)}) collective-permute-start(bf16[4,1,1,2,2,2,16,128]{7,6,0,5,4,3,2,1:T(8,128)(2,1)S(1)} %dynamic-slice_convert_fusion.2), channel_id=1, source_target_pairs={{0,2},{1,3},{2,0},{3,1},{4,6},{5,7},{6,4},{7,5},{8,10},{9,11},{10,... | collective-permute-start | bytes 393224 | tf_op jit(solution)/shard_map/ppermute | solution.py:48
  53.9 6.0 %collective-permute-start.9 = (bf16[4,1,2,1,2,2,16,128]{7,6,0,5,4,3,2,1:T(8,128)(2,1)S(1)}, bf16[4,1,2,1,2,2,16,128]{7,6,0,5,4,3,2,1:T(8,128)(2,1)S(1)}, u32[]{:S(2)}, u32[]{:S(2)}) collective-permute-start(bf16[4,1,2,1,2,2,16,128]{7,6,0,5,4,3,2,1:T(8,128)(2,1)S(1)} %dynamic-slice_convert_fusion.1), channel_id=1, source_target_pairs={{0,4},{4,0},{8,12},{12,8},{16,20},{20,16},{24,28},{28,24},{1,5},{5... | collective-permute-start | bytes 393224 | tf_op jit(solution)/shard_map/ppermute | solution.py:48
  55.5 6.9 %collective-permute-start.13 = (bf16[4,1,2,2,1,2,16,128]{7,6,0,5,4,3,2,1:T(8,128)(2,1)S(1)}, bf16[4,1,2,2,1,2,16,128]{7,6,0,5,4,3,2,1:T(8,128)(2,1)S(1)}, u32[]{:S(2)}, u32[]{:S(2)}) collective-permute-start(bf16[4,1,2,2,1,2,16,128]{7,6,0,5,4,3,2,1:T(8,128)(2,1)S(1)} %dynamic-slice_convert_fusion), channel_id=1, source_target_pairs={{0,8},{4,12},{8,0},{12,4},{16,24},{20,28},{24,16},{28,20},{1,9},{5... | collective-permute-start | bytes 393224 | tf_op jit(solution)/shard_map/ppermute | solution.py:48
  57.2 8.5 %collective-permute-start.6 = (bf16[4,1,1,1,2,2,16,128]{7,6,0,5,4,3,2,1:T(8,128)(2,1)S(1)}, bf16[4,1,1,1,2,2,16,128]{7,6,0,5,4,3,2,1:T(8,128)(2,1)S(1)}, u32[]{:S(2)}, u32[]{:S(2)}) collective-permute-start(bf16[4,1,1,1,2,2,16,128]{7,6,0,5,4,3,2,1:T(8,128)(2,1)S(1)} %dynamic-slice_convert_fusion.5), channel_id=1, source_target_pairs={{0,4},{4,0},{8,12},{12,8},{16,20},{20,16},{24,28},{28,24},{1,5},{5... | collective-permute-start | bytes 196616 | tf_op jit(solution)/shard_map/ppermute | solution.py:48
  60.0 6.6 %collective-permute-start.10 = (bf16[4,1,2,1,1,2,16,128]{7,6,0,5,4,3,2,1:T(8,128)(2,1)S(1)}, bf16[4,1,2,1,1,2,16,128]{7,6,0,5,4,3,2,1:T(8,128)(2,1)S(1)}, u32[]{:S(2)}, u32[]{:S(2)}) collective-permute-start(bf16[4,1,2,1,1,2,16,128]{7,6,0,5,4,3,2,1:T(8,128)(2,1)S(1)} %dynamic-slice_convert_fusion.4), channel_id=1, source_target_pairs={{0,8},{4,12},{8,0},{12,4},{16,24},{20,28},{24,16},{28,20},{1,9},{5... | collective-permute-start | bytes 196616 | tf_op jit(solution)/shard_map/ppermute | solution.py:48
  62.4 6.9 %collective-permute-start.14 = (bf16[4,1,2,2,1,1,16,128]{7,6,0,5,4,3,2,1:T(8,128)(2,1)S(1)}, bf16[4,1,2,2,1,1,16,128]{7,6,0,5,4,3,2,1:T(8,128)(2,1)S(1)}, u32[]{:S(2)}, u32[]{:S(2)}) collective-permute-start(bf16[4,1,2,2,1,1,16,128]{7,6,0,5,4,3,2,1:T(8,128)(2,1)S(1)} %dynamic-slice_convert_fusion.3), channel_id=1, source_target_pairs={{0,16},{4,20},{8,24},{12,28},{16,0},{20,4},{24,8},{28,12},{1,17},{... | collective-permute-start | bytes 196616 | tf_op jit(solution)/shard_map/ppermute | solution.py:48
  65.8 5.3 %collective-permute-start.7 = (bf16[4,1,1,1,1,2,16,128]{7,6,0,5,4,3,2,1:T(8,128)(2,1)S(1)}, bf16[4,1,1,1,1,2,16,128]{7,6,0,5,4,3,2,1:T(8,128)(2,1)S(1)}, u32[]{:S(2)}, u32[]{:S(2)}) collective-permute-start(bf16[4,1,1,1,1,2,16,128]{7,6,0,5,4,3,2,1:T(8,128)(2,1)S(1)} %dynamic-slice_convert_fusion.8), channel_id=1, source_target_pairs={{0,8},{4,12},{8,0},{12,4},{16,24},{20,28},{24,16},{28,20},{1,9},{5... | collective-permute-start | bytes 98312 | tf_op jit(solution)/shard_map/ppermute | solution.py:48
  66.6 5.7 %collective-permute-start.11 = (bf16[4,1,2,1,1,1,16,128]{7,6,0,5,4,3,2,1:T(8,128)(2,1)S(1)}, bf16[4,1,2,1,1,1,16,128]{7,6,0,5,4,3,2,1:T(8,128)(2,1)S(1)}, u32[]{:S(2)}, u32[]{:S(2)}) collective-permute-start(bf16[4,1,2,1,1,1,16,128]{7,6,0,5,4,3,2,1:T(8,128)(2,1)S(1)} %dynamic-slice_convert_fusion.7), channel_id=1, source_target_pairs={{0,16},{4,20},{8,24},{12,28},{16,0},{20,4},{24,8},{28,12},{1,17},{... | collective-permute-start | bytes 98312 | tf_op jit(solution)/shard_map/ppermute | solution.py:48
  69.3 4.0 %collective-permute-start.15 = (bf16[4,1,1,2,1,1,16,128]{7,6,0,5,4,3,2,1:T(8,128)(2,1)S(1)}, bf16[4,1,1,2,1,1,16,128]{7,6,0,5,4,3,2,1:T(8,128)(2,1)S(1)}, u32[]{:S(2)}, u32[]{:S(2)}) collective-permute-start(bf16[4,1,1,2,1,1,16,128]{7,6,0,5,4,3,2,1:T(8,128)(2,1)S(1)} %dynamic-slice_convert_fusion.6), channel_id=1, source_target_pairs={{0,2},{1,3},{2,0},{3,1},{4,6},{5,7},{6,4},{7,5},{8,10},{9,11},{10,... | collective-permute-start | bytes 98312 | tf_op jit(solution)/shard_map/ppermute | solution.py:48
  71.1 4.7 %collective-permute-start.8 = (bf16[4,1,1,1,1,1,16,128]{7,6,0,5,4,3,2,1:T(8,128)(2,1)S(1)}, bf16[4,1,1,1,1,1,16,128]{7,6,0,5,4,3,2,1:T(8,128)(2,1)S(1)}, u32[]{:S(2)}, u32[]{:S(2)}) collective-permute-start(bf16[4,1,1,1,1,1,16,128]{7,6,0,5,4,3,2,1:T(8,128)(2,1)S(1)} %dynamic-slice_convert_fusion.11), channel_id=1, source_target_pairs={{0,16},{4,20},{8,24},{12,28},{16,0},{20,4},{24,8},{28,12},{1,17},{... | collective-permute-start | bytes 49160 | tf_op jit(solution)/shard_map/ppermute | solution.py:48
  72.3 3.8 %collective-permute-start.12 = (bf16[4,1,1,1,1,1,16,128]{7,6,0,5,4,3,2,1:T(8,128)(2,1)S(1)}, bf16[4,1,1,1,1,1,16,128]{7,6,0,5,4,3,2,1:T(8,128)(2,1)S(1)}, u32[]{:S(2)}, u32[]{:S(2)}) collective-permute-start(bf16[4,1,1,1,1,1,16,128]{7,6,0,5,4,3,2,1:T(8,128)(2,1)S(1)} %dynamic-slice_convert_fusion.10), channel_id=1, source_target_pairs={{0,2},{1,3},{2,0},{3,1},{4,6},{5,7},{6,4},{7,5},{8,10},{9,11},{10,... | collective-permute-start | bytes 49160 | tf_op jit(solution)/shard_map/ppermute | solution.py:48
  73.4 3.8 %collective-permute-start.16 = (bf16[4,1,1,1,1,1,16,128]{7,6,0,5,4,3,2,1:T(8,128)(2,1)S(1)}, bf16[4,1,1,1,1,1,16,128]{7,6,0,5,4,3,2,1:T(8,128)(2,1)S(1)}, u32[]{:S(2)}, u32[]{:S(2)}) collective-permute-start(bf16[4,1,1,1,1,1,16,128]{7,6,0,5,4,3,2,1:T(8,128)(2,1)S(1)} %dynamic-slice_convert_fusion.9), channel_id=1, source_target_pairs={{0,4},{4,0},{8,12},{12,8},{16,20},{20,16},{24,28},{28,24},{1,5},{5... | collective-permute-start | bytes 49160 | tf_op jit(solution)/shard_map/ppermute | solution.py:48
  81.0 4.7 %collective-permute-start.17 = (bf16[4,1,1,1,1,1,16,128]{7,6,0,5,4,3,2,1:T(8,128)(2,1)S(1)}, bf16[4,1,1,1,1,1,16,128]{7,6,0,5,4,3,2,1:T(8,128)(2,1)S(1)}, u32[]{:S(2)}, u32[]{:S(2)}) collective-permute-start(bf16[4,1,1,1,1,1,16,128]{7,6,0,5,4,3,2,1:T(8,128)(2,1)S(1)} %get-tuple-element.32), channel_id=1, source_target_pairs={{0,16},{4,20},{8,24},{12,28},{16,0},{20,4},{24,8},{28,12},{1,17},{... | collective-permute-start | bytes 49160 | tf_op jit(solution)/shard_map/ppermute | solution.py:53
  83.3 4.1 %collective-permute-start.22 = (bf16[4,1,1,1,1,1,16,128]{7,6,0,5,4,3,2,1:T(8,128)(2,1)S(1)}, bf16[4,1,1,1,1,1,16,128]{7,6,0,5,4,3,2,1:T(8,128)(2,1)S(1)}, u32[]{:S(2)}, u32[]{:S(2)}) collective-permute-start(bf16[4,1,1,1,1,1,16,128]{7,6,0,5,4,3,2,1:T(8,128)(2,1)S(1)} %get-tuple-element.33), channel_id=1, source_target_pairs={{0,2},{1,3},{2,0},{3,1},{4,6},{5,7},{6,4},{7,5},{8,10},{9,11},{10,... | collective-permute-start | bytes 49160 | tf_op jit(solution)/shard_map/ppermute | solution.py:53
  84.3 4.6 %collective-permute-start.27 = (bf16[4,1,1,1,1,1,16,128]{7,6,0,5,4,3,2,1:T(8,128)(2,1)S(1)}, bf16[4,1,1,1,1,1,16,128]{7,6,0,5,4,3,2,1:T(8,128)(2,1)S(1)}, u32[]{:S(2)}, u32[]{:S(2)}) collective-permute-start(bf16[4,1,1,1,1,1,16,128]{7,6,0,5,4,3,2,1:T(8,128)(2,1)S(1)} %get-tuple-element.34), channel_id=1, source_target_pairs={{0,4},{4,0},{8,12},{12,8},{16,20},{20,16},{24,28},{28,24},{1,5},{5... | collective-permute-start | bytes 49160 | tf_op jit(solution)/shard_map/ppermute | solution.py:53
  85.7 5.2 %collective-permute-start.18 = (bf16[4,1,1,1,1,2,16,128]{7,6,0,5,4,3,2,1:T(8,128)(2,1)S(1)}, bf16[4,1,1,1,1,2,16,128]{7,6,0,5,4,3,2,1:T(8,128)(2,1)S(1)}, u32[]{:S(2)}, u32[]{:S(2)}) collective-permute-start(bf16[4,1,1,1,1,2,16,128]{7,6,0,5,4,3,2,1:T(8,128)(2,1)S(1)} %maximum_select_fusion.18), channel_id=1, source_target_pairs={{0,8},{4,12},{8,0},{12,4},{16,24},{20,28},{24,16},{28,20},{1,9},{5... | collective-permute-start | bytes 98312 | tf_op jit(solution)/shard_map/ppermute | solution.py:53
  87.4 5.9 %collective-permute-start.23 = (bf16[4,1,2,1,1,1,16,128]{7,6,0,2,5,4,3,1:T(8,128)(2,1)S(1)}, bf16[4,1,2,1,1,1,16,128]{7,6,0,2,5,4,3,1:T(8,128)(2,1)S(1)}, u32[]{:S(2)}, u32[]{:S(2)}) collective-permute-start(bf16[4,1,2,1,1,1,16,128]{7,6,0,2,5,4,3,1:T(8,128)(2,1)S(1)} %fusion.27), channel_id=1, source_target_pairs={{0,16},{4,20},{8,24},{12,28},{16,0},{20,4},{24,8},{28,12},{1,17},{... | collective-permute-start | bytes 98312 | tf_op jit(solution)/shard_map/ppermute | solution.py:53
  89.0 4.5 %collective-permute-start.28 = (bf16[4,1,1,2,1,1,16,128]{7,6,0,5,4,3,2,1:T(8,128)(2,1)S(1)}, bf16[4,1,1,2,1,1,16,128]{7,6,0,5,4,3,2,1:T(8,128)(2,1)S(1)}, u32[]{:S(2)}, u32[]{:S(2)}) collective-permute-start(bf16[4,1,1,2,1,1,16,128]{7,6,0,5,4,3,2,1:T(8,128)(2,1)S(1)} %maximum_select_fusion.22), channel_id=1, source_target_pairs={{0,2},{1,3},{2,0},{3,1},{4,6},{5,7},{6,4},{7,5},{8,10},{9,11},{10,... | collective-permute-start | bytes 98312 | tf_op jit(solution)/shard_map/ppermute | solution.py:53
  90.9 5.4 %collective-permute-start.19 = (bf16[4,1,1,1,2,2,16,128]{7,6,0,5,4,3,2,1:T(8,128)(2,1)S(1)}, bf16[4,1,1,1,2,2,16,128]{7,6,0,5,4,3,2,1:T(8,128)(2,1)S(1)}, u32[]{:S(2)}, u32[]{:S(2)}) collective-permute-start(bf16[4,1,1,1,2,2,16,128]{7,6,0,5,4,3,2,1:T(8,128)(2,1)S(1)} %maximum_select_fusion.13), channel_id=1, source_target_pairs={{0,4},{4,0},{8,12},{12,8},{16,20},{20,16},{24,28},{28,24},{1,5},{5... | collective-permute-start | bytes 196616 | tf_op jit(solution)/shard_map/ppermute | solution.py:53
  93.4 4.4 %collective-permute-start.24 = (bf16[4,1,2,1,1,2,16,128]{7,6,0,5,4,3,2,1:T(8,128)(2,1)S(1)}, bf16[4,1,2,1,1,2,16,128]{7,6,0,5,4,3,2,1:T(8,128)(2,1)S(1)}, u32[]{:S(2)}, u32[]{:S(2)}) collective-permute-start(bf16[4,1,2,1,1,2,16,128]{7,6,0,5,4,3,2,1:T(8,128)(2,1)S(1)} %copy.88), channel_id=1, source_target_pairs={{0,8},{4,12},{8,0},{12,4},{16,24},{20,28},{24,16},{28,20},{1,9},{5... | collective-permute-start | bytes 196616 | tf_op jit(solution)/shard_map/ppermute | solution.py:53
  93.5 6.2 %collective-permute-start.29 = (bf16[4,1,2,2,1,1,16,128]{7,6,0,5,4,3,2,1:T(8,128)(2,1)S(1)}, bf16[4,1,2,2,1,1,16,128]{7,6,0,5,4,3,2,1:T(8,128)(2,1)S(1)}, u32[]{:S(2)}, u32[]{:S(2)}) collective-permute-start(bf16[4,1,2,2,1,1,16,128]{7,6,0,5,4,3,2,1:T(8,128)(2,1)S(1)} %fusion.26), channel_id=1, source_target_pairs={{0,16},{4,20},{8,24},{12,28},{16,0},{20,4},{24,8},{28,12},{1,17},{... | collective-permute-start | bytes 196616 | tf_op jit(solution)/shard_map/ppermute | solution.py:53
  96.4 5.0 %collective-permute-start.20 = (bf16[4,1,1,2,2,2,16,128]{7,6,0,5,4,3,2,1:T(8,128)(2,1)S(1)}, bf16[4,1,1,2,2,2,16,128]{7,6,0,5,4,3,2,1:T(8,128)(2,1)S(1)}, u32[]{:S(2)}, u32[]{:S(2)}) collective-permute-start(bf16[4,1,1,2,2,2,16,128]{7,6,0,5,4,3,2,1:T(8,128)(2,1)S(1)} %maximum_select_fusion.7), channel_id=1, source_target_pairs={{0,2},{1,3},{2,0},{3,1},{4,6},{5,7},{6,4},{7,5},{8,10},{9,11},{10,... | collective-permute-start | bytes 393224 | tf_op jit(solution)/shard_map/ppermute | solution.py:53
  97.8 5.0 %collective-permute-start.25 = (bf16[4,1,2,1,2,2,16,128]{7,6,0,5,4,3,2,1:T(8,128)(2,1)S(1)}, bf16[4,1,2,1,2,2,16,128]{7,6,0,5,4,3,2,1:T(8,128)(2,1)S(1)}, u32[]{:S(2)}, u32[]{:S(2)}) collective-permute-start(bf16[4,1,2,1,2,2,16,128]{7,6,0,5,4,3,2,1:T(8,128)(2,1)S(1)} %maximum_select_fusion.9), channel_id=1, source_target_pairs={{0,4},{4,0},{8,12},{12,8},{16,20},{20,16},{24,28},{28,24},{1,5},{5... | collective-permute-start | bytes 393224 | tf_op jit(solution)/shard_map/ppermute | solution.py:53
  99.8 5.0 %collective-permute-start.30 = (bf16[4,1,2,2,1,2,16,128]{7,6,0,5,4,3,2,1:T(8,128)(2,1)S(1)}, bf16[4,1,2,2,1,2,16,128]{7,6,0,5,4,3,2,1:T(8,128)(2,1)S(1)}, u32[]{:S(2)}, u32[]{:S(2)}) collective-permute-start(bf16[4,1,2,2,1,2,16,128]{7,6,0,5,4,3,2,1:T(8,128)(2,1)S(1)} %maximum_select_fusion.11), channel_id=1, source_target_pairs={{0,8},{4,12},{8,0},{12,4},{16,24},{20,28},{24,16},{28,20},{1,9},{5... | collective-permute-start | bytes 393224 | tf_op jit(solution)/shard_map/ppermute | solution.py:53
  101.4 3.6 %collective-permute-start.21 = (bf16[4,1,2,2,2,2,16,128]{7,6,0,5,4,3,2,1:T(8,128)(2,1)S(1)}, bf16[4,1,2,2,2,2,16,128]{7,6,0,5,4,3,2,1:T(8,128)(2,1)S(1)}, u32[]{:S(2)}, u32[]{:S(2)}) collective-permute-start(bf16[4,1,2,2,2,2,16,128]{7,6,0,5,4,3,2,1:T(8,128)(2,1)S(1)} %maximum_select_fusion.3), channel_id=1, source_target_pairs={{0,1},{1,0},{2,3},{3,2},{4,5},{5,4},{6,7},{7,6},{8,9},{9,8},{10,11... | collective-permute-start | bytes 786440 | tf_op jit(solution)/shard_map/ppermute | solution.py:53
  102.8 2.3 %collective-permute-start.26 = (bf16[4,1,2,2,2,2,16,128]{7,6,0,5,4,3,2,1:T(8,128)(2,1)S(1)}, bf16[4,1,2,2,2,2,16,128]{7,6,0,5,4,3,2,1:T(8,128)(2,1)S(1)}, u32[]{:S(2)}, u32[]{:S(2)}) collective-permute-start(bf16[4,1,2,2,2,2,16,128]{7,6,0,5,4,3,2,1:T(8,128)(2,1)S(1)} %maximum_select_fusion.4), channel_id=1, source_target_pairs={{0,1},{1,0},{2,3},{3,2},{4,5},{5,4},{6,7},{7,6},{8,9},{9,8},{10,11... | collective-permute-start | bytes 786440 | tf_op jit(solution)/shard_map/ppermute | solution.py:53
  (12 other events, 79.2 us)
Sparse Core Ops, SparseCore 0:
  31.0 24.7 all-gather.1

commit v6 on v5

--- a/solution.py
+++ b/solution.py
@@ -90,7 +90,7 @@
     picked = jnp.take(extended, margin, axis=0)
     local = jnp.einsum("jerb,jebc->jrc", picked, inverse_blocks, preferred_element_type=jnp.float32)
     for step in range(nb):
-        wire = jnp.float32 if step == 0 else jnp.bfloat16
+        wire = jnp.float32
         parts = [halve(x, 1 + orders[s][step], *bits[orders[s][step]], wire) for s, x in enumerate(parts)]
         if step == 0:
             local, parts = lax.optimization_barrier((local, parts))

time: 122 us -> 130 us (1.066)
  waiting for transfers between devices: 12.9 us -> 20 us
    ppermute x15, waiting for transfers between devices: 2.39 us -> 7.72 us  [halve(): lax.ppermute(send.astype(wire), axis, pairs(axis, mask)).astype(x.dtype)]
    ppermute x15, waiting for transfers between devices: 7.19 us -> 8.8 us  [double(): recv = lax.ppermute(y, axis, pairs(axis, mask))]
    unnamed x26 -> x28, local copies, waits for them, and re-layouts: 2.77 us -> 3.56 us
  transfers between devices with their start and end apart: 33 -> 33, of which waited for: 11 -> 15; matrix products, arithmetic and copies ran while one was open for 17% -> 17% of each run, Pallas kernels for 0% -> 0%
where the time goes in v6:
time: 130 us; the launch traced here: 129 us
  starting transfers between devices  45.4 us (35%)
  local copies, waits for them, and re-layouts  21.5 us (17%)
  waiting for transfers between devices  20 us (15%)
  matrix products  16.1 us (12%)
  between operations  14 us (11%)
  other arithmetic  12 us (9%)
    ppermute x15, starting transfers between devices, halve(): lax.ppermute(send.astype(wire), axis, pairs(axis, mask)).astype(x.dtype)  26 us
    ppermute x15, starting transfers between devices, double(): recv = lax.ppermute(y, axis, pairs(axis, mask))  16.2 us
    ppermute x15, waiting for transfers between devices, double(): recv = lax.ppermute(y, axis, pairs(axis, mask))  8.8 us
    ppermute x15, waiting for transfers between devices, halve(): lax.ppermute(send.astype(wire), axis, pairs(axis, mask)).astype(x.dtype)  7.72 us
    dot_general x1, matrix products, per_device(): jnp.einsum('jerb,jebc->jrc', picked, inverse_blocks, preferred_element_ty...  5.12 us
    add x12, other arithmetic, halve(): keep + lax.ppermute(send.astype(wire), axis, pairs(axis, mask)).astype(x....  4.61 us
    gather x1, local copies, waits for them, and re-layouts, per_device(): picked = jnp.take(extended, margin, axis=0)  4.21 us
    dot_general x1, matrix products, per_device(): jnp.einsum('jqn,jqrc->nrc', onehot, terms, precision=lax.Precision.HIGHEST)  4.18 us
  transfers between devices with their start and end apart: 33, of which 15 were waited for; matrix products, arithmetic and copies ran while one was open for 17% of the time, Pallas kernels for 0%

profile of v6, /device:TPU:0, one launch (start us, length us, event | category | flops | bytes accessed | tf_op | source)
XLA Modules:
  0.0 129.1 jit_solution(166619293673987742)
XLA Ops:
  6.5 3.4 %convolution_bitcast_fusion.1 = f32[4,2,512,128]{2,3,1,0:T(8,128)} fusion(bf16[4,2,256,128]{3,2,1,0:T(8,128)(2,1)} %param.11, bf16[4,512,256]{2,1,0:T(8,128)(2,1)} %param.7), kind=kOutput, calls=%fused_computation.11 | convolution fusion | flops 268435456 | bytes 3670016 | tf_op jit(solution)/shard_map/jrb,jqbc->jqrc/dot_general | solution.py:76
  9.9 2.9 %copy.75 = f32[4,2,512,128]{3,0,1,2:T(4,128)} copy(f32[4,2,512,128]{2,3,1,0:T(8,128)} %convolution_bitcast_fusion.1) | data formatting | bytes 4194304 | tf_op jit(solution)/shard_map/jrb,jqbc->jqrc/transpose | solution.py:76
  12.9 4.2 %convolution_bitcast_fusion = f32[12,512,128]{2,0,1:T(8,128)S(1)} fusion(f32[4,2,512,128]{3,0,1,2:T(4,128)} %copy.75, s32[4,2]{0,1:T(2,128)S(1)} %copy-done.10), kind=kOutput, calls=%fused_computation.6 | convolution fusion | flops 75497568 | bytes 5242912 | tf_op jit(solution)/shard_map/jqn,jqrc->nrc/dot_general | solution.py:79
  17.1 1.8 %fusion.48 = (f32[4,512,128]{2,0,1:T(4,128)S(1)}, f32[4,512,128]{2,0,1:T(4,128)}, f32[4,512,128]{2,0,1:T(4,128)}) fusion(f32[12,512,128]{2,0,1:T(8,128)S(1)} %convolution_bitcast_fusion), kind=kLoop, calls=%fused_computation.129 | loop fusion | bytes 6291456 | tf_op jit(solution)/shard_map/slice | solution.py:89
  18.9 2.4 %constant_dynamic-slice_fusion.13 = (f32[4,1,2,2,2,2,16,128]{7,0,6,5,4,3,2,1:T(4,128)}, f32[4,1,2,2,2,2,16,128]{7,0,6,5,4,3,2,1:T(4,128)S(1)}, f32[4,1,2,2,2,2,1...) fusion(f32[4,2,2,2,2,2,16,128]{7,0,6,5,4,3,2,1:T(4,128)S(1)} %bitcast.119, s32[]{:T(128)S(6)} %select_n.673, ...), kind=kLoop, calls=%fused_computation.96 | loop fusion | bytes 4194312 | tf_op jit(solution)/shard_map/jit(dynamic_index_in_dim)/dynamic_slice | solution.py:46
  26.6 2.0 %collective-permute-start = (bf16[1,512,256]{2,1,0:T(8,128)(2,1)}, bf16[1,512,256]{2,1,0:T(8,128)(2,1)S(1)}, u32[]{:S(2)}, u32[]{:S(2)}) collective-permute-start(bf16[1,512,256]{2,1,0:T(8,128)(2,1)} %get-tuple-element.22), channel_id=1, source_target_pairs={{0,1},{1,2},{2,3},{3,4},{4,5},{5,6},{6,7},{7,8},{8,9},{9,10},{10,1... | collective-permute-start | bytes 786440 | tf_op jit(solution)/shard_map/ppermute | solution.py:15
  31.0 3.4 %collective-permute-done.1 = bf16[1,512,256]{2,1,0:T(8,128)(2,1)} collective-permute-done((bf16[1,512,256]{2,1,0:T(8,128)(2,1)}, bf16[1,512,256]{2,1,0:T(8,128)(2,1)}, u32[]{:S(2)}, u32[]{:S(2)}) %collective-permute-start.1) | collective-permute-done | bytes 262176 | tf_op jit(solution)/shard_map/ppermute | solution.py:17
  34.4 2.3 %pad_maximum_fusion = bf16[6,512,256]{2,1,0:T(8,128)(2,1)} fusion(bf16[1,512,256]{2,1,0:T(8,128)(2,1)} %collective-permute-done.1, bf16[4,512,256]{2,1,0:T(8,128)(2,1)S(1)} %copy-done.1, bf16[1,512,256]{2,1,0:T(8,128)(2,1)S(1)} %collective-permute-done), kind=kLoop, calls=%fused_computation.14 | loop fusion | flops 1572864 | bytes 3145728 | tf_op jit(solution)/shard_map/concatenate | solution.py:13
  36.7 4.2 %gather_fusion = bf16[16,512,256]{2,1,0:T(8,128)(2,1)} fusion(bf16[6,512,256]{2,1,0:T(8,128)(2,1)} %pad_maximum_fusion, s32[1024]{0:T(1024)S(1)} %pad_clamp_fusion.2), kind=kCustom, calls=%fused_computation | custom fusion | bytes 8388672 | tf_op jit(solution)/shard_map/jit(_take)/gather | solution.py:90
  41.0 5.1 %fusion.5 = f32[4,512,256]{2,1,0:T(8,128)} fusion(bf16[4,4,256,256]{3,2,1,0:T(8,128)(2,1)S(1)} %copy-done, bf16[4,4,512,256]{3,2,1,0:T(8,128)(2,1)} %bitcast.118, pred[4,4]{1,0:T(4,128)(4,1)S(1)} %compare_and_fusion.2), kind=kOutput, calls=%fused_computation.10 | convolution fusion | flops 1075838976 | bytes 8388624 | tf_op jit(solution)/shard_map/jerb,jebc->jrc/dot_general | solution.py:91
  50.4 4.4 %collective-permute-start.5 = (f32[4,1,1,2,2,2,16,128]{7,6,0,5,4,3,2,1:T(8,128)S(1)}, f32[4,1,1,2,2,2,16,128]{7,6,0,5,4,3,2,1:T(8,128)}, u32[]{:S(2)}, u32[]{:S(2)}) collective-permute-start(f32[4,1,1,2,2,2,16,128]{7,6,0,5,4,3,2,1:T(8,128)S(1)} %constant_dynamic-slice_fusion.11), channel_id=1, source_target_pairs={{0,2},{1,3},{2,0},{3,1},{4,6},{5,7},{6,4},{7,5},{8,10},{9,11},{10,... | collective-permute-start | bytes 786440 | tf_op jit(solution)/shard_map/ppermute | solution.py:48
  54.8 1.5 %collective-permute-start.9 = (f32[4,1,2,1,2,2,16,128]{7,6,0,5,4,3,2,1:T(8,128)S(1)}, f32[4,1,2,1,2,2,16,128]{7,6,0,5,4,3,2,1:T(8,128)S(1)}, u32[]{:S(2)}, u32[]{:S(2)}) collective-permute-start(f32[4,1,2,1,2,2,16,128]{7,6,0,5,4,3,2,1:T(8,128)S(1)} %constant_dynamic-slice_fusion.7), channel_id=1, source_target_pairs={{0,4},{4,0},{8,12},{12,8},{16,20},{20,16},{24,28},{28,24},{1,5},{5... | collective-permute-start | bytes 786440 | tf_op jit(solution)/shard_map/ppermute | solution.py:48
  56.3 1.6 %collective-permute-start.13 = (f32[4,1,2,2,1,2,16,128]{7,6,0,5,4,3,2,1:T(8,128)S(1)}, f32[4,1,2,2,1,2,16,128]{7,6,0,5,4,3,2,1:T(8,128)S(1)}, u32[]{:S(2)}, u32[]{:S(2)}) collective-permute-start(f32[4,1,2,2,1,2,16,128]{7,6,0,5,4,3,2,1:T(8,128)S(1)} %constant_dynamic-slice_fusion.3), channel_id=1, source_target_pairs={{0,8},{4,12},{8,0},{12,4},{16,24},{20,28},{24,16},{28,20},{1,9},{5... | collective-permute-start | bytes 786440 | tf_op jit(solution)/shard_map/ppermute | solution.py:48
  57.9 2.0 %collective-permute-done.5 = f32[4,1,1,2,2,2,16,128]{7,6,0,5,4,3,2,1:T(8,128)} collective-permute-done((f32[4,1,1,2,2,2,16,128]{7,6,0,5,4,3,2,1:T(8,128)S(1)}, f32[4,1,1,2,2,2,16,128]{7,6,0,5,4,3,2,1:T(8,128)}, u32[]{:S(2)}, u32[]{:S(2)}) %collective-permute-start.5) | collective-permute-done | bytes 262176 | tf_op jit(solution)/shard_map/ppermute | solution.py:48
  61.0 3.4 %collective-permute-start.6 = (f32[4,1,1,1,2,2,16,128]{7,6,0,5,4,3,2,1:T(8,128)S(1)}, f32[4,1,1,1,2,2,16,128]{7,6,0,5,4,3,2,1:T(8,128)S(1)}, u32[]{:S(2)}, u32[]{:S(2)}) collective-permute-start(f32[4,1,1,1,2,2,16,128]{7,6,0,5,4,3,2,1:T(8,128)S(1)} %constant_dynamic-slice_fusion.10), channel_id=1, source_target_pairs={{0,4},{4,0},{8,12},{12,8},{16,20},{20,16},{24,28},{28,24},{1,5},{5... | collective-permute-start | bytes 393224 | tf_op jit(solution)/shard_map/ppermute | solution.py:48
  64.5 2.7 %collective-permute-start.10 = (f32[4,1,2,1,1,2,16,128]{7,6,0,5,4,3,2,1:T(8,128)S(1)}, f32[4,1,2,1,1,2,16,128]{7,6,0,5,4,3,2,1:T(8,128)S(1)}, u32[]{:S(2)}, u32[]{:S(2)}) collective-permute-start(f32[4,1,2,1,1,2,16,128]{7,6,0,5,4,3,2,1:T(8,128)S(1)} %constant_dynamic-slice_fusion.6), channel_id=1, source_target_pairs={{0,8},{4,12},{8,0},{12,4},{16,24},{20,28},{24,16},{28,20},{1,9},{5... | collective-permute-start | bytes 393224 | tf_op jit(solution)/shard_map/ppermute | solution.py:48
  67.2 3.3 %collective-permute-start.14 = (f32[4,1,2,2,1,1,16,128]{7,6,0,5,4,3,2,1:T(8,128)S(1)}, f32[4,1,2,2,1,1,16,128]{7,6,0,5,4,3,2,1:T(8,128)S(1)}, u32[]{:S(2)}, u32[]{:S(2)}) collective-permute-start(f32[4,1,2,2,1,1,16,128]{7,6,0,5,4,3,2,1:T(8,128)S(1)} %constant_dynamic-slice_fusion.2), channel_id=1, source_target_pairs={{0,16},{4,20},{8,24},{12,28},{16,0},{20,4},{24,8},{28,12},{1,17},{... | collective-permute-start | bytes 393224 | tf_op jit(solution)/shard_map/ppermute | solution.py:48
  70.5 1.9 %collective-permute-start.7 = (f32[4,1,1,1,1,2,16,128]{7,6,0,5,4,3,2,1:T(8,128)S(1)}, f32[4,1,1,1,1,2,16,128]{7,6,0,5,4,3,2,1:T(8,128)S(1)}, u32[]{:S(2)}, u32[]{:S(2)}) collective-permute-start(f32[4,1,1,1,1,2,16,128]{7,6,0,5,4,3,2,1:T(8,128)S(1)} %constant_dynamic-slice_fusion.9), channel_id=1, source_target_pairs={{0,8},{4,12},{8,0},{12,4},{16,24},{20,28},{24,16},{28,20},{1,9},{5... | collective-permute-start | bytes 196616 | tf_op jit(solution)/shard_map/ppermute | solution.py:48
  76.9 2.1 %collective-permute-start.8 = (f32[4,1,1,1,1,1,16,128]{7,6,0,5,4,3,2,1:T(8,128)S(1)}, f32[4,1,1,1,1,1,16,128]{7,6,0,5,4,3,2,1:T(8,128)S(1)}, u32[]{:S(2)}, u32[]{:S(2)}) collective-permute-start(f32[4,1,1,1,1,1,16,128]{7,6,0,5,4,3,2,1:T(8,128)S(1)} %constant_dynamic-slice_fusion.8), channel_id=1, source_target_pairs={{0,16},{4,20},{8,24},{12,28},{16,0},{20,4},{24,8},{28,12},{1,17},{... | collective-permute-start | bytes 98312 | tf_op jit(solution)/shard_map/ppermute | solution.py:48
  79.0 1.4 %collective-permute-done.11 = f32[4,1,2,1,1,1,16,128]{7,6,0,5,4,3,2,1:T(8,128)S(1)} collective-permute-done((f32[4,1,2,1,1,1,16,128]{7,6,0,5,4,3,2,1:T(8,128)S(1)}, f32[4,1,2,1,1,1,16,128]{7,6,0,5,4,3,2,1:T(8,128)S(1)}, u32[]{:S(2)}, u32[]{:S(2)}) %collective-permute-start.11) | collective-permute-done | bytes 65568 | tf_op jit(solution)/shard_map/ppermute | solution.py:48
  80.7 2.0 %collective-permute-start.16 = (f32[4,1,1,1,1,1,16,128]{7,6,0,5,4,3,2,1:T(8,128)S(1)}, f32[4,1,1,1,1,1,16,128]{7,6,0,5,4,3,2,1:T(8,128)S(1)}, u32[]{:S(2)}, u32[]{:S(2)}) collective-permute-start(f32[4,1,1,1,1,1,16,128]{7,6,0,5,4,3,2,1:T(8,128)S(1)} %constant_dynamic-slice_fusion), channel_id=1, source_target_pairs={{0,4},{4,0},{8,12},{12,8},{16,20},{20,16},{24,28},{28,24},{1,5},{5... | collective-permute-start | bytes 98312 | tf_op jit(solution)/shard_map/ppermute | solution.py:48
  82.7 1.7 %collective-permute-done.12 = f32[4,1,1,1,1,1,16,128]{7,6,0,5,4,3,2,1:T(8,128)S(1)} collective-permute-done((f32[4,1,1,1,1,1,16,128]{7,6,0,5,4,3,2,1:T(8,128)S(1)}, f32[4,1,1,1,1,1,16,128]{7,6,0,5,4,3,2,1:T(8,128)S(1)}, u32[]{:S(2)}, u32[]{:S(2)}) %collective-permute-start.12) | collective-permute-done | bytes 32800 | tf_op jit(solution)/shard_map/ppermute | solution.py:48
  86.7 1.8 %fusion.13 = bf16[12,16,128]{2,1,0:T(8,128)(2,1)S(1)} fusion(bf16[12,4,136,128]{3,2,1,0:T(8,128)(2,1)} %all-gather.2.cloned.1.call-done, bf16[12,4,16,128]{3,2,1,0:T(8,128)(2,1)S(1)} %bitcast.132, pred[12,4]{1,0:T(8,128)(4,1)S(1)} %copy.84), kind=kOutput, calls=%fused_computation.17 | convolution fusion | flops 25288704 | bytes 1818672 | tf_op jit(solution)/shard_map/nerc,necd->nrd/dot_general | solution.py:100
  88.5 1.5 %collective-permute-start.17 = (bf16[4,1,1,1,1,1,16,128]{7,6,0,5,4,3,2,1:T(8,128)(2,1)S(1)}, bf16[4,1,1,1,1,1,16,128]{7,6,0,5,4,3,2,1:T(8,128)(2,1)S(1)}, u32[]{:S(2)}, u32[]{:S(2)}) collective-permute-start(bf16[4,1,1,1,1,1,16,128]{7,6,0,5,4,3,2,1:T(8,128)(2,1)S(1)} %get-tuple-element.32), channel_id=1, source_target_pairs={{0,16},{4,20},{8,24},{12,28},{16,0},{20,4},{24,8},{28,12},{1,17},{... | collective-permute-start | bytes 49160 | tf_op jit(solution)/shard_map/ppermute | solution.py:53
  90.7 1.4 %collective-permute-start.27 = (bf16[4,1,1,1,1,1,16,128]{7,6,0,5,4,3,2,1:T(8,128)(2,1)S(1)}, bf16[4,1,1,1,1,1,16,128]{7,6,0,5,4,3,2,1:T(8,128)(2,1)S(1)}, u32[]{:S(2)}, u32[]{:S(2)}) collective-permute-start(bf16[4,1,1,1,1,1,16,128]{7,6,0,5,4,3,2,1:T(8,128)(2,1)S(1)} %get-tuple-element.34), channel_id=1, source_target_pairs={{0,4},{4,0},{8,12},{12,8},{16,20},{20,16},{24,28},{28,24},{1,5},{5... | collective-permute-start | bytes 49160 | tf_op jit(solution)/shard_map/ppermute | solution.py:53
  93.2 2.4 %collective-permute-start.18 = (bf16[4,1,1,1,1,2,16,128]{7,6,0,5,4,3,2,1:T(8,128)(2,1)S(1)}, bf16[4,1,1,1,1,2,16,128]{7,6,0,5,4,3,2,1:T(8,128)(2,1)S(1)}, u32[]{:S(2)}, u32[]{:S(2)}) collective-permute-start(bf16[4,1,1,1,1,2,16,128]{7,6,0,5,4,3,2,1:T(8,128)(2,1)S(1)} %maximum_select_fusion.18), channel_id=1, source_target_pairs={{0,8},{4,12},{8,0},{12,4},{16,24},{20,28},{24,16},{28,20},{1,9},{5... | collective-permute-start | bytes 98312 | tf_op jit(solution)/shard_map/ppermute | solution.py:53
  95.6 2.1 %collective-permute-start.23 = (bf16[4,1,2,1,1,1,16,128]{7,6,0,2,5,4,3,1:T(8,128)(2,1)S(1)}, bf16[4,1,2,1,1,1,16,128]{7,6,0,2,5,4,3,1:T(8,128)(2,1)S(1)}, u32[]{:S(2)}, u32[]{:S(2)}) collective-permute-start(bf16[4,1,2,1,1,1,16,128]{7,6,0,2,5,4,3,1:T(8,128)(2,1)S(1)} %fusion.27), channel_id=1, source_target_pairs={{0,16},{4,20},{8,24},{12,28},{16,0},{20,4},{24,8},{28,12},{1,17},{... | collective-permute-start | bytes 98312 | tf_op jit(solution)/shard_map/ppermute | solution.py:53
  98.9 1.5 %collective-permute-start.19 = (bf16[4,1,1,1,2,2,16,128]{7,6,0,5,4,3,2,1:T(8,128)(2,1)S(1)}, bf16[4,1,1,1,2,2,16,128]{7,6,0,5,4,3,2,1:T(8,128)(2,1)S(1)}, u32[]{:S(2)}, u32[]{:S(2)}) collective-permute-start(bf16[4,1,1,1,2,2,16,128]{7,6,0,5,4,3,2,1:T(8,128)(2,1)S(1)} %maximum_select_fusion.13), channel_id=1, source_target_pairs={{0,4},{4,0},{8,12},{12,8},{16,20},{20,16},{24,28},{28,24},{1,5},{5... | collective-permute-start | bytes 196616 | tf_op jit(solution)/shard_map/ppermute | solution.py:53
  101.8 2.0 %collective-permute-start.29 = (bf16[4,1,2,2,1,1,16,128]{7,6,0,5,4,3,2,1:T(8,128)(2,1)S(1)}, bf16[4,1,2,2,1,1,16,128]{7,6,0,5,4,3,2,1:T(8,128)(2,1)S(1)}, u32[]{:S(2)}, u32[]{:S(2)}) collective-permute-start(bf16[4,1,2,2,1,1,16,128]{7,6,0,5,4,3,2,1:T(8,128)(2,1)S(1)} %fusion.26), channel_id=1, source_target_pairs={{0,16},{4,20},{8,24},{12,28},{16,0},{20,4},{24,8},{28,12},{1,17},{... | collective-permute-start | bytes 196616 | tf_op jit(solution)/shard_map/ppermute | solution.py:53
  110.3 2.5 %collective-permute-done.30 = bf16[4,1,2,2,1,2,16,128]{7,6,0,5,4,3,2,1:T(8,128)(2,1)S(1)} collective-permute-done((bf16[4,1,2,2,1,2,16,128]{7,6,0,5,4,3,2,1:T(8,128)(2,1)S(1)}, bf16[4,1,2,2,1,2,16,128]{7,6,0,5,4,3,2,1:T(8,128)(2,1)S(1)}, u32[]{:S(2)}, u32[]{:S(2)}) %collective-permute-start.30) | collective-permute-done | bytes 131104 | tf_op jit(solution)/shard_map/ppermute | solution.py:53
  117.1 2.2 %gather_fusion.2 = bf16[8,512,128]{2,1,0:T(8,128)(2,1)S(1)} fusion(bf16[12,512,128]{2,1,0:T(8,128)(2,1)} %pad_maximum_fusion.1, s32[1024]{0:T(1024)S(1)} %pad_clamp_fusion), kind=kCustom, calls=%fused_computation.2 | custom fusion | bytes 2097184 | tf_op jit(solution)/shard_map/jit(_take)/gather | solution.py:109
  119.3 1.7 %fusion.17 = f32[4,512,256,1]{2,1,3,0:T(8,128)S(1)} fusion(bf16[4,2,256,128]{3,2,1,0:T(8,128)(2,1)} %param.11, bf16[4,2,512,128]{3,2,1,0:T(8,128)(2,1)S(1)} %bitcast.121, pred[4,2]{1,0:T(4,128)(4,1)S(1)} %copy.82), kind=kOutput, calls=%fused_computation.19 | convolution fusion | flops 268959744 | bytes 3670024 | tf_op jit(solution)/shard_map/jqrc,jqbc->jrb/dot_general | solution.py:110
  (156 shorter events, 36.1 us)
Async XLA Ops:
  6.5 78.1 %all-gather.2.cloned.1.call-start = ((), (), s32[]{:S(2)}) async-start(), calls=%async_computation | async-start | bytes 2088960 | tf_op jit(solution)/shard_map/all_gather | solution.py:69
  22.1 23.9 %collective-permute-start.4 = (f32[4,1,2,2,2,2,16,128]{7,6,0,5,4,3,2,1:T(8,128)}, f32[4,1,2,2,2,2,16,128]{7,6,0,5,4,3,2,1:T(8,128)}, u32[]{:S(2)}, u32[]{:S(2)}) collective-permute-start(f32[4,1,2,2,2,2,16,128]{7,6,0,5,4,3,2,1:T(8,128)} %copy.110), channel_id=1, source_target_pairs={{0,1},{1,0},{2,3},{3,2},{4,5},{5,4},{6,7},{7,6},{8,9},{9,8},{10,11... | collective-permute-start | bytes 1572872 | tf_op jit(solution)/shard_map/ppermute | solution.py:48
  23.4 23.8 %collective-permute-start.3 = (f32[4,1,2,2,2,2,16,128]{7,6,0,5,4,3,2,1:T(8,128)}, f32[4,1,2,2,2,2,16,128]{7,6,0,5,4,3,2,1:T(8,128)}, u32[]{:S(2)}, u32[]{:S(2)}) collective-permute-start(f32[4,1,2,2,2,2,16,128]{7,6,0,5,4,3,2,1:T(8,128)} %copy.108), channel_id=1, source_target_pairs={{0,1},{1,0},{2,3},{3,2},{4,5},{5,4},{6,7},{7,6},{8,9},{9,8},{10,11... | collective-permute-start | bytes 1572872 | tf_op jit(solution)/shard_map/ppermute | solution.py:48
  25.3 23.1 %collective-permute-start.2 = (f32[4,1,2,2,2,2,16,128]{7,6,0,5,4,3,2,1:T(8,128)}, f32[4,1,2,2,2,2,16,128]{7,6,0,5,4,3,2,1:T(8,128)}, u32[]{:S(2)}, u32[]{:S(2)}) collective-permute-start(f32[4,1,2,2,2,2,16,128]{7,6,0,5,4,3,2,1:T(8,128)} %copy.106), channel_id=1, source_target_pairs={{0,1},{1,0},{2,3},{3,2},{4,5},{5,4},{6,7},{7,6},{8,9},{9,8},{10,11... | collective-permute-start | bytes 1572872 | tf_op jit(solution)/shard_map/ppermute | solution.py:48
  26.6 4.4 %collective-permute-start = (bf16[1,512,256]{2,1,0:T(8,128)(2,1)}, bf16[1,512,256]{2,1,0:T(8,128)(2,1)S(1)}, u32[]{:S(2)}, u32[]{:S(2)}) collective-permute-start(bf16[1,512,256]{2,1,0:T(8,128)(2,1)} %get-tuple-element.22), channel_id=1, source_target_pairs={{0,1},{1,2},{2,3},{3,4},{4,5},{5,6},{6,7},{7,8},{8,9},{9,10},{10,1... | collective-permute-start | bytes 786440 | tf_op jit(solution)/shard_map/ppermute | solution.py:15
  28.6 5.9 %collective-permute-start.1 = (bf16[1,512,256]{2,1,0:T(8,128)(2,1)}, bf16[1,512,256]{2,1,0:T(8,128)(2,1)}, u32[]{:S(2)}, u32[]{:S(2)}) collective-permute-start(bf16[1,512,256]{2,1,0:T(8,128)(2,1)} %get-tuple-element.23), channel_id=1, source_target_pairs={{1,0},{2,1},{3,2},{4,3},{5,4},{6,5},{7,6},{8,7},{9,8},{10,9},{11,1... | collective-permute-start | bytes 786440 | tf_op jit(solution)/shard_map/ppermute | solution.py:17
  50.4 9.6 %collective-permute-start.5 = (f32[4,1,1,2,2,2,16,128]{7,6,0,5,4,3,2,1:T(8,128)S(1)}, f32[4,1,1,2,2,2,16,128]{7,6,0,5,4,3,2,1:T(8,128)}, u32[]{:S(2)}, u32[]{:S(2)}) collective-permute-start(f32[4,1,1,2,2,2,16,128]{7,6,0,5,4,3,2,1:T(8,128)S(1)} %constant_dynamic-slice_fusion.11), channel_id=1, source_target_pairs={{0,2},{1,3},{2,0},{3,1},{4,6},{5,7},{6,4},{7,5},{8,10},{9,11},{10,... | collective-permute-start | bytes 786440 | tf_op jit(solution)/shard_map/ppermute | solution.py:48
  54.8 9.6 %collective-permute-start.9 = (f32[4,1,2,1,2,2,16,128]{7,6,0,5,4,3,2,1:T(8,128)S(1)}, f32[4,1,2,1,2,2,16,128]{7,6,0,5,4,3,2,1:T(8,128)S(1)}, u32[]{:S(2)}, u32[]{:S(2)}) collective-permute-start(f32[4,1,2,1,2,2,16,128]{7,6,0,5,4,3,2,1:T(8,128)S(1)} %constant_dynamic-slice_fusion.7), channel_id=1, source_target_pairs={{0,4},{4,0},{8,12},{12,8},{16,20},{20,16},{24,28},{28,24},{1,5},{5... | collective-permute-start | bytes 786440 | tf_op jit(solution)/shard_map/ppermute | solution.py:48
  56.3 10.9 %collective-permute-start.13 = (f32[4,1,2,2,1,2,16,128]{7,6,0,5,4,3,2,1:T(8,128)S(1)}, f32[4,1,2,2,1,2,16,128]{7,6,0,5,4,3,2,1:T(8,128)S(1)}, u32[]{:S(2)}, u32[]{:S(2)}) collective-permute-start(f32[4,1,2,2,1,2,16,128]{7,6,0,5,4,3,2,1:T(8,128)S(1)} %constant_dynamic-slice_fusion.3), channel_id=1, source_target_pairs={{0,8},{4,12},{8,0},{12,4},{16,24},{20,28},{24,16},{28,20},{1,9},{5... | collective-permute-start | bytes 786440 | tf_op jit(solution)/shard_map/ppermute | solution.py:48
  61.0 9.5 %collective-permute-start.6 = (f32[4,1,1,1,2,2,16,128]{7,6,0,5,4,3,2,1:T(8,128)S(1)}, f32[4,1,1,1,2,2,16,128]{7,6,0,5,4,3,2,1:T(8,128)S(1)}, u32[]{:S(2)}, u32[]{:S(2)}) collective-permute-start(f32[4,1,1,1,2,2,16,128]{7,6,0,5,4,3,2,1:T(8,128)S(1)} %constant_dynamic-slice_fusion.10), channel_id=1, source_target_pairs={{0,4},{4,0},{8,12},{12,8},{16,20},{20,16},{24,28},{28,24},{1,5},{5... | collective-permute-start | bytes 393224 | tf_op jit(solution)/shard_map/ppermute | solution.py:48
  64.5 9.3 %collective-permute-start.10 = (f32[4,1,2,1,1,2,16,128]{7,6,0,5,4,3,2,1:T(8,128)S(1)}, f32[4,1,2,1,1,2,16,128]{7,6,0,5,4,3,2,1:T(8,128)S(1)}, u32[]{:S(2)}, u32[]{:S(2)}) collective-permute-start(f32[4,1,2,1,1,2,16,128]{7,6,0,5,4,3,2,1:T(8,128)S(1)} %constant_dynamic-slice_fusion.6), channel_id=1, source_target_pairs={{0,8},{4,12},{8,0},{12,4},{16,24},{20,28},{24,16},{28,20},{1,9},{5... | collective-permute-start | bytes 393224 | tf_op jit(solution)/shard_map/ppermute | solution.py:48
  67.2 8.9 %collective-permute-start.14 = (f32[4,1,2,2,1,1,16,128]{7,6,0,5,4,3,2,1:T(8,128)S(1)}, f32[4,1,2,2,1,1,16,128]{7,6,0,5,4,3,2,1:T(8,128)S(1)}, u32[]{:S(2)}, u32[]{:S(2)}) collective-permute-start(f32[4,1,2,2,1,1,16,128]{7,6,0,5,4,3,2,1:T(8,128)S(1)} %constant_dynamic-slice_fusion.2), channel_id=1, source_target_pairs={{0,16},{4,20},{8,24},{12,28},{16,0},{20,4},{24,8},{28,12},{1,17},{... | collective-permute-start | bytes 393224 | tf_op jit(solution)/shard_map/ppermute | solution.py:48
  70.5 6.3 %collective-permute-start.7 = (f32[4,1,1,1,1,2,16,128]{7,6,0,5,4,3,2,1:T(8,128)S(1)}, f32[4,1,1,1,1,2,16,128]{7,6,0,5,4,3,2,1:T(8,128)S(1)}, u32[]{:S(2)}, u32[]{:S(2)}) collective-permute-start(f32[4,1,1,1,1,2,16,128]{7,6,0,5,4,3,2,1:T(8,128)S(1)} %constant_dynamic-slice_fusion.9), channel_id=1, source_target_pairs={{0,8},{4,12},{8,0},{12,4},{16,24},{20,28},{24,16},{28,20},{1,9},{5... | collective-permute-start | bytes 196616 | tf_op jit(solution)/shard_map/ppermute | solution.py:48
  73.8 6.6 %collective-permute-start.11 = (f32[4,1,2,1,1,1,16,128]{7,6,0,5,4,3,2,1:T(8,128)S(1)}, f32[4,1,2,1,1,1,16,128]{7,6,0,5,4,3,2,1:T(8,128)S(1)}, u32[]{:S(2)}, u32[]{:S(2)}) collective-permute-start(f32[4,1,2,1,1,1,16,128]{7,6,0,5,4,3,2,1:T(8,128)S(1)} %constant_dynamic-slice_fusion.5), channel_id=1, source_target_pairs={{0,16},{4,20},{8,24},{12,28},{16,0},{20,4},{24,8},{28,12},{1,17},{... | collective-permute-start | bytes 196616 | tf_op jit(solution)/shard_map/ppermute | solution.py:48
  76.2 4.4 %collective-permute-start.15 = (f32[4,1,1,2,1,1,16,128]{7,6,0,5,4,3,2,1:T(8,128)S(1)}, f32[4,1,1,2,1,1,16,128]{7,6,0,5,4,3,2,1:T(8,128)S(1)}, u32[]{:S(2)}, u32[]{:S(2)}) collective-permute-start(f32[4,1,1,2,1,1,16,128]{7,6,0,5,4,3,2,1:T(8,128)S(1)} %constant_dynamic-slice_fusion.1), channel_id=1, source_target_pairs={{0,2},{1,3},{2,0},{3,1},{4,6},{5,7},{6,4},{7,5},{8,10},{9,11},{10,... | collective-permute-start | bytes 196616 | tf_op jit(solution)/shard_map/ppermute | solution.py:48
  76.9 5.8 %collective-permute-start.8 = (f32[4,1,1,1,1,1,16,128]{7,6,0,5,4,3,2,1:T(8,128)S(1)}, f32[4,1,1,1,1,1,16,128]{7,6,0,5,4,3,2,1:T(8,128)S(1)}, u32[]{:S(2)}, u32[]{:S(2)}) collective-permute-start(f32[4,1,1,1,1,1,16,128]{7,6,0,5,4,3,2,1:T(8,128)S(1)} %constant_dynamic-slice_fusion.8), channel_id=1, source_target_pairs={{0,16},{4,20},{8,24},{12,28},{16,0},{20,4},{24,8},{28,12},{1,17},{... | collective-permute-start | bytes 98312 | tf_op jit(solution)/shard_map/ppermute | solution.py:48
  80.5 4.0 %collective-permute-start.12 = (f32[4,1,1,1,1,1,16,128]{7,6,0,5,4,3,2,1:T(8,128)S(1)}, f32[4,1,1,1,1,1,16,128]{7,6,0,5,4,3,2,1:T(8,128)S(1)}, u32[]{:S(2)}, u32[]{:S(2)}) collective-permute-start(f32[4,1,1,1,1,1,16,128]{7,6,0,5,4,3,2,1:T(8,128)S(1)} %constant_dynamic-slice_fusion.4), channel_id=1, source_target_pairs={{0,2},{1,3},{2,0},{3,1},{4,6},{5,7},{6,4},{7,5},{8,10},{9,11},{10,... | collective-permute-start | bytes 98312 | tf_op jit(solution)/shard_map/ppermute | solution.py:48
  80.7 4.0 %collective-permute-start.16 = (f32[4,1,1,1,1,1,16,128]{7,6,0,5,4,3,2,1:T(8,128)S(1)}, f32[4,1,1,1,1,1,16,128]{7,6,0,5,4,3,2,1:T(8,128)S(1)}, u32[]{:S(2)}, u32[]{:S(2)}) collective-permute-start(f32[4,1,1,1,1,1,16,128]{7,6,0,5,4,3,2,1:T(8,128)S(1)} %constant_dynamic-slice_fusion), channel_id=1, source_target_pairs={{0,4},{4,0},{8,12},{12,8},{16,20},{20,16},{24,28},{28,24},{1,5},{5... | collective-permute-start | bytes 98312 | tf_op jit(solution)/shard_map/ppermute | solution.py:48
  88.5 4.7 %collective-permute-start.17 = (bf16[4,1,1,1,1,1,16,128]{7,6,0,5,4,3,2,1:T(8,128)(2,1)S(1)}, bf16[4,1,1,1,1,1,16,128]{7,6,0,5,4,3,2,1:T(8,128)(2,1)S(1)}, u32[]{:S(2)}, u32[]{:S(2)}) collective-permute-start(bf16[4,1,1,1,1,1,16,128]{7,6,0,5,4,3,2,1:T(8,128)(2,1)S(1)} %get-tuple-element.32), channel_id=1, source_target_pairs={{0,16},{4,20},{8,24},{12,28},{16,0},{20,4},{24,8},{28,12},{1,17},{... | collective-permute-start | bytes 49160 | tf_op jit(solution)/shard_map/ppermute | solution.py:53
  90.2 5.4 %collective-permute-start.22 = (bf16[4,1,1,1,1,1,16,128]{7,6,0,5,4,3,2,1:T(8,128)(2,1)S(1)}, bf16[4,1,1,1,1,1,16,128]{7,6,0,5,4,3,2,1:T(8,128)(2,1)S(1)}, u32[]{:S(2)}, u32[]{:S(2)}) collective-permute-start(bf16[4,1,1,1,1,1,16,128]{7,6,0,5,4,3,2,1:T(8,128)(2,1)S(1)} %get-tuple-element.33), channel_id=1, source_target_pairs={{0,2},{1,3},{2,0},{3,1},{4,6},{5,7},{6,4},{7,5},{8,10},{9,11},{10,... | collective-permute-start | bytes 49160 | tf_op jit(solution)/shard_map/ppermute | solution.py:53
  90.7 6.9 %collective-permute-start.27 = (bf16[4,1,1,1,1,1,16,128]{7,6,0,5,4,3,2,1:T(8,128)(2,1)S(1)}, bf16[4,1,1,1,1,1,16,128]{7,6,0,5,4,3,2,1:T(8,128)(2,1)S(1)}, u32[]{:S(2)}, u32[]{:S(2)}) collective-permute-start(bf16[4,1,1,1,1,1,16,128]{7,6,0,5,4,3,2,1:T(8,128)(2,1)S(1)} %get-tuple-element.34), channel_id=1, source_target_pairs={{0,4},{4,0},{8,12},{12,8},{16,20},{20,16},{24,28},{28,24},{1,5},{5... | collective-permute-start | bytes 49160 | tf_op jit(solution)/shard_map/ppermute | solution.py:53
  93.2 5.7 %collective-permute-start.18 = (bf16[4,1,1,1,1,2,16,128]{7,6,0,5,4,3,2,1:T(8,128)(2,1)S(1)}, bf16[4,1,1,1,1,2,16,128]{7,6,0,5,4,3,2,1:T(8,128)(2,1)S(1)}, u32[]{:S(2)}, u32[]{:S(2)}) collective-permute-start(bf16[4,1,1,1,1,2,16,128]{7,6,0,5,4,3,2,1:T(8,128)(2,1)S(1)} %maximum_select_fusion.18), channel_id=1, source_target_pairs={{0,8},{4,12},{8,0},{12,4},{16,24},{20,28},{24,16},{28,20},{1,9},{5... | collective-permute-start | bytes 98312 | tf_op jit(solution)/shard_map/ppermute | solution.py:53
  95.6 5.2 %collective-permute-start.23 = (bf16[4,1,2,1,1,1,16,128]{7,6,0,2,5,4,3,1:T(8,128)(2,1)S(1)}, bf16[4,1,2,1,1,1,16,128]{7,6,0,2,5,4,3,1:T(8,128)(2,1)S(1)}, u32[]{:S(2)}, u32[]{:S(2)}) collective-permute-start(bf16[4,1,2,1,1,1,16,128]{7,6,0,2,5,4,3,1:T(8,128)(2,1)S(1)} %fusion.27), channel_id=1, source_target_pairs={{0,16},{4,20},{8,24},{12,28},{16,0},{20,4},{24,8},{28,12},{1,17},{... | collective-permute-start | bytes 98312 | tf_op jit(solution)/shard_map/ppermute | solution.py:53
  97.7 4.1 %collective-permute-start.28 = (bf16[4,1,1,2,1,1,16,128]{7,6,0,5,4,3,2,1:T(8,128)(2,1)S(1)}, bf16[4,1,1,2,1,1,16,128]{7,6,0,5,4,3,2,1:T(8,128)(2,1)S(1)}, u32[]{:S(2)}, u32[]{:S(2)}) collective-permute-start(bf16[4,1,1,2,1,1,16,128]{7,6,0,5,4,3,2,1:T(8,128)(2,1)S(1)} %maximum_select_fusion.22), channel_id=1, source_target_pairs={{0,2},{1,3},{2,0},{3,1},{4,6},{5,7},{6,4},{7,5},{8,10},{9,11},{10,... | collective-permute-start | bytes 98312 | tf_op jit(solution)/shard_map/ppermute | solution.py:53
  98.9 4.9 %collective-permute-start.19 = (bf16[4,1,1,1,2,2,16,128]{7,6,0,5,4,3,2,1:T(8,128)(2,1)S(1)}, bf16[4,1,1,1,2,2,16,128]{7,6,0,5,4,3,2,1:T(8,128)(2,1)S(1)}, u32[]{:S(2)}, u32[]{:S(2)}) collective-permute-start(bf16[4,1,1,1,2,2,16,128]{7,6,0,5,4,3,2,1:T(8,128)(2,1)S(1)} %maximum_select_fusion.13), channel_id=1, source_target_pairs={{0,4},{4,0},{8,12},{12,8},{16,20},{20,16},{24,28},{28,24},{1,5},{5... | collective-permute-start | bytes 196616 | tf_op jit(solution)/shard_map/ppermute | solution.py:53
  100.8 4.3 %collective-permute-start.24 = (bf16[4,1,2,1,1,2,16,128]{7,6,0,5,4,3,2,1:T(8,128)(2,1)S(1)}, bf16[4,1,2,1,1,2,16,128]{7,6,0,5,4,3,2,1:T(8,128)(2,1)S(1)}, u32[]{:S(2)}, u32[]{:S(2)}) collective-permute-start(bf16[4,1,2,1,1,2,16,128]{7,6,0,5,4,3,2,1:T(8,128)(2,1)S(1)} %copy.88), channel_id=1, source_target_pairs={{0,8},{4,12},{8,0},{12,4},{16,24},{20,28},{24,16},{28,20},{1,9},{5... | collective-permute-start | bytes 196616 | tf_op jit(solution)/shard_map/ppermute | solution.py:53
  101.8 5.9 %collective-permute-start.29 = (bf16[4,1,2,2,1,1,16,128]{7,6,0,5,4,3,2,1:T(8,128)(2,1)S(1)}, bf16[4,1,2,2,1,1,16,128]{7,6,0,5,4,3,2,1:T(8,128)(2,1)S(1)}, u32[]{:S(2)}, u32[]{:S(2)}) collective-permute-start(bf16[4,1,2,2,1,1,16,128]{7,6,0,5,4,3,2,1:T(8,128)(2,1)S(1)} %fusion.26), channel_id=1, source_target_pairs={{0,16},{4,20},{8,24},{12,28},{16,0},{20,4},{24,8},{28,12},{1,17},{... | collective-permute-start | bytes 196616 | tf_op jit(solution)/shard_map/ppermute | solution.py:53
  103.9 5.0 %collective-permute-start.20 = (bf16[4,1,1,2,2,2,16,128]{7,6,0,5,4,3,2,1:T(8,128)(2,1)S(1)}, bf16[4,1,1,2,2,2,16,128]{7,6,0,5,4,3,2,1:T(8,128)(2,1)S(1)}, u32[]{:S(2)}, u32[]{:S(2)}) collective-permute-start(bf16[4,1,1,2,2,2,16,128]{7,6,0,5,4,3,2,1:T(8,128)(2,1)S(1)} %maximum_select_fusion.7), channel_id=1, source_target_pairs={{0,2},{1,3},{2,0},{3,1},{4,6},{5,7},{6,4},{7,5},{8,10},{9,11},{10,... | collective-permute-start | bytes 393224 | tf_op jit(solution)/shard_map/ppermute | solution.py:53
  105.1 5.0 %collective-permute-start.25 = (bf16[4,1,2,1,2,2,16,128]{7,6,0,5,4,3,2,1:T(8,128)(2,1)S(1)}, bf16[4,1,2,1,2,2,16,128]{7,6,0,5,4,3,2,1:T(8,128)(2,1)S(1)}, u32[]{:S(2)}, u32[]{:S(2)}) collective-permute-start(bf16[4,1,2,1,2,2,16,128]{7,6,0,5,4,3,2,1:T(8,128)(2,1)S(1)} %maximum_select_fusion.9), channel_id=1, source_target_pairs={{0,4},{4,0},{8,12},{12,8},{16,20},{20,16},{24,28},{28,24},{1,5},{5... | collective-permute-start | bytes 393224 | tf_op jit(solution)/shard_map/ppermute | solution.py:53
  107.8 5.0 %collective-permute-start.30 = (bf16[4,1,2,2,1,2,16,128]{7,6,0,5,4,3,2,1:T(8,128)(2,1)S(1)}, bf16[4,1,2,2,1,2,16,128]{7,6,0,5,4,3,2,1:T(8,128)(2,1)S(1)}, u32[]{:S(2)}, u32[]{:S(2)}) collective-permute-start(bf16[4,1,2,2,1,2,16,128]{7,6,0,5,4,3,2,1:T(8,128)(2,1)S(1)} %maximum_select_fusion.11), channel_id=1, source_target_pairs={{0,8},{4,12},{8,0},{12,4},{16,24},{20,28},{24,16},{28,20},{1,9},{5... | collective-permute-start | bytes 393224 | tf_op jit(solution)/shard_map/ppermute | solution.py:53
  109.0 4.1 %collective-permute-start.21 = (bf16[4,1,2,2,2,2,16,128]{7,6,0,5,4,3,2,1:T(8,128)(2,1)S(1)}, bf16[4,1,2,2,2,2,16,128]{7,6,0,5,4,3,2,1:T(8,128)(2,1)S(1)}, u32[]{:S(2)}, u32[]{:S(2)}) collective-permute-start(bf16[4,1,2,2,2,2,16,128]{7,6,0,5,4,3,2,1:T(8,128)(2,1)S(1)} %maximum_select_fusion.3), channel_id=1, source_target_pairs={{0,1},{1,0},{2,3},{3,2},{4,5},{5,4},{6,7},{7,6},{8,9},{9,8},{10,11... | collective-permute-start | bytes 786440 | tf_op jit(solution)/shard_map/ppermute | solution.py:53
  110.2 3.0 %collective-permute-start.26 = (bf16[4,1,2,2,2,2,16,128]{7,6,0,5,4,3,2,1:T(8,128)(2,1)S(1)}, bf16[4,1,2,2,2,2,16,128]{7,6,0,5,4,3,2,1:T(8,128)(2,1)S(1)}, u32[]{:S(2)}, u32[]{:S(2)}) collective-permute-start(bf16[4,1,2,2,2,2,16,128]{7,6,0,5,4,3,2,1:T(8,128)(2,1)S(1)} %maximum_select_fusion.4), channel_id=1, source_target_pairs={{0,1},{1,0},{2,3},{3,2},{4,5},{5,4},{6,7},{7,6},{8,9},{9,8},{10,11... | collective-permute-start | bytes 786440 | tf_op jit(solution)/shard_map/ppermute | solution.py:53
  (13 other events, 80.0 us)
Sparse Core Ops, SparseCore 0:
  30.9 24.7 all-gather.1

commit v7 on v6

--- a/solution.py
+++ b/solution.py
@@ -90,7 +90,7 @@
     picked = jnp.take(extended, margin, axis=0)
     local = jnp.einsum("jerb,jebc->jrc", picked, inverse_blocks, preferred_element_type=jnp.float32)
     for step in range(nb):
-        wire = jnp.float32
+        wire = jnp.bfloat16 if step in (1, 2) else jnp.float32
         parts = [halve(x, 1 + orders[s][step], *bits[orders[s][step]], wire) for s, x in enumerate(parts)]
         if step == 0:
             local, parts = lax.optimization_barrier((local, parts))

time: 130 us -> 122 us (0.938)
  waiting for transfers between devices: 20 us -> 14.9 us
    ppermute x15, waiting for transfers between devices: 7.72 us -> 2.78 us  [halve(): lax.ppermute(send.astype(wire), axis, pairs(axis, mask)).astype(x.dtype)]
    unnamed x28 -> x26, local copies, waits for them, and re-layouts: 3.56 us -> 2.77 us
  transfers between devices with their start and end apart: 33 -> 33, of which waited for: 15 -> 13; matrix products, arithmetic and copies ran while one was open for 17% -> 17% of each run, Pallas kernels for 0% -> 0%
where the time goes in v7:
time: 122 us
  starting transfers between devices  44.9 us (37%)
  local copies, waits for them, and re-layouts  20.7 us (17%)
  matrix products  16.1 us (13%)
  waiting for transfers between devices  14.9 us (12%)
  between operations  14.1 us (12%)
  other arithmetic  11 us (9%)
    ppermute x15, starting transfers between devices, halve(): lax.ppermute(send.astype(wire), axis, pairs(axis, mask)).astype(x.dtype)  26.3 us
    ppermute x15, starting transfers between devices, double(): recv = lax.ppermute(y, axis, pairs(axis, mask))  15.4 us
    ppermute x15, waiting for transfers between devices, double(): recv = lax.ppermute(y, axis, pairs(axis, mask))  8.79 us
    dot_general x1, matrix products, per_device(): jnp.einsum('jerb,jebc->jrc', picked, inverse_blocks, preferred_element_ty...  5.13 us
    gather x1, local copies, waits for them, and re-layouts, per_device(): picked = jnp.take(extended, margin, axis=0)  4.2 us
    dot_general x1, matrix products, per_device(): jnp.einsum('jqn,jqrc->nrc', onehot, terms, precision=lax.Precision.HIGHEST)  4.18 us
    add x12, other arithmetic, halve(): keep + lax.ppermute(send.astype(wire), axis, pairs(axis, mask)).astype(x....  3.55 us
    dot_general x1, matrix products, per_device(): jnp.einsum('jrb,jqbc->jqrc', residual, basis, preferred_element_type=jnp....  3.38 us
  transfers between devices with their start and end apart: 33, of which 13 were waited for; matrix products, arithmetic and copies ran while one was open for 17% of the time, Pallas kernels for 0%

profile of v7, /device:TPU:0, one launch (start us, length us, event | category | flops | bytes accessed | tf_op | source)
XLA Modules:
  0.0 121.7 jit_solution(10293358561080791880)
XLA Ops:
  6.5 3.4 %convolution_bitcast_fusion.1 = f32[4,2,512,128]{2,3,1,0:T(8,128)} fusion(bf16[4,2,256,128]{3,2,1,0:T(8,128)(2,1)} %param.11, bf16[4,512,256]{2,1,0:T(8,128)(2,1)} %param.7), kind=kOutput, calls=%fused_computation.11 | convolution fusion | flops 268435456 | bytes 3670016 | tf_op jit(solution)/shard_map/jrb,jqbc->jqrc/dot_general | solution.py:76
  9.9 2.9 %copy.75 = f32[4,2,512,128]{3,0,1,2:T(4,128)} copy(f32[4,2,512,128]{2,3,1,0:T(8,128)} %convolution_bitcast_fusion.1) | data formatting | bytes 4194304 | tf_op jit(solution)/shard_map/jrb,jqbc->jqrc/transpose | solution.py:76
  12.9 4.2 %convolution_bitcast_fusion = f32[12,512,128]{2,0,1:T(8,128)S(1)} fusion(f32[4,2,512,128]{3,0,1,2:T(4,128)} %copy.75, s32[4,2]{0,1:T(2,128)S(1)} %copy-done.9), kind=kOutput, calls=%fused_computation.6 | convolution fusion | flops 75497568 | bytes 5242912 | tf_op jit(solution)/shard_map/jqn,jqrc->nrc/dot_general | solution.py:79
  17.0 1.8 %fusion.48 = (f32[4,512,128]{2,0,1:T(4,128)S(1)}, f32[4,512,128]{2,0,1:T(4,128)}, f32[4,512,128]{2,0,1:T(4,128)}) fusion(f32[12,512,128]{2,0,1:T(8,128)S(1)} %convolution_bitcast_fusion), kind=kLoop, calls=%fused_computation.129 | loop fusion | bytes 6291456 | tf_op jit(solution)/shard_map/slice | solution.py:89
  18.8 2.5 %constant_dynamic-slice_fusion.7 = (f32[4,1,2,2,2,2,16,128]{7,0,6,5,4,3,2,1:T(4,128)}, f32[4,1,2,2,2,2,16,128]{7,0,6,5,4,3,2,1:T(4,128)S(1)}, f32[4,1,2,2,2,2,16...) fusion(f32[4,2,2,2,2,2,16,128]{7,0,6,5,4,3,2,1:T(4,128)S(1)} %bitcast.119, s32[]{:T(128)S(6)} %select_n.673, ...), kind=kLoop, calls=%fused_computation.96 | loop fusion | bytes 4194312 | tf_op jit(solution)/shard_map/jit(dynamic_index_in_dim)/dynamic_slice | solution.py:46
  26.6 2.0 %collective-permute-start = (bf16[1,512,256]{2,1,0:T(8,128)(2,1)}, bf16[1,512,256]{2,1,0:T(8,128)(2,1)S(1)}, u32[]{:S(2)}, u32[]{:S(2)}) collective-permute-start(bf16[1,512,256]{2,1,0:T(8,128)(2,1)} %get-tuple-element.22), channel_id=1, source_target_pairs={{0,1},{1,2},{2,3},{3,4},{4,5},{5,6},{6,7},{7,8},{8,9},{9,10},{10,1... | collective-permute-start | bytes 786440 | tf_op jit(solution)/shard_map/ppermute | solution.py:15
  31.1 3.3 %collective-permute-done.1 = bf16[1,512,256]{2,1,0:T(8,128)(2,1)} collective-permute-done((bf16[1,512,256]{2,1,0:T(8,128)(2,1)}, bf16[1,512,256]{2,1,0:T(8,128)(2,1)}, u32[]{:S(2)}, u32[]{:S(2)}) %collective-permute-start.1) | collective-permute-done | bytes 262176 | tf_op jit(solution)/shard_map/ppermute | solution.py:17
  34.4 2.3 %pad_maximum_fusion = bf16[6,512,256]{2,1,0:T(8,128)(2,1)} fusion(bf16[1,512,256]{2,1,0:T(8,128)(2,1)} %collective-permute-done.1, bf16[4,512,256]{2,1,0:T(8,128)(2,1)S(1)} %copy-done.1, bf16[1,512,256]{2,1,0:T(8,128)(2,1)S(1)} %collective-permute-done), kind=kLoop, calls=%fused_computation.14 | loop fusion | flops 1572864 | bytes 3145728 | tf_op jit(solution)/shard_map/concatenate | solution.py:13
  36.7 4.2 %gather_fusion = bf16[16,512,256]{2,1,0:T(8,128)(2,1)} fusion(bf16[6,512,256]{2,1,0:T(8,128)(2,1)} %pad_maximum_fusion, s32[1024]{0:T(1024)S(1)} %pad_clamp_fusion.2), kind=kCustom, calls=%fused_computation | custom fusion | bytes 8388672 | tf_op jit(solution)/shard_map/jit(_take)/gather | solution.py:90
  40.9 5.1 %fusion.5 = f32[4,512,256]{2,1,0:T(8,128)} fusion(bf16[4,4,256,256]{3,2,1,0:T(8,128)(2,1)S(1)} %copy-done, bf16[4,4,512,256]{3,2,1,0:T(8,128)(2,1)} %bitcast.118, pred[4,4]{1,0:T(4,128)(4,1)S(1)} %compare_and_fusion.2), kind=kOutput, calls=%fused_computation.10 | convolution fusion | flops 1075838976 | bytes 8388624 | tf_op jit(solution)/shard_map/jerb,jebc->jrc/dot_general | solution.py:91
  49.6 4.4 %collective-permute-start.5 = (bf16[4,1,1,2,2,2,16,128]{7,6,0,5,4,3,2,1:T(8,128)(2,1)S(1)}, bf16[4,1,1,2,2,2,16,128]{7,6,0,5,4,3,2,1:T(8,128)(2,1)S(1)}, u32[]{:S(2)}, u32[]{:S(2)}) collective-permute-start(bf16[4,1,1,2,2,2,16,128]{7,6,0,5,4,3,2,1:T(8,128)(2,1)S(1)} %dynamic-slice_convert_fusion.2), channel_id=1, source_target_pairs={{0,2},{1,3},{2,0},{3,1},{4,6},{5,7},{6,4},{7,5},{8,10},{9,11},{10,... | collective-permute-start | bytes 393224 | tf_op jit(solution)/shard_map/ppermute | solution.py:48
  53.9 1.5 %collective-permute-start.9 = (bf16[4,1,2,1,2,2,16,128]{7,6,0,5,4,3,2,1:T(8,128)(2,1)S(1)}, bf16[4,1,2,1,2,2,16,128]{7,6,0,5,4,3,2,1:T(8,128)(2,1)S(1)}, u32[]{:S(2)}, u32[]{:S(2)}) collective-permute-start(bf16[4,1,2,1,2,2,16,128]{7,6,0,5,4,3,2,1:T(8,128)(2,1)S(1)} %dynamic-slice_convert_fusion.1), channel_id=1, source_target_pairs={{0,4},{4,0},{8,12},{12,8},{16,20},{20,16},{24,28},{28,24},{1,5},{5... | collective-permute-start | bytes 393224 | tf_op jit(solution)/shard_map/ppermute | solution.py:48
  55.5 1.6 %collective-permute-start.13 = (bf16[4,1,2,2,1,2,16,128]{7,6,0,5,4,3,2,1:T(8,128)(2,1)S(1)}, bf16[4,1,2,2,1,2,16,128]{7,6,0,5,4,3,2,1:T(8,128)(2,1)S(1)}, u32[]{:S(2)}, u32[]{:S(2)}) collective-permute-start(bf16[4,1,2,2,1,2,16,128]{7,6,0,5,4,3,2,1:T(8,128)(2,1)S(1)} %dynamic-slice_convert_fusion), channel_id=1, source_target_pairs={{0,8},{4,12},{8,0},{12,4},{16,24},{20,28},{24,16},{28,20},{1,9},{5... | collective-permute-start | bytes 393224 | tf_op jit(solution)/shard_map/ppermute | solution.py:48
  57.2 2.7 %collective-permute-start.6 = (bf16[4,1,1,1,2,2,16,128]{7,6,0,5,4,3,2,1:T(8,128)(2,1)S(1)}, bf16[4,1,1,1,2,2,16,128]{7,6,0,5,4,3,2,1:T(8,128)(2,1)S(1)}, u32[]{:S(2)}, u32[]{:S(2)}) collective-permute-start(bf16[4,1,1,1,2,2,16,128]{7,6,0,5,4,3,2,1:T(8,128)(2,1)S(1)} %dynamic-slice_convert_fusion.5), channel_id=1, source_target_pairs={{0,4},{4,0},{8,12},{12,8},{16,20},{20,16},{24,28},{28,24},{1,5},{5... | collective-permute-start | bytes 196616 | tf_op jit(solution)/shard_map/ppermute | solution.py:48
  60.0 2.4 %collective-permute-start.10 = (bf16[4,1,2,1,1,2,16,128]{7,6,0,5,4,3,2,1:T(8,128)(2,1)S(1)}, bf16[4,1,2,1,1,2,16,128]{7,6,0,5,4,3,2,1:T(8,128)(2,1)S(1)}, u32[]{:S(2)}, u32[]{:S(2)}) collective-permute-start(bf16[4,1,2,1,1,2,16,128]{7,6,0,5,4,3,2,1:T(8,128)(2,1)S(1)} %dynamic-slice_convert_fusion.4), channel_id=1, source_target_pairs={{0,8},{4,12},{8,0},{12,4},{16,24},{20,28},{24,16},{28,20},{1,9},{5... | collective-permute-start | bytes 196616 | tf_op jit(solution)/shard_map/ppermute | solution.py:48
  62.4 3.3 %collective-permute-start.14 = (bf16[4,1,2,2,1,1,16,128]{7,6,0,5,4,3,2,1:T(8,128)(2,1)S(1)}, bf16[4,1,2,2,1,1,16,128]{7,6,0,5,4,3,2,1:T(8,128)(2,1)S(1)}, u32[]{:S(2)}, u32[]{:S(2)}) collective-permute-start(bf16[4,1,2,2,1,1,16,128]{7,6,0,5,4,3,2,1:T(8,128)(2,1)S(1)} %dynamic-slice_convert_fusion.3), channel_id=1, source_target_pairs={{0,16},{4,20},{8,24},{12,28},{16,0},{20,4},{24,8},{28,12},{1,17},{... | collective-permute-start | bytes 196616 | tf_op jit(solution)/shard_map/ppermute | solution.py:48
  66.6 2.6 %collective-permute-start.11 = (f32[4,1,2,1,1,1,16,128]{7,6,0,5,4,3,2,1:T(8,128)S(1)}, f32[4,1,2,1,1,1,16,128]{7,6,0,5,4,3,2,1:T(8,128)S(1)}, u32[]{:S(2)}, u32[]{:S(2)}) collective-permute-start(f32[4,1,2,1,1,1,16,128]{7,6,0,5,4,3,2,1:T(8,128)S(1)} %constant_dynamic-slice_fusion.3), channel_id=1, source_target_pairs={{0,16},{4,20},{8,24},{12,28},{16,0},{20,4},{24,8},{28,12},{1,17},{... | collective-permute-start | bytes 196616 | tf_op jit(solution)/shard_map/ppermute | solution.py:48
  69.3 1.7 %collective-permute-start.15 = (f32[4,1,1,2,1,1,16,128]{7,6,0,5,4,3,2,1:T(8,128)S(1)}, f32[4,1,1,2,1,1,16,128]{7,6,0,5,4,3,2,1:T(8,128)S(1)}, u32[]{:S(2)}, u32[]{:S(2)}) collective-permute-start(f32[4,1,1,2,1,1,16,128]{7,6,0,5,4,3,2,1:T(8,128)S(1)} %constant_dynamic-slice_fusion.1), channel_id=1, source_target_pairs={{0,2},{1,3},{2,0},{3,1},{4,6},{5,7},{6,4},{7,5},{8,10},{9,11},{10,... | collective-permute-start | bytes 196616 | tf_op jit(solution)/shard_map/ppermute | solution.py:48
  71.1 1.5 %collective-permute-start.8 = (f32[4,1,1,1,1,1,16,128]{7,6,0,5,4,3,2,1:T(8,128)S(1)}, f32[4,1,1,1,1,1,16,128]{7,6,0,5,4,3,2,1:T(8,128)S(1)}, u32[]{:S(2)}, u32[]{:S(2)}) collective-permute-start(f32[4,1,1,1,1,1,16,128]{7,6,0,5,4,3,2,1:T(8,128)S(1)} %constant_dynamic-slice_fusion.4), channel_id=1, source_target_pairs={{0,16},{4,20},{8,24},{12,28},{16,0},{20,4},{24,8},{28,12},{1,17},{... | collective-permute-start | bytes 98312 | tf_op jit(solution)/shard_map/ppermute | solution.py:48
  72.7 1.4 %collective-permute-start.12 = (f32[4,1,1,1,1,1,16,128]{7,6,0,5,4,3,2,1:T(8,128)S(1)}, f32[4,1,1,1,1,1,16,128]{7,6,0,5,4,3,2,1:T(8,128)S(1)}, u32[]{:S(2)}, u32[]{:S(2)}) collective-permute-start(f32[4,1,1,1,1,1,16,128]{7,6,0,5,4,3,2,1:T(8,128)S(1)} %constant_dynamic-slice_fusion.2), channel_id=1, source_target_pairs={{0,2},{1,3},{2,0},{3,1},{4,6},{5,7},{6,4},{7,5},{8,10},{9,11},{10,... | collective-permute-start | bytes 98312 | tf_op jit(solution)/shard_map/ppermute | solution.py:48
  76.7 1.4 %collective-permute-done.16 = f32[4,1,1,1,1,1,16,128]{7,6,0,5,4,3,2,1:T(8,128)S(1)} collective-permute-done((f32[4,1,1,1,1,1,16,128]{7,6,0,5,4,3,2,1:T(8,128)S(1)}, f32[4,1,1,1,1,1,16,128]{7,6,0,5,4,3,2,1:T(8,128)S(1)}, u32[]{:S(2)}, u32[]{:S(2)}) %collective-permute-start.16) | collective-permute-done | bytes 32800 | tf_op jit(solution)/shard_map/ppermute | solution.py:48
  80.1 1.8 %fusion.13 = bf16[12,16,128]{2,1,0:T(8,128)(2,1)S(1)} fusion(bf16[12,4,136,128]{3,2,1,0:T(8,128)(2,1)} %all-gather.2.cloned.1.call-done, bf16[12,4,16,128]{3,2,1,0:T(8,128)(2,1)S(1)} %bitcast.132, pred[12,4]{1,0:T(8,128)(4,1)S(1)} %copy.84), kind=kOutput, calls=%fused_computation.17 | convolution fusion | flops 25288704 | bytes 1818672 | tf_op jit(solution)/shard_map/nerc,necd->nrd/dot_general | solution.py:100
  81.9 1.7 %collective-permute-start.17 = (bf16[4,1,1,1,1,1,16,128]{7,6,0,5,4,3,2,1:T(8,128)(2,1)S(1)}, bf16[4,1,1,1,1,1,16,128]{7,6,0,5,4,3,2,1:T(8,128)(2,1)S(1)}, u32[]{:S(2)}, u32[]{:S(2)}) collective-permute-start(bf16[4,1,1,1,1,1,16,128]{7,6,0,5,4,3,2,1:T(8,128)(2,1)S(1)} %get-tuple-element.32), channel_id=1, source_target_pairs={{0,16},{4,20},{8,24},{12,28},{16,0},{20,4},{24,8},{28,12},{1,17},{... | collective-permute-start | bytes 49160 | tf_op jit(solution)/shard_map/ppermute | solution.py:53
  83.8 1.5 %collective-permute-start.22 = (bf16[4,1,1,1,1,1,16,128]{7,6,0,5,4,3,2,1:T(8,128)(2,1)S(1)}, bf16[4,1,1,1,1,1,16,128]{7,6,0,5,4,3,2,1:T(8,128)(2,1)S(1)}, u32[]{:S(2)}, u32[]{:S(2)}) collective-permute-start(bf16[4,1,1,1,1,1,16,128]{7,6,0,5,4,3,2,1:T(8,128)(2,1)S(1)} %get-tuple-element.33), channel_id=1, source_target_pairs={{0,2},{1,3},{2,0},{3,1},{4,6},{5,7},{6,4},{7,5},{8,10},{9,11},{10,... | collective-permute-start | bytes 49160 | tf_op jit(solution)/shard_map/ppermute | solution.py:53
  88.1 1.9 %collective-permute-start.23 = (bf16[4,1,2,1,1,1,16,128]{7,6,0,2,5,4,3,1:T(8,128)(2,1)S(1)}, bf16[4,1,2,1,1,1,16,128]{7,6,0,2,5,4,3,1:T(8,128)(2,1)S(1)}, u32[]{:S(2)}, u32[]{:S(2)}) collective-permute-start(bf16[4,1,2,1,1,1,16,128]{7,6,0,2,5,4,3,1:T(8,128)(2,1)S(1)} %fusion.27), channel_id=1, source_target_pairs={{0,16},{4,20},{8,24},{12,28},{16,0},{20,4},{24,8},{28,12},{1,17},{... | collective-permute-start | bytes 98312 | tf_op jit(solution)/shard_map/ppermute | solution.py:53
  90.0 1.9 %collective-permute-start.28 = (bf16[4,1,1,2,1,1,16,128]{7,6,0,5,4,3,2,1:T(8,128)(2,1)S(1)}, bf16[4,1,1,2,1,1,16,128]{7,6,0,5,4,3,2,1:T(8,128)(2,1)S(1)}, u32[]{:S(2)}, u32[]{:S(2)}) collective-permute-start(bf16[4,1,1,2,1,1,16,128]{7,6,0,5,4,3,2,1:T(8,128)(2,1)S(1)} %maximum_select_fusion.22), channel_id=1, source_target_pairs={{0,2},{1,3},{2,0},{3,1},{4,6},{5,7},{6,4},{7,5},{8,10},{9,11},{10,... | collective-permute-start | bytes 98312 | tf_op jit(solution)/shard_map/ppermute | solution.py:53
  94.4 1.5 %collective-permute-start.29 = (bf16[4,1,2,2,1,1,16,128]{7,6,0,5,4,3,2,1:T(8,128)(2,1)S(1)}, bf16[4,1,2,2,1,1,16,128]{7,6,0,5,4,3,2,1:T(8,128)(2,1)S(1)}, u32[]{:S(2)}, u32[]{:S(2)}) collective-permute-start(bf16[4,1,2,2,1,1,16,128]{7,6,0,5,4,3,2,1:T(8,128)(2,1)S(1)} %fusion.26), channel_id=1, source_target_pairs={{0,16},{4,20},{8,24},{12,28},{16,0},{20,4},{24,8},{28,12},{1,17},{... | collective-permute-start | bytes 196616 | tf_op jit(solution)/shard_map/ppermute | solution.py:53
  98.8 1.6 %collective-permute-start.25 = (bf16[4,1,2,1,2,2,16,128]{7,6,0,5,4,3,2,1:T(8,128)(2,1)S(1)}, bf16[4,1,2,1,2,2,16,128]{7,6,0,5,4,3,2,1:T(8,128)(2,1)S(1)}, u32[]{:S(2)}, u32[]{:S(2)}) collective-permute-start(bf16[4,1,2,1,2,2,16,128]{7,6,0,5,4,3,2,1:T(8,128)(2,1)S(1)} %maximum_select_fusion.9), channel_id=1, source_target_pairs={{0,4},{4,0},{8,12},{12,8},{16,20},{20,16},{24,28},{28,24},{1,5},{5... | collective-permute-start | bytes 393224 | tf_op jit(solution)/shard_map/ppermute | solution.py:53
  102.1 1.8 %collective-permute-done.25 = bf16[4,1,2,1,2,2,16,128]{7,6,0,5,4,3,2,1:T(8,128)(2,1)S(1)} collective-permute-done((bf16[4,1,2,1,2,2,16,128]{7,6,0,5,4,3,2,1:T(8,128)(2,1)S(1)}, bf16[4,1,2,1,2,2,16,128]{7,6,0,5,4,3,2,1:T(8,128)(2,1)S(1)}, u32[]{:S(2)}, u32[]{:S(2)}) %collective-permute-start.25) | collective-permute-done | bytes 131104 | tf_op jit(solution)/shard_map/ppermute | solution.py:53
  103.9 1.5 %collective-permute-done.30 = bf16[4,1,2,2,1,2,16,128]{7,6,0,5,4,3,2,1:T(8,128)(2,1)S(1)} collective-permute-done((bf16[4,1,2,2,1,2,16,128]{7,6,0,5,4,3,2,1:T(8,128)(2,1)S(1)}, bf16[4,1,2,2,1,2,16,128]{7,6,0,5,4,3,2,1:T(8,128)(2,1)S(1)}, u32[]{:S(2)}, u32[]{:S(2)}) %collective-permute-start.30) | collective-permute-done | bytes 131104 | tf_op jit(solution)/shard_map/ppermute | solution.py:53
  109.8 2.2 %gather_fusion.2 = bf16[8,512,128]{2,1,0:T(8,128)(2,1)S(1)} fusion(bf16[12,512,128]{2,1,0:T(8,128)(2,1)} %pad_maximum_fusion.1, s32[1024]{0:T(1024)S(1)} %pad_clamp_fusion), kind=kCustom, calls=%fused_computation.2 | custom fusion | bytes 2097184 | tf_op jit(solution)/shard_map/jit(_take)/gather | solution.py:109
  111.9 1.7 %fusion.17 = f32[4,512,256,1]{2,1,3,0:T(8,128)S(1)} fusion(bf16[4,2,256,128]{3,2,1,0:T(8,128)(2,1)} %param.11, bf16[4,2,512,128]{3,2,1,0:T(8,128)(2,1)S(1)} %bitcast.121, pred[4,2]{1,0:T(4,128)(4,1)S(1)} %copy.82), kind=kOutput, calls=%fused_computation.19 | convolution fusion | flops 268959744 | bytes 3670024 | tf_op jit(solution)/shard_map/jqrc,jqbc->jrb/dot_general | solution.py:110
  (154 shorter events, 32.4 us)
Async XLA Ops:
  6.5 71.6 %all-gather.2.cloned.1.call-start = ((), (), s32[]{:S(2)}) async-start(), calls=%async_computation | async-start | bytes 2088960 | tf_op jit(solution)/shard_map/all_gather | solution.py:69
  22.1 23.9 %collective-permute-start.4 = (f32[4,1,2,2,2,2,16,128]{7,6,0,5,4,3,2,1:T(8,128)}, f32[4,1,2,2,2,2,16,128]{7,6,0,5,4,3,2,1:T(8,128)}, u32[]{:S(2)}, u32[]{:S(2)}) collective-permute-start(f32[4,1,2,2,2,2,16,128]{7,6,0,5,4,3,2,1:T(8,128)} %copy.110), channel_id=1, source_target_pairs={{0,1},{1,0},{2,3},{3,2},{4,5},{5,4},{6,7},{7,6},{8,9},{9,8},{10,11... | collective-permute-start | bytes 1572872 | tf_op jit(solution)/shard_map/ppermute | solution.py:48
  23.4 23.8 %collective-permute-start.3 = (f32[4,1,2,2,2,2,16,128]{7,6,0,5,4,3,2,1:T(8,128)}, f32[4,1,2,2,2,2,16,128]{7,6,0,5,4,3,2,1:T(8,128)}, u32[]{:S(2)}, u32[]{:S(2)}) collective-permute-start(f32[4,1,2,2,2,2,16,128]{7,6,0,5,4,3,2,1:T(8,128)} %copy.108), channel_id=1, source_target_pairs={{0,1},{1,0},{2,3},{3,2},{4,5},{5,4},{6,7},{7,6},{8,9},{9,8},{10,11... | collective-permute-start | bytes 1572872 | tf_op jit(solution)/shard_map/ppermute | solution.py:48
  25.3 23.1 %collective-permute-start.2 = (f32[4,1,2,2,2,2,16,128]{7,6,0,5,4,3,2,1:T(8,128)}, f32[4,1,2,2,2,2,16,128]{7,6,0,5,4,3,2,1:T(8,128)}, u32[]{:S(2)}, u32[]{:S(2)}) collective-permute-start(f32[4,1,2,2,2,2,16,128]{7,6,0,5,4,3,2,1:T(8,128)} %copy.106), channel_id=1, source_target_pairs={{0,1},{1,0},{2,3},{3,2},{4,5},{5,4},{6,7},{7,6},{8,9},{9,8},{10,11... | collective-permute-start | bytes 1572872 | tf_op jit(solution)/shard_map/ppermute | solution.py:48
  26.6 4.5 %collective-permute-start = (bf16[1,512,256]{2,1,0:T(8,128)(2,1)}, bf16[1,512,256]{2,1,0:T(8,128)(2,1)S(1)}, u32[]{:S(2)}, u32[]{:S(2)}) collective-permute-start(bf16[1,512,256]{2,1,0:T(8,128)(2,1)} %get-tuple-element.22), channel_id=1, source_target_pairs={{0,1},{1,2},{2,3},{3,4},{4,5},{5,6},{6,7},{7,8},{8,9},{9,10},{10,1... | collective-permute-start | bytes 786440 | tf_op jit(solution)/shard_map/ppermute | solution.py:15
  28.6 5.9 %collective-permute-start.1 = (bf16[1,512,256]{2,1,0:T(8,128)(2,1)}, bf16[1,512,256]{2,1,0:T(8,128)(2,1)}, u32[]{:S(2)}, u32[]{:S(2)}) collective-permute-start(bf16[1,512,256]{2,1,0:T(8,128)(2,1)} %get-tuple-element.23), channel_id=1, source_target_pairs={{1,0},{2,1},{3,2},{4,3},{5,4},{6,5},{7,6},{8,7},{9,8},{10,9},{11,1... | collective-permute-start | bytes 786440 | tf_op jit(solution)/shard_map/ppermute | solution.py:17
  49.6 7.6 %collective-permute-start.5 = (bf16[4,1,1,2,2,2,16,128]{7,6,0,5,4,3,2,1:T(8,128)(2,1)S(1)}, bf16[4,1,1,2,2,2,16,128]{7,6,0,5,4,3,2,1:T(8,128)(2,1)S(1)}, u32[]{:S(2)}, u32[]{:S(2)}) collective-permute-start(bf16[4,1,1,2,2,2,16,128]{7,6,0,5,4,3,2,1:T(8,128)(2,1)S(1)} %dynamic-slice_convert_fusion.2), channel_id=1, source_target_pairs={{0,2},{1,3},{2,0},{3,1},{4,6},{5,7},{6,4},{7,5},{8,10},{9,11},{10,... | collective-permute-start | bytes 393224 | tf_op jit(solution)/shard_map/ppermute | solution.py:48
  53.9 6.0 %collective-permute-start.9 = (bf16[4,1,2,1,2,2,16,128]{7,6,0,5,4,3,2,1:T(8,128)(2,1)S(1)}, bf16[4,1,2,1,2,2,16,128]{7,6,0,5,4,3,2,1:T(8,128)(2,1)S(1)}, u32[]{:S(2)}, u32[]{:S(2)}) collective-permute-start(bf16[4,1,2,1,2,2,16,128]{7,6,0,5,4,3,2,1:T(8,128)(2,1)S(1)} %dynamic-slice_convert_fusion.1), channel_id=1, source_target_pairs={{0,4},{4,0},{8,12},{12,8},{16,20},{20,16},{24,28},{28,24},{1,5},{5... | collective-permute-start | bytes 393224 | tf_op jit(solution)/shard_map/ppermute | solution.py:48
  55.5 6.9 %collective-permute-start.13 = (bf16[4,1,2,2,1,2,16,128]{7,6,0,5,4,3,2,1:T(8,128)(2,1)S(1)}, bf16[4,1,2,2,1,2,16,128]{7,6,0,5,4,3,2,1:T(8,128)(2,1)S(1)}, u32[]{:S(2)}, u32[]{:S(2)}) collective-permute-start(bf16[4,1,2,2,1,2,16,128]{7,6,0,5,4,3,2,1:T(8,128)(2,1)S(1)} %dynamic-slice_convert_fusion), channel_id=1, source_target_pairs={{0,8},{4,12},{8,0},{12,4},{16,24},{20,28},{24,16},{28,20},{1,9},{5... | collective-permute-start | bytes 393224 | tf_op jit(solution)/shard_map/ppermute | solution.py:48
  57.2 8.5 %collective-permute-start.6 = (bf16[4,1,1,1,2,2,16,128]{7,6,0,5,4,3,2,1:T(8,128)(2,1)S(1)}, bf16[4,1,1,1,2,2,16,128]{7,6,0,5,4,3,2,1:T(8,128)(2,1)S(1)}, u32[]{:S(2)}, u32[]{:S(2)}) collective-permute-start(bf16[4,1,1,1,2,2,16,128]{7,6,0,5,4,3,2,1:T(8,128)(2,1)S(1)} %dynamic-slice_convert_fusion.5), channel_id=1, source_target_pairs={{0,4},{4,0},{8,12},{12,8},{16,20},{20,16},{24,28},{28,24},{1,5},{5... | collective-permute-start | bytes 196616 | tf_op jit(solution)/shard_map/ppermute | solution.py:48
  60.0 6.6 %collective-permute-start.10 = (bf16[4,1,2,1,1,2,16,128]{7,6,0,5,4,3,2,1:T(8,128)(2,1)S(1)}, bf16[4,1,2,1,1,2,16,128]{7,6,0,5,4,3,2,1:T(8,128)(2,1)S(1)}, u32[]{:S(2)}, u32[]{:S(2)}) collective-permute-start(bf16[4,1,2,1,1,2,16,128]{7,6,0,5,4,3,2,1:T(8,128)(2,1)S(1)} %dynamic-slice_convert_fusion.4), channel_id=1, source_target_pairs={{0,8},{4,12},{8,0},{12,4},{16,24},{20,28},{24,16},{28,20},{1,9},{5... | collective-permute-start | bytes 196616 | tf_op jit(solution)/shard_map/ppermute | solution.py:48
  62.4 6.9 %collective-permute-start.14 = (bf16[4,1,2,2,1,1,16,128]{7,6,0,5,4,3,2,1:T(8,128)(2,1)S(1)}, bf16[4,1,2,2,1,1,16,128]{7,6,0,5,4,3,2,1:T(8,128)(2,1)S(1)}, u32[]{:S(2)}, u32[]{:S(2)}) collective-permute-start(bf16[4,1,2,2,1,1,16,128]{7,6,0,5,4,3,2,1:T(8,128)(2,1)S(1)} %dynamic-slice_convert_fusion.3), channel_id=1, source_target_pairs={{0,16},{4,20},{8,24},{12,28},{16,0},{20,4},{24,8},{28,12},{1,17},{... | collective-permute-start | bytes 196616 | tf_op jit(solution)/shard_map/ppermute | solution.py:48
  65.8 5.3 %collective-permute-start.7 = (f32[4,1,1,1,1,2,16,128]{7,6,0,5,4,3,2,1:T(8,128)S(1)}, f32[4,1,1,1,1,2,16,128]{7,6,0,5,4,3,2,1:T(8,128)S(1)}, u32[]{:S(2)}, u32[]{:S(2)}) collective-permute-start(f32[4,1,1,1,1,2,16,128]{7,6,0,5,4,3,2,1:T(8,128)S(1)} %constant_dynamic-slice_fusion.5), channel_id=1, source_target_pairs={{0,8},{4,12},{8,0},{12,4},{16,24},{20,28},{24,16},{28,20},{1,9},{5... | collective-permute-start | bytes 196616 | tf_op jit(solution)/shard_map/ppermute | solution.py:48
  66.6 6.0 %collective-permute-start.11 = (f32[4,1,2,1,1,1,16,128]{7,6,0,5,4,3,2,1:T(8,128)S(1)}, f32[4,1,2,1,1,1,16,128]{7,6,0,5,4,3,2,1:T(8,128)S(1)}, u32[]{:S(2)}, u32[]{:S(2)}) collective-permute-start(f32[4,1,2,1,1,1,16,128]{7,6,0,5,4,3,2,1:T(8,128)S(1)} %constant_dynamic-slice_fusion.3), channel_id=1, source_target_pairs={{0,16},{4,20},{8,24},{12,28},{16,0},{20,4},{24,8},{28,12},{1,17},{... | collective-permute-start | bytes 196616 | tf_op jit(solution)/shard_map/ppermute | solution.py:48
  69.3 4.7 %collective-permute-start.15 = (f32[4,1,1,2,1,1,16,128]{7,6,0,5,4,3,2,1:T(8,128)S(1)}, f32[4,1,1,2,1,1,16,128]{7,6,0,5,4,3,2,1:T(8,128)S(1)}, u32[]{:S(2)}, u32[]{:S(2)}) collective-permute-start(f32[4,1,1,2,1,1,16,128]{7,6,0,5,4,3,2,1:T(8,128)S(1)} %constant_dynamic-slice_fusion.1), channel_id=1, source_target_pairs={{0,2},{1,3},{2,0},{3,1},{4,6},{5,7},{6,4},{7,5},{8,10},{9,11},{10,... | collective-permute-start | bytes 196616 | tf_op jit(solution)/shard_map/ppermute | solution.py:48
  71.1 5.0 %collective-permute-start.8 = (f32[4,1,1,1,1,1,16,128]{7,6,0,5,4,3,2,1:T(8,128)S(1)}, f32[4,1,1,1,1,1,16,128]{7,6,0,5,4,3,2,1:T(8,128)S(1)}, u32[]{:S(2)}, u32[]{:S(2)}) collective-permute-start(f32[4,1,1,1,1,1,16,128]{7,6,0,5,4,3,2,1:T(8,128)S(1)} %constant_dynamic-slice_fusion.4), channel_id=1, source_target_pairs={{0,16},{4,20},{8,24},{12,28},{16,0},{20,4},{24,8},{28,12},{1,17},{... | collective-permute-start | bytes 98312 | tf_op jit(solution)/shard_map/ppermute | solution.py:48
  72.7 4.0 %collective-permute-start.12 = (f32[4,1,1,1,1,1,16,128]{7,6,0,5,4,3,2,1:T(8,128)S(1)}, f32[4,1,1,1,1,1,16,128]{7,6,0,5,4,3,2,1:T(8,128)S(1)}, u32[]{:S(2)}, u32[]{:S(2)}) collective-permute-start(f32[4,1,1,1,1,1,16,128]{7,6,0,5,4,3,2,1:T(8,128)S(1)} %constant_dynamic-slice_fusion.2), channel_id=1, source_target_pairs={{0,2},{1,3},{2,0},{3,1},{4,6},{5,7},{6,4},{7,5},{8,10},{9,11},{10,... | collective-permute-start | bytes 98312 | tf_op jit(solution)/shard_map/ppermute | solution.py:48
  74.1 4.0 %collective-permute-start.16 = (f32[4,1,1,1,1,1,16,128]{7,6,0,5,4,3,2,1:T(8,128)S(1)}, f32[4,1,1,1,1,1,16,128]{7,6,0,5,4,3,2,1:T(8,128)S(1)}, u32[]{:S(2)}, u32[]{:S(2)}) collective-permute-start(f32[4,1,1,1,1,1,16,128]{7,6,0,5,4,3,2,1:T(8,128)S(1)} %constant_dynamic-slice_fusion), channel_id=1, source_target_pairs={{0,4},{4,0},{8,12},{12,8},{16,20},{20,16},{24,28},{28,24},{1,5},{5... | collective-permute-start | bytes 98312 | tf_op jit(solution)/shard_map/ppermute | solution.py:48
  81.9 4.8 %collective-permute-start.17 = (bf16[4,1,1,1,1,1,16,128]{7,6,0,5,4,3,2,1:T(8,128)(2,1)S(1)}, bf16[4,1,1,1,1,1,16,128]{7,6,0,5,4,3,2,1:T(8,128)(2,1)S(1)}, u32[]{:S(2)}, u32[]{:S(2)}) collective-permute-start(bf16[4,1,1,1,1,1,16,128]{7,6,0,5,4,3,2,1:T(8,128)(2,1)S(1)} %get-tuple-element.32), channel_id=1, source_target_pairs={{0,16},{4,20},{8,24},{12,28},{16,0},{20,4},{24,8},{28,12},{1,17},{... | collective-permute-start | bytes 49160 | tf_op jit(solution)/shard_map/ppermute | solution.py:53
  83.8 4.3 %collective-permute-start.22 = (bf16[4,1,1,1,1,1,16,128]{7,6,0,5,4,3,2,1:T(8,128)(2,1)S(1)}, bf16[4,1,1,1,1,1,16,128]{7,6,0,5,4,3,2,1:T(8,128)(2,1)S(1)}, u32[]{:S(2)}, u32[]{:S(2)}) collective-permute-start(bf16[4,1,1,1,1,1,16,128]{7,6,0,5,4,3,2,1:T(8,128)(2,1)S(1)} %get-tuple-element.33), channel_id=1, source_target_pairs={{0,2},{1,3},{2,0},{3,1},{4,6},{5,7},{6,4},{7,5},{8,10},{9,11},{10,... | collective-permute-start | bytes 49160 | tf_op jit(solution)/shard_map/ppermute | solution.py:53
  85.3 4.7 %collective-permute-start.27 = (bf16[4,1,1,1,1,1,16,128]{7,6,0,5,4,3,2,1:T(8,128)(2,1)S(1)}, bf16[4,1,1,1,1,1,16,128]{7,6,0,5,4,3,2,1:T(8,128)(2,1)S(1)}, u32[]{:S(2)}, u32[]{:S(2)}) collective-permute-start(bf16[4,1,1,1,1,1,16,128]{7,6,0,5,4,3,2,1:T(8,128)(2,1)S(1)} %get-tuple-element.34), channel_id=1, source_target_pairs={{0,4},{4,0},{8,12},{12,8},{16,20},{20,16},{24,28},{28,24},{1,5},{5... | collective-permute-start | bytes 49160 | tf_op jit(solution)/shard_map/ppermute | solution.py:53
  86.8 5.2 %collective-permute-start.18 = (bf16[4,1,1,1,1,2,16,128]{7,6,0,5,4,3,2,1:T(8,128)(2,1)S(1)}, bf16[4,1,1,1,1,2,16,128]{7,6,0,5,4,3,2,1:T(8,128)(2,1)S(1)}, u32[]{:S(2)}, u32[]{:S(2)}) collective-permute-start(bf16[4,1,1,1,1,2,16,128]{7,6,0,5,4,3,2,1:T(8,128)(2,1)S(1)} %maximum_select_fusion.18), channel_id=1, source_target_pairs={{0,8},{4,12},{8,0},{12,4},{16,24},{20,28},{24,16},{28,20},{1,9},{5... | collective-permute-start | bytes 98312 | tf_op jit(solution)/shard_map/ppermute | solution.py:53
  88.1 5.6 %collective-permute-start.23 = (bf16[4,1,2,1,1,1,16,128]{7,6,0,2,5,4,3,1:T(8,128)(2,1)S(1)}, bf16[4,1,2,1,1,1,16,128]{7,6,0,2,5,4,3,1:T(8,128)(2,1)S(1)}, u32[]{:S(2)}, u32[]{:S(2)}) collective-permute-start(bf16[4,1,2,1,1,1,16,128]{7,6,0,2,5,4,3,1:T(8,128)(2,1)S(1)} %fusion.27), channel_id=1, source_target_pairs={{0,16},{4,20},{8,24},{12,28},{16,0},{20,4},{24,8},{28,12},{1,17},{... | collective-permute-start | bytes 98312 | tf_op jit(solution)/shard_map/ppermute | solution.py:53
  90.0 4.3 %collective-permute-start.28 = (bf16[4,1,1,2,1,1,16,128]{7,6,0,5,4,3,2,1:T(8,128)(2,1)S(1)}, bf16[4,1,1,2,1,1,16,128]{7,6,0,5,4,3,2,1:T(8,128)(2,1)S(1)}, u32[]{:S(2)}, u32[]{:S(2)}) collective-permute-start(bf16[4,1,1,2,1,1,16,128]{7,6,0,5,4,3,2,1:T(8,128)(2,1)S(1)} %maximum_select_fusion.22), channel_id=1, source_target_pairs={{0,2},{1,3},{2,0},{3,1},{4,6},{5,7},{6,4},{7,5},{8,10},{9,11},{10,... | collective-permute-start | bytes 98312 | tf_op jit(solution)/shard_map/ppermute | solution.py:53
  92.0 4.9 %collective-permute-start.19 = (bf16[4,1,1,1,2,2,16,128]{7,6,0,5,4,3,2,1:T(8,128)(2,1)S(1)}, bf16[4,1,1,1,2,2,16,128]{7,6,0,5,4,3,2,1:T(8,128)(2,1)S(1)}, u32[]{:S(2)}, u32[]{:S(2)}) collective-permute-start(bf16[4,1,1,1,2,2,16,128]{7,6,0,5,4,3,2,1:T(8,128)(2,1)S(1)} %maximum_select_fusion.13), channel_id=1, source_target_pairs={{0,4},{4,0},{8,12},{12,8},{16,20},{20,16},{24,28},{28,24},{1,5},{5... | collective-permute-start | bytes 196616 | tf_op jit(solution)/shard_map/ppermute | solution.py:53
  93.7 5.0 %collective-permute-start.24 = (bf16[4,1,2,1,1,2,16,128]{7,6,0,5,4,3,2,1:T(8,128)(2,1)S(1)}, bf16[4,1,2,1,1,2,16,128]{7,6,0,5,4,3,2,1:T(8,128)(2,1)S(1)}, u32[]{:S(2)}, u32[]{:S(2)}) collective-permute-start(bf16[4,1,2,1,1,2,16,128]{7,6,0,5,4,3,2,1:T(8,128)(2,1)S(1)} %copy.88), channel_id=1, source_target_pairs={{0,8},{4,12},{8,0},{12,4},{16,24},{20,28},{24,16},{28,20},{1,9},{5... | collective-permute-start | bytes 196616 | tf_op jit(solution)/shard_map/ppermute | solution.py:53
  94.4 6.0 %collective-permute-start.29 = (bf16[4,1,2,2,1,1,16,128]{7,6,0,5,4,3,2,1:T(8,128)(2,1)S(1)}, bf16[4,1,2,2,1,1,16,128]{7,6,0,5,4,3,2,1:T(8,128)(2,1)S(1)}, u32[]{:S(2)}, u32[]{:S(2)}) collective-permute-start(bf16[4,1,2,2,1,1,16,128]{7,6,0,5,4,3,2,1:T(8,128)(2,1)S(1)} %fusion.26), channel_id=1, source_target_pairs={{0,16},{4,20},{8,24},{12,28},{16,0},{20,4},{24,8},{28,12},{1,17},{... | collective-permute-start | bytes 196616 | tf_op jit(solution)/shard_map/ppermute | solution.py:53
  96.9 5.0 %collective-permute-start.20 = (bf16[4,1,1,2,2,2,16,128]{7,6,0,5,4,3,2,1:T(8,128)(2,1)S(1)}, bf16[4,1,1,2,2,2,16,128]{7,6,0,5,4,3,2,1:T(8,128)(2,1)S(1)}, u32[]{:S(2)}, u32[]{:S(2)}) collective-permute-start(bf16[4,1,1,2,2,2,16,128]{7,6,0,5,4,3,2,1:T(8,128)(2,1)S(1)} %maximum_select_fusion.7), channel_id=1, source_target_pairs={{0,2},{1,3},{2,0},{3,1},{4,6},{5,7},{6,4},{7,5},{8,10},{9,11},{10,... | collective-permute-start | bytes 393224 | tf_op jit(solution)/shard_map/ppermute | solution.py:53
  98.8 5.0 %collective-permute-start.25 = (bf16[4,1,2,1,2,2,16,128]{7,6,0,5,4,3,2,1:T(8,128)(2,1)S(1)}, bf16[4,1,2,1,2,2,16,128]{7,6,0,5,4,3,2,1:T(8,128)(2,1)S(1)}, u32[]{:S(2)}, u32[]{:S(2)}) collective-permute-start(bf16[4,1,2,1,2,2,16,128]{7,6,0,5,4,3,2,1:T(8,128)(2,1)S(1)} %maximum_select_fusion.9), channel_id=1, source_target_pairs={{0,4},{4,0},{8,12},{12,8},{16,20},{20,16},{24,28},{28,24},{1,5},{5... | collective-permute-start | bytes 393224 | tf_op jit(solution)/shard_map/ppermute | solution.py:53
  100.4 5.0 %collective-permute-start.30 = (bf16[4,1,2,2,1,2,16,128]{7,6,0,5,4,3,2,1:T(8,128)(2,1)S(1)}, bf16[4,1,2,2,1,2,16,128]{7,6,0,5,4,3,2,1:T(8,128)(2,1)S(1)}, u32[]{:S(2)}, u32[]{:S(2)}) collective-permute-start(bf16[4,1,2,2,1,2,16,128]{7,6,0,5,4,3,2,1:T(8,128)(2,1)S(1)} %maximum_select_fusion.11), channel_id=1, source_target_pairs={{0,8},{4,12},{8,0},{12,4},{16,24},{20,28},{24,16},{28,20},{1,9},{5... | collective-permute-start | bytes 393224 | tf_op jit(solution)/shard_map/ppermute | solution.py:53
  102.0 3.7 %collective-permute-start.21 = (bf16[4,1,2,2,2,2,16,128]{7,6,0,5,4,3,2,1:T(8,128)(2,1)S(1)}, bf16[4,1,2,2,2,2,16,128]{7,6,0,5,4,3,2,1:T(8,128)(2,1)S(1)}, u32[]{:S(2)}, u32[]{:S(2)}) collective-permute-start(bf16[4,1,2,2,2,2,16,128]{7,6,0,5,4,3,2,1:T(8,128)(2,1)S(1)} %maximum_select_fusion.3), channel_id=1, source_target_pairs={{0,1},{1,0},{2,3},{3,2},{4,5},{5,4},{6,7},{7,6},{8,9},{9,8},{10,11... | collective-permute-start | bytes 786440 | tf_op jit(solution)/shard_map/ppermute | solution.py:53
  103.9 2.0 %collective-permute-start.26 = (bf16[4,1,2,2,2,2,16,128]{7,6,0,5,4,3,2,1:T(8,128)(2,1)S(1)}, bf16[4,1,2,2,2,2,16,128]{7,6,0,5,4,3,2,1:T(8,128)(2,1)S(1)}, u32[]{:S(2)}, u32[]{:S(2)}) collective-permute-start(bf16[4,1,2,2,2,2,16,128]{7,6,0,5,4,3,2,1:T(8,128)(2,1)S(1)} %maximum_select_fusion.4), channel_id=1, source_target_pairs={{0,1},{1,0},{2,3},{3,2},{4,5},{5,4},{6,7},{7,6},{8,9},{9,8},{10,11... | collective-permute-start | bytes 786440 | tf_op jit(solution)/shard_map/ppermute | solution.py:53
  (12 other events, 79.2 us)
Sparse Core Ops, SparseCore 0:
  31.0 24.7 all-gather.1

commit v8 on v7

--- a/solution.py
+++ b/solution.py
@@ -86,13 +86,14 @@
     per = total_blocks // streams
     orders = stream_orders(nb, streams)
     split = restricted.reshape((total_blocks,) + (2,) * nb + (inner, width))
-    parts = [lax.slice_in_dim(split, s * per, (s + 1) * per, axis=0) for s in range(streams)]
+    whole = halve(split, 1, *bits[0], jnp.float32)
+    extended, inverse_blocks, whole = lax.optimization_barrier((extended, inverse_blocks, whole))
+    parts = [lax.slice_in_dim(whole, s * per, (s + 1) * per, axis=0) for s in range(streams)]
     picked = jnp.take(extended, margin, axis=0)
     local = jnp.einsum("jerb,jebc->jrc", picked, inverse_blocks, preferred_element_type=jnp.float32)
-    for step in range(nb):
-        wire = jnp.bfloat16 if step in (1, 2) else jnp.float32
-        parts = [halve(x, 1 + orders[s][step], *bits[orders[s][step]], wire) for s, x in enumerate(parts)]
-        if step == 0:
+    for step in range(1, nb):
+        parts = [halve(x, 1 + orders[s][step], *bits[orders[s][step]], jnp.float32) for s, x in enumerate(parts)]
+        if step == 1:
             local, parts = lax.optimization_barrier((local, parts))
     mine = jnp.concatenate(parts, axis=0).reshape(total_blocks, inner, width)
     coarse_in = mine.astype(jnp.bfloat16)
@@ -102,9 +103,10 @@
     ).astype(jnp.bfloat16)
     solved = solved.reshape((total_blocks,) + (1,) * nb + (inner, width))
     outs = [lax.slice_in_dim(solved, s * per, (s + 1) * per, axis=0) for s in range(streams)]
-    for step in reversed(range(nb)):
+    for step in reversed(range(1, nb)):
         outs = [double(y, 1 + orders[s][step], *bits[orders[s][step]]) for s, y in enumerate(outs)]
-    coarse_out = jnp.concatenate(outs, axis=0).reshape(total_blocks, rhs, width)
+    coarse_out = double(jnp.concatenate(outs, axis=0), 1, *bits[0])
+    coarse_out = coarse_out.reshape(total_blocks, rhs, width)
 
     lifted = jnp.take(coarse_out, interface, axis=0)
     spread = jnp.einsum("jqrc,jqbc->jrb", lifted, basis, preferred_element_type=jnp.float32)

time: 122 us -> 124 us (1.016)
  waiting for transfers between devices: 14.9 us -> 26.9 us
  starting transfers between devices: 44.9 us -> 34.6 us
  other arithmetic: 11 us -> 12.5 us
    ppermute x15 -> x13, waiting for transfers between devices: 2.78 us -> 9.04 us  [halve(): lax.ppermute(send.astype(wire), axis, pairs(axis, mask)).astype(x.dtype)]
    ppermute x15 -> x13, waiting for transfers between devices: 8.79 us -> 14.7 us  [double(): recv = lax.ppermute(y, axis, pairs(axis, mask))]
    ppermute x15 -> x13, starting transfers between devices: 26.3 us -> 20.7 us  [halve(): lax.ppermute(send.astype(wire), axis, pairs(axis, mask)).astype(x.dtype)]
    ppermute x15 -> x13, starting transfers between devices: 15.4 us -> 10.5 us  [double(): recv = lax.ppermute(y, axis, pairs(axis, mask))]
    slice x1, local copies, waits for them, and re-layouts: 1.8 us -> 0.17 us  [per_device(): lax.slice_in_dim(whole, s * per, (s + 1) * per, axis=0)]
    dynamic_slice x2 -> x1, local copies, waits for them, and re-layouts: 3.38 us -> 1.76 us  [halve(): keep = lax.dynamic_index_in_dim(x, v, axis=dim, keepdims=True)]
    add x12 -> x10, other arithmetic: 3.55 us -> 5.08 us  [halve(): keep + lax.ppermute(send.astype(wire), axis, pairs(axis, mask)).astype(x....]
    dynamic_slice x6 -> x12, local copies, waits for them, and re-layouts: 0.08 us -> 1.6 us  [halve(): send = lax.dynamic_index_in_dim(x, 1 - v, axis=dim, keepdims=True)]
  transfers between devices with their start and end apart: 33 -> 29, of which waited for: 13 -> 14; matrix products, arithmetic and copies ran while one was open for 17% -> 17% of each run, Pallas kernels for 0% -> 0%
where the time goes in v8:
time: 124 us
  starting transfers between devices  34.6 us (28%)
  waiting for transfers between devices  26.9 us (22%)
  local copies, waits for them, and re-layouts  20.2 us (16%)
  matrix products  15.7 us (13%)
  between operations  14 us (11%)
  other arithmetic  12.5 us (10%)
    ppermute x13, starting transfers between devices, halve(): lax.ppermute(send.astype(wire), axis, pairs(axis, mask)).astype(x.dtype)  20.7 us
    ppermute x13, waiting for transfers between devices, double(): recv = lax.ppermute(y, axis, pairs(axis, mask))  14.7 us
    ppermute x13, starting transfers between devices, double(): recv = lax.ppermute(y, axis, pairs(axis, mask))  10.5 us
    ppermute x13, waiting for transfers between devices, halve(): lax.ppermute(send.astype(wire), axis, pairs(axis, mask)).astype(x.dtype)  9.04 us
    add x10, other arithmetic, halve(): keep + lax.ppermute(send.astype(wire), axis, pairs(axis, mask)).astype(x....  5.08 us
    dot_general x1, matrix products, per_device(): jnp.einsum('jerb,jebc->jrc', picked, inverse_blocks, preferred_element_ty...  4.9 us
    gather x1, local copies, waits for them, and re-layouts, per_device(): picked = jnp.take(extended, margin, axis=0)  4.17 us
    dot_general x1, matrix products, per_device(): jnp.einsum('jqn,jqrc->nrc', onehot, terms, precision=lax.Precision.HIGHEST)  3.96 us
  transfers between devices with their start and end apart: 29, of which 14 were waited for; matrix products, arithmetic and copies ran while one was open for 17% of the time, Pallas kernels for 0%

profile of v8, /device:TPU:0, one launch (start us, length us, event | category | flops | bytes accessed | tf_op | source)
XLA Modules:
  0.0 123.8 jit_solution(15496058466997224847)
XLA Ops:
  6.5 3.4 %convolution_bitcast_fusion = f32[4,2,512,128]{2,3,1,0:T(8,128)} fusion(bf16[4,2,256,128]{3,2,1,0:T(8,128)(2,1)} %param.11, bf16[4,512,256]{2,1,0:T(8,128)(2,1)} %param.7), kind=kOutput, calls=%fused_computation.10 | convolution fusion | flops 268435456 | bytes 3670016 | tf_op jit(solution)/shard_map/jrb,jqbc->jqrc/dot_general | solution.py:76
  9.9 2.9 %copy.63 = f32[4,2,512,128]{3,0,1,2:T(4,128)} copy(f32[4,2,512,128]{2,3,1,0:T(8,128)} %convolution_bitcast_fusion) | data formatting | bytes 4194304 | tf_op jit(solution)/shard_map/jrb,jqbc->jqrc/transpose | solution.py:76
  12.8 4.0 %fusion.37 = f32[12,512,128,1]{2,0,3,1:T(8,128)S(1)} fusion(f32[4,2,512,128]{3,0,1,2:T(4,128)} %copy.63, s32[4,2]{0,1:T(2,128)S(1)} %copy-done.8), kind=kOutput, calls=%fused_computation.104 | convolution fusion | flops 75497568 | bytes 5242912 | tf_op jit(solution)/shard_map/jqn,jqrc->nrc/dot_general | solution.py:79
  16.8 1.8 %constant_dynamic-slice_fusion.13 = (f32[12,1,2,2,2,2,16,128]{7,0,6,5,4,3,2,1:T(8,128)}, f32[12,1,2,2,2,2,16,128]{7,0,6,5,4,3,2,1:T(8,128)S(1)}) fusion(f32[12,2,2,2,2,2,16,128]{7,0,6,5,4,3,2,1:T(8,128)S(1)} %bitcast.114, s32[]{:T(128)S(6)} %select_n.640, s32[]{:T(128)S(6)} %select_n.641), kind=kLoop, calls=%fused_computation.91 | loop fusion | bytes 6291464 | tf_op jit(solution)/shard_map/jit(dynamic_index_in_dim)/dynamic_slice | solution.py:46
  18.6 1.7 %copy.88 = f32[12,1,2,2,2,2,16,128]{7,6,0,5,4,3,2,1:T(8,128)} copy(f32[12,1,2,2,2,2,16,128]{7,0,6,5,4,3,2,1:T(8,128)S(1)} %get-tuple-element.20) | data formatting | bytes 3145728
  21.5 2.0 %collective-permute-start = (bf16[1,512,256]{2,1,0:T(8,128)(2,1)}, bf16[1,512,256]{2,1,0:T(8,128)(2,1)S(1)}, u32[]{:S(2)}, u32[]{:S(2)}) collective-permute-start(bf16[1,512,256]{2,1,0:T(8,128)(2,1)} %get-tuple-element.24), channel_id=1, source_target_pairs={{0,1},{1,2},{2,3},{3,4},{4,5},{5,6},{6,7},{7,8},{8,9},{9,10},{10,1... | collective-permute-start | bytes 786440 | tf_op jit(solution)/shard_map/ppermute | solution.py:15
  23.5 1.5 %collective-permute-start.1 = (bf16[1,512,256]{2,1,0:T(8,128)(2,1)}, bf16[1,512,256]{2,1,0:T(8,128)(2,1)}, u32[]{:S(2)}, u32[]{:S(2)}) collective-permute-start(bf16[1,512,256]{2,1,0:T(8,128)(2,1)} %get-tuple-element.25), channel_id=1, source_target_pairs={{1,0},{2,1},{3,2},{4,3},{5,4},{6,5},{7,6},{8,7},{9,8},{10,9},{11,1... | collective-permute-start | bytes 786440 | tf_op jit(solution)/shard_map/ppermute | solution.py:17
  26.2 3.1 %collective-permute-done.1 = bf16[1,512,256]{2,1,0:T(8,128)(2,1)} collective-permute-done((bf16[1,512,256]{2,1,0:T(8,128)(2,1)}, bf16[1,512,256]{2,1,0:T(8,128)(2,1)}, u32[]{:S(2)}, u32[]{:S(2)}) %collective-permute-start.1) | collective-permute-done | bytes 262176 | tf_op jit(solution)/shard_map/ppermute | solution.py:17
  29.3 2.3 %pad_maximum_fusion = bf16[6,512,256]{2,1,0:T(8,128)(2,1)} fusion(bf16[1,512,256]{2,1,0:T(8,128)(2,1)} %collective-permute-done.1, bf16[4,512,256]{2,1,0:T(8,128)(2,1)S(1)} %copy-done.2, bf16[1,512,256]{2,1,0:T(8,128)(2,1)S(1)} %collective-permute-done), kind=kLoop, calls=%fused_computation.13 | loop fusion | flops 1572864 | bytes 3145728 | tf_op jit(solution)/shard_map/concatenate | solution.py:13
  31.7 2.0 %copy_add_fusion = f32[12,1,2,2,2,2,16,128]{7,6,0,5,4,3,2,1:T(8,128)S(1)} fusion(f32[12,1,2,2,2,2,16,128]{7,6,0,5,4,3,2,1:T(8,128)} %collective-permute-done.2, f32[12,1,2,2,2,2,16,128]{7,0,6,5,4,3,2,1:T(8,128)S(1)} %copy-done.1), kind=kLoop, calls=%fused_computation.15 | loop fusion | flops 393216 | bytes 4718592 | tf_op jit(solution)/shard_map/add | solution.py:48
  35.4 6.4 %collective-permute-start.5 = (f32[4,1,2,2,1,2,16,128]{7,6,0,5,4,3,2,1:T(8,128)}, f32[4,1,2,2,1,2,16,128]{7,6,0,5,4,3,2,1:T(8,128)}, u32[]{:S(2)}, u32[]{:S(2)}) collective-permute-start(f32[4,1,2,2,1,2,16,128]{7,6,0,5,4,3,2,1:T(8,128)} %constant_dynamic-slice_fusion.9), channel_id=1, source_target_pairs={{0,8},{4,12},{8,0},{12,4},{16,24},{20,28},{24,16},{28,20},{1,9},{5... | collective-permute-start | bytes 786440 | tf_op jit(solution)/shard_map/ppermute | solution.py:48
  43.8 4.2 %gather_fusion = bf16[16,512,256]{2,1,0:T(8,128)(2,1)} fusion(bf16[6,512,256]{2,1,0:T(8,128)(2,1)} %pad_maximum_fusion, s32[1024]{0:T(1024)S(1)} %pad_clamp_fusion.2), kind=kCustom, calls=%fused_computation | custom fusion | bytes 8388672 | tf_op jit(solution)/shard_map/jit(_take)/gather | solution.py:92
  48.0 4.9 %fusion.5 = f32[4,512,256]{2,1,0:T(8,128)} fusion(bf16[4,4,256,256]{3,2,1,0:T(8,128)(2,1)S(1)} %copy-done, bf16[4,4,512,256]{3,2,1,0:T(8,128)(2,1)} %bitcast.116, pred[4,4]{1,0:T(4,128)(4,1)S(1)} %compare_and_fusion.2), kind=kOutput, calls=%fused_computation.9 | convolution fusion | flops 1075838976 | bytes 8388624 | tf_op jit(solution)/shard_map/jerb,jebc->jrc/dot_general | solution.py:93
  55.9 1.7 %collective-permute-start.6 = (f32[4,1,1,1,2,2,16,128]{7,6,0,5,4,3,2,1:T(8,128)S(1)}, f32[4,1,1,1,2,2,16,128]{7,6,0,5,4,3,2,1:T(8,128)S(1)}, u32[]{:S(2)}, u32[]{:S(2)}) collective-permute-start(f32[4,1,1,1,2,2,16,128]{7,6,0,5,4,3,2,1:T(8,128)S(1)} %constant_dynamic-slice_fusion.8), channel_id=1, source_target_pairs={{0,4},{4,0},{8,12},{12,8},{16,20},{20,16},{24,28},{28,24},{1,5},{5... | collective-permute-start | bytes 393224 | tf_op jit(solution)/shard_map/ppermute | solution.py:48
  59.1 2.6 %collective-permute-start.12 = (f32[4,1,2,2,1,1,16,128]{7,6,0,5,4,3,2,1:T(8,128)S(1)}, f32[4,1,2,2,1,1,16,128]{7,6,0,5,4,3,2,1:T(8,128)S(1)}, u32[]{:S(2)}, u32[]{:S(2)}) collective-permute-start(f32[4,1,2,2,1,1,16,128]{7,6,0,5,4,3,2,1:T(8,128)S(1)} %constant_dynamic-slice_fusion.2), channel_id=1, source_target_pairs={{0,16},{4,20},{8,24},{12,28},{16,0},{20,4},{24,8},{28,12},{1,17},{... | collective-permute-start | bytes 393224 | tf_op jit(solution)/shard_map/ppermute | solution.py:48
  62.7 3.9 %collective-permute-done.9 = f32[4,1,2,1,1,2,16,128]{7,6,0,5,4,3,2,1:T(8,128)S(1)} collective-permute-done((f32[4,1,2,1,1,2,16,128]{7,6,0,5,4,3,2,1:T(8,128)S(1)}, f32[4,1,2,1,1,2,16,128]{7,6,0,5,4,3,2,1:T(8,128)S(1)}, u32[]{:S(2)}, u32[]{:S(2)}) %collective-permute-start.9) | collective-permute-done | bytes 131104 | tf_op jit(solution)/shard_map/ppermute | solution.py:48
  66.8 1.6 %collective-permute-start.13 = (f32[4,1,1,2,1,1,16,128]{7,6,0,5,4,3,2,1:T(8,128)S(1)}, f32[4,1,1,2,1,1,16,128]{7,6,0,5,4,3,2,1:T(8,128)S(1)}, u32[]{:S(2)}, u32[]{:S(2)}) collective-permute-start(f32[4,1,1,2,1,1,16,128]{7,6,0,5,4,3,2,1:T(8,128)S(1)} %constant_dynamic-slice_fusion.1), channel_id=1, source_target_pairs={{0,2},{1,3},{2,0},{3,1},{4,6},{5,7},{6,4},{7,5},{8,10},{9,11},{10,... | collective-permute-start | bytes 196616 | tf_op jit(solution)/shard_map/ppermute | solution.py:48
  68.4 3.0 %collective-permute-start.8 = (f32[4,1,1,1,1,1,16,128]{7,6,0,5,4,3,2,1:T(8,128)S(1)}, f32[4,1,1,1,1,1,16,128]{7,6,0,5,4,3,2,1:T(8,128)S(1)}, u32[]{:S(2)}, u32[]{:S(2)}) collective-permute-start(f32[4,1,1,1,1,1,16,128]{7,6,0,5,4,3,2,1:T(8,128)S(1)} %constant_dynamic-slice_fusion.6), channel_id=1, source_target_pairs={{0,16},{4,20},{8,24},{12,28},{16,0},{20,4},{24,8},{28,12},{1,17},{... | collective-permute-start | bytes 98312 | tf_op jit(solution)/shard_map/ppermute | solution.py:48
  71.3 1.7 %collective-permute-done.10 = f32[4,1,2,1,1,1,16,128]{7,6,0,5,4,3,2,1:T(8,128)S(1)} collective-permute-done((f32[4,1,2,1,1,1,16,128]{7,6,0,5,4,3,2,1:T(8,128)S(1)}, f32[4,1,2,1,1,1,16,128]{7,6,0,5,4,3,2,1:T(8,128)S(1)}, u32[]{:S(2)}, u32[]{:S(2)}) %collective-permute-start.10) | collective-permute-done | bytes 65568 | tf_op jit(solution)/shard_map/ppermute | solution.py:48
  74.4 2.7 %collective-permute-done.11 = f32[4,1,1,1,1,1,16,128]{7,6,0,5,4,3,2,1:T(8,128)S(1)} collective-permute-done((f32[4,1,1,1,1,1,16,128]{7,6,0,5,4,3,2,1:T(8,128)S(1)}, f32[4,1,1,1,1,1,16,128]{7,6,0,5,4,3,2,1:T(8,128)S(1)}, u32[]{:S(2)}, u32[]{:S(2)}) %collective-permute-start.11) | collective-permute-done | bytes 32800 | tf_op jit(solution)/shard_map/ppermute | solution.py:48
  79.9 1.8 %fusion.13 = bf16[12,16,128]{2,1,0:T(8,128)(2,1)S(1)} fusion(bf16[12,4,136,128]{3,2,1,0:T(8,128)(2,1)} %all-gather.2.cloned.1.call-done, bf16[12,4,16,128]{3,2,1,0:T(8,128)(2,1)S(1)} %bitcast.124, pred[12,4]{1,0:T(8,128)(4,1)S(1)} %copy.68), kind=kOutput, calls=%fused_computation.17 | convolution fusion | flops 25288704 | bytes 1818672 | tf_op jit(solution)/shard_map/nerc,necd->nrd/dot_general | solution.py:101
  83.4 3.1 %collective-permute-done.15 = bf16[4,1,1,1,1,1,16,128]{7,6,0,5,4,3,2,1:T(8,128)(2,1)S(1)} collective-permute-done((bf16[4,1,1,1,1,1,16,128]{7,6,0,5,4,3,2,1:T(8,128)(2,1)S(1)}, bf16[4,1,1,1,1,1,16,128]{7,6,0,5,4,3,2,1:T(8,128)(2,1)S(1)}, u32[]{:S(2)}, u32[]{:S(2)}) %collective-permute-start.15) | collective-permute-done | bytes 16416 | tf_op jit(solution)/shard_map/ppermute | solution.py:53
  86.7 2.3 %collective-permute-start.20 = (bf16[4,1,2,1,1,1,16,128]{7,6,0,2,5,4,3,1:T(8,128)(2,1)S(1)}, bf16[4,1,2,1,1,1,16,128]{7,6,0,2,5,4,3,1:T(8,128)(2,1)S(1)}, u32[]{:S(2)}, u32[]{:S(2)}) collective-permute-start(bf16[4,1,2,1,1,1,16,128]{7,6,0,2,5,4,3,1:T(8,128)(2,1)S(1)} %fusion.27), channel_id=1, source_target_pairs={{0,16},{4,20},{8,24},{12,28},{16,0},{20,4},{24,8},{28,12},{1,17},{... | collective-permute-start | bytes 98312 | tf_op jit(solution)/shard_map/ppermute | solution.py:53
  89.0 1.6 %collective-permute-start.24 = (bf16[4,1,1,2,1,1,16,128]{7,6,0,5,4,3,2,1:T(8,128)(2,1)S(1)}, bf16[4,1,1,2,1,1,16,128]{7,6,0,5,4,3,2,1:T(8,128)(2,1)S(1)}, u32[]{:S(2)}, u32[]{:S(2)}) collective-permute-start(bf16[4,1,1,2,1,1,16,128]{7,6,0,5,4,3,2,1:T(8,128)(2,1)S(1)} %maximum_select_fusion.20), channel_id=1, source_target_pairs={{0,2},{1,3},{2,0},{3,1},{4,6},{5,7},{6,4},{7,5},{8,10},{9,11},{10,... | collective-permute-start | bytes 98312 | tf_op jit(solution)/shard_map/ppermute | solution.py:53
  91.6 2.4 %collective-permute-start.21 = (bf16[4,1,2,1,1,2,16,128]{7,6,0,5,4,3,2,1:T(8,128)(2,1)S(1)}, bf16[4,1,2,1,1,2,16,128]{7,6,0,5,4,3,2,1:T(8,128)(2,1)S(1)}, u32[]{:S(2)}, u32[]{:S(2)}) collective-permute-start(bf16[4,1,2,1,1,2,16,128]{7,6,0,5,4,3,2,1:T(8,128)(2,1)S(1)} %copy.71), channel_id=1, source_target_pairs={{0,8},{4,12},{8,0},{12,4},{16,24},{20,28},{24,16},{28,20},{1,9},{5... | collective-permute-start | bytes 196616 | tf_op jit(solution)/shard_map/ppermute | solution.py:53
  97.4 2.5 %collective-permute-done.25 = bf16[4,1,2,2,1,1,16,128]{7,6,0,5,4,3,2,1:T(8,128)(2,1)S(1)} collective-permute-done((bf16[4,1,2,2,1,1,16,128]{7,6,0,5,4,3,2,1:T(8,128)(2,1)S(1)}, bf16[4,1,2,2,1,1,16,128]{7,6,0,5,4,3,2,1:T(8,128)(2,1)S(1)}, u32[]{:S(2)}, u32[]{:S(2)}) %collective-permute-start.25) | collective-permute-done | bytes 65568 | tf_op jit(solution)/shard_map/ppermute | solution.py:53
  102.0 2.9 %collective-permute-done.26 = bf16[4,1,2,2,1,2,16,128]{7,6,0,5,4,3,2,1:T(8,128)(2,1)S(1)} collective-permute-done((bf16[4,1,2,2,1,2,16,128]{7,6,0,5,4,3,2,1:T(8,128)(2,1)S(1)}, bf16[4,1,2,2,1,2,16,128]{7,6,0,5,4,3,2,1:T(8,128)(2,1)S(1)}, u32[]{:S(2)}, u32[]{:S(2)}) %collective-permute-start.26) | collective-permute-done | bytes 131104 | tf_op jit(solution)/shard_map/ppermute | solution.py:53
  106.3 2.3 %collective-permute-done.27 = bf16[12,1,2,2,2,2,16,128]{7,6,0,5,4,3,2,1:T(8,128)(2,1)} collective-permute-done((bf16[12,1,2,2,2,2,16,128]{7,6,0,5,4,3,2,1:T(8,128)(2,1)}, bf16[12,1,2,2,2,2,16,128]{7,6,0,5,4,3,2,1:T(8,128)(2,1)}, u32[]{:S(2)}, u32[]{:S(2)}) %collective-permute-start.27) | collective-permute-done | bytes 786464 | tf_op jit(solution)/shard_map/ppermute | solution.py:53
  108.6 1.6 %maximum_select_fusion = bf16[12,2,2,2,2,2,16,128]{7,6,0,5,4,3,2,1:T(8,128)(2,1)S(1)} fusion(bf16[12,1,2,2,2,2,16,128]{7,6,0,5,4,3,2,1:T(8,128)(2,1)} %collective-permute-done.27, bf16[4,1,2,2,2,2,16,128]{7,6,0,5,4,3,2,1:T(8,128)(2,1)S(1)} %maximum_select_fusion.3, bf16[4,1,2,2,2,2,16,128]{7,6,0,5,4,3,2,1:T(8,128)(2,1)S(1)} %maximum_select_fusion.2, ...), kind=kLoop, calls=%fused_computation.14 | loop fusion | flops 5505024 | bytes 3145729 | tf_op jit(solution)/shard_map/jit(_where)/select_n | solution.py:54
  110.2 1.6 %copy.79 = bf16[12,2,2,2,2,2,16,128]{7,6,5,4,3,2,1,0:T(8,128)(2,1)} copy(bf16[12,2,2,2,2,2,16,128]{7,6,0,5,4,3,2,1:T(8,128)(2,1)S(1)} %maximum_select_fusion) | data formatting | bytes 3145728 | tf_op jit(solution)/shard_map/jit(_where)/select_n | solution.py:54
  111.8 2.2 %gather_fusion.2 = bf16[8,512,128]{2,1,0:T(8,128)(2,1)S(1)} fusion(bf16[12,512,128]{2,1,0:T(8,128)(2,1)} %bitcast.115, s32[1024]{0:T(1024)S(1)} %pad_clamp_fusion), kind=kCustom, calls=%fused_computation.2 | custom fusion | bytes 2097184 | tf_op jit(solution)/shard_map/jit(_take)/gather | solution.py:111
  114.0 1.7 %fusion.17 = f32[4,512,256,1]{2,1,3,0:T(8,128)S(1)} fusion(bf16[4,2,256,128]{3,2,1,0:T(8,128)(2,1)} %param.11, bf16[4,2,512,128]{3,2,1,0:T(8,128)(2,1)S(1)} %bitcast.117, pred[4,2]{1,0:T(4,128)(4,1)S(1)} %copy.66), kind=kOutput, calls=%fused_computation.19 | convolution fusion | flops 268959744 | bytes 3670024 | tf_op jit(solution)/shard_map/jqrc,jqbc->jrb/dot_general | solution.py:112
  (135 shorter events, 26.7 us)
Async XLA Ops:
  6.5 41.4 %copy-start = (bf16[4,4,256,256]{3,2,1,0:T(8,128)(2,1)S(1)}, bf16[4,4,256,256]{3,2,1,0:T(8,128)(2,1)}, u32[]{:S(2)}) copy-start(bf16[4,4,256,256]{3,2,1,0:T(8,128)(2,1)} %param.9) | copy-start | bytes 6291460
  6.5 71.4 %all-gather.2.cloned.1.call-start = ((), (), s32[]{:S(2)}) async-start(), calls=%async_computation | async-start | bytes 2088960 | tf_op jit(solution)/shard_map/all_gather | solution.py:69
  18.6 6.4 %copy-start.9 = (s32[3,4]{1,0:T(4,128)S(1)}, s32[3,4]{1,0:T(4,128)}, u32[]{:S(2)}) copy-start(s32[3,4]{1,0:T(4,128)} %param.12) | copy-start | bytes 148
  18.6 6.5 %copy-start.6 = (bf16[3,4,128,128]{3,2,1,0:T(8,128)(2,1)S(1)}, bf16[3,4,128,128]{3,2,1,0:T(8,128)(2,1)}, u32[]{:S(2)}) copy-start(bf16[3,4,128,128]{3,2,1,0:T(8,128)(2,1)} %param.13) | copy-start | bytes 1179652
  20.3 11.4 %collective-permute-start.2 = (f32[12,1,2,2,2,2,16,128]{7,6,0,5,4,3,2,1:T(8,128)}, f32[12,1,2,2,2,2,16,128]{7,6,0,5,4,3,2,1:T(8,128)}, u32[]{:S(2)}, u32[]{:S(2)}) collective-permute-start(f32[12,1,2,2,2,2,16,128]{7,6,0,5,4,3,2,1:T(8,128)} %copy.88), channel_id=1, source_target_pairs={{0,1},{1,0},{2,3},{3,2},{4,5},{5,4},{6,7},{7,6},{8,9},{9,8},{10,11... | collective-permute-start | bytes 4718600 | tf_op jit(solution)/shard_map/ppermute | solution.py:48
  21.5 4.7 %collective-permute-start = (bf16[1,512,256]{2,1,0:T(8,128)(2,1)}, bf16[1,512,256]{2,1,0:T(8,128)(2,1)S(1)}, u32[]{:S(2)}, u32[]{:S(2)}) collective-permute-start(bf16[1,512,256]{2,1,0:T(8,128)(2,1)} %get-tuple-element.24), channel_id=1, source_target_pairs={{0,1},{1,2},{2,3},{3,4},{4,5},{5,6},{6,7},{7,8},{8,9},{9,10},{10,1... | collective-permute-start | bytes 786440 | tf_op jit(solution)/shard_map/ppermute | solution.py:15
  23.5 5.8 %collective-permute-start.1 = (bf16[1,512,256]{2,1,0:T(8,128)(2,1)}, bf16[1,512,256]{2,1,0:T(8,128)(2,1)}, u32[]{:S(2)}, u32[]{:S(2)}) collective-permute-start(bf16[1,512,256]{2,1,0:T(8,128)(2,1)} %get-tuple-element.25), channel_id=1, source_target_pairs={{1,0},{2,1},{3,2},{4,3},{5,4},{6,5},{7,6},{8,7},{9,8},{10,9},{11,1... | collective-permute-start | bytes 786440 | tf_op jit(solution)/shard_map/ppermute | solution.py:17
  35.4 17.4 %collective-permute-start.5 = (f32[4,1,2,2,1,2,16,128]{7,6,0,5,4,3,2,1:T(8,128)}, f32[4,1,2,2,1,2,16,128]{7,6,0,5,4,3,2,1:T(8,128)}, u32[]{:S(2)}, u32[]{:S(2)}) collective-permute-start(f32[4,1,2,2,1,2,16,128]{7,6,0,5,4,3,2,1:T(8,128)} %constant_dynamic-slice_fusion.9), channel_id=1, source_target_pairs={{0,8},{4,12},{8,0},{12,4},{16,24},{20,28},{24,16},{28,20},{1,9},{5... | collective-permute-start | bytes 786440 | tf_op jit(solution)/shard_map/ppermute | solution.py:48
  42.6 11.3 %collective-permute-start.4 = (f32[4,1,2,1,2,2,16,128]{7,6,0,5,4,3,2,1:T(8,128)}, f32[4,1,2,1,2,2,16,128]{7,6,0,5,4,3,2,1:T(8,128)}, u32[]{:S(2)}, u32[]{:S(2)}) collective-permute-start(f32[4,1,2,1,2,2,16,128]{7,6,0,5,4,3,2,1:T(8,128)} %constant_dynamic-slice_fusion.10), channel_id=1, source_target_pairs={{0,4},{4,0},{8,12},{12,8},{16,20},{20,16},{24,28},{28,24},{1,5},{5... | collective-permute-start | bytes 786440 | tf_op jit(solution)/shard_map/ppermute | solution.py:48
  43.1 11.7 %collective-permute-start.3 = (f32[4,1,1,2,2,2,16,128]{7,6,0,5,4,3,2,1:T(8,128)S(1)}, f32[4,1,1,2,2,2,16,128]{7,6,0,5,4,3,2,1:T(8,128)}, u32[]{:S(2)}, u32[]{:S(2)}) collective-permute-start(f32[4,1,1,2,2,2,16,128]{7,6,0,5,4,3,2,1:T(8,128)S(1)} %constant_dynamic-slice_fusion.11), channel_id=1, source_target_pairs={{0,2},{1,3},{2,0},{3,1},{4,6},{5,7},{6,4},{7,5},{8,10},{9,11},{10,... | collective-permute-start | bytes 786440 | tf_op jit(solution)/shard_map/ppermute | solution.py:48
  55.9 5.8 %collective-permute-start.6 = (f32[4,1,1,1,2,2,16,128]{7,6,0,5,4,3,2,1:T(8,128)S(1)}, f32[4,1,1,1,2,2,16,128]{7,6,0,5,4,3,2,1:T(8,128)S(1)}, u32[]{:S(2)}, u32[]{:S(2)}) collective-permute-start(f32[4,1,1,1,2,2,16,128]{7,6,0,5,4,3,2,1:T(8,128)S(1)} %constant_dynamic-slice_fusion.8), channel_id=1, source_target_pairs={{0,4},{4,0},{8,12},{12,8},{16,20},{20,16},{24,28},{28,24},{1,5},{5... | collective-permute-start | bytes 393224 | tf_op jit(solution)/shard_map/ppermute | solution.py:48
  57.6 9.0 %collective-permute-start.9 = (f32[4,1,2,1,1,2,16,128]{7,6,0,5,4,3,2,1:T(8,128)S(1)}, f32[4,1,2,1,1,2,16,128]{7,6,0,5,4,3,2,1:T(8,128)S(1)}, u32[]{:S(2)}, u32[]{:S(2)}) collective-permute-start(f32[4,1,2,1,1,2,16,128]{7,6,0,5,4,3,2,1:T(8,128)S(1)} %constant_dynamic-slice_fusion.5), channel_id=1, source_target_pairs={{0,8},{4,12},{8,0},{12,4},{16,24},{20,28},{24,16},{28,20},{1,9},{5... | collective-permute-start | bytes 393224 | tf_op jit(solution)/shard_map/ppermute | solution.py:48
  59.1 7.7 %collective-permute-start.12 = (f32[4,1,2,2,1,1,16,128]{7,6,0,5,4,3,2,1:T(8,128)S(1)}, f32[4,1,2,2,1,1,16,128]{7,6,0,5,4,3,2,1:T(8,128)S(1)}, u32[]{:S(2)}, u32[]{:S(2)}) collective-permute-start(f32[4,1,2,2,1,1,16,128]{7,6,0,5,4,3,2,1:T(8,128)S(1)} %constant_dynamic-slice_fusion.2), channel_id=1, source_target_pairs={{0,16},{4,20},{8,24},{12,28},{16,0},{20,4},{24,8},{28,12},{1,17},{... | collective-permute-start | bytes 393224 | tf_op jit(solution)/shard_map/ppermute | solution.py:48
  61.7 6.6 %collective-permute-start.7 = (f32[4,1,1,1,1,2,16,128]{7,6,0,5,4,3,2,1:T(8,128)S(1)}, f32[4,1,1,1,1,2,16,128]{7,6,0,5,4,3,2,1:T(8,128)S(1)}, u32[]{:S(2)}, u32[]{:S(2)}) collective-permute-start(f32[4,1,1,1,1,2,16,128]{7,6,0,5,4,3,2,1:T(8,128)S(1)} %constant_dynamic-slice_fusion.7), channel_id=1, source_target_pairs={{0,8},{4,12},{8,0},{12,4},{16,24},{20,28},{24,16},{28,20},{1,9},{5... | collective-permute-start | bytes 196616 | tf_op jit(solution)/shard_map/ppermute | solution.py:48
  66.6 6.4 %collective-permute-start.10 = (f32[4,1,2,1,1,1,16,128]{7,6,0,5,4,3,2,1:T(8,128)S(1)}, f32[4,1,2,1,1,1,16,128]{7,6,0,5,4,3,2,1:T(8,128)S(1)}, u32[]{:S(2)}, u32[]{:S(2)}) collective-permute-start(f32[4,1,2,1,1,1,16,128]{7,6,0,5,4,3,2,1:T(8,128)S(1)} %constant_dynamic-slice_fusion.4), channel_id=1, source_target_pairs={{0,16},{4,20},{8,24},{12,28},{16,0},{20,4},{24,8},{28,12},{1,17},{... | collective-permute-start | bytes 196616 | tf_op jit(solution)/shard_map/ppermute | solution.py:48
  66.8 7.0 %collective-permute-start.13 = (f32[4,1,1,2,1,1,16,128]{7,6,0,5,4,3,2,1:T(8,128)S(1)}, f32[4,1,1,2,1,1,16,128]{7,6,0,5,4,3,2,1:T(8,128)S(1)}, u32[]{:S(2)}, u32[]{:S(2)}) collective-permute-start(f32[4,1,1,2,1,1,16,128]{7,6,0,5,4,3,2,1:T(8,128)S(1)} %constant_dynamic-slice_fusion.1), channel_id=1, source_target_pairs={{0,2},{1,3},{2,0},{3,1},{4,6},{5,7},{6,4},{7,5},{8,10},{9,11},{10,... | collective-permute-start | bytes 196616 | tf_op jit(solution)/shard_map/ppermute | solution.py:48
  68.4 6.0 %collective-permute-start.8 = (f32[4,1,1,1,1,1,16,128]{7,6,0,5,4,3,2,1:T(8,128)S(1)}, f32[4,1,1,1,1,1,16,128]{7,6,0,5,4,3,2,1:T(8,128)S(1)}, u32[]{:S(2)}, u32[]{:S(2)}) collective-permute-start(f32[4,1,1,1,1,1,16,128]{7,6,0,5,4,3,2,1:T(8,128)S(1)} %constant_dynamic-slice_fusion.6), channel_id=1, source_target_pairs={{0,16},{4,20},{8,24},{12,28},{16,0},{20,4},{24,8},{28,12},{1,17},{... | collective-permute-start | bytes 98312 | tf_op jit(solution)/shard_map/ppermute | solution.py:48
  73.0 4.0 %collective-permute-start.11 = (f32[4,1,1,1,1,1,16,128]{7,6,0,5,4,3,2,1:T(8,128)S(1)}, f32[4,1,1,1,1,1,16,128]{7,6,0,5,4,3,2,1:T(8,128)S(1)}, u32[]{:S(2)}, u32[]{:S(2)}) collective-permute-start(f32[4,1,1,1,1,1,16,128]{7,6,0,5,4,3,2,1:T(8,128)S(1)} %constant_dynamic-slice_fusion.3), channel_id=1, source_target_pairs={{0,2},{1,3},{2,0},{3,1},{4,6},{5,7},{6,4},{7,5},{8,10},{9,11},{10,... | collective-permute-start | bytes 98312 | tf_op jit(solution)/shard_map/ppermute | solution.py:48
  73.9 4.0 %collective-permute-start.14 = (f32[4,1,1,1,1,1,16,128]{7,6,0,5,4,3,2,1:T(8,128)S(1)}, f32[4,1,1,1,1,1,16,128]{7,6,0,5,4,3,2,1:T(8,128)S(1)}, u32[]{:S(2)}, u32[]{:S(2)}) collective-permute-start(f32[4,1,1,1,1,1,16,128]{7,6,0,5,4,3,2,1:T(8,128)S(1)} %constant_dynamic-slice_fusion), channel_id=1, source_target_pairs={{0,4},{4,0},{8,12},{12,8},{16,20},{20,16},{24,28},{28,24},{1,5},{5... | collective-permute-start | bytes 98312 | tf_op jit(solution)/shard_map/ppermute | solution.py:48
  81.7 4.8 %collective-permute-start.15 = (bf16[4,1,1,1,1,1,16,128]{7,6,0,5,4,3,2,1:T(8,128)(2,1)S(1)}, bf16[4,1,1,1,1,1,16,128]{7,6,0,5,4,3,2,1:T(8,128)(2,1)S(1)}, u32[]{:S(2)}, u32[]{:S(2)}) collective-permute-start(bf16[4,1,1,1,1,1,16,128]{7,6,0,5,4,3,2,1:T(8,128)(2,1)S(1)} %get-tuple-element.34), channel_id=1, source_target_pairs={{0,16},{4,20},{8,24},{12,28},{16,0},{20,4},{24,8},{28,12},{1,17},{... | collective-permute-start | bytes 49160 | tf_op jit(solution)/shard_map/ppermute | solution.py:53
  82.0 4.6 %collective-permute-start.19 = (bf16[4,1,1,1,1,1,16,128]{7,6,0,5,4,3,2,1:T(8,128)(2,1)S(1)}, bf16[4,1,1,1,1,1,16,128]{7,6,0,5,4,3,2,1:T(8,128)(2,1)S(1)}, u32[]{:S(2)}, u32[]{:S(2)}) collective-permute-start(bf16[4,1,1,1,1,1,16,128]{7,6,0,5,4,3,2,1:T(8,128)(2,1)S(1)} %get-tuple-element.35), channel_id=1, source_target_pairs={{0,2},{1,3},{2,0},{3,1},{4,6},{5,7},{6,4},{7,5},{8,10},{9,11},{10,... | collective-permute-start | bytes 49160 | tf_op jit(solution)/shard_map/ppermute | solution.py:53
  83.4 5.5 %collective-permute-start.23 = (bf16[4,1,1,1,1,1,16,128]{7,6,0,5,4,3,2,1:T(8,128)(2,1)S(1)}, bf16[4,1,1,1,1,1,16,128]{7,6,0,5,4,3,2,1:T(8,128)(2,1)S(1)}, u32[]{:S(2)}, u32[]{:S(2)}) collective-permute-start(bf16[4,1,1,1,1,1,16,128]{7,6,0,5,4,3,2,1:T(8,128)(2,1)S(1)} %get-tuple-element.36), channel_id=1, source_target_pairs={{0,4},{4,0},{8,12},{12,8},{16,20},{20,16},{24,28},{28,24},{1,5},{5... | collective-permute-start | bytes 49160 | tf_op jit(solution)/shard_map/ppermute | solution.py:53
  86.5 4.3 %collective-permute-start.16 = (bf16[4,1,1,1,1,2,16,128]{7,6,0,5,4,3,2,1:T(8,128)(2,1)S(1)}, bf16[4,1,1,1,1,2,16,128]{7,6,0,5,4,3,2,1:T(8,128)(2,1)S(1)}, u32[]{:S(2)}, u32[]{:S(2)}) collective-permute-start(bf16[4,1,1,1,1,2,16,128]{7,6,0,5,4,3,2,1:T(8,128)(2,1)S(1)} %maximum_select_fusion.16), channel_id=1, source_target_pairs={{0,8},{4,12},{8,0},{12,4},{16,24},{20,28},{24,16},{28,20},{1,9},{5... | collective-permute-start | bytes 98312 | tf_op jit(solution)/shard_map/ppermute | solution.py:53
  86.7 4.9 %collective-permute-start.20 = (bf16[4,1,2,1,1,1,16,128]{7,6,0,2,5,4,3,1:T(8,128)(2,1)S(1)}, bf16[4,1,2,1,1,1,16,128]{7,6,0,2,5,4,3,1:T(8,128)(2,1)S(1)}, u32[]{:S(2)}, u32[]{:S(2)}) collective-permute-start(bf16[4,1,2,1,1,1,16,128]{7,6,0,2,5,4,3,1:T(8,128)(2,1)S(1)} %fusion.27), channel_id=1, source_target_pairs={{0,16},{4,20},{8,24},{12,28},{16,0},{20,4},{24,8},{28,12},{1,17},{... | collective-permute-start | bytes 98312 | tf_op jit(solution)/shard_map/ppermute | solution.py:53
  89.0 4.9 %collective-permute-start.24 = (bf16[4,1,1,2,1,1,16,128]{7,6,0,5,4,3,2,1:T(8,128)(2,1)S(1)}, bf16[4,1,1,2,1,1,16,128]{7,6,0,5,4,3,2,1:T(8,128)(2,1)S(1)}, u32[]{:S(2)}, u32[]{:S(2)}) collective-permute-start(bf16[4,1,1,2,1,1,16,128]{7,6,0,5,4,3,2,1:T(8,128)(2,1)S(1)} %maximum_select_fusion.20), channel_id=1, source_target_pairs={{0,2},{1,3},{2,0},{3,1},{4,6},{5,7},{6,4},{7,5},{8,10},{9,11},{10,... | collective-permute-start | bytes 98312 | tf_op jit(solution)/shard_map/ppermute | solution.py:53
  90.8 5.0 %collective-permute-start.17 = (bf16[4,1,1,1,2,2,16,128]{7,6,0,5,4,3,2,1:T(8,128)(2,1)S(1)}, bf16[4,1,1,1,2,2,16,128]{7,6,0,5,4,3,2,1:T(8,128)(2,1)S(1)}, u32[]{:S(2)}, u32[]{:S(2)}) collective-permute-start(bf16[4,1,1,1,2,2,16,128]{7,6,0,5,4,3,2,1:T(8,128)(2,1)S(1)} %maximum_select_fusion.11), channel_id=1, source_target_pairs={{0,4},{4,0},{8,12},{12,8},{16,20},{20,16},{24,28},{28,24},{1,5},{5... | collective-permute-start | bytes 196616 | tf_op jit(solution)/shard_map/ppermute | solution.py:53
  91.6 5.4 %collective-permute-start.21 = (bf16[4,1,2,1,1,2,16,128]{7,6,0,5,4,3,2,1:T(8,128)(2,1)S(1)}, bf16[4,1,2,1,1,2,16,128]{7,6,0,5,4,3,2,1:T(8,128)(2,1)S(1)}, u32[]{:S(2)}, u32[]{:S(2)}) collective-permute-start(bf16[4,1,2,1,1,2,16,128]{7,6,0,5,4,3,2,1:T(8,128)(2,1)S(1)} %copy.71), channel_id=1, source_target_pairs={{0,8},{4,12},{8,0},{12,4},{16,24},{20,28},{24,16},{28,20},{1,9},{5... | collective-permute-start | bytes 196616 | tf_op jit(solution)/shard_map/ppermute | solution.py:53
  93.9 5.9 %collective-permute-start.25 = (bf16[4,1,2,2,1,1,16,128]{7,6,0,5,4,3,2,1:T(8,128)(2,1)S(1)}, bf16[4,1,2,2,1,1,16,128]{7,6,0,5,4,3,2,1:T(8,128)(2,1)S(1)}, u32[]{:S(2)}, u32[]{:S(2)}) collective-permute-start(bf16[4,1,2,2,1,1,16,128]{7,6,0,5,4,3,2,1:T(8,128)(2,1)S(1)} %fusion.26), channel_id=1, source_target_pairs={{0,16},{4,20},{8,24},{12,28},{16,0},{20,4},{24,8},{28,12},{1,17},{... | collective-permute-start | bytes 196616 | tf_op jit(solution)/shard_map/ppermute | solution.py:53
  95.8 5.0 %collective-permute-start.18 = (bf16[4,1,1,2,2,2,16,128]{7,6,0,5,4,3,2,1:T(8,128)(2,1)S(1)}, bf16[4,1,1,2,2,2,16,128]{7,6,0,5,4,3,2,1:T(8,128)(2,1)S(1)}, u32[]{:S(2)}, u32[]{:S(2)}) collective-permute-start(bf16[4,1,1,2,2,2,16,128]{7,6,0,5,4,3,2,1:T(8,128)(2,1)S(1)} %maximum_select_fusion.5), channel_id=1, source_target_pairs={{0,2},{1,3},{2,0},{3,1},{4,6},{5,7},{6,4},{7,5},{8,10},{9,11},{10,... | collective-permute-start | bytes 393224 | tf_op jit(solution)/shard_map/ppermute | solution.py:53
  97.0 5.0 %collective-permute-start.22 = (bf16[4,1,2,1,2,2,16,128]{7,6,0,5,4,3,2,1:T(8,128)(2,1)S(1)}, bf16[4,1,2,1,2,2,16,128]{7,6,0,5,4,3,2,1:T(8,128)(2,1)S(1)}, u32[]{:S(2)}, u32[]{:S(2)}) collective-permute-start(bf16[4,1,2,1,2,2,16,128]{7,6,0,5,4,3,2,1:T(8,128)(2,1)S(1)} %maximum_select_fusion.7), channel_id=1, source_target_pairs={{0,4},{4,0},{8,12},{12,8},{16,20},{20,16},{24,28},{28,24},{1,5},{5... | collective-permute-start | bytes 393224 | tf_op jit(solution)/shard_map/ppermute | solution.py:53
  99.9 5.0 %collective-permute-start.26 = (bf16[4,1,2,2,1,2,16,128]{7,6,0,5,4,3,2,1:T(8,128)(2,1)S(1)}, bf16[4,1,2,2,1,2,16,128]{7,6,0,5,4,3,2,1:T(8,128)(2,1)S(1)}, u32[]{:S(2)}, u32[]{:S(2)}) collective-permute-start(bf16[4,1,2,2,1,2,16,128]{7,6,0,5,4,3,2,1:T(8,128)(2,1)S(1)} %maximum_select_fusion.9), channel_id=1, source_target_pairs={{0,8},{4,12},{8,0},{12,4},{16,24},{20,28},{24,16},{28,20},{1,9},{5... | collective-permute-start | bytes 393224 | tf_op jit(solution)/shard_map/ppermute | solution.py:53
  105.9 2.6 %collective-permute-start.27 = (bf16[12,1,2,2,2,2,16,128]{7,6,0,5,4,3,2,1:T(8,128)(2,1)}, bf16[12,1,2,2,2,2,16,128]{7,6,0,5,4,3,2,1:T(8,128)(2,1)}, u32[]{:S(2)}, u32[]{:S(2)}) collective-permute-start(bf16[12,1,2,2,2,2,16,128]{7,6,0,5,4,3,2,1:T(8,128)(2,1)} %pad_maximum_fusion.1), channel_id=1, source_target_pairs={{0,1},{1,0},{2,3},{3,2},{4,5},{5,4},{6,7},{7,6},{8,9},{9,8},{10,11... | collective-permute-start | bytes 2359304 | tf_op jit(solution)/shard_map/ppermute | solution.py:53
  (7 other events, 23.7 us)
Sparse Core Ops, SparseCore 0:
  26.1 27.1 all-gather.1

commit v9 on v8

--- a/solution.py
+++ b/solution.py
@@ -1,7 +1,45 @@
 import jax
 import jax.numpy as jnp
 from jax import lax
+from jax.experimental import pallas as pl
+from jax.experimental.pallas import tpu as pltpu
 from jax.sharding import PartitionSpec as P
+
+
+def restrict_kernel(links, residual_ref, basis_ref, out_ref):
+    j = pl.program_id(0)
+    q = pl.program_id(1)
+
+    @pl.when((j == 0) & (q == 0))
+    def _():
+        out_ref[...] = jnp.zeros_like(out_ref)
+
+    n = links[j, q]
+    out_ref[n] += jnp.dot(residual_ref[0], basis_ref[0, 0], preferred_element_type=jnp.float32)
+
+
+def restrict(residual, basis, interface, total_blocks):
+    count, rhs, size = residual.shape
+    width = basis.shape[-1]
+    return pl.pallas_call(
+        restrict_kernel,
+        out_shape=jax.ShapeDtypeStruct((total_blocks, rhs, width), jnp.float32),
+        grid_spec=pltpu.PrefetchScalarGridSpec(
+            num_scalar_prefetch=1,
+            grid=(count, interface.shape[1]),
+            in_specs=[
+                pl.BlockSpec((1, rhs, size), lambda j, q, links: (j, 0, 0)),
+                pl.BlockSpec((1, 1, size, width), lambda j, q, links: (j, q, 0, 0)),
+            ],
+            out_specs=pl.BlockSpec((total_blocks, rhs, width), lambda j, q, links: (0, 0, 0)),
+        ),
+        compiler_params=pltpu.CompilerParams(dimension_semantics=("arbitrary", "arbitrary")),
+        cost_estimate=pl.CostEstimate(
+            flops=2 * count * interface.shape[1] * rhs * size * width,
+            bytes_accessed=residual.size * 2 + basis.size * 2 + total_blocks * rhs * width * 4,
+            transcendentals=0,
+        ),
+    )(interface, residual, basis)
 
 
 def with_halo(cells, sides, width):
@@ -73,10 +111,7 @@
     rhs = residual.shape[1]
     width = basis.shape[-1]
     total_blocks = pattern_all.shape[0]
-    terms = jnp.einsum("jrb,jqbc->jqrc", residual, basis, preferred_element_type=jnp.float32)
-    labels = jnp.arange(total_blocks, dtype=jnp.int32)
-    onehot = (interface[:, :, None] == labels[None, None, :]).astype(jnp.float32)
-    restricted = jnp.einsum("jqn,jqrc->nrc", onehot, terms, precision=lax.Precision.HIGHEST)
+    restricted = restrict(residual, basis, interface, total_blocks)
 
     bits = device_bits()
     nb = len(bits)

time: 124 us -> 123 us (level)
  Pallas kernels: 0 us -> 7.62 us
  matrix products: 15.7 us -> 8.34 us
  starting transfers between devices: 34.6 us -> 38.1 us
  waiting for transfers between devices: 26.9 us -> 24.2 us
  local copies, waits for them, and re-layouts: 20.2 us -> 18.3 us
    pallas_call x0 -> x1, Pallas kernels: none -> 7.62 us  [restrict(): pl.pallas_call(restrict_kernel, out_shape=jax.ShapeDtypeStruct((total_blo...]
    dot_general x2 -> x0, matrix products: 7.33 us -> none  [the longest x1 3.96 us: per_device(): jnp.einsum('jqn,jqrc->nrc', onehot, terms, precision=lax.Precision.HIGHEST)]
    ppermute x13, starting transfers between devices: 10.5 us -> 13.9 us  [double(): recv = lax.ppermute(y, axis, pairs(axis, mask))]
    ppermute x13, waiting for transfers between devices: 14.7 us -> 11.7 us  [double(): recv = lax.ppermute(y, axis, pairs(axis, mask))]
    transpose x1 -> x0, local copies, waits for them, and re-layouts: 2.91 us -> none  [per_device(): jnp.einsum('jrb,jqbc->jqrc', residual, basis, preferred_element_type=jnp....]
    dynamic_slice x12 -> x13, local copies, waits for them, and re-layouts: 1.6 us -> 4.5 us  [halve(): send = lax.dynamic_index_in_dim(x, 1 - v, axis=dim, keepdims=True)]
    dynamic_slice x1 -> x0, local copies, waits for them, and re-layouts: 1.76 us -> none  [halve(): keep = lax.dynamic_index_in_dim(x, v, axis=dim, keepdims=True)]
  transfers between devices with their start and end apart: 29 -> 29, of which waited for: 14 -> 12; matrix products, arithmetic and copies ran while one was open for 17% -> 17% of each run, Pallas kernels for 0% -> 0%
where the time goes in v9:
time: 123 us
  starting transfers between devices  38.1 us (31%)
  waiting for transfers between devices  24.2 us (20%)
  local copies, waits for them, and re-layouts  18.3 us (15%)
  between operations  14 us (11%)
  other arithmetic  12.1 us (10%)
  matrix products  8.34 us (7%)
  Pallas kernels  7.62 us (6%)
    ppermute x13, starting transfers between devices, halve(): lax.ppermute(send.astype(wire), axis, pairs(axis, mask)).astype(x.dtype)  20.8 us
    ppermute x13, starting transfers between devices, double(): recv = lax.ppermute(y, axis, pairs(axis, mask))  13.9 us
    ppermute x13, waiting for transfers between devices, double(): recv = lax.ppermute(y, axis, pairs(axis, mask))  11.7 us
    ppermute x13, waiting for transfers between devices, halve(): lax.ppermute(send.astype(wire), axis, pairs(axis, mask)).astype(x.dtype)  9.13 us
    pallas_call x1, Pallas kernels, restrict(): pl.pallas_call(restrict_kernel, out_shape=jax.ShapeDtypeStruct((total_blo...  7.62 us
    dot_general x1, matrix products, per_device(): jnp.einsum('jerb,jebc->jrc', picked, inverse_blocks, preferred_element_ty...  4.89 us
    add x10, other arithmetic, halve(): keep + lax.ppermute(send.astype(wire), axis, pairs(axis, mask)).astype(x....  4.81 us
    dynamic_slice x13, local copies, waits for them, and re-layouts, halve(): send = lax.dynamic_index_in_dim(x, 1 - v, axis=dim, keepdims=True)  4.5 us
  transfers between devices with their start and end apart: 29, of which 12 were waited for; matrix products, arithmetic and copies ran while one was open for 17% of the time, Pallas kernels for 0%

profile of v9, /device:TPU:0, one launch (start us, length us, event | category | flops | bytes accessed | tf_op | source)
XLA Modules:
  0.0 122.7 jit_solution(1013387852715472828)
XLA Ops:
  6.5 1.5 %copy.58.links = s32[4,2]{1,0:T(4,128)} copy(s32[4,2]{0,1:T(2,128)} %param.10) | data formatting | bytes 64 | tf_op args[3]
  8.0 7.6 %shard_map.73 = f32[12,512,128]{2,1,0:T(8,128)} custom-call(s32[4,2]{1,0:T(4,128)} %copy.58.links, bf16[4,512,256]{2,1,0:T(8,128)(2,1)} %residual_ref.1, bf16[4,2,256,128]{3,2,1,0:T(8,128)(2,1)} %basis_ref.1), custom_call_target="tpu_custom_call" | custom-call | flops 268435456 | bytes 4718592 | tf_op jit(solution)/shard_map/pallas_call | solution.py:24
  15.7 2.9 %constant_dynamic-slice_fusion.12 = f32[12,1,2,2,2,2,16,128]{7,6,5,4,3,2,1,0:T(8,128)} fusion(f32[12,2,2,2,2,2,16,128]{7,6,5,4,3,2,1,0:T(8,128)} %bitcast.99, s32[]{:T(128)S(6)} %select_n.641), kind=kLoop, calls=%fused_computation.88 | loop fusion | bytes 3145732 | tf_op jit(solution)/shard_map/jit(dynamic_index_in_dim)/dynamic_slice | solution.py:85
  19.8 2.0 %collective-permute-start = (bf16[1,512,256]{2,1,0:T(8,128)(2,1)}, bf16[1,512,256]{2,1,0:T(8,128)(2,1)S(1)}, u32[]{:S(2)}, u32[]{:S(2)}) collective-permute-start(bf16[1,512,256]{2,1,0:T(8,128)(2,1)} %get-tuple-element.22), channel_id=1, source_target_pairs={{0,1},{1,2},{2,3},{3,4},{4,5},{5,6},{6,7},{7,8},{8,9},{9,10},{10,1... | collective-permute-start | bytes 786440 | tf_op jit(solution)/shard_map/ppermute | solution.py:53
  24.3 3.3 %collective-permute-done.1 = bf16[1,512,256]{2,1,0:T(8,128)(2,1)} collective-permute-done((bf16[1,512,256]{2,1,0:T(8,128)(2,1)}, bf16[1,512,256]{2,1,0:T(8,128)(2,1)}, u32[]{:S(2)}, u32[]{:S(2)}) %collective-permute-start.1) | collective-permute-done | bytes 262176 | tf_op jit(solution)/shard_map/ppermute | solution.py:55
  27.7 2.3 %pad_maximum_fusion = bf16[6,512,256]{2,1,0:T(8,128)(2,1)} fusion(bf16[1,512,256]{2,1,0:T(8,128)(2,1)} %collective-permute-done.1, bf16[4,512,256]{2,1,0:T(8,128)(2,1)S(1)} %copy-done.2, bf16[1,512,256]{2,1,0:T(8,128)(2,1)S(1)} %collective-permute-done), kind=kLoop, calls=%fused_computation.12 | loop fusion | flops 1572864 | bytes 3145728 | tf_op jit(solution)/shard_map/concatenate | solution.py:51
  30.0 1.8 %dynamic-slice_add_fusion = f32[12,1,2,2,2,2,16,128]{7,6,5,4,3,2,1,0:T(8,128)S(1)} fusion(f32[12,1,2,2,2,2,16,128]{7,6,5,4,3,2,1,0:T(8,128)} %collective-permute-done.2, f32[12,2,2,2,2,2,16,128]{7,6,5,4,3,2,1,0:T(8,128)S(1)} %bitcast.100, s32[]{:T(128)S(6)} %select_n.640), kind=kLoop, calls=%fused_computation.14 | loop fusion | flops 393216 | bytes 4718596 | tf_op jit(solution)/shard_map/add | solution.py:86
  33.4 6.4 %collective-permute-start.5 = (f32[4,1,2,2,1,2,16,128]{7,6,5,4,3,2,1,0:T(8,128)}, f32[4,1,2,2,1,2,16,128]{7,6,5,4,3,2,1,0:T(8,128)}, u32[]{:S(2)}, u32[]{:S(2)}) collective-permute-start(f32[4,1,2,2,1,2,16,128]{7,6,5,4,3,2,1,0:T(8,128)} %constant_dynamic-slice_fusion.9), channel_id=1, source_target_pairs={{0,8},{4,12},{8,0},{12,4},{16,24},{20,28},{24,16},{28,20},{1,9},{5... | collective-permute-start | bytes 786440 | tf_op jit(solution)/shard_map/ppermute | solution.py:86
  41.7 4.2 %gather_fusion = bf16[16,512,256]{2,1,0:T(8,128)(2,1)} fusion(bf16[6,512,256]{2,1,0:T(8,128)(2,1)} %pad_maximum_fusion, s32[1024]{0:T(1024)S(1)} %pad_clamp_fusion.2), kind=kCustom, calls=%fused_computation | custom fusion | bytes 8388672 | tf_op jit(solution)/shard_map/jit(_take)/gather | solution.py:127
  46.0 4.9 %fusion.5 = f32[4,512,256]{2,1,0:T(8,128)} fusion(bf16[4,4,256,256]{3,2,1,0:T(8,128)(2,1)S(1)} %copy-done, bf16[4,4,512,256]{3,2,1,0:T(8,128)(2,1)} %bitcast.102, pred[4,4]{1,0:T(4,128)(4,1)S(1)} %compare_and_fusion.2), kind=kOutput, calls=%fused_computation.9 | convolution fusion | flops 1075838976 | bytes 8388624 | tf_op jit(solution)/shard_map/jerb,jebc->jrc/dot_general | solution.py:128
  53.9 1.8 %collective-permute-start.6 = (f32[4,1,1,1,2,2,16,128]{7,6,5,4,3,2,1,0:T(8,128)S(1)}, f32[4,1,1,1,2,2,16,128]{7,6,5,4,3,2,1,0:T(8,128)S(1)}, u32[]{:S(2)}, u32[]{:S(2)}) collective-permute-start(f32[4,1,1,1,2,2,16,128]{7,6,5,4,3,2,1,0:T(8,128)S(1)} %constant_dynamic-slice_fusion.8), channel_id=1, source_target_pairs={{0,4},{4,0},{8,12},{12,8},{16,20},{20,16},{24,28},{28,24},{1,5},{5... | collective-permute-start | bytes 393224 | tf_op jit(solution)/shard_map/ppermute | solution.py:86
  55.7 1.5 %collective-permute-start.9 = (f32[4,1,2,1,1,2,16,128]{7,6,5,4,3,2,1,0:T(8,128)S(1)}, f32[4,1,2,1,1,2,16,128]{7,6,5,4,3,2,1,0:T(8,128)S(1)}, u32[]{:S(2)}, u32[]{:S(2)}) collective-permute-start(f32[4,1,2,1,1,2,16,128]{7,6,5,4,3,2,1,0:T(8,128)S(1)} %constant_dynamic-slice_fusion.5), channel_id=1, source_target_pairs={{0,8},{4,12},{8,0},{12,4},{16,24},{20,28},{24,16},{28,20},{1,9},{5... | collective-permute-start | bytes 393224 | tf_op jit(solution)/shard_map/ppermute | solution.py:86
  57.2 2.6 %collective-permute-start.12 = (f32[4,1,2,2,1,1,16,128]{7,6,5,4,3,2,1,0:T(8,128)S(1)}, f32[4,1,2,2,1,1,16,128]{7,6,5,4,3,2,1,0:T(8,128)S(1)}, u32[]{:S(2)}, u32[]{:S(2)}) collective-permute-start(f32[4,1,2,2,1,1,16,128]{7,6,5,4,3,2,1,0:T(8,128)S(1)} %constant_dynamic-slice_fusion.2), channel_id=1, source_target_pairs={{0,16},{4,20},{8,24},{12,28},{16,0},{20,4},{24,8},{28,12},{1,17},{... | collective-permute-start | bytes 393224 | tf_op jit(solution)/shard_map/ppermute | solution.py:86
  61.0 3.8 %collective-permute-done.9 = f32[4,1,2,1,1,2,16,128]{7,6,5,4,3,2,1,0:T(8,128)S(1)} collective-permute-done((f32[4,1,2,1,1,2,16,128]{7,6,5,4,3,2,1,0:T(8,128)S(1)}, f32[4,1,2,1,1,2,16,128]{7,6,5,4,3,2,1,0:T(8,128)S(1)}, u32[]{:S(2)}, u32[]{:S(2)}) %collective-permute-start.9) | collective-permute-done | bytes 131104 | tf_op jit(solution)/shard_map/ppermute | solution.py:86
  66.4 3.0 %collective-permute-start.8 = (f32[4,1,1,1,1,1,16,128]{7,6,5,4,3,2,1,0:T(8,128)S(1)}, f32[4,1,1,1,1,1,16,128]{7,6,5,4,3,2,1,0:T(8,128)S(1)}, u32[]{:S(2)}, u32[]{:S(2)}) collective-permute-start(f32[4,1,1,1,1,1,16,128]{7,6,5,4,3,2,1,0:T(8,128)S(1)} %constant_dynamic-slice_fusion.6), channel_id=1, source_target_pairs={{0,16},{4,20},{8,24},{12,28},{16,0},{20,4},{24,8},{28,12},{1,17},{... | collective-permute-start | bytes 98312 | tf_op jit(solution)/shard_map/ppermute | solution.py:86
  69.3 1.5 %collective-permute-done.10 = f32[4,1,2,1,1,1,16,128]{7,6,5,4,3,2,1,0:T(8,128)S(1)} collective-permute-done((f32[4,1,2,1,1,1,16,128]{7,6,5,4,3,2,1,0:T(8,128)S(1)}, f32[4,1,2,1,1,1,16,128]{7,6,5,4,3,2,1,0:T(8,128)S(1)}, u32[]{:S(2)}, u32[]{:S(2)}) %collective-permute-start.10) | collective-permute-done | bytes 65568 | tf_op jit(solution)/shard_map/ppermute | solution.py:86
  72.3 2.5 %collective-permute-done.11 = f32[4,1,1,1,1,1,16,128]{7,6,5,4,3,2,1,0:T(8,128)S(1)} collective-permute-done((f32[4,1,1,1,1,1,16,128]{7,6,5,4,3,2,1,0:T(8,128)S(1)}, f32[4,1,1,1,1,1,16,128]{7,6,5,4,3,2,1,0:T(8,128)S(1)}, u32[]{:S(2)}, u32[]{:S(2)}) %collective-permute-start.11) | collective-permute-done | bytes 32800 | tf_op jit(solution)/shard_map/ppermute | solution.py:86
  74.8 1.4 %collective-permute-done.14 = f32[4,1,1,1,1,1,16,128]{7,6,5,4,3,2,1,0:T(8,128)S(1)} collective-permute-done((f32[4,1,1,1,1,1,16,128]{7,6,5,4,3,2,1,0:T(8,128)S(1)}, f32[4,1,1,1,1,1,16,128]{7,6,5,4,3,2,1,0:T(8,128)S(1)}, u32[]{:S(2)}, u32[]{:S(2)}) %collective-permute-start.14) | collective-permute-done | bytes 32800 | tf_op jit(solution)/shard_map/ppermute | solution.py:86
  78.2 1.8 %fusion.13 = bf16[12,16,128]{2,1,0:T(8,128)(2,1)S(1)} fusion(bf16[12,4,136,128]{3,2,1,0:T(8,128)(2,1)} %all-gather.2.cloned.1.call-done, bf16[12,4,16,128]{3,2,1,0:T(8,128)(2,1)S(1)} %bitcast.110, pred[12,4]{1,0:T(8,128)(4,1)S(1)} %copy.61), kind=kOutput, calls=%fused_computation.16 | convolution fusion | flops 25288704 | bytes 1818672 | tf_op jit(solution)/shard_map/nerc,necd->nrd/dot_general | solution.py:136
  80.1 1.5 %collective-permute-start.19 = (bf16[4,1,1,1,1,1,16,128]{7,6,0,5,4,3,2,1:T(8,128)(2,1)S(1)}, bf16[4,1,1,1,1,1,16,128]{7,6,0,5,4,3,2,1:T(8,128)(2,1)S(1)}, u32[]{:S(2)}, u32[]{:S(2)}) collective-permute-start(bf16[4,1,1,1,1,1,16,128]{7,6,0,5,4,3,2,1:T(8,128)(2,1)S(1)} %get-tuple-element.33), channel_id=1, source_target_pairs={{0,2},{1,3},{2,0},{3,1},{4,6},{5,7},{6,4},{7,5},{8,10},{9,11},{10,... | collective-permute-start | bytes 49160 | tf_op jit(solution)/shard_map/ppermute | solution.py:91
  81.6 3.1 %collective-permute-done.15 = bf16[4,1,1,1,1,1,16,128]{7,6,0,5,4,3,2,1:T(8,128)(2,1)S(1)} collective-permute-done((bf16[4,1,1,1,1,1,16,128]{7,6,0,5,4,3,2,1:T(8,128)(2,1)S(1)}, bf16[4,1,1,1,1,1,16,128]{7,6,0,5,4,3,2,1:T(8,128)(2,1)S(1)}, u32[]{:S(2)}, u32[]{:S(2)}) %collective-permute-start.15) | collective-permute-done | bytes 16416 | tf_op jit(solution)/shard_map/ppermute | solution.py:91
  84.8 2.1 %collective-permute-start.20 = (bf16[4,1,2,1,1,1,16,128]{7,6,0,2,5,4,3,1:T(8,128)(2,1)S(1)}, bf16[4,1,2,1,1,1,16,128]{7,6,0,2,5,4,3,1:T(8,128)(2,1)S(1)}, u32[]{:S(2)}, u32[]{:S(2)}) collective-permute-start(bf16[4,1,2,1,1,1,16,128]{7,6,0,2,5,4,3,1:T(8,128)(2,1)S(1)} %fusion.26), channel_id=1, source_target_pairs={{0,16},{4,20},{8,24},{12,28},{16,0},{20,4},{24,8},{28,12},{1,17},{... | collective-permute-start | bytes 98312 | tf_op jit(solution)/shard_map/ppermute | solution.py:91
  86.9 2.1 %collective-permute-start.24 = (bf16[4,1,1,2,1,1,16,128]{7,6,0,5,4,3,2,1:T(8,128)(2,1)S(1)}, bf16[4,1,1,2,1,1,16,128]{7,6,0,5,4,3,2,1:T(8,128)(2,1)S(1)}, u32[]{:S(2)}, u32[]{:S(2)}) collective-permute-start(bf16[4,1,1,2,1,1,16,128]{7,6,0,5,4,3,2,1:T(8,128)(2,1)S(1)} %maximum_select_fusion.20), channel_id=1, source_target_pairs={{0,2},{1,3},{2,0},{3,1},{4,6},{5,7},{6,4},{7,5},{8,10},{9,11},{10,... | collective-permute-start | bytes 98312 | tf_op jit(solution)/shard_map/ppermute | solution.py:91
  89.7 2.3 %collective-permute-start.21 = (bf16[4,1,2,1,1,2,16,128]{7,6,0,5,4,3,2,1:T(8,128)(2,1)S(1)}, bf16[4,1,2,1,1,2,16,128]{7,6,0,5,4,3,2,1:T(8,128)(2,1)S(1)}, u32[]{:S(2)}, u32[]{:S(2)}) collective-permute-start(bf16[4,1,2,1,1,2,16,128]{7,6,0,5,4,3,2,1:T(8,128)(2,1)S(1)} %copy.64), channel_id=1, source_target_pairs={{0,8},{4,12},{8,0},{12,4},{16,24},{20,28},{24,16},{28,20},{1,9},{5... | collective-permute-start | bytes 196616 | tf_op jit(solution)/shard_map/ppermute | solution.py:91
  94.8 4.0 %collective-permute-start.22 = (bf16[4,1,2,1,2,2,16,128]{7,6,0,5,4,3,2,1:T(8,128)(2,1)S(1)}, bf16[4,1,2,1,2,2,16,128]{7,6,0,5,4,3,2,1:T(8,128)(2,1)S(1)}, u32[]{:S(2)}, u32[]{:S(2)}) collective-permute-start(bf16[4,1,2,1,2,2,16,128]{7,6,0,5,4,3,2,1:T(8,128)(2,1)S(1)} %maximum_select_fusion.7), channel_id=1, source_target_pairs={{0,4},{4,0},{8,12},{12,8},{16,20},{20,16},{24,28},{28,24},{1,5},{5... | collective-permute-start | bytes 393224 | tf_op jit(solution)/shard_map/ppermute | solution.py:91
  99.1 2.6 %collective-permute-done.22 = bf16[4,1,2,1,2,2,16,128]{7,6,0,5,4,3,2,1:T(8,128)(2,1)S(1)} collective-permute-done((bf16[4,1,2,1,2,2,16,128]{7,6,0,5,4,3,2,1:T(8,128)(2,1)S(1)}, bf16[4,1,2,1,2,2,16,128]{7,6,0,5,4,3,2,1:T(8,128)(2,1)S(1)}, u32[]{:S(2)}, u32[]{:S(2)}) %collective-permute-start.22) | collective-permute-done | bytes 131104 | tf_op jit(solution)/shard_map/ppermute | solution.py:91
  101.7 2.1 %collective-permute-done.26 = bf16[4,1,2,2,1,2,16,128]{7,6,0,5,4,3,2,1:T(8,128)(2,1)S(1)} collective-permute-done((bf16[4,1,2,2,1,2,16,128]{7,6,0,5,4,3,2,1:T(8,128)(2,1)S(1)}, bf16[4,1,2,2,1,2,16,128]{7,6,0,5,4,3,2,1:T(8,128)(2,1)S(1)}, u32[]{:S(2)}, u32[]{:S(2)}) %collective-permute-start.26) | collective-permute-done | bytes 131104 | tf_op jit(solution)/shard_map/ppermute | solution.py:91
  105.1 2.3 %collective-permute-done.27 = bf16[12,1,2,2,2,2,16,128]{7,6,0,5,4,3,2,1:T(8,128)(2,1)} collective-permute-done((bf16[12,1,2,2,2,2,16,128]{7,6,0,5,4,3,2,1:T(8,128)(2,1)}, bf16[12,1,2,2,2,2,16,128]{7,6,0,5,4,3,2,1:T(8,128)(2,1)}, u32[]{:S(2)}, u32[]{:S(2)}) %collective-permute-start.27) | collective-permute-done | bytes 786464 | tf_op jit(solution)/shard_map/ppermute | solution.py:91
  107.5 1.6 %maximum_select_fusion = bf16[12,2,2,2,2,2,16,128]{7,6,0,5,4,3,2,1:T(8,128)(2,1)S(1)} fusion(bf16[12,1,2,2,2,2,16,128]{7,6,0,5,4,3,2,1:T(8,128)(2,1)} %collective-permute-done.27, bf16[4,1,2,2,2,2,16,128]{7,6,0,5,4,3,2,1:T(8,128)(2,1)S(1)} %maximum_select_fusion.3, bf16[4,1,2,2,2,2,16,128]{7,6,0,5,4,3,2,1:T(8,128)(2,1)S(1)} %maximum_select_fusion.2, ...), kind=kLoop, calls=%fused_computation.13 | loop fusion | flops 5505024 | bytes 3145729 | tf_op jit(solution)/shard_map/jit(_where)/select_n | solution.py:92
  109.1 1.7 %copy.72 = bf16[12,2,2,2,2,2,16,128]{7,6,5,4,3,2,1,0:T(8,128)(2,1)} copy(bf16[12,2,2,2,2,2,16,128]{7,6,0,5,4,3,2,1:T(8,128)(2,1)S(1)} %maximum_select_fusion) | data formatting | bytes 3145728 | tf_op jit(solution)/shard_map/jit(_where)/select_n | solution.py:92
  110.7 2.2 %gather_fusion.2 = bf16[8,512,128]{2,1,0:T(8,128)(2,1)S(1)} fusion(bf16[12,512,128]{2,1,0:T(8,128)(2,1)} %bitcast.101, s32[1024]{0:T(1024)S(1)} %pad_clamp_fusion), kind=kCustom, calls=%fused_computation.2 | custom fusion | bytes 2097184 | tf_op jit(solution)/shard_map/jit(_take)/gather | solution.py:146
  112.9 1.7 %fusion.16 = f32[4,512,256,1]{2,1,3,0:T(8,128)S(1)} fusion(bf16[4,2,256,128]{3,2,1,0:T(8,128)(2,1)} %basis_ref.1, bf16[4,2,512,128]{3,2,1,0:T(8,128)(2,1)S(1)} %bitcast.103, pred[4,2]{1,0:T(4,128)(4,1)S(1)} %copy.59), kind=kOutput, calls=%fused_computation.17 | convolution fusion | flops 268959744 | bytes 3670024 | tf_op jit(solution)/shard_map/jqrc,jqbc->jrb/dot_general | solution.py:147
  (133 shorter events, 22.9 us)
Async XLA Ops:
  6.5 39.4 %copy-start = (bf16[4,4,256,256]{3,2,1,0:T(8,128)(2,1)S(1)}, bf16[4,4,256,256]{3,2,1,0:T(8,128)(2,1)}, u32[]{:S(2)}) copy-start(bf16[4,4,256,256]{3,2,1,0:T(8,128)(2,1)} %param.9) | copy-start | bytes 6291460
  6.5 69.7 %all-gather.2.cloned.1.call-start = ((), (), s32[]{:S(2)}) async-start(), calls=%async_computation | async-start | bytes 2088960 | tf_op jit(solution)/shard_map/all_gather | solution.py:107
  15.7 7.5 %copy-start.9 = (s32[3,4]{1,0:T(4,128)S(1)}, s32[3,4]{1,0:T(4,128)}, u32[]{:S(2)}) copy-start(s32[3,4]{1,0:T(4,128)} %param.12) | copy-start | bytes 148
  15.7 7.6 %copy-start.6 = (bf16[3,4,128,128]{3,2,1,0:T(8,128)(2,1)S(1)}, bf16[3,4,128,128]{3,2,1,0:T(8,128)(2,1)}, u32[]{:S(2)}) copy-start(bf16[3,4,128,128]{3,2,1,0:T(8,128)(2,1)} %param.13) | copy-start | bytes 1179652
  18.6 11.4 %collective-permute-start.2 = (f32[12,1,2,2,2,2,16,128]{7,6,5,4,3,2,1,0:T(8,128)}, f32[12,1,2,2,2,2,16,128]{7,6,5,4,3,2,1,0:T(8,128)}, u32[]{:S(2)}, u32[]{:S(2)}) collective-permute-start(f32[12,1,2,2,2,2,16,128]{7,6,5,4,3,2,1,0:T(8,128)} %constant_dynamic-slice_fusion.12), channel_id=1, source_target_pairs={{0,1},{1,0},{2,3},{3,2},{4,5},{5,4},{6,7},{7,6},{8,9},{9,8},{10,11... | collective-permute-start | bytes 4718600 | tf_op jit(solution)/shard_map/ppermute | solution.py:86
  19.8 4.5 %collective-permute-start = (bf16[1,512,256]{2,1,0:T(8,128)(2,1)}, bf16[1,512,256]{2,1,0:T(8,128)(2,1)S(1)}, u32[]{:S(2)}, u32[]{:S(2)}) collective-permute-start(bf16[1,512,256]{2,1,0:T(8,128)(2,1)} %get-tuple-element.22), channel_id=1, source_target_pairs={{0,1},{1,2},{2,3},{3,4},{4,5},{5,6},{6,7},{7,8},{8,9},{9,10},{10,1... | collective-permute-start | bytes 786440 | tf_op jit(solution)/shard_map/ppermute | solution.py:53
  21.8 5.8 %collective-permute-start.1 = (bf16[1,512,256]{2,1,0:T(8,128)(2,1)}, bf16[1,512,256]{2,1,0:T(8,128)(2,1)}, u32[]{:S(2)}, u32[]{:S(2)}) collective-permute-start(bf16[1,512,256]{2,1,0:T(8,128)(2,1)} %get-tuple-element.23), channel_id=1, source_target_pairs={{1,0},{2,1},{3,2},{4,3},{5,4},{6,5},{7,6},{8,7},{9,8},{10,9},{11,1... | collective-permute-start | bytes 786440 | tf_op jit(solution)/shard_map/ppermute | solution.py:55
  33.4 17.5 %collective-permute-start.5 = (f32[4,1,2,2,1,2,16,128]{7,6,5,4,3,2,1,0:T(8,128)}, f32[4,1,2,2,1,2,16,128]{7,6,5,4,3,2,1,0:T(8,128)}, u32[]{:S(2)}, u32[]{:S(2)}) collective-permute-start(f32[4,1,2,2,1,2,16,128]{7,6,5,4,3,2,1,0:T(8,128)} %constant_dynamic-slice_fusion.9), channel_id=1, source_target_pairs={{0,8},{4,12},{8,0},{12,4},{16,24},{20,28},{24,16},{28,20},{1,9},{5... | collective-permute-start | bytes 786440 | tf_op jit(solution)/shard_map/ppermute | solution.py:86
  40.5 11.4 %collective-permute-start.4 = (f32[4,1,2,1,2,2,16,128]{7,6,5,4,3,2,1,0:T(8,128)}, f32[4,1,2,1,2,2,16,128]{7,6,5,4,3,2,1,0:T(8,128)}, u32[]{:S(2)}, u32[]{:S(2)}) collective-permute-start(f32[4,1,2,1,2,2,16,128]{7,6,5,4,3,2,1,0:T(8,128)} %constant_dynamic-slice_fusion.10), channel_id=1, source_target_pairs={{0,4},{4,0},{8,12},{12,8},{16,20},{20,16},{24,28},{28,24},{1,5},{5... | collective-permute-start | bytes 786440 | tf_op jit(solution)/shard_map/ppermute | solution.py:86
  41.1 11.7 %collective-permute-start.3 = (f32[4,1,1,2,2,2,16,128]{7,6,5,4,3,2,1,0:T(8,128)S(1)}, f32[4,1,1,2,2,2,16,128]{7,6,5,4,3,2,1,0:T(8,128)}, u32[]{:S(2)}, u32[]{:S(2)}) collective-permute-start(f32[4,1,1,2,2,2,16,128]{7,6,5,4,3,2,1,0:T(8,128)S(1)} %constant_dynamic-slice_fusion.11), channel_id=1, source_target_pairs={{0,2},{1,3},{2,0},{3,1},{4,6},{5,7},{6,4},{7,5},{8,10},{9,11},{10,... | collective-permute-start | bytes 786440 | tf_op jit(solution)/shard_map/ppermute | solution.py:86
  53.9 5.9 %collective-permute-start.6 = (f32[4,1,1,1,2,2,16,128]{7,6,5,4,3,2,1,0:T(8,128)S(1)}, f32[4,1,1,1,2,2,16,128]{7,6,5,4,3,2,1,0:T(8,128)S(1)}, u32[]{:S(2)}, u32[]{:S(2)}) collective-permute-start(f32[4,1,1,1,2,2,16,128]{7,6,5,4,3,2,1,0:T(8,128)S(1)} %constant_dynamic-slice_fusion.8), channel_id=1, source_target_pairs={{0,4},{4,0},{8,12},{12,8},{16,20},{20,16},{24,28},{28,24},{1,5},{5... | collective-permute-start | bytes 393224 | tf_op jit(solution)/shard_map/ppermute | solution.py:86
  55.7 9.1 %collective-permute-start.9 = (f32[4,1,2,1,1,2,16,128]{7,6,5,4,3,2,1,0:T(8,128)S(1)}, f32[4,1,2,1,1,2,16,128]{7,6,5,4,3,2,1,0:T(8,128)S(1)}, u32[]{:S(2)}, u32[]{:S(2)}) collective-permute-start(f32[4,1,2,1,1,2,16,128]{7,6,5,4,3,2,1,0:T(8,128)S(1)} %constant_dynamic-slice_fusion.5), channel_id=1, source_target_pairs={{0,8},{4,12},{8,0},{12,4},{16,24},{20,28},{24,16},{28,20},{1,9},{5... | collective-permute-start | bytes 393224 | tf_op jit(solution)/shard_map/ppermute | solution.py:86
  57.2 7.7 %collective-permute-start.12 = (f32[4,1,2,2,1,1,16,128]{7,6,5,4,3,2,1,0:T(8,128)S(1)}, f32[4,1,2,2,1,1,16,128]{7,6,5,4,3,2,1,0:T(8,128)S(1)}, u32[]{:S(2)}, u32[]{:S(2)}) collective-permute-start(f32[4,1,2,2,1,1,16,128]{7,6,5,4,3,2,1,0:T(8,128)S(1)} %constant_dynamic-slice_fusion.2), channel_id=1, source_target_pairs={{0,16},{4,20},{8,24},{12,28},{16,0},{20,4},{24,8},{28,12},{1,17},{... | collective-permute-start | bytes 393224 | tf_op jit(solution)/shard_map/ppermute | solution.py:86
  59.8 6.5 %collective-permute-start.7 = (f32[4,1,1,1,1,2,16,128]{7,6,5,4,3,2,1,0:T(8,128)S(1)}, f32[4,1,1,1,1,2,16,128]{7,6,5,4,3,2,1,0:T(8,128)S(1)}, u32[]{:S(2)}, u32[]{:S(2)}) collective-permute-start(f32[4,1,1,1,1,2,16,128]{7,6,5,4,3,2,1,0:T(8,128)S(1)} %constant_dynamic-slice_fusion.7), channel_id=1, source_target_pairs={{0,8},{4,12},{8,0},{12,4},{16,24},{20,28},{24,16},{28,20},{1,9},{5... | collective-permute-start | bytes 196616 | tf_op jit(solution)/shard_map/ppermute | solution.py:86
  64.8 5.9 %collective-permute-start.10 = (f32[4,1,2,1,1,1,16,128]{7,6,5,4,3,2,1,0:T(8,128)S(1)}, f32[4,1,2,1,1,1,16,128]{7,6,5,4,3,2,1,0:T(8,128)S(1)}, u32[]{:S(2)}, u32[]{:S(2)}) collective-permute-start(f32[4,1,2,1,1,1,16,128]{7,6,5,4,3,2,1,0:T(8,128)S(1)} %constant_dynamic-slice_fusion.4), channel_id=1, source_target_pairs={{0,16},{4,20},{8,24},{12,28},{16,0},{20,4},{24,8},{28,12},{1,17},{... | collective-permute-start | bytes 196616 | tf_op jit(solution)/shard_map/ppermute | solution.py:86
  65.0 7.2 %collective-permute-start.13 = (f32[4,1,1,2,1,1,16,128]{7,6,5,4,3,2,1,0:T(8,128)S(1)}, f32[4,1,1,2,1,1,16,128]{7,6,5,4,3,2,1,0:T(8,128)S(1)}, u32[]{:S(2)}, u32[]{:S(2)}) collective-permute-start(f32[4,1,1,2,1,1,16,128]{7,6,5,4,3,2,1,0:T(8,128)S(1)} %constant_dynamic-slice_fusion.1), channel_id=1, source_target_pairs={{0,2},{1,3},{2,0},{3,1},{4,6},{5,7},{6,4},{7,5},{8,10},{9,11},{10,... | collective-permute-start | bytes 196616 | tf_op jit(solution)/shard_map/ppermute | solution.py:86
  66.4 6.0 %collective-permute-start.8 = (f32[4,1,1,1,1,1,16,128]{7,6,5,4,3,2,1,0:T(8,128)S(1)}, f32[4,1,1,1,1,1,16,128]{7,6,5,4,3,2,1,0:T(8,128)S(1)}, u32[]{:S(2)}, u32[]{:S(2)}) collective-permute-start(f32[4,1,1,1,1,1,16,128]{7,6,5,4,3,2,1,0:T(8,128)S(1)} %constant_dynamic-slice_fusion.6), channel_id=1, source_target_pairs={{0,16},{4,20},{8,24},{12,28},{16,0},{20,4},{24,8},{28,12},{1,17},{... | collective-permute-start | bytes 98312 | tf_op jit(solution)/shard_map/ppermute | solution.py:86
  70.8 4.0 %collective-permute-start.11 = (f32[4,1,1,1,1,1,16,128]{7,6,5,4,3,2,1,0:T(8,128)S(1)}, f32[4,1,1,1,1,1,16,128]{7,6,5,4,3,2,1,0:T(8,128)S(1)}, u32[]{:S(2)}, u32[]{:S(2)}) collective-permute-start(f32[4,1,1,1,1,1,16,128]{7,6,5,4,3,2,1,0:T(8,128)S(1)} %constant_dynamic-slice_fusion.3), channel_id=1, source_target_pairs={{0,2},{1,3},{2,0},{3,1},{4,6},{5,7},{6,4},{7,5},{8,10},{9,11},{10,... | collective-permute-start | bytes 98312 | tf_op jit(solution)/shard_map/ppermute | solution.py:86
  72.2 4.0 %collective-permute-start.14 = (f32[4,1,1,1,1,1,16,128]{7,6,5,4,3,2,1,0:T(8,128)S(1)}, f32[4,1,1,1,1,1,16,128]{7,6,5,4,3,2,1,0:T(8,128)S(1)}, u32[]{:S(2)}, u32[]{:S(2)}) collective-permute-start(f32[4,1,1,1,1,1,16,128]{7,6,5,4,3,2,1,0:T(8,128)S(1)} %constant_dynamic-slice_fusion), channel_id=1, source_target_pairs={{0,4},{4,0},{8,12},{12,8},{16,20},{20,16},{24,28},{28,24},{1,5},{5... | collective-permute-start | bytes 98312 | tf_op jit(solution)/shard_map/ppermute | solution.py:86
  80.0 4.7 %collective-permute-start.15 = (bf16[4,1,1,1,1,1,16,128]{7,6,0,5,4,3,2,1:T(8,128)(2,1)S(1)}, bf16[4,1,1,1,1,1,16,128]{7,6,0,5,4,3,2,1:T(8,128)(2,1)S(1)}, u32[]{:S(2)}, u32[]{:S(2)}) collective-permute-start(bf16[4,1,1,1,1,1,16,128]{7,6,0,5,4,3,2,1:T(8,128)(2,1)S(1)} %get-tuple-element.32), channel_id=1, source_target_pairs={{0,16},{4,20},{8,24},{12,28},{16,0},{20,4},{24,8},{28,12},{1,17},{... | collective-permute-start | bytes 49160 | tf_op jit(solution)/shard_map/ppermute | solution.py:91
  80.1 4.7 %collective-permute-start.19 = (bf16[4,1,1,1,1,1,16,128]{7,6,0,5,4,3,2,1:T(8,128)(2,1)S(1)}, bf16[4,1,1,1,1,1,16,128]{7,6,0,5,4,3,2,1:T(8,128)(2,1)S(1)}, u32[]{:S(2)}, u32[]{:S(2)}) collective-permute-start(bf16[4,1,1,1,1,1,16,128]{7,6,0,5,4,3,2,1:T(8,128)(2,1)S(1)} %get-tuple-element.33), channel_id=1, source_target_pairs={{0,2},{1,3},{2,0},{3,1},{4,6},{5,7},{6,4},{7,5},{8,10},{9,11},{10,... | collective-permute-start | bytes 49160 | tf_op jit(solution)/shard_map/ppermute | solution.py:91
  81.6 5.3 %collective-permute-start.23 = (bf16[4,1,1,1,1,1,16,128]{7,6,0,5,4,3,2,1:T(8,128)(2,1)S(1)}, bf16[4,1,1,1,1,1,16,128]{7,6,0,5,4,3,2,1:T(8,128)(2,1)S(1)}, u32[]{:S(2)}, u32[]{:S(2)}) collective-permute-start(bf16[4,1,1,1,1,1,16,128]{7,6,0,5,4,3,2,1:T(8,128)(2,1)S(1)} %get-tuple-element.34), channel_id=1, source_target_pairs={{0,4},{4,0},{8,12},{12,8},{16,20},{20,16},{24,28},{28,24},{1,5},{5... | collective-permute-start | bytes 49160 | tf_op jit(solution)/shard_map/ppermute | solution.py:91
  84.7 4.3 %collective-permute-start.16 = (bf16[4,1,1,1,1,2,16,128]{7,6,0,5,4,3,2,1:T(8,128)(2,1)S(1)}, bf16[4,1,1,1,1,2,16,128]{7,6,0,5,4,3,2,1:T(8,128)(2,1)S(1)}, u32[]{:S(2)}, u32[]{:S(2)}) collective-permute-start(bf16[4,1,1,1,1,2,16,128]{7,6,0,5,4,3,2,1:T(8,128)(2,1)S(1)} %maximum_select_fusion.16), channel_id=1, source_target_pairs={{0,8},{4,12},{8,0},{12,4},{16,24},{20,28},{24,16},{28,20},{1,9},{5... | collective-permute-start | bytes 98312 | tf_op jit(solution)/shard_map/ppermute | solution.py:91
  84.8 4.9 %collective-permute-start.20 = (bf16[4,1,2,1,1,1,16,128]{7,6,0,2,5,4,3,1:T(8,128)(2,1)S(1)}, bf16[4,1,2,1,1,1,16,128]{7,6,0,2,5,4,3,1:T(8,128)(2,1)S(1)}, u32[]{:S(2)}, u32[]{:S(2)}) collective-permute-start(bf16[4,1,2,1,1,1,16,128]{7,6,0,2,5,4,3,1:T(8,128)(2,1)S(1)} %fusion.26), channel_id=1, source_target_pairs={{0,16},{4,20},{8,24},{12,28},{16,0},{20,4},{24,8},{28,12},{1,17},{... | collective-permute-start | bytes 98312 | tf_op jit(solution)/shard_map/ppermute | solution.py:91
  86.9 5.1 %collective-permute-start.24 = (bf16[4,1,1,2,1,1,16,128]{7,6,0,5,4,3,2,1:T(8,128)(2,1)S(1)}, bf16[4,1,1,2,1,1,16,128]{7,6,0,5,4,3,2,1:T(8,128)(2,1)S(1)}, u32[]{:S(2)}, u32[]{:S(2)}) collective-permute-start(bf16[4,1,1,2,1,1,16,128]{7,6,0,5,4,3,2,1:T(8,128)(2,1)S(1)} %maximum_select_fusion.20), channel_id=1, source_target_pairs={{0,2},{1,3},{2,0},{3,1},{4,6},{5,7},{6,4},{7,5},{8,10},{9,11},{10,... | collective-permute-start | bytes 98312 | tf_op jit(solution)/shard_map/ppermute | solution.py:91
  89.1 5.0 %collective-permute-start.17 = (bf16[4,1,1,1,2,2,16,128]{7,6,0,5,4,3,2,1:T(8,128)(2,1)S(1)}, bf16[4,1,1,1,2,2,16,128]{7,6,0,5,4,3,2,1:T(8,128)(2,1)S(1)}, u32[]{:S(2)}, u32[]{:S(2)}) collective-permute-start(bf16[4,1,1,1,2,2,16,128]{7,6,0,5,4,3,2,1:T(8,128)(2,1)S(1)} %maximum_select_fusion.11), channel_id=1, source_target_pairs={{0,4},{4,0},{8,12},{12,8},{16,20},{20,16},{24,28},{28,24},{1,5},{5... | collective-permute-start | bytes 196616 | tf_op jit(solution)/shard_map/ppermute | solution.py:91
  89.7 5.0 %collective-permute-start.21 = (bf16[4,1,2,1,1,2,16,128]{7,6,0,5,4,3,2,1:T(8,128)(2,1)S(1)}, bf16[4,1,2,1,1,2,16,128]{7,6,0,5,4,3,2,1:T(8,128)(2,1)S(1)}, u32[]{:S(2)}, u32[]{:S(2)}) collective-permute-start(bf16[4,1,2,1,1,2,16,128]{7,6,0,5,4,3,2,1:T(8,128)(2,1)S(1)} %copy.64), channel_id=1, source_target_pairs={{0,8},{4,12},{8,0},{12,4},{16,24},{20,28},{24,16},{28,20},{1,9},{5... | collective-permute-start | bytes 196616 | tf_op jit(solution)/shard_map/ppermute | solution.py:91
  92.1 6.7 %collective-permute-start.25 = (bf16[4,1,2,2,1,1,16,128]{7,6,0,5,4,3,2,1:T(8,128)(2,1)S(1)}, bf16[4,1,2,2,1,1,16,128]{7,6,0,5,4,3,2,1:T(8,128)(2,1)S(1)}, u32[]{:S(2)}, u32[]{:S(2)}) collective-permute-start(bf16[4,1,2,2,1,1,16,128]{7,6,0,5,4,3,2,1:T(8,128)(2,1)S(1)} %fusion.25), channel_id=1, source_target_pairs={{0,16},{4,20},{8,24},{12,28},{16,0},{20,4},{24,8},{28,12},{1,17},{... | collective-permute-start | bytes 196616 | tf_op jit(solution)/shard_map/ppermute | solution.py:91
  94.0 5.0 %collective-permute-start.18 = (bf16[4,1,1,2,2,2,16,128]{7,6,0,5,4,3,2,1:T(8,128)(2,1)S(1)}, bf16[4,1,1,2,2,2,16,128]{7,6,0,5,4,3,2,1:T(8,128)(2,1)S(1)}, u32[]{:S(2)}, u32[]{:S(2)}) collective-permute-start(bf16[4,1,1,2,2,2,16,128]{7,6,0,5,4,3,2,1:T(8,128)(2,1)S(1)} %maximum_select_fusion.5), channel_id=1, source_target_pairs={{0,2},{1,3},{2,0},{3,1},{4,6},{5,7},{6,4},{7,5},{8,10},{9,11},{10,... | collective-permute-start | bytes 393224 | tf_op jit(solution)/shard_map/ppermute | solution.py:91
  94.8 6.9 %collective-permute-start.22 = (bf16[4,1,2,1,2,2,16,128]{7,6,0,5,4,3,2,1:T(8,128)(2,1)S(1)}, bf16[4,1,2,1,2,2,16,128]{7,6,0,5,4,3,2,1:T(8,128)(2,1)S(1)}, u32[]{:S(2)}, u32[]{:S(2)}) collective-permute-start(bf16[4,1,2,1,2,2,16,128]{7,6,0,5,4,3,2,1:T(8,128)(2,1)S(1)} %maximum_select_fusion.7), channel_id=1, source_target_pairs={{0,4},{4,0},{8,12},{12,8},{16,20},{20,16},{24,28},{28,24},{1,5},{5... | collective-permute-start | bytes 393224 | tf_op jit(solution)/shard_map/ppermute | solution.py:91
  98.8 5.0 %collective-permute-start.26 = (bf16[4,1,2,2,1,2,16,128]{7,6,0,5,4,3,2,1:T(8,128)(2,1)S(1)}, bf16[4,1,2,2,1,2,16,128]{7,6,0,5,4,3,2,1:T(8,128)(2,1)S(1)}, u32[]{:S(2)}, u32[]{:S(2)}) collective-permute-start(bf16[4,1,2,2,1,2,16,128]{7,6,0,5,4,3,2,1:T(8,128)(2,1)S(1)} %maximum_select_fusion.9), channel_id=1, source_target_pairs={{0,8},{4,12},{8,0},{12,4},{16,24},{20,28},{24,16},{28,20},{1,9},{5... | collective-permute-start | bytes 393224 | tf_op jit(solution)/shard_map/ppermute | solution.py:91
  104.8 2.6 %collective-permute-start.27 = (bf16[12,1,2,2,2,2,16,128]{7,6,0,5,4,3,2,1:T(8,128)(2,1)}, bf16[12,1,2,2,2,2,16,128]{7,6,0,5,4,3,2,1:T(8,128)(2,1)}, u32[]{:S(2)}, u32[]{:S(2)}) collective-permute-start(bf16[12,1,2,2,2,2,16,128]{7,6,0,5,4,3,2,1:T(8,128)(2,1)} %pad_maximum_fusion.1), channel_id=1, source_target_pairs={{0,1},{1,0},{2,3},{3,2},{4,5},{5,4},{6,7},{7,6},{8,9},{9,8},{10,11... | collective-permute-start | bytes 2359304 | tf_op jit(solution)/shard_map/ppermute | solution.py:91
  (7 other events, 27.8 us)
Sparse Core Ops, SparseCore 0:
  24.2 27.3 all-gather.1

commit v10 on v9

--- a/solution.py
+++ b/solution.py
@@ -6,32 +6,39 @@
 from jax.sharding import PartitionSpec as P
 
 
-def restrict_kernel(links, residual_ref, basis_ref, out_ref):
+def restrict_kernel(links, half, residual_ref, basis_ref, keep_ref, send_ref):
     j = pl.program_id(0)
     q = pl.program_id(1)
 
     @pl.when((j == 0) & (q == 0))
     def _():
-        out_ref[...] = jnp.zeros_like(out_ref)
+        keep_ref[...] = jnp.zeros_like(keep_ref)
+        send_ref[...] = jnp.zeros_like(send_ref)
 
     n = links[j, q]
-    out_ref[n] += jnp.dot(residual_ref[0], basis_ref[0, 0], preferred_element_type=jnp.float32)
+    rows = keep_ref.shape[1]
+    mine = pl.multiple_of(half[0] * rows, rows)
+    other = pl.multiple_of((1 - half[0]) * rows, rows)
+    keep_ref[n] += jnp.dot(residual_ref[0, pl.ds(mine, rows), :], basis_ref[0, 0], preferred_element_type=jnp.float32)
+    send_ref[n] += jnp.dot(residual_ref[0, pl.ds(other, rows), :], basis_ref[0, 0], preferred_element_type=jnp.float32)
 
 
-def restrict(residual, basis, interface, total_blocks):
+def restrict(residual, basis, interface, total_blocks, half):
     count, rhs, size = residual.shape
     width = basis.shape[-1]
+    rows = rhs // 2
+    block = pl.BlockSpec((total_blocks, rows, width), lambda j, q, links, half: (0, 0, 0))
     return pl.pallas_call(
         restrict_kernel,
-        out_shape=jax.ShapeDtypeStruct((total_blocks, rhs, width), jnp.float32),
+        out_shape=[jax.ShapeDtypeStruct((total_blocks, rows, width), jnp.float32)] * 2,
         grid_spec=pltpu.PrefetchScalarGridSpec(
-            num_scalar_prefetch=1,
+            num_scalar_prefetch=2,
             grid=(count, interface.shape[1]),
             in_specs=[
-                pl.BlockSpec((1, rhs, size), lambda j, q, links: (j, 0, 0)),
-                pl.BlockSpec((1, 1, size, width), lambda j, q, links: (j, q, 0, 0)),
+                pl.BlockSpec((1, rhs, size), lambda j, q, links, half: (j, 0, 0)),
+                pl.BlockSpec((1, 1, size, width), lambda j, q, links, half: (j, q, 0, 0)),
             ],
-            out_specs=pl.BlockSpec((total_blocks, rhs, width), lambda j, q, links: (0, 0, 0)),
+            out_specs=[block, block],
         ),
         compiler_params=pltpu.CompilerParams(dimension_semantics=("arbitrary", "arbitrary")),
         cost_estimate=pl.CostEstimate(
@@ -39,7 +46,7 @@
             bytes_accessed=residual.size * 2 + basis.size * 2 + total_blocks * rhs * width * 4,
             transcendentals=0,
         ),
-    )(interface, residual, basis)
+    )(interface, half, residual, basis)
 
 
 def with_halo(cells, sides, width):
@@ -111,17 +118,18 @@
     rhs = residual.shape[1]
     width = basis.shape[-1]
     total_blocks = pattern_all.shape[0]
-    restricted = restrict(residual, basis, interface, total_blocks)
+    bits = device_bits()
+    own_half = bit_of(*bits[0])
+    keep, send = restrict(residual, basis, interface, total_blocks, own_half.reshape(1).astype(jnp.int32))
 
-    bits = device_bits()
     nb = len(bits)
     inner = rhs >> nb
     assert inner << nb == rhs
     streams = 3 if total_blocks % 3 == 0 else 1
     per = total_blocks // streams
     orders = stream_orders(nb, streams)
-    split = restricted.reshape((total_blocks,) + (2,) * nb + (inner, width))
-    whole = halve(split, 1, *bits[0], jnp.float32)
+    whole = keep + lax.ppermute(send, bits[0][0], pairs(*bits[0]))
+    whole = whole.reshape((total_blocks, 1) + (2,) * (nb - 1) + (inner, width))
     extended, inverse_blocks, whole = lax.optimization_barrier((extended, inverse_blocks, whole))
     parts = [lax.slice_in_dim(whole, s * per, (s + 1) * per, axis=0) for s in range(streams)]
     picked = jnp.take(extended, margin, axis=0)
@@ -140,10 +148,16 @@
     outs = [lax.slice_in_dim(solved, s * per, (s + 1) * per, axis=0) for s in range(streams)]
     for step in reversed(range(1, nb)):
         outs = [double(y, 1 + orders[s][step], *bits[orders[s][step]]) for s, y in enumerate(outs)]
-    coarse_out = double(jnp.concatenate(outs, axis=0), 1, *bits[0])
-    coarse_out = coarse_out.reshape(total_blocks, rhs, width)
+    own = jnp.concatenate(outs, axis=0).reshape(total_blocks, rhs // 2, width)
+    got = lax.ppermute(own, bits[0][0], pairs(*bits[0]))
+    own_rows = jnp.take(own, interface, axis=0)
+    got_rows = jnp.take(got, interface, axis=0)
+    lifted = jnp.where(
+        own_half == 0,
+        jnp.concatenate([own_rows, got_rows], axis=2),
+        jnp.concatenate([got_rows, own_rows], axis=2),
+    )
 
-    lifted = jnp.take(coarse_out, interface, axis=0)
     spread = jnp.einsum("jqrc,jqbc->jrb", lifted, basis, preferred_element_type=jnp.float32)
     return (local + spread).astype(jnp.bfloat16)
 

time: 123 us -> 117 us (0.951)
  other arithmetic: 12.1 us -> 9.65 us
  starting transfers between devices: 38.1 us -> 36.6 us
  local copies, waits for them, and re-layouts: 18.3 us -> 17 us
    dynamic_slice x13 -> x12, local copies, waits for them, and re-layouts: 4.5 us -> 1.62 us  [halve(): send = lax.dynamic_index_in_dim(x, 1 - v, axis=dim, keepdims=True)]
    ppermute x13 -> x12, starting transfers between devices: 13.9 us -> 11.7 us  [double(): recv = lax.ppermute(y, axis, pairs(axis, mask))]
    unnamed x22 -> x24, local copies, waits for them, and re-layouts: 2.49 us -> 4.41 us
    add x10 -> x9, other arithmetic: 4.81 us -> 3.05 us  [halve(): keep + lax.ppermute(send.astype(wire), axis, pairs(axis, mask)).astype(x....]
    select_n x13 -> x12, other arithmetic: 1.81 us -> 0.19 us  [double(): jnp.where(v == 0, jnp.concatenate([y, recv], axis=dim), jnp.concatenate([...]
    add x0 -> x1, other arithmetic: none -> 1.61 us  [per_device(): whole = keep + lax.ppermute(send, bits[0][0], pairs(*bits[0]))]
    select_n x2 -> x3, local copies, waits for them, and re-layouts: 1.66 us -> 0.06 us  [double(): jnp.where(v == 0, jnp.concatenate([y, recv], axis=dim), jnp.concatenate([...]
    ppermute x0 -> x2, waiting for transfers between devices: none -> 1.42 us  [the longest x1 1.42 us: per_device(): got = lax.ppermute(own, bits[0][0], pairs(*bits[0]))]
  transfers between devices with their start and end apart: 29 -> 29, of which waited for: 12 -> 11; matrix products, arithmetic and copies ran while one was open for 17% -> 19% of each run, Pallas kernels for 0% -> 0%
where the time goes in v10:
time: 117 us; the launch traced here: 116 us
  starting transfers between devices  36.6 us (31%)
  waiting for transfers between devices  24.1 us (21%)
  local copies, waits for them, and re-layouts  17 us (15%)
  between operations  14 us (12%)
  other arithmetic  9.65 us (8%)
  Pallas kernels  7.52 us (6%)
  matrix products  7.14 us (6%)
    ppermute x12, starting transfers between devices, halve(): lax.ppermute(send.astype(wire), axis, pairs(axis, mask)).astype(x.dtype)  20.3 us
    ppermute x12, starting transfers between devices, double(): recv = lax.ppermute(y, axis, pairs(axis, mask))  11.7 us
    ppermute x12, waiting for transfers between devices, double(): recv = lax.ppermute(y, axis, pairs(axis, mask))  10.7 us
    ppermute x12, waiting for transfers between devices, halve(): lax.ppermute(send.astype(wire), axis, pairs(axis, mask)).astype(x.dtype)  9.24 us
    pallas_call x1, Pallas kernels, restrict(): pl.pallas_call(restrict_kernel, out_shape=[jax.ShapeDtypeStruct((total_bl...  7.52 us
    dot_general x1, matrix products, per_device(): jnp.einsum('jerb,jebc->jrc', picked, inverse_blocks, preferred_element_ty...  4.89 us
    unnamed x24, local copies, waits for them, and re-layouts  4.41 us
    gather x1, local copies, waits for them, and re-layouts, per_device(): picked = jnp.take(extended, margin, axis=0)  4.24 us
  transfers between devices with their start and end apart: 29, of which 11 were waited for; matrix products, arithmetic and copies ran while one was open for 19% of the time, Pallas kernels for 0%

profile of v10, /device:TPU:0, one launch (start us, length us, event | category | flops | bytes accessed | tf_op | source)
XLA Modules:
  0.0 116.0 jit_solution(10110583147311121952)
XLA Ops:
  6.6 1.5 %copy.59.links = s32[4,2]{1,0:T(4,128)} copy(s32[4,2]{0,1:T(2,128)} %param.12) | data formatting | bytes 64 | tf_op args[3]
  8.1 7.5 %shard_map.73 = (f32[12,256,128]{2,1,0:T(8,128)}, f32[12,256,128]{2,1,0:T(8,128)}) custom-call(s32[4,2]{1,0:T(4,128)} %copy.59.links, s32[1]{0:T(128)} %bitcast.half, bf16[4,512,256]{2,1,0:T(8,128)(2,1)} %residual_ref.1, bf16[4,2,256,128]{3,2,1,0:T(8,128)(2,1)} %basis_ref.1), custom_call_target="tpu_custom_call" | custom-call | flops 268435456 | bytes 4718592 | tf_op jit(solution)/shard_map/pallas_call | solution.py:31
  16.1 1.9 %fusion.42 = (bf16[1,512,256]{2,1,0:T(8,128)(2,1)}, bf16[1,512,256]{2,1,0:T(8,128)(2,1)}) fusion(bf16[4,512,256]{2,1,0:T(8,128)(2,1)} %residual_ref.1), kind=kLoop, calls=%fused_computation.109 | loop fusion | bytes 1048576 | tf_op jit(solution)/shard_map/slice | solution.py:57
  17.9 2.7 %collective-permute-start = (bf16[1,512,256]{2,1,0:T(8,128)(2,1)}, bf16[1,512,256]{2,1,0:T(8,128)(2,1)}, u32[]{:S(2)}, u32[]{:S(2)}) collective-permute-start(bf16[1,512,256]{2,1,0:T(8,128)(2,1)} %get-tuple-element.27), channel_id=1, source_target_pairs={{0,1},{1,2},{2,3},{3,4},{4,5},{5,6},{6,7},{7,8},{8,9},{9,10},{10,1... | collective-permute-start | bytes 786440 | tf_op jit(solution)/shard_map/ppermute | solution.py:60
  20.6 1.3 %collective-permute-start.1 = (bf16[1,512,256]{2,1,0:T(8,128)(2,1)}, bf16[1,512,256]{2,1,0:T(8,128)(2,1)}, u32[]{:S(2)}, u32[]{:S(2)}) collective-permute-start(bf16[1,512,256]{2,1,0:T(8,128)(2,1)} %get-tuple-element.28), channel_id=1, source_target_pairs={{1,0},{2,1},{3,2},{4,3},{5,4},{6,5},{7,6},{8,7},{9,8},{10,9},{11,1... | collective-permute-start | bytes 786440 | tf_op jit(solution)/shard_map/ppermute | solution.py:62
  23.1 2.7 %collective-permute-done.1 = bf16[1,512,256]{2,1,0:T(8,128)(2,1)} collective-permute-done((bf16[1,512,256]{2,1,0:T(8,128)(2,1)}, bf16[1,512,256]{2,1,0:T(8,128)(2,1)}, u32[]{:S(2)}, u32[]{:S(2)}) %collective-permute-start.1) | collective-permute-done | bytes 262176 | tf_op jit(solution)/shard_map/ppermute | solution.py:62
  25.8 2.4 %pad_maximum_fusion = bf16[6,512,256]{2,1,0:T(8,128)(2,1)} fusion(bf16[1,512,256]{2,1,0:T(8,128)(2,1)} %collective-permute-done.1, bf16[4,512,256]{2,1,0:T(8,128)(2,1)S(1)} %copy-done.1, bf16[1,512,256]{2,1,0:T(8,128)(2,1)} %collective-permute-done), kind=kLoop, calls=%fused_computation.13 | loop fusion | flops 1572864 | bytes 3145728 | tf_op jit(solution)/shard_map/concatenate | solution.py:58
  28.1 1.6 %add.169 = f32[12,256,128]{2,1,0:T(8,128)S(1)} add(f32[12,256,128]{2,1,0:T(8,128)S(1)} %copy-done.5, f32[12,256,128]{2,1,0:T(8,128)} %collective-permute-done.2) | non-fusion elementwise | flops 393216 | bytes 4718592 | tf_op jit(solution)/shard_map/add | solution.py:131
  31.4 6.4 %collective-permute-start.5 = (f32[4,1,2,2,1,2,16,128]{7,6,5,4,3,2,0,1:T(8,128)}, f32[4,1,2,2,1,2,16,128]{7,6,5,4,3,2,0,1:T(8,128)}, u32[]{:S(2)}, u32[]{:S(2)}) collective-permute-start(f32[4,1,2,2,1,2,16,128]{7,6,5,4,3,2,0,1:T(8,128)} %constant_dynamic-slice_fusion.9), channel_id=1, source_target_pairs={{0,8},{4,12},{8,0},{12,4},{16,24},{20,28},{24,16},{28,20},{1,9},{5... | collective-permute-start | bytes 786440 | tf_op jit(solution)/shard_map/ppermute | solution.py:93
  39.8 4.2 %gather_fusion = bf16[16,512,256]{2,1,0:T(8,128)(2,1)} fusion(bf16[6,512,256]{2,1,0:T(8,128)(2,1)} %pad_maximum_fusion, s32[1024]{0:T(1024)S(1)} %pad_clamp_fusion.2), kind=kCustom, calls=%fused_computation.2 | custom fusion | bytes 8388672 | tf_op jit(solution)/shard_map/jit(_take)/gather | solution.py:135
  44.0 4.9 %fusion.5 = f32[4,512,256]{2,1,0:T(8,128)} fusion(bf16[4,4,256,256]{3,2,1,0:T(8,128)(2,1)S(1)} %copy-done, bf16[4,4,512,256]{3,2,1,0:T(8,128)(2,1)} %bitcast.87, pred[4,4]{1,0:T(4,128)(4,1)S(1)} %compare_and_fusion.2), kind=kOutput, calls=%fused_computation.10 | convolution fusion | flops 1075838976 | bytes 8388624 | tf_op jit(solution)/shard_map/jerb,jebc->jrc/dot_general | solution.py:136
  52.0 1.8 %collective-permute-start.6 = (f32[4,1,1,1,2,2,16,128]{7,6,5,4,3,2,0,1:T(8,128)S(1)}, f32[4,1,1,1,2,2,16,128]{7,6,5,4,3,2,0,1:T(8,128)S(1)}, u32[]{:S(2)}, u32[]{:S(2)}) collective-permute-start(f32[4,1,1,1,2,2,16,128]{7,6,5,4,3,2,0,1:T(8,128)S(1)} %constant_dynamic-slice_fusion.8), channel_id=1, source_target_pairs={{0,4},{4,0},{8,12},{12,8},{16,20},{20,16},{24,28},{28,24},{1,5},{5... | collective-permute-start | bytes 393224 | tf_op jit(solution)/shard_map/ppermute | solution.py:93
  53.8 1.5 %collective-permute-start.9 = (f32[4,1,2,1,1,2,16,128]{7,6,5,4,3,2,0,1:T(8,128)S(1)}, f32[4,1,2,1,1,2,16,128]{7,6,5,4,3,2,0,1:T(8,128)S(1)}, u32[]{:S(2)}, u32[]{:S(2)}) collective-permute-start(f32[4,1,2,1,1,2,16,128]{7,6,5,4,3,2,0,1:T(8,128)S(1)} %constant_dynamic-slice_fusion.5), channel_id=1, source_target_pairs={{0,8},{4,12},{8,0},{12,4},{16,24},{20,28},{24,16},{28,20},{1,9},{5... | collective-permute-start | bytes 393224 | tf_op jit(solution)/shard_map/ppermute | solution.py:93
  55.3 2.5 %collective-permute-start.12 = (f32[4,1,2,2,1,1,16,128]{7,6,5,4,3,2,0,1:T(8,128)S(1)}, f32[4,1,2,2,1,1,16,128]{7,6,5,4,3,2,0,1:T(8,128)S(1)}, u32[]{:S(2)}, u32[]{:S(2)}) collective-permute-start(f32[4,1,2,2,1,1,16,128]{7,6,5,4,3,2,0,1:T(8,128)S(1)} %constant_dynamic-slice_fusion.2), channel_id=1, source_target_pairs={{0,16},{4,20},{8,24},{12,28},{16,0},{20,4},{24,8},{28,12},{1,17},{... | collective-permute-start | bytes 393224 | tf_op jit(solution)/shard_map/ppermute | solution.py:93
  57.9 1.3 %collective-permute-start.7 = (f32[4,1,1,1,1,2,16,128]{7,6,5,4,3,2,0,1:T(8,128)S(1)}, f32[4,1,1,1,1,2,16,128]{7,6,5,4,3,2,0,1:T(8,128)S(1)}, u32[]{:S(2)}, u32[]{:S(2)}) collective-permute-start(f32[4,1,1,1,1,2,16,128]{7,6,5,4,3,2,0,1:T(8,128)S(1)} %constant_dynamic-slice_fusion.7), channel_id=1, source_target_pairs={{0,8},{4,12},{8,0},{12,4},{16,24},{20,28},{24,16},{28,20},{1,9},{5... | collective-permute-start | bytes 196616 | tf_op jit(solution)/shard_map/ppermute | solution.py:93
  59.2 3.8 %collective-permute-done.9 = f32[4,1,2,1,1,2,16,128]{7,6,5,4,3,2,0,1:T(8,128)S(1)} collective-permute-done((f32[4,1,2,1,1,2,16,128]{7,6,5,4,3,2,0,1:T(8,128)S(1)}, f32[4,1,2,1,1,2,16,128]{7,6,5,4,3,2,0,1:T(8,128)S(1)}, u32[]{:S(2)}, u32[]{:S(2)}) %collective-permute-start.9) | collective-permute-done | bytes 131104 | tf_op jit(solution)/shard_map/ppermute | solution.py:93
  64.4 3.0 %collective-permute-start.8 = (f32[4,1,1,1,1,1,16,128]{7,6,5,4,3,2,0,1:T(8,128)S(1)}, f32[4,1,1,1,1,1,16,128]{7,6,5,4,3,2,0,1:T(8,128)S(1)}, u32[]{:S(2)}, u32[]{:S(2)}) collective-permute-start(f32[4,1,1,1,1,1,16,128]{7,6,5,4,3,2,0,1:T(8,128)S(1)} %constant_dynamic-slice_fusion.6), channel_id=1, source_target_pairs={{0,16},{4,20},{8,24},{12,28},{16,0},{20,4},{24,8},{28,12},{1,17},{... | collective-permute-start | bytes 98312 | tf_op jit(solution)/shard_map/ppermute | solution.py:93
  67.4 1.6 %collective-permute-done.10 = f32[4,1,2,1,1,1,16,128]{7,6,5,4,3,2,0,1:T(8,128)S(1)} collective-permute-done((f32[4,1,2,1,1,1,16,128]{7,6,5,4,3,2,0,1:T(8,128)S(1)}, f32[4,1,2,1,1,1,16,128]{7,6,5,4,3,2,0,1:T(8,128)S(1)}, u32[]{:S(2)}, u32[]{:S(2)}) %collective-permute-start.10) | collective-permute-done | bytes 65568 | tf_op jit(solution)/shard_map/ppermute | solution.py:93
  69.0 1.2 %collective-permute-start.11 = (f32[4,1,1,1,1,1,16,128]{7,6,5,4,3,2,0,1:T(8,128)S(1)}, f32[4,1,1,1,1,1,16,128]{7,6,5,4,3,2,0,1:T(8,128)S(1)}, u32[]{:S(2)}, u32[]{:S(2)}) collective-permute-start(f32[4,1,1,1,1,1,16,128]{7,6,5,4,3,2,0,1:T(8,128)S(1)} %constant_dynamic-slice_fusion.3), channel_id=1, source_target_pairs={{0,2},{1,3},{2,0},{3,1},{4,6},{5,7},{6,4},{7,5},{8,10},{9,11},{10,... | collective-permute-start | bytes 98312 | tf_op jit(solution)/shard_map/ppermute | solution.py:93
  70.4 2.6 %collective-permute-done.11 = f32[4,1,1,1,1,1,16,128]{7,6,5,4,3,2,0,1:T(8,128)S(1)} collective-permute-done((f32[4,1,1,1,1,1,16,128]{7,6,5,4,3,2,0,1:T(8,128)S(1)}, f32[4,1,1,1,1,1,16,128]{7,6,5,4,3,2,0,1:T(8,128)S(1)}, u32[]{:S(2)}, u32[]{:S(2)}) %collective-permute-start.11) | collective-permute-done | bytes 32800 | tf_op jit(solution)/shard_map/ppermute | solution.py:93
  73.0 1.3 %collective-permute-done.14 = f32[4,1,1,1,1,1,16,128]{7,6,5,4,3,2,0,1:T(8,128)S(1)} collective-permute-done((f32[4,1,1,1,1,1,16,128]{7,6,5,4,3,2,0,1:T(8,128)S(1)}, f32[4,1,1,1,1,1,16,128]{7,6,5,4,3,2,0,1:T(8,128)S(1)}, u32[]{:S(2)}, u32[]{:S(2)}) %collective-permute-start.14) | collective-permute-done | bytes 32800 | tf_op jit(solution)/shard_map/ppermute | solution.py:93
  76.3 1.8 %fusion.13 = bf16[12,16,128]{2,1,0:T(8,128)(2,1)S(1)} fusion(bf16[12,4,136,128]{3,2,1,0:T(8,128)(2,1)} %all-gather.2.cloned.1.call-done, bf16[12,4,16,128]{3,2,1,0:T(8,128)(2,1)S(1)} %bitcast.97, pred[12,4]{1,0:T(8,128)(4,1)S(1)} %copy.62), kind=kOutput, calls=%fused_computation.15 | convolution fusion | flops 25288704 | bytes 1818672 | tf_op jit(solution)/shard_map/nerc,necd->nrd/dot_general | solution.py:144
  78.3 1.5 %collective-permute-start.19 = (bf16[4,1,1,1,1,1,16,128]{7,6,0,5,4,3,2,1:T(8,128)(2,1)S(1)}, bf16[4,1,1,1,1,1,16,128]{7,6,0,5,4,3,2,1:T(8,128)(2,1)S(1)}, u32[]{:S(2)}, u32[]{:S(2)}) collective-permute-start(bf16[4,1,1,1,1,1,16,128]{7,6,0,5,4,3,2,1:T(8,128)(2,1)S(1)} %get-tuple-element.31), channel_id=1, source_target_pairs={{0,2},{1,3},{2,0},{3,1},{4,6},{5,7},{6,4},{7,5},{8,10},{9,11},{10,... | collective-permute-start | bytes 49160 | tf_op jit(solution)/shard_map/ppermute | solution.py:98
  79.8 3.1 %collective-permute-done.15 = bf16[4,1,1,1,1,1,16,128]{7,6,0,5,4,3,2,1:T(8,128)(2,1)S(1)} collective-permute-done((bf16[4,1,1,1,1,1,16,128]{7,6,0,5,4,3,2,1:T(8,128)(2,1)S(1)}, bf16[4,1,1,1,1,1,16,128]{7,6,0,5,4,3,2,1:T(8,128)(2,1)S(1)}, u32[]{:S(2)}, u32[]{:S(2)}) %collective-permute-start.15) | collective-permute-done | bytes 16416 | tf_op jit(solution)/shard_map/ppermute | solution.py:98
  83.5 2.3 %collective-permute-start.20 = (bf16[4,1,2,1,1,1,16,128]{7,6,0,5,4,3,2,1:T(8,128)(2,1)S(1)}, bf16[4,1,2,1,1,1,16,128]{7,6,0,5,4,3,2,1:T(8,128)(2,1)S(1)}, u32[]{:S(2)}, u32[]{:S(2)}) collective-permute-start(bf16[4,1,2,1,1,1,16,128]{7,6,0,5,4,3,2,1:T(8,128)(2,1)S(1)} %maximum_select_fusion.16), channel_id=1, source_target_pairs={{0,16},{4,20},{8,24},{12,28},{16,0},{20,4},{24,8},{28,12},{1,17},{... | collective-permute-start | bytes 98312 | tf_op jit(solution)/shard_map/ppermute | solution.py:98
  88.2 1.7 %collective-permute-done.20 = bf16[4,1,2,1,1,1,16,128]{7,6,0,5,4,3,2,1:T(8,128)(2,1)S(1)} collective-permute-done((bf16[4,1,2,1,1,1,16,128]{7,6,0,5,4,3,2,1:T(8,128)(2,1)S(1)}, bf16[4,1,2,1,1,1,16,128]{7,6,0,5,4,3,2,1:T(8,128)(2,1)S(1)}, u32[]{:S(2)}, u32[]{:S(2)}) %collective-permute-start.20) | collective-permute-done | bytes 32800 | tf_op jit(solution)/shard_map/ppermute | solution.py:98
  90.1 1.9 %collective-permute-start.25 = (bf16[4,1,2,2,1,1,16,128]{7,6,0,5,4,3,2,1:T(8,128)(2,1)S(1)}, bf16[4,1,2,2,1,1,16,128]{7,6,0,5,4,3,2,1:T(8,128)(2,1)S(1)}, u32[]{:S(2)}, u32[]{:S(2)}) collective-permute-start(bf16[4,1,2,2,1,1,16,128]{7,6,0,5,4,3,2,1:T(8,128)(2,1)S(1)} %fusion.29), channel_id=1, source_target_pairs={{0,16},{4,20},{8,24},{12,28},{16,0},{20,4},{24,8},{28,12},{1,17},{... | collective-permute-start | bytes 196616 | tf_op jit(solution)/shard_map/ppermute | solution.py:98
  93.1 2.4 %collective-permute-done.21 = bf16[4,1,2,1,1,2,16,128]{7,6,0,5,4,3,2,1:T(8,128)(2,1)S(1)} collective-permute-done((bf16[4,1,2,1,1,2,16,128]{7,6,0,5,4,3,2,1:T(8,128)(2,1)S(1)}, bf16[4,1,2,1,1,2,16,128]{7,6,0,5,4,3,2,1:T(8,128)(2,1)S(1)}, u32[]{:S(2)}, u32[]{:S(2)}) %collective-permute-start.21) | collective-permute-done | bytes 65568 | tf_op jit(solution)/shard_map/ppermute | solution.py:98
  95.9 1.4 %collective-permute-start.26 = (bf16[4,1,2,2,1,2,16,128]{7,6,0,5,4,3,2,1:T(8,128)(2,1)S(1)}, bf16[4,1,2,2,1,2,16,128]{7,6,0,5,4,3,2,1:T(8,128)(2,1)S(1)}, u32[]{:S(2)}, u32[]{:S(2)}) collective-permute-start(bf16[4,1,2,2,1,2,16,128]{7,6,0,5,4,3,2,1:T(8,128)(2,1)S(1)} %maximum_select_fusion.7), channel_id=1, source_target_pairs={{0,8},{4,12},{8,0},{12,4},{16,24},{20,28},{24,16},{28,20},{1,9},{5... | collective-permute-start | bytes 393224 | tf_op jit(solution)/shard_map/ppermute | solution.py:98
  97.3 3.1 %collective-permute-done.22 = bf16[4,1,2,1,2,2,16,128]{7,6,0,5,4,3,2,1:T(8,128)(2,1)S(1)} collective-permute-done((bf16[4,1,2,1,2,2,16,128]{7,6,0,5,4,3,2,1:T(8,128)(2,1)S(1)}, bf16[4,1,2,1,2,2,16,128]{7,6,0,5,4,3,2,1:T(8,128)(2,1)S(1)}, u32[]{:S(2)}, u32[]{:S(2)}) %collective-permute-start.22) | collective-permute-done | bytes 131104 | tf_op jit(solution)/shard_map/ppermute | solution.py:98
  102.1 1.4 %collective-permute-done.27 = bf16[12,256,128]{2,1,0:T(8,128)(2,1)} collective-permute-done((bf16[12,256,128]{2,1,0:T(8,128)(2,1)S(1)}, bf16[12,256,128]{2,1,0:T(8,128)(2,1)}, u32[]{:S(2)}, u32[]{:S(2)}) %collective-permute-start.27) | collective-permute-done | bytes 786464 | tf_op jit(solution)/shard_map/ppermute | solution.py:152
  103.5 1.8 %gather_fusion.3 = bf16[8,256,128]{2,1,0:T(8,128)(2,1)S(1)} fusion(bf16[12,256,128]{2,1,0:T(8,128)(2,1)} %collective-permute-done.27, s32[1024]{0:T(1024)S(1)} %pad_clamp_fusion), kind=kCustom, calls=%fused_computation.1.clone | custom fusion | bytes 1048608 | tf_op jit(solution)/shard_map/jit(_take)/gather | solution.py:154
  (133 shorter events, 21.9 us)
Async XLA Ops:
  6.5 37.5 %copy-start = (bf16[4,4,256,256]{3,2,1,0:T(8,128)(2,1)S(1)}, bf16[4,4,256,256]{3,2,1,0:T(8,128)(2,1)}, u32[]{:S(2)}) copy-start(bf16[4,4,256,256]{3,2,1,0:T(8,128)(2,1)} %param.11) | copy-start | bytes 6291460
  6.5 19.2 %copy-start.1 = (bf16[4,512,256]{2,1,0:T(8,128)(2,1)S(1)}, bf16[4,512,256]{2,1,0:T(8,128)(2,1)}, u32[]{:S(2)}) copy-start(bf16[4,512,256]{2,1,0:T(8,128)(2,1)} %residual_ref.1) | copy-start | bytes 3145732
  6.5 16.3 %copy-start.8 = (s32[4,4]{1,0:T(4,128)S(1)}, s32[4,4]{1,0:T(4,128)}, u32[]{:S(2)}) copy-start(s32[4,4]{1,0:T(4,128)} %param.10) | copy-start | bytes 196
  6.5 67.7 %all-gather.2.cloned.1.call-start = ((), (), s32[]{:S(2)}) async-start(), calls=%async_computation | async-start | bytes 2088960 | tf_op jit(solution)/shard_map/all_gather | solution.py:114
  15.6 12.5 %collective-permute-start.2 = (f32[12,256,128]{2,1,0:T(8,128)}, f32[12,256,128]{2,1,0:T(8,128)}, u32[]{:S(2)}, u32[]{:S(2)}) collective-permute-start(f32[12,256,128]{2,1,0:T(8,128)} %get-tuple-element.16), channel_id=1, source_target_pairs={{0,1},{1,0},{2,3},{3,2},{4,5},{5,4},{6,7},{7,6},{8,9},{9,8},{10,11... | collective-permute-start | bytes 4718600 | tf_op jit(solution)/shard_map/ppermute | solution.py:131
  17.9 5.1 %collective-permute-start = (bf16[1,512,256]{2,1,0:T(8,128)(2,1)}, bf16[1,512,256]{2,1,0:T(8,128)(2,1)}, u32[]{:S(2)}, u32[]{:S(2)}) collective-permute-start(bf16[1,512,256]{2,1,0:T(8,128)(2,1)} %get-tuple-element.27), channel_id=1, source_target_pairs={{0,1},{1,2},{2,3},{3,4},{4,5},{5,6},{6,7},{7,8},{8,9},{9,10},{10,1... | collective-permute-start | bytes 786440 | tf_op jit(solution)/shard_map/ppermute | solution.py:60
  20.6 5.2 %collective-permute-start.1 = (bf16[1,512,256]{2,1,0:T(8,128)(2,1)}, bf16[1,512,256]{2,1,0:T(8,128)(2,1)}, u32[]{:S(2)}, u32[]{:S(2)}) collective-permute-start(bf16[1,512,256]{2,1,0:T(8,128)(2,1)} %get-tuple-element.28), channel_id=1, source_target_pairs={{1,0},{2,1},{3,2},{4,3},{5,4},{6,5},{7,6},{8,7},{9,8},{10,9},{11,1... | collective-permute-start | bytes 786440 | tf_op jit(solution)/shard_map/ppermute | solution.py:62
  31.4 17.5 %collective-permute-start.5 = (f32[4,1,2,2,1,2,16,128]{7,6,5,4,3,2,0,1:T(8,128)}, f32[4,1,2,2,1,2,16,128]{7,6,5,4,3,2,0,1:T(8,128)}, u32[]{:S(2)}, u32[]{:S(2)}) collective-permute-start(f32[4,1,2,2,1,2,16,128]{7,6,5,4,3,2,0,1:T(8,128)} %constant_dynamic-slice_fusion.9), channel_id=1, source_target_pairs={{0,8},{4,12},{8,0},{12,4},{16,24},{20,28},{24,16},{28,20},{1,9},{5... | collective-permute-start | bytes 786440 | tf_op jit(solution)/shard_map/ppermute | solution.py:93
  38.6 11.3 %collective-permute-start.4 = (f32[4,1,2,1,2,2,16,128]{7,6,5,4,3,2,0,1:T(8,128)}, f32[4,1,2,1,2,2,16,128]{7,6,5,4,3,2,0,1:T(8,128)}, u32[]{:S(2)}, u32[]{:S(2)}) collective-permute-start(f32[4,1,2,1,2,2,16,128]{7,6,5,4,3,2,0,1:T(8,128)} %constant_dynamic-slice_fusion.10), channel_id=1, source_target_pairs={{0,4},{4,0},{8,12},{12,8},{16,20},{20,16},{24,28},{28,24},{1,5},{5... | collective-permute-start | bytes 786440 | tf_op jit(solution)/shard_map/ppermute | solution.py:93
  39.2 11.8 %collective-permute-start.3 = (f32[4,1,1,2,2,2,16,128]{7,6,5,4,3,2,0,1:T(8,128)S(1)}, f32[4,1,1,2,2,2,16,128]{7,6,5,4,3,2,0,1:T(8,128)}, u32[]{:S(2)}, u32[]{:S(2)}) collective-permute-start(f32[4,1,1,2,2,2,16,128]{7,6,5,4,3,2,0,1:T(8,128)S(1)} %constant_dynamic-slice_fusion.11), channel_id=1, source_target_pairs={{0,2},{1,3},{2,0},{3,1},{4,6},{5,7},{6,4},{7,5},{8,10},{9,11},{10,... | collective-permute-start | bytes 786440 | tf_op jit(solution)/shard_map/ppermute | solution.py:93
  52.0 5.9 %collective-permute-start.6 = (f32[4,1,1,1,2,2,16,128]{7,6,5,4,3,2,0,1:T(8,128)S(1)}, f32[4,1,1,1,2,2,16,128]{7,6,5,4,3,2,0,1:T(8,128)S(1)}, u32[]{:S(2)}, u32[]{:S(2)}) collective-permute-start(f32[4,1,1,1,2,2,16,128]{7,6,5,4,3,2,0,1:T(8,128)S(1)} %constant_dynamic-slice_fusion.8), channel_id=1, source_target_pairs={{0,4},{4,0},{8,12},{12,8},{16,20},{20,16},{24,28},{28,24},{1,5},{5... | collective-permute-start | bytes 393224 | tf_op jit(solution)/shard_map/ppermute | solution.py:93
  53.8 9.2 %collective-permute-start.9 = (f32[4,1,2,1,1,2,16,128]{7,6,5,4,3,2,0,1:T(8,128)S(1)}, f32[4,1,2,1,1,2,16,128]{7,6,5,4,3,2,0,1:T(8,128)S(1)}, u32[]{:S(2)}, u32[]{:S(2)}) collective-permute-start(f32[4,1,2,1,1,2,16,128]{7,6,5,4,3,2,0,1:T(8,128)S(1)} %constant_dynamic-slice_fusion.5), channel_id=1, source_target_pairs={{0,8},{4,12},{8,0},{12,4},{16,24},{20,28},{24,16},{28,20},{1,9},{5... | collective-permute-start | bytes 393224 | tf_op jit(solution)/shard_map/ppermute | solution.py:93
  55.3 7.8 %collective-permute-start.12 = (f32[4,1,2,2,1,1,16,128]{7,6,5,4,3,2,0,1:T(8,128)S(1)}, f32[4,1,2,2,1,1,16,128]{7,6,5,4,3,2,0,1:T(8,128)S(1)}, u32[]{:S(2)}, u32[]{:S(2)}) collective-permute-start(f32[4,1,2,2,1,1,16,128]{7,6,5,4,3,2,0,1:T(8,128)S(1)} %constant_dynamic-slice_fusion.2), channel_id=1, source_target_pairs={{0,16},{4,20},{8,24},{12,28},{16,0},{20,4},{24,8},{28,12},{1,17},{... | collective-permute-start | bytes 393224 | tf_op jit(solution)/shard_map/ppermute | solution.py:93
  57.9 6.5 %collective-permute-start.7 = (f32[4,1,1,1,1,2,16,128]{7,6,5,4,3,2,0,1:T(8,128)S(1)}, f32[4,1,1,1,1,2,16,128]{7,6,5,4,3,2,0,1:T(8,128)S(1)}, u32[]{:S(2)}, u32[]{:S(2)}) collective-permute-start(f32[4,1,1,1,1,2,16,128]{7,6,5,4,3,2,0,1:T(8,128)S(1)} %constant_dynamic-slice_fusion.7), channel_id=1, source_target_pairs={{0,8},{4,12},{8,0},{12,4},{16,24},{20,28},{24,16},{28,20},{1,9},{5... | collective-permute-start | bytes 196616 | tf_op jit(solution)/shard_map/ppermute | solution.py:93
  63.0 5.9 %collective-permute-start.10 = (f32[4,1,2,1,1,1,16,128]{7,6,5,4,3,2,0,1:T(8,128)S(1)}, f32[4,1,2,1,1,1,16,128]{7,6,5,4,3,2,0,1:T(8,128)S(1)}, u32[]{:S(2)}, u32[]{:S(2)}) collective-permute-start(f32[4,1,2,1,1,1,16,128]{7,6,5,4,3,2,0,1:T(8,128)S(1)} %constant_dynamic-slice_fusion.4), channel_id=1, source_target_pairs={{0,16},{4,20},{8,24},{12,28},{16,0},{20,4},{24,8},{28,12},{1,17},{... | collective-permute-start | bytes 196616 | tf_op jit(solution)/shard_map/ppermute | solution.py:93
  63.2 7.1 %collective-permute-start.13 = (f32[4,1,1,2,1,1,16,128]{7,6,5,4,3,2,0,1:T(8,128)S(1)}, f32[4,1,1,2,1,1,16,128]{7,6,5,4,3,2,0,1:T(8,128)S(1)}, u32[]{:S(2)}, u32[]{:S(2)}) collective-permute-start(f32[4,1,1,2,1,1,16,128]{7,6,5,4,3,2,0,1:T(8,128)S(1)} %constant_dynamic-slice_fusion.1), channel_id=1, source_target_pairs={{0,2},{1,3},{2,0},{3,1},{4,6},{5,7},{6,4},{7,5},{8,10},{9,11},{10,... | collective-permute-start | bytes 196616 | tf_op jit(solution)/shard_map/ppermute | solution.py:93
  64.4 5.9 %collective-permute-start.8 = (f32[4,1,1,1,1,1,16,128]{7,6,5,4,3,2,0,1:T(8,128)S(1)}, f32[4,1,1,1,1,1,16,128]{7,6,5,4,3,2,0,1:T(8,128)S(1)}, u32[]{:S(2)}, u32[]{:S(2)}) collective-permute-start(f32[4,1,1,1,1,1,16,128]{7,6,5,4,3,2,0,1:T(8,128)S(1)} %constant_dynamic-slice_fusion.6), channel_id=1, source_target_pairs={{0,16},{4,20},{8,24},{12,28},{16,0},{20,4},{24,8},{28,12},{1,17},{... | collective-permute-start | bytes 98312 | tf_op jit(solution)/shard_map/ppermute | solution.py:93
  69.0 4.0 %collective-permute-start.11 = (f32[4,1,1,1,1,1,16,128]{7,6,5,4,3,2,0,1:T(8,128)S(1)}, f32[4,1,1,1,1,1,16,128]{7,6,5,4,3,2,0,1:T(8,128)S(1)}, u32[]{:S(2)}, u32[]{:S(2)}) collective-permute-start(f32[4,1,1,1,1,1,16,128]{7,6,5,4,3,2,0,1:T(8,128)S(1)} %constant_dynamic-slice_fusion.3), channel_id=1, source_target_pairs={{0,2},{1,3},{2,0},{3,1},{4,6},{5,7},{6,4},{7,5},{8,10},{9,11},{10,... | collective-permute-start | bytes 98312 | tf_op jit(solution)/shard_map/ppermute | solution.py:93
  70.3 4.0 %collective-permute-start.14 = (f32[4,1,1,1,1,1,16,128]{7,6,5,4,3,2,0,1:T(8,128)S(1)}, f32[4,1,1,1,1,1,16,128]{7,6,5,4,3,2,0,1:T(8,128)S(1)}, u32[]{:S(2)}, u32[]{:S(2)}) collective-permute-start(f32[4,1,1,1,1,1,16,128]{7,6,5,4,3,2,0,1:T(8,128)S(1)} %constant_dynamic-slice_fusion), channel_id=1, source_target_pairs={{0,4},{4,0},{8,12},{12,8},{16,20},{20,16},{24,28},{28,24},{1,5},{5... | collective-permute-start | bytes 98312 | tf_op jit(solution)/shard_map/ppermute | solution.py:93
  78.1 4.9 %collective-permute-start.15 = (bf16[4,1,1,1,1,1,16,128]{7,6,0,5,4,3,2,1:T(8,128)(2,1)S(1)}, bf16[4,1,1,1,1,1,16,128]{7,6,0,5,4,3,2,1:T(8,128)(2,1)S(1)}, u32[]{:S(2)}, u32[]{:S(2)}) collective-permute-start(bf16[4,1,1,1,1,1,16,128]{7,6,0,5,4,3,2,1:T(8,128)(2,1)S(1)} %get-tuple-element.30), channel_id=1, source_target_pairs={{0,16},{4,20},{8,24},{12,28},{16,0},{20,4},{24,8},{28,12},{1,17},{... | collective-permute-start | bytes 49160 | tf_op jit(solution)/shard_map/ppermute | solution.py:98
  78.3 5.2 %collective-permute-start.19 = (bf16[4,1,1,1,1,1,16,128]{7,6,0,5,4,3,2,1:T(8,128)(2,1)S(1)}, bf16[4,1,1,1,1,1,16,128]{7,6,0,5,4,3,2,1:T(8,128)(2,1)S(1)}, u32[]{:S(2)}, u32[]{:S(2)}) collective-permute-start(bf16[4,1,1,1,1,1,16,128]{7,6,0,5,4,3,2,1:T(8,128)(2,1)S(1)} %get-tuple-element.31), channel_id=1, source_target_pairs={{0,2},{1,3},{2,0},{3,1},{4,6},{5,7},{6,4},{7,5},{8,10},{9,11},{10,... | collective-permute-start | bytes 49160 | tf_op jit(solution)/shard_map/ppermute | solution.py:98
  79.8 6.1 %collective-permute-start.23 = (bf16[4,1,1,1,1,1,16,128]{7,6,0,5,4,3,2,1:T(8,128)(2,1)S(1)}, bf16[4,1,1,1,1,1,16,128]{7,6,0,5,4,3,2,1:T(8,128)(2,1)S(1)}, u32[]{:S(2)}, u32[]{:S(2)}) collective-permute-start(bf16[4,1,1,1,1,1,16,128]{7,6,0,5,4,3,2,1:T(8,128)(2,1)S(1)} %get-tuple-element.32), channel_id=1, source_target_pairs={{0,4},{4,0},{8,12},{12,8},{16,20},{20,16},{24,28},{28,24},{1,5},{5... | collective-permute-start | bytes 49160 | tf_op jit(solution)/shard_map/ppermute | solution.py:98
  83.0 4.2 %collective-permute-start.16 = (bf16[4,1,1,1,1,2,16,128]{7,6,0,5,4,3,2,1:T(8,128)(2,1)S(1)}, bf16[4,1,1,1,1,2,16,128]{7,6,0,5,4,3,2,1:T(8,128)(2,1)S(1)}, u32[]{:S(2)}, u32[]{:S(2)}) collective-permute-start(bf16[4,1,1,1,1,2,16,128]{7,6,0,5,4,3,2,1:T(8,128)(2,1)S(1)} %maximum_select_fusion.14), channel_id=1, source_target_pairs={{0,8},{4,12},{8,0},{12,4},{16,24},{20,28},{24,16},{28,20},{1,9},{5... | collective-permute-start | bytes 98312 | tf_op jit(solution)/shard_map/ppermute | solution.py:98
  83.5 6.3 %collective-permute-start.20 = (bf16[4,1,2,1,1,1,16,128]{7,6,0,5,4,3,2,1:T(8,128)(2,1)S(1)}, bf16[4,1,2,1,1,1,16,128]{7,6,0,5,4,3,2,1:T(8,128)(2,1)S(1)}, u32[]{:S(2)}, u32[]{:S(2)}) collective-permute-start(bf16[4,1,2,1,1,1,16,128]{7,6,0,5,4,3,2,1:T(8,128)(2,1)S(1)} %maximum_select_fusion.16), channel_id=1, source_target_pairs={{0,16},{4,20},{8,24},{12,28},{16,0},{20,4},{24,8},{28,12},{1,17},{... | collective-permute-start | bytes 98312 | tf_op jit(solution)/shard_map/ppermute | solution.py:98
  85.9 4.1 %collective-permute-start.24 = (bf16[4,1,1,2,1,1,16,128]{7,6,0,5,4,3,2,1:T(8,128)(2,1)S(1)}, bf16[4,1,1,2,1,1,16,128]{7,6,0,5,4,3,2,1:T(8,128)(2,1)S(1)}, u32[]{:S(2)}, u32[]{:S(2)}) collective-permute-start(bf16[4,1,1,2,1,1,16,128]{7,6,0,5,4,3,2,1:T(8,128)(2,1)S(1)} %maximum_select_fusion.18), channel_id=1, source_target_pairs={{0,2},{1,3},{2,0},{3,1},{4,6},{5,7},{6,4},{7,5},{8,10},{9,11},{10,... | collective-permute-start | bytes 98312 | tf_op jit(solution)/shard_map/ppermute | solution.py:98
  87.2 4.9 %collective-permute-start.17 = (bf16[4,1,1,1,2,2,16,128]{7,6,0,5,4,3,2,1:T(8,128)(2,1)S(1)}, bf16[4,1,1,1,2,2,16,128]{7,6,0,5,4,3,2,1:T(8,128)(2,1)S(1)}, u32[]{:S(2)}, u32[]{:S(2)}) collective-permute-start(bf16[4,1,1,1,2,2,16,128]{7,6,0,5,4,3,2,1:T(8,128)(2,1)S(1)} %maximum_select_fusion.9), channel_id=1, source_target_pairs={{0,4},{4,0},{8,12},{12,8},{16,20},{20,16},{24,28},{28,24},{1,5},{5... | collective-permute-start | bytes 196616 | tf_op jit(solution)/shard_map/ppermute | solution.py:98
  89.8 5.6 %collective-permute-start.21 = (bf16[4,1,2,1,1,2,16,128]{7,6,0,5,4,3,2,1:T(8,128)(2,1)S(1)}, bf16[4,1,2,1,1,2,16,128]{7,6,0,5,4,3,2,1:T(8,128)(2,1)S(1)}, u32[]{:S(2)}, u32[]{:S(2)}) collective-permute-start(bf16[4,1,2,1,1,2,16,128]{7,6,0,5,4,3,2,1:T(8,128)(2,1)S(1)} %maximum_select_fusion.11), channel_id=1, source_target_pairs={{0,8},{4,12},{8,0},{12,4},{16,24},{20,28},{24,16},{28,20},{1,9},{5... | collective-permute-start | bytes 196616 | tf_op jit(solution)/shard_map/ppermute | solution.py:98
  90.1 5.8 %collective-permute-start.25 = (bf16[4,1,2,2,1,1,16,128]{7,6,0,5,4,3,2,1:T(8,128)(2,1)S(1)}, bf16[4,1,2,2,1,1,16,128]{7,6,0,5,4,3,2,1:T(8,128)(2,1)S(1)}, u32[]{:S(2)}, u32[]{:S(2)}) collective-permute-start(bf16[4,1,2,2,1,1,16,128]{7,6,0,5,4,3,2,1:T(8,128)(2,1)S(1)} %fusion.29), channel_id=1, source_target_pairs={{0,16},{4,20},{8,24},{12,28},{16,0},{20,4},{24,8},{28,12},{1,17},{... | collective-permute-start | bytes 196616 | tf_op jit(solution)/shard_map/ppermute | solution.py:98
  92.1 5.2 %collective-permute-start.18 = (bf16[4,1,1,2,2,2,16,128]{7,6,0,5,4,3,2,1:T(8,128)(2,1)S(1)}, bf16[4,1,1,2,2,2,16,128]{7,6,0,5,4,3,2,1:T(8,128)(2,1)S(1)}, u32[]{:S(2)}, u32[]{:S(2)}) collective-permute-start(bf16[4,1,1,2,2,2,16,128]{7,6,0,5,4,3,2,1:T(8,128)(2,1)S(1)} %maximum_select_fusion.5), channel_id=1, source_target_pairs={{0,2},{1,3},{2,0},{3,1},{4,6},{5,7},{6,4},{7,5},{8,10},{9,11},{10,... | collective-permute-start | bytes 393224 | tf_op jit(solution)/shard_map/ppermute | solution.py:98
  95.4 5.0 %collective-permute-start.22 = (bf16[4,1,2,1,2,2,16,128]{7,6,0,5,4,3,2,1:T(8,128)(2,1)S(1)}, bf16[4,1,2,1,2,2,16,128]{7,6,0,5,4,3,2,1:T(8,128)(2,1)S(1)}, u32[]{:S(2)}, u32[]{:S(2)}) collective-permute-start(bf16[4,1,2,1,2,2,16,128]{7,6,0,5,4,3,2,1:T(8,128)(2,1)S(1)} %maximum_select_fusion.6), channel_id=1, source_target_pairs={{0,4},{4,0},{8,12},{12,8},{16,20},{20,16},{24,28},{28,24},{1,5},{5... | collective-permute-start | bytes 393224 | tf_op jit(solution)/shard_map/ppermute | solution.py:98
  95.9 5.0 %collective-permute-start.26 = (bf16[4,1,2,2,1,2,16,128]{7,6,0,5,4,3,2,1:T(8,128)(2,1)S(1)}, bf16[4,1,2,2,1,2,16,128]{7,6,0,5,4,3,2,1:T(8,128)(2,1)S(1)}, u32[]{:S(2)}, u32[]{:S(2)}) collective-permute-start(bf16[4,1,2,2,1,2,16,128]{7,6,0,5,4,3,2,1:T(8,128)(2,1)S(1)} %maximum_select_fusion.7), channel_id=1, source_target_pairs={{0,8},{4,12},{8,0},{12,4},{16,24},{20,28},{24,16},{28,20},{1,9},{5... | collective-permute-start | bytes 393224 | tf_op jit(solution)/shard_map/ppermute | solution.py:98
  101.0 2.5 %collective-permute-start.27 = (bf16[12,256,128]{2,1,0:T(8,128)(2,1)S(1)}, bf16[12,256,128]{2,1,0:T(8,128)(2,1)}, u32[]{:S(2)}, u32[]{:S(2)}) collective-permute-start(bf16[12,256,128]{2,1,0:T(8,128)(2,1)S(1)} %pad_maximum_fusion.1), channel_id=1, source_target_pairs={{0,1},{1,0},{2,3},{3,2},{4,5},{5,4},{6,7},{7,6},{8,9},{9,8},{10,11... | collective-permute-start | bytes 2359304 | tf_op jit(solution)/shard_map/ppermute | solution.py:152
  (8 other events, 48.1 us)
Sparse Core Ops, SparseCore 0:
  22.9 26.7 all-gather.1

commit v11 on v10

--- a/solution.py
+++ b/solution.py
@@ -8,45 +8,53 @@
 
 def restrict_kernel(links, half, residual_ref, basis_ref, keep_ref, send_ref):
     j = pl.program_id(0)
-    q = pl.program_id(1)
+    pairs_per = basis_ref.shape[1]
+    rows = keep_ref.shape[1]
 
-    @pl.when((j == 0) & (q == 0))
+    @pl.when(j == 0)
     def _():
         keep_ref[...] = jnp.zeros_like(keep_ref)
         send_ref[...] = jnp.zeros_like(send_ref)
 
-    n = links[j, q]
-    rows = keep_ref.shape[1]
-    mine = pl.multiple_of(half[0] * rows, rows)
-    other = pl.multiple_of((1 - half[0]) * rows, rows)
-    keep_ref[n] += jnp.dot(residual_ref[0, pl.ds(mine, rows), :], basis_ref[0, 0], preferred_element_type=jnp.float32)
-    send_ref[n] += jnp.dot(residual_ref[0, pl.ds(other, rows), :], basis_ref[0, 0], preferred_element_type=jnp.float32)
+    for q in range(pairs_per):
+        n = links[j * pairs_per + q]
+        term = jnp.dot(residual_ref[0], basis_ref[0, q], preferred_element_type=jnp.float32)
+
+        @pl.when(half[0] == 0)
+        def _():
+            keep_ref[n] += term[:rows]
+            send_ref[n] += term[rows:]
+
+        @pl.when(half[0] != 0)
+        def _():
+            keep_ref[n] += term[rows:]
+            send_ref[n] += term[:rows]
 
 
 def restrict(residual, basis, interface, total_blocks, half):
     count, rhs, size = residual.shape
     width = basis.shape[-1]
     rows = rhs // 2
-    block = pl.BlockSpec((total_blocks, rows, width), lambda j, q, links, half: (0, 0, 0))
+    block = pl.BlockSpec((total_blocks, rows, width), lambda j, links, half: (0, 0, 0))
     return pl.pallas_call(
         restrict_kernel,
         out_shape=[jax.ShapeDtypeStruct((total_blocks, rows, width), jnp.float32)] * 2,
         grid_spec=pltpu.PrefetchScalarGridSpec(
             num_scalar_prefetch=2,
-            grid=(count, interface.shape[1]),
+            grid=(count,),
             in_specs=[
-                pl.BlockSpec((1, rhs, size), lambda j, q, links, half: (j, 0, 0)),
-                pl.BlockSpec((1, 1, size, width), lambda j, q, links, half: (j, q, 0, 0)),
+                pl.BlockSpec((1, rhs, size), lambda j, links, half: (j, 0, 0)),
+                pl.BlockSpec((1, interface.shape[1], size, width), lambda j, links, half: (j, 0, 0, 0)),
             ],
             out_specs=[block, block],
         ),
-        compiler_params=pltpu.CompilerParams(dimension_semantics=("arbitrary", "arbitrary")),
+        compiler_params=pltpu.CompilerParams(dimension_semantics=("arbitrary",)),
         cost_estimate=pl.CostEstimate(
             flops=2 * count * interface.shape[1] * rhs * size * width,
             bytes_accessed=residual.size * 2 + basis.size * 2 + total_blocks * rhs * width * 4,
             transcendentals=0,
         ),
-    )(interface, half, residual, basis)
+    )(interface.reshape(-1), half, residual, basis)
 
 
 def with_halo(cells, sides, width):

time: 117 us -> 116 us (level)
  no operation moved by 1% of the time
where the time goes in v11:
time: 116 us; the launch traced here: 115 us
  starting transfers between devices  36.5 us (31%)
  waiting for transfers between devices  24.1 us (21%)
  local copies, waits for them, and re-layouts  17 us (15%)
  between operations  14 us (12%)
  other arithmetic  9.65 us (8%)
  matrix products  7.14 us (6%)
  Pallas kernels  6.44 us (6%)
    ppermute x12, starting transfers between devices, halve(): lax.ppermute(send.astype(wire), axis, pairs(axis, mask)).astype(x.dtype)  20.3 us
    ppermute x12, starting transfers between devices, double(): recv = lax.ppermute(y, axis, pairs(axis, mask))  11.7 us
    ppermute x12, waiting for transfers between devices, double(): recv = lax.ppermute(y, axis, pairs(axis, mask))  10.7 us
    ppermute x12, waiting for transfers between devices, halve(): lax.ppermute(send.astype(wire), axis, pairs(axis, mask)).astype(x.dtype)  9.28 us
    pallas_call x1, Pallas kernels, restrict(): pl.pallas_call(restrict_kernel, out_shape=[jax.ShapeDtypeStruct((total_bl...  6.44 us
    dot_general x1, matrix products, per_device(): jnp.einsum('jerb,jebc->jrc', picked, inverse_blocks, preferred_element_ty...  4.88 us
    gather x1, local copies, waits for them, and re-layouts, per_device(): picked = jnp.take(extended, margin, axis=0)  4.24 us
    unnamed x24, local copies, waits for them, and re-layouts  3.84 us
  transfers between devices with their start and end apart: 29, of which 11 were waited for; matrix products, arithmetic and copies ran while one was open for 19% of the time, Pallas kernels for 0%

profile of v11, /device:TPU:0, one launch (start us, length us, event | category | flops | bytes accessed | tf_op | source)
XLA Modules:
  0.0 115.0 jit_solution(4507883182208282153)
XLA Ops:
  8.1 6.4 %shard_map.73 = (f32[12,256,128]{2,1,0:T(8,128)}, f32[12,256,128]{2,1,0:T(8,128)}) custom-call(s32[8]{0:T(128)} %reshape.1691.links, s32[1]{0:T(128)} %bitcast.half, bf16[4,512,256]{2,1,0:T(8,128)(2,1)} %residual_ref.1, bf16[4,2,256,128]{3,2,1,0:T(8,128)(2,1)} %basis_ref.1), custom_call_target="tpu_custom_call" | custom-call | flops 268435456 | bytes 4718592 | tf_op jit(solution)/shard_map/pallas_call | solution.py:39
  15.0 1.9 %fusion.42 = (bf16[1,512,256]{2,1,0:T(8,128)(2,1)}, bf16[1,512,256]{2,1,0:T(8,128)(2,1)}) fusion(bf16[4,512,256]{2,1,0:T(8,128)(2,1)} %residual_ref.1), kind=kLoop, calls=%fused_computation.109 | loop fusion | bytes 1048576 | tf_op jit(solution)/shard_map/slice | solution.py:65
  16.9 2.7 %collective-permute-start = (bf16[1,512,256]{2,1,0:T(8,128)(2,1)}, bf16[1,512,256]{2,1,0:T(8,128)(2,1)}, u32[]{:S(2)}, u32[]{:S(2)}) collective-permute-start(bf16[1,512,256]{2,1,0:T(8,128)(2,1)} %get-tuple-element.27), channel_id=1, source_target_pairs={{0,1},{1,2},{2,3},{3,4},{4,5},{5,6},{6,7},{7,8},{8,9},{9,10},{10,1... | collective-permute-start | bytes 786440 | tf_op jit(solution)/shard_map/ppermute | solution.py:68
  19.5 1.3 %collective-permute-start.1 = (bf16[1,512,256]{2,1,0:T(8,128)(2,1)}, bf16[1,512,256]{2,1,0:T(8,128)(2,1)}, u32[]{:S(2)}, u32[]{:S(2)}) collective-permute-start(bf16[1,512,256]{2,1,0:T(8,128)(2,1)} %get-tuple-element.28), channel_id=1, source_target_pairs={{1,0},{2,1},{3,2},{4,3},{5,4},{6,5},{7,6},{8,7},{9,8},{10,9},{11,1... | collective-permute-start | bytes 786440 | tf_op jit(solution)/shard_map/ppermute | solution.py:70
  22.0 2.7 %collective-permute-done.1 = bf16[1,512,256]{2,1,0:T(8,128)(2,1)} collective-permute-done((bf16[1,512,256]{2,1,0:T(8,128)(2,1)}, bf16[1,512,256]{2,1,0:T(8,128)(2,1)}, u32[]{:S(2)}, u32[]{:S(2)}) %collective-permute-start.1) | collective-permute-done | bytes 262176 | tf_op jit(solution)/shard_map/ppermute | solution.py:70
  24.7 2.4 %pad_maximum_fusion = bf16[6,512,256]{2,1,0:T(8,128)(2,1)} fusion(bf16[1,512,256]{2,1,0:T(8,128)(2,1)} %collective-permute-done.1, bf16[4,512,256]{2,1,0:T(8,128)(2,1)S(1)} %copy-done.1, bf16[1,512,256]{2,1,0:T(8,128)(2,1)} %collective-permute-done), kind=kLoop, calls=%fused_computation.13 | loop fusion | flops 1572864 | bytes 3145728 | tf_op jit(solution)/shard_map/concatenate | solution.py:66
  27.1 1.6 %add.169 = f32[12,256,128]{2,1,0:T(8,128)S(1)} add(f32[12,256,128]{2,1,0:T(8,128)S(1)} %copy-done.5, f32[12,256,128]{2,1,0:T(8,128)} %collective-permute-done.2) | non-fusion elementwise | flops 393216 | bytes 4718592 | tf_op jit(solution)/shard_map/add | solution.py:139
  30.4 6.4 %collective-permute-start.5 = (f32[4,1,2,2,1,2,16,128]{7,6,5,4,3,2,0,1:T(8,128)}, f32[4,1,2,2,1,2,16,128]{7,6,5,4,3,2,0,1:T(8,128)}, u32[]{:S(2)}, u32[]{:S(2)}) collective-permute-start(f32[4,1,2,2,1,2,16,128]{7,6,5,4,3,2,0,1:T(8,128)} %constant_dynamic-slice_fusion.9), channel_id=1, source_target_pairs={{0,8},{4,12},{8,0},{12,4},{16,24},{20,28},{24,16},{28,20},{1,9},{5... | collective-permute-start | bytes 786440 | tf_op jit(solution)/shard_map/ppermute | solution.py:101
  38.7 4.2 %gather_fusion = bf16[16,512,256]{2,1,0:T(8,128)(2,1)} fusion(bf16[6,512,256]{2,1,0:T(8,128)(2,1)} %pad_maximum_fusion, s32[1024]{0:T(1024)S(1)} %pad_clamp_fusion.2), kind=kCustom, calls=%fused_computation.2 | custom fusion | bytes 8388672 | tf_op jit(solution)/shard_map/jit(_take)/gather | solution.py:143
  43.0 4.9 %fusion.5 = f32[4,512,256]{2,1,0:T(8,128)} fusion(bf16[4,4,256,256]{3,2,1,0:T(8,128)(2,1)S(1)} %copy-done, bf16[4,4,512,256]{3,2,1,0:T(8,128)(2,1)} %bitcast.87, pred[4,4]{1,0:T(4,128)(4,1)S(1)} %compare_and_fusion.2), kind=kOutput, calls=%fused_computation.10 | convolution fusion | flops 1075838976 | bytes 8388624 | tf_op jit(solution)/shard_map/jerb,jebc->jrc/dot_general | solution.py:144
  50.9 1.8 %collective-permute-start.6 = (f32[4,1,1,1,2,2,16,128]{7,6,5,4,3,2,0,1:T(8,128)S(1)}, f32[4,1,1,1,2,2,16,128]{7,6,5,4,3,2,0,1:T(8,128)S(1)}, u32[]{:S(2)}, u32[]{:S(2)}) collective-permute-start(f32[4,1,1,1,2,2,16,128]{7,6,5,4,3,2,0,1:T(8,128)S(1)} %constant_dynamic-slice_fusion.8), channel_id=1, source_target_pairs={{0,4},{4,0},{8,12},{12,8},{16,20},{20,16},{24,28},{28,24},{1,5},{5... | collective-permute-start | bytes 393224 | tf_op jit(solution)/shard_map/ppermute | solution.py:101
  52.8 1.5 %collective-permute-start.9 = (f32[4,1,2,1,1,2,16,128]{7,6,5,4,3,2,0,1:T(8,128)S(1)}, f32[4,1,2,1,1,2,16,128]{7,6,5,4,3,2,0,1:T(8,128)S(1)}, u32[]{:S(2)}, u32[]{:S(2)}) collective-permute-start(f32[4,1,2,1,1,2,16,128]{7,6,5,4,3,2,0,1:T(8,128)S(1)} %constant_dynamic-slice_fusion.5), channel_id=1, source_target_pairs={{0,8},{4,12},{8,0},{12,4},{16,24},{20,28},{24,16},{28,20},{1,9},{5... | collective-permute-start | bytes 393224 | tf_op jit(solution)/shard_map/ppermute | solution.py:101
  54.3 2.5 %collective-permute-start.12 = (f32[4,1,2,2,1,1,16,128]{7,6,5,4,3,2,0,1:T(8,128)S(1)}, f32[4,1,2,2,1,1,16,128]{7,6,5,4,3,2,0,1:T(8,128)S(1)}, u32[]{:S(2)}, u32[]{:S(2)}) collective-permute-start(f32[4,1,2,2,1,1,16,128]{7,6,5,4,3,2,0,1:T(8,128)S(1)} %constant_dynamic-slice_fusion.2), channel_id=1, source_target_pairs={{0,16},{4,20},{8,24},{12,28},{16,0},{20,4},{24,8},{28,12},{1,17},{... | collective-permute-start | bytes 393224 | tf_op jit(solution)/shard_map/ppermute | solution.py:101
  56.8 1.3 %collective-permute-start.7 = (f32[4,1,1,1,1,2,16,128]{7,6,5,4,3,2,0,1:T(8,128)S(1)}, f32[4,1,1,1,1,2,16,128]{7,6,5,4,3,2,0,1:T(8,128)S(1)}, u32[]{:S(2)}, u32[]{:S(2)}) collective-permute-start(f32[4,1,1,1,1,2,16,128]{7,6,5,4,3,2,0,1:T(8,128)S(1)} %constant_dynamic-slice_fusion.7), channel_id=1, source_target_pairs={{0,8},{4,12},{8,0},{12,4},{16,24},{20,28},{24,16},{28,20},{1,9},{5... | collective-permute-start | bytes 196616 | tf_op jit(solution)/shard_map/ppermute | solution.py:101
  58.1 3.8 %collective-permute-done.9 = f32[4,1,2,1,1,2,16,128]{7,6,5,4,3,2,0,1:T(8,128)S(1)} collective-permute-done((f32[4,1,2,1,1,2,16,128]{7,6,5,4,3,2,0,1:T(8,128)S(1)}, f32[4,1,2,1,1,2,16,128]{7,6,5,4,3,2,0,1:T(8,128)S(1)}, u32[]{:S(2)}, u32[]{:S(2)}) %collective-permute-start.9) | collective-permute-done | bytes 131104 | tf_op jit(solution)/shard_map/ppermute | solution.py:101
  62.1 1.2 %collective-permute-start.13 = (f32[4,1,1,2,1,1,16,128]{7,6,5,4,3,2,0,1:T(8,128)S(1)}, f32[4,1,1,2,1,1,16,128]{7,6,5,4,3,2,0,1:T(8,128)S(1)}, u32[]{:S(2)}, u32[]{:S(2)}) collective-permute-start(f32[4,1,1,2,1,1,16,128]{7,6,5,4,3,2,0,1:T(8,128)S(1)} %constant_dynamic-slice_fusion.1), channel_id=1, source_target_pairs={{0,2},{1,3},{2,0},{3,1},{4,6},{5,7},{6,4},{7,5},{8,10},{9,11},{10,... | collective-permute-start | bytes 196616 | tf_op jit(solution)/shard_map/ppermute | solution.py:101
  63.4 3.0 %collective-permute-start.8 = (f32[4,1,1,1,1,1,16,128]{7,6,5,4,3,2,0,1:T(8,128)S(1)}, f32[4,1,1,1,1,1,16,128]{7,6,5,4,3,2,0,1:T(8,128)S(1)}, u32[]{:S(2)}, u32[]{:S(2)}) collective-permute-start(f32[4,1,1,1,1,1,16,128]{7,6,5,4,3,2,0,1:T(8,128)S(1)} %constant_dynamic-slice_fusion.6), channel_id=1, source_target_pairs={{0,16},{4,20},{8,24},{12,28},{16,0},{20,4},{24,8},{28,12},{1,17},{... | collective-permute-start | bytes 98312 | tf_op jit(solution)/shard_map/ppermute | solution.py:101
  66.3 1.6 %collective-permute-done.10 = f32[4,1,2,1,1,1,16,128]{7,6,5,4,3,2,0,1:T(8,128)S(1)} collective-permute-done((f32[4,1,2,1,1,1,16,128]{7,6,5,4,3,2,0,1:T(8,128)S(1)}, f32[4,1,2,1,1,1,16,128]{7,6,5,4,3,2,0,1:T(8,128)S(1)}, u32[]{:S(2)}, u32[]{:S(2)}) %collective-permute-start.10) | collective-permute-done | bytes 65568 | tf_op jit(solution)/shard_map/ppermute | solution.py:101
  67.9 1.2 %collective-permute-start.11 = (f32[4,1,1,1,1,1,16,128]{7,6,5,4,3,2,0,1:T(8,128)S(1)}, f32[4,1,1,1,1,1,16,128]{7,6,5,4,3,2,0,1:T(8,128)S(1)}, u32[]{:S(2)}, u32[]{:S(2)}) collective-permute-start(f32[4,1,1,1,1,1,16,128]{7,6,5,4,3,2,0,1:T(8,128)S(1)} %constant_dynamic-slice_fusion.3), channel_id=1, source_target_pairs={{0,2},{1,3},{2,0},{3,1},{4,6},{5,7},{6,4},{7,5},{8,10},{9,11},{10,... | collective-permute-start | bytes 98312 | tf_op jit(solution)/shard_map/ppermute | solution.py:101
  69.3 2.6 %collective-permute-done.11 = f32[4,1,1,1,1,1,16,128]{7,6,5,4,3,2,0,1:T(8,128)S(1)} collective-permute-done((f32[4,1,1,1,1,1,16,128]{7,6,5,4,3,2,0,1:T(8,128)S(1)}, f32[4,1,1,1,1,1,16,128]{7,6,5,4,3,2,0,1:T(8,128)S(1)}, u32[]{:S(2)}, u32[]{:S(2)}) %collective-permute-start.11) | collective-permute-done | bytes 32800 | tf_op jit(solution)/shard_map/ppermute | solution.py:101
  71.9 1.3 %collective-permute-done.14 = f32[4,1,1,1,1,1,16,128]{7,6,5,4,3,2,0,1:T(8,128)S(1)} collective-permute-done((f32[4,1,1,1,1,1,16,128]{7,6,5,4,3,2,0,1:T(8,128)S(1)}, f32[4,1,1,1,1,1,16,128]{7,6,5,4,3,2,0,1:T(8,128)S(1)}, u32[]{:S(2)}, u32[]{:S(2)}) %collective-permute-start.14) | collective-permute-done | bytes 32800 | tf_op jit(solution)/shard_map/ppermute | solution.py:101
  75.2 1.8 %fusion.13 = bf16[12,16,128]{2,1,0:T(8,128)(2,1)S(1)} fusion(bf16[12,4,136,128]{3,2,1,0:T(8,128)(2,1)} %all-gather.2.cloned.1.call-done, bf16[12,4,16,128]{3,2,1,0:T(8,128)(2,1)S(1)} %bitcast.97, pred[12,4]{1,0:T(8,128)(4,1)S(1)} %copy.62), kind=kOutput, calls=%fused_computation.15 | convolution fusion | flops 25288704 | bytes 1818672 | tf_op jit(solution)/shard_map/nerc,necd->nrd/dot_general | solution.py:152
  77.3 1.5 %collective-permute-start.19 = (bf16[4,1,1,1,1,1,16,128]{7,6,0,5,4,3,2,1:T(8,128)(2,1)S(1)}, bf16[4,1,1,1,1,1,16,128]{7,6,0,5,4,3,2,1:T(8,128)(2,1)S(1)}, u32[]{:S(2)}, u32[]{:S(2)}) collective-permute-start(bf16[4,1,1,1,1,1,16,128]{7,6,0,5,4,3,2,1:T(8,128)(2,1)S(1)} %get-tuple-element.31), channel_id=1, source_target_pairs={{0,2},{1,3},{2,0},{3,1},{4,6},{5,7},{6,4},{7,5},{8,10},{9,11},{10,... | collective-permute-start | bytes 49160 | tf_op jit(solution)/shard_map/ppermute | solution.py:106
  78.8 3.1 %collective-permute-done.15 = bf16[4,1,1,1,1,1,16,128]{7,6,0,5,4,3,2,1:T(8,128)(2,1)S(1)} collective-permute-done((bf16[4,1,1,1,1,1,16,128]{7,6,0,5,4,3,2,1:T(8,128)(2,1)S(1)}, bf16[4,1,1,1,1,1,16,128]{7,6,0,5,4,3,2,1:T(8,128)(2,1)S(1)}, u32[]{:S(2)}, u32[]{:S(2)}) %collective-permute-start.15) | collective-permute-done | bytes 16416 | tf_op jit(solution)/shard_map/ppermute | solution.py:106
  82.5 2.3 %collective-permute-start.20 = (bf16[4,1,2,1,1,1,16,128]{7,6,0,5,4,3,2,1:T(8,128)(2,1)S(1)}, bf16[4,1,2,1,1,1,16,128]{7,6,0,5,4,3,2,1:T(8,128)(2,1)S(1)}, u32[]{:S(2)}, u32[]{:S(2)}) collective-permute-start(bf16[4,1,2,1,1,1,16,128]{7,6,0,5,4,3,2,1:T(8,128)(2,1)S(1)} %maximum_select_fusion.16), channel_id=1, source_target_pairs={{0,16},{4,20},{8,24},{12,28},{16,0},{20,4},{24,8},{28,12},{1,17},{... | collective-permute-start | bytes 98312 | tf_op jit(solution)/shard_map/ppermute | solution.py:106
  87.1 1.7 %collective-permute-done.20 = bf16[4,1,2,1,1,1,16,128]{7,6,0,5,4,3,2,1:T(8,128)(2,1)S(1)} collective-permute-done((bf16[4,1,2,1,1,1,16,128]{7,6,0,5,4,3,2,1:T(8,128)(2,1)S(1)}, bf16[4,1,2,1,1,1,16,128]{7,6,0,5,4,3,2,1:T(8,128)(2,1)S(1)}, u32[]{:S(2)}, u32[]{:S(2)}) %collective-permute-start.20) | collective-permute-done | bytes 32800 | tf_op jit(solution)/shard_map/ppermute | solution.py:106
  89.0 2.0 %collective-permute-start.25 = (bf16[4,1,2,2,1,1,16,128]{7,6,0,5,4,3,2,1:T(8,128)(2,1)S(1)}, bf16[4,1,2,2,1,1,16,128]{7,6,0,5,4,3,2,1:T(8,128)(2,1)S(1)}, u32[]{:S(2)}, u32[]{:S(2)}) collective-permute-start(bf16[4,1,2,2,1,1,16,128]{7,6,0,5,4,3,2,1:T(8,128)(2,1)S(1)} %fusion.29), channel_id=1, source_target_pairs={{0,16},{4,20},{8,24},{12,28},{16,0},{20,4},{24,8},{28,12},{1,17},{... | collective-permute-start | bytes 196616 | tf_op jit(solution)/shard_map/ppermute | solution.py:106
  92.0 2.4 %collective-permute-done.21 = bf16[4,1,2,1,1,2,16,128]{7,6,0,5,4,3,2,1:T(8,128)(2,1)S(1)} collective-permute-done((bf16[4,1,2,1,1,2,16,128]{7,6,0,5,4,3,2,1:T(8,128)(2,1)S(1)}, bf16[4,1,2,1,1,2,16,128]{7,6,0,5,4,3,2,1:T(8,128)(2,1)S(1)}, u32[]{:S(2)}, u32[]{:S(2)}) %collective-permute-start.21) | collective-permute-done | bytes 65568 | tf_op jit(solution)/shard_map/ppermute | solution.py:106
  94.8 1.4 %collective-permute-start.26 = (bf16[4,1,2,2,1,2,16,128]{7,6,0,5,4,3,2,1:T(8,128)(2,1)S(1)}, bf16[4,1,2,2,1,2,16,128]{7,6,0,5,4,3,2,1:T(8,128)(2,1)S(1)}, u32[]{:S(2)}, u32[]{:S(2)}) collective-permute-start(bf16[4,1,2,2,1,2,16,128]{7,6,0,5,4,3,2,1:T(8,128)(2,1)S(1)} %maximum_select_fusion.7), channel_id=1, source_target_pairs={{0,8},{4,12},{8,0},{12,4},{16,24},{20,28},{24,16},{28,20},{1,9},{5... | collective-permute-start | bytes 393224 | tf_op jit(solution)/shard_map/ppermute | solution.py:106
  96.3 3.1 %collective-permute-done.22 = bf16[4,1,2,1,2,2,16,128]{7,6,0,5,4,3,2,1:T(8,128)(2,1)S(1)} collective-permute-done((bf16[4,1,2,1,2,2,16,128]{7,6,0,5,4,3,2,1:T(8,128)(2,1)S(1)}, bf16[4,1,2,1,2,2,16,128]{7,6,0,5,4,3,2,1:T(8,128)(2,1)S(1)}, u32[]{:S(2)}, u32[]{:S(2)}) %collective-permute-start.22) | collective-permute-done | bytes 131104 | tf_op jit(solution)/shard_map/ppermute | solution.py:106
  101.1 1.4 %collective-permute-done.27 = bf16[12,256,128]{2,1,0:T(8,128)(2,1)} collective-permute-done((bf16[12,256,128]{2,1,0:T(8,128)(2,1)S(1)}, bf16[12,256,128]{2,1,0:T(8,128)(2,1)}, u32[]{:S(2)}, u32[]{:S(2)}) %collective-permute-start.27) | collective-permute-done | bytes 786464 | tf_op jit(solution)/shard_map/ppermute | solution.py:160
  102.5 1.8 %gather_fusion.3 = bf16[8,256,128]{2,1,0:T(8,128)(2,1)S(1)} fusion(bf16[12,256,128]{2,1,0:T(8,128)(2,1)} %collective-permute-done.27, s32[1024]{0:T(1024)S(1)} %pad_clamp_fusion), kind=kCustom, calls=%fused_computation.1.clone | custom fusion | bytes 1048608 | tf_op jit(solution)/shard_map/jit(_take)/gather | solution.py:162
  (134 shorter events, 22.2 us)
Async XLA Ops:
  6.5 36.4 %copy-start = (bf16[4,4,256,256]{3,2,1,0:T(8,128)(2,1)S(1)}, bf16[4,4,256,256]{3,2,1,0:T(8,128)(2,1)}, u32[]{:S(2)}) copy-start(bf16[4,4,256,256]{3,2,1,0:T(8,128)(2,1)} %param.11) | copy-start | bytes 6291460
  6.5 18.2 %copy-start.1 = (bf16[4,512,256]{2,1,0:T(8,128)(2,1)S(1)}, bf16[4,512,256]{2,1,0:T(8,128)(2,1)}, u32[]{:S(2)}) copy-start(bf16[4,512,256]{2,1,0:T(8,128)(2,1)} %residual_ref.1) | copy-start | bytes 3145732
  6.5 15.2 %copy-start.8 = (s32[4,4]{1,0:T(4,128)S(1)}, s32[4,4]{1,0:T(4,128)}, u32[]{:S(2)}) copy-start(s32[4,4]{1,0:T(4,128)} %param.10) | copy-start | bytes 196
  6.5 66.7 %all-gather.2.cloned.1.call-start = ((), (), s32[]{:S(2)}) async-start(), calls=%async_computation | async-start | bytes 2088960 | tf_op jit(solution)/shard_map/all_gather | solution.py:122
  14.6 12.5 %collective-permute-start.2 = (f32[12,256,128]{2,1,0:T(8,128)}, f32[12,256,128]{2,1,0:T(8,128)}, u32[]{:S(2)}, u32[]{:S(2)}) collective-permute-start(f32[12,256,128]{2,1,0:T(8,128)} %get-tuple-element.16), channel_id=1, source_target_pairs={{0,1},{1,0},{2,3},{3,2},{4,5},{5,4},{6,7},{7,6},{8,9},{9,8},{10,11... | collective-permute-start | bytes 4718600 | tf_op jit(solution)/shard_map/ppermute | solution.py:139
  16.9 5.1 %collective-permute-start = (bf16[1,512,256]{2,1,0:T(8,128)(2,1)}, bf16[1,512,256]{2,1,0:T(8,128)(2,1)}, u32[]{:S(2)}, u32[]{:S(2)}) collective-permute-start(bf16[1,512,256]{2,1,0:T(8,128)(2,1)} %get-tuple-element.27), channel_id=1, source_target_pairs={{0,1},{1,2},{2,3},{3,4},{4,5},{5,6},{6,7},{7,8},{8,9},{9,10},{10,1... | collective-permute-start | bytes 786440 | tf_op jit(solution)/shard_map/ppermute | solution.py:68
  19.5 5.2 %collective-permute-start.1 = (bf16[1,512,256]{2,1,0:T(8,128)(2,1)}, bf16[1,512,256]{2,1,0:T(8,128)(2,1)}, u32[]{:S(2)}, u32[]{:S(2)}) collective-permute-start(bf16[1,512,256]{2,1,0:T(8,128)(2,1)} %get-tuple-element.28), channel_id=1, source_target_pairs={{1,0},{2,1},{3,2},{4,3},{5,4},{6,5},{7,6},{8,7},{9,8},{10,9},{11,1... | collective-permute-start | bytes 786440 | tf_op jit(solution)/shard_map/ppermute | solution.py:70
  30.4 17.5 %collective-permute-start.5 = (f32[4,1,2,2,1,2,16,128]{7,6,5,4,3,2,0,1:T(8,128)}, f32[4,1,2,2,1,2,16,128]{7,6,5,4,3,2,0,1:T(8,128)}, u32[]{:S(2)}, u32[]{:S(2)}) collective-permute-start(f32[4,1,2,2,1,2,16,128]{7,6,5,4,3,2,0,1:T(8,128)} %constant_dynamic-slice_fusion.9), channel_id=1, source_target_pairs={{0,8},{4,12},{8,0},{12,4},{16,24},{20,28},{24,16},{28,20},{1,9},{5... | collective-permute-start | bytes 786440 | tf_op jit(solution)/shard_map/ppermute | solution.py:101
  37.5 11.3 %collective-permute-start.4 = (f32[4,1,2,1,2,2,16,128]{7,6,5,4,3,2,0,1:T(8,128)}, f32[4,1,2,1,2,2,16,128]{7,6,5,4,3,2,0,1:T(8,128)}, u32[]{:S(2)}, u32[]{:S(2)}) collective-permute-start(f32[4,1,2,1,2,2,16,128]{7,6,5,4,3,2,0,1:T(8,128)} %constant_dynamic-slice_fusion.10), channel_id=1, source_target_pairs={{0,4},{4,0},{8,12},{12,8},{16,20},{20,16},{24,28},{28,24},{1,5},{5... | collective-permute-start | bytes 786440 | tf_op jit(solution)/shard_map/ppermute | solution.py:101
  38.1 11.8 %collective-permute-start.3 = (f32[4,1,1,2,2,2,16,128]{7,6,5,4,3,2,0,1:T(8,128)S(1)}, f32[4,1,1,2,2,2,16,128]{7,6,5,4,3,2,0,1:T(8,128)}, u32[]{:S(2)}, u32[]{:S(2)}) collective-permute-start(f32[4,1,1,2,2,2,16,128]{7,6,5,4,3,2,0,1:T(8,128)S(1)} %constant_dynamic-slice_fusion.11), channel_id=1, source_target_pairs={{0,2},{1,3},{2,0},{3,1},{4,6},{5,7},{6,4},{7,5},{8,10},{9,11},{10,... | collective-permute-start | bytes 786440 | tf_op jit(solution)/shard_map/ppermute | solution.py:101
  50.9 5.9 %collective-permute-start.6 = (f32[4,1,1,1,2,2,16,128]{7,6,5,4,3,2,0,1:T(8,128)S(1)}, f32[4,1,1,1,2,2,16,128]{7,6,5,4,3,2,0,1:T(8,128)S(1)}, u32[]{:S(2)}, u32[]{:S(2)}) collective-permute-start(f32[4,1,1,1,2,2,16,128]{7,6,5,4,3,2,0,1:T(8,128)S(1)} %constant_dynamic-slice_fusion.8), channel_id=1, source_target_pairs={{0,4},{4,0},{8,12},{12,8},{16,20},{20,16},{24,28},{28,24},{1,5},{5... | collective-permute-start | bytes 393224 | tf_op jit(solution)/shard_map/ppermute | solution.py:101
  52.8 9.2 %collective-permute-start.9 = (f32[4,1,2,1,1,2,16,128]{7,6,5,4,3,2,0,1:T(8,128)S(1)}, f32[4,1,2,1,1,2,16,128]{7,6,5,4,3,2,0,1:T(8,128)S(1)}, u32[]{:S(2)}, u32[]{:S(2)}) collective-permute-start(f32[4,1,2,1,1,2,16,128]{7,6,5,4,3,2,0,1:T(8,128)S(1)} %constant_dynamic-slice_fusion.5), channel_id=1, source_target_pairs={{0,8},{4,12},{8,0},{12,4},{16,24},{20,28},{24,16},{28,20},{1,9},{5... | collective-permute-start | bytes 393224 | tf_op jit(solution)/shard_map/ppermute | solution.py:101
  54.3 7.8 %collective-permute-start.12 = (f32[4,1,2,2,1,1,16,128]{7,6,5,4,3,2,0,1:T(8,128)S(1)}, f32[4,1,2,2,1,1,16,128]{7,6,5,4,3,2,0,1:T(8,128)S(1)}, u32[]{:S(2)}, u32[]{:S(2)}) collective-permute-start(f32[4,1,2,2,1,1,16,128]{7,6,5,4,3,2,0,1:T(8,128)S(1)} %constant_dynamic-slice_fusion.2), channel_id=1, source_target_pairs={{0,16},{4,20},{8,24},{12,28},{16,0},{20,4},{24,8},{28,12},{1,17},{... | collective-permute-start | bytes 393224 | tf_op jit(solution)/shard_map/ppermute | solution.py:101
  56.8 6.5 %collective-permute-start.7 = (f32[4,1,1,1,1,2,16,128]{7,6,5,4,3,2,0,1:T(8,128)S(1)}, f32[4,1,1,1,1,2,16,128]{7,6,5,4,3,2,0,1:T(8,128)S(1)}, u32[]{:S(2)}, u32[]{:S(2)}) collective-permute-start(f32[4,1,1,1,1,2,16,128]{7,6,5,4,3,2,0,1:T(8,128)S(1)} %constant_dynamic-slice_fusion.7), channel_id=1, source_target_pairs={{0,8},{4,12},{8,0},{12,4},{16,24},{20,28},{24,16},{28,20},{1,9},{5... | collective-permute-start | bytes 196616 | tf_op jit(solution)/shard_map/ppermute | solution.py:101
  62.0 5.9 %collective-permute-start.10 = (f32[4,1,2,1,1,1,16,128]{7,6,5,4,3,2,0,1:T(8,128)S(1)}, f32[4,1,2,1,1,1,16,128]{7,6,5,4,3,2,0,1:T(8,128)S(1)}, u32[]{:S(2)}, u32[]{:S(2)}) collective-permute-start(f32[4,1,2,1,1,1,16,128]{7,6,5,4,3,2,0,1:T(8,128)S(1)} %constant_dynamic-slice_fusion.4), channel_id=1, source_target_pairs={{0,16},{4,20},{8,24},{12,28},{16,0},{20,4},{24,8},{28,12},{1,17},{... | collective-permute-start | bytes 196616 | tf_op jit(solution)/shard_map/ppermute | solution.py:101
  62.1 7.0 %collective-permute-start.13 = (f32[4,1,1,2,1,1,16,128]{7,6,5,4,3,2,0,1:T(8,128)S(1)}, f32[4,1,1,2,1,1,16,128]{7,6,5,4,3,2,0,1:T(8,128)S(1)}, u32[]{:S(2)}, u32[]{:S(2)}) collective-permute-start(f32[4,1,1,2,1,1,16,128]{7,6,5,4,3,2,0,1:T(8,128)S(1)} %constant_dynamic-slice_fusion.1), channel_id=1, source_target_pairs={{0,2},{1,3},{2,0},{3,1},{4,6},{5,7},{6,4},{7,5},{8,10},{9,11},{10,... | collective-permute-start | bytes 196616 | tf_op jit(solution)/shard_map/ppermute | solution.py:101
  63.4 5.9 %collective-permute-start.8 = (f32[4,1,1,1,1,1,16,128]{7,6,5,4,3,2,0,1:T(8,128)S(1)}, f32[4,1,1,1,1,1,16,128]{7,6,5,4,3,2,0,1:T(8,128)S(1)}, u32[]{:S(2)}, u32[]{:S(2)}) collective-permute-start(f32[4,1,1,1,1,1,16,128]{7,6,5,4,3,2,0,1:T(8,128)S(1)} %constant_dynamic-slice_fusion.6), channel_id=1, source_target_pairs={{0,16},{4,20},{8,24},{12,28},{16,0},{20,4},{24,8},{28,12},{1,17},{... | collective-permute-start | bytes 98312 | tf_op jit(solution)/shard_map/ppermute | solution.py:101
  67.9 4.0 %collective-permute-start.11 = (f32[4,1,1,1,1,1,16,128]{7,6,5,4,3,2,0,1:T(8,128)S(1)}, f32[4,1,1,1,1,1,16,128]{7,6,5,4,3,2,0,1:T(8,128)S(1)}, u32[]{:S(2)}, u32[]{:S(2)}) collective-permute-start(f32[4,1,1,1,1,1,16,128]{7,6,5,4,3,2,0,1:T(8,128)S(1)} %constant_dynamic-slice_fusion.3), channel_id=1, source_target_pairs={{0,2},{1,3},{2,0},{3,1},{4,6},{5,7},{6,4},{7,5},{8,10},{9,11},{10,... | collective-permute-start | bytes 98312 | tf_op jit(solution)/shard_map/ppermute | solution.py:101
  69.2 4.0 %collective-permute-start.14 = (f32[4,1,1,1,1,1,16,128]{7,6,5,4,3,2,0,1:T(8,128)S(1)}, f32[4,1,1,1,1,1,16,128]{7,6,5,4,3,2,0,1:T(8,128)S(1)}, u32[]{:S(2)}, u32[]{:S(2)}) collective-permute-start(f32[4,1,1,1,1,1,16,128]{7,6,5,4,3,2,0,1:T(8,128)S(1)} %constant_dynamic-slice_fusion), channel_id=1, source_target_pairs={{0,4},{4,0},{8,12},{12,8},{16,20},{20,16},{24,28},{28,24},{1,5},{5... | collective-permute-start | bytes 98312 | tf_op jit(solution)/shard_map/ppermute | solution.py:101
  77.0 4.9 %collective-permute-start.15 = (bf16[4,1,1,1,1,1,16,128]{7,6,0,5,4,3,2,1:T(8,128)(2,1)S(1)}, bf16[4,1,1,1,1,1,16,128]{7,6,0,5,4,3,2,1:T(8,128)(2,1)S(1)}, u32[]{:S(2)}, u32[]{:S(2)}) collective-permute-start(bf16[4,1,1,1,1,1,16,128]{7,6,0,5,4,3,2,1:T(8,128)(2,1)S(1)} %get-tuple-element.30), channel_id=1, source_target_pairs={{0,16},{4,20},{8,24},{12,28},{16,0},{20,4},{24,8},{28,12},{1,17},{... | collective-permute-start | bytes 49160 | tf_op jit(solution)/shard_map/ppermute | solution.py:106
  77.3 5.2 %collective-permute-start.19 = (bf16[4,1,1,1,1,1,16,128]{7,6,0,5,4,3,2,1:T(8,128)(2,1)S(1)}, bf16[4,1,1,1,1,1,16,128]{7,6,0,5,4,3,2,1:T(8,128)(2,1)S(1)}, u32[]{:S(2)}, u32[]{:S(2)}) collective-permute-start(bf16[4,1,1,1,1,1,16,128]{7,6,0,5,4,3,2,1:T(8,128)(2,1)S(1)} %get-tuple-element.31), channel_id=1, source_target_pairs={{0,2},{1,3},{2,0},{3,1},{4,6},{5,7},{6,4},{7,5},{8,10},{9,11},{10,... | collective-permute-start | bytes 49160 | tf_op jit(solution)/shard_map/ppermute | solution.py:106
  78.8 6.1 %collective-permute-start.23 = (bf16[4,1,1,1,1,1,16,128]{7,6,0,5,4,3,2,1:T(8,128)(2,1)S(1)}, bf16[4,1,1,1,1,1,16,128]{7,6,0,5,4,3,2,1:T(8,128)(2,1)S(1)}, u32[]{:S(2)}, u32[]{:S(2)}) collective-permute-start(bf16[4,1,1,1,1,1,16,128]{7,6,0,5,4,3,2,1:T(8,128)(2,1)S(1)} %get-tuple-element.32), channel_id=1, source_target_pairs={{0,4},{4,0},{8,12},{12,8},{16,20},{20,16},{24,28},{28,24},{1,5},{5... | collective-permute-start | bytes 49160 | tf_op jit(solution)/shard_map/ppermute | solution.py:106
  81.9 4.2 %collective-permute-start.16 = (bf16[4,1,1,1,1,2,16,128]{7,6,0,5,4,3,2,1:T(8,128)(2,1)S(1)}, bf16[4,1,1,1,1,2,16,128]{7,6,0,5,4,3,2,1:T(8,128)(2,1)S(1)}, u32[]{:S(2)}, u32[]{:S(2)}) collective-permute-start(bf16[4,1,1,1,1,2,16,128]{7,6,0,5,4,3,2,1:T(8,128)(2,1)S(1)} %maximum_select_fusion.14), channel_id=1, source_target_pairs={{0,8},{4,12},{8,0},{12,4},{16,24},{20,28},{24,16},{28,20},{1,9},{5... | collective-permute-start | bytes 98312 | tf_op jit(solution)/shard_map/ppermute | solution.py:106
  82.5 6.3 %collective-permute-start.20 = (bf16[4,1,2,1,1,1,16,128]{7,6,0,5,4,3,2,1:T(8,128)(2,1)S(1)}, bf16[4,1,2,1,1,1,16,128]{7,6,0,5,4,3,2,1:T(8,128)(2,1)S(1)}, u32[]{:S(2)}, u32[]{:S(2)}) collective-permute-start(bf16[4,1,2,1,1,1,16,128]{7,6,0,5,4,3,2,1:T(8,128)(2,1)S(1)} %maximum_select_fusion.16), channel_id=1, source_target_pairs={{0,16},{4,20},{8,24},{12,28},{16,0},{20,4},{24,8},{28,12},{1,17},{... | collective-permute-start | bytes 98312 | tf_op jit(solution)/shard_map/ppermute | solution.py:106
  84.8 4.1 %collective-permute-start.24 = (bf16[4,1,1,2,1,1,16,128]{7,6,0,5,4,3,2,1:T(8,128)(2,1)S(1)}, bf16[4,1,1,2,1,1,16,128]{7,6,0,5,4,3,2,1:T(8,128)(2,1)S(1)}, u32[]{:S(2)}, u32[]{:S(2)}) collective-permute-start(bf16[4,1,1,2,1,1,16,128]{7,6,0,5,4,3,2,1:T(8,128)(2,1)S(1)} %maximum_select_fusion.18), channel_id=1, source_target_pairs={{0,2},{1,3},{2,0},{3,1},{4,6},{5,7},{6,4},{7,5},{8,10},{9,11},{10,... | collective-permute-start | bytes 98312 | tf_op jit(solution)/shard_map/ppermute | solution.py:106
  86.1 4.9 %collective-permute-start.17 = (bf16[4,1,1,1,2,2,16,128]{7,6,0,5,4,3,2,1:T(8,128)(2,1)S(1)}, bf16[4,1,1,1,2,2,16,128]{7,6,0,5,4,3,2,1:T(8,128)(2,1)S(1)}, u32[]{:S(2)}, u32[]{:S(2)}) collective-permute-start(bf16[4,1,1,1,2,2,16,128]{7,6,0,5,4,3,2,1:T(8,128)(2,1)S(1)} %maximum_select_fusion.9), channel_id=1, source_target_pairs={{0,4},{4,0},{8,12},{12,8},{16,20},{20,16},{24,28},{28,24},{1,5},{5... | collective-permute-start | bytes 196616 | tf_op jit(solution)/shard_map/ppermute | solution.py:106
  88.8 5.6 %collective-permute-start.21 = (bf16[4,1,2,1,1,2,16,128]{7,6,0,5,4,3,2,1:T(8,128)(2,1)S(1)}, bf16[4,1,2,1,1,2,16,128]{7,6,0,5,4,3,2,1:T(8,128)(2,1)S(1)}, u32[]{:S(2)}, u32[]{:S(2)}) collective-permute-start(bf16[4,1,2,1,1,2,16,128]{7,6,0,5,4,3,2,1:T(8,128)(2,1)S(1)} %maximum_select_fusion.11), channel_id=1, source_target_pairs={{0,8},{4,12},{8,0},{12,4},{16,24},{20,28},{24,16},{28,20},{1,9},{5... | collective-permute-start | bytes 196616 | tf_op jit(solution)/shard_map/ppermute | solution.py:106
  89.0 5.8 %collective-permute-start.25 = (bf16[4,1,2,2,1,1,16,128]{7,6,0,5,4,3,2,1:T(8,128)(2,1)S(1)}, bf16[4,1,2,2,1,1,16,128]{7,6,0,5,4,3,2,1:T(8,128)(2,1)S(1)}, u32[]{:S(2)}, u32[]{:S(2)}) collective-permute-start(bf16[4,1,2,2,1,1,16,128]{7,6,0,5,4,3,2,1:T(8,128)(2,1)S(1)} %fusion.29), channel_id=1, source_target_pairs={{0,16},{4,20},{8,24},{12,28},{16,0},{20,4},{24,8},{28,12},{1,17},{... | collective-permute-start | bytes 196616 | tf_op jit(solution)/shard_map/ppermute | solution.py:106
  91.1 5.2 %collective-permute-start.18 = (bf16[4,1,1,2,2,2,16,128]{7,6,0,5,4,3,2,1:T(8,128)(2,1)S(1)}, bf16[4,1,1,2,2,2,16,128]{7,6,0,5,4,3,2,1:T(8,128)(2,1)S(1)}, u32[]{:S(2)}, u32[]{:S(2)}) collective-permute-start(bf16[4,1,1,2,2,2,16,128]{7,6,0,5,4,3,2,1:T(8,128)(2,1)S(1)} %maximum_select_fusion.5), channel_id=1, source_target_pairs={{0,2},{1,3},{2,0},{3,1},{4,6},{5,7},{6,4},{7,5},{8,10},{9,11},{10,... | collective-permute-start | bytes 393224 | tf_op jit(solution)/shard_map/ppermute | solution.py:106
  94.4 5.0 %collective-permute-start.22 = (bf16[4,1,2,1,2,2,16,128]{7,6,0,5,4,3,2,1:T(8,128)(2,1)S(1)}, bf16[4,1,2,1,2,2,16,128]{7,6,0,5,4,3,2,1:T(8,128)(2,1)S(1)}, u32[]{:S(2)}, u32[]{:S(2)}) collective-permute-start(bf16[4,1,2,1,2,2,16,128]{7,6,0,5,4,3,2,1:T(8,128)(2,1)S(1)} %maximum_select_fusion.6), channel_id=1, source_target_pairs={{0,4},{4,0},{8,12},{12,8},{16,20},{20,16},{24,28},{28,24},{1,5},{5... | collective-permute-start | bytes 393224 | tf_op jit(solution)/shard_map/ppermute | solution.py:106
  94.8 5.0 %collective-permute-start.26 = (bf16[4,1,2,2,1,2,16,128]{7,6,0,5,4,3,2,1:T(8,128)(2,1)S(1)}, bf16[4,1,2,2,1,2,16,128]{7,6,0,5,4,3,2,1:T(8,128)(2,1)S(1)}, u32[]{:S(2)}, u32[]{:S(2)}) collective-permute-start(bf16[4,1,2,2,1,2,16,128]{7,6,0,5,4,3,2,1:T(8,128)(2,1)S(1)} %maximum_select_fusion.7), channel_id=1, source_target_pairs={{0,8},{4,12},{8,0},{12,4},{16,24},{20,28},{24,16},{28,20},{1,9},{5... | collective-permute-start | bytes 393224 | tf_op jit(solution)/shard_map/ppermute | solution.py:106
  100.0 2.5 %collective-permute-start.27 = (bf16[12,256,128]{2,1,0:T(8,128)(2,1)S(1)}, bf16[12,256,128]{2,1,0:T(8,128)(2,1)}, u32[]{:S(2)}, u32[]{:S(2)}) collective-permute-start(bf16[12,256,128]{2,1,0:T(8,128)(2,1)S(1)} %pad_maximum_fusion.1), channel_id=1, source_target_pairs={{0,1},{1,0},{2,3},{3,2},{4,5},{5,4},{6,7},{7,6},{8,9},{9,8},{10,11... | collective-permute-start | bytes 2359304 | tf_op jit(solution)/shard_map/ppermute | solution.py:160
  (8 other events, 45.9 us)
Sparse Core Ops, SparseCore 0:
  21.9 26.7 all-gather.1

commit v12 on v11

--- a/solution.py
+++ b/solution.py
@@ -1,3 +1,5 @@
+import functools
+
 import jax
 import jax.numpy as jnp
 from jax import lax
@@ -6,55 +8,50 @@
 from jax.sharding import PartitionSpec as P
 
 
-def restrict_kernel(links, half, residual_ref, basis_ref, keep_ref, send_ref):
+def restrict_kernel(links, half, residual_ref, basis_ref, out_ref, *, upper):
     j = pl.program_id(0)
     pairs_per = basis_ref.shape[1]
-    rows = keep_ref.shape[1]
+    rows = out_ref.shape[1]
 
     @pl.when(j == 0)
     def _():
-        keep_ref[...] = jnp.zeros_like(keep_ref)
-        send_ref[...] = jnp.zeros_like(send_ref)
+        out_ref[...] = jnp.zeros_like(out_ref)
 
     for q in range(pairs_per):
         n = links[j * pairs_per + q]
-        term = jnp.dot(residual_ref[0], basis_ref[0, q], preferred_element_type=jnp.float32)
 
-        @pl.when(half[0] == 0)
+        @pl.when(half[0] == upper)
         def _():
-            keep_ref[n] += term[:rows]
-            send_ref[n] += term[rows:]
+            out_ref[n] += jnp.dot(residual_ref[0, :rows], basis_ref[0, q], preferred_element_type=jnp.float32)
 
-        @pl.when(half[0] != 0)
+        @pl.when(half[0] != upper)
         def _():
-            keep_ref[n] += term[rows:]
-            send_ref[n] += term[:rows]
+            out_ref[n] += jnp.dot(residual_ref[0, rows:], basis_ref[0, q], preferred_element_type=jnp.float32)
 
 
-def restrict(residual, basis, interface, total_blocks, half):
+def restrict(residual, basis, links, total_blocks, half, upper):
     count, rhs, size = residual.shape
     width = basis.shape[-1]
     rows = rhs // 2
-    block = pl.BlockSpec((total_blocks, rows, width), lambda j, links, half: (0, 0, 0))
     return pl.pallas_call(
-        restrict_kernel,
-        out_shape=[jax.ShapeDtypeStruct((total_blocks, rows, width), jnp.float32)] * 2,
+        functools.partial(restrict_kernel, upper=upper),
+        out_shape=jax.ShapeDtypeStruct((total_blocks, rows, width), jnp.float32),
         grid_spec=pltpu.PrefetchScalarGridSpec(
             num_scalar_prefetch=2,
             grid=(count,),
             in_specs=[
                 pl.BlockSpec((1, rhs, size), lambda j, links, half: (j, 0, 0)),
-                pl.BlockSpec((1, interface.shape[1], size, width), lambda j, links, half: (j, 0, 0, 0)),
+                pl.BlockSpec((1, basis.shape[1], size, width), lambda j, links, half: (j, 0, 0, 0)),
             ],
-            out_specs=[block, block],
+            out_specs=pl.BlockSpec((total_blocks, rows, width), lambda j, links, half: (0, 0, 0)),
         ),
         compiler_params=pltpu.CompilerParams(dimension_semantics=("arbitrary",)),
         cost_estimate=pl.CostEstimate(
-            flops=2 * count * interface.shape[1] * rhs * size * width,
-            bytes_accessed=residual.size * 2 + basis.size * 2 + total_blocks * rhs * width * 4,
+            flops=count * basis.shape[1] * rhs * size * width,
+            bytes_accessed=residual.size * 2 + basis.size * 2 + total_blocks * rows * width * 4,
             transcendentals=0,
         ),
-    )(interface.reshape(-1), half, residual, basis)
+    )(links, half, residual, basis)
 
 
 def with_halo(cells, sides, width):
@@ -128,7 +125,9 @@
     total_blocks = pattern_all.shape[0]
     bits = device_bits()
     own_half = bit_of(*bits[0])
-    keep, send = restrict(residual, basis, interface, total_blocks, own_half.reshape(1).astype(jnp.int32))
+    links = interface.reshape(-1)
+    half = own_half.reshape(1).astype(jnp.int32)
+    send = restrict(residual, basis, links, total_blocks, half, 1)
 
     nb = len(bits)
     inner = rhs >> nb
@@ -136,7 +135,8 @@
     streams = 3 if total_blocks % 3 == 0 else 1
     per = total_blocks // streams
     orders = stream_orders(nb, streams)
-    whole = keep + lax.ppermute(send, bits[0][0], pairs(*bits[0]))
+    got = lax.ppermute(send, bits[0][0], pairs(*bits[0]))
+    whole = restrict(residual, basis, links, total_blocks, half, 0) + got
     whole = whole.reshape((total_blocks, 1) + (2,) * (nb - 1) + (inner, width))
     extended, inverse_blocks, whole = lax.optimization_barrier((extended, inverse_blocks, whole))
     parts = [lax.slice_in_dim(whole, s * per, (s + 1) * per, axis=0) for s in range(streams)]

time: 116 us -> 114 us (0.983)
  waiting for transfers between devices: 24.1 us -> 16.7 us
  Pallas kernels: 6.44 us -> 10.4 us
  starting transfers between devices: 36.5 us -> 38.9 us
    pallas_call x1 -> x2, Pallas kernels: 6.44 us -> 10.4 us  [restrict(): pl.pallas_call(functools.partial(restrict_kernel, upper=upper), out_shape...]
    ppermute x12, starting transfers between devices: 11.7 us -> 15.3 us  [double(): recv = lax.ppermute(y, axis, pairs(axis, mask))]
    ppermute x12, waiting for transfers between devices: 10.7 us -> 7.31 us  [double(): recv = lax.ppermute(y, axis, pairs(axis, mask))]
    ppermute x1, waiting for transfers between devices: 2.69 us -> 0.01 us  [with_halo(): lax.ppermute(head, axis, [((i + 1) % count, i) for i in range(ends)])]
    ppermute x12, waiting for transfers between devices: 9.28 us -> 7.95 us  [halve(): lax.ppermute(send.astype(wire), axis, pairs(axis, mask)).astype(x.dtype)]
    ppermute x12, starting transfers between devices: 20.3 us -> 19.1 us  [halve(): lax.ppermute(send.astype(wire), axis, pairs(axis, mask)).astype(x.dtype)]
    unnamed x24 -> x26, local copies, waits for them, and re-layouts: 3.84 us -> 3.84 us
  transfers between devices with their start and end apart: 29 -> 29, of which waited for: 11 -> 13; matrix products, arithmetic and copies ran while one was open for 19% -> 19% of each run, Pallas kernels for 0% -> 5%
where the time goes in v12:
time: 114 us; the launch traced here: 113 us
  starting transfers between devices  38.9 us (34%)
  waiting for transfers between devices  16.7 us (15%)
  local copies, waits for them, and re-layouts  16 us (14%)
  between operations  14 us (12%)
  Pallas kernels  10.4 us (9%)
  other arithmetic  9.83 us (9%)
  matrix products  7.16 us (6%)
    ppermute x12, starting transfers between devices, halve(): lax.ppermute(send.astype(wire), axis, pairs(axis, mask)).astype(x.dtype)  19.1 us
    ppermute x12, starting transfers between devices, double(): recv = lax.ppermute(y, axis, pairs(axis, mask))  15.3 us
    pallas_call x2, Pallas kernels, restrict(): pl.pallas_call(functools.partial(restrict_kernel, upper=upper), out_shape...  10.4 us
    ppermute x12, waiting for transfers between devices, halve(): lax.ppermute(send.astype(wire), axis, pairs(axis, mask)).astype(x.dtype)  7.95 us
    ppermute x12, waiting for transfers between devices, double(): recv = lax.ppermute(y, axis, pairs(axis, mask))  7.31 us
    dot_general x1, matrix products, per_device(): jnp.einsum('jerb,jebc->jrc', picked, inverse_blocks, preferred_element_ty...  4.91 us
    gather x1, local copies, waits for them, and re-layouts, per_device(): picked = jnp.take(extended, margin, axis=0)  4.18 us
    unnamed x26, local copies, waits for them, and re-layouts  3.84 us
  transfers between devices with their start and end apart: 29, of which 13 were waited for; matrix products, arithmetic and copies ran while one was open for 19% of the time, Pallas kernels for 5%

profile of v12, /device:TPU:0, one launch (start us, length us, event | category | flops | bytes accessed | tf_op | source)
XLA Modules:
  0.0 113.0 jit_solution(5863070809216574280)
XLA Ops:
  8.1 5.2 %shard_map.74 = f32[12,256,128]{2,1,0:T(8,128)} custom-call(s32[8]{0:T(128)} %reshape.1691.links, s32[1]{0:T(128)} %bitcast.half, bf16[4,512,256]{2,1,0:T(8,128)(2,1)} %residual_ref.3, bf16[4,2,256,128]{3,2,1,0:T(8,128)(2,1)} %basis_ref.3), custom_call_target="tpu_custom_call" | custom-call | flops 134217728 | bytes 3145728 | tf_op jit(solution)/shard_map/pallas_call | solution.py:36
  14.6 2.7 %collective-permute-start = (bf16[1,512,256]{2,1,0:T(8,128)(2,1)}, bf16[1,512,256]{2,1,0:T(8,128)(2,1)}, u32[]{:S(2)}, u32[]{:S(2)}) collective-permute-start(bf16[1,512,256]{2,1,0:T(8,128)(2,1)} %get-tuple-element.23), channel_id=1, source_target_pairs={{0,1},{1,2},{2,3},{3,4},{4,5},{5,6},{6,7},{7,8},{8,9},{9,10},{10,1... | collective-permute-start | bytes 786440 | tf_op jit(solution)/shard_map/ppermute | solution.py:65
  17.3 1.3 %collective-permute-start.1 = (bf16[1,512,256]{2,1,0:T(8,128)(2,1)}, bf16[1,512,256]{2,1,0:T(8,128)(2,1)}, u32[]{:S(2)}, u32[]{:S(2)}) collective-permute-start(bf16[1,512,256]{2,1,0:T(8,128)(2,1)} %get-tuple-element.24), channel_id=1, source_target_pairs={{1,0},{2,1},{3,2},{4,3},{5,4},{6,5},{7,6},{8,7},{9,8},{10,9},{11,1... | collective-permute-start | bytes 786440 | tf_op jit(solution)/shard_map/ppermute | solution.py:67
  19.7 5.2 %shard_map.73 = f32[12,256,128]{2,1,0:T(8,128)} custom-call(s32[8]{0:T(128)} %reshape.1691.links, s32[1]{0:T(128)} %bitcast.half, bf16[4,512,256]{2,1,0:T(8,128)(2,1)} %residual_ref.3, bf16[4,2,256,128]{3,2,1,0:T(8,128)(2,1)} %basis_ref.3), custom_call_target="tpu_custom_call" | custom-call | flops 134217728 | bytes 3145728 | tf_op jit(solution)/shard_map/pallas_call | solution.py:36
  25.0 2.5 %pad_maximum_fusion = bf16[6,512,256]{2,1,0:T(8,128)(2,1)} fusion(bf16[1,512,256]{2,1,0:T(8,128)(2,1)} %collective-permute-done.1, bf16[4,512,256]{2,1,0:T(8,128)(2,1)S(1)} %copy-done.2, bf16[1,512,256]{2,1,0:T(8,128)(2,1)} %collective-permute-done), kind=kLoop, calls=%fused_computation.13 | loop fusion | flops 1572864 | bytes 3145728 | tf_op jit(solution)/shard_map/concatenate | solution.py:63
  27.5 1.6 %add.169 = f32[12,256,128]{2,1,0:T(8,128)S(1)} add(f32[12,256,128]{2,1,0:T(8,128)S(1)} %copy-done.3, f32[12,256,128]{2,1,0:T(8,128)} %collective-permute-done.2) | non-fusion elementwise | flops 393216 | bytes 4718592 | tf_op jit(solution)/shard_map/add | solution.py:139
  30.8 6.0 %collective-permute-start.5 = (f32[4,1,2,2,1,2,16,128]{7,6,5,4,3,2,0,1:T(8,128)}, f32[4,1,2,2,1,2,16,128]{7,6,5,4,3,2,0,1:T(8,128)}, u32[]{:S(2)}, u32[]{:S(2)}) collective-permute-start(f32[4,1,2,2,1,2,16,128]{7,6,5,4,3,2,0,1:T(8,128)} %constant_dynamic-slice_fusion.9), channel_id=1, source_target_pairs={{0,8},{4,12},{8,0},{12,4},{16,24},{20,28},{24,16},{28,20},{1,9},{5... | collective-permute-start | bytes 786440 | tf_op jit(solution)/shard_map/ppermute | solution.py:98
  38.8 4.2 %gather_fusion = bf16[16,512,256]{2,1,0:T(8,128)(2,1)} fusion(bf16[6,512,256]{2,1,0:T(8,128)(2,1)} %pad_maximum_fusion, s32[1024]{0:T(1024)S(1)} %pad_clamp_fusion.2), kind=kCustom, calls=%fused_computation.2 | custom fusion | bytes 8388672 | tf_op jit(solution)/shard_map/jit(_take)/gather | solution.py:143
  43.0 4.9 %fusion.5 = f32[4,512,256]{2,1,0:T(8,128)} fusion(bf16[4,4,256,256]{3,2,1,0:T(8,128)(2,1)S(1)} %copy-done, bf16[4,4,512,256]{3,2,1,0:T(8,128)(2,1)} %bitcast.87, pred[4,4]{1,0:T(4,128)(4,1)S(1)} %compare_and_fusion.2), kind=kOutput, calls=%fused_computation.10 | convolution fusion | flops 1075838976 | bytes 8388624 | tf_op jit(solution)/shard_map/jerb,jebc->jrc/dot_general | solution.py:144
  52.2 2.9 %collective-permute-start.12 = (f32[4,1,2,2,1,1,16,128]{7,6,5,4,3,2,0,1:T(8,128)S(1)}, f32[4,1,2,2,1,1,16,128]{7,6,5,4,3,2,0,1:T(8,128)S(1)}, u32[]{:S(2)}, u32[]{:S(2)}) collective-permute-start(f32[4,1,2,2,1,1,16,128]{7,6,5,4,3,2,0,1:T(8,128)S(1)} %constant_dynamic-slice_fusion.2), channel_id=1, source_target_pairs={{0,16},{4,20},{8,24},{12,28},{16,0},{20,4},{24,8},{28,12},{1,17},{... | collective-permute-start | bytes 393224 | tf_op jit(solution)/shard_map/ppermute | solution.py:98
  55.1 1.8 %collective-permute-done.6 = f32[4,1,1,1,2,2,16,128]{7,6,5,4,3,2,0,1:T(8,128)S(1)} collective-permute-done((f32[4,1,1,1,2,2,16,128]{7,6,5,4,3,2,0,1:T(8,128)S(1)}, f32[4,1,1,1,2,2,16,128]{7,6,5,4,3,2,0,1:T(8,128)S(1)}, u32[]{:S(2)}, u32[]{:S(2)}) %collective-permute-start.6) | collective-permute-done | bytes 131104 | tf_op jit(solution)/shard_map/ppermute | solution.py:98
  57.4 2.4 %collective-permute-done.9 = f32[4,1,2,1,1,2,16,128]{7,6,5,4,3,2,0,1:T(8,128)S(1)} collective-permute-done((f32[4,1,2,1,1,2,16,128]{7,6,5,4,3,2,0,1:T(8,128)S(1)}, f32[4,1,2,1,1,2,16,128]{7,6,5,4,3,2,0,1:T(8,128)S(1)}, u32[]{:S(2)}, u32[]{:S(2)}) %collective-permute-start.9) | collective-permute-done | bytes 131104 | tf_op jit(solution)/shard_map/ppermute | solution.py:98
  60.3 2.5 %collective-permute-start.13 = (f32[4,1,1,2,1,1,16,128]{7,6,5,4,3,2,0,1:T(8,128)S(1)}, f32[4,1,1,2,1,1,16,128]{7,6,5,4,3,2,0,1:T(8,128)S(1)}, u32[]{:S(2)}, u32[]{:S(2)}) collective-permute-start(f32[4,1,1,2,1,1,16,128]{7,6,5,4,3,2,0,1:T(8,128)S(1)} %constant_dynamic-slice_fusion.1), channel_id=1, source_target_pairs={{0,2},{1,3},{2,0},{3,1},{4,6},{5,7},{6,4},{7,5},{8,10},{9,11},{10,... | collective-permute-start | bytes 196616 | tf_op jit(solution)/shard_map/ppermute | solution.py:98
  62.8 1.4 %collective-permute-start.8 = (f32[4,1,1,1,1,1,16,128]{7,6,5,4,3,2,0,1:T(8,128)S(1)}, f32[4,1,1,1,1,1,16,128]{7,6,5,4,3,2,0,1:T(8,128)S(1)}, u32[]{:S(2)}, u32[]{:S(2)}) collective-permute-start(f32[4,1,1,1,1,1,16,128]{7,6,5,4,3,2,0,1:T(8,128)S(1)} %constant_dynamic-slice_fusion.6), channel_id=1, source_target_pairs={{0,16},{4,20},{8,24},{12,28},{16,0},{20,4},{24,8},{28,12},{1,17},{... | collective-permute-start | bytes 98312 | tf_op jit(solution)/shard_map/ppermute | solution.py:98
  65.3 1.6 %collective-permute-start.11 = (f32[4,1,1,1,1,1,16,128]{7,6,5,4,3,2,0,1:T(8,128)S(1)}, f32[4,1,1,1,1,1,16,128]{7,6,5,4,3,2,0,1:T(8,128)S(1)}, u32[]{:S(2)}, u32[]{:S(2)}) collective-permute-start(f32[4,1,1,1,1,1,16,128]{7,6,5,4,3,2,0,1:T(8,128)S(1)} %constant_dynamic-slice_fusion.3), channel_id=1, source_target_pairs={{0,2},{1,3},{2,0},{3,1},{4,6},{5,7},{6,4},{7,5},{8,10},{9,11},{10,... | collective-permute-start | bytes 98312 | tf_op jit(solution)/shard_map/ppermute | solution.py:98
  67.0 1.3 %collective-permute-start.14 = (f32[4,1,1,1,1,1,16,128]{7,6,5,4,3,2,0,1:T(8,128)S(1)}, f32[4,1,1,1,1,1,16,128]{7,6,5,4,3,2,0,1:T(8,128)S(1)}, u32[]{:S(2)}, u32[]{:S(2)}) collective-permute-start(f32[4,1,1,1,1,1,16,128]{7,6,5,4,3,2,0,1:T(8,128)S(1)} %constant_dynamic-slice_fusion), channel_id=1, source_target_pairs={{0,4},{4,0},{8,12},{12,8},{16,20},{20,16},{24,28},{28,24},{1,5},{5... | collective-permute-start | bytes 98312 | tf_op jit(solution)/shard_map/ppermute | solution.py:98
  69.3 1.7 %collective-permute-done.14 = f32[4,1,1,1,1,1,16,128]{7,6,5,4,3,2,0,1:T(8,128)S(1)} collective-permute-done((f32[4,1,1,1,1,1,16,128]{7,6,5,4,3,2,0,1:T(8,128)S(1)}, f32[4,1,1,1,1,1,16,128]{7,6,5,4,3,2,0,1:T(8,128)S(1)}, u32[]{:S(2)}, u32[]{:S(2)}) %collective-permute-start.14) | collective-permute-done | bytes 32800 | tf_op jit(solution)/shard_map/ppermute | solution.py:98
  73.0 1.8 %fusion.13 = bf16[12,16,128]{2,1,0:T(8,128)(2,1)S(1)} fusion(bf16[12,4,136,128]{3,2,1,0:T(8,128)(2,1)} %all-gather.2.cloned.1.call-done, bf16[12,4,16,128]{3,2,1,0:T(8,128)(2,1)S(1)} %bitcast.97, pred[12,4]{1,0:T(8,128)(4,1)S(1)} %copy.62), kind=kOutput, calls=%fused_computation.15 | convolution fusion | flops 25288704 | bytes 1818672 | tf_op jit(solution)/shard_map/nerc,necd->nrd/dot_general | solution.py:152
  76.3 1.7 %collective-permute-start.23 = (bf16[4,1,1,1,1,1,16,128]{7,6,0,5,4,3,2,1:T(8,128)(2,1)S(1)}, bf16[4,1,1,1,1,1,16,128]{7,6,0,5,4,3,2,1:T(8,128)(2,1)S(1)}, u32[]{:S(2)}, u32[]{:S(2)}) collective-permute-start(bf16[4,1,1,1,1,1,16,128]{7,6,0,5,4,3,2,1:T(8,128)(2,1)S(1)} %get-tuple-element.28), channel_id=1, source_target_pairs={{0,4},{4,0},{8,12},{12,8},{16,20},{20,16},{24,28},{28,24},{1,5},{5... | collective-permute-start | bytes 49160 | tf_op jit(solution)/shard_map/ppermute | solution.py:103
  78.0 1.5 %collective-permute-done.15 = bf16[4,1,1,1,1,1,16,128]{7,6,0,5,4,3,2,1:T(8,128)(2,1)S(1)} collective-permute-done((bf16[4,1,1,1,1,1,16,128]{7,6,0,5,4,3,2,1:T(8,128)(2,1)S(1)}, bf16[4,1,1,1,1,1,16,128]{7,6,0,5,4,3,2,1:T(8,128)(2,1)S(1)}, u32[]{:S(2)}, u32[]{:S(2)}) %collective-permute-start.15) | collective-permute-done | bytes 16416 | tf_op jit(solution)/shard_map/ppermute | solution.py:103
  79.5 1.2 %collective-permute-start.16 = (bf16[4,1,1,1,1,2,16,128]{7,6,0,5,4,3,2,1:T(8,128)(2,1)S(1)}, bf16[4,1,1,1,1,2,16,128]{7,6,0,5,4,3,2,1:T(8,128)(2,1)S(1)}, u32[]{:S(2)}, u32[]{:S(2)}) collective-permute-start(bf16[4,1,1,1,1,2,16,128]{7,6,0,5,4,3,2,1:T(8,128)(2,1)S(1)} %maximum_select_fusion.14), channel_id=1, source_target_pairs={{0,8},{4,12},{8,0},{12,4},{16,24},{20,28},{24,16},{28,20},{1,9},{5... | collective-permute-start | bytes 98312 | tf_op jit(solution)/shard_map/ppermute | solution.py:103
  80.8 2.1 %collective-permute-start.20 = (bf16[4,1,2,1,1,1,16,128]{7,6,0,5,4,3,2,1:T(8,128)(2,1)S(1)}, bf16[4,1,2,1,1,1,16,128]{7,6,0,5,4,3,2,1:T(8,128)(2,1)S(1)}, u32[]{:S(2)}, u32[]{:S(2)}) collective-permute-start(bf16[4,1,2,1,1,1,16,128]{7,6,0,5,4,3,2,1:T(8,128)(2,1)S(1)} %maximum_select_fusion.16), channel_id=1, source_target_pairs={{0,16},{4,20},{8,24},{12,28},{16,0},{20,4},{24,8},{28,12},{1,17},{... | collective-permute-start | bytes 98312 | tf_op jit(solution)/shard_map/ppermute | solution.py:103
  84.0 1.8 %collective-permute-start.17 = (bf16[4,1,1,1,2,2,16,128]{7,6,0,5,4,3,2,1:T(8,128)(2,1)S(1)}, bf16[4,1,1,1,2,2,16,128]{7,6,0,5,4,3,2,1:T(8,128)(2,1)S(1)}, u32[]{:S(2)}, u32[]{:S(2)}) collective-permute-start(bf16[4,1,1,1,2,2,16,128]{7,6,0,5,4,3,2,1:T(8,128)(2,1)S(1)} %maximum_select_fusion.9), channel_id=1, source_target_pairs={{0,4},{4,0},{8,12},{12,8},{16,20},{20,16},{24,28},{28,24},{1,5},{5... | collective-permute-start | bytes 196616 | tf_op jit(solution)/shard_map/ppermute | solution.py:103
  86.9 1.5 %collective-permute-start.25 = (bf16[4,1,2,2,1,1,16,128]{7,6,0,5,4,3,2,1:T(8,128)(2,1)S(1)}, bf16[4,1,2,2,1,1,16,128]{7,6,0,5,4,3,2,1:T(8,128)(2,1)S(1)}, u32[]{:S(2)}, u32[]{:S(2)}) collective-permute-start(bf16[4,1,2,2,1,1,16,128]{7,6,0,5,4,3,2,1:T(8,128)(2,1)S(1)} %fusion.29), channel_id=1, source_target_pairs={{0,16},{4,20},{8,24},{12,28},{16,0},{20,4},{24,8},{28,12},{1,17},{... | collective-permute-start | bytes 196616 | tf_op jit(solution)/shard_map/ppermute | solution.py:103
  88.4 1.7 %collective-permute-start.18 = (bf16[4,1,1,2,2,2,16,128]{7,6,0,5,4,3,2,1:T(8,128)(2,1)S(1)}, bf16[4,1,1,2,2,2,16,128]{7,6,0,5,4,3,2,1:T(8,128)(2,1)S(1)}, u32[]{:S(2)}, u32[]{:S(2)}) collective-permute-start(bf16[4,1,1,2,2,2,16,128]{7,6,0,5,4,3,2,1:T(8,128)(2,1)S(1)} %maximum_select_fusion.5), channel_id=1, source_target_pairs={{0,2},{1,3},{2,0},{3,1},{4,6},{5,7},{6,4},{7,5},{8,10},{9,11},{10,... | collective-permute-start | bytes 393224 | tf_op jit(solution)/shard_map/ppermute | solution.py:103
  90.2 1.4 %collective-permute-start.22 = (bf16[4,1,2,1,2,2,16,128]{7,6,0,5,4,3,2,1:T(8,128)(2,1)S(1)}, bf16[4,1,2,1,2,2,16,128]{7,6,0,5,4,3,2,1:T(8,128)(2,1)S(1)}, u32[]{:S(2)}, u32[]{:S(2)}) collective-permute-start(bf16[4,1,2,1,2,2,16,128]{7,6,0,5,4,3,2,1:T(8,128)(2,1)S(1)} %maximum_select_fusion.6), channel_id=1, source_target_pairs={{0,4},{4,0},{8,12},{12,8},{16,20},{20,16},{24,28},{28,24},{1,5},{5... | collective-permute-start | bytes 393224 | tf_op jit(solution)/shard_map/ppermute | solution.py:103
  91.6 1.2 %collective-permute-done.25 = bf16[4,1,2,2,1,1,16,128]{7,6,0,5,4,3,2,1:T(8,128)(2,1)S(1)} collective-permute-done((bf16[4,1,2,2,1,1,16,128]{7,6,0,5,4,3,2,1:T(8,128)(2,1)S(1)}, bf16[4,1,2,2,1,1,16,128]{7,6,0,5,4,3,2,1:T(8,128)(2,1)S(1)}, u32[]{:S(2)}, u32[]{:S(2)}) %collective-permute-start.25) | collective-permute-done | bytes 65568 | tf_op jit(solution)/shard_map/ppermute | solution.py:103
  93.5 1.7 %collective-permute-done.22 = bf16[4,1,2,1,2,2,16,128]{7,6,0,5,4,3,2,1:T(8,128)(2,1)S(1)} collective-permute-done((bf16[4,1,2,1,2,2,16,128]{7,6,0,5,4,3,2,1:T(8,128)(2,1)S(1)}, bf16[4,1,2,1,2,2,16,128]{7,6,0,5,4,3,2,1:T(8,128)(2,1)S(1)}, u32[]{:S(2)}, u32[]{:S(2)}) %collective-permute-start.22) | collective-permute-done | bytes 131104 | tf_op jit(solution)/shard_map/ppermute | solution.py:103
  95.3 2.6 %collective-permute-done.26 = bf16[4,1,2,2,1,2,16,128]{7,6,0,5,4,3,2,1:T(8,128)(2,1)S(1)} collective-permute-done((bf16[4,1,2,2,1,2,16,128]{7,6,0,5,4,3,2,1:T(8,128)(2,1)S(1)}, bf16[4,1,2,2,1,2,16,128]{7,6,0,5,4,3,2,1:T(8,128)(2,1)S(1)}, u32[]{:S(2)}, u32[]{:S(2)}) %collective-permute-start.26) | collective-permute-done | bytes 131104 | tf_op jit(solution)/shard_map/ppermute | solution.py:103
  99.1 1.4 %collective-permute-done.27 = bf16[12,256,128]{2,1,0:T(8,128)(2,1)} collective-permute-done((bf16[12,256,128]{2,1,0:T(8,128)(2,1)S(1)}, bf16[12,256,128]{2,1,0:T(8,128)(2,1)}, u32[]{:S(2)}, u32[]{:S(2)}) %collective-permute-start.27) | collective-permute-done | bytes 786464 | tf_op jit(solution)/shard_map/ppermute | solution.py:160
  100.5 1.8 %gather_fusion.3 = bf16[8,256,128]{2,1,0:T(8,128)(2,1)S(1)} fusion(bf16[12,256,128]{2,1,0:T(8,128)(2,1)} %collective-permute-done.27, s32[1024]{0:T(1024)S(1)} %pad_clamp_fusion), kind=kCustom, calls=%fused_computation.1.clone | custom fusion | bytes 1048608 | tf_op jit(solution)/shard_map/jit(_take)/gather | solution.py:162
  104.9 1.2 %fusion.3 = bf16[4,512,256]{2,1,0:T(8,128)(2,1)} fusion(f32[4,512,256]{2,1,0:T(8,128)S(1)} %copy-done.4, f32[4,512,256,1]{2,1,3,0:T(8,128)S(1)} %fusion.16), kind=kLoop, calls=%fused_computation.8 | loop fusion | flops 1048576 | bytes 5242880 | tf_op jit(solution)/shard_map/convert_element_type | solution.py:170
  (137 shorter events, 25.3 us)
Async XLA Ops:
  6.5 36.5 %copy-start = (bf16[4,4,256,256]{3,2,1,0:T(8,128)(2,1)S(1)}, bf16[4,4,256,256]{3,2,1,0:T(8,128)(2,1)}, u32[]{:S(2)}) copy-start(bf16[4,4,256,256]{3,2,1,0:T(8,128)(2,1)} %param.11) | copy-start | bytes 6291460
  6.5 64.5 %all-gather.2.cloned.1.call-start = ((), (), s32[]{:S(2)}) async-start(), calls=%async_computation | async-start | bytes 2088960 | tf_op jit(solution)/shard_map/all_gather | solution.py:119
  8.1 10.5 %copy-start.8 = (bf16[3,4,128,128]{3,2,1,0:T(8,128)(2,1)S(1)}, bf16[3,4,128,128]{3,2,1,0:T(8,128)(2,1)}, u32[]{:S(2)}) copy-start(bf16[3,4,128,128]{3,2,1,0:T(8,128)(2,1)} %param.15) | copy-start | bytes 1179652
  8.1 11.4 %copy-start.9 = (s32[4,4]{1,0:T(4,128)S(1)}, s32[4,4]{1,0:T(4,128)}, u32[]{:S(2)}) copy-start(s32[4,4]{1,0:T(4,128)} %param.10) | copy-start | bytes 196
  13.3 14.2 %collective-permute-start.2 = (f32[12,256,128]{2,1,0:T(8,128)}, f32[12,256,128]{2,1,0:T(8,128)}, u32[]{:S(2)}, u32[]{:S(2)}) collective-permute-start(f32[12,256,128]{2,1,0:T(8,128)} %shard_map.74), channel_id=1, source_target_pairs={{0,1},{1,0},{2,3},{3,2},{4,5},{5,4},{6,7},{7,6},{8,9},{9,8},{10,11... | collective-permute-start | bytes 4718600 | tf_op jit(solution)/shard_map/ppermute | solution.py:138
  14.6 10.4 %collective-permute-start = (bf16[1,512,256]{2,1,0:T(8,128)(2,1)}, bf16[1,512,256]{2,1,0:T(8,128)(2,1)}, u32[]{:S(2)}, u32[]{:S(2)}) collective-permute-start(bf16[1,512,256]{2,1,0:T(8,128)(2,1)} %get-tuple-element.23), channel_id=1, source_target_pairs={{0,1},{1,2},{2,3},{3,4},{4,5},{5,6},{6,7},{7,8},{8,9},{9,10},{10,1... | collective-permute-start | bytes 786440 | tf_op jit(solution)/shard_map/ppermute | solution.py:65
  17.3 7.7 %collective-permute-start.1 = (bf16[1,512,256]{2,1,0:T(8,128)(2,1)}, bf16[1,512,256]{2,1,0:T(8,128)(2,1)}, u32[]{:S(2)}, u32[]{:S(2)}) collective-permute-start(bf16[1,512,256]{2,1,0:T(8,128)(2,1)} %get-tuple-element.24), channel_id=1, source_target_pairs={{1,0},{2,1},{3,2},{4,3},{5,4},{6,5},{7,6},{8,7},{9,8},{10,9},{11,1... | collective-permute-start | bytes 786440 | tf_op jit(solution)/shard_map/ppermute | solution.py:67
  30.8 17.2 %collective-permute-start.5 = (f32[4,1,2,2,1,2,16,128]{7,6,5,4,3,2,0,1:T(8,128)}, f32[4,1,2,2,1,2,16,128]{7,6,5,4,3,2,0,1:T(8,128)}, u32[]{:S(2)}, u32[]{:S(2)}) collective-permute-start(f32[4,1,2,2,1,2,16,128]{7,6,5,4,3,2,0,1:T(8,128)} %constant_dynamic-slice_fusion.9), channel_id=1, source_target_pairs={{0,8},{4,12},{8,0},{12,4},{16,24},{20,28},{24,16},{28,20},{1,9},{5... | collective-permute-start | bytes 786440 | tf_op jit(solution)/shard_map/ppermute | solution.py:98
  37.5 11.4 %collective-permute-start.4 = (f32[4,1,2,1,2,2,16,128]{7,6,5,4,3,2,0,1:T(8,128)}, f32[4,1,2,1,2,2,16,128]{7,6,5,4,3,2,0,1:T(8,128)}, u32[]{:S(2)}, u32[]{:S(2)}) collective-permute-start(f32[4,1,2,1,2,2,16,128]{7,6,5,4,3,2,0,1:T(8,128)} %constant_dynamic-slice_fusion.10), channel_id=1, source_target_pairs={{0,4},{4,0},{8,12},{12,8},{16,20},{20,16},{24,28},{28,24},{1,5},{5... | collective-permute-start | bytes 786440 | tf_op jit(solution)/shard_map/ppermute | solution.py:98
  38.2 11.7 %collective-permute-start.3 = (f32[4,1,1,2,2,2,16,128]{7,6,5,4,3,2,0,1:T(8,128)S(1)}, f32[4,1,1,2,2,2,16,128]{7,6,5,4,3,2,0,1:T(8,128)}, u32[]{:S(2)}, u32[]{:S(2)}) collective-permute-start(f32[4,1,1,2,2,2,16,128]{7,6,5,4,3,2,0,1:T(8,128)S(1)} %constant_dynamic-slice_fusion.11), channel_id=1, source_target_pairs={{0,2},{1,3},{2,0},{3,1},{4,6},{5,7},{6,4},{7,5},{8,10},{9,11},{10,... | collective-permute-start | bytes 786440 | tf_op jit(solution)/shard_map/ppermute | solution.py:98
  51.0 5.9 %collective-permute-start.6 = (f32[4,1,1,1,2,2,16,128]{7,6,5,4,3,2,0,1:T(8,128)S(1)}, f32[4,1,1,1,2,2,16,128]{7,6,5,4,3,2,0,1:T(8,128)S(1)}, u32[]{:S(2)}, u32[]{:S(2)}) collective-permute-start(f32[4,1,1,1,2,2,16,128]{7,6,5,4,3,2,0,1:T(8,128)S(1)} %constant_dynamic-slice_fusion.8), channel_id=1, source_target_pairs={{0,4},{4,0},{8,12},{12,8},{16,20},{20,16},{24,28},{28,24},{1,5},{5... | collective-permute-start | bytes 393224 | tf_op jit(solution)/shard_map/ppermute | solution.py:98
  51.9 7.9 %collective-permute-start.9 = (f32[4,1,2,1,1,2,16,128]{7,6,5,4,3,2,0,1:T(8,128)S(1)}, f32[4,1,2,1,1,2,16,128]{7,6,5,4,3,2,0,1:T(8,128)S(1)}, u32[]{:S(2)}, u32[]{:S(2)}) collective-permute-start(f32[4,1,2,1,1,2,16,128]{7,6,5,4,3,2,0,1:T(8,128)S(1)} %constant_dynamic-slice_fusion.5), channel_id=1, source_target_pairs={{0,8},{4,12},{8,0},{12,4},{16,24},{20,28},{24,16},{28,20},{1,9},{5... | collective-permute-start | bytes 393224 | tf_op jit(solution)/shard_map/ppermute | solution.py:98
  52.2 8.1 %collective-permute-start.12 = (f32[4,1,2,2,1,1,16,128]{7,6,5,4,3,2,0,1:T(8,128)S(1)}, f32[4,1,2,2,1,1,16,128]{7,6,5,4,3,2,0,1:T(8,128)S(1)}, u32[]{:S(2)}, u32[]{:S(2)}) collective-permute-start(f32[4,1,2,2,1,1,16,128]{7,6,5,4,3,2,0,1:T(8,128)S(1)} %constant_dynamic-slice_fusion.2), channel_id=1, source_target_pairs={{0,16},{4,20},{8,24},{12,28},{16,0},{20,4},{24,8},{28,12},{1,17},{... | collective-permute-start | bytes 393224 | tf_op jit(solution)/shard_map/ppermute | solution.py:98
  56.9 5.9 %collective-permute-start.7 = (f32[4,1,1,1,1,2,16,128]{7,6,5,4,3,2,0,1:T(8,128)S(1)}, f32[4,1,1,1,1,2,16,128]{7,6,5,4,3,2,0,1:T(8,128)S(1)}, u32[]{:S(2)}, u32[]{:S(2)}) collective-permute-start(f32[4,1,1,1,1,2,16,128]{7,6,5,4,3,2,0,1:T(8,128)S(1)} %constant_dynamic-slice_fusion.7), channel_id=1, source_target_pairs={{0,8},{4,12},{8,0},{12,4},{16,24},{20,28},{24,16},{28,20},{1,9},{5... | collective-permute-start | bytes 196616 | tf_op jit(solution)/shard_map/ppermute | solution.py:98
  59.8 5.4 %collective-permute-start.10 = (f32[4,1,2,1,1,1,16,128]{7,6,5,4,3,2,0,1:T(8,128)S(1)}, f32[4,1,2,1,1,1,16,128]{7,6,5,4,3,2,0,1:T(8,128)S(1)}, u32[]{:S(2)}, u32[]{:S(2)}) collective-permute-start(f32[4,1,2,1,1,1,16,128]{7,6,5,4,3,2,0,1:T(8,128)S(1)} %constant_dynamic-slice_fusion.4), channel_id=1, source_target_pairs={{0,16},{4,20},{8,24},{12,28},{16,0},{20,4},{24,8},{28,12},{1,17},{... | collective-permute-start | bytes 196616 | tf_op jit(solution)/shard_map/ppermute | solution.py:98
  60.3 6.6 %collective-permute-start.13 = (f32[4,1,1,2,1,1,16,128]{7,6,5,4,3,2,0,1:T(8,128)S(1)}, f32[4,1,1,2,1,1,16,128]{7,6,5,4,3,2,0,1:T(8,128)S(1)}, u32[]{:S(2)}, u32[]{:S(2)}) collective-permute-start(f32[4,1,1,2,1,1,16,128]{7,6,5,4,3,2,0,1:T(8,128)S(1)} %constant_dynamic-slice_fusion.1), channel_id=1, source_target_pairs={{0,2},{1,3},{2,0},{3,1},{4,6},{5,7},{6,4},{7,5},{8,10},{9,11},{10,... | collective-permute-start | bytes 196616 | tf_op jit(solution)/shard_map/ppermute | solution.py:98
  62.8 5.5 %collective-permute-start.8 = (f32[4,1,1,1,1,1,16,128]{7,6,5,4,3,2,0,1:T(8,128)S(1)}, f32[4,1,1,1,1,1,16,128]{7,6,5,4,3,2,0,1:T(8,128)S(1)}, u32[]{:S(2)}, u32[]{:S(2)}) collective-permute-start(f32[4,1,1,1,1,1,16,128]{7,6,5,4,3,2,0,1:T(8,128)S(1)} %constant_dynamic-slice_fusion.6), channel_id=1, source_target_pairs={{0,16},{4,20},{8,24},{12,28},{16,0},{20,4},{24,8},{28,12},{1,17},{... | collective-permute-start | bytes 98312 | tf_op jit(solution)/shard_map/ppermute | solution.py:98
  65.3 4.0 %collective-permute-start.11 = (f32[4,1,1,1,1,1,16,128]{7,6,5,4,3,2,0,1:T(8,128)S(1)}, f32[4,1,1,1,1,1,16,128]{7,6,5,4,3,2,0,1:T(8,128)S(1)}, u32[]{:S(2)}, u32[]{:S(2)}) collective-permute-start(f32[4,1,1,1,1,1,16,128]{7,6,5,4,3,2,0,1:T(8,128)S(1)} %constant_dynamic-slice_fusion.3), channel_id=1, source_target_pairs={{0,2},{1,3},{2,0},{3,1},{4,6},{5,7},{6,4},{7,5},{8,10},{9,11},{10,... | collective-permute-start | bytes 98312 | tf_op jit(solution)/shard_map/ppermute | solution.py:98
  67.0 4.0 %collective-permute-start.14 = (f32[4,1,1,1,1,1,16,128]{7,6,5,4,3,2,0,1:T(8,128)S(1)}, f32[4,1,1,1,1,1,16,128]{7,6,5,4,3,2,0,1:T(8,128)S(1)}, u32[]{:S(2)}, u32[]{:S(2)}) collective-permute-start(f32[4,1,1,1,1,1,16,128]{7,6,5,4,3,2,0,1:T(8,128)S(1)} %constant_dynamic-slice_fusion), channel_id=1, source_target_pairs={{0,4},{4,0},{8,12},{12,8},{16,20},{20,16},{24,28},{28,24},{1,5},{5... | collective-permute-start | bytes 98312 | tf_op jit(solution)/shard_map/ppermute | solution.py:98
  74.8 4.7 %collective-permute-start.15 = (bf16[4,1,1,1,1,1,16,128]{7,6,0,5,4,3,2,1:T(8,128)(2,1)S(1)}, bf16[4,1,1,1,1,1,16,128]{7,6,0,5,4,3,2,1:T(8,128)(2,1)S(1)}, u32[]{:S(2)}, u32[]{:S(2)}) collective-permute-start(bf16[4,1,1,1,1,1,16,128]{7,6,0,5,4,3,2,1:T(8,128)(2,1)S(1)} %get-tuple-element.26), channel_id=1, source_target_pairs={{0,16},{4,20},{8,24},{12,28},{16,0},{20,4},{24,8},{28,12},{1,17},{... | collective-permute-start | bytes 49160 | tf_op jit(solution)/shard_map/ppermute | solution.py:103
  76.0 4.8 %collective-permute-start.19 = (bf16[4,1,1,1,1,1,16,128]{7,6,0,5,4,3,2,1:T(8,128)(2,1)S(1)}, bf16[4,1,1,1,1,1,16,128]{7,6,0,5,4,3,2,1:T(8,128)(2,1)S(1)}, u32[]{:S(2)}, u32[]{:S(2)}) collective-permute-start(bf16[4,1,1,1,1,1,16,128]{7,6,0,5,4,3,2,1:T(8,128)(2,1)S(1)} %get-tuple-element.27), channel_id=1, source_target_pairs={{0,2},{1,3},{2,0},{3,1},{4,6},{5,7},{6,4},{7,5},{8,10},{9,11},{10,... | collective-permute-start | bytes 49160 | tf_op jit(solution)/shard_map/ppermute | solution.py:103
  76.3 6.6 %collective-permute-start.23 = (bf16[4,1,1,1,1,1,16,128]{7,6,0,5,4,3,2,1:T(8,128)(2,1)S(1)}, bf16[4,1,1,1,1,1,16,128]{7,6,0,5,4,3,2,1:T(8,128)(2,1)S(1)}, u32[]{:S(2)}, u32[]{:S(2)}) collective-permute-start(bf16[4,1,1,1,1,1,16,128]{7,6,0,5,4,3,2,1:T(8,128)(2,1)S(1)} %get-tuple-element.28), channel_id=1, source_target_pairs={{0,4},{4,0},{8,12},{12,8},{16,20},{20,16},{24,28},{28,24},{1,5},{5... | collective-permute-start | bytes 49160 | tf_op jit(solution)/shard_map/ppermute | solution.py:103
  79.5 4.5 %collective-permute-start.16 = (bf16[4,1,1,1,1,2,16,128]{7,6,0,5,4,3,2,1:T(8,128)(2,1)S(1)}, bf16[4,1,1,1,1,2,16,128]{7,6,0,5,4,3,2,1:T(8,128)(2,1)S(1)}, u32[]{:S(2)}, u32[]{:S(2)}) collective-permute-start(bf16[4,1,1,1,1,2,16,128]{7,6,0,5,4,3,2,1:T(8,128)(2,1)S(1)} %maximum_select_fusion.14), channel_id=1, source_target_pairs={{0,8},{4,12},{8,0},{12,4},{16,24},{20,28},{24,16},{28,20},{1,9},{5... | collective-permute-start | bytes 98312 | tf_op jit(solution)/shard_map/ppermute | solution.py:103
  80.8 5.0 %collective-permute-start.20 = (bf16[4,1,2,1,1,1,16,128]{7,6,0,5,4,3,2,1:T(8,128)(2,1)S(1)}, bf16[4,1,2,1,1,1,16,128]{7,6,0,5,4,3,2,1:T(8,128)(2,1)S(1)}, u32[]{:S(2)}, u32[]{:S(2)}) collective-permute-start(bf16[4,1,2,1,1,1,16,128]{7,6,0,5,4,3,2,1:T(8,128)(2,1)S(1)} %maximum_select_fusion.16), channel_id=1, source_target_pairs={{0,16},{4,20},{8,24},{12,28},{16,0},{20,4},{24,8},{28,12},{1,17},{... | collective-permute-start | bytes 98312 | tf_op jit(solution)/shard_map/ppermute | solution.py:103
  82.9 4.0 %collective-permute-start.24 = (bf16[4,1,1,2,1,1,16,128]{7,6,0,5,4,3,2,1:T(8,128)(2,1)S(1)}, bf16[4,1,1,2,1,1,16,128]{7,6,0,5,4,3,2,1:T(8,128)(2,1)S(1)}, u32[]{:S(2)}, u32[]{:S(2)}) collective-permute-start(bf16[4,1,1,2,1,1,16,128]{7,6,0,5,4,3,2,1:T(8,128)(2,1)S(1)} %maximum_select_fusion.18), channel_id=1, source_target_pairs={{0,2},{1,3},{2,0},{3,1},{4,6},{5,7},{6,4},{7,5},{8,10},{9,11},{10,... | collective-permute-start | bytes 98312 | tf_op jit(solution)/shard_map/ppermute | solution.py:103
  84.0 4.4 %collective-permute-start.17 = (bf16[4,1,1,1,2,2,16,128]{7,6,0,5,4,3,2,1:T(8,128)(2,1)S(1)}, bf16[4,1,1,1,2,2,16,128]{7,6,0,5,4,3,2,1:T(8,128)(2,1)S(1)}, u32[]{:S(2)}, u32[]{:S(2)}) collective-permute-start(bf16[4,1,1,1,2,2,16,128]{7,6,0,5,4,3,2,1:T(8,128)(2,1)S(1)} %maximum_select_fusion.9), channel_id=1, source_target_pairs={{0,4},{4,0},{8,12},{12,8},{16,20},{20,16},{24,28},{28,24},{1,5},{5... | collective-permute-start | bytes 196616 | tf_op jit(solution)/shard_map/ppermute | solution.py:103
  85.8 4.4 %collective-permute-start.21 = (bf16[4,1,2,1,1,2,16,128]{7,6,0,5,4,3,2,1:T(8,128)(2,1)S(1)}, bf16[4,1,2,1,1,2,16,128]{7,6,0,5,4,3,2,1:T(8,128)(2,1)S(1)}, u32[]{:S(2)}, u32[]{:S(2)}) collective-permute-start(bf16[4,1,2,1,1,2,16,128]{7,6,0,5,4,3,2,1:T(8,128)(2,1)S(1)} %maximum_select_fusion.11), channel_id=1, source_target_pairs={{0,8},{4,12},{8,0},{12,4},{16,24},{20,28},{24,16},{28,20},{1,9},{5... | collective-permute-start | bytes 196616 | tf_op jit(solution)/shard_map/ppermute | solution.py:103
  86.9 5.9 %collective-permute-start.25 = (bf16[4,1,2,2,1,1,16,128]{7,6,0,5,4,3,2,1:T(8,128)(2,1)S(1)}, bf16[4,1,2,2,1,1,16,128]{7,6,0,5,4,3,2,1:T(8,128)(2,1)S(1)}, u32[]{:S(2)}, u32[]{:S(2)}) collective-permute-start(bf16[4,1,2,2,1,1,16,128]{7,6,0,5,4,3,2,1:T(8,128)(2,1)S(1)} %fusion.29), channel_id=1, source_target_pairs={{0,16},{4,20},{8,24},{12,28},{16,0},{20,4},{24,8},{28,12},{1,17},{... | collective-permute-start | bytes 196616 | tf_op jit(solution)/shard_map/ppermute | solution.py:103
  88.4 5.0 %collective-permute-start.18 = (bf16[4,1,1,2,2,2,16,128]{7,6,0,5,4,3,2,1:T(8,128)(2,1)S(1)}, bf16[4,1,1,2,2,2,16,128]{7,6,0,5,4,3,2,1:T(8,128)(2,1)S(1)}, u32[]{:S(2)}, u32[]{:S(2)}) collective-permute-start(bf16[4,1,1,2,2,2,16,128]{7,6,0,5,4,3,2,1:T(8,128)(2,1)S(1)} %maximum_select_fusion.5), channel_id=1, source_target_pairs={{0,2},{1,3},{2,0},{3,1},{4,6},{5,7},{6,4},{7,5},{8,10},{9,11},{10,... | collective-permute-start | bytes 393224 | tf_op jit(solution)/shard_map/ppermute | solution.py:103
  90.2 5.0 %collective-permute-start.22 = (bf16[4,1,2,1,2,2,16,128]{7,6,0,5,4,3,2,1:T(8,128)(2,1)S(1)}, bf16[4,1,2,1,2,2,16,128]{7,6,0,5,4,3,2,1:T(8,128)(2,1)S(1)}, u32[]{:S(2)}, u32[]{:S(2)}) collective-permute-start(bf16[4,1,2,1,2,2,16,128]{7,6,0,5,4,3,2,1:T(8,128)(2,1)S(1)} %maximum_select_fusion.6), channel_id=1, source_target_pairs={{0,4},{4,0},{8,12},{12,8},{16,20},{20,16},{24,28},{28,24},{1,5},{5... | collective-permute-start | bytes 393224 | tf_op jit(solution)/shard_map/ppermute | solution.py:103
  92.8 5.0 %collective-permute-start.26 = (bf16[4,1,2,2,1,2,16,128]{7,6,0,5,4,3,2,1:T(8,128)(2,1)S(1)}, bf16[4,1,2,2,1,2,16,128]{7,6,0,5,4,3,2,1:T(8,128)(2,1)S(1)}, u32[]{:S(2)}, u32[]{:S(2)}) collective-permute-start(bf16[4,1,2,2,1,2,16,128]{7,6,0,5,4,3,2,1:T(8,128)(2,1)S(1)} %maximum_select_fusion.7), channel_id=1, source_target_pairs={{0,8},{4,12},{8,0},{12,4},{16,24},{20,28},{24,16},{28,20},{1,9},{5... | collective-permute-start | bytes 393224 | tf_op jit(solution)/shard_map/ppermute | solution.py:103
  98.0 2.5 %collective-permute-start.27 = (bf16[12,256,128]{2,1,0:T(8,128)(2,1)S(1)}, bf16[12,256,128]{2,1,0:T(8,128)(2,1)}, u32[]{:S(2)}, u32[]{:S(2)}) collective-permute-start(bf16[12,256,128]{2,1,0:T(8,128)(2,1)S(1)} %pad_maximum_fusion.1), channel_id=1, source_target_pairs={{0,1},{1,0},{2,3},{3,2},{4,5},{5,4},{6,7},{7,6},{8,9},{9,8},{10,11... | collective-permute-start | bytes 2359304 | tf_op jit(solution)/shard_map/ppermute | solution.py:160
  (9 other events, 38.6 us)
Sparse Core Ops, SparseCore 0:
  19.6 25.6 all-gather.1

commit v13 on v12

--- a/solution.py
+++ b/solution.py
@@ -116,7 +116,12 @@
 def per_device(residual, margin, inverse_blocks, interface, basis, coarse_pattern, coarse_inverse):
     rows, cols = coarse_inverse.shape[-2:]
     tags = jnp.broadcast_to(coarse_pattern.astype(jnp.bfloat16)[:, :, None, None], coarse_pattern.shape + (8, cols))
-    packed = lax.all_gather(jnp.concatenate([coarse_inverse, tags], axis=2), "coarse", axis=0, tiled=True)
+    packed = jnp.concatenate([coarse_inverse, tags], axis=2)
+    coarse_bits = [bit for bit in device_bits() if bit[0] == "coarse"]
+    packed = packed.reshape((1,) * len(coarse_bits) + packed.shape)
+    for k in reversed(range(len(coarse_bits))):
+        packed = double(packed, len(coarse_bits) - 1 - k, *coarse_bits[k])
+    packed = packed.reshape((-1,) + packed.shape[len(coarse_bits) + 1:])
     inverse_all = packed[:, :, :rows, :]
     pattern_all = packed[:, :, rows, 0].astype(jnp.int32)
     extended = with_halo(residual, ((("sub", "coarse"), 0),), 1)

time: 114 us -> 112 us (0.982)
  between operations: 14 us -> 0.6 us
  other arithmetic: 9.83 us -> 16.8 us
  waiting for transfers between devices: 16.7 us -> 20.2 us
  starting transfers between devices: 38.9 us -> 40.1 us
    select_n x12 -> x14, other arithmetic: 0.19 us -> 4.86 us  [double(): jnp.where(v == 0, jnp.concatenate([y, recv], axis=dim), jnp.concatenate([...]
    ppermute x12 -> x14, starting transfers between devices: 15.3 us -> 18.6 us  [double(): recv = lax.ppermute(y, axis, pairs(axis, mask))]
    ppermute x12 -> x14, waiting for transfers between devices: 7.31 us -> 10.2 us  [double(): recv = lax.ppermute(y, axis, pairs(axis, mask))]
    concatenate x6 -> x7, other arithmetic: 0.07 us -> 1.86 us  [double(): jnp.concatenate([y, recv], axis=dim)]
    ppermute x12, starting transfers between devices: 19.1 us -> 17.7 us  [halve(): lax.ppermute(send.astype(wire), axis, pairs(axis, mask)).astype(x.dtype)]
    unnamed x26 -> x20, local copies, waits for them, and re-layouts: 3.84 us -> 4.9 us
  transfers between devices with their start and end apart: 29 -> 30, of which waited for: 13 -> 15; matrix products, arithmetic and copies ran while one was open for 19% -> 21% of each run, Pallas kernels for 5% -> 9%
where the time goes in v13:
time: 112 us; the launch traced here: 111 us
  starting transfers between devices  40.1 us (36%)
  waiting for transfers between devices  20.2 us (18%)
  other arithmetic  16.8 us (15%)
  local copies, waits for them, and re-layouts  16 us (14%)
  Pallas kernels  10.3 us (9%)
  matrix products  7.17 us (6%)
    ppermute x14, starting transfers between devices, double(): recv = lax.ppermute(y, axis, pairs(axis, mask))  18.6 us
    ppermute x12, starting transfers between devices, halve(): lax.ppermute(send.astype(wire), axis, pairs(axis, mask)).astype(x.dtype)  17.7 us
    pallas_call x2, Pallas kernels, restrict(): pl.pallas_call(functools.partial(restrict_kernel, upper=upper), out_shape...  10.3 us
    ppermute x14, waiting for transfers between devices, double(): recv = lax.ppermute(y, axis, pairs(axis, mask))  10.2 us
    ppermute x12, waiting for transfers between devices, halve(): lax.ppermute(send.astype(wire), axis, pairs(axis, mask)).astype(x.dtype)  8.57 us
    dot_general x1, matrix products, per_device(): jnp.einsum('jerb,jebc->jrc', picked, inverse_blocks, preferred_element_ty...  4.92 us
    unnamed x20, local copies, waits for them, and re-layouts  4.9 us
    select_n x14, other arithmetic, double(): jnp.where(v == 0, jnp.concatenate([y, recv], axis=dim), jnp.concatenate([...  4.86 us
  transfers between devices with their start and end apart: 30, of which 15 were waited for; matrix products, arithmetic and copies ran while one was open for 21% of the time, Pallas kernels for 9%

profile of v13, /device:TPU:0, one launch (start us, length us, event | category | flops | bytes accessed | tf_op | source)
XLA Modules:
  0.0 111.2 jit_solution(9490220932625313813)
XLA Ops:
  0.9 1.8 %maximum_bitcast_fusion = bf16[1,1,3,4,136,128]{5,4,3,2,1,0:T(8,128)(2,1)} fusion(bf16[3,4,8,128]{3,2,1,0:T(8,128)(2,1)S(1)} %broadcast_in_dim.40, bf16[3,4,128,128]{3,2,1,0:T(8,128)(2,1)} %param.15), kind=kLoop, calls=%fused_computation.29 | loop fusion | flops 835584 | bytes 835584 | tf_op jit(solution)/shard_map/concatenate | solution.py:104
  2.7 3.0 %collective-permute-start.6 = (bf16[1,1,3,4,136,128]{5,4,3,2,1,0:T(8,128)(2,1)}, bf16[1,1,3,4,136,128]{5,4,3,2,1,0:T(8,128)(2,1)}, u32[]{:S(2)}, u32[]{:S(2)}) collective-permute-start(bf16[1,1,3,4,136,128]{5,4,3,2,1,0:T(8,128)(2,1)} %maximum_bitcast_fusion), channel_id=1, source_target_pairs={{0,2},{1,3},{2,0},{3,1},{4,6},{5,7},{6,4},{7,5},{8,10},{9,11},{10,... | collective-permute-start | bytes 1253384 | tf_op jit(solution)/shard_map/ppermute | solution.py:103
  7.0 5.2 %shard_map.74 = f32[12,256,128]{2,1,0:T(8,128)} custom-call(s32[8]{0:T(128)} %reshape.1757.links, s32[1]{0:T(128)} %bitcast.half, bf16[4,512,256]{2,1,0:T(8,128)(2,1)} %residual_ref.3, bf16[4,2,256,128]{3,2,1,0:T(8,128)(2,1)} %basis_ref.3), custom_call_target="tpu_custom_call" | custom-call | flops 134217728 | bytes 3145728 | tf_op jit(solution)/shard_map/pallas_call | solution.py:36
  12.2 3.4 %collective-permute-done.6 = bf16[1,1,3,4,136,128]{5,4,3,2,1,0:T(8,128)(2,1)} collective-permute-done((bf16[1,1,3,4,136,128]{5,4,3,2,1,0:T(8,128)(2,1)}, bf16[1,1,3,4,136,128]{5,4,3,2,1,0:T(8,128)(2,1)}, u32[]{:S(2)}, u32[]{:S(2)}) %collective-permute-start.6) | collective-permute-done | bytes 417824 | tf_op jit(solution)/shard_map/ppermute | solution.py:103
  15.6 2.4 %maximum_select_fusion.3 = bf16[2,1,3,4,136,128]{5,4,3,2,1,0:T(8,128)(2,1)} fusion(bf16[1,1,3,4,136,128]{5,4,3,2,1,0:T(8,128)(2,1)} %collective-permute-done.6, bf16[1,1,3,4,136,128]{5,4,3,2,1,0:T(8,128)(2,1)} %maximum_bitcast_fusion, pred[]{:T(512)S(6)} %eq.54), kind=kLoop, calls=%fused_computation.25 | loop fusion | flops 1253376 | bytes 1671169 | tf_op jit(solution)/shard_map/jit(_where)/select_n | solution.py:104
  18.8 2.4 %collective-permute-start = (bf16[1,512,256]{2,1,0:T(8,128)(2,1)}, bf16[1,512,256]{2,1,0:T(8,128)(2,1)S(1)}, u32[]{:S(2)}, u32[]{:S(2)}) collective-permute-start(bf16[1,512,256]{2,1,0:T(8,128)(2,1)} %get-tuple-element.23), channel_id=1, source_target_pairs={{0,1},{1,2},{2,3},{3,4},{4,5},{5,6},{6,7},{7,8},{8,9},{9,10},{10,1... | collective-permute-start | bytes 786440 | tf_op jit(solution)/shard_map/ppermute | solution.py:65
  21.2 1.3 %collective-permute-start.1 = (bf16[1,512,256]{2,1,0:T(8,128)(2,1)S(1)}, bf16[1,512,256]{2,1,0:T(8,128)(2,1)S(1)}, u32[]{:S(2)}, u32[]{:S(2)}) collective-permute-start(bf16[1,512,256]{2,1,0:T(8,128)(2,1)S(1)} %get-tuple-element.24), channel_id=1, source_target_pairs={{1,0},{2,1},{3,2},{4,3},{5,4},{6,5},{7,6},{8,7},{9,8},{10,9},{11,1... | collective-permute-start | bytes 786440 | tf_op jit(solution)/shard_map/ppermute | solution.py:67
  22.7 5.1 %shard_map.73 = f32[12,256,128]{2,1,0:T(8,128)} custom-call(s32[8]{0:T(128)} %reshape.1757.links, s32[1]{0:T(128)} %bitcast.half, bf16[4,512,256]{2,1,0:T(8,128)(2,1)} %residual_ref.3, bf16[4,2,256,128]{3,2,1,0:T(8,128)(2,1)} %basis_ref.3), custom_call_target="tpu_custom_call" | custom-call | flops 134217728 | bytes 3145728 | tf_op jit(solution)/shard_map/pallas_call | solution.py:36
  27.8 2.6 %pad_maximum_fusion = bf16[6,512,256]{2,1,0:T(8,128)(2,1)} fusion(bf16[1,512,256]{2,1,0:T(8,128)(2,1)S(1)} %collective-permute-done.1, bf16[4,512,256]{2,1,0:T(8,128)(2,1)} %residual_ref.3, bf16[1,512,256]{2,1,0:T(8,128)(2,1)S(1)} %collective-permute-done), kind=kLoop, calls=%fused_computation.14 | loop fusion | flops 1572864 | bytes 3145728 | tf_op jit(solution)/shard_map/concatenate | solution.py:63
  30.4 2.3 %maximum_select_fusion = bf16[2,2,3,4,136,128]{5,4,3,2,1,0:T(8,128)(2,1)S(1)} fusion(bf16[2,1,3,4,136,128]{5,4,3,2,1,0:T(8,128)(2,1)} %collective-permute-done.7, bf16[2,1,3,4,136,128]{5,4,3,2,1,0:T(8,128)(2,1)} %maximum_select_fusion.3, pred[]{:T(512)S(6)} %eq.53), kind=kLoop, calls=%fused_computation.10 | loop fusion | flops 2506752 | bytes 3342337 | tf_op jit(solution)/shard_map/jit(_where)/select_n | solution.py:104
  34.4 2.0 %add.171 = f32[12,256,128]{2,1,0:T(8,128)S(1)} add(f32[12,256,128]{2,1,0:T(8,128)} %shard_map.73, f32[12,256,128]{2,1,0:T(8,128)} %collective-permute-done.2) | non-fusion elementwise | flops 393216 | bytes 4718592 | tf_op jit(solution)/shard_map/add | solution.py:144
  38.1 5.4 %collective-permute-start.5 = (f32[4,1,2,2,1,2,16,128]{7,6,5,4,3,2,0,1:T(8,128)}, f32[4,1,2,2,1,2,16,128]{7,6,5,4,3,2,0,1:T(8,128)}, u32[]{:S(2)}, u32[]{:S(2)}) collective-permute-start(f32[4,1,2,2,1,2,16,128]{7,6,5,4,3,2,0,1:T(8,128)} %constant_dynamic-slice_fusion.9), channel_id=1, source_target_pairs={{0,8},{4,12},{8,0},{12,4},{16,24},{20,28},{24,16},{28,20},{1,9},{5... | collective-permute-start | bytes 786440 | tf_op jit(solution)/shard_map/ppermute | solution.py:98
  45.6 4.2 %gather_fusion = bf16[16,512,256]{2,1,0:T(8,128)(2,1)} fusion(bf16[6,512,256]{2,1,0:T(8,128)(2,1)} %pad_maximum_fusion, s32[1024]{0:T(1024)S(1)} %pad_clamp_fusion.2), kind=kCustom, calls=%fused_computation.2 | custom fusion | bytes 8388672 | tf_op jit(solution)/shard_map/jit(_take)/gather | solution.py:148
  49.8 4.9 %fusion.5 = f32[4,512,256]{2,1,0:T(8,128)} fusion(bf16[4,4,256,256]{3,2,1,0:T(8,128)(2,1)S(1)} %copy-done, bf16[4,4,512,256]{3,2,1,0:T(8,128)(2,1)} %bitcast.90, pred[4,4]{1,0:T(4,128)(4,1)S(1)} %compare_and_fusion.2), kind=kOutput, calls=%fused_computation.11 | convolution fusion | flops 1075838976 | bytes 8388624 | tf_op jit(solution)/shard_map/jerb,jebc->jrc/dot_general | solution.py:149
  58.9 3.0 %collective-permute-start.14 = (f32[4,1,2,2,1,1,16,128]{7,6,5,4,3,2,0,1:T(8,128)S(1)}, f32[4,1,2,2,1,1,16,128]{7,6,5,4,3,2,0,1:T(8,128)S(1)}, u32[]{:S(2)}, u32[]{:S(2)}) collective-permute-start(f32[4,1,2,2,1,1,16,128]{7,6,5,4,3,2,0,1:T(8,128)S(1)} %constant_dynamic-slice_fusion.2), channel_id=1, source_target_pairs={{0,16},{4,20},{8,24},{12,28},{16,0},{20,4},{24,8},{28,12},{1,17},{... | collective-permute-start | bytes 393224 | tf_op jit(solution)/shard_map/ppermute | solution.py:98
  61.8 2.0 %collective-permute-done.8 = f32[4,1,1,1,2,2,16,128]{7,6,5,4,3,2,0,1:T(8,128)S(1)} collective-permute-done((f32[4,1,1,1,2,2,16,128]{7,6,5,4,3,2,0,1:T(8,128)S(1)}, f32[4,1,1,1,2,2,16,128]{7,6,5,4,3,2,0,1:T(8,128)S(1)}, u32[]{:S(2)}, u32[]{:S(2)}) %collective-permute-start.8) | collective-permute-done | bytes 131104 | tf_op jit(solution)/shard_map/ppermute | solution.py:98
  64.4 3.3 %collective-permute-done.11 = f32[4,1,2,1,1,2,16,128]{7,6,5,4,3,2,0,1:T(8,128)S(1)} collective-permute-done((f32[4,1,2,1,1,2,16,128]{7,6,5,4,3,2,0,1:T(8,128)S(1)}, f32[4,1,2,1,1,2,16,128]{7,6,5,4,3,2,0,1:T(8,128)S(1)}, u32[]{:S(2)}, u32[]{:S(2)}) %collective-permute-start.11) | collective-permute-done | bytes 131104 | tf_op jit(solution)/shard_map/ppermute | solution.py:98
  67.9 1.5 %collective-permute-start.15 = (f32[4,1,1,2,1,1,16,128]{7,6,5,4,3,2,0,1:T(8,128)S(1)}, f32[4,1,1,2,1,1,16,128]{7,6,5,4,3,2,0,1:T(8,128)S(1)}, u32[]{:S(2)}, u32[]{:S(2)}) collective-permute-start(f32[4,1,1,2,1,1,16,128]{7,6,5,4,3,2,0,1:T(8,128)S(1)} %constant_dynamic-slice_fusion.1), channel_id=1, source_target_pairs={{0,2},{1,3},{2,0},{3,1},{4,6},{5,7},{6,4},{7,5},{8,10},{9,11},{10,... | collective-permute-start | bytes 196616 | tf_op jit(solution)/shard_map/ppermute | solution.py:98
  69.4 2.5 %collective-permute-start.10 = (f32[4,1,1,1,1,1,16,128]{7,6,5,4,3,2,0,1:T(8,128)S(1)}, f32[4,1,1,1,1,1,16,128]{7,6,5,4,3,2,0,1:T(8,128)S(1)}, u32[]{:S(2)}, u32[]{:S(2)}) collective-permute-start(f32[4,1,1,1,1,1,16,128]{7,6,5,4,3,2,0,1:T(8,128)S(1)} %constant_dynamic-slice_fusion.6), channel_id=1, source_target_pairs={{0,16},{4,20},{8,24},{12,28},{16,0},{20,4},{24,8},{28,12},{1,17},{... | collective-permute-start | bytes 98312 | tf_op jit(solution)/shard_map/ppermute | solution.py:98
  71.8 1.4 %collective-permute-done.12 = f32[4,1,2,1,1,1,16,128]{7,6,5,4,3,2,0,1:T(8,128)S(1)} collective-permute-done((f32[4,1,2,1,1,1,16,128]{7,6,5,4,3,2,0,1:T(8,128)S(1)}, f32[4,1,2,1,1,1,16,128]{7,6,5,4,3,2,0,1:T(8,128)S(1)}, u32[]{:S(2)}, u32[]{:S(2)}) %collective-permute-start.12) | collective-permute-done | bytes 65568 | tf_op jit(solution)/shard_map/ppermute | solution.py:98
  73.4 2.3 %collective-permute-start.16 = (f32[4,1,1,1,1,1,16,128]{7,6,5,4,3,2,0,1:T(8,128)S(1)}, f32[4,1,1,1,1,1,16,128]{7,6,5,4,3,2,0,1:T(8,128)S(1)}, u32[]{:S(2)}, u32[]{:S(2)}) collective-permute-start(f32[4,1,1,1,1,1,16,128]{7,6,5,4,3,2,0,1:T(8,128)S(1)} %constant_dynamic-slice_fusion), channel_id=1, source_target_pairs={{0,4},{4,0},{8,12},{12,8},{16,20},{20,16},{24,28},{28,24},{1,5},{5... | collective-permute-start | bytes 98312 | tf_op jit(solution)/shard_map/ppermute | solution.py:98
  75.7 1.5 %collective-permute-done.13 = f32[4,1,1,1,1,1,16,128]{7,6,5,4,3,2,0,1:T(8,128)S(1)} collective-permute-done((f32[4,1,1,1,1,1,16,128]{7,6,5,4,3,2,0,1:T(8,128)S(1)}, f32[4,1,1,1,1,1,16,128]{7,6,5,4,3,2,0,1:T(8,128)S(1)}, u32[]{:S(2)}, u32[]{:S(2)}) %collective-permute-start.13) | collective-permute-done | bytes 32800 | tf_op jit(solution)/shard_map/ppermute | solution.py:98
  78.3 1.8 %fusion.13 = bf16[12,16,128]{2,1,0:T(8,128)(2,1)S(1)} fusion(bf16[12,4,136,128]{3,2,1,0:T(8,128)(2,1)} %bitcast.94, bf16[12,4,16,128]{3,2,1,0:T(8,128)(2,1)S(1)} %bitcast.102, pred[12,4]{1,0:T(8,128)(4,1)S(1)} %copy.62), kind=kOutput, calls=%fused_computation.16 | convolution fusion | flops 25288704 | bytes 1818672 | tf_op jit(solution)/shard_map/nerc,necd->nrd/dot_general | solution.py:157
  80.1 1.8 %collective-permute-start.17 = (bf16[4,1,1,1,1,1,16,128]{7,6,0,5,4,3,2,1:T(8,128)(2,1)S(1)}, bf16[4,1,1,1,1,1,16,128]{7,6,0,5,4,3,2,1:T(8,128)(2,1)S(1)}, u32[]{:S(2)}, u32[]{:S(2)}) collective-permute-start(bf16[4,1,1,1,1,1,16,128]{7,6,0,5,4,3,2,1:T(8,128)(2,1)S(1)} %get-tuple-element.26), channel_id=1, source_target_pairs={{0,16},{4,20},{8,24},{12,28},{16,0},{20,4},{24,8},{28,12},{1,17},{... | collective-permute-start | bytes 49160 | tf_op jit(solution)/shard_map/ppermute | solution.py:103
  82.1 2.0 %collective-permute-start.25 = (bf16[4,1,1,1,1,1,16,128]{7,6,0,5,4,3,2,1:T(8,128)(2,1)S(1)}, bf16[4,1,1,1,1,1,16,128]{7,6,0,5,4,3,2,1:T(8,128)(2,1)S(1)}, u32[]{:S(2)}, u32[]{:S(2)}) collective-permute-start(bf16[4,1,1,1,1,1,16,128]{7,6,0,5,4,3,2,1:T(8,128)(2,1)S(1)} %get-tuple-element.28), channel_id=1, source_target_pairs={{0,4},{4,0},{8,12},{12,8},{16,20},{20,16},{24,28},{28,24},{1,5},{5... | collective-permute-start | bytes 49160 | tf_op jit(solution)/shard_map/ppermute | solution.py:103
  84.8 1.4 %collective-permute-start.18 = (bf16[4,1,1,1,1,2,16,128]{7,6,0,5,4,3,2,1:T(8,128)(2,1)S(1)}, bf16[4,1,1,1,1,2,16,128]{7,6,0,5,4,3,2,1:T(8,128)(2,1)S(1)}, u32[]{:S(2)}, u32[]{:S(2)}) collective-permute-start(bf16[4,1,1,1,1,2,16,128]{7,6,0,5,4,3,2,1:T(8,128)(2,1)S(1)} %maximum_select_fusion.16), channel_id=1, source_target_pairs={{0,8},{4,12},{8,0},{12,4},{16,24},{20,28},{24,16},{28,20},{1,9},{5... | collective-permute-start | bytes 98312 | tf_op jit(solution)/shard_map/ppermute | solution.py:103
  86.2 2.1 %collective-permute-start.22 = (bf16[4,1,2,1,1,1,16,128]{7,6,0,5,4,3,2,1:T(8,128)(2,1)S(1)}, bf16[4,1,2,1,1,1,16,128]{7,6,0,5,4,3,2,1:T(8,128)(2,1)S(1)}, u32[]{:S(2)}, u32[]{:S(2)}) collective-permute-start(bf16[4,1,2,1,1,1,16,128]{7,6,0,5,4,3,2,1:T(8,128)(2,1)S(1)} %maximum_select_fusion.18), channel_id=1, source_target_pairs={{0,16},{4,20},{8,24},{12,28},{16,0},{20,4},{24,8},{28,12},{1,17},{... | collective-permute-start | bytes 98312 | tf_op jit(solution)/shard_map/ppermute | solution.py:103
  88.3 1.6 %collective-permute-start.26 = (bf16[4,1,1,2,1,1,16,128]{7,6,0,5,4,3,2,1:T(8,128)(2,1)S(1)}, bf16[4,1,1,2,1,1,16,128]{7,6,0,5,4,3,2,1:T(8,128)(2,1)S(1)}, u32[]{:S(2)}, u32[]{:S(2)}) collective-permute-start(bf16[4,1,1,2,1,1,16,128]{7,6,0,5,4,3,2,1:T(8,128)(2,1)S(1)} %maximum_select_fusion.20), channel_id=1, source_target_pairs={{0,2},{1,3},{2,0},{3,1},{4,6},{5,7},{6,4},{7,5},{8,10},{9,11},{10,... | collective-permute-start | bytes 98312 | tf_op jit(solution)/shard_map/ppermute | solution.py:103
  97.9 1.4 %collective-permute-start.28 = (bf16[4,1,2,2,1,2,16,128]{7,6,0,5,4,3,2,1:T(8,128)(2,1)S(1)}, bf16[4,1,2,2,1,2,16,128]{7,6,0,5,4,3,2,1:T(8,128)(2,1)S(1)}, u32[]{:S(2)}, u32[]{:S(2)}) collective-permute-start(bf16[4,1,2,2,1,2,16,128]{7,6,0,5,4,3,2,1:T(8,128)(2,1)S(1)} %maximum_select_fusion.9), channel_id=1, source_target_pairs={{0,8},{4,12},{8,0},{12,4},{16,24},{20,28},{24,16},{28,20},{1,9},{5... | collective-permute-start | bytes 393224 | tf_op jit(solution)/shard_map/ppermute | solution.py:103
  101.4 1.5 %collective-permute-done.28 = bf16[4,1,2,2,1,2,16,128]{7,6,0,5,4,3,2,1:T(8,128)(2,1)S(1)} collective-permute-done((bf16[4,1,2,2,1,2,16,128]{7,6,0,5,4,3,2,1:T(8,128)(2,1)S(1)}, bf16[4,1,2,2,1,2,16,128]{7,6,0,5,4,3,2,1:T(8,128)(2,1)S(1)}, u32[]{:S(2)}, u32[]{:S(2)}) %collective-permute-start.28) | collective-permute-done | bytes 131104 | tf_op jit(solution)/shard_map/ppermute | solution.py:103
  104.1 1.4 %collective-permute-done.29 = bf16[12,256,128]{2,1,0:T(8,128)(2,1)} collective-permute-done((bf16[12,256,128]{2,1,0:T(8,128)(2,1)S(1)}, bf16[12,256,128]{2,1,0:T(8,128)(2,1)}, u32[]{:S(2)}, u32[]{:S(2)}) %collective-permute-start.29) | collective-permute-done | bytes 786464 | tf_op jit(solution)/shard_map/ppermute | solution.py:165
  105.5 1.8 %gather_fusion.3 = bf16[8,256,128]{2,1,0:T(8,128)(2,1)S(1)} fusion(bf16[12,256,128]{2,1,0:T(8,128)(2,1)} %collective-permute-done.29, s32[1024]{0:T(1024)S(1)} %pad_clamp_fusion), kind=kCustom, calls=%fused_computation.1.clone | custom fusion | bytes 1048608 | tf_op jit(solution)/shard_map/jit(_take)/gather | solution.py:167
  (134 shorter events, 30.3 us)
Async XLA Ops:
  0.0 49.8 %copy-start = (bf16[4,4,256,256]{3,2,1,0:T(8,128)(2,1)S(1)}, bf16[4,4,256,256]{3,2,1,0:T(8,128)(2,1)}, u32[]{:S(2)}) copy-start(bf16[4,4,256,256]{3,2,1,0:T(8,128)(2,1)} %param.11) | copy-start | bytes 6291460
  2.7 12.9 %collective-permute-start.6 = (bf16[1,1,3,4,136,128]{5,4,3,2,1,0:T(8,128)(2,1)}, bf16[1,1,3,4,136,128]{5,4,3,2,1,0:T(8,128)(2,1)}, u32[]{:S(2)}, u32[]{:S(2)}) collective-permute-start(bf16[1,1,3,4,136,128]{5,4,3,2,1,0:T(8,128)(2,1)} %maximum_bitcast_fusion), channel_id=1, source_target_pairs={{0,2},{1,3},{2,0},{3,1},{4,6},{5,7},{6,4},{7,5},{8,10},{9,11},{10,... | collective-permute-start | bytes 1253384 | tf_op jit(solution)/shard_map/ppermute | solution.py:103
  7.0 11.0 %copy-start.1 = (bf16[4,512,256]{2,1,0:T(8,128)(2,1)S(1)}, bf16[4,512,256]{2,1,0:T(8,128)(2,1)}, u32[]{:S(2)}) copy-start(bf16[4,512,256]{2,1,0:T(8,128)(2,1)} %residual_ref.3) | copy-start | bytes 3145732
  12.2 22.2 %collective-permute-start.2 = (f32[12,256,128]{2,1,0:T(8,128)}, f32[12,256,128]{2,1,0:T(8,128)}, u32[]{:S(2)}, u32[]{:S(2)}) collective-permute-start(f32[12,256,128]{2,1,0:T(8,128)} %shard_map.74), channel_id=1, source_target_pairs={{0,1},{1,0},{2,3},{3,2},{4,5},{5,4},{6,7},{7,6},{8,9},{9,8},{10,11... | collective-permute-start | bytes 4718600 | tf_op jit(solution)/shard_map/ppermute | solution.py:143
  18.0 12.4 %collective-permute-start.7 = (bf16[2,1,3,4,136,128]{5,4,3,2,1,0:T(8,128)(2,1)}, bf16[2,1,3,4,136,128]{5,4,3,2,1,0:T(8,128)(2,1)}, u32[]{:S(2)}, u32[]{:S(2)}) collective-permute-start(bf16[2,1,3,4,136,128]{5,4,3,2,1,0:T(8,128)(2,1)} %maximum_select_fusion.3), channel_id=1, source_target_pairs={{0,1},{1,0},{2,3},{3,2},{4,5},{5,4},{6,7},{7,6},{8,9},{9,8},{10,11... | collective-permute-start | bytes 2506760 | tf_op jit(solution)/shard_map/ppermute | solution.py:103
  18.8 9.0 %collective-permute-start = (bf16[1,512,256]{2,1,0:T(8,128)(2,1)}, bf16[1,512,256]{2,1,0:T(8,128)(2,1)S(1)}, u32[]{:S(2)}, u32[]{:S(2)}) collective-permute-start(bf16[1,512,256]{2,1,0:T(8,128)(2,1)} %get-tuple-element.23), channel_id=1, source_target_pairs={{0,1},{1,2},{2,3},{3,4},{4,5},{5,6},{6,7},{7,8},{8,9},{9,10},{10,1... | collective-permute-start | bytes 786440 | tf_op jit(solution)/shard_map/ppermute | solution.py:65
  21.2 6.6 %collective-permute-start.1 = (bf16[1,512,256]{2,1,0:T(8,128)(2,1)S(1)}, bf16[1,512,256]{2,1,0:T(8,128)(2,1)S(1)}, u32[]{:S(2)}, u32[]{:S(2)}) collective-permute-start(bf16[1,512,256]{2,1,0:T(8,128)(2,1)S(1)} %get-tuple-element.24), channel_id=1, source_target_pairs={{1,0},{2,1},{3,2},{4,3},{5,4},{6,5},{7,6},{8,7},{9,8},{10,9},{11,1... | collective-permute-start | bytes 786440 | tf_op jit(solution)/shard_map/ppermute | solution.py:67
  38.1 16.6 %collective-permute-start.5 = (f32[4,1,2,2,1,2,16,128]{7,6,5,4,3,2,0,1:T(8,128)}, f32[4,1,2,2,1,2,16,128]{7,6,5,4,3,2,0,1:T(8,128)}, u32[]{:S(2)}, u32[]{:S(2)}) collective-permute-start(f32[4,1,2,2,1,2,16,128]{7,6,5,4,3,2,0,1:T(8,128)} %constant_dynamic-slice_fusion.9), channel_id=1, source_target_pairs={{0,8},{4,12},{8,0},{12,4},{16,24},{20,28},{24,16},{28,20},{1,9},{5... | collective-permute-start | bytes 786440 | tf_op jit(solution)/shard_map/ppermute | solution.py:98
  44.3 11.4 %collective-permute-start.4 = (f32[4,1,2,1,2,2,16,128]{7,6,5,4,3,2,0,1:T(8,128)}, f32[4,1,2,1,2,2,16,128]{7,6,5,4,3,2,0,1:T(8,128)}, u32[]{:S(2)}, u32[]{:S(2)}) collective-permute-start(f32[4,1,2,1,2,2,16,128]{7,6,5,4,3,2,0,1:T(8,128)} %constant_dynamic-slice_fusion.10), channel_id=1, source_target_pairs={{0,4},{4,0},{8,12},{12,8},{16,20},{20,16},{24,28},{28,24},{1,5},{5... | collective-permute-start | bytes 786440 | tf_op jit(solution)/shard_map/ppermute | solution.py:98
  44.9 11.8 %collective-permute-start.3 = (f32[4,1,1,2,2,2,16,128]{7,6,5,4,3,2,0,1:T(8,128)S(1)}, f32[4,1,1,2,2,2,16,128]{7,6,5,4,3,2,0,1:T(8,128)}, u32[]{:S(2)}, u32[]{:S(2)}) collective-permute-start(f32[4,1,1,2,2,2,16,128]{7,6,5,4,3,2,0,1:T(8,128)S(1)} %constant_dynamic-slice_fusion.11), channel_id=1, source_target_pairs={{0,2},{1,3},{2,0},{3,1},{4,6},{5,7},{6,4},{7,5},{8,10},{9,11},{10,... | collective-permute-start | bytes 786440 | tf_op jit(solution)/shard_map/ppermute | solution.py:98
  57.7 6.1 %collective-permute-start.8 = (f32[4,1,1,1,2,2,16,128]{7,6,5,4,3,2,0,1:T(8,128)S(1)}, f32[4,1,1,1,2,2,16,128]{7,6,5,4,3,2,0,1:T(8,128)S(1)}, u32[]{:S(2)}, u32[]{:S(2)}) collective-permute-start(f32[4,1,1,1,2,2,16,128]{7,6,5,4,3,2,0,1:T(8,128)S(1)} %constant_dynamic-slice_fusion.8), channel_id=1, source_target_pairs={{0,4},{4,0},{8,12},{12,8},{16,20},{20,16},{24,28},{28,24},{1,5},{5... | collective-permute-start | bytes 393224 | tf_op jit(solution)/shard_map/ppermute | solution.py:98
  58.7 9.0 %collective-permute-start.11 = (f32[4,1,2,1,1,2,16,128]{7,6,5,4,3,2,0,1:T(8,128)S(1)}, f32[4,1,2,1,1,2,16,128]{7,6,5,4,3,2,0,1:T(8,128)S(1)}, u32[]{:S(2)}, u32[]{:S(2)}) collective-permute-start(f32[4,1,2,1,1,2,16,128]{7,6,5,4,3,2,0,1:T(8,128)S(1)} %constant_dynamic-slice_fusion.5), channel_id=1, source_target_pairs={{0,8},{4,12},{8,0},{12,4},{16,24},{20,28},{24,16},{28,20},{1,9},{5... | collective-permute-start | bytes 393224 | tf_op jit(solution)/shard_map/ppermute | solution.py:98
  58.9 8.9 %collective-permute-start.14 = (f32[4,1,2,2,1,1,16,128]{7,6,5,4,3,2,0,1:T(8,128)S(1)}, f32[4,1,2,2,1,1,16,128]{7,6,5,4,3,2,0,1:T(8,128)S(1)}, u32[]{:S(2)}, u32[]{:S(2)}) collective-permute-start(f32[4,1,2,2,1,1,16,128]{7,6,5,4,3,2,0,1:T(8,128)S(1)} %constant_dynamic-slice_fusion.2), channel_id=1, source_target_pairs={{0,16},{4,20},{8,24},{12,28},{16,0},{20,4},{24,8},{28,12},{1,17},{... | collective-permute-start | bytes 393224 | tf_op jit(solution)/shard_map/ppermute | solution.py:98
  63.9 5.4 %collective-permute-start.9 = (f32[4,1,1,1,1,2,16,128]{7,6,5,4,3,2,0,1:T(8,128)S(1)}, f32[4,1,1,1,1,2,16,128]{7,6,5,4,3,2,0,1:T(8,128)S(1)}, u32[]{:S(2)}, u32[]{:S(2)}) collective-permute-start(f32[4,1,1,1,1,2,16,128]{7,6,5,4,3,2,0,1:T(8,128)S(1)} %constant_dynamic-slice_fusion.7), channel_id=1, source_target_pairs={{0,8},{4,12},{8,0},{12,4},{16,24},{20,28},{24,16},{28,20},{1,9},{5... | collective-permute-start | bytes 196616 | tf_op jit(solution)/shard_map/ppermute | solution.py:98
  67.7 5.5 %collective-permute-start.12 = (f32[4,1,2,1,1,1,16,128]{7,6,5,4,3,2,0,1:T(8,128)S(1)}, f32[4,1,2,1,1,1,16,128]{7,6,5,4,3,2,0,1:T(8,128)S(1)}, u32[]{:S(2)}, u32[]{:S(2)}) collective-permute-start(f32[4,1,2,1,1,1,16,128]{7,6,5,4,3,2,0,1:T(8,128)S(1)} %constant_dynamic-slice_fusion.4), channel_id=1, source_target_pairs={{0,16},{4,20},{8,24},{12,28},{16,0},{20,4},{24,8},{28,12},{1,17},{... | collective-permute-start | bytes 196616 | tf_op jit(solution)/shard_map/ppermute | solution.py:98
  67.9 5.5 %collective-permute-start.15 = (f32[4,1,1,2,1,1,16,128]{7,6,5,4,3,2,0,1:T(8,128)S(1)}, f32[4,1,1,2,1,1,16,128]{7,6,5,4,3,2,0,1:T(8,128)S(1)}, u32[]{:S(2)}, u32[]{:S(2)}) collective-permute-start(f32[4,1,1,2,1,1,16,128]{7,6,5,4,3,2,0,1:T(8,128)S(1)} %constant_dynamic-slice_fusion.1), channel_id=1, source_target_pairs={{0,2},{1,3},{2,0},{3,1},{4,6},{5,7},{6,4},{7,5},{8,10},{9,11},{10,... | collective-permute-start | bytes 196616 | tf_op jit(solution)/shard_map/ppermute | solution.py:98
  69.4 6.4 %collective-permute-start.10 = (f32[4,1,1,1,1,1,16,128]{7,6,5,4,3,2,0,1:T(8,128)S(1)}, f32[4,1,1,1,1,1,16,128]{7,6,5,4,3,2,0,1:T(8,128)S(1)}, u32[]{:S(2)}, u32[]{:S(2)}) collective-permute-start(f32[4,1,1,1,1,1,16,128]{7,6,5,4,3,2,0,1:T(8,128)S(1)} %constant_dynamic-slice_fusion.6), channel_id=1, source_target_pairs={{0,16},{4,20},{8,24},{12,28},{16,0},{20,4},{24,8},{28,12},{1,17},{... | collective-permute-start | bytes 98312 | tf_op jit(solution)/shard_map/ppermute | solution.py:98
  73.3 4.0 %collective-permute-start.13 = (f32[4,1,1,1,1,1,16,128]{7,6,5,4,3,2,0,1:T(8,128)S(1)}, f32[4,1,1,1,1,1,16,128]{7,6,5,4,3,2,0,1:T(8,128)S(1)}, u32[]{:S(2)}, u32[]{:S(2)}) collective-permute-start(f32[4,1,1,1,1,1,16,128]{7,6,5,4,3,2,0,1:T(8,128)S(1)} %constant_dynamic-slice_fusion.3), channel_id=1, source_target_pairs={{0,2},{1,3},{2,0},{3,1},{4,6},{5,7},{6,4},{7,5},{8,10},{9,11},{10,... | collective-permute-start | bytes 98312 | tf_op jit(solution)/shard_map/ppermute | solution.py:98
  73.4 4.2 %collective-permute-start.16 = (f32[4,1,1,1,1,1,16,128]{7,6,5,4,3,2,0,1:T(8,128)S(1)}, f32[4,1,1,1,1,1,16,128]{7,6,5,4,3,2,0,1:T(8,128)S(1)}, u32[]{:S(2)}, u32[]{:S(2)}) collective-permute-start(f32[4,1,1,1,1,1,16,128]{7,6,5,4,3,2,0,1:T(8,128)S(1)} %constant_dynamic-slice_fusion), channel_id=1, source_target_pairs={{0,4},{4,0},{8,12},{12,8},{16,20},{20,16},{24,28},{28,24},{1,5},{5... | collective-permute-start | bytes 98312 | tf_op jit(solution)/shard_map/ppermute | solution.py:98
  80.1 4.7 %collective-permute-start.17 = (bf16[4,1,1,1,1,1,16,128]{7,6,0,5,4,3,2,1:T(8,128)(2,1)S(1)}, bf16[4,1,1,1,1,1,16,128]{7,6,0,5,4,3,2,1:T(8,128)(2,1)S(1)}, u32[]{:S(2)}, u32[]{:S(2)}) collective-permute-start(bf16[4,1,1,1,1,1,16,128]{7,6,0,5,4,3,2,1:T(8,128)(2,1)S(1)} %get-tuple-element.26), channel_id=1, source_target_pairs={{0,16},{4,20},{8,24},{12,28},{16,0},{20,4},{24,8},{28,12},{1,17},{... | collective-permute-start | bytes 49160 | tf_op jit(solution)/shard_map/ppermute | solution.py:103
  81.8 4.4 %collective-permute-start.21 = (bf16[4,1,1,1,1,1,16,128]{7,6,0,5,4,3,2,1:T(8,128)(2,1)S(1)}, bf16[4,1,1,1,1,1,16,128]{7,6,0,5,4,3,2,1:T(8,128)(2,1)S(1)}, u32[]{:S(2)}, u32[]{:S(2)}) collective-permute-start(bf16[4,1,1,1,1,1,16,128]{7,6,0,5,4,3,2,1:T(8,128)(2,1)S(1)} %get-tuple-element.27), channel_id=1, source_target_pairs={{0,2},{1,3},{2,0},{3,1},{4,6},{5,7},{6,4},{7,5},{8,10},{9,11},{10,... | collective-permute-start | bytes 49160 | tf_op jit(solution)/shard_map/ppermute | solution.py:103
  82.1 6.2 %collective-permute-start.25 = (bf16[4,1,1,1,1,1,16,128]{7,6,0,5,4,3,2,1:T(8,128)(2,1)S(1)}, bf16[4,1,1,1,1,1,16,128]{7,6,0,5,4,3,2,1:T(8,128)(2,1)S(1)}, u32[]{:S(2)}, u32[]{:S(2)}) collective-permute-start(bf16[4,1,1,1,1,1,16,128]{7,6,0,5,4,3,2,1:T(8,128)(2,1)S(1)} %get-tuple-element.28), channel_id=1, source_target_pairs={{0,4},{4,0},{8,12},{12,8},{16,20},{20,16},{24,28},{28,24},{1,5},{5... | collective-permute-start | bytes 49160 | tf_op jit(solution)/shard_map/ppermute | solution.py:103
  84.8 5.2 %collective-permute-start.18 = (bf16[4,1,1,1,1,2,16,128]{7,6,0,5,4,3,2,1:T(8,128)(2,1)S(1)}, bf16[4,1,1,1,1,2,16,128]{7,6,0,5,4,3,2,1:T(8,128)(2,1)S(1)}, u32[]{:S(2)}, u32[]{:S(2)}) collective-permute-start(bf16[4,1,1,1,1,2,16,128]{7,6,0,5,4,3,2,1:T(8,128)(2,1)S(1)} %maximum_select_fusion.16), channel_id=1, source_target_pairs={{0,8},{4,12},{8,0},{12,4},{16,24},{20,28},{24,16},{28,20},{1,9},{5... | collective-permute-start | bytes 98312 | tf_op jit(solution)/shard_map/ppermute | solution.py:103
  86.2 5.0 %collective-permute-start.22 = (bf16[4,1,2,1,1,1,16,128]{7,6,0,5,4,3,2,1:T(8,128)(2,1)S(1)}, bf16[4,1,2,1,1,1,16,128]{7,6,0,5,4,3,2,1:T(8,128)(2,1)S(1)}, u32[]{:S(2)}, u32[]{:S(2)}) collective-permute-start(bf16[4,1,2,1,1,1,16,128]{7,6,0,5,4,3,2,1:T(8,128)(2,1)S(1)} %maximum_select_fusion.18), channel_id=1, source_target_pairs={{0,16},{4,20},{8,24},{12,28},{16,0},{20,4},{24,8},{28,12},{1,17},{... | collective-permute-start | bytes 98312 | tf_op jit(solution)/shard_map/ppermute | solution.py:103
  88.3 4.3 %collective-permute-start.26 = (bf16[4,1,1,2,1,1,16,128]{7,6,0,5,4,3,2,1:T(8,128)(2,1)S(1)}, bf16[4,1,1,2,1,1,16,128]{7,6,0,5,4,3,2,1:T(8,128)(2,1)S(1)}, u32[]{:S(2)}, u32[]{:S(2)}) collective-permute-start(bf16[4,1,1,2,1,1,16,128]{7,6,0,5,4,3,2,1:T(8,128)(2,1)S(1)} %maximum_select_fusion.20), channel_id=1, source_target_pairs={{0,2},{1,3},{2,0},{3,1},{4,6},{5,7},{6,4},{7,5},{8,10},{9,11},{10,... | collective-permute-start | bytes 98312 | tf_op jit(solution)/shard_map/ppermute | solution.py:103
  90.0 5.0 %collective-permute-start.19 = (bf16[4,1,1,1,2,2,16,128]{7,6,0,5,4,3,2,1:T(8,128)(2,1)S(1)}, bf16[4,1,1,1,2,2,16,128]{7,6,0,5,4,3,2,1:T(8,128)(2,1)S(1)}, u32[]{:S(2)}, u32[]{:S(2)}) collective-permute-start(bf16[4,1,1,1,2,2,16,128]{7,6,0,5,4,3,2,1:T(8,128)(2,1)S(1)} %maximum_select_fusion.11), channel_id=1, source_target_pairs={{0,4},{4,0},{8,12},{12,8},{16,20},{20,16},{24,28},{28,24},{1,5},{5... | collective-permute-start | bytes 196616 | tf_op jit(solution)/shard_map/ppermute | solution.py:103
  91.2 5.0 %collective-permute-start.23 = (bf16[4,1,2,1,1,2,16,128]{7,6,0,5,4,3,2,1:T(8,128)(2,1)S(1)}, bf16[4,1,2,1,1,2,16,128]{7,6,0,5,4,3,2,1:T(8,128)(2,1)S(1)}, u32[]{:S(2)}, u32[]{:S(2)}) collective-permute-start(bf16[4,1,2,1,1,2,16,128]{7,6,0,5,4,3,2,1:T(8,128)(2,1)S(1)} %maximum_select_fusion.13), channel_id=1, source_target_pairs={{0,8},{4,12},{8,0},{12,4},{16,24},{20,28},{24,16},{28,20},{1,9},{5... | collective-permute-start | bytes 196616 | tf_op jit(solution)/shard_map/ppermute | solution.py:103
  92.6 5.2 %collective-permute-start.27 = (bf16[4,1,2,2,1,1,16,128]{7,6,0,5,4,3,2,1:T(8,128)(2,1)S(1)}, bf16[4,1,2,2,1,1,16,128]{7,6,0,5,4,3,2,1:T(8,128)(2,1)S(1)}, u32[]{:S(2)}, u32[]{:S(2)}) collective-permute-start(bf16[4,1,2,2,1,1,16,128]{7,6,0,5,4,3,2,1:T(8,128)(2,1)S(1)} %fusion.29), channel_id=1, source_target_pairs={{0,16},{4,20},{8,24},{12,28},{16,0},{20,4},{24,8},{28,12},{1,17},{... | collective-permute-start | bytes 196616 | tf_op jit(solution)/shard_map/ppermute | solution.py:103
  95.1 5.0 %collective-permute-start.20 = (bf16[4,1,1,2,2,2,16,128]{7,6,0,5,4,3,2,1:T(8,128)(2,1)S(1)}, bf16[4,1,1,2,2,2,16,128]{7,6,0,5,4,3,2,1:T(8,128)(2,1)S(1)}, u32[]{:S(2)}, u32[]{:S(2)}) collective-permute-start(bf16[4,1,1,2,2,2,16,128]{7,6,0,5,4,3,2,1:T(8,128)(2,1)S(1)} %maximum_select_fusion.7), channel_id=1, source_target_pairs={{0,2},{1,3},{2,0},{3,1},{4,6},{5,7},{6,4},{7,5},{8,10},{9,11},{10,... | collective-permute-start | bytes 393224 | tf_op jit(solution)/shard_map/ppermute | solution.py:103
  96.3 5.0 %collective-permute-start.24 = (bf16[4,1,2,1,2,2,16,128]{7,6,0,5,4,3,2,1:T(8,128)(2,1)S(1)}, bf16[4,1,2,1,2,2,16,128]{7,6,0,5,4,3,2,1:T(8,128)(2,1)S(1)}, u32[]{:S(2)}, u32[]{:S(2)}) collective-permute-start(bf16[4,1,2,1,2,2,16,128]{7,6,0,5,4,3,2,1:T(8,128)(2,1)S(1)} %maximum_select_fusion.8), channel_id=1, source_target_pairs={{0,4},{4,0},{8,12},{12,8},{16,20},{20,16},{24,28},{28,24},{1,5},{5... | collective-permute-start | bytes 393224 | tf_op jit(solution)/shard_map/ppermute | solution.py:103
  97.9 5.0 %collective-permute-start.28 = (bf16[4,1,2,2,1,2,16,128]{7,6,0,5,4,3,2,1:T(8,128)(2,1)S(1)}, bf16[4,1,2,2,1,2,16,128]{7,6,0,5,4,3,2,1:T(8,128)(2,1)S(1)}, u32[]{:S(2)}, u32[]{:S(2)}) collective-permute-start(bf16[4,1,2,2,1,2,16,128]{7,6,0,5,4,3,2,1:T(8,128)(2,1)S(1)} %maximum_select_fusion.9), channel_id=1, source_target_pairs={{0,8},{4,12},{8,0},{12,4},{16,24},{20,28},{24,16},{28,20},{1,9},{5... | collective-permute-start | bytes 393224 | tf_op jit(solution)/shard_map/ppermute | solution.py:103
  103.1 2.5 %collective-permute-start.29 = (bf16[12,256,128]{2,1,0:T(8,128)(2,1)S(1)}, bf16[12,256,128]{2,1,0:T(8,128)(2,1)}, u32[]{:S(2)}, u32[]{:S(2)}) collective-permute-start(bf16[12,256,128]{2,1,0:T(8,128)(2,1)S(1)} %pad_maximum_fusion.1), channel_id=1, source_target_pairs={{0,1},{1,0},{2,3},{3,2},{4,5},{5,4},{6,7},{7,6},{8,9},{9,8},{10,11... | collective-permute-start | bytes 2359304 | tf_op jit(solution)/shard_map/ppermute | solution.py:165
  (7 other events, 22.9 us)

commit v14 on v12

--- a/solution.py
+++ b/solution.py
@@ -116,7 +116,15 @@
 def per_device(residual, margin, inverse_blocks, interface, basis, coarse_pattern, coarse_inverse):
     rows, cols = coarse_inverse.shape[-2:]
     tags = jnp.broadcast_to(coarse_pattern.astype(jnp.bfloat16)[:, :, None, None], coarse_pattern.shape + (8, cols))
-    packed = lax.all_gather(jnp.concatenate([coarse_inverse, tags], axis=2), "coarse", axis=0, tiled=True)
+    packed = jnp.concatenate([coarse_inverse, tags], axis=2)
+    xors = [0]
+    for axis, mask in reversed([bit for bit in device_bits() if bit[0] == "coarse"]):
+        packed = jnp.concatenate([packed, lax.ppermute(packed, axis, pairs(axis, mask))], axis=0)
+        xors = xors + [x ^ mask for x in xors]
+    slot_of = jnp.array([xors.index(x) for x in range(len(xors))], jnp.int32)
+    own_rows = coarse_inverse.shape[0]
+    labels = jnp.arange(len(xors) * own_rows, dtype=jnp.int32)
+    order = slot_of[(labels // own_rows) ^ lax.axis_index("coarse")] * own_rows + labels % own_rows
     inverse_all = packed[:, :, :rows, :]
     pattern_all = packed[:, :, rows, 0].astype(jnp.int32)
     extended = with_halo(residual, ((("sub", "coarse"), 0),), 1)
@@ -152,6 +160,7 @@
     solved = jnp.einsum(
         "nerc,necd->nrd", chosen, inverse_all, preferred_element_type=jnp.float32
     ).astype(jnp.bfloat16)
+    solved = jnp.take(solved, order, axis=0)
     solved = solved.reshape((total_blocks,) + (1,) * nb + (inner, width))
     outs = [lax.slice_in_dim(solved, s * per, (s + 1) * per, axis=0) for s in range(streams)]
     for step in reversed(range(1, nb)):

time: 114 us -> 118 us (1.035)
  between operations: 14 us -> 0.55 us
  waiting for transfers between devices: 16.7 us -> 28.8 us
  other arithmetic: 9.83 us -> 13 us
  local copies, waits for them, and re-layouts: 16 us -> 17.8 us
    ppermute x0 -> x2, waiting for transfers between devices: none -> 11.9 us  [per_device(): lax.ppermute(packed, axis, pairs(axis, mask))]
    ppermute x0 -> x2, starting transfers between devices: none -> 4.2 us  [per_device(): lax.ppermute(packed, axis, pairs(axis, mask))]
    ppermute x12, starting transfers between devices: 19.1 us -> 16.5 us  [halve(): lax.ppermute(send.astype(wire), axis, pairs(axis, mask)).astype(x.dtype)]
    gather x0 -> x2, local copies, waits for them, and re-layouts: none -> 1.23 us  [the longest x1 0.66 us: per_device(): slot_of[labels // own_rows ^ lax.axis_index('coarse')] * own_rows]
    and x0 -> x1, other arithmetic: none -> 1.19 us  [per_device(): solved = jnp.take(solved, order, axis=0)]
    unnamed x26 -> x40, local copies, waits for them, and re-layouts: 3.84 us -> 4.67 us
  transfers between devices with their start and end apart: 29 -> 30, of which waited for: 13 -> 15; matrix products, arithmetic and copies ran while one was open for 19% -> 19% of each run, Pallas kernels for 5% -> 4%
where the time goes in v14:
time: 118 us; the launch traced here: 117 us
  starting transfers between devices  40 us (34%)
  waiting for transfers between devices  28.8 us (24%)
  local copies, waits for them, and re-layouts  17.8 us (15%)
  other arithmetic  13 us (11%)
  Pallas kernels  10.2 us (9%)
  matrix products  6.89 us (6%)
    ppermute x12, starting transfers between devices, halve(): lax.ppermute(send.astype(wire), axis, pairs(axis, mask)).astype(x.dtype)  16.5 us
    ppermute x12, starting transfers between devices, double(): recv = lax.ppermute(y, axis, pairs(axis, mask))  14.9 us
    ppermute x2, waiting for transfers between devices, per_device(): lax.ppermute(packed, axis, pairs(axis, mask))  11.9 us
    pallas_call x2, Pallas kernels, restrict(): pl.pallas_call(functools.partial(restrict_kernel, upper=upper), out_shape...  10.2 us
    ppermute x12, waiting for transfers between devices, halve(): lax.ppermute(send.astype(wire), axis, pairs(axis, mask)).astype(x.dtype)  8.06 us
    ppermute x12, waiting for transfers between devices, double(): recv = lax.ppermute(y, axis, pairs(axis, mask))  7.36 us
    dot_general x1, matrix products, per_device(): jnp.einsum('jerb,jebc->jrc', picked, inverse_blocks, preferred_element_ty...  4.91 us
    unnamed x40, local copies, waits for them, and re-layouts  4.67 us
  transfers between devices with their start and end apart: 30, of which 15 were waited for; matrix products, arithmetic and copies ran while one was open for 19% of the time, Pallas kernels for 4%

profile of v14, /device:TPU:0, one launch (start us, length us, event | category | flops | bytes accessed | tf_op | source)
XLA Modules:
  0.0 117.2 jit_solution(4125100434274007782)
XLA Ops:
  1.5 5.2 %shard_map.83 = f32[12,256,128]{2,1,0:T(8,128)} custom-call(s32[8]{0:T(128)} %reshape.1777.links, s32[1]{0:T(128)} %bitcast.half, bf16[4,512,256]{2,1,0:T(8,128)(2,1)} %residual_ref.3, bf16[4,2,256,128]{3,2,1,0:T(8,128)(2,1)} %basis_ref.3), custom_call_target="tpu_custom_call" | custom-call | flops 134217728 | bytes 3145728 | tf_op jit(solution)/shard_map/pallas_call | solution.py:36
  8.0 2.7 %collective-permute-start = (bf16[1,512,256]{2,1,0:T(8,128)(2,1)}, bf16[1,512,256]{2,1,0:T(8,128)(2,1)}, u32[]{:S(2)}, u32[]{:S(2)}) collective-permute-start(bf16[1,512,256]{2,1,0:T(8,128)(2,1)} %get-tuple-element.23), channel_id=1, source_target_pairs={{0,1},{1,2},{2,3},{3,4},{4,5},{5,6},{6,7},{7,8},{8,9},{9,10},{10,1... | collective-permute-start | bytes 786440 | tf_op jit(solution)/shard_map/ppermute | solution.py:65
  10.7 1.3 %collective-permute-start.1 = (bf16[1,512,256]{2,1,0:T(8,128)(2,1)}, bf16[1,512,256]{2,1,0:T(8,128)(2,1)}, u32[]{:S(2)}, u32[]{:S(2)}) collective-permute-start(bf16[1,512,256]{2,1,0:T(8,128)(2,1)} %get-tuple-element.24), channel_id=1, source_target_pairs={{1,0},{2,1},{3,2},{4,3},{5,4},{6,5},{7,6},{8,7},{9,8},{10,9},{11,1... | collective-permute-start | bytes 786440 | tf_op jit(solution)/shard_map/ppermute | solution.py:67
  12.1 4.2 %collective-permute-start.6 = (bf16[3,4,136,128]{3,2,1,0:T(8,128)(2,1)S(1)}, bf16[3,4,136,128]{3,2,1,0:T(8,128)(2,1)S(1)}, u32[]{:S(2)}, u32[]{:S(2)}) collective-permute-start(bf16[3,4,136,128]{3,2,1,0:T(8,128)(2,1)S(1)} %pad_maximum_fusion.13), channel_id=1, source_target_pairs={{0,2},{1,3},{2,0},{3,1},{4,6},{5,7},{6,4},{7,5},{8,10},{9,11},{10,... | collective-permute-start | bytes 1253384 | tf_op jit(solution)/shard_map/ppermute | solution.py:122
  17.1 11.9 %collective-permute-done.6 = bf16[3,4,136,128]{3,2,1,0:T(8,128)(2,1)S(1)} collective-permute-done((bf16[3,4,136,128]{3,2,1,0:T(8,128)(2,1)S(1)}, bf16[3,4,136,128]{3,2,1,0:T(8,128)(2,1)S(1)}, u32[]{:S(2)}, u32[]{:S(2)}) %collective-permute-start.6) | collective-permute-done | bytes 417824 | tf_op jit(solution)/shard_map/ppermute | solution.py:122
  30.9 1.2 %compare_and_fusion.2 = pred[12]{0:T(512)(128)(4,1)} fusion(s32[12]{0:T(128)} %copy-done.18), kind=kLoop, calls=%fused_computation.112 | loop fusion | flops 168 | bytes 60 | tf_op jit(solution)/shard_map/jit(_take)/and | solution.py:163
  32.0 5.0 %shard_map.82 = f32[12,256,128]{2,1,0:T(8,128)} custom-call(s32[8]{0:T(128)} %reshape.1777.links, s32[1]{0:T(128)} %bitcast.half, bf16[4,512,256]{2,1,0:T(8,128)(2,1)} %residual_ref.3, bf16[4,2,256,128]{3,2,1,0:T(8,128)(2,1)} %basis_ref.3), custom_call_target="tpu_custom_call" | custom-call | flops 134217728 | bytes 3145728 | tf_op jit(solution)/shard_map/pallas_call | solution.py:36
  37.6 2.4 %pad_maximum_fusion.6 = bf16[6,512,256]{2,1,0:T(8,128)(2,1)} fusion(bf16[1,512,256]{2,1,0:T(8,128)(2,1)} %collective-permute-done.1, bf16[4,512,256]{2,1,0:T(8,128)(2,1)S(1)} %copy-done.3, bf16[1,512,256]{2,1,0:T(8,128)(2,1)} %collective-permute-done), kind=kLoop, calls=%fused_computation.18 | loop fusion | flops 1572864 | bytes 3145728 | tf_op jit(solution)/shard_map/concatenate | solution.py:63
  41.3 2.0 %add.233 = f32[12,256,128]{2,1,0:T(8,128)S(1)} add(f32[12,256,128]{2,1,0:T(8,128)} %shard_map.82, f32[12,256,128]{2,1,0:T(8,128)} %collective-permute-done.2) | non-fusion elementwise | flops 393216 | bytes 4718592 | tf_op jit(solution)/shard_map/add | solution.py:147
  45.0 3.0 %collective-permute-start.5 = (f32[4,1,2,2,1,2,16,128]{7,6,5,4,3,2,0,1:T(8,128)}, f32[4,1,2,2,1,2,16,128]{7,6,5,4,3,2,0,1:T(8,128)}, u32[]{:S(2)}, u32[]{:S(2)}) collective-permute-start(f32[4,1,2,2,1,2,16,128]{7,6,5,4,3,2,0,1:T(8,128)} %constant_dynamic-slice_fusion.9), channel_id=1, source_target_pairs={{0,8},{4,12},{8,0},{12,4},{16,24},{20,28},{24,16},{28,20},{1,9},{5... | collective-permute-start | bytes 786440 | tf_op jit(solution)/shard_map/ppermute | solution.py:98
  51.0 4.2 %gather_fusion = bf16[16,512,256]{2,1,0:T(8,128)(2,1)} fusion(bf16[6,512,256]{2,1,0:T(8,128)(2,1)} %pad_maximum_fusion.6, s32[1024]{0:T(1024)S(1)} %pad_clamp_fusion.4), kind=kCustom, calls=%fused_computation.2 | custom fusion | bytes 8388672 | tf_op jit(solution)/shard_map/jit(_take)/gather | solution.py:151
  55.2 4.9 %fusion.5 = f32[4,512,256]{2,1,0:T(8,128)} fusion(bf16[4,4,256,256]{3,2,1,0:T(8,128)(2,1)S(1)} %copy-done, bf16[4,4,512,256]{3,2,1,0:T(8,128)(2,1)} %bitcast.93, pred[4,4]{1,0:T(4,128)(4,1)} %compare_and_fusion.3), kind=kOutput, calls=%fused_computation.12 | convolution fusion | flops 1075838976 | bytes 8388624 | tf_op jit(solution)/shard_map/jerb,jebc->jrc/dot_general | solution.py:152
  64.2 2.7 %collective-permute-start.14 = (f32[4,1,2,2,1,1,16,128]{7,6,5,4,3,2,0,1:T(8,128)S(1)}, f32[4,1,2,2,1,1,16,128]{7,6,5,4,3,2,0,1:T(8,128)S(1)}, u32[]{:S(2)}, u32[]{:S(2)}) collective-permute-start(f32[4,1,2,2,1,1,16,128]{7,6,5,4,3,2,0,1:T(8,128)S(1)} %constant_dynamic-slice_fusion.2), channel_id=1, source_target_pairs={{0,16},{4,20},{8,24},{12,28},{16,0},{20,4},{24,8},{28,12},{1,17},{... | collective-permute-start | bytes 393224 | tf_op jit(solution)/shard_map/ppermute | solution.py:98
  66.9 1.3 %collective-permute-done.8 = f32[4,1,1,1,2,2,16,128]{7,6,5,4,3,2,0,1:T(8,128)S(1)} collective-permute-done((f32[4,1,1,1,2,2,16,128]{7,6,5,4,3,2,0,1:T(8,128)S(1)}, f32[4,1,1,1,2,2,16,128]{7,6,5,4,3,2,0,1:T(8,128)S(1)}, u32[]{:S(2)}, u32[]{:S(2)}) %collective-permute-start.8) | collective-permute-done | bytes 131104 | tf_op jit(solution)/shard_map/ppermute | solution.py:98
  68.8 3.5 %collective-permute-done.11 = f32[4,1,2,1,1,2,16,128]{7,6,5,4,3,2,0,1:T(8,128)S(1)} collective-permute-done((f32[4,1,2,1,1,2,16,128]{7,6,5,4,3,2,0,1:T(8,128)S(1)}, f32[4,1,2,1,1,2,16,128]{7,6,5,4,3,2,0,1:T(8,128)S(1)}, u32[]{:S(2)}, u32[]{:S(2)}) %collective-permute-start.11) | collective-permute-done | bytes 131104 | tf_op jit(solution)/shard_map/ppermute | solution.py:98
  72.9 2.1 %collective-permute-start.15 = (f32[4,1,1,2,1,1,16,128]{7,6,5,4,3,2,0,1:T(8,128)S(1)}, f32[4,1,1,2,1,1,16,128]{7,6,5,4,3,2,0,1:T(8,128)S(1)}, u32[]{:S(2)}, u32[]{:S(2)}) collective-permute-start(f32[4,1,1,2,1,1,16,128]{7,6,5,4,3,2,0,1:T(8,128)S(1)} %constant_dynamic-slice_fusion.1), channel_id=1, source_target_pairs={{0,2},{1,3},{2,0},{3,1},{4,6},{5,7},{6,4},{7,5},{8,10},{9,11},{10,... | collective-permute-start | bytes 196616 | tf_op jit(solution)/shard_map/ppermute | solution.py:98
  75.0 2.2 %collective-permute-start.10 = (f32[4,1,1,1,1,1,16,128]{7,6,5,4,3,2,0,1:T(8,128)S(1)}, f32[4,1,1,1,1,1,16,128]{7,6,5,4,3,2,0,1:T(8,128)S(1)}, u32[]{:S(2)}, u32[]{:S(2)}) collective-permute-start(f32[4,1,1,1,1,1,16,128]{7,6,5,4,3,2,0,1:T(8,128)S(1)} %constant_dynamic-slice_fusion.6), channel_id=1, source_target_pairs={{0,16},{4,20},{8,24},{12,28},{16,0},{20,4},{24,8},{28,12},{1,17},{... | collective-permute-start | bytes 98312 | tf_op jit(solution)/shard_map/ppermute | solution.py:98
  77.6 1.8 %collective-permute-start.13 = (f32[4,1,1,1,1,1,16,128]{7,6,5,4,3,2,0,1:T(8,128)S(1)}, f32[4,1,1,1,1,1,16,128]{7,6,5,4,3,2,0,1:T(8,128)S(1)}, u32[]{:S(2)}, u32[]{:S(2)}) collective-permute-start(f32[4,1,1,1,1,1,16,128]{7,6,5,4,3,2,0,1:T(8,128)S(1)} %constant_dynamic-slice_fusion.3), channel_id=1, source_target_pairs={{0,2},{1,3},{2,0},{3,1},{4,6},{5,7},{6,4},{7,5},{8,10},{9,11},{10,... | collective-permute-start | bytes 98312 | tf_op jit(solution)/shard_map/ppermute | solution.py:98
  81.5 1.8 %collective-permute-done.16 = f32[4,1,1,1,1,1,16,128]{7,6,5,4,3,2,0,1:T(8,128)S(1)} collective-permute-done((f32[4,1,1,1,1,1,16,128]{7,6,5,4,3,2,0,1:T(8,128)S(1)}, f32[4,1,1,1,1,1,16,128]{7,6,5,4,3,2,0,1:T(8,128)S(1)}, u32[]{:S(2)}, u32[]{:S(2)}) %collective-permute-start.16) | collective-permute-done | bytes 32800 | tf_op jit(solution)/shard_map/ppermute | solution.py:98
  84.0 1.5 %fusion.11 = bf16[12,16,128]{2,1,0:T(8,128)(2,1)S(1)} fusion(bf16[6,4,136,128]{3,2,1,0:T(8,128)(2,1)} %collective-permute-done.7, bf16[3,4,136,128]{3,2,1,0:T(8,128)(2,1)S(1)} %copy-done.11, bf16[3,4,8,128]{3,2,1,0:T(8,128)(2,1)} %copy-done.12, bf16[3,4,128,128]{3,2,1,0:T(8,128)(2,1)S(1)} %copy-done.4, bf16[12,4,16,128]{3,2,1,0:T(8,128)(2,1)S(1)} %bitcast.103, ...), kind=kOutput, calls=%fused_computation.20 | convolution fusion | flops 31580160 | bytes 1916976 | tf_op jit(solution)/shard_map/nerc,necd->nrd/dot_general | solution.py:160
  88.9 2.0 %collective-permute-done.17 = bf16[4,1,1,1,1,1,16,128]{7,6,0,5,4,3,2,1:T(8,128)(2,1)S(1)} collective-permute-done((bf16[4,1,1,1,1,1,16,128]{7,6,0,5,4,3,2,1:T(8,128)(2,1)S(1)}, bf16[4,1,1,1,1,1,16,128]{7,6,0,5,4,3,2,1:T(8,128)(2,1)S(1)}, u32[]{:S(2)}, u32[]{:S(2)}) %collective-permute-start.17) | collective-permute-done | bytes 16416 | tf_op jit(solution)/shard_map/ppermute | solution.py:103
  92.1 2.2 %collective-permute-start.22 = (bf16[4,1,2,1,1,1,16,128]{7,6,0,5,4,3,2,1:T(8,128)(2,1)S(1)}, bf16[4,1,2,1,1,1,16,128]{7,6,0,5,4,3,2,1:T(8,128)(2,1)S(1)}, u32[]{:S(2)}, u32[]{:S(2)}) collective-permute-start(bf16[4,1,2,1,1,1,16,128]{7,6,0,5,4,3,2,1:T(8,128)(2,1)S(1)} %maximum_select_fusion.16), channel_id=1, source_target_pairs={{0,16},{4,20},{8,24},{12,28},{16,0},{20,4},{24,8},{28,12},{1,17},{... | collective-permute-start | bytes 98312 | tf_op jit(solution)/shard_map/ppermute | solution.py:103
  94.2 1.8 %collective-permute-start.26 = (bf16[4,1,1,2,1,1,16,128]{7,6,0,5,4,3,2,1:T(8,128)(2,1)S(1)}, bf16[4,1,1,2,1,1,16,128]{7,6,0,5,4,3,2,1:T(8,128)(2,1)S(1)}, u32[]{:S(2)}, u32[]{:S(2)}) collective-permute-start(bf16[4,1,1,2,1,1,16,128]{7,6,0,5,4,3,2,1:T(8,128)(2,1)S(1)} %maximum_select_fusion.18), channel_id=1, source_target_pairs={{0,2},{1,3},{2,0},{3,1},{4,6},{5,7},{6,4},{7,5},{8,10},{9,11},{10,... | collective-permute-start | bytes 98312 | tf_op jit(solution)/shard_map/ppermute | solution.py:103
  98.6 1.6 %collective-permute-start.27 = (bf16[4,1,2,2,1,1,16,128]{7,6,0,5,4,3,2,1:T(8,128)(2,1)S(1)}, bf16[4,1,2,2,1,1,16,128]{7,6,0,5,4,3,2,1:T(8,128)(2,1)S(1)}, u32[]{:S(2)}, u32[]{:S(2)}) collective-permute-start(bf16[4,1,2,2,1,1,16,128]{7,6,0,5,4,3,2,1:T(8,128)(2,1)S(1)} %fusion.25), channel_id=1, source_target_pairs={{0,16},{4,20},{8,24},{12,28},{16,0},{20,4},{24,8},{28,12},{1,17},{... | collective-permute-start | bytes 196616 | tf_op jit(solution)/shard_map/ppermute | solution.py:103
  100.5 1.5 %collective-permute-start.20 = (bf16[4,1,1,2,2,2,16,128]{7,6,0,5,4,3,2,1:T(8,128)(2,1)S(1)}, bf16[4,1,1,2,2,2,16,128]{7,6,0,5,4,3,2,1:T(8,128)(2,1)S(1)}, u32[]{:S(2)}, u32[]{:S(2)}) collective-permute-start(bf16[4,1,1,2,2,2,16,128]{7,6,0,5,4,3,2,1:T(8,128)(2,1)S(1)} %maximum_select_fusion.5), channel_id=1, source_target_pairs={{0,2},{1,3},{2,0},{3,1},{4,6},{5,7},{6,4},{7,5},{8,10},{9,11},{10,... | collective-permute-start | bytes 393224 | tf_op jit(solution)/shard_map/ppermute | solution.py:103
  102.4 1.2 %collective-permute-start.24 = (bf16[4,1,2,1,2,2,16,128]{7,6,0,5,4,3,2,1:T(8,128)(2,1)S(1)}, bf16[4,1,2,1,2,2,16,128]{7,6,0,5,4,3,2,1:T(8,128)(2,1)S(1)}, u32[]{:S(2)}, u32[]{:S(2)}) collective-permute-start(bf16[4,1,2,1,2,2,16,128]{7,6,0,5,4,3,2,1:T(8,128)(2,1)S(1)} %maximum_select_fusion.6), channel_id=1, source_target_pairs={{0,4},{4,0},{8,12},{12,8},{16,20},{20,16},{24,28},{28,24},{1,5},{5... | collective-permute-start | bytes 393224 | tf_op jit(solution)/shard_map/ppermute | solution.py:103
  103.9 1.6 %collective-permute-start.28 = (bf16[4,1,2,2,1,2,16,128]{7,6,0,5,4,3,2,1:T(8,128)(2,1)S(1)}, bf16[4,1,2,2,1,2,16,128]{7,6,0,5,4,3,2,1:T(8,128)(2,1)S(1)}, u32[]{:S(2)}, u32[]{:S(2)}) collective-permute-start(bf16[4,1,2,2,1,2,16,128]{7,6,0,5,4,3,2,1:T(8,128)(2,1)S(1)} %maximum_select_fusion.7), channel_id=1, source_target_pairs={{0,8},{4,12},{8,0},{12,4},{16,24},{20,28},{24,16},{28,20},{1,9},{5... | collective-permute-start | bytes 393224 | tf_op jit(solution)/shard_map/ppermute | solution.py:103
  105.6 1.8 %collective-permute-done.24 = bf16[4,1,2,1,2,2,16,128]{7,6,0,5,4,3,2,1:T(8,128)(2,1)S(1)} collective-permute-done((bf16[4,1,2,1,2,2,16,128]{7,6,0,5,4,3,2,1:T(8,128)(2,1)S(1)}, bf16[4,1,2,1,2,2,16,128]{7,6,0,5,4,3,2,1:T(8,128)(2,1)S(1)}, u32[]{:S(2)}, u32[]{:S(2)}) %collective-permute-start.24) | collective-permute-done | bytes 131104 | tf_op jit(solution)/shard_map/ppermute | solution.py:103
  107.5 1.4 %collective-permute-done.28 = bf16[4,1,2,2,1,2,16,128]{7,6,0,5,4,3,2,1:T(8,128)(2,1)S(1)} collective-permute-done((bf16[4,1,2,2,1,2,16,128]{7,6,0,5,4,3,2,1:T(8,128)(2,1)S(1)}, bf16[4,1,2,2,1,2,16,128]{7,6,0,5,4,3,2,1:T(8,128)(2,1)S(1)}, u32[]{:S(2)}, u32[]{:S(2)}) %collective-permute-start.28) | collective-permute-done | bytes 131104 | tf_op jit(solution)/shard_map/ppermute | solution.py:103
  110.1 1.4 %collective-permute-done.29 = bf16[12,256,128]{2,1,0:T(8,128)(2,1)} collective-permute-done((bf16[12,256,128]{2,1,0:T(8,128)(2,1)S(1)}, bf16[12,256,128]{2,1,0:T(8,128)(2,1)}, u32[]{:S(2)}, u32[]{:S(2)}) %collective-permute-start.29) | collective-permute-done | bytes 786464 | tf_op jit(solution)/shard_map/ppermute | solution.py:169
  111.5 1.8 %gather_fusion.5 = bf16[8,256,128]{2,1,0:T(8,128)(2,1)S(1)} fusion(bf16[12,256,128]{2,1,0:T(8,128)(2,1)} %collective-permute-done.29, s32[1024]{0:T(1024)S(1)} %pad_clamp_fusion), kind=kCustom, calls=%fused_computation.1.clone | custom fusion | bytes 1048608 | tf_op jit(solution)/shard_map/jit(_take)/gather | solution.py:171
  115.9 1.2 %fusion.3 = bf16[4,512,256]{2,1,0:T(8,128)(2,1)} fusion(f32[4,512,256]{2,1,0:T(8,128)S(1)} %copy-done.5, f32[4,512,256,1]{2,1,3,0:T(8,128)S(1)} %fusion.12), kind=kLoop, calls=%fused_computation.10 | loop fusion | flops 1048576 | bytes 5242880 | tf_op jit(solution)/shard_map/convert_element_type | solution.py:179
  (161 shorter events, 32.2 us)
Async XLA Ops:
  0.0 55.2 %copy-start = (bf16[4,4,256,256]{3,2,1,0:T(8,128)(2,1)S(1)}, bf16[4,4,256,256]{3,2,1,0:T(8,128)(2,1)}, u32[]{:S(2)}) copy-start(bf16[4,4,256,256]{3,2,1,0:T(8,128)(2,1)} %param.12) | copy-start | bytes 6291460
  6.7 34.6 %collective-permute-start.2 = (f32[12,256,128]{2,1,0:T(8,128)}, f32[12,256,128]{2,1,0:T(8,128)}, u32[]{:S(2)}, u32[]{:S(2)}) collective-permute-start(f32[12,256,128]{2,1,0:T(8,128)} %shard_map.83), channel_id=1, source_target_pairs={{0,1},{1,0},{2,3},{3,2},{4,5},{5,4},{6,7},{7,6},{8,9},{9,8},{10,11... | collective-permute-start | bytes 4718600 | tf_op jit(solution)/shard_map/ppermute | solution.py:146
  8.0 29.6 %collective-permute-start = (bf16[1,512,256]{2,1,0:T(8,128)(2,1)}, bf16[1,512,256]{2,1,0:T(8,128)(2,1)}, u32[]{:S(2)}, u32[]{:S(2)}) collective-permute-start(bf16[1,512,256]{2,1,0:T(8,128)(2,1)} %get-tuple-element.23), channel_id=1, source_target_pairs={{0,1},{1,2},{2,3},{3,4},{4,5},{5,6},{6,7},{7,8},{8,9},{9,10},{10,1... | collective-permute-start | bytes 786440 | tf_op jit(solution)/shard_map/ppermute | solution.py:65
  10.7 26.9 %collective-permute-start.1 = (bf16[1,512,256]{2,1,0:T(8,128)(2,1)}, bf16[1,512,256]{2,1,0:T(8,128)(2,1)}, u32[]{:S(2)}, u32[]{:S(2)}) collective-permute-start(bf16[1,512,256]{2,1,0:T(8,128)(2,1)} %get-tuple-element.24), channel_id=1, source_target_pairs={{1,0},{2,1},{3,2},{4,3},{5,4},{6,5},{7,6},{8,7},{9,8},{10,9},{11,1... | collective-permute-start | bytes 786440 | tf_op jit(solution)/shard_map/ppermute | solution.py:67
  12.1 16.9 %collective-permute-start.6 = (bf16[3,4,136,128]{3,2,1,0:T(8,128)(2,1)S(1)}, bf16[3,4,136,128]{3,2,1,0:T(8,128)(2,1)S(1)}, u32[]{:S(2)}, u32[]{:S(2)}) collective-permute-start(bf16[3,4,136,128]{3,2,1,0:T(8,128)(2,1)S(1)} %pad_maximum_fusion.13), channel_id=1, source_target_pairs={{0,2},{1,3},{2,0},{3,1},{4,6},{5,7},{6,4},{7,5},{8,10},{9,11},{10,... | collective-permute-start | bytes 1253384 | tf_op jit(solution)/shard_map/ppermute | solution.py:122
  30.8 9.2 %collective-permute-start.7 = (bf16[6,4,136,128]{3,2,1,0:T(8,128)(2,1)}, bf16[6,4,136,128]{3,2,1,0:T(8,128)(2,1)}, u32[]{:S(2)}, u32[]{:S(2)}) collective-permute-start(bf16[6,4,136,128]{3,2,1,0:T(8,128)(2,1)} %pad_maximum_fusion.11), channel_id=1, source_target_pairs={{0,1},{1,0},{2,3},{3,2},{4,5},{5,4},{6,7},{7,6},{8,9},{9,8},{10,11... | collective-permute-start | bytes 2506760 | tf_op jit(solution)/shard_map/ppermute | solution.py:122
  45.0 15.1 %collective-permute-start.5 = (f32[4,1,2,2,1,2,16,128]{7,6,5,4,3,2,0,1:T(8,128)}, f32[4,1,2,2,1,2,16,128]{7,6,5,4,3,2,0,1:T(8,128)}, u32[]{:S(2)}, u32[]{:S(2)}) collective-permute-start(f32[4,1,2,2,1,2,16,128]{7,6,5,4,3,2,0,1:T(8,128)} %constant_dynamic-slice_fusion.9), channel_id=1, source_target_pairs={{0,8},{4,12},{8,0},{12,4},{16,24},{20,28},{24,16},{28,20},{1,9},{5... | collective-permute-start | bytes 786440 | tf_op jit(solution)/shard_map/ppermute | solution.py:98
  48.7 12.4 %collective-permute-start.4 = (f32[4,1,2,1,2,2,16,128]{7,6,5,4,3,2,0,1:T(8,128)}, f32[4,1,2,1,2,2,16,128]{7,6,5,4,3,2,0,1:T(8,128)}, u32[]{:S(2)}, u32[]{:S(2)}) collective-permute-start(f32[4,1,2,1,2,2,16,128]{7,6,5,4,3,2,0,1:T(8,128)} %constant_dynamic-slice_fusion.10), channel_id=1, source_target_pairs={{0,4},{4,0},{8,12},{12,8},{16,20},{20,16},{24,28},{28,24},{1,5},{5... | collective-permute-start | bytes 786440 | tf_op jit(solution)/shard_map/ppermute | solution.py:98
  50.0 12.1 %collective-permute-start.3 = (f32[4,1,1,2,2,2,16,128]{7,6,5,4,3,2,0,1:T(8,128)}, f32[4,1,1,2,2,2,16,128]{7,6,5,4,3,2,0,1:T(8,128)}, u32[]{:S(2)}, u32[]{:S(2)}) collective-permute-start(f32[4,1,1,2,2,2,16,128]{7,6,5,4,3,2,0,1:T(8,128)} %constant_dynamic-slice_fusion.11), channel_id=1, source_target_pairs={{0,2},{1,3},{2,0},{3,1},{4,6},{5,7},{6,4},{7,5},{8,10},{9,11},{10,... | collective-permute-start | bytes 786440 | tf_op jit(solution)/shard_map/ppermute | solution.py:98
  63.1 20.9 %copy-start.11 = (bf16[3,4,136,128]{3,2,1,0:T(8,128)(2,1)S(1)}, bf16[3,4,136,128]{3,2,1,0:T(8,128)(2,1)}, u32[]{:S(2)}) copy-start(bf16[3,4,136,128]{3,2,1,0:T(8,128)(2,1)} %copy-done.9) | copy-start | bytes 1253380
  63.2 5.1 %collective-permute-start.8 = (f32[4,1,1,1,2,2,16,128]{7,6,5,4,3,2,0,1:T(8,128)S(1)}, f32[4,1,1,1,2,2,16,128]{7,6,5,4,3,2,0,1:T(8,128)S(1)}, u32[]{:S(2)}, u32[]{:S(2)}) collective-permute-start(f32[4,1,1,1,2,2,16,128]{7,6,5,4,3,2,0,1:T(8,128)S(1)} %constant_dynamic-slice_fusion.8), channel_id=1, source_target_pairs={{0,4},{4,0},{8,12},{12,8},{16,20},{20,16},{24,28},{28,24},{1,5},{5... | collective-permute-start | bytes 393224 | tf_op jit(solution)/shard_map/ppermute | solution.py:98
  63.7 8.5 %collective-permute-start.11 = (f32[4,1,2,1,1,2,16,128]{7,6,5,4,3,2,0,1:T(8,128)S(1)}, f32[4,1,2,1,1,2,16,128]{7,6,5,4,3,2,0,1:T(8,128)S(1)}, u32[]{:S(2)}, u32[]{:S(2)}) collective-permute-start(f32[4,1,2,1,1,2,16,128]{7,6,5,4,3,2,0,1:T(8,128)S(1)} %constant_dynamic-slice_fusion.5), channel_id=1, source_target_pairs={{0,8},{4,12},{8,0},{12,4},{16,24},{20,28},{24,16},{28,20},{1,9},{5... | collective-permute-start | bytes 393224 | tf_op jit(solution)/shard_map/ppermute | solution.py:98
  64.2 8.7 %collective-permute-start.14 = (f32[4,1,2,2,1,1,16,128]{7,6,5,4,3,2,0,1:T(8,128)S(1)}, f32[4,1,2,2,1,1,16,128]{7,6,5,4,3,2,0,1:T(8,128)S(1)}, u32[]{:S(2)}, u32[]{:S(2)}) collective-permute-start(f32[4,1,2,2,1,1,16,128]{7,6,5,4,3,2,0,1:T(8,128)S(1)} %constant_dynamic-slice_fusion.2), channel_id=1, source_target_pairs={{0,16},{4,20},{8,24},{12,28},{16,0},{20,4},{24,8},{28,12},{1,17},{... | collective-permute-start | bytes 393224 | tf_op jit(solution)/shard_map/ppermute | solution.py:98
  68.3 6.8 %collective-permute-start.9 = (f32[4,1,1,1,1,2,16,128]{7,6,5,4,3,2,0,1:T(8,128)S(1)}, f32[4,1,1,1,1,2,16,128]{7,6,5,4,3,2,0,1:T(8,128)S(1)}, u32[]{:S(2)}, u32[]{:S(2)}) collective-permute-start(f32[4,1,1,1,1,2,16,128]{7,6,5,4,3,2,0,1:T(8,128)S(1)} %constant_dynamic-slice_fusion.7), channel_id=1, source_target_pairs={{0,8},{4,12},{8,0},{12,4},{16,24},{20,28},{24,16},{28,20},{1,9},{5... | collective-permute-start | bytes 196616 | tf_op jit(solution)/shard_map/ppermute | solution.py:98
  72.3 5.2 %collective-permute-start.12 = (f32[4,1,2,1,1,1,16,128]{7,6,5,4,3,2,0,1:T(8,128)S(1)}, f32[4,1,2,1,1,1,16,128]{7,6,5,4,3,2,0,1:T(8,128)S(1)}, u32[]{:S(2)}, u32[]{:S(2)}) collective-permute-start(f32[4,1,2,1,1,1,16,128]{7,6,5,4,3,2,0,1:T(8,128)S(1)} %constant_dynamic-slice_fusion.4), channel_id=1, source_target_pairs={{0,16},{4,20},{8,24},{12,28},{16,0},{20,4},{24,8},{28,12},{1,17},{... | collective-permute-start | bytes 196616 | tf_op jit(solution)/shard_map/ppermute | solution.py:98
  72.9 6.4 %collective-permute-start.15 = (f32[4,1,1,2,1,1,16,128]{7,6,5,4,3,2,0,1:T(8,128)S(1)}, f32[4,1,1,2,1,1,16,128]{7,6,5,4,3,2,0,1:T(8,128)S(1)}, u32[]{:S(2)}, u32[]{:S(2)}) collective-permute-start(f32[4,1,1,2,1,1,16,128]{7,6,5,4,3,2,0,1:T(8,128)S(1)} %constant_dynamic-slice_fusion.1), channel_id=1, source_target_pairs={{0,2},{1,3},{2,0},{3,1},{4,6},{5,7},{6,4},{7,5},{8,10},{9,11},{10,... | collective-permute-start | bytes 196616 | tf_op jit(solution)/shard_map/ppermute | solution.py:98
  75.0 5.4 %collective-permute-start.10 = (f32[4,1,1,1,1,1,16,128]{7,6,5,4,3,2,0,1:T(8,128)S(1)}, f32[4,1,1,1,1,1,16,128]{7,6,5,4,3,2,0,1:T(8,128)S(1)}, u32[]{:S(2)}, u32[]{:S(2)}) collective-permute-start(f32[4,1,1,1,1,1,16,128]{7,6,5,4,3,2,0,1:T(8,128)S(1)} %constant_dynamic-slice_fusion.6), channel_id=1, source_target_pairs={{0,16},{4,20},{8,24},{12,28},{16,0},{20,4},{24,8},{28,12},{1,17},{... | collective-permute-start | bytes 98312 | tf_op jit(solution)/shard_map/ppermute | solution.py:98
  77.6 4.0 %collective-permute-start.13 = (f32[4,1,1,1,1,1,16,128]{7,6,5,4,3,2,0,1:T(8,128)S(1)}, f32[4,1,1,1,1,1,16,128]{7,6,5,4,3,2,0,1:T(8,128)S(1)}, u32[]{:S(2)}, u32[]{:S(2)}) collective-permute-start(f32[4,1,1,1,1,1,16,128]{7,6,5,4,3,2,0,1:T(8,128)S(1)} %constant_dynamic-slice_fusion.3), channel_id=1, source_target_pairs={{0,2},{1,3},{2,0},{3,1},{4,6},{5,7},{6,4},{7,5},{8,10},{9,11},{10,... | collective-permute-start | bytes 98312 | tf_op jit(solution)/shard_map/ppermute | solution.py:98
  79.4 4.0 %collective-permute-start.16 = (f32[4,1,1,1,1,1,16,128]{7,6,5,4,3,2,0,1:T(8,128)S(1)}, f32[4,1,1,1,1,1,16,128]{7,6,5,4,3,2,0,1:T(8,128)S(1)}, u32[]{:S(2)}, u32[]{:S(2)}) collective-permute-start(f32[4,1,1,1,1,1,16,128]{7,6,5,4,3,2,0,1:T(8,128)S(1)} %constant_dynamic-slice_fusion), channel_id=1, source_target_pairs={{0,4},{4,0},{8,12},{12,8},{16,20},{20,16},{24,28},{28,24},{1,5},{5... | collective-permute-start | bytes 98312 | tf_op jit(solution)/shard_map/ppermute | solution.py:98
  86.3 4.7 %collective-permute-start.17 = (bf16[4,1,1,1,1,1,16,128]{7,6,0,5,4,3,2,1:T(8,128)(2,1)S(1)}, bf16[4,1,1,1,1,1,16,128]{7,6,0,5,4,3,2,1:T(8,128)(2,1)S(1)}, u32[]{:S(2)}, u32[]{:S(2)}) collective-permute-start(bf16[4,1,1,1,1,1,16,128]{7,6,0,5,4,3,2,1:T(8,128)(2,1)S(1)} %get-tuple-element.26), channel_id=1, source_target_pairs={{0,16},{4,20},{8,24},{12,28},{16,0},{20,4},{24,8},{28,12},{1,17},{... | collective-permute-start | bytes 49160 | tf_op jit(solution)/shard_map/ppermute | solution.py:103
  87.2 4.9 %collective-permute-start.21 = (bf16[4,1,1,1,1,1,16,128]{7,6,0,5,4,3,2,1:T(8,128)(2,1)S(1)}, bf16[4,1,1,1,1,1,16,128]{7,6,0,5,4,3,2,1:T(8,128)(2,1)S(1)}, u32[]{:S(2)}, u32[]{:S(2)}) collective-permute-start(bf16[4,1,1,1,1,1,16,128]{7,6,0,5,4,3,2,1:T(8,128)(2,1)S(1)} %get-tuple-element.27), channel_id=1, source_target_pairs={{0,2},{1,3},{2,0},{3,1},{4,6},{5,7},{6,4},{7,5},{8,10},{9,11},{10,... | collective-permute-start | bytes 49160 | tf_op jit(solution)/shard_map/ppermute | solution.py:103
  88.4 5.9 %collective-permute-start.25 = (bf16[4,1,1,1,1,1,16,128]{7,6,0,5,4,3,2,1:T(8,128)(2,1)S(1)}, bf16[4,1,1,1,1,1,16,128]{7,6,0,5,4,3,2,1:T(8,128)(2,1)S(1)}, u32[]{:S(2)}, u32[]{:S(2)}) collective-permute-start(bf16[4,1,1,1,1,1,16,128]{7,6,0,5,4,3,2,1:T(8,128)(2,1)S(1)} %get-tuple-element.28), channel_id=1, source_target_pairs={{0,4},{4,0},{8,12},{12,8},{16,20},{20,16},{24,28},{28,24},{1,5},{5... | collective-permute-start | bytes 49160 | tf_op jit(solution)/shard_map/ppermute | solution.py:103
  91.0 5.2 %collective-permute-start.18 = (bf16[4,1,1,1,1,2,16,128]{7,6,0,5,4,3,2,1:T(8,128)(2,1)S(1)}, bf16[4,1,1,1,1,2,16,128]{7,6,0,5,4,3,2,1:T(8,128)(2,1)S(1)}, u32[]{:S(2)}, u32[]{:S(2)}) collective-permute-start(bf16[4,1,1,1,1,2,16,128]{7,6,0,5,4,3,2,1:T(8,128)(2,1)S(1)} %maximum_select_fusion.14), channel_id=1, source_target_pairs={{0,8},{4,12},{8,0},{12,4},{16,24},{20,28},{24,16},{28,20},{1,9},{5... | collective-permute-start | bytes 98312 | tf_op jit(solution)/shard_map/ppermute | solution.py:103
  92.1 5.9 %collective-permute-start.22 = (bf16[4,1,2,1,1,1,16,128]{7,6,0,5,4,3,2,1:T(8,128)(2,1)S(1)}, bf16[4,1,2,1,1,1,16,128]{7,6,0,5,4,3,2,1:T(8,128)(2,1)S(1)}, u32[]{:S(2)}, u32[]{:S(2)}) collective-permute-start(bf16[4,1,2,1,1,1,16,128]{7,6,0,5,4,3,2,1:T(8,128)(2,1)S(1)} %maximum_select_fusion.16), channel_id=1, source_target_pairs={{0,16},{4,20},{8,24},{12,28},{16,0},{20,4},{24,8},{28,12},{1,17},{... | collective-permute-start | bytes 98312 | tf_op jit(solution)/shard_map/ppermute | solution.py:103
  94.2 4.4 %collective-permute-start.26 = (bf16[4,1,1,2,1,1,16,128]{7,6,0,5,4,3,2,1:T(8,128)(2,1)S(1)}, bf16[4,1,1,2,1,1,16,128]{7,6,0,5,4,3,2,1:T(8,128)(2,1)S(1)}, u32[]{:S(2)}, u32[]{:S(2)}) collective-permute-start(bf16[4,1,1,2,1,1,16,128]{7,6,0,5,4,3,2,1:T(8,128)(2,1)S(1)} %maximum_select_fusion.18), channel_id=1, source_target_pairs={{0,2},{1,3},{2,0},{3,1},{4,6},{5,7},{6,4},{7,5},{8,10},{9,11},{10,... | collective-permute-start | bytes 98312 | tf_op jit(solution)/shard_map/ppermute | solution.py:103
  96.2 4.3 %collective-permute-start.19 = (bf16[4,1,1,1,2,2,16,128]{7,6,0,5,4,3,2,1:T(8,128)(2,1)S(1)}, bf16[4,1,1,1,2,2,16,128]{7,6,0,5,4,3,2,1:T(8,128)(2,1)S(1)}, u32[]{:S(2)}, u32[]{:S(2)}) collective-permute-start(bf16[4,1,1,1,2,2,16,128]{7,6,0,5,4,3,2,1:T(8,128)(2,1)S(1)} %maximum_select_fusion.9), channel_id=1, source_target_pairs={{0,4},{4,0},{8,12},{12,8},{16,20},{20,16},{24,28},{28,24},{1,5},{5... | collective-permute-start | bytes 196616 | tf_op jit(solution)/shard_map/ppermute | solution.py:103
  98.0 4.3 %collective-permute-start.23 = (bf16[4,1,2,1,1,2,16,128]{7,6,0,5,4,3,2,1:T(8,128)(2,1)S(1)}, bf16[4,1,2,1,1,2,16,128]{7,6,0,5,4,3,2,1:T(8,128)(2,1)S(1)}, u32[]{:S(2)}, u32[]{:S(2)}) collective-permute-start(bf16[4,1,2,1,1,2,16,128]{7,6,0,5,4,3,2,1:T(8,128)(2,1)S(1)} %maximum_select_fusion.11), channel_id=1, source_target_pairs={{0,8},{4,12},{8,0},{12,4},{16,24},{20,28},{24,16},{28,20},{1,9},{5... | collective-permute-start | bytes 196616 | tf_op jit(solution)/shard_map/ppermute | solution.py:103
  98.6 5.2 %collective-permute-start.27 = (bf16[4,1,2,2,1,1,16,128]{7,6,0,5,4,3,2,1:T(8,128)(2,1)S(1)}, bf16[4,1,2,2,1,1,16,128]{7,6,0,5,4,3,2,1:T(8,128)(2,1)S(1)}, u32[]{:S(2)}, u32[]{:S(2)}) collective-permute-start(bf16[4,1,2,2,1,1,16,128]{7,6,0,5,4,3,2,1:T(8,128)(2,1)S(1)} %fusion.25), channel_id=1, source_target_pairs={{0,16},{4,20},{8,24},{12,28},{16,0},{20,4},{24,8},{28,12},{1,17},{... | collective-permute-start | bytes 196616 | tf_op jit(solution)/shard_map/ppermute | solution.py:103
  100.5 5.0 %collective-permute-start.20 = (bf16[4,1,1,2,2,2,16,128]{7,6,0,5,4,3,2,1:T(8,128)(2,1)S(1)}, bf16[4,1,1,2,2,2,16,128]{7,6,0,5,4,3,2,1:T(8,128)(2,1)S(1)}, u32[]{:S(2)}, u32[]{:S(2)}) collective-permute-start(bf16[4,1,1,2,2,2,16,128]{7,6,0,5,4,3,2,1:T(8,128)(2,1)S(1)} %maximum_select_fusion.5), channel_id=1, source_target_pairs={{0,2},{1,3},{2,0},{3,1},{4,6},{5,7},{6,4},{7,5},{8,10},{9,11},{10,... | collective-permute-start | bytes 393224 | tf_op jit(solution)/shard_map/ppermute | solution.py:103
  102.4 5.0 %collective-permute-start.24 = (bf16[4,1,2,1,2,2,16,128]{7,6,0,5,4,3,2,1:T(8,128)(2,1)S(1)}, bf16[4,1,2,1,2,2,16,128]{7,6,0,5,4,3,2,1:T(8,128)(2,1)S(1)}, u32[]{:S(2)}, u32[]{:S(2)}) collective-permute-start(bf16[4,1,2,1,2,2,16,128]{7,6,0,5,4,3,2,1:T(8,128)(2,1)S(1)} %maximum_select_fusion.6), channel_id=1, source_target_pairs={{0,4},{4,0},{8,12},{12,8},{16,20},{20,16},{24,28},{28,24},{1,5},{5... | collective-permute-start | bytes 393224 | tf_op jit(solution)/shard_map/ppermute | solution.py:103
  103.9 5.0 %collective-permute-start.28 = (bf16[4,1,2,2,1,2,16,128]{7,6,0,5,4,3,2,1:T(8,128)(2,1)S(1)}, bf16[4,1,2,2,1,2,16,128]{7,6,0,5,4,3,2,1:T(8,128)(2,1)S(1)}, u32[]{:S(2)}, u32[]{:S(2)}) collective-permute-start(bf16[4,1,2,2,1,2,16,128]{7,6,0,5,4,3,2,1:T(8,128)(2,1)S(1)} %maximum_select_fusion.7), channel_id=1, source_target_pairs={{0,8},{4,12},{8,0},{12,4},{16,24},{20,28},{24,16},{28,20},{1,9},{5... | collective-permute-start | bytes 393224 | tf_op jit(solution)/shard_map/ppermute | solution.py:103
  109.0 2.5 %collective-permute-start.29 = (bf16[12,256,128]{2,1,0:T(8,128)(2,1)S(1)}, bf16[12,256,128]{2,1,0:T(8,128)(2,1)}, u32[]{:S(2)}, u32[]{:S(2)}) collective-permute-start(bf16[12,256,128]{2,1,0:T(8,128)(2,1)S(1)} %pad_maximum_fusion.12), channel_id=1, source_target_pairs={{0,1},{1,0},{2,3},{3,2},{4,5},{5,4},{6,7},{7,6},{8,9},{9,8},{10,11... | collective-permute-start | bytes 2359304 | tf_op jit(solution)/shard_map/ppermute | solution.py:169
  (17 other events, 114.2 us)

commit v15 on v12

--- a/solution.py
+++ b/solution.py
@@ -116,13 +116,12 @@
 def per_device(residual, margin, inverse_blocks, interface, basis, coarse_pattern, coarse_inverse):
     rows, cols = coarse_inverse.shape[-2:]
     tags = jnp.broadcast_to(coarse_pattern.astype(jnp.bfloat16)[:, :, None, None], coarse_pattern.shape + (8, cols))
-    packed = lax.all_gather(jnp.concatenate([coarse_inverse, tags], axis=2), "coarse", axis=0, tiled=True)
-    inverse_all = packed[:, :, :rows, :]
-    pattern_all = packed[:, :, rows, 0].astype(jnp.int32)
+    packed = jnp.concatenate([coarse_inverse, tags], axis=2)
+    own_rows = coarse_inverse.shape[0]
     extended = with_halo(residual, ((("sub", "coarse"), 0),), 1)
     rhs = residual.shape[1]
     width = basis.shape[-1]
-    total_blocks = pattern_all.shape[0]
+    total_blocks = own_rows * lax.axis_size("coarse")
     bits = device_bits()
     own_half = bit_of(*bits[0])
     links = interface.reshape(-1)
@@ -142,16 +141,37 @@
     parts = [lax.slice_in_dim(whole, s * per, (s + 1) * per, axis=0) for s in range(streams)]
     picked = jnp.take(extended, margin, axis=0)
     local = jnp.einsum("jerb,jebc->jrc", picked, inverse_blocks, preferred_element_type=jnp.float32)
+    exchanges = list(reversed([bit for bit in bits if bit[0] == "coarse"]))
+    assert nb >= len(exchanges) + 2
+    xors = [0]
+    arriving = None
     for step in range(1, nb):
         parts = [halve(x, 1 + orders[s][step], *bits[orders[s][step]], jnp.float32) for s, x in enumerate(parts)]
         if step == 1:
             local, parts = lax.optimization_barrier((local, parts))
+        k = step - 1
+        if arriving is not None:
+            arriving, parts = lax.optimization_barrier((arriving, parts))
+            packed = jnp.concatenate([packed, arriving], axis=0)
+            arriving = None
+        if k < len(exchanges):
+            packed, parts = lax.optimization_barrier((packed, parts))
+            axis, mask = exchanges[k]
+            arriving = lax.ppermute(packed, axis, pairs(axis, mask))
+            xors = xors + [x ^ mask for x in xors]
+    assert arriving is None
+    slot_of = jnp.array([xors.index(x) for x in range(len(xors))], jnp.int32)
+    labels = jnp.arange(len(xors) * own_rows, dtype=jnp.int32)
+    order = slot_of[(labels // own_rows) ^ lax.axis_index("coarse")] * own_rows + labels % own_rows
+    inverse_all = packed[:, :, :rows, :]
+    pattern_all = packed[:, :, rows, 0].astype(jnp.int32)
     mine = jnp.concatenate(parts, axis=0).reshape(total_blocks, inner, width)
     coarse_in = mine.astype(jnp.bfloat16)
     chosen = jnp.take(coarse_in, pattern_all, axis=0)
     solved = jnp.einsum(
         "nerc,necd->nrd", chosen, inverse_all, preferred_element_type=jnp.float32
     ).astype(jnp.bfloat16)
+    solved = jnp.take(solved, order, axis=0)
     solved = solved.reshape((total_blocks,) + (1,) * nb + (inner, width))
     outs = [lax.slice_in_dim(solved, s * per, (s + 1) * per, axis=0) for s in range(streams)]
     for step in reversed(range(1, nb)):

time: 114 us -> 112 us (0.982)
  between operations: 14 us -> 0.75 us
  waiting for transfers between devices: 16.7 us -> 27.4 us
  local copies, waits for them, and re-layouts: 16 us -> 17.7 us
  starting transfers between devices: 38.9 us -> 37.7 us
    ppermute x0 -> x2, waiting for transfers between devices: none -> 5.83 us  [per_device(): arriving = lax.ppermute(packed, axis, pairs(axis, mask))]
    ppermute x12, waiting for transfers between devices: 7.31 us -> 11.4 us  [double(): recv = lax.ppermute(y, axis, pairs(axis, mask))]
    ppermute x12, starting transfers between devices: 15.3 us -> 13.2 us  [double(): recv = lax.ppermute(y, axis, pairs(axis, mask))]
    ppermute x0 -> x2, starting transfers between devices: none -> 2.08 us  [per_device(): arriving = lax.ppermute(packed, axis, pairs(axis, mask))]
    unnamed x26 -> x33, local copies, waits for them, and re-layouts: 3.84 us -> 5.12 us
    gather x0 -> x2, local copies, waits for them, and re-layouts: none -> 1.23 us  [the longest x1 0.66 us: per_device(): slot_of[labels // own_rows ^ lax.axis_index('coarse')] * own_rows]
    ppermute x12, starting transfers between devices: 19.1 us -> 17.9 us  [halve(): lax.ppermute(send.astype(wire), axis, pairs(axis, mask)).astype(x.dtype)]
  transfers between devices with their start and end apart: 29 -> 30, of which waited for: 13 -> 14; matrix products, arithmetic and copies ran while one was open for 19% -> 17% of each run, Pallas kernels for 5% -> 5%
where the time goes in v15:
time: 112 us; the launch traced here: 111 us
  starting transfers between devices  37.7 us (34%)
  waiting for transfers between devices  27.4 us (24%)
  local copies, waits for them, and re-layouts  17.7 us (16%)
  Pallas kernels  10.2 us (9%)
  other arithmetic  10.1 us (9%)
  matrix products  7.16 us (6%)
    ppermute x12, starting transfers between devices, halve(): lax.ppermute(send.astype(wire), axis, pairs(axis, mask)).astype(x.dtype)  17.9 us
    ppermute x12, starting transfers between devices, double(): recv = lax.ppermute(y, axis, pairs(axis, mask))  13.2 us
    ppermute x12, waiting for transfers between devices, double(): recv = lax.ppermute(y, axis, pairs(axis, mask))  11.4 us
    pallas_call x2, Pallas kernels, restrict(): pl.pallas_call(functools.partial(restrict_kernel, upper=upper), out_shape...  10.2 us
    ppermute x12, waiting for transfers between devices, halve(): lax.ppermute(send.astype(wire), axis, pairs(axis, mask)).astype(x.dtype)  8.73 us
    ppermute x2, waiting for transfers between devices, per_device(): arriving = lax.ppermute(packed, axis, pairs(axis, mask))  5.83 us
    unnamed x33, local copies, waits for them, and re-layouts  5.12 us
    dot_general x1, matrix products, per_device(): jnp.einsum('jerb,jebc->jrc', picked, inverse_blocks, preferred_element_ty...  4.91 us
  transfers between devices with their start and end apart: 30, of which 14 were waited for; matrix products, arithmetic and copies ran while one was open for 17% of the time, Pallas kernels for 5%

profile of v15, /device:TPU:0, one launch (start us, length us, event | category | flops | bytes accessed | tf_op | source)
XLA Modules:
  0.0 110.9 jit_solution(1082971125193411654)
XLA Ops:
  1.6 5.2 %shard_map.83 = f32[12,256,128]{2,1,0:T(8,128)} custom-call(s32[8]{0:T(128)} %reshape.1777.links, s32[1]{0:T(128)} %bitcast.half, bf16[4,512,256]{2,1,0:T(8,128)(2,1)} %residual_ref.3, bf16[4,2,256,128]{3,2,1,0:T(8,128)(2,1)} %basis_ref.3), custom_call_target="tpu_custom_call" | custom-call | flops 134217728 | bytes 3145728 | tf_op jit(solution)/shard_map/pallas_call | solution.py:36
  8.0 2.7 %collective-permute-start = (bf16[1,512,256]{2,1,0:T(8,128)(2,1)}, bf16[1,512,256]{2,1,0:T(8,128)(2,1)}, u32[]{:S(2)}, u32[]{:S(2)}) collective-permute-start(bf16[1,512,256]{2,1,0:T(8,128)(2,1)} %get-tuple-element.55), channel_id=1, source_target_pairs={{0,1},{1,2},{2,3},{3,4},{4,5},{5,6},{6,7},{7,8},{8,9},{9,10},{10,1... | collective-permute-start | bytes 786440 | tf_op jit(solution)/shard_map/ppermute | solution.py:65
  13.9 5.0 %shard_map.82 = f32[12,256,128]{2,1,0:T(8,128)} custom-call(s32[8]{0:T(128)} %reshape.1777.links, s32[1]{0:T(128)} %bitcast.half, bf16[4,512,256]{2,1,0:T(8,128)(2,1)} %residual_ref.3, bf16[4,2,256,128]{3,2,1,0:T(8,128)(2,1)} %basis_ref.3), custom_call_target="tpu_custom_call" | custom-call | flops 134217728 | bytes 3145728 | tf_op jit(solution)/shard_map/pallas_call | solution.py:36
  19.0 2.5 %pad_maximum_fusion = bf16[6,512,256]{2,1,0:T(8,128)(2,1)} fusion(bf16[1,512,256]{2,1,0:T(8,128)(2,1)} %collective-permute-done.1, bf16[4,512,256]{2,1,0:T(8,128)(2,1)S(1)} %copy-done.3, bf16[1,512,256]{2,1,0:T(8,128)(2,1)} %collective-permute-done), kind=kLoop, calls=%fused_computation.15 | loop fusion | flops 1572864 | bytes 3145728 | tf_op jit(solution)/shard_map/concatenate | solution.py:63
  21.5 1.6 %add.233 = f32[12,256,128]{2,1,0:T(8,128)S(1)} add(f32[12,256,128]{2,1,0:T(8,128)S(1)} %copy-done.4, f32[12,256,128]{2,1,0:T(8,128)} %collective-permute-done.2) | non-fusion elementwise | flops 393216 | bytes 4718592 | tf_op jit(solution)/shard_map/add | solution.py:138
  24.8 6.0 %collective-permute-start.5 = (f32[4,1,2,2,1,2,16,128]{7,6,5,4,3,2,0,1:T(8,128)}, f32[4,1,2,2,1,2,16,128]{7,6,5,4,3,2,0,1:T(8,128)}, u32[]{:S(2)}, u32[]{:S(2)}) collective-permute-start(f32[4,1,2,2,1,2,16,128]{7,6,5,4,3,2,0,1:T(8,128)} %constant_dynamic-slice_fusion.9), channel_id=1, source_target_pairs={{0,8},{4,12},{8,0},{12,4},{16,24},{20,28},{24,16},{28,20},{1,9},{5... | collective-permute-start | bytes 786440 | tf_op jit(solution)/shard_map/ppermute | solution.py:98
  32.8 4.2 %gather_fusion = bf16[16,512,256]{2,1,0:T(8,128)(2,1)} fusion(bf16[6,512,256]{2,1,0:T(8,128)(2,1)} %pad_maximum_fusion, s32[1024]{0:T(1024)S(1)} %pad_clamp_fusion.4), kind=kCustom, calls=%fused_computation.2 | custom fusion | bytes 8388672 | tf_op jit(solution)/shard_map/jit(_take)/gather | solution.py:142
  37.0 4.9 %fusion.5 = f32[4,512,256]{2,1,0:T(8,128)} fusion(bf16[4,4,256,256]{3,2,1,0:T(8,128)(2,1)S(1)} %copy-done, bf16[4,4,512,256]{3,2,1,0:T(8,128)(2,1)} %bitcast.93, pred[4,4]{1,0:T(4,128)(4,1)S(1)} %compare_and_fusion.3), kind=kOutput, calls=%fused_computation.12 | convolution fusion | flops 1075838976 | bytes 8388624 | tf_op jit(solution)/shard_map/jerb,jebc->jrc/dot_general | solution.py:143
  45.6 2.7 %collective-permute-start.9 = (f32[4,1,2,2,1,1,16,128]{7,6,5,4,3,2,0,1:T(8,128)S(1)}, f32[4,1,2,2,1,1,16,128]{7,6,5,4,3,2,0,1:T(8,128)S(1)}, u32[]{:S(2)}, u32[]{:S(2)}) collective-permute-start(f32[4,1,2,2,1,1,16,128]{7,6,5,4,3,2,0,1:T(8,128)S(1)} %constant_dynamic-slice_fusion.6), channel_id=1, source_target_pairs={{0,16},{4,20},{8,24},{12,28},{16,0},{20,4},{24,8},{28,12},{1,17},{... | collective-permute-start | bytes 393224 | tf_op jit(solution)/shard_map/ppermute | solution.py:98
  49.1 2.0 %collective-permute-start.6 = (bf16[3,4,136,128]{3,2,1,0:T(8,128)(2,1)S(1)}, bf16[3,4,136,128]{3,2,1,0:T(8,128)(2,1)S(1)}, u32[]{:S(2)}, u32[]{:S(2)}) collective-permute-start(bf16[3,4,136,128]{3,2,1,0:T(8,128)(2,1)S(1)} %copy-done.9), channel_id=1, source_target_pairs={{0,2},{1,3},{2,0},{3,1},{4,6},{5,7},{6,4},{7,5},{8,10},{9,11},{10,... | collective-permute-start | bytes 1253384 | tf_op jit(solution)/shard_map/ppermute | solution.py:160
  51.1 2.0 %collective-permute-done.8 = f32[4,1,2,1,1,2,16,128]{7,6,5,4,3,2,0,1:T(8,128)S(1)} collective-permute-done((f32[4,1,2,1,1,2,16,128]{7,6,5,4,3,2,0,1:T(8,128)S(1)}, f32[4,1,2,1,1,2,16,128]{7,6,5,4,3,2,0,1:T(8,128)S(1)}, u32[]{:S(2)}, u32[]{:S(2)}) %collective-permute-start.8) | collective-permute-done | bytes 131104 | tf_op jit(solution)/shard_map/ppermute | solution.py:98
  53.3 5.8 %collective-permute-done.6 = bf16[3,4,136,128]{3,2,1,0:T(8,128)(2,1)S(1)} collective-permute-done((bf16[3,4,136,128]{3,2,1,0:T(8,128)(2,1)S(1)}, bf16[3,4,136,128]{3,2,1,0:T(8,128)(2,1)S(1)}, u32[]{:S(2)}, u32[]{:S(2)}) %collective-permute-start.6) | collective-permute-done | bytes 417824 | tf_op jit(solution)/shard_map/ppermute | solution.py:160
  60.1 1.6 %collective-permute-start.11 = (f32[4,1,1,1,1,2,16,128]{7,6,5,4,3,2,0,1:T(8,128)S(1)}, f32[4,1,1,1,1,2,16,128]{7,6,5,4,3,2,0,1:T(8,128)S(1)}, u32[]{:S(2)}, u32[]{:S(2)}) collective-permute-start(f32[4,1,1,1,1,2,16,128]{7,6,5,4,3,2,0,1:T(8,128)S(1)} %constant_dynamic-slice_fusion.5), channel_id=1, source_target_pairs={{0,8},{4,12},{8,0},{12,4},{16,24},{20,28},{24,16},{28,20},{1,9},{5... | collective-permute-start | bytes 196616 | tf_op jit(solution)/shard_map/ppermute | solution.py:98
  61.7 2.3 %collective-permute-done.13 = f32[4,1,1,2,1,1,16,128]{7,6,5,4,3,2,0,1:T(8,128)S(1)} collective-permute-done((f32[4,1,1,2,1,1,16,128]{7,6,5,4,3,2,0,1:T(8,128)S(1)}, f32[4,1,1,2,1,1,16,128]{7,6,5,4,3,2,0,1:T(8,128)S(1)}, u32[]{:S(2)}, u32[]{:S(2)}) %collective-permute-start.13) | collective-permute-done | bytes 65568 | tf_op jit(solution)/shard_map/ppermute | solution.py:98
  64.0 2.4 %collective-permute-done.12 = f32[4,1,2,1,1,1,16,128]{7,6,5,4,3,2,0,1:T(8,128)S(1)} collective-permute-done((f32[4,1,2,1,1,1,16,128]{7,6,5,4,3,2,0,1:T(8,128)S(1)}, f32[4,1,2,1,1,1,16,128]{7,6,5,4,3,2,0,1:T(8,128)S(1)}, u32[]{:S(2)}, u32[]{:S(2)}) %collective-permute-start.12) | collective-permute-done | bytes 65568 | tf_op jit(solution)/shard_map/ppermute | solution.py:98
  69.2 1.4 %collective-permute-start.15 = (f32[4,1,1,1,1,1,16,128]{7,6,5,4,3,2,0,1:T(8,128)S(1)}, f32[4,1,1,1,1,1,16,128]{7,6,5,4,3,2,0,1:T(8,128)S(1)}, u32[]{:S(2)}, u32[]{:S(2)}) collective-permute-start(f32[4,1,1,1,1,1,16,128]{7,6,5,4,3,2,0,1:T(8,128)S(1)} %constant_dynamic-slice_fusion.1), channel_id=1, source_target_pairs={{0,2},{1,3},{2,0},{3,1},{4,6},{5,7},{6,4},{7,5},{8,10},{9,11},{10,... | collective-permute-start | bytes 98312 | tf_op jit(solution)/shard_map/ppermute | solution.py:98
  70.6 1.6 %collective-permute-start.16 = (f32[4,1,1,1,1,1,16,128]{7,6,5,4,3,2,0,1:T(8,128)S(1)}, f32[4,1,1,1,1,1,16,128]{7,6,5,4,3,2,0,1:T(8,128)S(1)}, u32[]{:S(2)}, u32[]{:S(2)}) collective-permute-start(f32[4,1,1,1,1,1,16,128]{7,6,5,4,3,2,0,1:T(8,128)S(1)} %constant_dynamic-slice_fusion), channel_id=1, source_target_pairs={{0,4},{4,0},{8,12},{12,8},{16,20},{20,16},{24,28},{28,24},{1,5},{5... | collective-permute-start | bytes 98312 | tf_op jit(solution)/shard_map/ppermute | solution.py:98
  73.1 1.4 %collective-permute-done.16 = f32[4,1,1,1,1,1,16,128]{7,6,5,4,3,2,0,1:T(8,128)S(1)} collective-permute-done((f32[4,1,1,1,1,1,16,128]{7,6,5,4,3,2,0,1:T(8,128)S(1)}, f32[4,1,1,1,1,1,16,128]{7,6,5,4,3,2,0,1:T(8,128)S(1)}, u32[]{:S(2)}, u32[]{:S(2)}) %collective-permute-start.16) | collective-permute-done | bytes 32800 | tf_op jit(solution)/shard_map/ppermute | solution.py:98
  75.2 1.8 %fusion.13 = bf16[12,16,128]{2,1,0:T(8,128)(2,1)S(1)} fusion(bf16[12,4,136,128]{3,2,1,0:T(8,128)(2,1)} %copy-done.10, bf16[12,4,16,128]{3,2,1,0:T(8,128)(2,1)S(1)} %bitcast.103, pred[12,4]{1,0:T(8,128)(4,1)S(1)} %copy.64), kind=kOutput, calls=%fused_computation.17 | convolution fusion | flops 25288704 | bytes 1818672 | tf_op jit(solution)/shard_map/nerc,necd->nrd/dot_general | solution.py:171
  77.6 2.0 %collective-permute-start.17 = (bf16[4,1,1,1,1,1,16,128]{7,6,0,5,4,3,2,1:T(8,128)(2,1)S(1)}, bf16[4,1,1,1,1,1,16,128]{7,6,0,5,4,3,2,1:T(8,128)(2,1)S(1)}, u32[]{:S(2)}, u32[]{:S(2)}) collective-permute-start(bf16[4,1,1,1,1,1,16,128]{7,6,0,5,4,3,2,1:T(8,128)(2,1)S(1)} %get-tuple-element.58), channel_id=1, source_target_pairs={{0,16},{4,20},{8,24},{12,28},{16,0},{20,4},{24,8},{28,12},{1,17},{... | collective-permute-start | bytes 49160 | tf_op jit(solution)/shard_map/ppermute | solution.py:103
  80.0 1.7 %collective-permute-start.25 = (bf16[4,1,1,1,1,1,16,128]{7,6,0,5,4,3,2,1:T(8,128)(2,1)S(1)}, bf16[4,1,1,1,1,1,16,128]{7,6,0,5,4,3,2,1:T(8,128)(2,1)S(1)}, u32[]{:S(2)}, u32[]{:S(2)}) collective-permute-start(bf16[4,1,1,1,1,1,16,128]{7,6,0,5,4,3,2,1:T(8,128)(2,1)S(1)} %get-tuple-element.60), channel_id=1, source_target_pairs={{0,4},{4,0},{8,12},{12,8},{16,20},{20,16},{24,28},{28,24},{1,5},{5... | collective-permute-start | bytes 49160 | tf_op jit(solution)/shard_map/ppermute | solution.py:103
  82.4 1.7 %collective-permute-start.18 = (bf16[4,1,1,1,1,2,16,128]{7,6,0,5,4,3,2,1:T(8,128)(2,1)S(1)}, bf16[4,1,1,1,1,2,16,128]{7,6,0,5,4,3,2,1:T(8,128)(2,1)S(1)}, u32[]{:S(2)}, u32[]{:S(2)}) collective-permute-start(bf16[4,1,1,1,1,2,16,128]{7,6,0,5,4,3,2,1:T(8,128)(2,1)S(1)} %maximum_select_fusion.14), channel_id=1, source_target_pairs={{0,8},{4,12},{8,0},{12,4},{16,24},{20,28},{24,16},{28,20},{1,9},{5... | collective-permute-start | bytes 98312 | tf_op jit(solution)/shard_map/ppermute | solution.py:103
  84.8 1.3 %collective-permute-start.26 = (bf16[4,1,1,2,1,1,16,128]{7,6,0,5,4,3,2,1:T(8,128)(2,1)S(1)}, bf16[4,1,1,2,1,1,16,128]{7,6,0,5,4,3,2,1:T(8,128)(2,1)S(1)}, u32[]{:S(2)}, u32[]{:S(2)}) collective-permute-start(bf16[4,1,1,2,1,1,16,128]{7,6,0,5,4,3,2,1:T(8,128)(2,1)S(1)} %maximum_select_fusion.18), channel_id=1, source_target_pairs={{0,2},{1,3},{2,0},{3,1},{4,6},{5,7},{6,4},{7,5},{8,10},{9,11},{10,... | collective-permute-start | bytes 98312 | tf_op jit(solution)/shard_map/ppermute | solution.py:103
  86.4 1.8 %collective-permute-start.19 = (bf16[4,1,1,1,2,2,16,128]{7,6,0,5,4,3,2,1:T(8,128)(2,1)S(1)}, bf16[4,1,1,1,2,2,16,128]{7,6,0,5,4,3,2,1:T(8,128)(2,1)S(1)}, u32[]{:S(2)}, u32[]{:S(2)}) collective-permute-start(bf16[4,1,1,1,2,2,16,128]{7,6,0,5,4,3,2,1:T(8,128)(2,1)S(1)} %maximum_select_fusion.9), channel_id=1, source_target_pairs={{0,4},{4,0},{8,12},{12,8},{16,20},{20,16},{24,28},{28,24},{1,5},{5... | collective-permute-start | bytes 196616 | tf_op jit(solution)/shard_map/ppermute | solution.py:103
  88.1 2.1 %collective-permute-done.22 = bf16[4,1,2,1,1,1,16,128]{7,6,0,5,4,3,2,1:T(8,128)(2,1)S(1)} collective-permute-done((bf16[4,1,2,1,1,1,16,128]{7,6,0,5,4,3,2,1:T(8,128)(2,1)S(1)}, bf16[4,1,2,1,1,1,16,128]{7,6,0,5,4,3,2,1:T(8,128)(2,1)S(1)}, u32[]{:S(2)}, u32[]{:S(2)}) %collective-permute-start.22) | collective-permute-done | bytes 32800 | tf_op jit(solution)/shard_map/ppermute | solution.py:103
  90.3 1.5 %collective-permute-start.27 = (bf16[4,1,2,2,1,1,16,128]{7,6,0,5,4,3,2,1:T(8,128)(2,1)S(1)}, bf16[4,1,2,2,1,1,16,128]{7,6,0,5,4,3,2,1:T(8,128)(2,1)S(1)}, u32[]{:S(2)}, u32[]{:S(2)}) collective-permute-start(bf16[4,1,2,2,1,1,16,128]{7,6,0,5,4,3,2,1:T(8,128)(2,1)S(1)} %fusion.29), channel_id=1, source_target_pairs={{0,16},{4,20},{8,24},{12,28},{16,0},{20,4},{24,8},{28,12},{1,17},{... | collective-permute-start | bytes 196616 | tf_op jit(solution)/shard_map/ppermute | solution.py:103
  92.2 3.7 %collective-permute-done.23 = bf16[4,1,2,1,1,2,16,128]{7,6,0,5,4,3,2,1:T(8,128)(2,1)S(1)} collective-permute-done((bf16[4,1,2,1,1,2,16,128]{7,6,0,5,4,3,2,1:T(8,128)(2,1)S(1)}, bf16[4,1,2,1,1,2,16,128]{7,6,0,5,4,3,2,1:T(8,128)(2,1)S(1)}, u32[]{:S(2)}, u32[]{:S(2)}) %collective-permute-start.23) | collective-permute-done | bytes 65568 | tf_op jit(solution)/shard_map/ppermute | solution.py:103
  95.9 1.7 %collective-permute-start.24 = (bf16[4,1,2,1,2,2,16,128]{7,6,0,5,4,3,2,1:T(8,128)(2,1)S(1)}, bf16[4,1,2,1,2,2,16,128]{7,6,0,5,4,3,2,1:T(8,128)(2,1)S(1)}, u32[]{:S(2)}, u32[]{:S(2)}) collective-permute-start(bf16[4,1,2,1,2,2,16,128]{7,6,0,5,4,3,2,1:T(8,128)(2,1)S(1)} %maximum_select_fusion.6), channel_id=1, source_target_pairs={{0,4},{4,0},{8,12},{12,8},{16,20},{20,16},{24,28},{28,24},{1,5},{5... | collective-permute-start | bytes 393224 | tf_op jit(solution)/shard_map/ppermute | solution.py:103
  97.8 3.2 %collective-permute-done.24 = bf16[4,1,2,1,2,2,16,128]{7,6,0,5,4,3,2,1:T(8,128)(2,1)S(1)} collective-permute-done((bf16[4,1,2,1,2,2,16,128]{7,6,0,5,4,3,2,1:T(8,128)(2,1)S(1)}, bf16[4,1,2,1,2,2,16,128]{7,6,0,5,4,3,2,1:T(8,128)(2,1)S(1)}, u32[]{:S(2)}, u32[]{:S(2)}) %collective-permute-start.24) | collective-permute-done | bytes 131104 | tf_op jit(solution)/shard_map/ppermute | solution.py:103
  101.0 1.7 %collective-permute-done.28 = bf16[4,1,2,2,1,2,16,128]{7,6,0,5,4,3,2,1:T(8,128)(2,1)S(1)} collective-permute-done((bf16[4,1,2,2,1,2,16,128]{7,6,0,5,4,3,2,1:T(8,128)(2,1)S(1)}, bf16[4,1,2,2,1,2,16,128]{7,6,0,5,4,3,2,1:T(8,128)(2,1)S(1)}, u32[]{:S(2)}, u32[]{:S(2)}) %collective-permute-start.28) | collective-permute-done | bytes 131104 | tf_op jit(solution)/shard_map/ppermute | solution.py:103
  103.9 1.4 %collective-permute-done.29 = bf16[12,256,128]{2,1,0:T(8,128)(2,1)} collective-permute-done((bf16[12,256,128]{2,1,0:T(8,128)(2,1)S(1)}, bf16[12,256,128]{2,1,0:T(8,128)(2,1)}, u32[]{:S(2)}, u32[]{:S(2)}) %collective-permute-start.29) | collective-permute-done | bytes 786464 | tf_op jit(solution)/shard_map/ppermute | solution.py:180
  105.3 1.8 %gather_fusion.5 = bf16[8,256,128]{2,1,0:T(8,128)(2,1)S(1)} fusion(bf16[12,256,128]{2,1,0:T(8,128)(2,1)} %collective-permute-done.29, s32[1024]{0:T(1024)S(1)} %pad_clamp_fusion), kind=kCustom, calls=%fused_computation.1.clone | custom fusion | bytes 1048608 | tf_op jit(solution)/shard_map/jit(_take)/gather | solution.py:182
  (155 shorter events, 27.8 us)
Async XLA Ops:
  0.0 37.0 %copy-start = (bf16[4,4,256,256]{3,2,1,0:T(8,128)(2,1)S(1)}, bf16[4,4,256,256]{3,2,1,0:T(8,128)(2,1)}, u32[]{:S(2)}) copy-start(bf16[4,4,256,256]{3,2,1,0:T(8,128)(2,1)} %param.12) | copy-start | bytes 6291460
  1.6 11.3 %copy-start.11 = (bf16[3,4,128,128]{3,2,1,0:T(8,128)(2,1)S(1)}, bf16[3,4,128,128]{3,2,1,0:T(8,128)(2,1)}, u32[]{:S(2)}) copy-start(bf16[3,4,128,128]{3,2,1,0:T(8,128)(2,1)} %param.16) | copy-start | bytes 1179652
  6.8 14.8 %collective-permute-start.2 = (f32[12,256,128]{2,1,0:T(8,128)}, f32[12,256,128]{2,1,0:T(8,128)}, u32[]{:S(2)}, u32[]{:S(2)}) collective-permute-start(f32[12,256,128]{2,1,0:T(8,128)} %shard_map.83), channel_id=1, source_target_pairs={{0,1},{1,0},{2,3},{3,2},{4,5},{5,4},{6,7},{7,6},{8,9},{9,8},{10,11... | collective-permute-start | bytes 4718600 | tf_op jit(solution)/shard_map/ppermute | solution.py:137
  8.0 10.9 %collective-permute-start = (bf16[1,512,256]{2,1,0:T(8,128)(2,1)}, bf16[1,512,256]{2,1,0:T(8,128)(2,1)}, u32[]{:S(2)}, u32[]{:S(2)}) collective-permute-start(bf16[1,512,256]{2,1,0:T(8,128)(2,1)} %get-tuple-element.55), channel_id=1, source_target_pairs={{0,1},{1,2},{2,3},{3,4},{4,5},{5,6},{6,7},{7,8},{8,9},{9,10},{10,1... | collective-permute-start | bytes 786440 | tf_op jit(solution)/shard_map/ppermute | solution.py:65
  10.7 8.3 %collective-permute-start.1 = (bf16[1,512,256]{2,1,0:T(8,128)(2,1)}, bf16[1,512,256]{2,1,0:T(8,128)(2,1)}, u32[]{:S(2)}, u32[]{:S(2)}) collective-permute-start(bf16[1,512,256]{2,1,0:T(8,128)(2,1)} %get-tuple-element.56), channel_id=1, source_target_pairs={{1,0},{2,1},{3,2},{4,3},{5,4},{6,5},{7,6},{8,7},{9,8},{10,9},{11,1... | collective-permute-start | bytes 786440 | tf_op jit(solution)/shard_map/ppermute | solution.py:67
  24.8 17.1 %collective-permute-start.5 = (f32[4,1,2,2,1,2,16,128]{7,6,5,4,3,2,0,1:T(8,128)}, f32[4,1,2,2,1,2,16,128]{7,6,5,4,3,2,0,1:T(8,128)}, u32[]{:S(2)}, u32[]{:S(2)}) collective-permute-start(f32[4,1,2,2,1,2,16,128]{7,6,5,4,3,2,0,1:T(8,128)} %constant_dynamic-slice_fusion.9), channel_id=1, source_target_pairs={{0,8},{4,12},{8,0},{12,4},{16,24},{20,28},{24,16},{28,20},{1,9},{5... | collective-permute-start | bytes 786440 | tf_op jit(solution)/shard_map/ppermute | solution.py:98
  31.5 11.5 %collective-permute-start.4 = (f32[4,1,2,1,2,2,16,128]{7,6,5,4,3,2,0,1:T(8,128)}, f32[4,1,2,1,2,2,16,128]{7,6,5,4,3,2,0,1:T(8,128)}, u32[]{:S(2)}, u32[]{:S(2)}) collective-permute-start(f32[4,1,2,1,2,2,16,128]{7,6,5,4,3,2,0,1:T(8,128)} %constant_dynamic-slice_fusion.10), channel_id=1, source_target_pairs={{0,4},{4,0},{8,12},{12,8},{16,20},{20,16},{24,28},{28,24},{1,5},{5... | collective-permute-start | bytes 786440 | tf_op jit(solution)/shard_map/ppermute | solution.py:98
  32.1 11.9 %collective-permute-start.3 = (f32[4,1,1,2,2,2,16,128]{7,6,5,4,3,2,0,1:T(8,128)S(1)}, f32[4,1,1,2,2,2,16,128]{7,6,5,4,3,2,0,1:T(8,128)}, u32[]{:S(2)}, u32[]{:S(2)}) collective-permute-start(f32[4,1,1,2,2,2,16,128]{7,6,5,4,3,2,0,1:T(8,128)S(1)} %constant_dynamic-slice_fusion.11), channel_id=1, source_target_pairs={{0,2},{1,3},{2,0},{3,1},{4,6},{5,7},{6,4},{7,5},{8,10},{9,11},{10,... | collective-permute-start | bytes 786440 | tf_op jit(solution)/shard_map/ppermute | solution.py:98
  45.0 8.1 %collective-permute-start.8 = (f32[4,1,2,1,1,2,16,128]{7,6,5,4,3,2,0,1:T(8,128)S(1)}, f32[4,1,2,1,1,2,16,128]{7,6,5,4,3,2,0,1:T(8,128)S(1)}, u32[]{:S(2)}, u32[]{:S(2)}) collective-permute-start(f32[4,1,2,1,1,2,16,128]{7,6,5,4,3,2,0,1:T(8,128)S(1)} %constant_dynamic-slice_fusion.7), channel_id=1, source_target_pairs={{0,8},{4,12},{8,0},{12,4},{16,24},{20,28},{24,16},{28,20},{1,9},{5... | collective-permute-start | bytes 393224 | tf_op jit(solution)/shard_map/ppermute | solution.py:98
  45.6 7.7 %collective-permute-start.9 = (f32[4,1,2,2,1,1,16,128]{7,6,5,4,3,2,0,1:T(8,128)S(1)}, f32[4,1,2,2,1,1,16,128]{7,6,5,4,3,2,0,1:T(8,128)S(1)}, u32[]{:S(2)}, u32[]{:S(2)}) collective-permute-start(f32[4,1,2,2,1,1,16,128]{7,6,5,4,3,2,0,1:T(8,128)S(1)} %constant_dynamic-slice_fusion.6), channel_id=1, source_target_pairs={{0,16},{4,20},{8,24},{12,28},{16,0},{20,4},{24,8},{28,12},{1,17},{... | collective-permute-start | bytes 393224 | tf_op jit(solution)/shard_map/ppermute | solution.py:98
  48.2 5.0 %collective-permute-start.7 = (f32[4,1,1,1,2,2,16,128]{7,6,5,4,3,2,0,1:T(8,128)S(1)}, f32[4,1,1,1,2,2,16,128]{7,6,5,4,3,2,0,1:T(8,128)S(1)}, u32[]{:S(2)}, u32[]{:S(2)}) collective-permute-start(f32[4,1,1,1,2,2,16,128]{7,6,5,4,3,2,0,1:T(8,128)S(1)} %constant_dynamic-slice_fusion.8), channel_id=1, source_target_pairs={{0,4},{4,0},{8,12},{12,8},{16,20},{20,16},{24,28},{28,24},{1,5},{5... | collective-permute-start | bytes 393224 | tf_op jit(solution)/shard_map/ppermute | solution.py:98
  49.1 10.0 %collective-permute-start.6 = (bf16[3,4,136,128]{3,2,1,0:T(8,128)(2,1)S(1)}, bf16[3,4,136,128]{3,2,1,0:T(8,128)(2,1)S(1)}, u32[]{:S(2)}, u32[]{:S(2)}) collective-permute-start(bf16[3,4,136,128]{3,2,1,0:T(8,128)(2,1)S(1)} %copy-done.9), channel_id=1, source_target_pairs={{0,2},{1,3},{2,0},{3,1},{4,6},{5,7},{6,4},{7,5},{8,10},{9,11},{10,... | collective-permute-start | bytes 1253384 | tf_op jit(solution)/shard_map/ppermute | solution.py:160
  59.2 7.2 %collective-permute-start.10 = (bf16[6,4,136,128]{3,2,1,0:T(8,128)(2,1)S(1)}, bf16[6,4,136,128]{3,2,1,0:T(8,128)(2,1)S(1)}, u32[]{:S(2)}, u32[]{:S(2)}) collective-permute-start(bf16[6,4,136,128]{3,2,1,0:T(8,128)(2,1)S(1)} %pad_maximum_fusion.1), channel_id=1, source_target_pairs={{0,1},{1,0},{2,3},{3,2},{4,5},{5,4},{6,7},{7,6},{8,9},{9,8},{10,11... | collective-permute-start | bytes 2506760 | tf_op jit(solution)/shard_map/ppermute | solution.py:160
  59.4 4.6 %collective-permute-start.13 = (f32[4,1,1,2,1,1,16,128]{7,6,5,4,3,2,0,1:T(8,128)S(1)}, f32[4,1,1,2,1,1,16,128]{7,6,5,4,3,2,0,1:T(8,128)S(1)}, u32[]{:S(2)}, u32[]{:S(2)}) collective-permute-start(f32[4,1,1,2,1,1,16,128]{7,6,5,4,3,2,0,1:T(8,128)S(1)} %constant_dynamic-slice_fusion.3), channel_id=1, source_target_pairs={{0,2},{1,3},{2,0},{3,1},{4,6},{5,7},{6,4},{7,5},{8,10},{9,11},{10,... | collective-permute-start | bytes 196616 | tf_op jit(solution)/shard_map/ppermute | solution.py:98
  59.8 6.6 %collective-permute-start.12 = (f32[4,1,2,1,1,1,16,128]{7,6,5,4,3,2,0,1:T(8,128)S(1)}, f32[4,1,2,1,1,1,16,128]{7,6,5,4,3,2,0,1:T(8,128)S(1)}, u32[]{:S(2)}, u32[]{:S(2)}) collective-permute-start(f32[4,1,2,1,1,1,16,128]{7,6,5,4,3,2,0,1:T(8,128)S(1)} %constant_dynamic-slice_fusion.4), channel_id=1, source_target_pairs={{0,16},{4,20},{8,24},{12,28},{16,0},{20,4},{24,8},{28,12},{1,17},{... | collective-permute-start | bytes 196616 | tf_op jit(solution)/shard_map/ppermute | solution.py:98
  60.1 6.3 %collective-permute-start.11 = (f32[4,1,1,1,1,2,16,128]{7,6,5,4,3,2,0,1:T(8,128)S(1)}, f32[4,1,1,1,1,2,16,128]{7,6,5,4,3,2,0,1:T(8,128)S(1)}, u32[]{:S(2)}, u32[]{:S(2)}) collective-permute-start(f32[4,1,1,1,1,2,16,128]{7,6,5,4,3,2,0,1:T(8,128)S(1)} %constant_dynamic-slice_fusion.5), channel_id=1, source_target_pairs={{0,8},{4,12},{8,0},{12,4},{16,24},{20,28},{24,16},{28,20},{1,9},{5... | collective-permute-start | bytes 196616 | tf_op jit(solution)/shard_map/ppermute | solution.py:98
  67.9 5.2 %collective-permute-start.14 = (f32[4,1,1,1,1,1,16,128]{7,6,5,4,3,2,0,1:T(8,128)S(1)}, f32[4,1,1,1,1,1,16,128]{7,6,5,4,3,2,0,1:T(8,128)S(1)}, u32[]{:S(2)}, u32[]{:S(2)}) collective-permute-start(f32[4,1,1,1,1,1,16,128]{7,6,5,4,3,2,0,1:T(8,128)S(1)} %constant_dynamic-slice_fusion.2), channel_id=1, source_target_pairs={{0,16},{4,20},{8,24},{12,28},{16,0},{20,4},{24,8},{28,12},{1,17},{... | collective-permute-start | bytes 98312 | tf_op jit(solution)/shard_map/ppermute | solution.py:98
  69.2 3.9 %collective-permute-start.15 = (f32[4,1,1,1,1,1,16,128]{7,6,5,4,3,2,0,1:T(8,128)S(1)}, f32[4,1,1,1,1,1,16,128]{7,6,5,4,3,2,0,1:T(8,128)S(1)}, u32[]{:S(2)}, u32[]{:S(2)}) collective-permute-start(f32[4,1,1,1,1,1,16,128]{7,6,5,4,3,2,0,1:T(8,128)S(1)} %constant_dynamic-slice_fusion.1), channel_id=1, source_target_pairs={{0,2},{1,3},{2,0},{3,1},{4,6},{5,7},{6,4},{7,5},{8,10},{9,11},{10,... | collective-permute-start | bytes 98312 | tf_op jit(solution)/shard_map/ppermute | solution.py:98
  70.6 3.9 %collective-permute-start.16 = (f32[4,1,1,1,1,1,16,128]{7,6,5,4,3,2,0,1:T(8,128)S(1)}, f32[4,1,1,1,1,1,16,128]{7,6,5,4,3,2,0,1:T(8,128)S(1)}, u32[]{:S(2)}, u32[]{:S(2)}) collective-permute-start(f32[4,1,1,1,1,1,16,128]{7,6,5,4,3,2,0,1:T(8,128)S(1)} %constant_dynamic-slice_fusion), channel_id=1, source_target_pairs={{0,4},{4,0},{8,12},{12,8},{16,20},{20,16},{24,28},{28,24},{1,5},{5... | collective-permute-start | bytes 98312 | tf_op jit(solution)/shard_map/ppermute | solution.py:98
  77.6 4.7 %collective-permute-start.17 = (bf16[4,1,1,1,1,1,16,128]{7,6,0,5,4,3,2,1:T(8,128)(2,1)S(1)}, bf16[4,1,1,1,1,1,16,128]{7,6,0,5,4,3,2,1:T(8,128)(2,1)S(1)}, u32[]{:S(2)}, u32[]{:S(2)}) collective-permute-start(bf16[4,1,1,1,1,1,16,128]{7,6,0,5,4,3,2,1:T(8,128)(2,1)S(1)} %get-tuple-element.58), channel_id=1, source_target_pairs={{0,16},{4,20},{8,24},{12,28},{16,0},{20,4},{24,8},{28,12},{1,17},{... | collective-permute-start | bytes 49160 | tf_op jit(solution)/shard_map/ppermute | solution.py:103
  79.7 4.4 %collective-permute-start.21 = (bf16[4,1,1,1,1,1,16,128]{7,6,0,5,4,3,2,1:T(8,128)(2,1)S(1)}, bf16[4,1,1,1,1,1,16,128]{7,6,0,5,4,3,2,1:T(8,128)(2,1)S(1)}, u32[]{:S(2)}, u32[]{:S(2)}) collective-permute-start(bf16[4,1,1,1,1,1,16,128]{7,6,0,5,4,3,2,1:T(8,128)(2,1)S(1)} %get-tuple-element.59), channel_id=1, source_target_pairs={{0,2},{1,3},{2,0},{3,1},{4,6},{5,7},{6,4},{7,5},{8,10},{9,11},{10,... | collective-permute-start | bytes 49160 | tf_op jit(solution)/shard_map/ppermute | solution.py:103
  80.0 4.7 %collective-permute-start.25 = (bf16[4,1,1,1,1,1,16,128]{7,6,0,5,4,3,2,1:T(8,128)(2,1)S(1)}, bf16[4,1,1,1,1,1,16,128]{7,6,0,5,4,3,2,1:T(8,128)(2,1)S(1)}, u32[]{:S(2)}, u32[]{:S(2)}) collective-permute-start(bf16[4,1,1,1,1,1,16,128]{7,6,0,5,4,3,2,1:T(8,128)(2,1)S(1)} %get-tuple-element.60), channel_id=1, source_target_pairs={{0,4},{4,0},{8,12},{12,8},{16,20},{20,16},{24,28},{28,24},{1,5},{5... | collective-permute-start | bytes 49160 | tf_op jit(solution)/shard_map/ppermute | solution.py:103
  82.4 4.0 %collective-permute-start.18 = (bf16[4,1,1,1,1,2,16,128]{7,6,0,5,4,3,2,1:T(8,128)(2,1)S(1)}, bf16[4,1,1,1,1,2,16,128]{7,6,0,5,4,3,2,1:T(8,128)(2,1)S(1)}, u32[]{:S(2)}, u32[]{:S(2)}) collective-permute-start(bf16[4,1,1,1,1,2,16,128]{7,6,0,5,4,3,2,1:T(8,128)(2,1)S(1)} %maximum_select_fusion.14), channel_id=1, source_target_pairs={{0,8},{4,12},{8,0},{12,4},{16,24},{20,28},{24,16},{28,20},{1,9},{5... | collective-permute-start | bytes 98312 | tf_op jit(solution)/shard_map/ppermute | solution.py:103
  84.0 6.2 %collective-permute-start.22 = (bf16[4,1,2,1,1,1,16,128]{7,6,0,5,4,3,2,1:T(8,128)(2,1)S(1)}, bf16[4,1,2,1,1,1,16,128]{7,6,0,5,4,3,2,1:T(8,128)(2,1)S(1)}, u32[]{:S(2)}, u32[]{:S(2)}) collective-permute-start(bf16[4,1,2,1,1,1,16,128]{7,6,0,5,4,3,2,1:T(8,128)(2,1)S(1)} %maximum_select_fusion.16), channel_id=1, source_target_pairs={{0,16},{4,20},{8,24},{12,28},{16,0},{20,4},{24,8},{28,12},{1,17},{... | collective-permute-start | bytes 98312 | tf_op jit(solution)/shard_map/ppermute | solution.py:103
  84.8 5.5 %collective-permute-start.26 = (bf16[4,1,1,2,1,1,16,128]{7,6,0,5,4,3,2,1:T(8,128)(2,1)S(1)}, bf16[4,1,1,2,1,1,16,128]{7,6,0,5,4,3,2,1:T(8,128)(2,1)S(1)}, u32[]{:S(2)}, u32[]{:S(2)}) collective-permute-start(bf16[4,1,1,2,1,1,16,128]{7,6,0,5,4,3,2,1:T(8,128)(2,1)S(1)} %maximum_select_fusion.18), channel_id=1, source_target_pairs={{0,2},{1,3},{2,0},{3,1},{4,6},{5,7},{6,4},{7,5},{8,10},{9,11},{10,... | collective-permute-start | bytes 98312 | tf_op jit(solution)/shard_map/ppermute | solution.py:103
  86.4 5.5 %collective-permute-start.19 = (bf16[4,1,1,1,2,2,16,128]{7,6,0,5,4,3,2,1:T(8,128)(2,1)S(1)}, bf16[4,1,1,1,2,2,16,128]{7,6,0,5,4,3,2,1:T(8,128)(2,1)S(1)}, u32[]{:S(2)}, u32[]{:S(2)}) collective-permute-start(bf16[4,1,1,1,2,2,16,128]{7,6,0,5,4,3,2,1:T(8,128)(2,1)S(1)} %maximum_select_fusion.9), channel_id=1, source_target_pairs={{0,4},{4,0},{8,12},{12,8},{16,20},{20,16},{24,28},{28,24},{1,5},{5... | collective-permute-start | bytes 196616 | tf_op jit(solution)/shard_map/ppermute | solution.py:103
  90.2 5.7 %collective-permute-start.23 = (bf16[4,1,2,1,1,2,16,128]{7,6,0,5,4,3,2,1:T(8,128)(2,1)S(1)}, bf16[4,1,2,1,1,2,16,128]{7,6,0,5,4,3,2,1:T(8,128)(2,1)S(1)}, u32[]{:S(2)}, u32[]{:S(2)}) collective-permute-start(bf16[4,1,2,1,1,2,16,128]{7,6,0,5,4,3,2,1:T(8,128)(2,1)S(1)} %maximum_select_fusion.11), channel_id=1, source_target_pairs={{0,8},{4,12},{8,0},{12,4},{16,24},{20,28},{24,16},{28,20},{1,9},{5... | collective-permute-start | bytes 196616 | tf_op jit(solution)/shard_map/ppermute | solution.py:103
  90.3 7.3 %collective-permute-start.27 = (bf16[4,1,2,2,1,1,16,128]{7,6,0,5,4,3,2,1:T(8,128)(2,1)S(1)}, bf16[4,1,2,2,1,1,16,128]{7,6,0,5,4,3,2,1:T(8,128)(2,1)S(1)}, u32[]{:S(2)}, u32[]{:S(2)}) collective-permute-start(bf16[4,1,2,2,1,1,16,128]{7,6,0,5,4,3,2,1:T(8,128)(2,1)S(1)} %fusion.29), channel_id=1, source_target_pairs={{0,16},{4,20},{8,24},{12,28},{16,0},{20,4},{24,8},{28,12},{1,17},{... | collective-permute-start | bytes 196616 | tf_op jit(solution)/shard_map/ppermute | solution.py:103
  91.9 5.8 %collective-permute-start.20 = (bf16[4,1,1,2,2,2,16,128]{7,6,0,5,4,3,2,1:T(8,128)(2,1)S(1)}, bf16[4,1,1,2,2,2,16,128]{7,6,0,5,4,3,2,1:T(8,128)(2,1)S(1)}, u32[]{:S(2)}, u32[]{:S(2)}) collective-permute-start(bf16[4,1,1,2,2,2,16,128]{7,6,0,5,4,3,2,1:T(8,128)(2,1)S(1)} %maximum_select_fusion.5), channel_id=1, source_target_pairs={{0,2},{1,3},{2,0},{3,1},{4,6},{5,7},{6,4},{7,5},{8,10},{9,11},{10,... | collective-permute-start | bytes 393224 | tf_op jit(solution)/shard_map/ppermute | solution.py:103
  95.9 5.0 %collective-permute-start.24 = (bf16[4,1,2,1,2,2,16,128]{7,6,0,5,4,3,2,1:T(8,128)(2,1)S(1)}, bf16[4,1,2,1,2,2,16,128]{7,6,0,5,4,3,2,1:T(8,128)(2,1)S(1)}, u32[]{:S(2)}, u32[]{:S(2)}) collective-permute-start(bf16[4,1,2,1,2,2,16,128]{7,6,0,5,4,3,2,1:T(8,128)(2,1)S(1)} %maximum_select_fusion.6), channel_id=1, source_target_pairs={{0,4},{4,0},{8,12},{12,8},{16,20},{20,16},{24,28},{28,24},{1,5},{5... | collective-permute-start | bytes 393224 | tf_op jit(solution)/shard_map/ppermute | solution.py:103
  97.6 5.0 %collective-permute-start.28 = (bf16[4,1,2,2,1,2,16,128]{7,6,0,5,4,3,2,1:T(8,128)(2,1)S(1)}, bf16[4,1,2,2,1,2,16,128]{7,6,0,5,4,3,2,1:T(8,128)(2,1)S(1)}, u32[]{:S(2)}, u32[]{:S(2)}) collective-permute-start(bf16[4,1,2,2,1,2,16,128]{7,6,0,5,4,3,2,1:T(8,128)(2,1)S(1)} %maximum_select_fusion.7), channel_id=1, source_target_pairs={{0,8},{4,12},{8,0},{12,4},{16,24},{20,28},{24,16},{28,20},{1,9},{5... | collective-permute-start | bytes 393224 | tf_op jit(solution)/shard_map/ppermute | solution.py:103
  102.8 2.5 %collective-permute-start.29 = (bf16[12,256,128]{2,1,0:T(8,128)(2,1)S(1)}, bf16[12,256,128]{2,1,0:T(8,128)(2,1)}, u32[]{:S(2)}, u32[]{:S(2)}) collective-permute-start(bf16[12,256,128]{2,1,0:T(8,128)(2,1)S(1)} %pad_maximum_fusion.2), channel_id=1, source_target_pairs={{0,1},{1,0},{2,3},{3,2},{4,5},{5,4},{6,7},{7,6},{8,9},{9,8},{10,11... | collective-permute-start | bytes 2359304 | tf_op jit(solution)/shard_map/ppermute | solution.py:180
  (13 other events, 69.2 us)

commit v16 on v15

--- a/solution.py
+++ b/solution.py
@@ -137,19 +137,21 @@
     got = lax.ppermute(send, bits[0][0], pairs(*bits[0]))
     whole = restrict(residual, basis, links, total_blocks, half, 0) + got
     whole = whole.reshape((total_blocks, 1) + (2,) * (nb - 1) + (inner, width))
-    extended, inverse_blocks, whole = lax.optimization_barrier((extended, inverse_blocks, whole))
+    exchanges = list(reversed([bit for bit in bits if bit[0] == "coarse"]))
+    assert nb >= len(exchanges) + 1
+    arriving = lax.ppermute(packed, exchanges[0][0], pairs(*exchanges[0]))
+    xors = [0, exchanges[0][1]]
+    extended, inverse_blocks, whole, arriving = lax.optimization_barrier((extended, inverse_blocks, whole, arriving))
+    packed = jnp.concatenate([packed, arriving], axis=0)
+    arriving = None
     parts = [lax.slice_in_dim(whole, s * per, (s + 1) * per, axis=0) for s in range(streams)]
     picked = jnp.take(extended, margin, axis=0)
     local = jnp.einsum("jerb,jebc->jrc", picked, inverse_blocks, preferred_element_type=jnp.float32)
-    exchanges = list(reversed([bit for bit in bits if bit[0] == "coarse"]))
-    assert nb >= len(exchanges) + 2
-    xors = [0]
-    arriving = None
     for step in range(1, nb):
         parts = [halve(x, 1 + orders[s][step], *bits[orders[s][step]], jnp.float32) for s, x in enumerate(parts)]
         if step == 1:
             local, parts = lax.optimization_barrier((local, parts))
-        k = step - 1
+        k = step
         if arriving is not None:
             arriving, parts = lax.optimization_barrier((arriving, parts))
             packed = jnp.concatenate([packed, arriving], axis=0)

time: 112 us -> 109 us (0.973)
  waiting for transfers between devices: 27.4 us -> 21.3 us
  other arithmetic: 10.1 us -> 12.6 us
  local copies, waits for them, and re-layouts: 17.7 us -> 19.5 us
    ppermute x2 -> x1, waiting for transfers between devices: 5.83 us -> 0.01 us  [per_device(): arriving = lax.ppermute(packed, axis, pairs(axis, mask))]
    ppermute x0 -> x1, starting transfers between devices: none -> 4.14 us  [per_device(): arriving = lax.ppermute(packed, exchanges[0][0], pairs(*exchanges[0]))]
    ppermute x12, starting transfers between devices: 17.9 us -> 14.6 us  [halve(): lax.ppermute(send.astype(wire), axis, pairs(axis, mask)).astype(x.dtype)]
    ppermute x12, waiting for transfers between devices: 11.4 us -> 8.47 us  [double(): recv = lax.ppermute(y, axis, pairs(axis, mask))]
    ppermute x12, waiting for transfers between devices: 8.73 us -> 11.4 us  [halve(): lax.ppermute(send.astype(wire), axis, pairs(axis, mask)).astype(x.dtype)]
    ppermute x2 -> x1, starting transfers between devices: 2.08 us -> 0.01 us  [per_device(): arriving = lax.ppermute(packed, axis, pairs(axis, mask))]
    unnamed x33 -> x37, local copies, waits for them, and re-layouts: 5.12 us -> 5.71 us
  transfers between devices with their start and end apart: 30 -> 30, of which waited for: 14 -> 13; matrix products, arithmetic and copies ran while one was open for 17% -> 22% of each run, Pallas kernels for 5% -> 5%
where the time goes in v16:
time: 109 us
  starting transfers between devices  37.1 us (34%)
  waiting for transfers between devices  21.3 us (20%)
  local copies, waits for them, and re-layouts  19.5 us (18%)
  other arithmetic  12.6 us (12%)
  Pallas kernels  10.2 us (9%)
  matrix products  7.15 us (7%)
    ppermute x12, starting transfers between devices, halve(): lax.ppermute(send.astype(wire), axis, pairs(axis, mask)).astype(x.dtype)  14.6 us
    ppermute x12, starting transfers between devices, double(): recv = lax.ppermute(y, axis, pairs(axis, mask))  13.9 us
    ppermute x12, waiting for transfers between devices, halve(): lax.ppermute(send.astype(wire), axis, pairs(axis, mask)).astype(x.dtype)  11.4 us
    pallas_call x2, Pallas kernels, restrict(): pl.pallas_call(functools.partial(restrict_kernel, upper=upper), out_shape...  10.2 us
    ppermute x12, waiting for transfers between devices, double(): recv = lax.ppermute(y, axis, pairs(axis, mask))  8.47 us
    unnamed x37, local copies, waits for them, and re-layouts  5.71 us
    dot_general x1, matrix products, per_device(): jnp.einsum('jerb,jebc->jrc', picked, inverse_blocks, preferred_element_ty...  4.9 us
    gather x1, local copies, waits for them, and re-layouts, per_device(): picked = jnp.take(extended, margin, axis=0)  4.2 us
  transfers between devices with their start and end apart: 30, of which 13 were waited for; matrix products, arithmetic and copies ran while one was open for 22% of the time, Pallas kernels for 5%

profile of v16, /device:TPU:0, one launch (start us, length us, event | category | flops | bytes accessed | tf_op | source)
XLA Modules:
  0.0 108.5 jit_solution(16486128872565081266)
XLA Ops:
  1.6 5.1 %shard_map.83 = f32[12,256,128]{2,1,0:T(8,128)} custom-call(s32[8]{0:T(128)} %reshape.1777.links, s32[1]{0:T(128)} %bitcast.half, bf16[4,512,256]{2,1,0:T(8,128)(2,1)} %residual_ref.3, bf16[4,2,256,128]{3,2,1,0:T(8,128)(2,1)} %basis_ref.3), custom_call_target="tpu_custom_call" | custom-call | flops 134217728 | bytes 3145728 | tf_op jit(solution)/shard_map/pallas_call | solution.py:36
  8.0 2.7 %collective-permute-start = (bf16[1,512,256]{2,1,0:T(8,128)(2,1)}, bf16[1,512,256]{2,1,0:T(8,128)(2,1)}, u32[]{:S(2)}, u32[]{:S(2)}) collective-permute-start(bf16[1,512,256]{2,1,0:T(8,128)(2,1)} %get-tuple-element.41), channel_id=1, source_target_pairs={{0,1},{1,2},{2,3},{3,4},{4,5},{5,6},{6,7},{7,8},{8,9},{9,10},{10,1... | collective-permute-start | bytes 786440 | tf_op jit(solution)/shard_map/ppermute | solution.py:65
  10.6 1.3 %collective-permute-start.1 = (bf16[1,512,256]{2,1,0:T(8,128)(2,1)}, bf16[1,512,256]{2,1,0:T(8,128)(2,1)}, u32[]{:S(2)}, u32[]{:S(2)}) collective-permute-start(bf16[1,512,256]{2,1,0:T(8,128)(2,1)} %get-tuple-element.42), channel_id=1, source_target_pairs={{1,0},{2,1},{3,2},{4,3},{5,4},{6,5},{7,6},{8,7},{9,8},{10,9},{11,1... | collective-permute-start | bytes 786440 | tf_op jit(solution)/shard_map/ppermute | solution.py:67
  13.4 4.1 %collective-permute-start.3 = (bf16[3,4,136,128]{3,2,1,0:T(8,128)(2,1)}, bf16[3,4,136,128]{3,2,1,0:T(8,128)(2,1)}, u32[]{:S(2)}, u32[]{:S(2)}) collective-permute-start(bf16[3,4,136,128]{3,2,1,0:T(8,128)(2,1)} %pad_maximum_fusion.3), channel_id=1, source_target_pairs={{0,2},{1,3},{2,0},{3,1},{4,6},{5,7},{6,4},{7,5},{8,10},{9,11},{10,... | collective-permute-start | bytes 1253384 | tf_op jit(solution)/shard_map/ppermute | solution.py:142
  20.2 5.0 %shard_map.82 = f32[12,256,128]{2,1,0:T(8,128)} custom-call(s32[8]{0:T(128)} %reshape.1777.links, s32[1]{0:T(128)} %bitcast.half, bf16[4,512,256]{2,1,0:T(8,128)(2,1)} %residual_ref.3, bf16[4,2,256,128]{3,2,1,0:T(8,128)(2,1)} %basis_ref.3), custom_call_target="tpu_custom_call" | custom-call | flops 134217728 | bytes 3145728 | tf_op jit(solution)/shard_map/pallas_call | solution.py:36
  25.8 2.4 %pad_maximum_fusion = bf16[6,512,256]{2,1,0:T(8,128)(2,1)} fusion(bf16[1,512,256]{2,1,0:T(8,128)(2,1)} %collective-permute-done.1, bf16[4,512,256]{2,1,0:T(8,128)(2,1)S(1)} %copy-done.3, bf16[1,512,256]{2,1,0:T(8,128)(2,1)} %collective-permute-done), kind=kLoop, calls=%fused_computation.15 | loop fusion | flops 1572864 | bytes 3145728 | tf_op jit(solution)/shard_map/concatenate | solution.py:63
  28.2 1.6 %add.233 = f32[12,256,128]{2,1,0:T(8,128)S(1)} add(f32[12,256,128]{2,1,0:T(8,128)S(1)} %copy-done.4, f32[12,256,128]{2,1,0:T(8,128)} %collective-permute-done.2) | non-fusion elementwise | flops 393216 | bytes 4718592 | tf_op jit(solution)/shard_map/add | solution.py:138
  31.5 2.3 %collective-permute-start.6 = (f32[4,1,2,2,1,2,16,128]{7,6,5,4,3,2,0,1:T(8,128)}, f32[4,1,2,2,1,2,16,128]{7,6,5,4,3,2,0,1:T(8,128)}, u32[]{:S(2)}, u32[]{:S(2)}) collective-permute-start(f32[4,1,2,2,1,2,16,128]{7,6,5,4,3,2,0,1:T(8,128)} %constant_dynamic-slice_fusion.9), channel_id=1, source_target_pairs={{0,8},{4,12},{8,0},{12,4},{16,24},{20,28},{24,16},{28,20},{1,9},{5... | collective-permute-start | bytes 786440 | tf_op jit(solution)/shard_map/ppermute | solution.py:98
  36.0 2.3 %collective-permute-start.4 = (f32[4,1,1,2,2,2,16,128]{7,6,5,4,3,2,0,1:T(8,128)}, f32[4,1,1,2,2,2,16,128]{7,6,5,4,3,2,0,1:T(8,128)}, u32[]{:S(2)}, u32[]{:S(2)}) collective-permute-start(f32[4,1,1,2,2,2,16,128]{7,6,5,4,3,2,0,1:T(8,128)} %constant_dynamic-slice_fusion.11), channel_id=1, source_target_pairs={{0,2},{1,3},{2,0},{3,1},{4,6},{5,7},{6,4},{7,5},{8,10},{9,11},{10,... | collective-permute-start | bytes 786440 | tf_op jit(solution)/shard_map/ppermute | solution.py:98
  38.3 4.2 %gather_fusion = bf16[16,512,256]{2,1,0:T(8,128)(2,1)} fusion(bf16[6,512,256]{2,1,0:T(8,128)(2,1)} %pad_maximum_fusion, s32[1024]{0:T(1024)S(1)} %pad_clamp_fusion.4), kind=kCustom, calls=%fused_computation.2 | custom fusion | bytes 8388672 | tf_op jit(solution)/shard_map/jit(_take)/gather | solution.py:148
  42.5 4.9 %fusion.5 = f32[4,512,256]{2,1,0:T(8,128)} fusion(bf16[4,4,256,256]{3,2,1,0:T(8,128)(2,1)S(1)} %copy-done, bf16[4,4,512,256]{3,2,1,0:T(8,128)(2,1)} %bitcast.93, pred[4,4]{1,0:T(4,128)(4,1)S(1)} %copy-done.16), kind=kOutput, calls=%fused_computation.12 | convolution fusion | flops 1075838976 | bytes 8388624 | tf_op jit(solution)/shard_map/jerb,jebc->jrc/dot_general | solution.py:149
  51.5 1.8 %collective-permute-start.10 = (f32[4,1,2,2,1,1,16,128]{7,6,5,4,3,2,0,1:T(8,128)S(1)}, f32[4,1,2,2,1,1,16,128]{7,6,5,4,3,2,0,1:T(8,128)S(1)}, u32[]{:S(2)}, u32[]{:S(2)}) collective-permute-start(f32[4,1,2,2,1,1,16,128]{7,6,5,4,3,2,0,1:T(8,128)S(1)} %constant_dynamic-slice_fusion.6), channel_id=1, source_target_pairs={{0,16},{4,20},{8,24},{12,28},{16,0},{20,4},{24,8},{28,12},{1,17},{... | collective-permute-start | bytes 393224 | tf_op jit(solution)/shard_map/ppermute | solution.py:98
  53.3 1.4 %collective-permute-start.9 = (f32[4,1,2,1,1,2,16,128]{7,6,5,4,3,2,0,1:T(8,128)S(1)}, f32[4,1,2,1,1,2,16,128]{7,6,5,4,3,2,0,1:T(8,128)S(1)}, u32[]{:S(2)}, u32[]{:S(2)}) collective-permute-start(f32[4,1,2,1,1,2,16,128]{7,6,5,4,3,2,0,1:T(8,128)S(1)} %constant_dynamic-slice_fusion.7), channel_id=1, source_target_pairs={{0,8},{4,12},{8,0},{12,4},{16,24},{20,28},{24,16},{28,20},{1,9},{5... | collective-permute-start | bytes 393224 | tf_op jit(solution)/shard_map/ppermute | solution.py:98
  55.4 4.5 %collective-permute-done.9 = f32[4,1,2,1,1,2,16,128]{7,6,5,4,3,2,0,1:T(8,128)S(1)} collective-permute-done((f32[4,1,2,1,1,2,16,128]{7,6,5,4,3,2,0,1:T(8,128)S(1)}, f32[4,1,2,1,1,2,16,128]{7,6,5,4,3,2,0,1:T(8,128)S(1)}, u32[]{:S(2)}, u32[]{:S(2)}) %collective-permute-start.9) | collective-permute-done | bytes 131104 | tf_op jit(solution)/shard_map/ppermute | solution.py:98
  64.5 2.7 %collective-permute-done.11 = f32[4,1,1,1,1,2,16,128]{7,6,5,4,3,2,0,1:T(8,128)S(1)} collective-permute-done((f32[4,1,1,1,1,2,16,128]{7,6,5,4,3,2,0,1:T(8,128)S(1)}, f32[4,1,1,1,1,2,16,128]{7,6,5,4,3,2,0,1:T(8,128)S(1)}, u32[]{:S(2)}, u32[]{:S(2)}) %collective-permute-start.11) | collective-permute-done | bytes 65568 | tf_op jit(solution)/shard_map/ppermute | solution.py:98
  68.2 2.1 %collective-permute-start.14 = (f32[4,1,1,1,1,1,16,128]{7,6,5,4,3,2,0,1:T(8,128)S(1)}, f32[4,1,1,1,1,1,16,128]{7,6,5,4,3,2,0,1:T(8,128)S(1)}, u32[]{:S(2)}, u32[]{:S(2)}) collective-permute-start(f32[4,1,1,1,1,1,16,128]{7,6,5,4,3,2,0,1:T(8,128)S(1)} %constant_dynamic-slice_fusion.2), channel_id=1, source_target_pairs={{0,2},{1,3},{2,0},{3,1},{4,6},{5,7},{6,4},{7,5},{8,10},{9,11},{10,... | collective-permute-start | bytes 98312 | tf_op jit(solution)/shard_map/ppermute | solution.py:98
  70.3 1.3 %collective-permute-start.16 = (f32[4,1,1,1,1,1,16,128]{7,6,5,4,3,2,0,1:T(8,128)S(1)}, f32[4,1,1,1,1,1,16,128]{7,6,5,4,3,2,0,1:T(8,128)S(1)}, u32[]{:S(2)}, u32[]{:S(2)}) collective-permute-start(f32[4,1,1,1,1,1,16,128]{7,6,5,4,3,2,0,1:T(8,128)S(1)} %constant_dynamic-slice_fusion), channel_id=1, source_target_pairs={{0,4},{4,0},{8,12},{12,8},{16,20},{20,16},{24,28},{28,24},{1,5},{5... | collective-permute-start | bytes 98312 | tf_op jit(solution)/shard_map/ppermute | solution.py:98
  72.4 1.9 %collective-permute-done.16 = f32[4,1,1,1,1,1,16,128]{7,6,5,4,3,2,0,1:T(8,128)S(1)} collective-permute-done((f32[4,1,1,1,1,1,16,128]{7,6,5,4,3,2,0,1:T(8,128)S(1)}, f32[4,1,1,1,1,1,16,128]{7,6,5,4,3,2,0,1:T(8,128)S(1)}, u32[]{:S(2)}, u32[]{:S(2)}) %collective-permute-start.16) | collective-permute-done | bytes 32800 | tf_op jit(solution)/shard_map/ppermute | solution.py:98
  75.0 1.8 %fusion.13 = bf16[12,16,128]{2,1,0:T(8,128)(2,1)S(1)} fusion(bf16[12,4,136,128]{3,2,1,0:T(8,128)(2,1)} %copy-done.10, bf16[12,4,16,128]{3,2,1,0:T(8,128)(2,1)S(1)} %bitcast.103, pred[12,4]{1,0:T(8,128)(4,1)S(1)} %copy.64), kind=kOutput, calls=%fused_computation.17 | convolution fusion | flops 25288704 | bytes 1818672 | tf_op jit(solution)/shard_map/nerc,necd->nrd/dot_general | solution.py:173
  77.6 2.0 %collective-permute-start.21 = (bf16[4,1,1,1,1,1,16,128]{7,6,0,5,4,3,2,1:T(8,128)(2,1)S(1)}, bf16[4,1,1,1,1,1,16,128]{7,6,0,5,4,3,2,1:T(8,128)(2,1)S(1)}, u32[]{:S(2)}, u32[]{:S(2)}) collective-permute-start(bf16[4,1,1,1,1,1,16,128]{7,6,0,5,4,3,2,1:T(8,128)(2,1)S(1)} %get-tuple-element.45), channel_id=1, source_target_pairs={{0,2},{1,3},{2,0},{3,1},{4,6},{5,7},{6,4},{7,5},{8,10},{9,11},{10,... | collective-permute-start | bytes 49160 | tf_op jit(solution)/shard_map/ppermute | solution.py:103
  80.4 1.7 %collective-permute-done.17 = bf16[4,1,1,1,1,1,16,128]{7,6,0,5,4,3,2,1:T(8,128)(2,1)S(1)} collective-permute-done((bf16[4,1,1,1,1,1,16,128]{7,6,0,5,4,3,2,1:T(8,128)(2,1)S(1)}, bf16[4,1,1,1,1,1,16,128]{7,6,0,5,4,3,2,1:T(8,128)(2,1)S(1)}, u32[]{:S(2)}, u32[]{:S(2)}) %collective-permute-start.17) | collective-permute-done | bytes 16416 | tf_op jit(solution)/shard_map/ppermute | solution.py:103
  82.3 2.0 %collective-permute-start.22 = (bf16[4,1,2,1,1,1,16,128]{7,6,0,5,4,3,2,1:T(8,128)(2,1)S(1)}, bf16[4,1,2,1,1,1,16,128]{7,6,0,5,4,3,2,1:T(8,128)(2,1)S(1)}, u32[]{:S(2)}, u32[]{:S(2)}) collective-permute-start(bf16[4,1,2,1,1,1,16,128]{7,6,0,5,4,3,2,1:T(8,128)(2,1)S(1)} %maximum_select_fusion.16), channel_id=1, source_target_pairs={{0,16},{4,20},{8,24},{12,28},{16,0},{20,4},{24,8},{28,12},{1,17},{... | collective-permute-start | bytes 98312 | tf_op jit(solution)/shard_map/ppermute | solution.py:103
  86.2 1.7 %collective-permute-start.19 = (bf16[4,1,1,1,2,2,16,128]{7,6,0,5,4,3,2,1:T(8,128)(2,1)S(1)}, bf16[4,1,1,1,2,2,16,128]{7,6,0,5,4,3,2,1:T(8,128)(2,1)S(1)}, u32[]{:S(2)}, u32[]{:S(2)}) collective-permute-start(bf16[4,1,1,1,2,2,16,128]{7,6,0,5,4,3,2,1:T(8,128)(2,1)S(1)} %maximum_select_fusion.9), channel_id=1, source_target_pairs={{0,4},{4,0},{8,12},{12,8},{16,20},{20,16},{24,28},{28,24},{1,5},{5... | collective-permute-start | bytes 196616 | tf_op jit(solution)/shard_map/ppermute | solution.py:103
  87.9 1.4 %collective-permute-start.23 = (bf16[4,1,2,1,1,2,16,128]{7,6,0,5,4,3,2,1:T(8,128)(2,1)S(1)}, bf16[4,1,2,1,1,2,16,128]{7,6,0,5,4,3,2,1:T(8,128)(2,1)S(1)}, u32[]{:S(2)}, u32[]{:S(2)}) collective-permute-start(bf16[4,1,2,1,1,2,16,128]{7,6,0,5,4,3,2,1:T(8,128)(2,1)S(1)} %maximum_select_fusion.11), channel_id=1, source_target_pairs={{0,8},{4,12},{8,0},{12,4},{16,24},{20,28},{24,16},{28,20},{1,9},{5... | collective-permute-start | bytes 196616 | tf_op jit(solution)/shard_map/ppermute | solution.py:103
  89.3 1.6 %collective-permute-start.27 = (bf16[4,1,2,2,1,1,16,128]{7,6,0,5,4,3,2,1:T(8,128)(2,1)S(1)}, bf16[4,1,2,2,1,1,16,128]{7,6,0,5,4,3,2,1:T(8,128)(2,1)S(1)}, u32[]{:S(2)}, u32[]{:S(2)}) collective-permute-start(bf16[4,1,2,2,1,1,16,128]{7,6,0,5,4,3,2,1:T(8,128)(2,1)S(1)} %fusion.29), channel_id=1, source_target_pairs={{0,16},{4,20},{8,24},{12,28},{16,0},{20,4},{24,8},{28,12},{1,17},{... | collective-permute-start | bytes 196616 | tf_op jit(solution)/shard_map/ppermute | solution.py:103
  90.9 1.8 %collective-permute-start.20 = (bf16[4,1,1,2,2,2,16,128]{7,6,0,5,4,3,2,1:T(8,128)(2,1)S(1)}, bf16[4,1,1,2,2,2,16,128]{7,6,0,5,4,3,2,1:T(8,128)(2,1)S(1)}, u32[]{:S(2)}, u32[]{:S(2)}) collective-permute-start(bf16[4,1,1,2,2,2,16,128]{7,6,0,5,4,3,2,1:T(8,128)(2,1)S(1)} %maximum_select_fusion.5), channel_id=1, source_target_pairs={{0,2},{1,3},{2,0},{3,1},{4,6},{5,7},{6,4},{7,5},{8,10},{9,11},{10,... | collective-permute-start | bytes 393224 | tf_op jit(solution)/shard_map/ppermute | solution.py:103
  92.7 1.2 %collective-permute-start.24 = (bf16[4,1,2,1,2,2,16,128]{7,6,0,5,4,3,2,1:T(8,128)(2,1)S(1)}, bf16[4,1,2,1,2,2,16,128]{7,6,0,5,4,3,2,1:T(8,128)(2,1)S(1)}, u32[]{:S(2)}, u32[]{:S(2)}) collective-permute-start(bf16[4,1,2,1,2,2,16,128]{7,6,0,5,4,3,2,1:T(8,128)(2,1)S(1)} %maximum_select_fusion.6), channel_id=1, source_target_pairs={{0,4},{4,0},{8,12},{12,8},{16,20},{20,16},{24,28},{28,24},{1,5},{5... | collective-permute-start | bytes 393224 | tf_op jit(solution)/shard_map/ppermute | solution.py:103
  94.0 1.2 %collective-permute-done.27 = bf16[4,1,2,2,1,1,16,128]{7,6,0,5,4,3,2,1:T(8,128)(2,1)S(1)} collective-permute-done((bf16[4,1,2,2,1,1,16,128]{7,6,0,5,4,3,2,1:T(8,128)(2,1)S(1)}, bf16[4,1,2,2,1,1,16,128]{7,6,0,5,4,3,2,1:T(8,128)(2,1)S(1)}, u32[]{:S(2)}, u32[]{:S(2)}) %collective-permute-start.27) | collective-permute-done | bytes 65568 | tf_op jit(solution)/shard_map/ppermute | solution.py:103
  96.0 1.7 %collective-permute-done.24 = bf16[4,1,2,1,2,2,16,128]{7,6,0,5,4,3,2,1:T(8,128)(2,1)S(1)} collective-permute-done((bf16[4,1,2,1,2,2,16,128]{7,6,0,5,4,3,2,1:T(8,128)(2,1)S(1)}, bf16[4,1,2,1,2,2,16,128]{7,6,0,5,4,3,2,1:T(8,128)(2,1)S(1)}, u32[]{:S(2)}, u32[]{:S(2)}) %collective-permute-start.24) | collective-permute-done | bytes 131104 | tf_op jit(solution)/shard_map/ppermute | solution.py:103
  97.8 2.4 %collective-permute-done.28 = bf16[4,1,2,2,1,2,16,128]{7,6,0,5,4,3,2,1:T(8,128)(2,1)S(1)} collective-permute-done((bf16[4,1,2,2,1,2,16,128]{7,6,0,5,4,3,2,1:T(8,128)(2,1)S(1)}, bf16[4,1,2,2,1,2,16,128]{7,6,0,5,4,3,2,1:T(8,128)(2,1)S(1)}, u32[]{:S(2)}, u32[]{:S(2)}) %collective-permute-start.28) | collective-permute-done | bytes 131104 | tf_op jit(solution)/shard_map/ppermute | solution.py:103
  101.5 1.4 %collective-permute-done.29 = bf16[12,256,128]{2,1,0:T(8,128)(2,1)} collective-permute-done((bf16[12,256,128]{2,1,0:T(8,128)(2,1)S(1)}, bf16[12,256,128]{2,1,0:T(8,128)(2,1)}, u32[]{:S(2)}, u32[]{:S(2)}) %collective-permute-start.29) | collective-permute-done | bytes 786464 | tf_op jit(solution)/shard_map/ppermute | solution.py:182
  102.9 1.8 %gather_fusion.5 = bf16[8,256,128]{2,1,0:T(8,128)(2,1)S(1)} fusion(bf16[12,256,128]{2,1,0:T(8,128)(2,1)} %collective-permute-done.29, s32[1024]{0:T(1024)S(1)} %pad_clamp_fusion), kind=kCustom, calls=%fused_computation.1.clone | custom fusion | bytes 1048608 | tf_op jit(solution)/shard_map/jit(_take)/gather | solution.py:184
  (159 shorter events, 32.4 us)
Async XLA Ops:
  0.0 42.4 %copy-start = (bf16[4,4,256,256]{3,2,1,0:T(8,128)(2,1)S(1)}, bf16[4,4,256,256]{3,2,1,0:T(8,128)(2,1)}, u32[]{:S(2)}) copy-start(bf16[4,4,256,256]{3,2,1,0:T(8,128)(2,1)} %param.12) | copy-start | bytes 6291460
  1.5 16.1 %copy-start.1 = (s32[4]{0:T(128)S(1)}, s32[4]{0:T(128)}, u32[]{:S(2)}) copy-start(s32[4]{0:T(128)} %constant.312.clone) | copy-start | bytes 52
  6.7 21.5 %collective-permute-start.2 = (f32[12,256,128]{2,1,0:T(8,128)}, f32[12,256,128]{2,1,0:T(8,128)}, u32[]{:S(2)}, u32[]{:S(2)}) collective-permute-start(f32[12,256,128]{2,1,0:T(8,128)} %shard_map.83), channel_id=1, source_target_pairs={{0,1},{1,0},{2,3},{3,2},{4,5},{5,4},{6,7},{7,6},{8,9},{9,8},{10,11... | collective-permute-start | bytes 4718600 | tf_op jit(solution)/shard_map/ppermute | solution.py:137
  8.0 17.8 %collective-permute-start = (bf16[1,512,256]{2,1,0:T(8,128)(2,1)}, bf16[1,512,256]{2,1,0:T(8,128)(2,1)}, u32[]{:S(2)}, u32[]{:S(2)}) collective-permute-start(bf16[1,512,256]{2,1,0:T(8,128)(2,1)} %get-tuple-element.41), channel_id=1, source_target_pairs={{0,1},{1,2},{2,3},{3,4},{4,5},{5,6},{6,7},{7,8},{8,9},{9,10},{10,1... | collective-permute-start | bytes 786440 | tf_op jit(solution)/shard_map/ppermute | solution.py:65
  10.6 15.1 %collective-permute-start.1 = (bf16[1,512,256]{2,1,0:T(8,128)(2,1)}, bf16[1,512,256]{2,1,0:T(8,128)(2,1)}, u32[]{:S(2)}, u32[]{:S(2)}) collective-permute-start(bf16[1,512,256]{2,1,0:T(8,128)(2,1)} %get-tuple-element.42), channel_id=1, source_target_pairs={{1,0},{2,1},{3,2},{4,3},{5,4},{6,5},{7,6},{8,7},{9,8},{10,9},{11,1... | collective-permute-start | bytes 786440 | tf_op jit(solution)/shard_map/ppermute | solution.py:67
  13.4 16.4 %collective-permute-start.3 = (bf16[3,4,136,128]{3,2,1,0:T(8,128)(2,1)}, bf16[3,4,136,128]{3,2,1,0:T(8,128)(2,1)}, u32[]{:S(2)}, u32[]{:S(2)}) collective-permute-start(bf16[3,4,136,128]{3,2,1,0:T(8,128)(2,1)} %pad_maximum_fusion.3), channel_id=1, source_target_pairs={{0,2},{1,3},{2,0},{3,1},{4,6},{5,7},{6,4},{7,5},{8,10},{9,11},{10,... | collective-permute-start | bytes 1253384 | tf_op jit(solution)/shard_map/ppermute | solution.py:142
  31.5 17.0 %collective-permute-start.6 = (f32[4,1,2,2,1,2,16,128]{7,6,5,4,3,2,0,1:T(8,128)}, f32[4,1,2,2,1,2,16,128]{7,6,5,4,3,2,0,1:T(8,128)}, u32[]{:S(2)}, u32[]{:S(2)}) collective-permute-start(f32[4,1,2,2,1,2,16,128]{7,6,5,4,3,2,0,1:T(8,128)} %constant_dynamic-slice_fusion.9), channel_id=1, source_target_pairs={{0,8},{4,12},{8,0},{12,4},{16,24},{20,28},{24,16},{28,20},{1,9},{5... | collective-permute-start | bytes 786440 | tf_op jit(solution)/shard_map/ppermute | solution.py:98
  34.5 15.0 %collective-permute-start.5 = (f32[4,1,2,1,2,2,16,128]{7,6,5,4,3,2,0,1:T(8,128)}, f32[4,1,2,1,2,2,16,128]{7,6,5,4,3,2,0,1:T(8,128)}, u32[]{:S(2)}, u32[]{:S(2)}) collective-permute-start(f32[4,1,2,1,2,2,16,128]{7,6,5,4,3,2,0,1:T(8,128)} %constant_dynamic-slice_fusion.10), channel_id=1, source_target_pairs={{0,4},{4,0},{8,12},{12,8},{16,20},{20,16},{24,28},{28,24},{1,5},{5... | collective-permute-start | bytes 786440 | tf_op jit(solution)/shard_map/ppermute | solution.py:98
  36.0 14.5 %collective-permute-start.4 = (f32[4,1,1,2,2,2,16,128]{7,6,5,4,3,2,0,1:T(8,128)}, f32[4,1,1,2,2,2,16,128]{7,6,5,4,3,2,0,1:T(8,128)}, u32[]{:S(2)}, u32[]{:S(2)}) collective-permute-start(f32[4,1,1,2,2,2,16,128]{7,6,5,4,3,2,0,1:T(8,128)} %constant_dynamic-slice_fusion.11), channel_id=1, source_target_pairs={{0,2},{1,3},{2,0},{3,1},{4,6},{5,7},{6,4},{7,5},{8,10},{9,11},{10,... | collective-permute-start | bytes 786440 | tf_op jit(solution)/shard_map/ppermute | solution.py:98
  51.5 9.2 %collective-permute-start.10 = (f32[4,1,2,2,1,1,16,128]{7,6,5,4,3,2,0,1:T(8,128)S(1)}, f32[4,1,2,2,1,1,16,128]{7,6,5,4,3,2,0,1:T(8,128)S(1)}, u32[]{:S(2)}, u32[]{:S(2)}) collective-permute-start(f32[4,1,2,2,1,1,16,128]{7,6,5,4,3,2,0,1:T(8,128)S(1)} %constant_dynamic-slice_fusion.6), channel_id=1, source_target_pairs={{0,16},{4,20},{8,24},{12,28},{16,0},{20,4},{24,8},{28,12},{1,17},{... | collective-permute-start | bytes 393224 | tf_op jit(solution)/shard_map/ppermute | solution.py:98
  53.3 6.6 %collective-permute-start.9 = (f32[4,1,2,1,1,2,16,128]{7,6,5,4,3,2,0,1:T(8,128)S(1)}, f32[4,1,2,1,1,2,16,128]{7,6,5,4,3,2,0,1:T(8,128)S(1)}, u32[]{:S(2)}, u32[]{:S(2)}) collective-permute-start(f32[4,1,2,1,1,2,16,128]{7,6,5,4,3,2,0,1:T(8,128)S(1)} %constant_dynamic-slice_fusion.7), channel_id=1, source_target_pairs={{0,8},{4,12},{8,0},{12,4},{16,24},{20,28},{24,16},{28,20},{1,9},{5... | collective-permute-start | bytes 393224 | tf_op jit(solution)/shard_map/ppermute | solution.py:98
  54.7 6.1 %collective-permute-start.7 = (bf16[6,4,136,128]{3,2,1,0:T(8,128)(2,1)S(1)}, bf16[6,4,136,128]{3,2,1,0:T(8,128)(2,1)S(1)}, u32[]{:S(2)}, u32[]{:S(2)}) collective-permute-start(bf16[6,4,136,128]{3,2,1,0:T(8,128)(2,1)S(1)} %pad_maximum_fusion.1), channel_id=1, source_target_pairs={{0,1},{1,0},{2,3},{3,2},{4,5},{5,4},{6,7},{7,6},{8,9},{9,8},{10,11... | collective-permute-start | bytes 2506760 | tf_op jit(solution)/shard_map/ppermute | solution.py:162
  54.7 6.0 %collective-permute-start.8 = (f32[4,1,1,1,2,2,16,128]{7,6,5,4,3,2,0,1:T(8,128)S(1)}, f32[4,1,1,1,2,2,16,128]{7,6,5,4,3,2,0,1:T(8,128)S(1)}, u32[]{:S(2)}, u32[]{:S(2)}) collective-permute-start(f32[4,1,1,1,2,2,16,128]{7,6,5,4,3,2,0,1:T(8,128)S(1)} %constant_dynamic-slice_fusion.8), channel_id=1, source_target_pairs={{0,4},{4,0},{8,12},{12,8},{16,20},{20,16},{24,28},{28,24},{1,5},{5... | collective-permute-start | bytes 393224 | tf_op jit(solution)/shard_map/ppermute | solution.py:98
  62.2 5.0 %collective-permute-start.11 = (f32[4,1,1,1,1,2,16,128]{7,6,5,4,3,2,0,1:T(8,128)S(1)}, f32[4,1,1,1,1,2,16,128]{7,6,5,4,3,2,0,1:T(8,128)S(1)}, u32[]{:S(2)}, u32[]{:S(2)}) collective-permute-start(f32[4,1,1,1,1,2,16,128]{7,6,5,4,3,2,0,1:T(8,128)S(1)} %constant_dynamic-slice_fusion.5), channel_id=1, source_target_pairs={{0,8},{4,12},{8,0},{12,4},{16,24},{20,28},{24,16},{28,20},{1,9},{5... | collective-permute-start | bytes 196616 | tf_op jit(solution)/shard_map/ppermute | solution.py:98
  63.0 5.2 %collective-permute-start.13 = (f32[4,1,2,1,1,1,16,128]{7,6,5,4,3,2,0,1:T(8,128)S(1)}, f32[4,1,2,1,1,1,16,128]{7,6,5,4,3,2,0,1:T(8,128)S(1)}, u32[]{:S(2)}, u32[]{:S(2)}) collective-permute-start(f32[4,1,2,1,1,1,16,128]{7,6,5,4,3,2,0,1:T(8,128)S(1)} %constant_dynamic-slice_fusion.3), channel_id=1, source_target_pairs={{0,16},{4,20},{8,24},{12,28},{16,0},{20,4},{24,8},{28,12},{1,17},{... | collective-permute-start | bytes 196616 | tf_op jit(solution)/shard_map/ppermute | solution.py:98
  64.2 6.1 %collective-permute-start.15 = (f32[4,1,1,2,1,1,16,128]{7,6,5,4,3,2,0,1:T(8,128)S(1)}, f32[4,1,1,2,1,1,16,128]{7,6,5,4,3,2,0,1:T(8,128)S(1)}, u32[]{:S(2)}, u32[]{:S(2)}) collective-permute-start(f32[4,1,1,2,1,1,16,128]{7,6,5,4,3,2,0,1:T(8,128)S(1)} %constant_dynamic-slice_fusion.1), channel_id=1, source_target_pairs={{0,2},{1,3},{2,0},{3,1},{4,6},{5,7},{6,4},{7,5},{8,10},{9,11},{10,... | collective-permute-start | bytes 196616 | tf_op jit(solution)/shard_map/ppermute | solution.py:98
  67.3 5.1 %collective-permute-start.12 = (f32[4,1,1,1,1,1,16,128]{7,6,5,4,3,2,0,1:T(8,128)S(1)}, f32[4,1,1,1,1,1,16,128]{7,6,5,4,3,2,0,1:T(8,128)S(1)}, u32[]{:S(2)}, u32[]{:S(2)}) collective-permute-start(f32[4,1,1,1,1,1,16,128]{7,6,5,4,3,2,0,1:T(8,128)S(1)} %constant_dynamic-slice_fusion.4), channel_id=1, source_target_pairs={{0,16},{4,20},{8,24},{12,28},{16,0},{20,4},{24,8},{28,12},{1,17},{... | collective-permute-start | bytes 98312 | tf_op jit(solution)/shard_map/ppermute | solution.py:98
  68.2 4.2 %collective-permute-start.14 = (f32[4,1,1,1,1,1,16,128]{7,6,5,4,3,2,0,1:T(8,128)S(1)}, f32[4,1,1,1,1,1,16,128]{7,6,5,4,3,2,0,1:T(8,128)S(1)}, u32[]{:S(2)}, u32[]{:S(2)}) collective-permute-start(f32[4,1,1,1,1,1,16,128]{7,6,5,4,3,2,0,1:T(8,128)S(1)} %constant_dynamic-slice_fusion.2), channel_id=1, source_target_pairs={{0,2},{1,3},{2,0},{3,1},{4,6},{5,7},{6,4},{7,5},{8,10},{9,11},{10,... | collective-permute-start | bytes 98312 | tf_op jit(solution)/shard_map/ppermute | solution.py:98
  70.3 4.0 %collective-permute-start.16 = (f32[4,1,1,1,1,1,16,128]{7,6,5,4,3,2,0,1:T(8,128)S(1)}, f32[4,1,1,1,1,1,16,128]{7,6,5,4,3,2,0,1:T(8,128)S(1)}, u32[]{:S(2)}, u32[]{:S(2)}) collective-permute-start(f32[4,1,1,1,1,1,16,128]{7,6,5,4,3,2,0,1:T(8,128)S(1)} %constant_dynamic-slice_fusion), channel_id=1, source_target_pairs={{0,4},{4,0},{8,12},{12,8},{16,20},{20,16},{24,28},{28,24},{1,5},{5... | collective-permute-start | bytes 98312 | tf_op jit(solution)/shard_map/ppermute | solution.py:98
  77.4 4.7 %collective-permute-start.17 = (bf16[4,1,1,1,1,1,16,128]{7,6,0,5,4,3,2,1:T(8,128)(2,1)S(1)}, bf16[4,1,1,1,1,1,16,128]{7,6,0,5,4,3,2,1:T(8,128)(2,1)S(1)}, u32[]{:S(2)}, u32[]{:S(2)}) collective-permute-start(bf16[4,1,1,1,1,1,16,128]{7,6,0,5,4,3,2,1:T(8,128)(2,1)S(1)} %get-tuple-element.44), channel_id=1, source_target_pairs={{0,16},{4,20},{8,24},{12,28},{16,0},{20,4},{24,8},{28,12},{1,17},{... | collective-permute-start | bytes 49160 | tf_op jit(solution)/shard_map/ppermute | solution.py:103
  77.6 4.6 %collective-permute-start.21 = (bf16[4,1,1,1,1,1,16,128]{7,6,0,5,4,3,2,1:T(8,128)(2,1)S(1)}, bf16[4,1,1,1,1,1,16,128]{7,6,0,5,4,3,2,1:T(8,128)(2,1)S(1)}, u32[]{:S(2)}, u32[]{:S(2)}) collective-permute-start(bf16[4,1,1,1,1,1,16,128]{7,6,0,5,4,3,2,1:T(8,128)(2,1)S(1)} %get-tuple-element.45), channel_id=1, source_target_pairs={{0,2},{1,3},{2,0},{3,1},{4,6},{5,7},{6,4},{7,5},{8,10},{9,11},{10,... | collective-permute-start | bytes 49160 | tf_op jit(solution)/shard_map/ppermute | solution.py:103
  79.6 4.6 %collective-permute-start.25 = (bf16[4,1,1,1,1,1,16,128]{7,6,0,5,4,3,2,1:T(8,128)(2,1)S(1)}, bf16[4,1,1,1,1,1,16,128]{7,6,0,5,4,3,2,1:T(8,128)(2,1)S(1)}, u32[]{:S(2)}, u32[]{:S(2)}) collective-permute-start(bf16[4,1,1,1,1,1,16,128]{7,6,0,5,4,3,2,1:T(8,128)(2,1)S(1)} %get-tuple-element.46), channel_id=1, source_target_pairs={{0,4},{4,0},{8,12},{12,8},{16,20},{20,16},{24,28},{28,24},{1,5},{5... | collective-permute-start | bytes 49160 | tf_op jit(solution)/shard_map/ppermute | solution.py:103
  82.2 4.0 %collective-permute-start.18 = (bf16[4,1,1,1,1,2,16,128]{7,6,0,5,4,3,2,1:T(8,128)(2,1)S(1)}, bf16[4,1,1,1,1,2,16,128]{7,6,0,5,4,3,2,1:T(8,128)(2,1)S(1)}, u32[]{:S(2)}, u32[]{:S(2)}) collective-permute-start(bf16[4,1,1,1,1,2,16,128]{7,6,0,5,4,3,2,1:T(8,128)(2,1)S(1)} %maximum_select_fusion.14), channel_id=1, source_target_pairs={{0,8},{4,12},{8,0},{12,4},{16,24},{20,28},{24,16},{28,20},{1,9},{5... | collective-permute-start | bytes 98312 | tf_op jit(solution)/shard_map/ppermute | solution.py:103
  82.3 5.6 %collective-permute-start.22 = (bf16[4,1,2,1,1,1,16,128]{7,6,0,5,4,3,2,1:T(8,128)(2,1)S(1)}, bf16[4,1,2,1,1,1,16,128]{7,6,0,5,4,3,2,1:T(8,128)(2,1)S(1)}, u32[]{:S(2)}, u32[]{:S(2)}) collective-permute-start(bf16[4,1,2,1,1,1,16,128]{7,6,0,5,4,3,2,1:T(8,128)(2,1)S(1)} %maximum_select_fusion.16), channel_id=1, source_target_pairs={{0,16},{4,20},{8,24},{12,28},{16,0},{20,4},{24,8},{28,12},{1,17},{... | collective-permute-start | bytes 98312 | tf_op jit(solution)/shard_map/ppermute | solution.py:103
  84.3 5.0 %collective-permute-start.26 = (bf16[4,1,1,2,1,1,16,128]{7,6,0,5,4,3,2,1:T(8,128)(2,1)S(1)}, bf16[4,1,1,2,1,1,16,128]{7,6,0,5,4,3,2,1:T(8,128)(2,1)S(1)}, u32[]{:S(2)}, u32[]{:S(2)}) collective-permute-start(bf16[4,1,1,2,1,1,16,128]{7,6,0,5,4,3,2,1:T(8,128)(2,1)S(1)} %maximum_select_fusion.18), channel_id=1, source_target_pairs={{0,2},{1,3},{2,0},{3,1},{4,6},{5,7},{6,4},{7,5},{8,10},{9,11},{10,... | collective-permute-start | bytes 98312 | tf_op jit(solution)/shard_map/ppermute | solution.py:103
  86.2 4.7 %collective-permute-start.19 = (bf16[4,1,1,1,2,2,16,128]{7,6,0,5,4,3,2,1:T(8,128)(2,1)S(1)}, bf16[4,1,1,1,2,2,16,128]{7,6,0,5,4,3,2,1:T(8,128)(2,1)S(1)}, u32[]{:S(2)}, u32[]{:S(2)}) collective-permute-start(bf16[4,1,1,1,2,2,16,128]{7,6,0,5,4,3,2,1:T(8,128)(2,1)S(1)} %maximum_select_fusion.9), channel_id=1, source_target_pairs={{0,4},{4,0},{8,12},{12,8},{16,20},{20,16},{24,28},{28,24},{1,5},{5... | collective-permute-start | bytes 196616 | tf_op jit(solution)/shard_map/ppermute | solution.py:103
  87.9 4.9 %collective-permute-start.23 = (bf16[4,1,2,1,1,2,16,128]{7,6,0,5,4,3,2,1:T(8,128)(2,1)S(1)}, bf16[4,1,2,1,1,2,16,128]{7,6,0,5,4,3,2,1:T(8,128)(2,1)S(1)}, u32[]{:S(2)}, u32[]{:S(2)}) collective-permute-start(bf16[4,1,2,1,1,2,16,128]{7,6,0,5,4,3,2,1:T(8,128)(2,1)S(1)} %maximum_select_fusion.11), channel_id=1, source_target_pairs={{0,8},{4,12},{8,0},{12,4},{16,24},{20,28},{24,16},{28,20},{1,9},{5... | collective-permute-start | bytes 196616 | tf_op jit(solution)/shard_map/ppermute | solution.py:103
  89.3 5.9 %collective-permute-start.27 = (bf16[4,1,2,2,1,1,16,128]{7,6,0,5,4,3,2,1:T(8,128)(2,1)S(1)}, bf16[4,1,2,2,1,1,16,128]{7,6,0,5,4,3,2,1:T(8,128)(2,1)S(1)}, u32[]{:S(2)}, u32[]{:S(2)}) collective-permute-start(bf16[4,1,2,2,1,1,16,128]{7,6,0,5,4,3,2,1:T(8,128)(2,1)S(1)} %fusion.29), channel_id=1, source_target_pairs={{0,16},{4,20},{8,24},{12,28},{16,0},{20,4},{24,8},{28,12},{1,17},{... | collective-permute-start | bytes 196616 | tf_op jit(solution)/shard_map/ppermute | solution.py:103
  90.9 5.0 %collective-permute-start.20 = (bf16[4,1,1,2,2,2,16,128]{7,6,0,5,4,3,2,1:T(8,128)(2,1)S(1)}, bf16[4,1,1,2,2,2,16,128]{7,6,0,5,4,3,2,1:T(8,128)(2,1)S(1)}, u32[]{:S(2)}, u32[]{:S(2)}) collective-permute-start(bf16[4,1,1,2,2,2,16,128]{7,6,0,5,4,3,2,1:T(8,128)(2,1)S(1)} %maximum_select_fusion.5), channel_id=1, source_target_pairs={{0,2},{1,3},{2,0},{3,1},{4,6},{5,7},{6,4},{7,5},{8,10},{9,11},{10,... | collective-permute-start | bytes 393224 | tf_op jit(solution)/shard_map/ppermute | solution.py:103
  92.7 5.0 %collective-permute-start.24 = (bf16[4,1,2,1,2,2,16,128]{7,6,0,5,4,3,2,1:T(8,128)(2,1)S(1)}, bf16[4,1,2,1,2,2,16,128]{7,6,0,5,4,3,2,1:T(8,128)(2,1)S(1)}, u32[]{:S(2)}, u32[]{:S(2)}) collective-permute-start(bf16[4,1,2,1,2,2,16,128]{7,6,0,5,4,3,2,1:T(8,128)(2,1)S(1)} %maximum_select_fusion.6), channel_id=1, source_target_pairs={{0,4},{4,0},{8,12},{12,8},{16,20},{20,16},{24,28},{28,24},{1,5},{5... | collective-permute-start | bytes 393224 | tf_op jit(solution)/shard_map/ppermute | solution.py:103
  95.2 5.0 %collective-permute-start.28 = (bf16[4,1,2,2,1,2,16,128]{7,6,0,5,4,3,2,1:T(8,128)(2,1)S(1)}, bf16[4,1,2,2,1,2,16,128]{7,6,0,5,4,3,2,1:T(8,128)(2,1)S(1)}, u32[]{:S(2)}, u32[]{:S(2)}) collective-permute-start(bf16[4,1,2,2,1,2,16,128]{7,6,0,5,4,3,2,1:T(8,128)(2,1)S(1)} %maximum_select_fusion.7), channel_id=1, source_target_pairs={{0,8},{4,12},{8,0},{12,4},{16,24},{20,28},{24,16},{28,20},{1,9},{5... | collective-permute-start | bytes 393224 | tf_op jit(solution)/shard_map/ppermute | solution.py:103
  100.4 2.5 %collective-permute-start.29 = (bf16[12,256,128]{2,1,0:T(8,128)(2,1)S(1)}, bf16[12,256,128]{2,1,0:T(8,128)(2,1)}, u32[]{:S(2)}, u32[]{:S(2)}) collective-permute-start(bf16[12,256,128]{2,1,0:T(8,128)(2,1)S(1)} %pad_maximum_fusion.2), channel_id=1, source_target_pairs={{0,1},{1,0},{2,3},{3,2},{4,5},{5,4},{6,7},{7,6},{8,9},{9,8},{10,11... | collective-permute-start | bytes 2359304 | tf_op jit(solution)/shard_map/ppermute | solution.py:182
  (15 other events, 87.1 us)

commit v17 on v15

--- a/solution.py
+++ b/solution.py
@@ -124,6 +124,13 @@
     total_blocks = own_rows * lax.axis_size("coarse")
     bits = device_bits()
     own_half = bit_of(*bits[0])
+    exchanges = list(reversed([bit for bit in bits if bit[0] == "coarse"]))
+    assert len(bits) >= len(exchanges) + 1
+    arriving = lax.ppermute(packed, exchanges[0][0], pairs(*exchanges[0]))
+    xors = [0, exchanges[0][1]]
+    residual, extended, arriving = lax.optimization_barrier((residual, extended, arriving))
+    packed = jnp.concatenate([packed, arriving], axis=0)
+    arriving = None
     links = interface.reshape(-1)
     half = own_half.reshape(1).astype(jnp.int32)
     send = restrict(residual, basis, links, total_blocks, half, 1)
@@ -141,15 +148,11 @@
     parts = [lax.slice_in_dim(whole, s * per, (s + 1) * per, axis=0) for s in range(streams)]
     picked = jnp.take(extended, margin, axis=0)
     local = jnp.einsum("jerb,jebc->jrc", picked, inverse_blocks, preferred_element_type=jnp.float32)
-    exchanges = list(reversed([bit for bit in bits if bit[0] == "coarse"]))
-    assert nb >= len(exchanges) + 2
-    xors = [0]
-    arriving = None
     for step in range(1, nb):
         parts = [halve(x, 1 + orders[s][step], *bits[orders[s][step]], jnp.float32) for s, x in enumerate(parts)]
         if step == 1:
             local, parts = lax.optimization_barrier((local, parts))
-        k = step - 1
+        k = step
         if arriving is not None:
             arriving, parts = lax.optimization_barrier((arriving, parts))
             packed = jnp.concatenate([packed, arriving], axis=0)

time: 112 us -> 116 us (1.036)
  waiting for transfers between devices: 27.4 us -> 23.2 us
  starting transfers between devices: 37.7 us -> 40.8 us
  other arithmetic: 10.1 us -> 12.8 us
  local copies, waits for them, and re-layouts: 17.7 us -> 20.4 us
    ppermute x1, starting transfers between devices: 0.44 us -> 7.06 us  [per_device(): got = lax.ppermute(send, bits[0][0], pairs(*bits[0]))]
    ppermute x2 -> x1, waiting for transfers between devices: 5.83 us -> 0.01 us  [per_device(): arriving = lax.ppermute(packed, axis, pairs(axis, mask))]
    ppermute x0 -> x1, starting transfers between devices: none -> 2.97 us  [per_device(): arriving = lax.ppermute(packed, exchanges[0][0], pairs(*exchanges[0]))]
    ppermute x12, starting transfers between devices: 17.9 us -> 15.1 us  [halve(): lax.ppermute(send.astype(wire), axis, pairs(axis, mask)).astype(x.dtype)]
    ppermute x2 -> x1, starting transfers between devices: 2.08 us -> 0.01 us  [per_device(): arriving = lax.ppermute(packed, axis, pairs(axis, mask))]
    ppermute x12, waiting for transfers between devices: 11.4 us -> 9.44 us  [double(): recv = lax.ppermute(y, axis, pairs(axis, mask))]
    ppermute x12, waiting for transfers between devices: 8.73 us -> 10.4 us  [halve(): lax.ppermute(send.astype(wire), axis, pairs(axis, mask)).astype(x.dtype)]
    ppermute x1, starting transfers between devices: 2.66 us -> 1.46 us  [with_halo(): lax.ppermute(tail, axis, [(i, (i + 1) % count) for i in range(ends)])]
  transfers between devices with their start and end apart: 30 -> 30, of which waited for: 14 -> 19; matrix products, arithmetic and copies ran while one was open for 17% -> 20% of each run, Pallas kernels for 5% -> 4%
where the time goes in v17:
time: 116 us; the launch traced here: 115 us
  starting transfers between devices  40.8 us (35%)
  waiting for transfers between devices  23.2 us (20%)
  local copies, waits for them, and re-layouts  20.4 us (18%)
  other arithmetic  12.8 us (11%)
  Pallas kernels  10 us (9%)
  matrix products  7.18 us (6%)
    ppermute x12, starting transfers between devices, halve(): lax.ppermute(send.astype(wire), axis, pairs(axis, mask)).astype(x.dtype)  15.1 us
    ppermute x12, starting transfers between devices, double(): recv = lax.ppermute(y, axis, pairs(axis, mask))  12.8 us
    ppermute x12, waiting for transfers between devices, halve(): lax.ppermute(send.astype(wire), axis, pairs(axis, mask)).astype(x.dtype)  10.4 us
    pallas_call x2, Pallas kernels, restrict(): pl.pallas_call(functools.partial(restrict_kernel, upper=upper), out_shape...  10 us
    ppermute x12, waiting for transfers between devices, double(): recv = lax.ppermute(y, axis, pairs(axis, mask))  9.44 us
    ppermute x1, starting transfers between devices, per_device(): got = lax.ppermute(send, bits[0][0], pairs(*bits[0]))  7.06 us
    dot_general x1, matrix products, per_device(): jnp.einsum('jerb,jebc->jrc', picked, inverse_blocks, preferred_element_ty...  4.93 us
    unnamed x29, local copies, waits for them, and re-layouts  4.22 us
  transfers between devices with their start and end apart: 30, of which 19 were waited for; matrix products, arithmetic and copies ran while one was open for 20% of the time, Pallas kernels for 4%

profile of v17, /device:TPU:0, one launch (start us, length us, event | category | flops | bytes accessed | tf_op | source)
XLA Modules:
  0.0 114.9 jit_solution(8056646522220068752)
XLA Ops:
  0.9 1.8 %pad_maximum_fusion.3 = bf16[3,4,136,128]{3,2,1,0:T(8,128)(2,1)} fusion(bf16[3,4,8,128]{3,2,1,0:T(8,128)(2,1)S(1)} %broadcast_in_dim.49, bf16[3,4,128,128]{3,2,1,0:T(8,128)(2,1)} %param.16), kind=kLoop, calls=%fused_computation.30 | loop fusion | flops 835584 | bytes 835584 | tf_op jit(solution)/shard_map/concatenate | solution.py:119
  2.7 3.0 %collective-permute-start.2 = (bf16[3,4,136,128]{3,2,1,0:T(8,128)(2,1)}, bf16[3,4,136,128]{3,2,1,0:T(8,128)(2,1)}, u32[]{:S(2)}, u32[]{:S(2)}) collective-permute-start(bf16[3,4,136,128]{3,2,1,0:T(8,128)(2,1)} %pad_maximum_fusion.3), channel_id=1, source_target_pairs={{0,2},{1,3},{2,0},{3,1},{4,6},{5,7},{6,4},{7,5},{8,10},{9,11},{10,... | collective-permute-start | bytes 1253384 | tf_op jit(solution)/shard_map/ppermute | solution.py:129
  5.7 1.9 %fusion.47 = (bf16[1,512,256]{2,1,0:T(8,128)(2,1)}, bf16[1,512,256]{2,1,0:T(8,128)(2,1)}) fusion(bf16[4,512,256]{2,1,0:T(8,128)(2,1)} %residual_ref.1), kind=kLoop, calls=%fused_computation.132 | loop fusion | bytes 1048576 | tf_op jit(solution)/shard_map/slice | solution.py:62
  7.6 1.5 %collective-permute-start = (bf16[1,512,256]{2,1,0:T(8,128)(2,1)}, bf16[1,512,256]{2,1,0:T(8,128)(2,1)S(1)}, u32[]{:S(2)}, u32[]{:S(2)}) collective-permute-start(bf16[1,512,256]{2,1,0:T(8,128)(2,1)} %get-tuple-element.45), channel_id=1, source_target_pairs={{0,1},{1,2},{2,3},{3,4},{4,5},{5,6},{6,7},{7,8},{8,9},{9,10},{10,1... | collective-permute-start | bytes 786440 | tf_op jit(solution)/shard_map/ppermute | solution.py:65
  12.9 2.3 %pad_maximum_fusion = bf16[6,512,256]{2,1,0:T(8,128)(2,1)} fusion(bf16[1,512,256]{2,1,0:T(8,128)(2,1)} %collective-permute-done.1, bf16[4,512,256]{2,1,0:T(8,128)(2,1)S(1)} %copy-done.2, bf16[1,512,256]{2,1,0:T(8,128)(2,1)S(1)} %collective-permute-done), kind=kLoop, calls=%fused_computation.15 | loop fusion | flops 1572864 | bytes 3145728 | tf_op jit(solution)/shard_map/concatenate | solution.py:63
  16.1 5.0 %shard_map.83 = f32[12,256,128]{2,1,0:T(8,128)} custom-call(s32[8]{0:T(128)} %reshape.1777.links, s32[1]{0:T(128)} %bitcast.half, bf16[4,512,256]{2,1,0:T(8,128)(2,1)} %residual_ref.1, bf16[4,2,256,128]{3,2,1,0:T(8,128)(2,1)} %basis_ref.3), custom_call_target="tpu_custom_call" | custom-call | flops 134217728 | bytes 3145728 | tf_op jit(solution)/shard_map/pallas_call | solution.py:36
  21.1 7.1 %collective-permute-start.3 = (f32[12,256,128]{2,1,0:T(8,128)}, f32[12,256,128]{2,1,0:T(8,128)}, u32[]{:S(2)}, u32[]{:S(2)}) collective-permute-start(f32[12,256,128]{2,1,0:T(8,128)} %shard_map.83), channel_id=1, source_target_pairs={{0,1},{1,0},{2,3},{3,2},{4,5},{5,4},{6,7},{7,6},{8,9},{9,8},{10,11... | collective-permute-start | bytes 4718600 | tf_op jit(solution)/shard_map/ppermute | solution.py:144
  29.0 5.0 %shard_map.82 = f32[12,256,128]{2,1,0:T(8,128)} custom-call(s32[8]{0:T(128)} %reshape.1777.links, s32[1]{0:T(128)} %bitcast.half, bf16[4,512,256]{2,1,0:T(8,128)(2,1)} %residual_ref.1, bf16[4,2,256,128]{3,2,1,0:T(8,128)(2,1)} %basis_ref.3), custom_call_target="tpu_custom_call" | custom-call | flops 134217728 | bytes 3145728 | tf_op jit(solution)/shard_map/pallas_call | solution.py:36
  35.6 1.6 %add.233 = f32[12,256,128]{2,1,0:T(8,128)S(1)} add(f32[12,256,128]{2,1,0:T(8,128)S(1)} %copy-done.3, f32[12,256,128]{2,1,0:T(8,128)} %collective-permute-done.3) | non-fusion elementwise | flops 393216 | bytes 4718592 | tf_op jit(solution)/shard_map/add | solution.py:145
  38.2 2.2 %collective-permute-start.6 = (f32[4,1,2,2,1,2,16,128]{7,6,5,4,3,2,0,1:T(8,128)}, f32[4,1,2,2,1,2,16,128]{7,6,5,4,3,2,0,1:T(8,128)}, u32[]{:S(2)}, u32[]{:S(2)}) collective-permute-start(f32[4,1,2,2,1,2,16,128]{7,6,5,4,3,2,0,1:T(8,128)} %constant_dynamic-slice_fusion.9), channel_id=1, source_target_pairs={{0,8},{4,12},{8,0},{12,4},{16,24},{20,28},{24,16},{28,20},{1,9},{5... | collective-permute-start | bytes 786440 | tf_op jit(solution)/shard_map/ppermute | solution.py:98
  41.2 1.5 %collective-permute-start.5 = (f32[4,1,2,1,2,2,16,128]{7,6,5,4,3,2,0,1:T(8,128)}, f32[4,1,2,1,2,2,16,128]{7,6,5,4,3,2,0,1:T(8,128)}, u32[]{:S(2)}, u32[]{:S(2)}) collective-permute-start(f32[4,1,2,1,2,2,16,128]{7,6,5,4,3,2,0,1:T(8,128)} %constant_dynamic-slice_fusion.10), channel_id=1, source_target_pairs={{0,4},{4,0},{8,12},{12,8},{16,20},{20,16},{24,28},{28,24},{1,5},{5... | collective-permute-start | bytes 786440 | tf_op jit(solution)/shard_map/ppermute | solution.py:98
  43.4 1.6 %collective-permute-start.4 = (f32[4,1,1,2,2,2,16,128]{7,6,5,4,3,2,0,1:T(8,128)}, f32[4,1,1,2,2,2,16,128]{7,6,5,4,3,2,0,1:T(8,128)}, u32[]{:S(2)}, u32[]{:S(2)}) collective-permute-start(f32[4,1,1,2,2,2,16,128]{7,6,5,4,3,2,0,1:T(8,128)} %constant_dynamic-slice_fusion.11), channel_id=1, source_target_pairs={{0,2},{1,3},{2,0},{3,1},{4,6},{5,7},{6,4},{7,5},{8,10},{9,11},{10,... | collective-permute-start | bytes 786440 | tf_op jit(solution)/shard_map/ppermute | solution.py:98
  45.0 4.2 %gather_fusion = bf16[16,512,256]{2,1,0:T(8,128)(2,1)} fusion(bf16[6,512,256]{2,1,0:T(8,128)(2,1)} %pad_maximum_fusion, s32[1024]{0:T(1024)S(1)} %pad_clamp_fusion.4), kind=kCustom, calls=%fused_computation.2 | custom fusion | bytes 8388672 | tf_op jit(solution)/shard_map/jit(_take)/gather | solution.py:149
  49.2 4.9 %fusion.5 = f32[4,512,256]{2,1,0:T(8,128)} fusion(bf16[4,4,256,256]{3,2,1,0:T(8,128)(2,1)S(1)} %copy-done, bf16[4,4,512,256]{3,2,1,0:T(8,128)(2,1)} %bitcast.93, pred[4,4]{1,0:T(4,128)(4,1)S(1)} %compare_and_fusion.3), kind=kOutput, calls=%fused_computation.12 | convolution fusion | flops 1075838976 | bytes 8388624 | tf_op jit(solution)/shard_map/jerb,jebc->jrc/dot_general | solution.py:150
  58.3 2.0 %collective-permute-start.9 = (f32[4,1,2,1,1,2,16,128]{7,6,5,4,3,2,0,1:T(8,128)S(1)}, f32[4,1,2,1,1,2,16,128]{7,6,5,4,3,2,0,1:T(8,128)S(1)}, u32[]{:S(2)}, u32[]{:S(2)}) collective-permute-start(f32[4,1,2,1,1,2,16,128]{7,6,5,4,3,2,0,1:T(8,128)S(1)} %constant_dynamic-slice_fusion.7), channel_id=1, source_target_pairs={{0,8},{4,12},{8,0},{12,4},{16,24},{20,28},{24,16},{28,20},{1,9},{5... | collective-permute-start | bytes 393224 | tf_op jit(solution)/shard_map/ppermute | solution.py:98
  61.9 4.3 %collective-permute-done.9 = f32[4,1,2,1,1,2,16,128]{7,6,5,4,3,2,0,1:T(8,128)S(1)} collective-permute-done((f32[4,1,2,1,1,2,16,128]{7,6,5,4,3,2,0,1:T(8,128)S(1)}, f32[4,1,2,1,1,2,16,128]{7,6,5,4,3,2,0,1:T(8,128)S(1)}, u32[]{:S(2)}, u32[]{:S(2)}) %collective-permute-start.9) | collective-permute-done | bytes 131104 | tf_op jit(solution)/shard_map/ppermute | solution.py:98
  68.9 2.1 %collective-permute-start.13 = (f32[4,1,2,1,1,1,16,128]{7,6,5,4,3,2,0,1:T(8,128)S(1)}, f32[4,1,2,1,1,1,16,128]{7,6,5,4,3,2,0,1:T(8,128)S(1)}, u32[]{:S(2)}, u32[]{:S(2)}) collective-permute-start(f32[4,1,2,1,1,1,16,128]{7,6,5,4,3,2,0,1:T(8,128)S(1)} %constant_dynamic-slice_fusion.3), channel_id=1, source_target_pairs={{0,16},{4,20},{8,24},{12,28},{16,0},{20,4},{24,8},{28,12},{1,17},{... | collective-permute-start | bytes 196616 | tf_op jit(solution)/shard_map/ppermute | solution.py:98
  71.8 1.7 %collective-permute-done.11 = f32[4,1,1,1,1,2,16,128]{7,6,5,4,3,2,0,1:T(8,128)S(1)} collective-permute-done((f32[4,1,1,1,1,2,16,128]{7,6,5,4,3,2,0,1:T(8,128)S(1)}, f32[4,1,1,1,1,2,16,128]{7,6,5,4,3,2,0,1:T(8,128)S(1)}, u32[]{:S(2)}, u32[]{:S(2)}) %collective-permute-start.11) | collective-permute-done | bytes 65568 | tf_op jit(solution)/shard_map/ppermute | solution.py:98
  74.3 2.6 %collective-permute-start.14 = (f32[4,1,1,1,1,1,16,128]{7,6,5,4,3,2,0,1:T(8,128)S(1)}, f32[4,1,1,1,1,1,16,128]{7,6,5,4,3,2,0,1:T(8,128)S(1)}, u32[]{:S(2)}, u32[]{:S(2)}) collective-permute-start(f32[4,1,1,1,1,1,16,128]{7,6,5,4,3,2,0,1:T(8,128)S(1)} %constant_dynamic-slice_fusion.2), channel_id=1, source_target_pairs={{0,2},{1,3},{2,0},{3,1},{4,6},{5,7},{6,4},{7,5},{8,10},{9,11},{10,... | collective-permute-start | bytes 98312 | tf_op jit(solution)/shard_map/ppermute | solution.py:98
  78.8 2.1 %collective-permute-done.16 = f32[4,1,1,1,1,1,16,128]{7,6,5,4,3,2,0,1:T(8,128)S(1)} collective-permute-done((f32[4,1,1,1,1,1,16,128]{7,6,5,4,3,2,0,1:T(8,128)S(1)}, f32[4,1,1,1,1,1,16,128]{7,6,5,4,3,2,0,1:T(8,128)S(1)}, u32[]{:S(2)}, u32[]{:S(2)}) %collective-permute-start.16) | collective-permute-done | bytes 32800 | tf_op jit(solution)/shard_map/ppermute | solution.py:98
  81.6 1.8 %fusion.13 = bf16[12,16,128]{2,1,0:T(8,128)(2,1)S(1)} fusion(bf16[12,4,136,128]{3,2,1,0:T(8,128)(2,1)} %constant_dynamic-update-slice_fusion, bf16[12,4,16,128]{3,2,1,0:T(8,128)(2,1)S(1)} %bitcast.103, pred[12,4]{1,0:T(8,128)(4,1)S(1)} %copy.64), kind=kOutput, calls=%fused_computation.17 | convolution fusion | flops 25288704 | bytes 1818672 | tf_op jit(solution)/shard_map/nerc,necd->nrd/dot_general | solution.py:174
  84.1 1.6 %collective-permute-start.21 = (bf16[4,1,1,1,1,1,16,128]{7,6,0,5,4,3,2,1:T(8,128)(2,1)S(1)}, bf16[4,1,1,1,1,1,16,128]{7,6,0,5,4,3,2,1:T(8,128)(2,1)S(1)}, u32[]{:S(2)}, u32[]{:S(2)}) collective-permute-start(bf16[4,1,1,1,1,1,16,128]{7,6,0,5,4,3,2,1:T(8,128)(2,1)S(1)} %get-tuple-element.49), channel_id=1, source_target_pairs={{0,2},{1,3},{2,0},{3,1},{4,6},{5,7},{6,4},{7,5},{8,10},{9,11},{10,... | collective-permute-start | bytes 49160 | tf_op jit(solution)/shard_map/ppermute | solution.py:103
  87.2 1.6 %collective-permute-done.17 = bf16[4,1,1,1,1,1,16,128]{7,6,0,5,4,3,2,1:T(8,128)(2,1)S(1)} collective-permute-done((bf16[4,1,1,1,1,1,16,128]{7,6,0,5,4,3,2,1:T(8,128)(2,1)S(1)}, bf16[4,1,1,1,1,1,16,128]{7,6,0,5,4,3,2,1:T(8,128)(2,1)S(1)}, u32[]{:S(2)}, u32[]{:S(2)}) %collective-permute-start.17) | collective-permute-done | bytes 16416 | tf_op jit(solution)/shard_map/ppermute | solution.py:103
  88.9 2.0 %collective-permute-start.22 = (bf16[4,1,2,1,1,1,16,128]{7,6,0,5,4,3,2,1:T(8,128)(2,1)S(1)}, bf16[4,1,2,1,1,1,16,128]{7,6,0,5,4,3,2,1:T(8,128)(2,1)S(1)}, u32[]{:S(2)}, u32[]{:S(2)}) collective-permute-start(bf16[4,1,2,1,1,1,16,128]{7,6,0,5,4,3,2,1:T(8,128)(2,1)S(1)} %maximum_select_fusion.16), channel_id=1, source_target_pairs={{0,16},{4,20},{8,24},{12,28},{16,0},{20,4},{24,8},{28,12},{1,17},{... | collective-permute-start | bytes 98312 | tf_op jit(solution)/shard_map/ppermute | solution.py:103
  90.9 1.6 %collective-permute-start.26 = (bf16[4,1,1,2,1,1,16,128]{7,6,0,5,4,3,2,1:T(8,128)(2,1)S(1)}, bf16[4,1,1,2,1,1,16,128]{7,6,0,5,4,3,2,1:T(8,128)(2,1)S(1)}, u32[]{:S(2)}, u32[]{:S(2)}) collective-permute-start(bf16[4,1,1,2,1,1,16,128]{7,6,0,5,4,3,2,1:T(8,128)(2,1)S(1)} %maximum_select_fusion.18), channel_id=1, source_target_pairs={{0,2},{1,3},{2,0},{3,1},{4,6},{5,7},{6,4},{7,5},{8,10},{9,11},{10,... | collective-permute-start | bytes 98312 | tf_op jit(solution)/shard_map/ppermute | solution.py:103
  94.1 1.7 %collective-permute-start.23 = (bf16[4,1,2,1,1,2,16,128]{7,6,0,5,4,3,2,1:T(8,128)(2,1)S(1)}, bf16[4,1,2,1,1,2,16,128]{7,6,0,5,4,3,2,1:T(8,128)(2,1)S(1)}, u32[]{:S(2)}, u32[]{:S(2)}) collective-permute-start(bf16[4,1,2,1,1,2,16,128]{7,6,0,5,4,3,2,1:T(8,128)(2,1)S(1)} %maximum_select_fusion.11), channel_id=1, source_target_pairs={{0,8},{4,12},{8,0},{12,4},{16,24},{20,28},{24,16},{28,20},{1,9},{5... | collective-permute-start | bytes 196616 | tf_op jit(solution)/shard_map/ppermute | solution.py:103
  97.1 1.4 %collective-permute-start.20 = (bf16[4,1,1,2,2,2,16,128]{7,6,0,5,4,3,2,1:T(8,128)(2,1)S(1)}, bf16[4,1,1,2,2,2,16,128]{7,6,0,5,4,3,2,1:T(8,128)(2,1)S(1)}, u32[]{:S(2)}, u32[]{:S(2)}) collective-permute-start(bf16[4,1,1,2,2,2,16,128]{7,6,0,5,4,3,2,1:T(8,128)(2,1)S(1)} %maximum_select_fusion.5), channel_id=1, source_target_pairs={{0,2},{1,3},{2,0},{3,1},{4,6},{5,7},{6,4},{7,5},{8,10},{9,11},{10,... | collective-permute-start | bytes 393224 | tf_op jit(solution)/shard_map/ppermute | solution.py:103
  99.0 1.6 %collective-permute-start.24 = (bf16[4,1,2,1,2,2,16,128]{7,6,0,5,4,3,2,1:T(8,128)(2,1)S(1)}, bf16[4,1,2,1,2,2,16,128]{7,6,0,5,4,3,2,1:T(8,128)(2,1)S(1)}, u32[]{:S(2)}, u32[]{:S(2)}) collective-permute-start(bf16[4,1,2,1,2,2,16,128]{7,6,0,5,4,3,2,1:T(8,128)(2,1)S(1)} %maximum_select_fusion.6), channel_id=1, source_target_pairs={{0,4},{4,0},{8,12},{12,8},{16,20},{20,16},{24,28},{28,24},{1,5},{5... | collective-permute-start | bytes 393224 | tf_op jit(solution)/shard_map/ppermute | solution.py:103
  102.2 1.9 %collective-permute-done.24 = bf16[4,1,2,1,2,2,16,128]{7,6,0,5,4,3,2,1:T(8,128)(2,1)S(1)} collective-permute-done((bf16[4,1,2,1,2,2,16,128]{7,6,0,5,4,3,2,1:T(8,128)(2,1)S(1)}, bf16[4,1,2,1,2,2,16,128]{7,6,0,5,4,3,2,1:T(8,128)(2,1)S(1)}, u32[]{:S(2)}, u32[]{:S(2)}) %collective-permute-start.24) | collective-permute-done | bytes 131104 | tf_op jit(solution)/shard_map/ppermute | solution.py:103
  104.1 2.5 %collective-permute-done.28 = bf16[4,1,2,2,1,2,16,128]{7,6,0,5,4,3,2,1:T(8,128)(2,1)S(1)} collective-permute-done((bf16[4,1,2,2,1,2,16,128]{7,6,0,5,4,3,2,1:T(8,128)(2,1)S(1)}, bf16[4,1,2,2,1,2,16,128]{7,6,0,5,4,3,2,1:T(8,128)(2,1)S(1)}, u32[]{:S(2)}, u32[]{:S(2)}) %collective-permute-start.28) | collective-permute-done | bytes 131104 | tf_op jit(solution)/shard_map/ppermute | solution.py:103
  107.9 1.4 %collective-permute-done.29 = bf16[12,256,128]{2,1,0:T(8,128)(2,1)} collective-permute-done((bf16[12,256,128]{2,1,0:T(8,128)(2,1)S(1)}, bf16[12,256,128]{2,1,0:T(8,128)(2,1)}, u32[]{:S(2)}, u32[]{:S(2)}) %collective-permute-start.29) | collective-permute-done | bytes 786464 | tf_op jit(solution)/shard_map/ppermute | solution.py:183
  109.3 1.8 %gather_fusion.5 = bf16[8,256,128]{2,1,0:T(8,128)(2,1)S(1)} fusion(bf16[12,256,128]{2,1,0:T(8,128)(2,1)} %collective-permute-done.29, s32[1024]{0:T(1024)S(1)} %pad_clamp_fusion), kind=kCustom, calls=%fused_computation.1.clone | custom fusion | bytes 1048608 | tf_op jit(solution)/shard_map/jit(_take)/gather | solution.py:185
  (151 shorter events, 35.0 us)
Async XLA Ops:
  0.0 49.2 %copy-start = (bf16[4,4,256,256]{3,2,1,0:T(8,128)(2,1)S(1)}, bf16[4,4,256,256]{3,2,1,0:T(8,128)(2,1)}, u32[]{:S(2)}) copy-start(bf16[4,4,256,256]{3,2,1,0:T(8,128)(2,1)} %param.12) | copy-start | bytes 6291460
  2.7 13.3 %collective-permute-start.2 = (bf16[3,4,136,128]{3,2,1,0:T(8,128)(2,1)}, bf16[3,4,136,128]{3,2,1,0:T(8,128)(2,1)}, u32[]{:S(2)}, u32[]{:S(2)}) collective-permute-start(bf16[3,4,136,128]{3,2,1,0:T(8,128)(2,1)} %pad_maximum_fusion.3), channel_id=1, source_target_pairs={{0,2},{1,3},{2,0},{3,1},{4,6},{5,7},{6,4},{7,5},{8,10},{9,11},{10,... | collective-permute-start | bytes 1253384 | tf_op jit(solution)/shard_map/ppermute | solution.py:129
  7.6 4.2 %collective-permute-start = (bf16[1,512,256]{2,1,0:T(8,128)(2,1)}, bf16[1,512,256]{2,1,0:T(8,128)(2,1)S(1)}, u32[]{:S(2)}, u32[]{:S(2)}) collective-permute-start(bf16[1,512,256]{2,1,0:T(8,128)(2,1)} %get-tuple-element.45), channel_id=1, source_target_pairs={{0,1},{1,2},{2,3},{3,4},{4,5},{5,6},{6,7},{7,8},{8,9},{9,10},{10,1... | collective-permute-start | bytes 786440 | tf_op jit(solution)/shard_map/ppermute | solution.py:65
  9.1 3.8 %collective-permute-start.1 = (bf16[1,512,256]{2,1,0:T(8,128)(2,1)}, bf16[1,512,256]{2,1,0:T(8,128)(2,1)}, u32[]{:S(2)}, u32[]{:S(2)}) collective-permute-start(bf16[1,512,256]{2,1,0:T(8,128)(2,1)} %get-tuple-element.46), channel_id=1, source_target_pairs={{1,0},{2,1},{3,2},{4,3},{5,4},{6,5},{7,6},{8,7},{9,8},{10,9},{11,1... | collective-permute-start | bytes 786440 | tf_op jit(solution)/shard_map/ppermute | solution.py:67
  15.2 13.1 %copy-start.1 = (s32[4]{0:T(128)S(1)}, s32[4]{0:T(128)}, u32[]{:S(2)}) copy-start(s32[4]{0:T(128)} %constant.312.clone) | copy-start | bytes 52
  21.1 14.1 %collective-permute-start.3 = (f32[12,256,128]{2,1,0:T(8,128)}, f32[12,256,128]{2,1,0:T(8,128)}, u32[]{:S(2)}, u32[]{:S(2)}) collective-permute-start(f32[12,256,128]{2,1,0:T(8,128)} %shard_map.83), channel_id=1, source_target_pairs={{0,1},{1,0},{2,3},{3,2},{4,5},{5,4},{6,7},{7,6},{8,9},{9,8},{10,11... | collective-permute-start | bytes 4718600 | tf_op jit(solution)/shard_map/ppermute | solution.py:144
  38.2 15.9 %collective-permute-start.6 = (f32[4,1,2,2,1,2,16,128]{7,6,5,4,3,2,0,1:T(8,128)}, f32[4,1,2,2,1,2,16,128]{7,6,5,4,3,2,0,1:T(8,128)}, u32[]{:S(2)}, u32[]{:S(2)}) collective-permute-start(f32[4,1,2,2,1,2,16,128]{7,6,5,4,3,2,0,1:T(8,128)} %constant_dynamic-slice_fusion.9), channel_id=1, source_target_pairs={{0,8},{4,12},{8,0},{12,4},{16,24},{20,28},{24,16},{28,20},{1,9},{5... | collective-permute-start | bytes 786440 | tf_op jit(solution)/shard_map/ppermute | solution.py:98
  41.2 13.9 %collective-permute-start.5 = (f32[4,1,2,1,2,2,16,128]{7,6,5,4,3,2,0,1:T(8,128)}, f32[4,1,2,1,2,2,16,128]{7,6,5,4,3,2,0,1:T(8,128)}, u32[]{:S(2)}, u32[]{:S(2)}) collective-permute-start(f32[4,1,2,1,2,2,16,128]{7,6,5,4,3,2,0,1:T(8,128)} %constant_dynamic-slice_fusion.10), channel_id=1, source_target_pairs={{0,4},{4,0},{8,12},{12,8},{16,20},{20,16},{24,28},{28,24},{1,5},{5... | collective-permute-start | bytes 786440 | tf_op jit(solution)/shard_map/ppermute | solution.py:98
  43.4 12.7 %collective-permute-start.4 = (f32[4,1,1,2,2,2,16,128]{7,6,5,4,3,2,0,1:T(8,128)}, f32[4,1,1,2,2,2,16,128]{7,6,5,4,3,2,0,1:T(8,128)}, u32[]{:S(2)}, u32[]{:S(2)}) collective-permute-start(f32[4,1,1,2,2,2,16,128]{7,6,5,4,3,2,0,1:T(8,128)} %constant_dynamic-slice_fusion.11), channel_id=1, source_target_pairs={{0,2},{1,3},{2,0},{3,1},{4,6},{5,7},{6,4},{7,5},{8,10},{9,11},{10,... | collective-permute-start | bytes 786440 | tf_op jit(solution)/shard_map/ppermute | solution.py:98
  57.1 9.2 %collective-permute-start.10 = (f32[4,1,2,2,1,1,16,128]{7,6,5,4,3,2,0,1:T(8,128)S(1)}, f32[4,1,2,2,1,1,16,128]{7,6,5,4,3,2,0,1:T(8,128)S(1)}, u32[]{:S(2)}, u32[]{:S(2)}) collective-permute-start(f32[4,1,2,2,1,1,16,128]{7,6,5,4,3,2,0,1:T(8,128)S(1)} %constant_dynamic-slice_fusion.6), channel_id=1, source_target_pairs={{0,16},{4,20},{8,24},{12,28},{16,0},{20,4},{24,8},{28,12},{1,17},{... | collective-permute-start | bytes 393224 | tf_op jit(solution)/shard_map/ppermute | solution.py:98
  58.3 7.9 %collective-permute-start.9 = (f32[4,1,2,1,1,2,16,128]{7,6,5,4,3,2,0,1:T(8,128)S(1)}, f32[4,1,2,1,1,2,16,128]{7,6,5,4,3,2,0,1:T(8,128)S(1)}, u32[]{:S(2)}, u32[]{:S(2)}) collective-permute-start(f32[4,1,2,1,1,2,16,128]{7,6,5,4,3,2,0,1:T(8,128)S(1)} %constant_dynamic-slice_fusion.7), channel_id=1, source_target_pairs={{0,8},{4,12},{8,0},{12,4},{16,24},{20,28},{24,16},{28,20},{1,9},{5... | collective-permute-start | bytes 393224 | tf_op jit(solution)/shard_map/ppermute | solution.py:98
  60.3 6.1 %collective-permute-start.7 = (bf16[6,4,136,128]{3,2,1,0:T(8,128)(2,1)S(1)}, bf16[6,4,136,128]{3,2,1,0:T(8,128)(2,1)S(1)}, u32[]{:S(2)}, u32[]{:S(2)}) collective-permute-start(bf16[6,4,136,128]{3,2,1,0:T(8,128)(2,1)S(1)} %pad_maximum_fusion.1), channel_id=1, source_target_pairs={{0,1},{1,0},{2,3},{3,2},{4,5},{5,4},{6,7},{7,6},{8,9},{9,8},{10,11... | collective-permute-start | bytes 2506760 | tf_op jit(solution)/shard_map/ppermute | solution.py:163
  60.3 6.0 %collective-permute-start.8 = (f32[4,1,1,1,2,2,16,128]{7,6,5,4,3,2,0,1:T(8,128)S(1)}, f32[4,1,1,1,2,2,16,128]{7,6,5,4,3,2,0,1:T(8,128)S(1)}, u32[]{:S(2)}, u32[]{:S(2)}) collective-permute-start(f32[4,1,1,1,2,2,16,128]{7,6,5,4,3,2,0,1:T(8,128)S(1)} %constant_dynamic-slice_fusion.8), channel_id=1, source_target_pairs={{0,4},{4,0},{8,12},{12,8},{16,20},{20,16},{24,28},{28,24},{1,5},{5... | collective-permute-start | bytes 393224 | tf_op jit(solution)/shard_map/ppermute | solution.py:98
  68.4 5.0 %collective-permute-start.11 = (f32[4,1,1,1,1,2,16,128]{7,6,5,4,3,2,0,1:T(8,128)S(1)}, f32[4,1,1,1,1,2,16,128]{7,6,5,4,3,2,0,1:T(8,128)S(1)}, u32[]{:S(2)}, u32[]{:S(2)}) collective-permute-start(f32[4,1,1,1,1,2,16,128]{7,6,5,4,3,2,0,1:T(8,128)S(1)} %constant_dynamic-slice_fusion.5), channel_id=1, source_target_pairs={{0,8},{4,12},{8,0},{12,4},{16,24},{20,28},{24,16},{28,20},{1,9},{5... | collective-permute-start | bytes 196616 | tf_op jit(solution)/shard_map/ppermute | solution.py:98
  68.9 5.4 %collective-permute-start.13 = (f32[4,1,2,1,1,1,16,128]{7,6,5,4,3,2,0,1:T(8,128)S(1)}, f32[4,1,2,1,1,1,16,128]{7,6,5,4,3,2,0,1:T(8,128)S(1)}, u32[]{:S(2)}, u32[]{:S(2)}) collective-permute-start(f32[4,1,2,1,1,1,16,128]{7,6,5,4,3,2,0,1:T(8,128)S(1)} %constant_dynamic-slice_fusion.3), channel_id=1, source_target_pairs={{0,16},{4,20},{8,24},{12,28},{16,0},{20,4},{24,8},{28,12},{1,17},{... | collective-permute-start | bytes 196616 | tf_op jit(solution)/shard_map/ppermute | solution.py:98
  71.0 5.9 %collective-permute-start.15 = (f32[4,1,1,2,1,1,16,128]{7,6,5,4,3,2,0,1:T(8,128)S(1)}, f32[4,1,1,2,1,1,16,128]{7,6,5,4,3,2,0,1:T(8,128)S(1)}, u32[]{:S(2)}, u32[]{:S(2)}) collective-permute-start(f32[4,1,1,2,1,1,16,128]{7,6,5,4,3,2,0,1:T(8,128)S(1)} %constant_dynamic-slice_fusion.1), channel_id=1, source_target_pairs={{0,2},{1,3},{2,0},{3,1},{4,6},{5,7},{6,4},{7,5},{8,10},{9,11},{10,... | collective-permute-start | bytes 196616 | tf_op jit(solution)/shard_map/ppermute | solution.py:98
  73.5 4.9 %collective-permute-start.12 = (f32[4,1,1,1,1,1,16,128]{7,6,5,4,3,2,0,1:T(8,128)S(1)}, f32[4,1,1,1,1,1,16,128]{7,6,5,4,3,2,0,1:T(8,128)S(1)}, u32[]{:S(2)}, u32[]{:S(2)}) collective-permute-start(f32[4,1,1,1,1,1,16,128]{7,6,5,4,3,2,0,1:T(8,128)S(1)} %constant_dynamic-slice_fusion.4), channel_id=1, source_target_pairs={{0,16},{4,20},{8,24},{12,28},{16,0},{20,4},{24,8},{28,12},{1,17},{... | collective-permute-start | bytes 98312 | tf_op jit(solution)/shard_map/ppermute | solution.py:98
  74.3 4.5 %collective-permute-start.14 = (f32[4,1,1,1,1,1,16,128]{7,6,5,4,3,2,0,1:T(8,128)S(1)}, f32[4,1,1,1,1,1,16,128]{7,6,5,4,3,2,0,1:T(8,128)S(1)}, u32[]{:S(2)}, u32[]{:S(2)}) collective-permute-start(f32[4,1,1,1,1,1,16,128]{7,6,5,4,3,2,0,1:T(8,128)S(1)} %constant_dynamic-slice_fusion.2), channel_id=1, source_target_pairs={{0,2},{1,3},{2,0},{3,1},{4,6},{5,7},{6,4},{7,5},{8,10},{9,11},{10,... | collective-permute-start | bytes 98312 | tf_op jit(solution)/shard_map/ppermute | solution.py:98
  76.9 4.0 %collective-permute-start.16 = (f32[4,1,1,1,1,1,16,128]{7,6,5,4,3,2,0,1:T(8,128)S(1)}, f32[4,1,1,1,1,1,16,128]{7,6,5,4,3,2,0,1:T(8,128)S(1)}, u32[]{:S(2)}, u32[]{:S(2)}) collective-permute-start(f32[4,1,1,1,1,1,16,128]{7,6,5,4,3,2,0,1:T(8,128)S(1)} %constant_dynamic-slice_fusion), channel_id=1, source_target_pairs={{0,4},{4,0},{8,12},{12,8},{16,20},{20,16},{24,28},{28,24},{1,5},{5... | collective-permute-start | bytes 98312 | tf_op jit(solution)/shard_map/ppermute | solution.py:98
  84.0 4.7 %collective-permute-start.17 = (bf16[4,1,1,1,1,1,16,128]{7,6,0,5,4,3,2,1:T(8,128)(2,1)S(1)}, bf16[4,1,1,1,1,1,16,128]{7,6,0,5,4,3,2,1:T(8,128)(2,1)S(1)}, u32[]{:S(2)}, u32[]{:S(2)}) collective-permute-start(bf16[4,1,1,1,1,1,16,128]{7,6,0,5,4,3,2,1:T(8,128)(2,1)S(1)} %get-tuple-element.48), channel_id=1, source_target_pairs={{0,16},{4,20},{8,24},{12,28},{16,0},{20,4},{24,8},{28,12},{1,17},{... | collective-permute-start | bytes 49160 | tf_op jit(solution)/shard_map/ppermute | solution.py:103
  84.1 4.7 %collective-permute-start.21 = (bf16[4,1,1,1,1,1,16,128]{7,6,0,5,4,3,2,1:T(8,128)(2,1)S(1)}, bf16[4,1,1,1,1,1,16,128]{7,6,0,5,4,3,2,1:T(8,128)(2,1)S(1)}, u32[]{:S(2)}, u32[]{:S(2)}) collective-permute-start(bf16[4,1,1,1,1,1,16,128]{7,6,0,5,4,3,2,1:T(8,128)(2,1)S(1)} %get-tuple-element.49), channel_id=1, source_target_pairs={{0,2},{1,3},{2,0},{3,1},{4,6},{5,7},{6,4},{7,5},{8,10},{9,11},{10,... | collective-permute-start | bytes 49160 | tf_op jit(solution)/shard_map/ppermute | solution.py:103
  85.8 5.1 %collective-permute-start.25 = (bf16[4,1,1,1,1,1,16,128]{7,6,0,5,4,3,2,1:T(8,128)(2,1)S(1)}, bf16[4,1,1,1,1,1,16,128]{7,6,0,5,4,3,2,1:T(8,128)(2,1)S(1)}, u32[]{:S(2)}, u32[]{:S(2)}) collective-permute-start(bf16[4,1,1,1,1,1,16,128]{7,6,0,5,4,3,2,1:T(8,128)(2,1)S(1)} %get-tuple-element.50), channel_id=1, source_target_pairs={{0,4},{4,0},{8,12},{12,8},{16,20},{20,16},{24,28},{28,24},{1,5},{5... | collective-permute-start | bytes 49160 | tf_op jit(solution)/shard_map/ppermute | solution.py:103
  88.8 4.0 %collective-permute-start.18 = (bf16[4,1,1,1,1,2,16,128]{7,6,0,5,4,3,2,1:T(8,128)(2,1)S(1)}, bf16[4,1,1,1,1,2,16,128]{7,6,0,5,4,3,2,1:T(8,128)(2,1)S(1)}, u32[]{:S(2)}, u32[]{:S(2)}) collective-permute-start(bf16[4,1,1,1,1,2,16,128]{7,6,0,5,4,3,2,1:T(8,128)(2,1)S(1)} %maximum_select_fusion.14), channel_id=1, source_target_pairs={{0,8},{4,12},{8,0},{12,4},{16,24},{20,28},{24,16},{28,20},{1,9},{5... | collective-permute-start | bytes 98312 | tf_op jit(solution)/shard_map/ppermute | solution.py:103
  88.9 5.2 %collective-permute-start.22 = (bf16[4,1,2,1,1,1,16,128]{7,6,0,5,4,3,2,1:T(8,128)(2,1)S(1)}, bf16[4,1,2,1,1,1,16,128]{7,6,0,5,4,3,2,1:T(8,128)(2,1)S(1)}, u32[]{:S(2)}, u32[]{:S(2)}) collective-permute-start(bf16[4,1,2,1,1,1,16,128]{7,6,0,5,4,3,2,1:T(8,128)(2,1)S(1)} %maximum_select_fusion.16), channel_id=1, source_target_pairs={{0,16},{4,20},{8,24},{12,28},{16,0},{20,4},{24,8},{28,12},{1,17},{... | collective-permute-start | bytes 98312 | tf_op jit(solution)/shard_map/ppermute | solution.py:103
  90.9 5.0 %collective-permute-start.26 = (bf16[4,1,1,2,1,1,16,128]{7,6,0,5,4,3,2,1:T(8,128)(2,1)S(1)}, bf16[4,1,1,2,1,1,16,128]{7,6,0,5,4,3,2,1:T(8,128)(2,1)S(1)}, u32[]{:S(2)}, u32[]{:S(2)}) collective-permute-start(bf16[4,1,1,2,1,1,16,128]{7,6,0,5,4,3,2,1:T(8,128)(2,1)S(1)} %maximum_select_fusion.18), channel_id=1, source_target_pairs={{0,2},{1,3},{2,0},{3,1},{4,6},{5,7},{6,4},{7,5},{8,10},{9,11},{10,... | collective-permute-start | bytes 98312 | tf_op jit(solution)/shard_map/ppermute | solution.py:103
  92.8 4.3 %collective-permute-start.19 = (bf16[4,1,1,1,2,2,16,128]{7,6,0,5,4,3,2,1:T(8,128)(2,1)S(1)}, bf16[4,1,1,1,2,2,16,128]{7,6,0,5,4,3,2,1:T(8,128)(2,1)S(1)}, u32[]{:S(2)}, u32[]{:S(2)}) collective-permute-start(bf16[4,1,1,1,2,2,16,128]{7,6,0,5,4,3,2,1:T(8,128)(2,1)S(1)} %maximum_select_fusion.9), channel_id=1, source_target_pairs={{0,4},{4,0},{8,12},{12,8},{16,20},{20,16},{24,28},{28,24},{1,5},{5... | collective-permute-start | bytes 196616 | tf_op jit(solution)/shard_map/ppermute | solution.py:103
  94.1 4.9 %collective-permute-start.23 = (bf16[4,1,2,1,1,2,16,128]{7,6,0,5,4,3,2,1:T(8,128)(2,1)S(1)}, bf16[4,1,2,1,1,2,16,128]{7,6,0,5,4,3,2,1:T(8,128)(2,1)S(1)}, u32[]{:S(2)}, u32[]{:S(2)}) collective-permute-start(bf16[4,1,2,1,1,2,16,128]{7,6,0,5,4,3,2,1:T(8,128)(2,1)S(1)} %maximum_select_fusion.11), channel_id=1, source_target_pairs={{0,8},{4,12},{8,0},{12,4},{16,24},{20,28},{24,16},{28,20},{1,9},{5... | collective-permute-start | bytes 196616 | tf_op jit(solution)/shard_map/ppermute | solution.py:103
  95.9 5.8 %collective-permute-start.27 = (bf16[4,1,2,2,1,1,16,128]{7,6,0,5,4,3,2,1:T(8,128)(2,1)S(1)}, bf16[4,1,2,2,1,1,16,128]{7,6,0,5,4,3,2,1:T(8,128)(2,1)S(1)}, u32[]{:S(2)}, u32[]{:S(2)}) collective-permute-start(bf16[4,1,2,2,1,1,16,128]{7,6,0,5,4,3,2,1:T(8,128)(2,1)S(1)} %fusion.29), channel_id=1, source_target_pairs={{0,16},{4,20},{8,24},{12,28},{16,0},{20,4},{24,8},{28,12},{1,17},{... | collective-permute-start | bytes 196616 | tf_op jit(solution)/shard_map/ppermute | solution.py:103
  97.1 5.0 %collective-permute-start.20 = (bf16[4,1,1,2,2,2,16,128]{7,6,0,5,4,3,2,1:T(8,128)(2,1)S(1)}, bf16[4,1,1,2,2,2,16,128]{7,6,0,5,4,3,2,1:T(8,128)(2,1)S(1)}, u32[]{:S(2)}, u32[]{:S(2)}) collective-permute-start(bf16[4,1,1,2,2,2,16,128]{7,6,0,5,4,3,2,1:T(8,128)(2,1)S(1)} %maximum_select_fusion.5), channel_id=1, source_target_pairs={{0,2},{1,3},{2,0},{3,1},{4,6},{5,7},{6,4},{7,5},{8,10},{9,11},{10,... | collective-permute-start | bytes 393224 | tf_op jit(solution)/shard_map/ppermute | solution.py:103
  99.0 5.0 %collective-permute-start.24 = (bf16[4,1,2,1,2,2,16,128]{7,6,0,5,4,3,2,1:T(8,128)(2,1)S(1)}, bf16[4,1,2,1,2,2,16,128]{7,6,0,5,4,3,2,1:T(8,128)(2,1)S(1)}, u32[]{:S(2)}, u32[]{:S(2)}) collective-permute-start(bf16[4,1,2,1,2,2,16,128]{7,6,0,5,4,3,2,1:T(8,128)(2,1)S(1)} %maximum_select_fusion.6), channel_id=1, source_target_pairs={{0,4},{4,0},{8,12},{12,8},{16,20},{20,16},{24,28},{28,24},{1,5},{5... | collective-permute-start | bytes 393224 | tf_op jit(solution)/shard_map/ppermute | solution.py:103
  101.6 5.0 %collective-permute-start.28 = (bf16[4,1,2,2,1,2,16,128]{7,6,0,5,4,3,2,1:T(8,128)(2,1)S(1)}, bf16[4,1,2,2,1,2,16,128]{7,6,0,5,4,3,2,1:T(8,128)(2,1)S(1)}, u32[]{:S(2)}, u32[]{:S(2)}) collective-permute-start(bf16[4,1,2,2,1,2,16,128]{7,6,0,5,4,3,2,1:T(8,128)(2,1)S(1)} %maximum_select_fusion.7), channel_id=1, source_target_pairs={{0,8},{4,12},{8,0},{12,4},{16,24},{20,28},{24,16},{28,20},{1,9},{5... | collective-permute-start | bytes 393224 | tf_op jit(solution)/shard_map/ppermute | solution.py:103
  106.8 2.5 %collective-permute-start.29 = (bf16[12,256,128]{2,1,0:T(8,128)(2,1)S(1)}, bf16[12,256,128]{2,1,0:T(8,128)(2,1)}, u32[]{:S(2)}, u32[]{:S(2)}) collective-permute-start(bf16[12,256,128]{2,1,0:T(8,128)(2,1)S(1)} %pad_maximum_fusion.2), channel_id=1, source_target_pairs={{0,1},{1,0},{2,3},{3,2},{4,5},{5,4},{6,7},{7,6},{8,9},{9,8},{10,11... | collective-permute-start | bytes 2359304 | tf_op jit(solution)/shard_map/ppermute | solution.py:183
  (11 other events, 65.4 us)

commit v18 on v16

--- a/solution.py
+++ b/solution.py
@@ -175,10 +175,9 @@
     ).astype(jnp.bfloat16)
     solved = jnp.take(solved, order, axis=0)
     solved = solved.reshape((total_blocks,) + (1,) * nb + (inner, width))
-    outs = [lax.slice_in_dim(solved, s * per, (s + 1) * per, axis=0) for s in range(streams)]
     for step in reversed(range(1, nb)):
-        outs = [double(y, 1 + orders[s][step], *bits[orders[s][step]]) for s, y in enumerate(outs)]
-    own = jnp.concatenate(outs, axis=0).reshape(total_blocks, rhs // 2, width)
+        solved = double(solved, 1 + orders[0][step], *bits[orders[0][step]])
+    own = solved.reshape(total_blocks, rhs // 2, width)
     got = lax.ppermute(own, bits[0][0], pairs(*bits[0]))
     own_rows = jnp.take(own, interface, axis=0)
     got_rows = jnp.take(got, interface, axis=0)

time: 109 us -> 111 us (1.018)
  starting transfers between devices: 37.1 us -> 24.3 us
  waiting for transfers between devices: 21.3 us -> 34 us
  local copies, waits for them, and re-layouts: 19.5 us -> 21.2 us
    ppermute x12 -> x4, waiting for transfers between devices: 8.47 us -> 20.6 us  [double(): recv = lax.ppermute(y, axis, pairs(axis, mask))]
    ppermute x12 -> x4, starting transfers between devices: 13.9 us -> 2.51 us  [double(): recv = lax.ppermute(y, axis, pairs(axis, mask))]
    ppermute x12, starting transfers between devices: 14.6 us -> 13.2 us  [halve(): lax.ppermute(send.astype(wire), axis, pairs(axis, mask)).astype(x.dtype)]
    unnamed x37 -> x35, local copies, waits for them, and re-layouts: 5.71 us -> 5.43 us
  transfers between devices with their start and end apart: 30 -> 22, of which waited for: 13 -> 12; matrix products, arithmetic and copies ran while one was open for 22% -> 23% of each run, Pallas kernels for 5% -> 5%
where the time goes in v18:
time: 111 us; the launch traced here: 110 us
  waiting for transfers between devices  34 us (31%)
  starting transfers between devices  24.3 us (22%)
  local copies, waits for them, and re-layouts  21.2 us (19%)
  other arithmetic  12.8 us (12%)
  Pallas kernels  10.2 us (9%)
  matrix products  7.17 us (6%)
    ppermute x4, waiting for transfers between devices, double(): recv = lax.ppermute(y, axis, pairs(axis, mask))  20.6 us
    ppermute x12, starting transfers between devices, halve(): lax.ppermute(send.astype(wire), axis, pairs(axis, mask)).astype(x.dtype)  13.2 us
    ppermute x12, waiting for transfers between devices, halve(): lax.ppermute(send.astype(wire), axis, pairs(axis, mask)).astype(x.dtype)  11.9 us
    pallas_call x2, Pallas kernels, restrict(): pl.pallas_call(functools.partial(restrict_kernel, upper=upper), out_shape...  10.2 us
    unnamed x35, local copies, waits for them, and re-layouts  5.43 us
    dot_general x1, matrix products, per_device(): jnp.einsum('jerb,jebc->jrc', picked, inverse_blocks, preferred_element_ty...  4.92 us
    gather x1, local copies, waits for them, and re-layouts, per_device(): picked = jnp.take(extended, margin, axis=0)  4.21 us
    ppermute x1, starting transfers between devices, per_device(): arriving = lax.ppermute(packed, exchanges[0][0], pairs(*exchanges[0]))  4.15 us
  transfers between devices with their start and end apart: 22, of which 12 were waited for; matrix products, arithmetic and copies ran while one was open for 23% of the time, Pallas kernels for 5%

profile of v18, /device:TPU:0, one launch (start us, length us, event | category | flops | bytes accessed | tf_op | source)
XLA Modules:
  0.0 110.2 jit_solution(6152542305080529423)
XLA Ops:
  1.6 5.2 %shard_map.83 = f32[12,256,128]{2,1,0:T(8,128)} custom-call(s32[8]{0:T(128)} %reshape.688.links, s32[1]{0:T(128)} %bitcast.half, bf16[4,512,256]{2,1,0:T(8,128)(2,1)} %residual_ref.3, bf16[4,2,256,128]{3,2,1,0:T(8,128)(2,1)} %basis_ref.3), custom_call_target="tpu_custom_call" | custom-call | flops 134217728 | bytes 3145728 | tf_op jit(solution)/shard_map/pallas_call | solution.py:36
  8.1 2.6 %collective-permute-start = (bf16[1,512,256]{2,1,0:T(8,128)(2,1)}, bf16[1,512,256]{2,1,0:T(8,128)(2,1)}, u32[]{:S(2)}, u32[]{:S(2)}) collective-permute-start(bf16[1,512,256]{2,1,0:T(8,128)(2,1)} %get-tuple-element.41), channel_id=1, source_target_pairs={{0,1},{1,2},{2,3},{3,4},{4,5},{5,6},{6,7},{7,8},{8,9},{9,10},{10,1... | collective-permute-start | bytes 786440 | tf_op jit(solution)/shard_map/ppermute | solution.py:65
  10.7 1.3 %collective-permute-start.1 = (bf16[1,512,256]{2,1,0:T(8,128)(2,1)}, bf16[1,512,256]{2,1,0:T(8,128)(2,1)}, u32[]{:S(2)}, u32[]{:S(2)}) collective-permute-start(bf16[1,512,256]{2,1,0:T(8,128)(2,1)} %get-tuple-element.42), channel_id=1, source_target_pairs={{1,0},{2,1},{3,2},{4,3},{5,4},{6,5},{7,6},{8,7},{9,8},{10,9},{11,1... | collective-permute-start | bytes 786440 | tf_op jit(solution)/shard_map/ppermute | solution.py:67
  13.5 4.1 %collective-permute-start.3 = (bf16[3,4,136,128]{3,2,1,0:T(8,128)(2,1)}, bf16[3,4,136,128]{3,2,1,0:T(8,128)(2,1)}, u32[]{:S(2)}, u32[]{:S(2)}) collective-permute-start(bf16[3,4,136,128]{3,2,1,0:T(8,128)(2,1)} %pad_maximum_fusion.2), channel_id=1, source_target_pairs={{0,2},{1,3},{2,0},{3,1},{4,6},{5,7},{6,4},{7,5},{8,10},{9,11},{10,... | collective-permute-start | bytes 1253384 | tf_op jit(solution)/shard_map/ppermute | solution.py:142
  17.8 1.2 %gather_fusion.1 = s32[12]{0:T(128)} fusion(s32[4]{0:T(128)S(1)} %copy-done.1, s32[1024]{0:T(1024)S(1)} %pad_clamp_fusion.3), kind=kCustom, calls=%fused_computation.3 | custom fusion | bytes 144 | tf_op jit(solution)/shard_map/gather | solution.py:167
  20.5 5.0 %shard_map.82 = f32[12,256,128]{2,1,0:T(8,128)} custom-call(s32[8]{0:T(128)} %reshape.688.links, s32[1]{0:T(128)} %bitcast.half, bf16[4,512,256]{2,1,0:T(8,128)(2,1)} %residual_ref.3, bf16[4,2,256,128]{3,2,1,0:T(8,128)(2,1)} %basis_ref.3), custom_call_target="tpu_custom_call" | custom-call | flops 134217728 | bytes 3145728 | tf_op jit(solution)/shard_map/pallas_call | solution.py:36
  26.2 2.4 %pad_maximum_fusion = bf16[6,512,256]{2,1,0:T(8,128)(2,1)} fusion(bf16[1,512,256]{2,1,0:T(8,128)(2,1)} %collective-permute-done.1, bf16[4,512,256]{2,1,0:T(8,128)(2,1)S(1)} %copy-done.3, bf16[1,512,256]{2,1,0:T(8,128)(2,1)} %collective-permute-done), kind=kLoop, calls=%fused_computation.15 | loop fusion | flops 1572864 | bytes 3145728 | tf_op jit(solution)/shard_map/concatenate | solution.py:63
  28.6 1.6 %add.225 = f32[12,256,128]{2,1,0:T(8,128)S(1)} add(f32[12,256,128]{2,1,0:T(8,128)S(1)} %copy-done.4, f32[12,256,128]{2,1,0:T(8,128)} %collective-permute-done.2) | non-fusion elementwise | flops 393216 | bytes 4718592 | tf_op jit(solution)/shard_map/add | solution.py:138
  31.8 2.0 %collective-permute-start.6 = (f32[4,1,2,2,1,2,16,128]{7,6,5,4,3,2,0,1:T(8,128)}, f32[4,1,2,2,1,2,16,128]{7,6,5,4,3,2,0,1:T(8,128)}, u32[]{:S(2)}, u32[]{:S(2)}) collective-permute-start(f32[4,1,2,2,1,2,16,128]{7,6,5,4,3,2,0,1:T(8,128)} %constant_dynamic-slice_fusion.9), channel_id=1, source_target_pairs={{0,8},{4,12},{8,0},{12,4},{16,24},{20,28},{24,16},{28,20},{1,9},{5... | collective-permute-start | bytes 786440 | tf_op jit(solution)/shard_map/ppermute | solution.py:98
  34.5 1.1 collective-permute-start.5
  36.4 2.0 %collective-permute-start.4 = (f32[4,1,1,2,2,2,16,128]{7,6,5,4,3,2,0,1:T(8,128)}, f32[4,1,1,2,2,2,16,128]{7,6,5,4,3,2,0,1:T(8,128)}, u32[]{:S(2)}, u32[]{:S(2)}) collective-permute-start(f32[4,1,1,2,2,2,16,128]{7,6,5,4,3,2,0,1:T(8,128)} %constant_dynamic-slice_fusion.11), channel_id=1, source_target_pairs={{0,2},{1,3},{2,0},{3,1},{4,6},{5,7},{6,4},{7,5},{8,10},{9,11},{10,... | collective-permute-start | bytes 786440 | tf_op jit(solution)/shard_map/ppermute | solution.py:98
  38.4 4.2 %gather_fusion = bf16[16,512,256]{2,1,0:T(8,128)(2,1)} fusion(bf16[6,512,256]{2,1,0:T(8,128)(2,1)} %pad_maximum_fusion, s32[1024]{0:T(1024)S(1)} %pad_clamp_fusion.4), kind=kCustom, calls=%fused_computation.2 | custom fusion | bytes 8388672 | tf_op jit(solution)/shard_map/jit(_take)/gather | solution.py:148
  42.6 4.9 %fusion.5 = f32[4,512,256]{2,1,0:T(8,128)} fusion(bf16[4,4,256,256]{3,2,1,0:T(8,128)(2,1)S(1)} %copy-done, bf16[4,4,512,256]{3,2,1,0:T(8,128)(2,1)} %bitcast.63, pred[4,4]{1,0:T(4,128)(4,1)S(1)} %copy-done.15), kind=kOutput, calls=%fused_computation.12 | convolution fusion | flops 1075838976 | bytes 8388624 | tf_op jit(solution)/shard_map/jerb,jebc->jrc/dot_general | solution.py:149
  47.5 1.1 pad_maximum_fusion.1
  51.6 2.0 %collective-permute-start.10 = (f32[4,1,2,2,1,1,16,128]{7,6,5,4,3,2,0,1:T(8,128)S(1)}, f32[4,1,2,2,1,1,16,128]{7,6,5,4,3,2,0,1:T(8,128)S(1)}, u32[]{:S(2)}, u32[]{:S(2)}) collective-permute-start(f32[4,1,2,2,1,1,16,128]{7,6,5,4,3,2,0,1:T(8,128)S(1)} %constant_dynamic-slice_fusion.6), channel_id=1, source_target_pairs={{0,16},{4,20},{8,24},{12,28},{16,0},{20,4},{24,8},{28,12},{1,17},{... | collective-permute-start | bytes 393224 | tf_op jit(solution)/shard_map/ppermute | solution.py:98
  53.7 1.1 %collective-permute-start.9 = (f32[4,1,2,1,1,2,16,128]{7,6,5,4,3,2,0,1:T(8,128)S(1)}, f32[4,1,2,1,1,2,16,128]{7,6,5,4,3,2,0,1:T(8,128)S(1)}, u32[]{:S(2)}, u32[]{:S(2)}) collective-permute-start(f32[4,1,2,1,1,2,16,128]{7,6,5,4,3,2,0,1:T(8,128)S(1)} %constant_dynamic-slice_fusion.7), channel_id=1, source_target_pairs={{0,8},{4,12},{8,0},{12,4},{16,24},{20,28},{24,16},{28,20},{1,9},{5... | collective-permute-start | bytes 393224 | tf_op jit(solution)/shard_map/ppermute | solution.py:98
  56.7 3.4 %collective-permute-done.9 = f32[4,1,2,1,1,2,16,128]{7,6,5,4,3,2,0,1:T(8,128)S(1)} collective-permute-done((f32[4,1,2,1,1,2,16,128]{7,6,5,4,3,2,0,1:T(8,128)S(1)}, f32[4,1,2,1,1,2,16,128]{7,6,5,4,3,2,0,1:T(8,128)S(1)}, u32[]{:S(2)}, u32[]{:S(2)}) %collective-permute-start.9) | collective-permute-done | bytes 131104 | tf_op jit(solution)/shard_map/ppermute | solution.py:98
  65.2 2.7 %collective-permute-done.11 = f32[4,1,1,1,1,2,16,128]{7,6,5,4,3,2,0,1:T(8,128)S(1)} collective-permute-done((f32[4,1,1,1,1,2,16,128]{7,6,5,4,3,2,0,1:T(8,128)S(1)}, f32[4,1,1,1,1,2,16,128]{7,6,5,4,3,2,0,1:T(8,128)S(1)}, u32[]{:S(2)}, u32[]{:S(2)}) %collective-permute-start.11) | collective-permute-done | bytes 65568 | tf_op jit(solution)/shard_map/ppermute | solution.py:98
  68.0 2.3 %collective-permute-done.13 = f32[4,1,2,1,1,1,16,128]{7,6,5,4,3,2,0,1:T(8,128)S(1)} collective-permute-done((f32[4,1,2,1,1,1,16,128]{7,6,5,4,3,2,0,1:T(8,128)S(1)}, f32[4,1,2,1,1,1,16,128]{7,6,5,4,3,2,0,1:T(8,128)S(1)}, u32[]{:S(2)}, u32[]{:S(2)}) %collective-permute-start.13) | collective-permute-done | bytes 65568 | tf_op jit(solution)/shard_map/ppermute | solution.py:98
  71.3 1.1 collective-permute-start.16
  73.1 1.2 %collective-permute-done.14 = f32[4,1,1,1,1,1,16,128]{7,6,5,4,3,2,0,1:T(8,128)S(1)} collective-permute-done((f32[4,1,1,1,1,1,16,128]{7,6,5,4,3,2,0,1:T(8,128)S(1)}, f32[4,1,1,1,1,1,16,128]{7,6,5,4,3,2,0,1:T(8,128)S(1)}, u32[]{:S(2)}, u32[]{:S(2)}) %collective-permute-start.14) | collective-permute-done | bytes 32800 | tf_op jit(solution)/shard_map/ppermute | solution.py:98
  75.9 1.8 %fusion.13 = bf16[12,16,128]{2,1,0:T(8,128)(2,1)S(1)} fusion(bf16[12,4,136,128]{3,2,1,0:T(8,128)(2,1)} %constant_dynamic-update-slice_fusion, bf16[12,4,16,128]{3,2,1,0:T(8,128)(2,1)S(1)} %bitcast.69, pred[12,4]{1,0:T(8,128)(4,1)S(1)} %copy.42), kind=kOutput, calls=%fused_computation.17 | convolution fusion | flops 25288704 | bytes 1818672 | tf_op jit(solution)/shard_map/nerc,necd->nrd/dot_general | solution.py:173
  78.5 4.9 %collective-permute-done.17 = bf16[12,1,1,1,1,1,16,128]{7,6,0,5,4,3,2,1:T(8,128)(2,1)S(1)} collective-permute-done((bf16[12,1,1,1,1,1,16,128]{7,6,0,5,4,3,2,1:T(8,128)(2,1)S(1)}, bf16[12,1,1,1,1,1,16,128]{7,6,0,5,4,3,2,1:T(8,128)(2,1)S(1)}, u32[]{:S(2)}, u32[]{:S(2)}) %collective-permute-start.17) | collective-permute-done | bytes 49184 | tf_op jit(solution)/shard_map/ppermute | solution.py:103
  83.5 4.6 %collective-permute-done.18 = bf16[12,1,1,1,1,2,16,128]{7,6,0,5,4,3,2,1:T(8,128)(2,1)S(1)} collective-permute-done((bf16[12,1,1,1,1,2,16,128]{7,6,0,5,4,3,2,1:T(8,128)(2,1)S(1)}, bf16[12,1,1,1,1,2,16,128]{7,6,0,5,4,3,2,1:T(8,128)(2,1)S(1)}, u32[]{:S(2)}, u32[]{:S(2)}) %collective-permute-start.18) | collective-permute-done | bytes 98336 | tf_op jit(solution)/shard_map/ppermute | solution.py:103
  88.1 1.1 collective-permute-start.19
  89.2 4.6 %collective-permute-done.19 = bf16[12,1,1,1,2,2,16,128]{7,6,0,5,4,3,2,1:T(8,128)(2,1)S(1)} collective-permute-done((bf16[12,1,1,1,2,2,16,128]{7,6,0,5,4,3,2,1:T(8,128)(2,1)S(1)}, bf16[12,1,1,1,2,2,16,128]{7,6,0,5,4,3,2,1:T(8,128)(2,1)S(1)}, u32[]{:S(2)}, u32[]{:S(2)}) %collective-permute-start.19) | collective-permute-done | bytes 196640 | tf_op jit(solution)/shard_map/ppermute | solution.py:103
  93.9 1.3 %collective-permute-start.20 = (bf16[12,1,1,2,2,2,16,128]{7,6,0,5,4,3,2,1:T(8,128)(2,1)S(1)}, bf16[12,1,1,2,2,2,16,128]{7,6,0,5,4,3,2,1:T(8,128)(2,1)S(1)}, u32[]{:S(2)}, u32[]{:S(2)}) collective-permute-start(bf16[12,1,1,2,2,2,16,128]{7,6,0,5,4,3,2,1:T(8,128)(2,1)S(1)} %maximum_select_fusion.3), channel_id=1, source_target_pairs={{0,2},{1,3},{2,0},{3,1},{4,6},{5,7},{6,4},{7,5},{8,10},{9,11},{10,... | collective-permute-start | bytes 1179656 | tf_op jit(solution)/shard_map/ppermute | solution.py:103
  95.2 6.5 %collective-permute-done.20 = bf16[12,1,1,2,2,2,16,128]{7,6,0,5,4,3,2,1:T(8,128)(2,1)S(1)} collective-permute-done((bf16[12,1,1,2,2,2,16,128]{7,6,0,5,4,3,2,1:T(8,128)(2,1)S(1)}, bf16[12,1,1,2,2,2,16,128]{7,6,0,5,4,3,2,1:T(8,128)(2,1)S(1)}, u32[]{:S(2)}, u32[]{:S(2)}) %collective-permute-start.20) | collective-permute-done | bytes 393248 | tf_op jit(solution)/shard_map/ppermute | solution.py:103
  103.2 1.4 %collective-permute-done.21 = bf16[12,256,128]{2,1,0:T(8,128)(2,1)} collective-permute-done((bf16[12,256,128]{2,1,0:T(8,128)(2,1)S(1)}, bf16[12,256,128]{2,1,0:T(8,128)(2,1)}, u32[]{:S(2)}, u32[]{:S(2)}) %collective-permute-start.21) | collective-permute-done | bytes 786464 | tf_op jit(solution)/shard_map/ppermute | solution.py:181
  104.6 1.8 %gather_fusion.5 = bf16[8,256,128]{2,1,0:T(8,128)(2,1)S(1)} fusion(bf16[12,256,128]{2,1,0:T(8,128)(2,1)} %collective-permute-done.21, s32[1024]{0:T(1024)S(1)} %pad_clamp_fusion), kind=kCustom, calls=%fused_computation.1.clone | custom fusion | bytes 1048608 | tf_op jit(solution)/shard_map/jit(_take)/gather | solution.py:183
  107.9 1.1 %copy-done.5 = f32[4,512,256]{2,1,0:T(8,128)S(1)} copy-done((f32[4,512,256]{2,1,0:T(8,128)S(1)}, f32[4,512,256]{2,1,0:T(8,128)}, u32[]{:S(2)}) %copy-start.5) | copy-done | bytes 2097176
  109.0 1.2 %fusion.3 = bf16[4,512,256]{2,1,0:T(8,128)(2,1)} fusion(f32[4,512,256]{2,1,0:T(8,128)S(1)} %copy-done.5, f32[4,512,256,1]{2,1,3,0:T(8,128)S(1)} %fusion.16), kind=kLoop, calls=%fused_computation.10 | loop fusion | flops 1048576 | bytes 5242880 | tf_op jit(solution)/shard_map/convert_element_type | solution.py:191
  (126 shorter events, 26.8 us)
Async XLA Ops:
  0.0 42.6 %copy-start = (bf16[4,4,256,256]{3,2,1,0:T(8,128)(2,1)S(1)}, bf16[4,4,256,256]{3,2,1,0:T(8,128)(2,1)}, u32[]{:S(2)}) copy-start(bf16[4,4,256,256]{3,2,1,0:T(8,128)(2,1)} %param.12) | copy-start | bytes 6291460
  0.0 7.2 %copy-start.2 = (bf16[4,512,256]{2,1,0:T(8,128)(2,1)S(1)}, bf16[4,512,256]{2,1,0:T(8,128)(2,1)}, u32[]{:S(2)}) copy-start(bf16[4,512,256]{2,1,0:T(8,128)(2,1)} %residual_ref.3) | copy-start | bytes 3145732
  1.6 10.4 %copy-start.14 = (s32[3,4]{1,0:T(4,128)S(1)}, s32[3,4]{1,0:T(4,128)}, u32[]{:S(2)}) copy-start(s32[3,4]{1,0:T(4,128)} %param.15) | copy-start | bytes 148
  1.6 11.1 %copy-start.9 = (bf16[3,4,128,128]{3,2,1,0:T(8,128)(2,1)S(1)}, bf16[3,4,128,128]{3,2,1,0:T(8,128)(2,1)}, u32[]{:S(2)}) copy-start(bf16[3,4,128,128]{3,2,1,0:T(8,128)(2,1)} %param.16) | copy-start | bytes 1179652
  1.6 16.1 %copy-start.12 = (s32[4,4]{1,0:T(4,128)S(1)}, s32[4,4]{1,0:T(4,128)}, u32[]{:S(2)}) copy-start(s32[4,4]{1,0:T(4,128)} %param.11) | copy-start | bytes 196
  1.6 16.2 %copy-start.1 = (s32[4]{0:T(128)S(1)}, s32[4]{0:T(128)}, u32[]{:S(2)}) copy-start(s32[4]{0:T(128)} %constant.280.clone) | copy-start | bytes 52
  6.8 21.8 %collective-permute-start.2 = (f32[12,256,128]{2,1,0:T(8,128)}, f32[12,256,128]{2,1,0:T(8,128)}, u32[]{:S(2)}, u32[]{:S(2)}) collective-permute-start(f32[12,256,128]{2,1,0:T(8,128)} %shard_map.83), channel_id=1, source_target_pairs={{0,1},{1,0},{2,3},{3,2},{4,5},{5,4},{6,7},{7,6},{8,9},{9,8},{10,11... | collective-permute-start | bytes 4718600 | tf_op jit(solution)/shard_map/ppermute | solution.py:137
  8.1 18.1 %collective-permute-start = (bf16[1,512,256]{2,1,0:T(8,128)(2,1)}, bf16[1,512,256]{2,1,0:T(8,128)(2,1)}, u32[]{:S(2)}, u32[]{:S(2)}) collective-permute-start(bf16[1,512,256]{2,1,0:T(8,128)(2,1)} %get-tuple-element.41), channel_id=1, source_target_pairs={{0,1},{1,2},{2,3},{3,4},{4,5},{5,6},{6,7},{7,8},{8,9},{9,10},{10,1... | collective-permute-start | bytes 786440 | tf_op jit(solution)/shard_map/ppermute | solution.py:65
  10.7 15.4 %collective-permute-start.1 = (bf16[1,512,256]{2,1,0:T(8,128)(2,1)}, bf16[1,512,256]{2,1,0:T(8,128)(2,1)}, u32[]{:S(2)}, u32[]{:S(2)}) collective-permute-start(bf16[1,512,256]{2,1,0:T(8,128)(2,1)} %get-tuple-element.42), channel_id=1, source_target_pairs={{1,0},{2,1},{3,2},{4,3},{5,4},{6,5},{7,6},{8,7},{9,8},{10,9},{11,1... | collective-permute-start | bytes 786440 | tf_op jit(solution)/shard_map/ppermute | solution.py:67
  13.5 12.6 %copy-start.3 = (bf16[4,512,256]{2,1,0:T(8,128)(2,1)S(1)}, bf16[4,512,256]{2,1,0:T(8,128)(2,1)}, u32[]{:S(2)}) copy-start(bf16[4,512,256]{2,1,0:T(8,128)(2,1)} %residual_ref.3) | copy-start | bytes 3145732
  13.5 16.7 %collective-permute-start.3 = (bf16[3,4,136,128]{3,2,1,0:T(8,128)(2,1)}, bf16[3,4,136,128]{3,2,1,0:T(8,128)(2,1)}, u32[]{:S(2)}, u32[]{:S(2)}) collective-permute-start(bf16[3,4,136,128]{3,2,1,0:T(8,128)(2,1)} %pad_maximum_fusion.2), channel_id=1, source_target_pairs={{0,2},{1,3},{2,0},{3,1},{4,6},{5,7},{6,4},{7,5},{8,10},{9,11},{10,... | collective-permute-start | bytes 1253384 | tf_op jit(solution)/shard_map/ppermute | solution.py:142
  31.8 16.8 %collective-permute-start.6 = (f32[4,1,2,2,1,2,16,128]{7,6,5,4,3,2,0,1:T(8,128)}, f32[4,1,2,2,1,2,16,128]{7,6,5,4,3,2,0,1:T(8,128)}, u32[]{:S(2)}, u32[]{:S(2)}) collective-permute-start(f32[4,1,2,2,1,2,16,128]{7,6,5,4,3,2,0,1:T(8,128)} %constant_dynamic-slice_fusion.9), channel_id=1, source_target_pairs={{0,8},{4,12},{8,0},{12,4},{16,24},{20,28},{24,16},{28,20},{1,9},{5... | collective-permute-start | bytes 786440 | tf_op jit(solution)/shard_map/ppermute | solution.py:98
  34.5 15.1 %collective-permute-start.5 = (f32[4,1,2,1,2,2,16,128]{7,6,5,4,3,2,0,1:T(8,128)}, f32[4,1,2,1,2,2,16,128]{7,6,5,4,3,2,0,1:T(8,128)}, u32[]{:S(2)}, u32[]{:S(2)}) collective-permute-start(f32[4,1,2,1,2,2,16,128]{7,6,5,4,3,2,0,1:T(8,128)} %constant_dynamic-slice_fusion.10), channel_id=1, source_target_pairs={{0,4},{4,0},{8,12},{12,8},{16,20},{20,16},{24,28},{28,24},{1,5},{5... | collective-permute-start | bytes 786440 | tf_op jit(solution)/shard_map/ppermute | solution.py:98
  36.4 6.2 %copy-start.15 = (pred[4,4]{1,0:T(4,128)(4,1)S(1)}, pred[4,4]{1,0:T(4,128)(4,1)}, u32[]{:S(2)}) copy-start(pred[4,4]{1,0:T(4,128)(4,1)} %compare_and_fusion.3) | copy-start | bytes 52
  36.4 14.2 %collective-permute-start.4 = (f32[4,1,1,2,2,2,16,128]{7,6,5,4,3,2,0,1:T(8,128)}, f32[4,1,1,2,2,2,16,128]{7,6,5,4,3,2,0,1:T(8,128)}, u32[]{:S(2)}, u32[]{:S(2)}) collective-permute-start(f32[4,1,1,2,2,2,16,128]{7,6,5,4,3,2,0,1:T(8,128)} %constant_dynamic-slice_fusion.11), channel_id=1, source_target_pairs={{0,2},{1,3},{2,0},{3,1},{4,6},{5,7},{6,4},{7,5},{8,10},{9,11},{10,... | collective-permute-start | bytes 786440 | tf_op jit(solution)/shard_map/ppermute | solution.py:98
  42.6 6.0 %copy-start.7 = (f32[4,1,2,2,2,2,16,128]{7,6,5,4,3,2,0,1:T(8,128)S(1)}, f32[4,1,2,2,2,2,16,128]{7,6,5,4,3,2,0,1:T(8,128)}, u32[]{:S(2)}) copy-start(f32[4,1,2,2,2,2,16,128]{7,6,5,4,3,2,0,1:T(8,128)} %copy-done.6) | copy-start | bytes 1572868
  51.6 9.2 %collective-permute-start.10 = (f32[4,1,2,2,1,1,16,128]{7,6,5,4,3,2,0,1:T(8,128)S(1)}, f32[4,1,2,2,1,1,16,128]{7,6,5,4,3,2,0,1:T(8,128)S(1)}, u32[]{:S(2)}, u32[]{:S(2)}) collective-permute-start(f32[4,1,2,2,1,1,16,128]{7,6,5,4,3,2,0,1:T(8,128)S(1)} %constant_dynamic-slice_fusion.6), channel_id=1, source_target_pairs={{0,16},{4,20},{8,24},{12,28},{16,0},{20,4},{24,8},{28,12},{1,17},{... | collective-permute-start | bytes 393224 | tf_op jit(solution)/shard_map/ppermute | solution.py:98
  53.7 6.4 %collective-permute-start.9 = (f32[4,1,2,1,1,2,16,128]{7,6,5,4,3,2,0,1:T(8,128)S(1)}, f32[4,1,2,1,1,2,16,128]{7,6,5,4,3,2,0,1:T(8,128)S(1)}, u32[]{:S(2)}, u32[]{:S(2)}) collective-permute-start(f32[4,1,2,1,1,2,16,128]{7,6,5,4,3,2,0,1:T(8,128)S(1)} %constant_dynamic-slice_fusion.7), channel_id=1, source_target_pairs={{0,8},{4,12},{8,0},{12,4},{16,24},{20,28},{24,16},{28,20},{1,9},{5... | collective-permute-start | bytes 393224 | tf_op jit(solution)/shard_map/ppermute | solution.py:98
  54.8 6.1 %collective-permute-start.7 = (bf16[6,4,136,128]{3,2,1,0:T(8,128)(2,1)S(1)}, bf16[6,4,136,128]{3,2,1,0:T(8,128)(2,1)S(1)}, u32[]{:S(2)}, u32[]{:S(2)}) collective-permute-start(bf16[6,4,136,128]{3,2,1,0:T(8,128)(2,1)S(1)} %pad_maximum_fusion.1), channel_id=1, source_target_pairs={{0,1},{1,0},{2,3},{3,2},{4,5},{5,4},{6,7},{7,6},{8,9},{9,8},{10,11... | collective-permute-start | bytes 2506760 | tf_op jit(solution)/shard_map/ppermute | solution.py:162
  54.8 6.0 %collective-permute-start.8 = (f32[4,1,1,1,2,2,16,128]{7,6,5,4,3,2,0,1:T(8,128)S(1)}, f32[4,1,1,1,2,2,16,128]{7,6,5,4,3,2,0,1:T(8,128)S(1)}, u32[]{:S(2)}, u32[]{:S(2)}) collective-permute-start(f32[4,1,1,1,2,2,16,128]{7,6,5,4,3,2,0,1:T(8,128)S(1)} %constant_dynamic-slice_fusion.8), channel_id=1, source_target_pairs={{0,4},{4,0},{8,12},{12,8},{16,20},{20,16},{24,28},{28,24},{1,5},{5... | collective-permute-start | bytes 393224 | tf_op jit(solution)/shard_map/ppermute | solution.py:98
  62.9 4.9 %collective-permute-start.11 = (f32[4,1,1,1,1,2,16,128]{7,6,5,4,3,2,0,1:T(8,128)S(1)}, f32[4,1,1,1,1,2,16,128]{7,6,5,4,3,2,0,1:T(8,128)S(1)}, u32[]{:S(2)}, u32[]{:S(2)}) collective-permute-start(f32[4,1,1,1,1,2,16,128]{7,6,5,4,3,2,0,1:T(8,128)S(1)} %constant_dynamic-slice_fusion.5), channel_id=1, source_target_pairs={{0,8},{4,12},{8,0},{12,4},{16,24},{20,28},{24,16},{28,20},{1,9},{5... | collective-permute-start | bytes 196616 | tf_op jit(solution)/shard_map/ppermute | solution.py:98
  64.0 6.3 %collective-permute-start.13 = (f32[4,1,2,1,1,1,16,128]{7,6,5,4,3,2,0,1:T(8,128)S(1)}, f32[4,1,2,1,1,1,16,128]{7,6,5,4,3,2,0,1:T(8,128)S(1)}, u32[]{:S(2)}, u32[]{:S(2)}) collective-permute-start(f32[4,1,2,1,1,1,16,128]{7,6,5,4,3,2,0,1:T(8,128)S(1)} %constant_dynamic-slice_fusion.3), channel_id=1, source_target_pairs={{0,16},{4,20},{8,24},{12,28},{16,0},{20,4},{24,8},{28,12},{1,17},{... | collective-permute-start | bytes 196616 | tf_op jit(solution)/shard_map/ppermute | solution.py:98
  64.9 6.3 %collective-permute-start.15 = (f32[4,1,1,2,1,1,16,128]{7,6,5,4,3,2,0,1:T(8,128)S(1)}, f32[4,1,1,2,1,1,16,128]{7,6,5,4,3,2,0,1:T(8,128)S(1)}, u32[]{:S(2)}, u32[]{:S(2)}) collective-permute-start(f32[4,1,1,2,1,1,16,128]{7,6,5,4,3,2,0,1:T(8,128)S(1)} %constant_dynamic-slice_fusion.1), channel_id=1, source_target_pairs={{0,2},{1,3},{2,0},{3,1},{4,6},{5,7},{6,4},{7,5},{8,10},{9,11},{10,... | collective-permute-start | bytes 196616 | tf_op jit(solution)/shard_map/ppermute | solution.py:98
  67.9 5.2 %collective-permute-start.12 = (f32[4,1,1,1,1,1,16,128]{7,6,5,4,3,2,0,1:T(8,128)S(1)}, f32[4,1,1,1,1,1,16,128]{7,6,5,4,3,2,0,1:T(8,128)S(1)}, u32[]{:S(2)}, u32[]{:S(2)}) collective-permute-start(f32[4,1,1,1,1,1,16,128]{7,6,5,4,3,2,0,1:T(8,128)S(1)} %constant_dynamic-slice_fusion.4), channel_id=1, source_target_pairs={{0,16},{4,20},{8,24},{12,28},{16,0},{20,4},{24,8},{28,12},{1,17},{... | collective-permute-start | bytes 98312 | tf_op jit(solution)/shard_map/ppermute | solution.py:98
  70.3 4.0 %collective-permute-start.14 = (f32[4,1,1,1,1,1,16,128]{7,6,5,4,3,2,0,1:T(8,128)S(1)}, f32[4,1,1,1,1,1,16,128]{7,6,5,4,3,2,0,1:T(8,128)S(1)}, u32[]{:S(2)}, u32[]{:S(2)}) collective-permute-start(f32[4,1,1,1,1,1,16,128]{7,6,5,4,3,2,0,1:T(8,128)S(1)} %constant_dynamic-slice_fusion.2), channel_id=1, source_target_pairs={{0,2},{1,3},{2,0},{3,1},{4,6},{5,7},{6,4},{7,5},{8,10},{9,11},{10,... | collective-permute-start | bytes 98312 | tf_op jit(solution)/shard_map/ppermute | solution.py:98
  71.3 4.0 %collective-permute-start.16 = (f32[4,1,1,1,1,1,16,128]{7,6,5,4,3,2,0,1:T(8,128)S(1)}, f32[4,1,1,1,1,1,16,128]{7,6,5,4,3,2,0,1:T(8,128)S(1)}, u32[]{:S(2)}, u32[]{:S(2)}) collective-permute-start(f32[4,1,1,1,1,1,16,128]{7,6,5,4,3,2,0,1:T(8,128)S(1)} %constant_dynamic-slice_fusion), channel_id=1, source_target_pairs={{0,4},{4,0},{8,12},{12,8},{16,20},{20,16},{24,28},{28,24},{1,5},{5... | collective-permute-start | bytes 98312 | tf_op jit(solution)/shard_map/ppermute | solution.py:98
  78.3 5.1 %collective-permute-start.17 = (bf16[12,1,1,1,1,1,16,128]{7,6,0,5,4,3,2,1:T(8,128)(2,1)S(1)}, bf16[12,1,1,1,1,1,16,128]{7,6,0,5,4,3,2,1:T(8,128)(2,1)S(1)}, u32[]{:S(2)}, u32[]{:S(2)}) collective-permute-start(bf16[12,1,1,1,1,1,16,128]{7,6,0,5,4,3,2,1:T(8,128)(2,1)S(1)} %bitcast_select_fusion), channel_id=1, source_target_pairs={{0,16},{4,20},{8,24},{12,28},{16,0},{20,4},{24,8},{28,12},{1,17},{... | collective-permute-start | bytes 147464 | tf_op jit(solution)/shard_map/ppermute | solution.py:103
  83.4 4.7 %collective-permute-start.18 = (bf16[12,1,1,1,1,2,16,128]{7,6,0,5,4,3,2,1:T(8,128)(2,1)S(1)}, bf16[12,1,1,1,1,2,16,128]{7,6,0,5,4,3,2,1:T(8,128)(2,1)S(1)}, u32[]{:S(2)}, u32[]{:S(2)}) collective-permute-start(bf16[12,1,1,1,1,2,16,128]{7,6,0,5,4,3,2,1:T(8,128)(2,1)S(1)} %maximum_select_fusion.7), channel_id=1, source_target_pairs={{0,8},{4,12},{8,0},{12,4},{16,24},{20,28},{24,16},{28,20},{1,9},{5... | collective-permute-start | bytes 294920 | tf_op jit(solution)/shard_map/ppermute | solution.py:103
  88.1 5.7 %collective-permute-start.19 = (bf16[12,1,1,1,2,2,16,128]{7,6,0,5,4,3,2,1:T(8,128)(2,1)S(1)}, bf16[12,1,1,1,2,2,16,128]{7,6,0,5,4,3,2,1:T(8,128)(2,1)S(1)}, u32[]{:S(2)}, u32[]{:S(2)}) collective-permute-start(bf16[12,1,1,1,2,2,16,128]{7,6,0,5,4,3,2,1:T(8,128)(2,1)S(1)} %maximum_select_fusion.5), channel_id=1, source_target_pairs={{0,4},{4,0},{8,12},{12,8},{16,20},{20,16},{24,28},{28,24},{1,5},{5... | collective-permute-start | bytes 589832 | tf_op jit(solution)/shard_map/ppermute | solution.py:103
  89.2 13.0 %copy-start.13 = (s32[4,2]{0,1:T(2,128)S(1)}, s32[4,2]{0,1:T(2,128)}, u32[]{:S(2)}) copy-start(s32[4,2]{0,1:T(2,128)} %param.13) | copy-start | bytes 100
  93.9 7.8 %collective-permute-start.20 = (bf16[12,1,1,2,2,2,16,128]{7,6,0,5,4,3,2,1:T(8,128)(2,1)S(1)}, bf16[12,1,1,2,2,2,16,128]{7,6,0,5,4,3,2,1:T(8,128)(2,1)S(1)}, u32[]{:S(2)}, u32[]{:S(2)}) collective-permute-start(bf16[12,1,1,2,2,2,16,128]{7,6,0,5,4,3,2,1:T(8,128)(2,1)S(1)} %maximum_select_fusion.3), channel_id=1, source_target_pairs={{0,2},{1,3},{2,0},{3,1},{4,6},{5,7},{6,4},{7,5},{8,10},{9,11},{10,... | collective-permute-start | bytes 1179656 | tf_op jit(solution)/shard_map/ppermute | solution.py:103
  102.1 2.5 %collective-permute-start.21 = (bf16[12,256,128]{2,1,0:T(8,128)(2,1)S(1)}, bf16[12,256,128]{2,1,0:T(8,128)(2,1)}, u32[]{:S(2)}, u32[]{:S(2)}) collective-permute-start(bf16[12,256,128]{2,1,0:T(8,128)(2,1)S(1)} %bitcast.64), channel_id=1, source_target_pairs={{0,1},{1,0},{2,3},{3,2},{4,5},{5,4},{6,7},{7,6},{8,9},{9,8},{10,11... | collective-permute-start | bytes 2359304 | tf_op jit(solution)/shard_map/ppermute | solution.py:181
  (6 other events, 12.0 us)

commit v19 on v16

--- a/solution.py
+++ b/solution.py
@@ -141,7 +141,7 @@
     assert nb >= len(exchanges) + 1
     arriving = lax.ppermute(packed, exchanges[0][0], pairs(*exchanges[0]))
     xors = [0, exchanges[0][1]]
-    extended, inverse_blocks, whole, arriving = lax.optimization_barrier((extended, inverse_blocks, whole, arriving))
+    margin, inverse_blocks, whole, arriving = lax.optimization_barrier((margin, inverse_blocks, whole, arriving))
     packed = jnp.concatenate([packed, arriving], axis=0)
     arriving = None
     parts = [lax.slice_in_dim(whole, s * per, (s + 1) * per, axis=0) for s in range(streams)]

time: 109 us -> 110 us (level)
  waiting for transfers between devices: 21.3 us -> 23.9 us
  local copies, waits for them, and re-layouts: 19.5 us -> 18.4 us
    ppermute x12, starting transfers between devices: 14.6 us -> 19.3 us  [halve(): lax.ppermute(send.astype(wire), axis, pairs(axis, mask)).astype(x.dtype)]
    ppermute x12, starting transfers between devices: 13.9 us -> 11.2 us  [double(): recv = lax.ppermute(y, axis, pairs(axis, mask))]
    ppermute x12, waiting for transfers between devices: 8.47 us -> 11.1 us  [double(): recv = lax.ppermute(y, axis, pairs(axis, mask))]
    ppermute x1, starting transfers between devices: 4.14 us -> 2.53 us  [per_device(): arriving = lax.ppermute(packed, exchanges[0][0], pairs(*exchanges[0]))]
  transfers between devices with their start and end apart: 30 -> 30, of which waited for: 13 -> 14; matrix products, arithmetic and copies ran while one was open for 22% -> 20% of each run, Pallas kernels for 5% -> 5%
where the time goes in v19:
time: 110 us
  starting transfers between devices  37.8 us (34%)
  waiting for transfers between devices  23.9 us (22%)
  local copies, waits for them, and re-layouts  18.4 us (17%)
  other arithmetic  11.5 us (10%)
  Pallas kernels  10.2 us (9%)
  matrix products  7.15 us (6%)
    ppermute x12, starting transfers between devices, halve(): lax.ppermute(send.astype(wire), axis, pairs(axis, mask)).astype(x.dtype)  19.3 us
    ppermute x12, waiting for transfers between devices, halve(): lax.ppermute(send.astype(wire), axis, pairs(axis, mask)).astype(x.dtype)  11.4 us
    ppermute x12, starting transfers between devices, double(): recv = lax.ppermute(y, axis, pairs(axis, mask))  11.2 us
    ppermute x12, waiting for transfers between devices, double(): recv = lax.ppermute(y, axis, pairs(axis, mask))  11.1 us
    pallas_call x2, Pallas kernels, restrict(): pl.pallas_call(functools.partial(restrict_kernel, upper=upper), out_shape...  10.2 us
    unnamed x37, local copies, waits for them, and re-layouts  5.11 us
    dot_general x1, matrix products, per_device(): jnp.einsum('jerb,jebc->jrc', picked, inverse_blocks, preferred_element_ty...  4.9 us
    gather x1, local copies, waits for them, and re-layouts, per_device(): picked = jnp.take(extended, margin, axis=0)  4.2 us
  transfers between devices with their start and end apart: 30, of which 14 were waited for; matrix products, arithmetic and copies ran while one was open for 20% of the time, Pallas kernels for 5%

profile of v19, /device:TPU:0, one launch (start us, length us, event | category | flops | bytes accessed | tf_op | source)
XLA Modules:
  0.0 109.6 jit_solution(286558266066837271)
XLA Ops:
  1.6 5.1 %shard_map.83 = f32[12,256,128]{2,1,0:T(8,128)} custom-call(s32[8]{0:T(128)} %reshape.1777.links, s32[1]{0:T(128)} %bitcast.half, bf16[4,512,256]{2,1,0:T(8,128)(2,1)} %residual_ref.3, bf16[4,2,256,128]{3,2,1,0:T(8,128)(2,1)} %basis_ref.3), custom_call_target="tpu_custom_call" | custom-call | flops 134217728 | bytes 3145728 | tf_op jit(solution)/shard_map/pallas_call | solution.py:36
  8.0 2.5 %collective-permute-start.1 = (bf16[3,4,136,128]{3,2,1,0:T(8,128)(2,1)}, bf16[3,4,136,128]{3,2,1,0:T(8,128)(2,1)}, u32[]{:S(2)}, u32[]{:S(2)}) collective-permute-start(bf16[3,4,136,128]{3,2,1,0:T(8,128)(2,1)} %pad_maximum_fusion.3), channel_id=1, source_target_pairs={{0,2},{1,3},{2,0},{3,1},{4,6},{5,7},{6,4},{7,5},{8,10},{9,11},{10,... | collective-permute-start | bytes 1253384 | tf_op jit(solution)/shard_map/ppermute | solution.py:142
  11.4 3.0 %collective-permute-start.2 = (bf16[1,512,256]{2,1,0:T(8,128)(2,1)}, bf16[1,512,256]{2,1,0:T(8,128)(2,1)}, u32[]{:S(2)}, u32[]{:S(2)}) collective-permute-start(bf16[1,512,256]{2,1,0:T(8,128)(2,1)} %get-tuple-element.41), channel_id=1, source_target_pairs={{0,1},{1,2},{2,3},{3,4},{4,5},{5,6},{6,7},{7,8},{8,9},{9,10},{10,1... | collective-permute-start | bytes 786440 | tf_op jit(solution)/shard_map/ppermute | solution.py:65
  14.4 1.3 %collective-permute-start.3 = (bf16[1,512,256]{2,1,0:T(8,128)(2,1)}, bf16[1,512,256]{2,1,0:T(8,128)(2,1)}, u32[]{:S(2)}, u32[]{:S(2)}) collective-permute-start(bf16[1,512,256]{2,1,0:T(8,128)(2,1)} %get-tuple-element.42), channel_id=1, source_target_pairs={{1,0},{2,1},{3,2},{4,3},{5,4},{6,5},{7,6},{8,7},{9,8},{10,9},{11,1... | collective-permute-start | bytes 786440 | tf_op jit(solution)/shard_map/ppermute | solution.py:67
  16.5 5.0 %shard_map.82 = f32[12,256,128]{2,1,0:T(8,128)} custom-call(s32[8]{0:T(128)} %reshape.1777.links, s32[1]{0:T(128)} %bitcast.half, bf16[4,512,256]{2,1,0:T(8,128)(2,1)} %residual_ref.3, bf16[4,2,256,128]{3,2,1,0:T(8,128)(2,1)} %basis_ref.3), custom_call_target="tpu_custom_call" | custom-call | flops 134217728 | bytes 3145728 | tf_op jit(solution)/shard_map/pallas_call | solution.py:36
  21.6 2.5 %pad_maximum_fusion = bf16[6,512,256]{2,1,0:T(8,128)(2,1)} fusion(bf16[1,512,256]{2,1,0:T(8,128)(2,1)} %collective-permute-done.3, bf16[4,512,256]{2,1,0:T(8,128)(2,1)S(1)} %copy-done.3, bf16[1,512,256]{2,1,0:T(8,128)(2,1)} %collective-permute-done.2), kind=kLoop, calls=%fused_computation.15 | loop fusion | flops 1572864 | bytes 3145728 | tf_op jit(solution)/shard_map/concatenate | solution.py:63
  24.1 1.6 %add.232 = f32[12,256,128]{2,1,0:T(8,128)S(1)} add(f32[12,256,128]{2,1,0:T(8,128)S(1)} %copy-done.4, f32[12,256,128]{2,1,0:T(8,128)} %collective-permute-done) | non-fusion elementwise | flops 393216 | bytes 4718592 | tf_op jit(solution)/shard_map/add | solution.py:138
  27.9 4.8 %collective-permute-start.6 = (f32[4,1,2,2,1,2,16,128]{7,6,5,4,3,2,0,1:T(8,128)}, f32[4,1,2,2,1,2,16,128]{7,6,5,4,3,2,0,1:T(8,128)}, u32[]{:S(2)}, u32[]{:S(2)}) collective-permute-start(f32[4,1,2,2,1,2,16,128]{7,6,5,4,3,2,0,1:T(8,128)} %constant_dynamic-slice_fusion.9), channel_id=1, source_target_pairs={{0,8},{4,12},{8,0},{12,4},{16,24},{20,28},{24,16},{28,20},{1,9},{5... | collective-permute-start | bytes 786440 | tf_op jit(solution)/shard_map/ppermute | solution.py:98
  34.8 4.5 %collective-permute-start.4 = (f32[4,1,1,2,2,2,16,128]{7,6,5,4,3,2,0,1:T(8,128)}, f32[4,1,1,2,2,2,16,128]{7,6,5,4,3,2,0,1:T(8,128)}, u32[]{:S(2)}, u32[]{:S(2)}) collective-permute-start(f32[4,1,1,2,2,2,16,128]{7,6,5,4,3,2,0,1:T(8,128)} %constant_dynamic-slice_fusion.11), channel_id=1, source_target_pairs={{0,2},{1,3},{2,0},{3,1},{4,6},{5,7},{6,4},{7,5},{8,10},{9,11},{10,... | collective-permute-start | bytes 786440 | tf_op jit(solution)/shard_map/ppermute | solution.py:98
  39.4 4.2 %gather_fusion = bf16[16,512,256]{2,1,0:T(8,128)(2,1)} fusion(bf16[6,512,256]{2,1,0:T(8,128)(2,1)} %pad_maximum_fusion, s32[1024]{0:T(1024)S(1)} %pad_clamp_fusion.4), kind=kCustom, calls=%fused_computation.2 | custom fusion | bytes 8388672 | tf_op jit(solution)/shard_map/jit(_take)/gather | solution.py:148
  43.6 4.9 %fusion.5 = f32[4,512,256]{2,1,0:T(8,128)} fusion(bf16[4,4,256,256]{3,2,1,0:T(8,128)(2,1)S(1)} %copy-done, bf16[4,4,512,256]{3,2,1,0:T(8,128)(2,1)} %bitcast.93, pred[4,4]{1,0:T(4,128)(4,1)S(1)} %copy-done.16), kind=kOutput, calls=%fused_computation.12 | convolution fusion | flops 1075838976 | bytes 8388624 | tf_op jit(solution)/shard_map/jerb,jebc->jrc/dot_general | solution.py:149
  52.6 1.2 %collective-permute-start.10 = (f32[4,1,2,2,1,1,16,128]{7,6,5,4,3,2,0,1:T(8,128)S(1)}, f32[4,1,2,2,1,1,16,128]{7,6,5,4,3,2,0,1:T(8,128)S(1)}, u32[]{:S(2)}, u32[]{:S(2)}) collective-permute-start(f32[4,1,2,2,1,1,16,128]{7,6,5,4,3,2,0,1:T(8,128)S(1)} %constant_dynamic-slice_fusion.6), channel_id=1, source_target_pairs={{0,16},{4,20},{8,24},{12,28},{16,0},{20,4},{24,8},{28,12},{1,17},{... | collective-permute-start | bytes 393224 | tf_op jit(solution)/shard_map/ppermute | solution.py:98
  53.8 2.0 %collective-permute-start.9 = (f32[4,1,2,1,1,2,16,128]{7,6,5,4,3,2,0,1:T(8,128)S(1)}, f32[4,1,2,1,1,2,16,128]{7,6,5,4,3,2,0,1:T(8,128)S(1)}, u32[]{:S(2)}, u32[]{:S(2)}) collective-permute-start(f32[4,1,2,1,1,2,16,128]{7,6,5,4,3,2,0,1:T(8,128)S(1)} %constant_dynamic-slice_fusion.7), channel_id=1, source_target_pairs={{0,8},{4,12},{8,0},{12,4},{16,24},{20,28},{24,16},{28,20},{1,9},{5... | collective-permute-start | bytes 393224 | tf_op jit(solution)/shard_map/ppermute | solution.py:98
  56.5 4.3 %collective-permute-done.9 = f32[4,1,2,1,1,2,16,128]{7,6,5,4,3,2,0,1:T(8,128)S(1)} collective-permute-done((f32[4,1,2,1,1,2,16,128]{7,6,5,4,3,2,0,1:T(8,128)S(1)}, f32[4,1,2,1,1,2,16,128]{7,6,5,4,3,2,0,1:T(8,128)S(1)}, u32[]{:S(2)}, u32[]{:S(2)}) %collective-permute-start.9) | collective-permute-done | bytes 131104 | tf_op jit(solution)/shard_map/ppermute | solution.py:98
  62.0 1.2 %copy-done.10 = bf16[12,4,136,128]{3,2,1,0:T(8,128)(2,1)} copy-done((bf16[12,4,136,128]{3,2,1,0:T(8,128)(2,1)}, bf16[12,4,136,128]{3,2,1,0:T(8,128)(2,1)S(1)}, u32[]{:S(2)}) %copy-start.10) | copy-done | bytes 1671192
  63.8 1.5 %collective-permute-start.13 = (f32[4,1,2,1,1,1,16,128]{7,6,5,4,3,2,0,1:T(8,128)S(1)}, f32[4,1,2,1,1,1,16,128]{7,6,5,4,3,2,0,1:T(8,128)S(1)}, u32[]{:S(2)}, u32[]{:S(2)}) collective-permute-start(f32[4,1,2,1,1,1,16,128]{7,6,5,4,3,2,0,1:T(8,128)S(1)} %constant_dynamic-slice_fusion.3), channel_id=1, source_target_pairs={{0,16},{4,20},{8,24},{12,28},{16,0},{20,4},{24,8},{28,12},{1,17},{... | collective-permute-start | bytes 196616 | tf_op jit(solution)/shard_map/ppermute | solution.py:98
  66.3 2.1 %collective-permute-done.11 = f32[4,1,1,1,1,2,16,128]{7,6,5,4,3,2,0,1:T(8,128)S(1)} collective-permute-done((f32[4,1,1,1,1,2,16,128]{7,6,5,4,3,2,0,1:T(8,128)S(1)}, f32[4,1,1,1,1,2,16,128]{7,6,5,4,3,2,0,1:T(8,128)S(1)}, u32[]{:S(2)}, u32[]{:S(2)}) %collective-permute-start.11) | collective-permute-done | bytes 65568 | tf_op jit(solution)/shard_map/ppermute | solution.py:98
  69.3 2.2 %collective-permute-start.14 = (f32[4,1,1,1,1,1,16,128]{7,6,5,4,3,2,0,1:T(8,128)S(1)}, f32[4,1,1,1,1,1,16,128]{7,6,5,4,3,2,0,1:T(8,128)S(1)}, u32[]{:S(2)}, u32[]{:S(2)}) collective-permute-start(f32[4,1,1,1,1,1,16,128]{7,6,5,4,3,2,0,1:T(8,128)S(1)} %constant_dynamic-slice_fusion.2), channel_id=1, source_target_pairs={{0,2},{1,3},{2,0},{3,1},{4,6},{5,7},{6,4},{7,5},{8,10},{9,11},{10,... | collective-permute-start | bytes 98312 | tf_op jit(solution)/shard_map/ppermute | solution.py:98
  72.2 1.2 %collective-permute-done.12 = f32[4,1,1,1,1,1,16,128]{7,6,5,4,3,2,0,1:T(8,128)S(1)} collective-permute-done((f32[4,1,1,1,1,1,16,128]{7,6,5,4,3,2,0,1:T(8,128)S(1)}, f32[4,1,1,1,1,1,16,128]{7,6,5,4,3,2,0,1:T(8,128)S(1)}, u32[]{:S(2)}, u32[]{:S(2)}) %collective-permute-start.12) | collective-permute-done | bytes 32800 | tf_op jit(solution)/shard_map/ppermute | solution.py:98
  73.5 2.0 %collective-permute-done.16 = f32[4,1,1,1,1,1,16,128]{7,6,5,4,3,2,0,1:T(8,128)S(1)} collective-permute-done((f32[4,1,1,1,1,1,16,128]{7,6,5,4,3,2,0,1:T(8,128)S(1)}, f32[4,1,1,1,1,1,16,128]{7,6,5,4,3,2,0,1:T(8,128)S(1)}, u32[]{:S(2)}, u32[]{:S(2)}) %collective-permute-start.16) | collective-permute-done | bytes 32800 | tf_op jit(solution)/shard_map/ppermute | solution.py:98
  76.1 1.8 %fusion.13 = bf16[12,16,128]{2,1,0:T(8,128)(2,1)S(1)} fusion(bf16[12,4,136,128]{3,2,1,0:T(8,128)(2,1)} %copy-done.10, bf16[12,4,16,128]{3,2,1,0:T(8,128)(2,1)S(1)} %bitcast.103, pred[12,4]{1,0:T(8,128)(4,1)S(1)} %copy.64), kind=kOutput, calls=%fused_computation.17 | convolution fusion | flops 25288704 | bytes 1818672 | tf_op jit(solution)/shard_map/nerc,necd->nrd/dot_general | solution.py:173
  81.4 2.2 %collective-permute-done.17 = bf16[4,1,1,1,1,1,16,128]{7,6,0,5,4,3,2,1:T(8,128)(2,1)S(1)} collective-permute-done((bf16[4,1,1,1,1,1,16,128]{7,6,0,5,4,3,2,1:T(8,128)(2,1)S(1)}, bf16[4,1,1,1,1,1,16,128]{7,6,0,5,4,3,2,1:T(8,128)(2,1)S(1)}, u32[]{:S(2)}, u32[]{:S(2)}) %collective-permute-start.17) | collective-permute-done | bytes 16416 | tf_op jit(solution)/shard_map/ppermute | solution.py:103
  83.8 1.6 %collective-permute-start.22 = (bf16[4,1,2,1,1,1,16,128]{7,6,0,5,4,3,2,1:T(8,128)(2,1)S(1)}, bf16[4,1,2,1,1,1,16,128]{7,6,0,5,4,3,2,1:T(8,128)(2,1)S(1)}, u32[]{:S(2)}, u32[]{:S(2)}) collective-permute-start(bf16[4,1,2,1,1,1,16,128]{7,6,0,5,4,3,2,1:T(8,128)(2,1)S(1)} %maximum_select_fusion.16), channel_id=1, source_target_pairs={{0,16},{4,20},{8,24},{12,28},{16,0},{20,4},{24,8},{28,12},{1,17},{... | collective-permute-start | bytes 98312 | tf_op jit(solution)/shard_map/ppermute | solution.py:103
  86.4 2.3 %collective-permute-done.18 = bf16[4,1,1,1,1,2,16,128]{7,6,0,5,4,3,2,1:T(8,128)(2,1)S(1)} collective-permute-done((bf16[4,1,1,1,1,2,16,128]{7,6,0,5,4,3,2,1:T(8,128)(2,1)S(1)}, bf16[4,1,1,1,1,2,16,128]{7,6,0,5,4,3,2,1:T(8,128)(2,1)S(1)}, u32[]{:S(2)}, u32[]{:S(2)}) %collective-permute-start.18) | collective-permute-done | bytes 32800 | tf_op jit(solution)/shard_map/ppermute | solution.py:103
  88.8 1.9 %collective-permute-start.23 = (bf16[4,1,2,1,1,2,16,128]{7,6,0,5,4,3,2,1:T(8,128)(2,1)S(1)}, bf16[4,1,2,1,1,2,16,128]{7,6,0,5,4,3,2,1:T(8,128)(2,1)S(1)}, u32[]{:S(2)}, u32[]{:S(2)}) collective-permute-start(bf16[4,1,2,1,1,2,16,128]{7,6,0,5,4,3,2,1:T(8,128)(2,1)S(1)} %maximum_select_fusion.11), channel_id=1, source_target_pairs={{0,8},{4,12},{8,0},{12,4},{16,24},{20,28},{24,16},{28,20},{1,9},{5... | collective-permute-start | bytes 196616 | tf_op jit(solution)/shard_map/ppermute | solution.py:103
  90.8 1.6 %collective-permute-start.27 = (bf16[4,1,2,2,1,1,16,128]{7,6,0,5,4,3,2,1:T(8,128)(2,1)S(1)}, bf16[4,1,2,2,1,1,16,128]{7,6,0,5,4,3,2,1:T(8,128)(2,1)S(1)}, u32[]{:S(2)}, u32[]{:S(2)}) collective-permute-start(bf16[4,1,2,2,1,1,16,128]{7,6,0,5,4,3,2,1:T(8,128)(2,1)S(1)} %fusion.29), channel_id=1, source_target_pairs={{0,16},{4,20},{8,24},{12,28},{16,0},{20,4},{24,8},{28,12},{1,17},{... | collective-permute-start | bytes 196616 | tf_op jit(solution)/shard_map/ppermute | solution.py:103
  93.7 1.6 %collective-permute-start.24 = (bf16[4,1,2,1,2,2,16,128]{7,6,0,5,4,3,2,1:T(8,128)(2,1)S(1)}, bf16[4,1,2,1,2,2,16,128]{7,6,0,5,4,3,2,1:T(8,128)(2,1)S(1)}, u32[]{:S(2)}, u32[]{:S(2)}) collective-permute-start(bf16[4,1,2,1,2,2,16,128]{7,6,0,5,4,3,2,1:T(8,128)(2,1)S(1)} %maximum_select_fusion.6), channel_id=1, source_target_pairs={{0,4},{4,0},{8,12},{12,8},{16,20},{20,16},{24,28},{28,24},{1,5},{5... | collective-permute-start | bytes 393224 | tf_op jit(solution)/shard_map/ppermute | solution.py:103
  96.4 1.7 %collective-permute-done.20 = bf16[4,1,1,2,2,2,16,128]{7,6,0,5,4,3,2,1:T(8,128)(2,1)S(1)} collective-permute-done((bf16[4,1,1,2,2,2,16,128]{7,6,0,5,4,3,2,1:T(8,128)(2,1)S(1)}, bf16[4,1,1,2,2,2,16,128]{7,6,0,5,4,3,2,1:T(8,128)(2,1)S(1)}, u32[]{:S(2)}, u32[]{:S(2)}) %collective-permute-start.20) | collective-permute-done | bytes 131104 | tf_op jit(solution)/shard_map/ppermute | solution.py:103
  98.8 2.6 %collective-permute-done.28 = bf16[4,1,2,2,1,2,16,128]{7,6,0,5,4,3,2,1:T(8,128)(2,1)S(1)} collective-permute-done((bf16[4,1,2,2,1,2,16,128]{7,6,0,5,4,3,2,1:T(8,128)(2,1)S(1)}, bf16[4,1,2,2,1,2,16,128]{7,6,0,5,4,3,2,1:T(8,128)(2,1)S(1)}, u32[]{:S(2)}, u32[]{:S(2)}) %collective-permute-start.28) | collective-permute-done | bytes 131104 | tf_op jit(solution)/shard_map/ppermute | solution.py:103
  102.6 1.4 %collective-permute-done.29 = bf16[12,256,128]{2,1,0:T(8,128)(2,1)} collective-permute-done((bf16[12,256,128]{2,1,0:T(8,128)(2,1)S(1)}, bf16[12,256,128]{2,1,0:T(8,128)(2,1)}, u32[]{:S(2)}, u32[]{:S(2)}) %collective-permute-start.29) | collective-permute-done | bytes 786464 | tf_op jit(solution)/shard_map/ppermute | solution.py:182
  104.0 1.8 %gather_fusion.5 = bf16[8,256,128]{2,1,0:T(8,128)(2,1)S(1)} fusion(bf16[12,256,128]{2,1,0:T(8,128)(2,1)} %collective-permute-done.29, s32[1024]{0:T(1024)S(1)} %pad_clamp_fusion), kind=kCustom, calls=%fused_computation.1.clone | custom fusion | bytes 1048608 | tf_op jit(solution)/shard_map/jit(_take)/gather | solution.py:184
  108.4 1.2 %fusion.3 = bf16[4,512,256]{2,1,0:T(8,128)(2,1)} fusion(f32[4,512,256]{2,1,0:T(8,128)S(1)} %copy-done.5, f32[4,512,256,1]{2,1,3,0:T(8,128)S(1)} %fusion.16), kind=kLoop, calls=%fused_computation.10 | loop fusion | flops 1048576 | bytes 5242880 | tf_op jit(solution)/shard_map/convert_element_type | solution.py:192
  (159 shorter events, 29.8 us)
Async XLA Ops:
  0.0 43.6 %copy-start = (bf16[4,4,256,256]{3,2,1,0:T(8,128)(2,1)S(1)}, bf16[4,4,256,256]{3,2,1,0:T(8,128)(2,1)}, u32[]{:S(2)}) copy-start(bf16[4,4,256,256]{3,2,1,0:T(8,128)(2,1)} %param.12) | copy-start | bytes 6291460
  1.6 14.1 %copy-start.1 = (s32[4]{0:T(128)S(1)}, s32[4]{0:T(128)}, u32[]{:S(2)}) copy-start(s32[4]{0:T(128)} %constant.312.clone) | copy-start | bytes 52
  6.7 17.4 %collective-permute-start = (f32[12,256,128]{2,1,0:T(8,128)}, f32[12,256,128]{2,1,0:T(8,128)}, u32[]{:S(2)}, u32[]{:S(2)}) collective-permute-start(f32[12,256,128]{2,1,0:T(8,128)} %shard_map.83), channel_id=1, source_target_pairs={{0,1},{1,0},{2,3},{3,2},{4,5},{5,4},{6,7},{7,6},{8,9},{9,8},{10,11... | collective-permute-start | bytes 4718600 | tf_op jit(solution)/shard_map/ppermute | solution.py:137
  8.0 17.7 %collective-permute-start.1 = (bf16[3,4,136,128]{3,2,1,0:T(8,128)(2,1)}, bf16[3,4,136,128]{3,2,1,0:T(8,128)(2,1)}, u32[]{:S(2)}, u32[]{:S(2)}) collective-permute-start(bf16[3,4,136,128]{3,2,1,0:T(8,128)(2,1)} %pad_maximum_fusion.3), channel_id=1, source_target_pairs={{0,2},{1,3},{2,0},{3,1},{4,6},{5,7},{6,4},{7,5},{8,10},{9,11},{10,... | collective-permute-start | bytes 1253384 | tf_op jit(solution)/shard_map/ppermute | solution.py:142
  11.4 10.1 %collective-permute-start.2 = (bf16[1,512,256]{2,1,0:T(8,128)(2,1)}, bf16[1,512,256]{2,1,0:T(8,128)(2,1)}, u32[]{:S(2)}, u32[]{:S(2)}) collective-permute-start(bf16[1,512,256]{2,1,0:T(8,128)(2,1)} %get-tuple-element.41), channel_id=1, source_target_pairs={{0,1},{1,2},{2,3},{3,4},{4,5},{5,6},{6,7},{7,8},{8,9},{9,10},{10,1... | collective-permute-start | bytes 786440 | tf_op jit(solution)/shard_map/ppermute | solution.py:65
  14.4 7.2 %collective-permute-start.3 = (bf16[1,512,256]{2,1,0:T(8,128)(2,1)}, bf16[1,512,256]{2,1,0:T(8,128)(2,1)}, u32[]{:S(2)}, u32[]{:S(2)}) collective-permute-start(bf16[1,512,256]{2,1,0:T(8,128)(2,1)} %get-tuple-element.42), channel_id=1, source_target_pairs={{1,0},{2,1},{3,2},{4,3},{5,4},{6,5},{7,6},{8,7},{9,8},{10,9},{11,1... | collective-permute-start | bytes 786440 | tf_op jit(solution)/shard_map/ppermute | solution.py:67
  27.9 21.6 %collective-permute-start.6 = (f32[4,1,2,2,1,2,16,128]{7,6,5,4,3,2,0,1:T(8,128)}, f32[4,1,2,2,1,2,16,128]{7,6,5,4,3,2,0,1:T(8,128)}, u32[]{:S(2)}, u32[]{:S(2)}) collective-permute-start(f32[4,1,2,2,1,2,16,128]{7,6,5,4,3,2,0,1:T(8,128)} %constant_dynamic-slice_fusion.9), channel_id=1, source_target_pairs={{0,8},{4,12},{8,0},{12,4},{16,24},{20,28},{24,16},{28,20},{1,9},{5... | collective-permute-start | bytes 786440 | tf_op jit(solution)/shard_map/ppermute | solution.py:98
  33.5 17.1 %collective-permute-start.5 = (f32[4,1,2,1,2,2,16,128]{7,6,5,4,3,2,0,1:T(8,128)}, f32[4,1,2,1,2,2,16,128]{7,6,5,4,3,2,0,1:T(8,128)}, u32[]{:S(2)}, u32[]{:S(2)}) collective-permute-start(f32[4,1,2,1,2,2,16,128]{7,6,5,4,3,2,0,1:T(8,128)} %constant_dynamic-slice_fusion.10), channel_id=1, source_target_pairs={{0,4},{4,0},{8,12},{12,8},{16,20},{20,16},{24,28},{28,24},{1,5},{5... | collective-permute-start | bytes 786440 | tf_op jit(solution)/shard_map/ppermute | solution.py:98
  34.8 16.8 %collective-permute-start.4 = (f32[4,1,1,2,2,2,16,128]{7,6,5,4,3,2,0,1:T(8,128)}, f32[4,1,1,2,2,2,16,128]{7,6,5,4,3,2,0,1:T(8,128)}, u32[]{:S(2)}, u32[]{:S(2)}) collective-permute-start(f32[4,1,1,2,2,2,16,128]{7,6,5,4,3,2,0,1:T(8,128)} %constant_dynamic-slice_fusion.11), channel_id=1, source_target_pairs={{0,2},{1,3},{2,0},{3,1},{4,6},{5,7},{6,4},{7,5},{8,10},{9,11},{10,... | collective-permute-start | bytes 786440 | tf_op jit(solution)/shard_map/ppermute | solution.py:98
  52.6 9.2 %collective-permute-start.10 = (f32[4,1,2,2,1,1,16,128]{7,6,5,4,3,2,0,1:T(8,128)S(1)}, f32[4,1,2,2,1,1,16,128]{7,6,5,4,3,2,0,1:T(8,128)S(1)}, u32[]{:S(2)}, u32[]{:S(2)}) collective-permute-start(f32[4,1,2,2,1,1,16,128]{7,6,5,4,3,2,0,1:T(8,128)S(1)} %constant_dynamic-slice_fusion.6), channel_id=1, source_target_pairs={{0,16},{4,20},{8,24},{12,28},{16,0},{20,4},{24,8},{28,12},{1,17},{... | collective-permute-start | bytes 393224 | tf_op jit(solution)/shard_map/ppermute | solution.py:98
  53.8 7.0 %collective-permute-start.9 = (f32[4,1,2,1,1,2,16,128]{7,6,5,4,3,2,0,1:T(8,128)S(1)}, f32[4,1,2,1,1,2,16,128]{7,6,5,4,3,2,0,1:T(8,128)S(1)}, u32[]{:S(2)}, u32[]{:S(2)}) collective-permute-start(f32[4,1,2,1,1,2,16,128]{7,6,5,4,3,2,0,1:T(8,128)S(1)} %constant_dynamic-slice_fusion.7), channel_id=1, source_target_pairs={{0,8},{4,12},{8,0},{12,4},{16,24},{20,28},{24,16},{28,20},{1,9},{5... | collective-permute-start | bytes 393224 | tf_op jit(solution)/shard_map/ppermute | solution.py:98
  55.8 6.1 %collective-permute-start.7 = (bf16[6,4,136,128]{3,2,1,0:T(8,128)(2,1)S(1)}, bf16[6,4,136,128]{3,2,1,0:T(8,128)(2,1)S(1)}, u32[]{:S(2)}, u32[]{:S(2)}) collective-permute-start(bf16[6,4,136,128]{3,2,1,0:T(8,128)(2,1)S(1)} %pad_maximum_fusion.1), channel_id=1, source_target_pairs={{0,1},{1,0},{2,3},{3,2},{4,5},{5,4},{6,7},{7,6},{8,9},{9,8},{10,11... | collective-permute-start | bytes 2506760 | tf_op jit(solution)/shard_map/ppermute | solution.py:162
  55.8 6.0 %collective-permute-start.8 = (f32[4,1,1,1,2,2,16,128]{7,6,5,4,3,2,0,1:T(8,128)S(1)}, f32[4,1,1,1,2,2,16,128]{7,6,5,4,3,2,0,1:T(8,128)S(1)}, u32[]{:S(2)}, u32[]{:S(2)}) collective-permute-start(f32[4,1,1,1,2,2,16,128]{7,6,5,4,3,2,0,1:T(8,128)S(1)} %constant_dynamic-slice_fusion.8), channel_id=1, source_target_pairs={{0,4},{4,0},{8,12},{12,8},{16,20},{20,16},{24,28},{28,24},{1,5},{5... | collective-permute-start | bytes 393224 | tf_op jit(solution)/shard_map/ppermute | solution.py:98
  63.4 5.0 %collective-permute-start.11 = (f32[4,1,1,1,1,2,16,128]{7,6,5,4,3,2,0,1:T(8,128)S(1)}, f32[4,1,1,1,1,2,16,128]{7,6,5,4,3,2,0,1:T(8,128)S(1)}, u32[]{:S(2)}, u32[]{:S(2)}) collective-permute-start(f32[4,1,1,1,1,2,16,128]{7,6,5,4,3,2,0,1:T(8,128)S(1)} %constant_dynamic-slice_fusion.5), channel_id=1, source_target_pairs={{0,8},{4,12},{8,0},{12,4},{16,24},{20,28},{24,16},{28,20},{1,9},{5... | collective-permute-start | bytes 196616 | tf_op jit(solution)/shard_map/ppermute | solution.py:98
  63.8 5.4 %collective-permute-start.13 = (f32[4,1,2,1,1,1,16,128]{7,6,5,4,3,2,0,1:T(8,128)S(1)}, f32[4,1,2,1,1,1,16,128]{7,6,5,4,3,2,0,1:T(8,128)S(1)}, u32[]{:S(2)}, u32[]{:S(2)}) collective-permute-start(f32[4,1,2,1,1,1,16,128]{7,6,5,4,3,2,0,1:T(8,128)S(1)} %constant_dynamic-slice_fusion.3), channel_id=1, source_target_pairs={{0,16},{4,20},{8,24},{12,28},{16,0},{20,4},{24,8},{28,12},{1,17},{... | collective-permute-start | bytes 196616 | tf_op jit(solution)/shard_map/ppermute | solution.py:98
  65.4 6.1 %collective-permute-start.15 = (f32[4,1,1,2,1,1,16,128]{7,6,5,4,3,2,0,1:T(8,128)S(1)}, f32[4,1,1,2,1,1,16,128]{7,6,5,4,3,2,0,1:T(8,128)S(1)}, u32[]{:S(2)}, u32[]{:S(2)}) collective-permute-start(f32[4,1,1,2,1,1,16,128]{7,6,5,4,3,2,0,1:T(8,128)S(1)} %constant_dynamic-slice_fusion.1), channel_id=1, source_target_pairs={{0,2},{1,3},{2,0},{3,1},{4,6},{5,7},{6,4},{7,5},{8,10},{9,11},{10,... | collective-permute-start | bytes 196616 | tf_op jit(solution)/shard_map/ppermute | solution.py:98
  68.4 5.1 %collective-permute-start.12 = (f32[4,1,1,1,1,1,16,128]{7,6,5,4,3,2,0,1:T(8,128)S(1)}, f32[4,1,1,1,1,1,16,128]{7,6,5,4,3,2,0,1:T(8,128)S(1)}, u32[]{:S(2)}, u32[]{:S(2)}) collective-permute-start(f32[4,1,1,1,1,1,16,128]{7,6,5,4,3,2,0,1:T(8,128)S(1)} %constant_dynamic-slice_fusion.4), channel_id=1, source_target_pairs={{0,16},{4,20},{8,24},{12,28},{16,0},{20,4},{24,8},{28,12},{1,17},{... | collective-permute-start | bytes 98312 | tf_op jit(solution)/shard_map/ppermute | solution.py:98
  69.3 4.2 %collective-permute-start.14 = (f32[4,1,1,1,1,1,16,128]{7,6,5,4,3,2,0,1:T(8,128)S(1)}, f32[4,1,1,1,1,1,16,128]{7,6,5,4,3,2,0,1:T(8,128)S(1)}, u32[]{:S(2)}, u32[]{:S(2)}) collective-permute-start(f32[4,1,1,1,1,1,16,128]{7,6,5,4,3,2,0,1:T(8,128)S(1)} %constant_dynamic-slice_fusion.2), channel_id=1, source_target_pairs={{0,2},{1,3},{2,0},{3,1},{4,6},{5,7},{6,4},{7,5},{8,10},{9,11},{10,... | collective-permute-start | bytes 98312 | tf_op jit(solution)/shard_map/ppermute | solution.py:98
  71.5 4.0 %collective-permute-start.16 = (f32[4,1,1,1,1,1,16,128]{7,6,5,4,3,2,0,1:T(8,128)S(1)}, f32[4,1,1,1,1,1,16,128]{7,6,5,4,3,2,0,1:T(8,128)S(1)}, u32[]{:S(2)}, u32[]{:S(2)}) collective-permute-start(f32[4,1,1,1,1,1,16,128]{7,6,5,4,3,2,0,1:T(8,128)S(1)} %constant_dynamic-slice_fusion), channel_id=1, source_target_pairs={{0,4},{4,0},{8,12},{12,8},{16,20},{20,16},{24,28},{28,24},{1,5},{5... | collective-permute-start | bytes 98312 | tf_op jit(solution)/shard_map/ppermute | solution.py:98
  78.6 5.1 %collective-permute-start.17 = (bf16[4,1,1,1,1,1,16,128]{7,6,0,5,4,3,2,1:T(8,128)(2,1)S(1)}, bf16[4,1,1,1,1,1,16,128]{7,6,0,5,4,3,2,1:T(8,128)(2,1)S(1)}, u32[]{:S(2)}, u32[]{:S(2)}) collective-permute-start(bf16[4,1,1,1,1,1,16,128]{7,6,0,5,4,3,2,1:T(8,128)(2,1)S(1)} %get-tuple-element.44), channel_id=1, source_target_pairs={{0,16},{4,20},{8,24},{12,28},{16,0},{20,4},{24,8},{28,12},{1,17},{... | collective-permute-start | bytes 49160 | tf_op jit(solution)/shard_map/ppermute | solution.py:103
  79.6 4.2 %collective-permute-start.21 = (bf16[4,1,1,1,1,1,16,128]{7,6,0,5,4,3,2,1:T(8,128)(2,1)S(1)}, bf16[4,1,1,1,1,1,16,128]{7,6,0,5,4,3,2,1:T(8,128)(2,1)S(1)}, u32[]{:S(2)}, u32[]{:S(2)}) collective-permute-start(bf16[4,1,1,1,1,1,16,128]{7,6,0,5,4,3,2,1:T(8,128)(2,1)S(1)} %get-tuple-element.45), channel_id=1, source_target_pairs={{0,2},{1,3},{2,0},{3,1},{4,6},{5,7},{6,4},{7,5},{8,10},{9,11},{10,... | collective-permute-start | bytes 49160 | tf_op jit(solution)/shard_map/ppermute | solution.py:103
  80.7 4.7 %collective-permute-start.25 = (bf16[4,1,1,1,1,1,16,128]{7,6,0,5,4,3,2,1:T(8,128)(2,1)S(1)}, bf16[4,1,1,1,1,1,16,128]{7,6,0,5,4,3,2,1:T(8,128)(2,1)S(1)}, u32[]{:S(2)}, u32[]{:S(2)}) collective-permute-start(bf16[4,1,1,1,1,1,16,128]{7,6,0,5,4,3,2,1:T(8,128)(2,1)S(1)} %get-tuple-element.46), channel_id=1, source_target_pairs={{0,4},{4,0},{8,12},{12,8},{16,20},{20,16},{24,28},{28,24},{1,5},{5... | collective-permute-start | bytes 49160 | tf_op jit(solution)/shard_map/ppermute | solution.py:103
  83.7 5.0 %collective-permute-start.18 = (bf16[4,1,1,1,1,2,16,128]{7,6,0,5,4,3,2,1:T(8,128)(2,1)S(1)}, bf16[4,1,1,1,1,2,16,128]{7,6,0,5,4,3,2,1:T(8,128)(2,1)S(1)}, u32[]{:S(2)}, u32[]{:S(2)}) collective-permute-start(bf16[4,1,1,1,1,2,16,128]{7,6,0,5,4,3,2,1:T(8,128)(2,1)S(1)} %maximum_select_fusion.14), channel_id=1, source_target_pairs={{0,8},{4,12},{8,0},{12,4},{16,24},{20,28},{24,16},{28,20},{1,9},{5... | collective-permute-start | bytes 98312 | tf_op jit(solution)/shard_map/ppermute | solution.py:103
  83.8 5.0 %collective-permute-start.22 = (bf16[4,1,2,1,1,1,16,128]{7,6,0,5,4,3,2,1:T(8,128)(2,1)S(1)}, bf16[4,1,2,1,1,1,16,128]{7,6,0,5,4,3,2,1:T(8,128)(2,1)S(1)}, u32[]{:S(2)}, u32[]{:S(2)}) collective-permute-start(bf16[4,1,2,1,1,1,16,128]{7,6,0,5,4,3,2,1:T(8,128)(2,1)S(1)} %maximum_select_fusion.16), channel_id=1, source_target_pairs={{0,16},{4,20},{8,24},{12,28},{16,0},{20,4},{24,8},{28,12},{1,17},{... | collective-permute-start | bytes 98312 | tf_op jit(solution)/shard_map/ppermute | solution.py:103
  85.4 5.3 %collective-permute-start.26 = (bf16[4,1,1,2,1,1,16,128]{7,6,0,5,4,3,2,1:T(8,128)(2,1)S(1)}, bf16[4,1,1,2,1,1,16,128]{7,6,0,5,4,3,2,1:T(8,128)(2,1)S(1)}, u32[]{:S(2)}, u32[]{:S(2)}) collective-permute-start(bf16[4,1,1,2,1,1,16,128]{7,6,0,5,4,3,2,1:T(8,128)(2,1)S(1)} %maximum_select_fusion.18), channel_id=1, source_target_pairs={{0,2},{1,3},{2,0},{3,1},{4,6},{5,7},{6,4},{7,5},{8,10},{9,11},{10,... | collective-permute-start | bytes 98312 | tf_op jit(solution)/shard_map/ppermute | solution.py:103
  88.7 4.3 %collective-permute-start.19 = (bf16[4,1,1,1,2,2,16,128]{7,6,0,5,4,3,2,1:T(8,128)(2,1)S(1)}, bf16[4,1,1,1,2,2,16,128]{7,6,0,5,4,3,2,1:T(8,128)(2,1)S(1)}, u32[]{:S(2)}, u32[]{:S(2)}) collective-permute-start(bf16[4,1,1,1,2,2,16,128]{7,6,0,5,4,3,2,1:T(8,128)(2,1)S(1)} %maximum_select_fusion.9), channel_id=1, source_target_pairs={{0,4},{4,0},{8,12},{12,8},{16,20},{20,16},{24,28},{28,24},{1,5},{5... | collective-permute-start | bytes 196616 | tf_op jit(solution)/shard_map/ppermute | solution.py:103
  88.8 4.8 %collective-permute-start.23 = (bf16[4,1,2,1,1,2,16,128]{7,6,0,5,4,3,2,1:T(8,128)(2,1)S(1)}, bf16[4,1,2,1,1,2,16,128]{7,6,0,5,4,3,2,1:T(8,128)(2,1)S(1)}, u32[]{:S(2)}, u32[]{:S(2)}) collective-permute-start(bf16[4,1,2,1,1,2,16,128]{7,6,0,5,4,3,2,1:T(8,128)(2,1)S(1)} %maximum_select_fusion.11), channel_id=1, source_target_pairs={{0,8},{4,12},{8,0},{12,4},{16,24},{20,28},{24,16},{28,20},{1,9},{5... | collective-permute-start | bytes 196616 | tf_op jit(solution)/shard_map/ppermute | solution.py:103
  90.8 5.6 %collective-permute-start.27 = (bf16[4,1,2,2,1,1,16,128]{7,6,0,5,4,3,2,1:T(8,128)(2,1)S(1)}, bf16[4,1,2,2,1,1,16,128]{7,6,0,5,4,3,2,1:T(8,128)(2,1)S(1)}, u32[]{:S(2)}, u32[]{:S(2)}) collective-permute-start(bf16[4,1,2,2,1,1,16,128]{7,6,0,5,4,3,2,1:T(8,128)(2,1)S(1)} %fusion.29), channel_id=1, source_target_pairs={{0,16},{4,20},{8,24},{12,28},{16,0},{20,4},{24,8},{28,12},{1,17},{... | collective-permute-start | bytes 196616 | tf_op jit(solution)/shard_map/ppermute | solution.py:103
  93.1 5.0 %collective-permute-start.20 = (bf16[4,1,1,2,2,2,16,128]{7,6,0,5,4,3,2,1:T(8,128)(2,1)S(1)}, bf16[4,1,1,2,2,2,16,128]{7,6,0,5,4,3,2,1:T(8,128)(2,1)S(1)}, u32[]{:S(2)}, u32[]{:S(2)}) collective-permute-start(bf16[4,1,1,2,2,2,16,128]{7,6,0,5,4,3,2,1:T(8,128)(2,1)S(1)} %maximum_select_fusion.5), channel_id=1, source_target_pairs={{0,2},{1,3},{2,0},{3,1},{4,6},{5,7},{6,4},{7,5},{8,10},{9,11},{10,... | collective-permute-start | bytes 393224 | tf_op jit(solution)/shard_map/ppermute | solution.py:103
  93.7 5.0 %collective-permute-start.24 = (bf16[4,1,2,1,2,2,16,128]{7,6,0,5,4,3,2,1:T(8,128)(2,1)S(1)}, bf16[4,1,2,1,2,2,16,128]{7,6,0,5,4,3,2,1:T(8,128)(2,1)S(1)}, u32[]{:S(2)}, u32[]{:S(2)}) collective-permute-start(bf16[4,1,2,1,2,2,16,128]{7,6,0,5,4,3,2,1:T(8,128)(2,1)S(1)} %maximum_select_fusion.6), channel_id=1, source_target_pairs={{0,4},{4,0},{8,12},{12,8},{16,20},{20,16},{24,28},{28,24},{1,5},{5... | collective-permute-start | bytes 393224 | tf_op jit(solution)/shard_map/ppermute | solution.py:103
  96.3 5.0 %collective-permute-start.28 = (bf16[4,1,2,2,1,2,16,128]{7,6,0,5,4,3,2,1:T(8,128)(2,1)S(1)}, bf16[4,1,2,2,1,2,16,128]{7,6,0,5,4,3,2,1:T(8,128)(2,1)S(1)}, u32[]{:S(2)}, u32[]{:S(2)}) collective-permute-start(bf16[4,1,2,2,1,2,16,128]{7,6,0,5,4,3,2,1:T(8,128)(2,1)S(1)} %maximum_select_fusion.7), channel_id=1, source_target_pairs={{0,8},{4,12},{8,0},{12,4},{16,24},{20,28},{24,16},{28,20},{1,9},{5... | collective-permute-start | bytes 393224 | tf_op jit(solution)/shard_map/ppermute | solution.py:103
  101.5 2.5 %collective-permute-start.29 = (bf16[12,256,128]{2,1,0:T(8,128)(2,1)S(1)}, bf16[12,256,128]{2,1,0:T(8,128)(2,1)}, u32[]{:S(2)}, u32[]{:S(2)}) collective-permute-start(bf16[12,256,128]{2,1,0:T(8,128)(2,1)S(1)} %pad_maximum_fusion.2), channel_id=1, source_target_pairs={{0,1},{1,0},{2,3},{3,2},{4,5},{5,4},{6,7},{7,6},{8,9},{9,8},{10,11... | collective-permute-start | bytes 2359304 | tf_op jit(solution)/shard_map/ppermute | solution.py:182
  (15 other events, 66.7 us)

commit v20 on v16

--- a/solution.py
+++ b/solution.py
@@ -145,12 +145,17 @@
     packed = jnp.concatenate([packed, arriving], axis=0)
     arriving = None
     parts = [lax.slice_in_dim(whole, s * per, (s + 1) * per, axis=0) for s in range(streams)]
-    picked = jnp.take(extended, margin, axis=0)
-    local = jnp.einsum("jerb,jebc->jrc", picked, inverse_blocks, preferred_element_type=jnp.float32)
+    split_at = margin.shape[0] // 2
+    picked = jnp.take(extended, margin[:split_at], axis=0)
+    local = [jnp.einsum("jerb,jebc->jrc", picked, inverse_blocks[:split_at], preferred_element_type=jnp.float32)]
     for step in range(1, nb):
         parts = [halve(x, 1 + orders[s][step], *bits[orders[s][step]], jnp.float32) for s, x in enumerate(parts)]
         if step == 1:
-            local, parts = lax.optimization_barrier((local, parts))
+            local[0], extended, parts = lax.optimization_barrier((local[0], extended, parts))
+            picked = jnp.take(extended, margin[split_at:], axis=0)
+            local.append(jnp.einsum("jerb,jebc->jrc", picked, inverse_blocks[split_at:], preferred_element_type=jnp.float32))
+        if step == 2:
+            local[1], parts = lax.optimization_barrier((local[1], parts))
         k = step
         if arriving is not None:
             arriving, parts = lax.optimization_barrier((arriving, parts))
@@ -189,7 +194,7 @@
     )
 
     spread = jnp.einsum("jqrc,jqbc->jrb", lifted, basis, preferred_element_type=jnp.float32)
-    return (local + spread).astype(jnp.bfloat16)
+    return (jnp.concatenate(local, axis=0) + spread).astype(jnp.bfloat16)
 
 
 def solution(mesh):

time: 109 us -> 106 us (0.972)
  other arithmetic: 12.6 us -> 8.23 us
  matrix products: 7.15 us -> 10.6 us
  starting transfers between devices: 37.1 us -> 35.6 us
  waiting for transfers between devices: 21.3 us -> 20 us
    ppermute x12, waiting for transfers between devices: 11.4 us -> 6.9 us  [halve(): lax.ppermute(send.astype(wire), axis, pairs(axis, mask)).astype(x.dtype)]
    dot_general x1 -> x2, matrix products: 4.9 us -> 7.29 us  [the longest x1 3.67 us: per_device(): jnp.einsum('jerb,jebc->jrc', picked, inverse_blocks[:split_at], preferred...]
    ppermute x1, waiting for transfers between devices: 0.01 us -> 2.05 us  [per_device(): arriving = lax.ppermute(packed, exchanges[0][0], pairs(*exchanges[0]))]
    concatenate x1, local copies, waits for them, and re-layouts: 0.12 us -> 2.11 us  [per_device(): packed = jnp.concatenate([packed, arriving], axis=0)]
    ppermute x12, starting transfers between devices: 13.9 us -> 12.4 us  [double(): recv = lax.ppermute(y, axis, pairs(axis, mask))]
    ppermute x12, waiting for transfers between devices: 8.47 us -> 9.76 us  [double(): recv = lax.ppermute(y, axis, pairs(axis, mask))]
    convert_element_type x1 -> x0, other arithmetic: 1.21 us -> none  [per_device(): return (local + spread).astype(jnp.bfloat16)]
    concatenate x1, other arithmetic: 2.41 us -> 1.22 us  [with_halo(): jnp.concatenate([lax.ppermute(tail, axis, [(i, (i + 1) % count) for i in...]
  transfers between devices with their start and end apart: 30 -> 30, of which waited for: 13 -> 14; matrix products, arithmetic and copies ran while one was open for 22% -> 22% of each run, Pallas kernels for 5% -> 5%
where the time goes in v20:
time: 106 us; the launch traced here: 105 us
  starting transfers between devices  35.6 us (34%)
  waiting for transfers between devices  20 us (19%)
  local copies, waits for them, and re-layouts  19.7 us (19%)
  matrix products  10.6 us (10%)
  Pallas kernels  10.2 us (10%)
  other arithmetic  8.23 us (8%)
    ppermute x12, starting transfers between devices, halve(): lax.ppermute(send.astype(wire), axis, pairs(axis, mask)).astype(x.dtype)  14.6 us
    ppermute x12, starting transfers between devices, double(): recv = lax.ppermute(y, axis, pairs(axis, mask))  12.4 us
    pallas_call x2, Pallas kernels, restrict(): pl.pallas_call(functools.partial(restrict_kernel, upper=upper), out_shape...  10.2 us
    ppermute x12, waiting for transfers between devices, double(): recv = lax.ppermute(y, axis, pairs(axis, mask))  9.76 us
    ppermute x12, waiting for transfers between devices, halve(): lax.ppermute(send.astype(wire), axis, pairs(axis, mask)).astype(x.dtype)  6.9 us
    unnamed x55, local copies, waits for them, and re-layouts  4.88 us
    ppermute x1, starting transfers between devices, per_device(): arriving = lax.ppermute(packed, exchanges[0][0], pairs(*exchanges[0]))  4.81 us
    dot_general x1, matrix products, per_device(): jnp.einsum('jerb,jebc->jrc', picked, inverse_blocks[:split_at], preferred...  3.67 us
  transfers between devices with their start and end apart: 30, of which 14 were waited for; matrix products, arithmetic and copies ran while one was open for 22% of the time, Pallas kernels for 5%

profile of v20, /device:TPU:0, one launch (start us, length us, event | category | flops | bytes accessed | tf_op | source)
XLA Modules:
  0.0 105.1 jit_solution(5635271051206615253)
XLA Ops:
  1.5 5.1 %shard_map.83 = f32[12,256,128]{2,1,0:T(8,128)} custom-call(s32[8]{0:T(128)} %reshape.1777.links, s32[1]{0:T(128)} %bitcast.half, bf16[4,512,256]{2,1,0:T(8,128)(2,1)} %residual_ref.3, bf16[4,2,256,128]{3,2,1,0:T(8,128)(2,1)} %basis_ref.3), custom_call_target="tpu_custom_call" | custom-call | flops 134217728 | bytes 3145728 | tf_op jit(solution)/shard_map/pallas_call | solution.py:36
  7.1 2.0 %collective-permute-start = (bf16[1,512,256]{2,1,0:T(8,128)(2,1)S(1)}, bf16[1,512,256]{2,1,0:T(8,128)(2,1)S(1)}, u32[]{:S(2)}, u32[]{:S(2)}) collective-permute-start(bf16[1,512,256]{2,1,0:T(8,128)(2,1)S(1)} %get-tuple-element.52), channel_id=1, source_target_pairs={{0,1},{1,2},{2,3},{3,4},{4,5},{5,6},{6,7},{7,8},{8,9},{9,10},{10,1... | collective-permute-start | bytes 786440 | tf_op jit(solution)/shard_map/ppermute | solution.py:65
  9.1 1.3 %collective-permute-start.1 = (bf16[1,512,256]{2,1,0:T(8,128)(2,1)S(1)}, bf16[1,512,256]{2,1,0:T(8,128)(2,1)}, u32[]{:S(2)}, u32[]{:S(2)}) collective-permute-start(bf16[1,512,256]{2,1,0:T(8,128)(2,1)S(1)} %get-tuple-element.53), channel_id=1, source_target_pairs={{1,0},{2,1},{3,2},{4,3},{5,4},{6,5},{7,6},{8,7},{9,8},{10,9},{11,1... | collective-permute-start | bytes 786440 | tf_op jit(solution)/shard_map/ppermute | solution.py:67
  11.3 4.8 %collective-permute-start.3 = (bf16[3,4,136,128]{3,2,1,0:T(8,128)(2,1)}, bf16[3,4,136,128]{3,2,1,0:T(8,128)(2,1)S(1)}, u32[]{:S(2)}, u32[]{:S(2)}) collective-permute-start(bf16[3,4,136,128]{3,2,1,0:T(8,128)(2,1)} %pad_maximum_fusion.3), channel_id=1, source_target_pairs={{0,2},{1,3},{2,0},{3,1},{4,6},{5,7},{6,4},{7,5},{8,10},{9,11},{10,... | collective-permute-start | bytes 1253384 | tf_op jit(solution)/shard_map/ppermute | solution.py:142
  17.2 5.1 %shard_map.82 = f32[12,256,128]{2,1,0:T(8,128)} custom-call(s32[8]{0:T(128)} %reshape.1777.links, s32[1]{0:T(128)} %bitcast.half, bf16[4,512,256]{2,1,0:T(8,128)(2,1)} %residual_ref.3, bf16[4,2,256,128]{3,2,1,0:T(8,128)(2,1)} %basis_ref.3), custom_call_target="tpu_custom_call" | custom-call | flops 134217728 | bytes 3145728 | tf_op jit(solution)/shard_map/pallas_call | solution.py:36
  23.6 1.2 %pad_maximum_fusion = bf16[6,512,256]{2,1,0:T(8,128)(2,1)S(1)} fusion(bf16[1,512,256]{2,1,0:T(8,128)(2,1)} %collective-permute-done.1, bf16[4,512,256]{2,1,0:T(8,128)(2,1)S(1)} %copy-done.2, bf16[1,512,256]{2,1,0:T(8,128)(2,1)} %copy-done.16), kind=kLoop, calls=%fused_computation.17 | loop fusion | flops 1572864 | bytes 3145728 | tf_op jit(solution)/shard_map/concatenate | solution.py:63
  24.8 1.6 %add.231 = f32[12,256,128]{2,1,0:T(8,128)S(1)} add(f32[12,256,128]{2,1,0:T(8,128)S(1)} %copy-done.3, f32[12,256,128]{2,1,0:T(8,128)} %collective-permute-done.2) | non-fusion elementwise | flops 393216 | bytes 4718592 | tf_op jit(solution)/shard_map/add | solution.py:138
  26.4 2.1 %collective-permute-done.3 = bf16[3,4,136,128]{3,2,1,0:T(8,128)(2,1)S(1)} collective-permute-done((bf16[3,4,136,128]{3,2,1,0:T(8,128)(2,1)}, bf16[3,4,136,128]{3,2,1,0:T(8,128)(2,1)S(1)}, u32[]{:S(2)}, u32[]{:S(2)}) %collective-permute-start.3) | collective-permute-done | bytes 417824 | tf_op jit(solution)/shard_map/ppermute | solution.py:142
  30.2 2.4 %collective-permute-start.6 = (f32[4,1,2,2,1,2,16,128]{7,6,5,4,3,2,0,1:T(8,128)}, f32[4,1,2,2,1,2,16,128]{7,6,5,4,3,2,0,1:T(8,128)}, u32[]{:S(2)}, u32[]{:S(2)}) collective-permute-start(f32[4,1,2,2,1,2,16,128]{7,6,5,4,3,2,0,1:T(8,128)} %constant_dynamic-slice_fusion.9), channel_id=1, source_target_pairs={{0,8},{4,12},{8,0},{12,4},{16,24},{20,28},{24,16},{28,20},{1,9},{5... | collective-permute-start | bytes 786440 | tf_op jit(solution)/shard_map/ppermute | solution.py:98
  34.7 2.1 %collective-permute-start.4 = (f32[4,1,1,2,2,2,16,128]{7,6,5,4,3,2,0,1:T(8,128)}, f32[4,1,1,2,2,2,16,128]{7,6,5,4,3,2,0,1:T(8,128)}, u32[]{:S(2)}, u32[]{:S(2)}) collective-permute-start(f32[4,1,1,2,2,2,16,128]{7,6,5,4,3,2,0,1:T(8,128)} %constant_dynamic-slice_fusion.11), channel_id=1, source_target_pairs={{0,2},{1,3},{2,0},{3,1},{4,6},{5,7},{6,4},{7,5},{8,10},{9,11},{10,... | collective-permute-start | bytes 786440 | tf_op jit(solution)/shard_map/ppermute | solution.py:98
  36.7 2.0 %gather_fusion.3 = bf16[8,512,256]{2,1,0:T(8,128)(2,1)} fusion(bf16[6,512,256]{2,1,0:T(8,128)(2,1)S(1)} %pad_maximum_fusion, s32[1024]{0:T(1024)S(1)} %get-tuple-element.75), kind=kCustom, calls=%fused_computation.clone | custom fusion | bytes 4194336 | tf_op jit(solution)/shard_map/jit(_take)/gather | solution.py:149
  38.8 3.7 %fusion.9 = f32[2,512,256]{2,1,0:T(8,128)} fusion(bf16[2,4,512,256]{3,2,1,0:T(8,128)(2,1)} %bitcast.95, pred[2,4]{1,0:T(4,128)(4,1)S(1)} %copy-done.23, bf16[4,4,256,256]{3,2,1,0:T(8,128)(2,1)} %param.14), kind=kOutput, calls=%fused_computation.18 | convolution fusion | flops 537919488 | bytes 4194312 | tf_op jit(solution)/shard_map/jerb,jebc->jrc/dot_general | solution.py:150
  47.6 2.0 %collective-permute-start.8 = (f32[4,1,2,1,1,2,16,128]{7,6,5,4,3,2,0,1:T(8,128)}, f32[4,1,2,1,1,2,16,128]{7,6,5,4,3,2,0,1:T(8,128)S(1)}, u32[]{:S(2)}, u32[]{:S(2)}) collective-permute-start(f32[4,1,2,1,1,2,16,128]{7,6,5,4,3,2,0,1:T(8,128)} %constant_dynamic-slice_fusion.7), channel_id=1, source_target_pairs={{0,8},{4,12},{8,0},{12,4},{16,24},{20,28},{24,16},{28,20},{1,9},{5... | collective-permute-start | bytes 393224 | tf_op jit(solution)/shard_map/ppermute | solution.py:98
  50.1 2.0 %gather_fusion.4 = bf16[8,512,256]{2,1,0:T(8,128)(2,1)} fusion(bf16[6,512,256]{2,1,0:T(8,128)(2,1)S(1)} %pad_maximum_fusion, s32[1024]{0:T(1024)S(1)} %get-tuple-element.74), kind=kCustom, calls=%fused_computation.2.clone | custom fusion | bytes 4194336 | tf_op jit(solution)/shard_map/jit(_take)/gather | solution.py:155
  52.1 3.6 %fusion.12 = f32[2,512,256]{2,1,0:T(8,128)} fusion(bf16[2,4,512,256]{3,2,1,0:T(8,128)(2,1)} %bitcast.94, pred[2,4]{1,0:T(4,128)(4,1)S(1)} %copy-done.22, bf16[4,4,256,256]{3,2,1,0:T(8,128)(2,1)} %param.14), kind=kOutput, calls=%fused_computation.19 | convolution fusion | flops 537919488 | bytes 4194312 | tf_op jit(solution)/shard_map/jerb,jebc->jrc/dot_general | solution.py:156
  56.9 2.1 %constant_dynamic-update-slice_fusion = bf16[12,4,136,128]{3,2,1,0:T(8,128)(2,1)} fusion(bf16[12,4,136,128]{3,2,1,0:T(8,128)(2,1)} %constant_dynamic-update-slice_fusion.1, bf16[6,4,136,128]{3,2,1,0:T(8,128)(2,1)} %collective-permute-done.10), kind=kLoop, calls=%fused_computation.106 | loop fusion | bytes 1671168 | tf_op jit(solution)/shard_map/concatenate | solution.py:162
  60.0 1.6 %collective-permute-start.11 = (f32[4,1,1,1,1,2,16,128]{7,6,5,4,3,2,0,1:T(8,128)S(1)}, f32[4,1,1,1,1,2,16,128]{7,6,5,4,3,2,0,1:T(8,128)S(1)}, u32[]{:S(2)}, u32[]{:S(2)}) collective-permute-start(f32[4,1,1,1,1,2,16,128]{7,6,5,4,3,2,0,1:T(8,128)S(1)} %constant_dynamic-slice_fusion.5), channel_id=1, source_target_pairs={{0,8},{4,12},{8,0},{12,4},{16,24},{20,28},{24,16},{28,20},{1,9},{5... | collective-permute-start | bytes 196616 | tf_op jit(solution)/shard_map/ppermute | solution.py:98
  63.2 1.4 %collective-permute-done.11 = f32[4,1,1,1,1,2,16,128]{7,6,5,4,3,2,0,1:T(8,128)S(1)} collective-permute-done((f32[4,1,1,1,1,2,16,128]{7,6,5,4,3,2,0,1:T(8,128)S(1)}, f32[4,1,1,1,1,2,16,128]{7,6,5,4,3,2,0,1:T(8,128)S(1)}, u32[]{:S(2)}, u32[]{:S(2)}) %collective-permute-start.11) | collective-permute-done | bytes 65568 | tf_op jit(solution)/shard_map/ppermute | solution.py:98
  64.6 1.3 %collective-permute-start.12 = (f32[4,1,1,1,1,1,16,128]{7,6,5,4,3,2,0,1:T(8,128)S(1)}, f32[4,1,1,1,1,1,16,128]{7,6,5,4,3,2,0,1:T(8,128)S(1)}, u32[]{:S(2)}, u32[]{:S(2)}) collective-permute-start(f32[4,1,1,1,1,1,16,128]{7,6,5,4,3,2,0,1:T(8,128)S(1)} %constant_dynamic-slice_fusion.4), channel_id=1, source_target_pairs={{0,16},{4,20},{8,24},{12,28},{16,0},{20,4},{24,8},{28,12},{1,17},{... | collective-permute-start | bytes 98312 | tf_op jit(solution)/shard_map/ppermute | solution.py:98
  65.9 2.2 %collective-permute-done.13 = f32[4,1,2,1,1,1,16,128]{7,6,5,4,3,2,0,1:T(8,128)S(1)} collective-permute-done((f32[4,1,2,1,1,1,16,128]{7,6,5,4,3,2,0,1:T(8,128)S(1)}, f32[4,1,2,1,1,1,16,128]{7,6,5,4,3,2,0,1:T(8,128)S(1)}, u32[]{:S(2)}, u32[]{:S(2)}) %collective-permute-start.13) | collective-permute-done | bytes 65568 | tf_op jit(solution)/shard_map/ppermute | solution.py:98
  69.9 2.2 %collective-permute-done.14 = f32[4,1,1,1,1,1,16,128]{7,6,5,4,3,2,0,1:T(8,128)S(1)} collective-permute-done((f32[4,1,1,1,1,1,16,128]{7,6,5,4,3,2,0,1:T(8,128)S(1)}, f32[4,1,1,1,1,1,16,128]{7,6,5,4,3,2,0,1:T(8,128)S(1)}, u32[]{:S(2)}, u32[]{:S(2)}) %collective-permute-start.14) | collective-permute-done | bytes 32800 | tf_op jit(solution)/shard_map/ppermute | solution.py:98
  73.8 1.8 %fusion.18 = bf16[12,16,128]{2,1,0:T(8,128)(2,1)S(1)} fusion(bf16[12,4,136,128]{3,2,1,0:T(8,128)(2,1)} %constant_dynamic-update-slice_fusion, bf16[12,4,16,128]{3,2,1,0:T(8,128)(2,1)S(1)} %bitcast.105, pred[12,4]{1,0:T(8,128)(4,1)S(1)} %copy.64), kind=kOutput, calls=%fused_computation.21 | convolution fusion | flops 25288704 | bytes 1818672 | tf_op jit(solution)/shard_map/nerc,necd->nrd/dot_general | solution.py:178
  77.8 1.8 %collective-permute-start.25 = (bf16[4,1,1,1,1,1,16,128]{7,6,0,5,4,3,2,1:T(8,128)(2,1)S(1)}, bf16[4,1,1,1,1,1,16,128]{7,6,0,5,4,3,2,1:T(8,128)(2,1)S(1)}, u32[]{:S(2)}, u32[]{:S(2)}) collective-permute-start(bf16[4,1,1,1,1,1,16,128]{7,6,0,5,4,3,2,1:T(8,128)(2,1)S(1)} %get-tuple-element.57), channel_id=1, source_target_pairs={{0,4},{4,0},{8,12},{12,8},{16,20},{20,16},{24,28},{28,24},{1,5},{5... | collective-permute-start | bytes 49160 | tf_op jit(solution)/shard_map/ppermute | solution.py:103
  79.7 1.3 %collective-permute-done.17 = bf16[4,1,1,1,1,1,16,128]{7,6,0,5,4,3,2,1:T(8,128)(2,1)S(1)} collective-permute-done((bf16[4,1,1,1,1,1,16,128]{7,6,0,5,4,3,2,1:T(8,128)(2,1)S(1)}, bf16[4,1,1,1,1,1,16,128]{7,6,0,5,4,3,2,1:T(8,128)(2,1)S(1)}, u32[]{:S(2)}, u32[]{:S(2)}) %collective-permute-start.17) | collective-permute-done | bytes 16416 | tf_op jit(solution)/shard_map/ppermute | solution.py:103
  81.1 2.0 %collective-permute-start.22 = (bf16[4,1,2,1,1,1,16,128]{7,6,0,5,4,3,2,1:T(8,128)(2,1)S(1)}, bf16[4,1,2,1,1,1,16,128]{7,6,0,5,4,3,2,1:T(8,128)(2,1)S(1)}, u32[]{:S(2)}, u32[]{:S(2)}) collective-permute-start(bf16[4,1,2,1,1,1,16,128]{7,6,0,5,4,3,2,1:T(8,128)(2,1)S(1)} %maximum_select_fusion.16), channel_id=1, source_target_pairs={{0,16},{4,20},{8,24},{12,28},{16,0},{20,4},{24,8},{28,12},{1,17},{... | collective-permute-start | bytes 98312 | tf_op jit(solution)/shard_map/ppermute | solution.py:103
  86.1 2.0 %collective-permute-start.23 = (bf16[4,1,2,1,1,2,16,128]{7,6,0,5,4,3,2,1:T(8,128)(2,1)S(1)}, bf16[4,1,2,1,1,2,16,128]{7,6,0,5,4,3,2,1:T(8,128)(2,1)S(1)}, u32[]{:S(2)}, u32[]{:S(2)}) collective-permute-start(bf16[4,1,2,1,1,2,16,128]{7,6,0,5,4,3,2,1:T(8,128)(2,1)S(1)} %maximum_select_fusion.11), channel_id=1, source_target_pairs={{0,8},{4,12},{8,0},{12,4},{16,24},{20,28},{24,16},{28,20},{1,9},{5... | collective-permute-start | bytes 196616 | tf_op jit(solution)/shard_map/ppermute | solution.py:103
  88.5 1.3 %collective-permute-done.19 = bf16[4,1,1,1,2,2,16,128]{7,6,0,5,4,3,2,1:T(8,128)(2,1)S(1)} collective-permute-done((bf16[4,1,1,1,2,2,16,128]{7,6,0,5,4,3,2,1:T(8,128)(2,1)S(1)}, bf16[4,1,1,1,2,2,16,128]{7,6,0,5,4,3,2,1:T(8,128)(2,1)S(1)}, u32[]{:S(2)}, u32[]{:S(2)}) %collective-permute-start.19) | collective-permute-done | bytes 65568 | tf_op jit(solution)/shard_map/ppermute | solution.py:103
  91.1 1.2 %collective-permute-start.24 = (bf16[4,1,2,1,2,2,16,128]{7,6,0,5,4,3,2,1:T(8,128)(2,1)S(1)}, bf16[4,1,2,1,2,2,16,128]{7,6,0,5,4,3,2,1:T(8,128)(2,1)S(1)}, u32[]{:S(2)}, u32[]{:S(2)}) collective-permute-start(bf16[4,1,2,1,2,2,16,128]{7,6,0,5,4,3,2,1:T(8,128)(2,1)S(1)} %maximum_select_fusion.6), channel_id=1, source_target_pairs={{0,4},{4,0},{8,12},{12,8},{16,20},{20,16},{24,28},{28,24},{1,5},{5... | collective-permute-start | bytes 393224 | tf_op jit(solution)/shard_map/ppermute | solution.py:103
  92.3 1.5 %collective-permute-done.27 = bf16[4,1,2,2,1,1,16,128]{7,6,0,5,4,3,2,1:T(8,128)(2,1)S(1)} collective-permute-done((bf16[4,1,2,2,1,1,16,128]{7,6,0,5,4,3,2,1:T(8,128)(2,1)S(1)}, bf16[4,1,2,2,1,1,16,128]{7,6,0,5,4,3,2,1:T(8,128)(2,1)S(1)}, u32[]{:S(2)}, u32[]{:S(2)}) %collective-permute-start.27) | collective-permute-done | bytes 65568 | tf_op jit(solution)/shard_map/ppermute | solution.py:103
  96.2 2.7 %collective-permute-done.28 = bf16[4,1,2,2,1,2,16,128]{7,6,0,5,4,3,2,1:T(8,128)(2,1)S(1)} collective-permute-done((bf16[4,1,2,2,1,2,16,128]{7,6,0,5,4,3,2,1:T(8,128)(2,1)S(1)}, bf16[4,1,2,2,1,2,16,128]{7,6,0,5,4,3,2,1:T(8,128)(2,1)S(1)}, u32[]{:S(2)}, u32[]{:S(2)}) %collective-permute-start.28) | collective-permute-done | bytes 131104 | tf_op jit(solution)/shard_map/ppermute | solution.py:103
  100.1 1.3 %collective-permute-done.29 = bf16[12,256,128]{2,1,0:T(8,128)(2,1)S(1)} collective-permute-done((bf16[12,256,128]{2,1,0:T(8,128)(2,1)S(1)}, bf16[12,256,128]{2,1,0:T(8,128)(2,1)S(1)}, u32[]{:S(2)}, u32[]{:S(2)}) %collective-permute-start.29) | collective-permute-done | bytes 786464 | tf_op jit(solution)/shard_map/ppermute | solution.py:187
  103.6 1.5 %fusion = bf16[4,512,256]{2,1,0:T(8,128)(2,1)} fusion(f32[2,512,256]{2,1,0:T(8,128)S(1)} %copy-done.25, f32[2,512,256]{2,1,0:T(8,128)S(1)} %copy-done.24, bf16[4,2,256,128]{3,2,1,0:T(8,128)(2,1)S(1)} %copy-done.8, bf16[4,2,256,128]{3,2,1,0:T(8,128)(2,1)S(1)} %get-tuple-element.73, bf16[4,2,256,128]{3,2,1,0:T(8,128)(2,1)S(1)} %get-tuple-element.72, pred[]{:T(512)S(6)} %eq.51), kind=kOutput, calls=%fused_computation.8 | convolution fusion | flops 274726912 | bytes 4718593 | tf_op jit(solution)/shard_map/jqrc,jqbc->jrb/dot_general | solution.py:196
  (179 shorter events, 34.0 us)
Async XLA Ops:
  1.4 14.7 %copy-start.19 = (s32[4,4]{1,0:T(4,128)S(1)}, s32[4,4]{1,0:T(4,128)}, u32[]{:S(2)}) copy-start(s32[4,4]{1,0:T(4,128)} %param.13) | copy-start | bytes 196
  1.4 14.9 %copy-start = (s32[4]{0:T(128)S(1)}, s32[4]{0:T(128)}, u32[]{:S(2)}) copy-start(s32[4]{0:T(128)} %constant.308.clone) | copy-start | bytes 52
  6.6 18.2 %collective-permute-start.2 = (f32[12,256,128]{2,1,0:T(8,128)}, f32[12,256,128]{2,1,0:T(8,128)}, u32[]{:S(2)}, u32[]{:S(2)}) collective-permute-start(f32[12,256,128]{2,1,0:T(8,128)} %shard_map.83), channel_id=1, source_target_pairs={{0,1},{1,0},{2,3},{3,2},{4,5},{5,4},{6,7},{7,6},{8,9},{9,8},{10,11... | collective-permute-start | bytes 4718600 | tf_op jit(solution)/shard_map/ppermute | solution.py:137
  7.1 15.7 %collective-permute-start = (bf16[1,512,256]{2,1,0:T(8,128)(2,1)S(1)}, bf16[1,512,256]{2,1,0:T(8,128)(2,1)S(1)}, u32[]{:S(2)}, u32[]{:S(2)}) collective-permute-start(bf16[1,512,256]{2,1,0:T(8,128)(2,1)S(1)} %get-tuple-element.52), channel_id=1, source_target_pairs={{0,1},{1,2},{2,3},{3,4},{4,5},{5,6},{6,7},{7,8},{8,9},{9,10},{10,1... | collective-permute-start | bytes 786440 | tf_op jit(solution)/shard_map/ppermute | solution.py:65
  9.1 14.5 %collective-permute-start.1 = (bf16[1,512,256]{2,1,0:T(8,128)(2,1)S(1)}, bf16[1,512,256]{2,1,0:T(8,128)(2,1)}, u32[]{:S(2)}, u32[]{:S(2)}) collective-permute-start(bf16[1,512,256]{2,1,0:T(8,128)(2,1)S(1)} %get-tuple-element.53), channel_id=1, source_target_pairs={{1,0},{2,1},{3,2},{4,3},{5,4},{6,5},{7,6},{8,7},{9,8},{10,9},{11,1... | collective-permute-start | bytes 786440 | tf_op jit(solution)/shard_map/ppermute | solution.py:67
  11.3 17.2 %collective-permute-start.3 = (bf16[3,4,136,128]{3,2,1,0:T(8,128)(2,1)}, bf16[3,4,136,128]{3,2,1,0:T(8,128)(2,1)S(1)}, u32[]{:S(2)}, u32[]{:S(2)}) collective-permute-start(bf16[3,4,136,128]{3,2,1,0:T(8,128)(2,1)} %pad_maximum_fusion.3), channel_id=1, source_target_pairs={{0,2},{1,3},{2,0},{3,1},{4,6},{5,7},{6,4},{7,5},{8,10},{9,11},{10,... | collective-permute-start | bytes 1253384 | tf_op jit(solution)/shard_map/ppermute | solution.py:142
  30.2 12.4 %collective-permute-start.6 = (f32[4,1,2,2,1,2,16,128]{7,6,5,4,3,2,0,1:T(8,128)}, f32[4,1,2,2,1,2,16,128]{7,6,5,4,3,2,0,1:T(8,128)}, u32[]{:S(2)}, u32[]{:S(2)}) collective-permute-start(f32[4,1,2,2,1,2,16,128]{7,6,5,4,3,2,0,1:T(8,128)} %constant_dynamic-slice_fusion.9), channel_id=1, source_target_pairs={{0,8},{4,12},{8,0},{12,4},{16,24},{20,28},{24,16},{28,20},{1,9},{5... | collective-permute-start | bytes 786440 | tf_op jit(solution)/shard_map/ppermute | solution.py:98
  33.3 10.3 %collective-permute-start.5 = (f32[4,1,2,1,2,2,16,128]{7,6,5,4,3,2,0,1:T(8,128)}, f32[4,1,2,1,2,2,16,128]{7,6,5,4,3,2,0,1:T(8,128)}, u32[]{:S(2)}, u32[]{:S(2)}) collective-permute-start(f32[4,1,2,1,2,2,16,128]{7,6,5,4,3,2,0,1:T(8,128)} %constant_dynamic-slice_fusion.10), channel_id=1, source_target_pairs={{0,4},{4,0},{8,12},{12,8},{16,20},{20,16},{24,28},{28,24},{1,5},{5... | collective-permute-start | bytes 786440 | tf_op jit(solution)/shard_map/ppermute | solution.py:98
  34.7 10.0 %collective-permute-start.4 = (f32[4,1,1,2,2,2,16,128]{7,6,5,4,3,2,0,1:T(8,128)}, f32[4,1,1,2,2,2,16,128]{7,6,5,4,3,2,0,1:T(8,128)}, u32[]{:S(2)}, u32[]{:S(2)}) collective-permute-start(f32[4,1,1,2,2,2,16,128]{7,6,5,4,3,2,0,1:T(8,128)} %constant_dynamic-slice_fusion.11), channel_id=1, source_target_pairs={{0,2},{1,3},{2,0},{3,1},{4,6},{5,7},{6,4},{7,5},{8,10},{9,11},{10,... | collective-permute-start | bytes 786440 | tf_op jit(solution)/shard_map/ppermute | solution.py:98
  45.8 11.1 %collective-permute-start.9 = (f32[4,1,2,2,1,1,16,128]{7,6,5,4,3,2,0,1:T(8,128)S(1)}, f32[4,1,2,2,1,1,16,128]{7,6,5,4,3,2,0,1:T(8,128)S(1)}, u32[]{:S(2)}, u32[]{:S(2)}) collective-permute-start(f32[4,1,2,2,1,1,16,128]{7,6,5,4,3,2,0,1:T(8,128)S(1)} %constant_dynamic-slice_fusion.6), channel_id=1, source_target_pairs={{0,16},{4,20},{8,24},{12,28},{16,0},{20,4},{24,8},{28,12},{1,17},{... | collective-permute-start | bytes 393224 | tf_op jit(solution)/shard_map/ppermute | solution.py:98
  47.6 9.2 %collective-permute-start.8 = (f32[4,1,2,1,1,2,16,128]{7,6,5,4,3,2,0,1:T(8,128)}, f32[4,1,2,1,1,2,16,128]{7,6,5,4,3,2,0,1:T(8,128)S(1)}, u32[]{:S(2)}, u32[]{:S(2)}) collective-permute-start(f32[4,1,2,1,1,2,16,128]{7,6,5,4,3,2,0,1:T(8,128)} %constant_dynamic-slice_fusion.7), channel_id=1, source_target_pairs={{0,8},{4,12},{8,0},{12,4},{16,24},{20,28},{24,16},{28,20},{1,9},{5... | collective-permute-start | bytes 393224 | tf_op jit(solution)/shard_map/ppermute | solution.py:98
  49.5 7.2 %collective-permute-start.7 = (f32[4,1,1,1,2,2,16,128]{7,6,5,4,3,2,0,1:T(8,128)S(1)}, f32[4,1,1,1,2,2,16,128]{7,6,5,4,3,2,0,1:T(8,128)S(1)}, u32[]{:S(2)}, u32[]{:S(2)}) collective-permute-start(f32[4,1,1,1,2,2,16,128]{7,6,5,4,3,2,0,1:T(8,128)S(1)} %constant_dynamic-slice_fusion.8), channel_id=1, source_target_pairs={{0,4},{4,0},{8,12},{12,8},{16,20},{20,16},{24,28},{28,24},{1,5},{5... | collective-permute-start | bytes 393224 | tf_op jit(solution)/shard_map/ppermute | solution.py:98
  50.1 6.8 %collective-permute-start.10 = (bf16[6,4,136,128]{3,2,1,0:T(8,128)(2,1)S(1)}, bf16[6,4,136,128]{3,2,1,0:T(8,128)(2,1)}, u32[]{:S(2)}, u32[]{:S(2)}) collective-permute-start(bf16[6,4,136,128]{3,2,1,0:T(8,128)(2,1)S(1)} %pad_maximum_fusion.1), channel_id=1, source_target_pairs={{0,1},{1,0},{2,3},{3,2},{4,5},{5,4},{6,7},{7,6},{8,9},{9,8},{10,11... | collective-permute-start | bytes 2506760 | tf_op jit(solution)/shard_map/ppermute | solution.py:167
  60.0 4.6 %collective-permute-start.11 = (f32[4,1,1,1,1,2,16,128]{7,6,5,4,3,2,0,1:T(8,128)S(1)}, f32[4,1,1,1,1,2,16,128]{7,6,5,4,3,2,0,1:T(8,128)S(1)}, u32[]{:S(2)}, u32[]{:S(2)}) collective-permute-start(f32[4,1,1,1,1,2,16,128]{7,6,5,4,3,2,0,1:T(8,128)S(1)} %constant_dynamic-slice_fusion.5), channel_id=1, source_target_pairs={{0,8},{4,12},{8,0},{12,4},{16,24},{20,28},{24,16},{28,20},{1,9},{5... | collective-permute-start | bytes 196616 | tf_op jit(solution)/shard_map/ppermute | solution.py:98
  61.7 6.5 %collective-permute-start.13 = (f32[4,1,2,1,1,1,16,128]{7,6,5,4,3,2,0,1:T(8,128)S(1)}, f32[4,1,2,1,1,1,16,128]{7,6,5,4,3,2,0,1:T(8,128)S(1)}, u32[]{:S(2)}, u32[]{:S(2)}) collective-permute-start(f32[4,1,2,1,1,1,16,128]{7,6,5,4,3,2,0,1:T(8,128)S(1)} %constant_dynamic-slice_fusion.3), channel_id=1, source_target_pairs={{0,16},{4,20},{8,24},{12,28},{16,0},{20,4},{24,8},{28,12},{1,17},{... | collective-permute-start | bytes 196616 | tf_op jit(solution)/shard_map/ppermute | solution.py:98
  62.0 7.1 %collective-permute-start.15 = (f32[4,1,1,2,1,1,16,128]{7,6,5,4,3,2,0,1:T(8,128)S(1)}, f32[4,1,1,2,1,1,16,128]{7,6,5,4,3,2,0,1:T(8,128)S(1)}, u32[]{:S(2)}, u32[]{:S(2)}) collective-permute-start(f32[4,1,1,2,1,1,16,128]{7,6,5,4,3,2,0,1:T(8,128)S(1)} %constant_dynamic-slice_fusion.1), channel_id=1, source_target_pairs={{0,2},{1,3},{2,0},{3,1},{4,6},{5,7},{6,4},{7,5},{8,10},{9,11},{10,... | collective-permute-start | bytes 196616 | tf_op jit(solution)/shard_map/ppermute | solution.py:98
  64.6 5.3 %collective-permute-start.12 = (f32[4,1,1,1,1,1,16,128]{7,6,5,4,3,2,0,1:T(8,128)S(1)}, f32[4,1,1,1,1,1,16,128]{7,6,5,4,3,2,0,1:T(8,128)S(1)}, u32[]{:S(2)}, u32[]{:S(2)}) collective-permute-start(f32[4,1,1,1,1,1,16,128]{7,6,5,4,3,2,0,1:T(8,128)S(1)} %constant_dynamic-slice_fusion.4), channel_id=1, source_target_pairs={{0,16},{4,20},{8,24},{12,28},{16,0},{20,4},{24,8},{28,12},{1,17},{... | collective-permute-start | bytes 98312 | tf_op jit(solution)/shard_map/ppermute | solution.py:98
  68.2 4.0 %collective-permute-start.14 = (f32[4,1,1,1,1,1,16,128]{7,6,5,4,3,2,0,1:T(8,128)S(1)}, f32[4,1,1,1,1,1,16,128]{7,6,5,4,3,2,0,1:T(8,128)S(1)}, u32[]{:S(2)}, u32[]{:S(2)}) collective-permute-start(f32[4,1,1,1,1,1,16,128]{7,6,5,4,3,2,0,1:T(8,128)S(1)} %constant_dynamic-slice_fusion.2), channel_id=1, source_target_pairs={{0,2},{1,3},{2,0},{3,1},{4,6},{5,7},{6,4},{7,5},{8,10},{9,11},{10,... | collective-permute-start | bytes 98312 | tf_op jit(solution)/shard_map/ppermute | solution.py:98
  69.2 4.0 %collective-permute-start.16 = (f32[4,1,1,1,1,1,16,128]{7,6,5,4,3,2,0,1:T(8,128)S(1)}, f32[4,1,1,1,1,1,16,128]{7,6,5,4,3,2,0,1:T(8,128)S(1)}, u32[]{:S(2)}, u32[]{:S(2)}) collective-permute-start(f32[4,1,1,1,1,1,16,128]{7,6,5,4,3,2,0,1:T(8,128)S(1)} %constant_dynamic-slice_fusion), channel_id=1, source_target_pairs={{0,4},{4,0},{8,12},{12,8},{16,20},{20,16},{24,28},{28,24},{1,5},{5... | collective-permute-start | bytes 98312 | tf_op jit(solution)/shard_map/ppermute | solution.py:98
  76.3 4.7 %collective-permute-start.17 = (bf16[4,1,1,1,1,1,16,128]{7,6,0,5,4,3,2,1:T(8,128)(2,1)S(1)}, bf16[4,1,1,1,1,1,16,128]{7,6,0,5,4,3,2,1:T(8,128)(2,1)S(1)}, u32[]{:S(2)}, u32[]{:S(2)}) collective-permute-start(bf16[4,1,1,1,1,1,16,128]{7,6,0,5,4,3,2,1:T(8,128)(2,1)S(1)} %get-tuple-element.55), channel_id=1, source_target_pairs={{0,16},{4,20},{8,24},{12,28},{16,0},{20,4},{24,8},{28,12},{1,17},{... | collective-permute-start | bytes 49160 | tf_op jit(solution)/shard_map/ppermute | solution.py:103
  76.7 4.4 %collective-permute-start.21 = (bf16[4,1,1,1,1,1,16,128]{7,6,0,5,4,3,2,1:T(8,128)(2,1)S(1)}, bf16[4,1,1,1,1,1,16,128]{7,6,0,5,4,3,2,1:T(8,128)(2,1)S(1)}, u32[]{:S(2)}, u32[]{:S(2)}) collective-permute-start(bf16[4,1,1,1,1,1,16,128]{7,6,0,5,4,3,2,1:T(8,128)(2,1)S(1)} %get-tuple-element.56), channel_id=1, source_target_pairs={{0,2},{1,3},{2,0},{3,1},{4,6},{5,7},{6,4},{7,5},{8,10},{9,11},{10,... | collective-permute-start | bytes 49160 | tf_op jit(solution)/shard_map/ppermute | solution.py:103
  77.8 5.3 %collective-permute-start.25 = (bf16[4,1,1,1,1,1,16,128]{7,6,0,5,4,3,2,1:T(8,128)(2,1)S(1)}, bf16[4,1,1,1,1,1,16,128]{7,6,0,5,4,3,2,1:T(8,128)(2,1)S(1)}, u32[]{:S(2)}, u32[]{:S(2)}) collective-permute-start(bf16[4,1,1,1,1,1,16,128]{7,6,0,5,4,3,2,1:T(8,128)(2,1)S(1)} %get-tuple-element.57), channel_id=1, source_target_pairs={{0,4},{4,0},{8,12},{12,8},{16,20},{20,16},{24,28},{28,24},{1,5},{5... | collective-permute-start | bytes 49160 | tf_op jit(solution)/shard_map/ppermute | solution.py:103
  81.0 4.0 %collective-permute-start.18 = (bf16[4,1,1,1,1,2,16,128]{7,6,0,5,4,3,2,1:T(8,128)(2,1)S(1)}, bf16[4,1,1,1,1,2,16,128]{7,6,0,5,4,3,2,1:T(8,128)(2,1)S(1)}, u32[]{:S(2)}, u32[]{:S(2)}) collective-permute-start(bf16[4,1,1,1,1,2,16,128]{7,6,0,5,4,3,2,1:T(8,128)(2,1)S(1)} %maximum_select_fusion.14), channel_id=1, source_target_pairs={{0,8},{4,12},{8,0},{12,4},{16,24},{20,28},{24,16},{28,20},{1,9},{5... | collective-permute-start | bytes 98312 | tf_op jit(solution)/shard_map/ppermute | solution.py:103
  81.1 5.0 %collective-permute-start.22 = (bf16[4,1,2,1,1,1,16,128]{7,6,0,5,4,3,2,1:T(8,128)(2,1)S(1)}, bf16[4,1,2,1,1,1,16,128]{7,6,0,5,4,3,2,1:T(8,128)(2,1)S(1)}, u32[]{:S(2)}, u32[]{:S(2)}) collective-permute-start(bf16[4,1,2,1,1,1,16,128]{7,6,0,5,4,3,2,1:T(8,128)(2,1)S(1)} %maximum_select_fusion.16), channel_id=1, source_target_pairs={{0,16},{4,20},{8,24},{12,28},{16,0},{20,4},{24,8},{28,12},{1,17},{... | collective-permute-start | bytes 98312 | tf_op jit(solution)/shard_map/ppermute | solution.py:103
  83.1 5.0 %collective-permute-start.26 = (bf16[4,1,1,2,1,1,16,128]{7,6,0,5,4,3,2,1:T(8,128)(2,1)S(1)}, bf16[4,1,1,2,1,1,16,128]{7,6,0,5,4,3,2,1:T(8,128)(2,1)S(1)}, u32[]{:S(2)}, u32[]{:S(2)}) collective-permute-start(bf16[4,1,1,2,1,1,16,128]{7,6,0,5,4,3,2,1:T(8,128)(2,1)S(1)} %maximum_select_fusion.18), channel_id=1, source_target_pairs={{0,2},{1,3},{2,0},{3,1},{4,6},{5,7},{6,4},{7,5},{8,10},{9,11},{10,... | collective-permute-start | bytes 98312 | tf_op jit(solution)/shard_map/ppermute | solution.py:103
  85.0 4.9 %collective-permute-start.19 = (bf16[4,1,1,1,2,2,16,128]{7,6,0,5,4,3,2,1:T(8,128)(2,1)S(1)}, bf16[4,1,1,1,2,2,16,128]{7,6,0,5,4,3,2,1:T(8,128)(2,1)S(1)}, u32[]{:S(2)}, u32[]{:S(2)}) collective-permute-start(bf16[4,1,1,1,2,2,16,128]{7,6,0,5,4,3,2,1:T(8,128)(2,1)S(1)} %maximum_select_fusion.9), channel_id=1, source_target_pairs={{0,4},{4,0},{8,12},{12,8},{16,20},{20,16},{24,28},{28,24},{1,5},{5... | collective-permute-start | bytes 196616 | tf_op jit(solution)/shard_map/ppermute | solution.py:103
  86.1 5.0 %collective-permute-start.23 = (bf16[4,1,2,1,1,2,16,128]{7,6,0,5,4,3,2,1:T(8,128)(2,1)S(1)}, bf16[4,1,2,1,1,2,16,128]{7,6,0,5,4,3,2,1:T(8,128)(2,1)S(1)}, u32[]{:S(2)}, u32[]{:S(2)}) collective-permute-start(bf16[4,1,2,1,1,2,16,128]{7,6,0,5,4,3,2,1:T(8,128)(2,1)S(1)} %maximum_select_fusion.11), channel_id=1, source_target_pairs={{0,8},{4,12},{8,0},{12,4},{16,24},{20,28},{24,16},{28,20},{1,9},{5... | collective-permute-start | bytes 196616 | tf_op jit(solution)/shard_map/ppermute | solution.py:103
  88.1 5.7 %collective-permute-start.27 = (bf16[4,1,2,2,1,1,16,128]{7,6,0,5,4,3,2,1:T(8,128)(2,1)S(1)}, bf16[4,1,2,2,1,1,16,128]{7,6,0,5,4,3,2,1:T(8,128)(2,1)S(1)}, u32[]{:S(2)}, u32[]{:S(2)}) collective-permute-start(bf16[4,1,2,2,1,1,16,128]{7,6,0,5,4,3,2,1:T(8,128)(2,1)S(1)} %fusion.37), channel_id=1, source_target_pairs={{0,16},{4,20},{8,24},{12,28},{16,0},{20,4},{24,8},{28,12},{1,17},{... | collective-permute-start | bytes 196616 | tf_op jit(solution)/shard_map/ppermute | solution.py:103
  89.9 5.0 %collective-permute-start.20 = (bf16[4,1,1,2,2,2,16,128]{7,6,0,5,4,3,2,1:T(8,128)(2,1)S(1)}, bf16[4,1,1,2,2,2,16,128]{7,6,0,5,4,3,2,1:T(8,128)(2,1)S(1)}, u32[]{:S(2)}, u32[]{:S(2)}) collective-permute-start(bf16[4,1,1,2,2,2,16,128]{7,6,0,5,4,3,2,1:T(8,128)(2,1)S(1)} %maximum_select_fusion.5), channel_id=1, source_target_pairs={{0,2},{1,3},{2,0},{3,1},{4,6},{5,7},{6,4},{7,5},{8,10},{9,11},{10,... | collective-permute-start | bytes 393224 | tf_op jit(solution)/shard_map/ppermute | solution.py:103
  91.1 5.0 %collective-permute-start.24 = (bf16[4,1,2,1,2,2,16,128]{7,6,0,5,4,3,2,1:T(8,128)(2,1)S(1)}, bf16[4,1,2,1,2,2,16,128]{7,6,0,5,4,3,2,1:T(8,128)(2,1)S(1)}, u32[]{:S(2)}, u32[]{:S(2)}) collective-permute-start(bf16[4,1,2,1,2,2,16,128]{7,6,0,5,4,3,2,1:T(8,128)(2,1)S(1)} %maximum_select_fusion.6), channel_id=1, source_target_pairs={{0,4},{4,0},{8,12},{12,8},{16,20},{20,16},{24,28},{28,24},{1,5},{5... | collective-permute-start | bytes 393224 | tf_op jit(solution)/shard_map/ppermute | solution.py:103
  93.8 5.0 %collective-permute-start.28 = (bf16[4,1,2,2,1,2,16,128]{7,6,0,5,4,3,2,1:T(8,128)(2,1)S(1)}, bf16[4,1,2,2,1,2,16,128]{7,6,0,5,4,3,2,1:T(8,128)(2,1)S(1)}, u32[]{:S(2)}, u32[]{:S(2)}) collective-permute-start(bf16[4,1,2,2,1,2,16,128]{7,6,0,5,4,3,2,1:T(8,128)(2,1)S(1)} %maximum_select_fusion.7), channel_id=1, source_target_pairs={{0,8},{4,12},{8,0},{12,4},{16,24},{20,28},{24,16},{28,20},{1,9},{5... | collective-permute-start | bytes 393224 | tf_op jit(solution)/shard_map/ppermute | solution.py:103
  99.0 2.4 %collective-permute-start.29 = (bf16[12,256,128]{2,1,0:T(8,128)(2,1)S(1)}, bf16[12,256,128]{2,1,0:T(8,128)(2,1)S(1)}, u32[]{:S(2)}, u32[]{:S(2)}) collective-permute-start(bf16[12,256,128]{2,1,0:T(8,128)(2,1)S(1)} %pad_maximum_fusion.2), channel_id=1, source_target_pairs={{0,1},{1,0},{2,3},{3,2},{4,5},{5,4},{6,7},{7,6},{8,9},{9,8},{10,11... | collective-permute-start | bytes 2359304 | tf_op jit(solution)/shard_map/ppermute | solution.py:187
  (24 other events, 101.3 us)

commit v21 on v16

--- a/solution.py
+++ b/solution.py
@@ -145,12 +145,24 @@
     packed = jnp.concatenate([packed, arriving], axis=0)
     arriving = None
     parts = [lax.slice_in_dim(whole, s * per, (s + 1) * per, axis=0) for s in range(streams)]
-    picked = jnp.take(extended, margin, axis=0)
-    local = jnp.einsum("jerb,jebc->jrc", picked, inverse_blocks, preferred_element_type=jnp.float32)
+    count = margin.shape[0]
+    sizes = [count // 2] + [1] * (count - count // 2)
+    assert nb - 1 >= len(sizes)
+    edges = [sum(sizes[:k]) for k in range(len(sizes) + 1)]
+
+    def solve_blocks(k, extended):
+        picked = jnp.take(extended, margin[edges[k]:edges[k + 1]], axis=0)
+        return jnp.einsum(
+            "jerb,jebc->jrc", picked, inverse_blocks[edges[k]:edges[k + 1]], preferred_element_type=jnp.float32
+        )
+
+    local = [solve_blocks(0, extended)]
     for step in range(1, nb):
         parts = [halve(x, 1 + orders[s][step], *bits[orders[s][step]], jnp.float32) for s, x in enumerate(parts)]
-        if step == 1:
-            local, parts = lax.optimization_barrier((local, parts))
+        if step <= len(sizes):
+            local[step - 1], extended, parts = lax.optimization_barrier((local[step - 1], extended, parts))
+            if step < len(sizes):
+                local.append(solve_blocks(step, extended))
         k = step
         if arriving is not None:
             arriving, parts = lax.optimization_barrier((arriving, parts))
@@ -189,7 +201,7 @@
     )
 
     spread = jnp.einsum("jqrc,jqbc->jrb", lifted, basis, preferred_element_type=jnp.float32)
-    return (local + spread).astype(jnp.bfloat16)
+    return (jnp.concatenate(local, axis=0) + spread).astype(jnp.bfloat16)
 
 
 def solution(mesh):

time: 109 us -> 110 us (level)
  matrix products: 7.15 us -> 12.4 us
  other arithmetic: 12.6 us -> 9.27 us
    ppermute x12, waiting for transfers between devices: 11.4 us -> 7.09 us  [halve(): lax.ppermute(send.astype(wire), axis, pairs(axis, mask)).astype(x.dtype)]
    dot_general x1 -> x3, matrix products: 4.9 us -> 9.14 us  [solve_blocks(): jnp.einsum('jerb,jebc->jrc', picked, inverse_blocks[edges[k]:edges[k + 1]...]
    ppermute x12, waiting for transfers between devices: 8.47 us -> 11.3 us  [double(): recv = lax.ppermute(y, axis, pairs(axis, mask))]
    ppermute x12, starting transfers between devices: 13.9 us -> 11.6 us  [double(): recv = lax.ppermute(y, axis, pairs(axis, mask))]
    ppermute x12, starting transfers between devices: 14.6 us -> 15.9 us  [halve(): lax.ppermute(send.astype(wire), axis, pairs(axis, mask)).astype(x.dtype)]
    convert_element_type x1 -> x0, other arithmetic: 1.21 us -> none  [per_device(): return (local + spread).astype(jnp.bfloat16)]
    concatenate x1, other arithmetic: 2.41 us -> 1.22 us  [with_halo(): jnp.concatenate([lax.ppermute(tail, axis, [(i, (i + 1) % count) for i in...]
    concatenate x1, local copies, waits for them, and re-layouts: 0.12 us -> 1.26 us  [per_device(): packed = jnp.concatenate([packed, arriving], axis=0)]
  transfers between devices with their start and end apart: 30 -> 30, of which waited for: 13 -> 13; matrix products, arithmetic and copies ran while one was open for 22% -> 25% of each run, Pallas kernels for 5% -> 5%
where the time goes in v21:
time: 110 us; the launch traced here: 109 us
  starting transfers between devices  36.1 us (33%)
  waiting for transfers between devices  20.3 us (18%)
  local copies, waits for them, and re-layouts  20.1 us (18%)
  matrix products  12.4 us (11%)
  Pallas kernels  10.2 us (9%)
  other arithmetic  9.27 us (8%)
    ppermute x12, starting transfers between devices, halve(): lax.ppermute(send.astype(wire), axis, pairs(axis, mask)).astype(x.dtype)  15.9 us
    ppermute x12, starting transfers between devices, double(): recv = lax.ppermute(y, axis, pairs(axis, mask))  11.6 us
    ppermute x12, waiting for transfers between devices, double(): recv = lax.ppermute(y, axis, pairs(axis, mask))  11.3 us
    pallas_call x2, Pallas kernels, restrict(): pl.pallas_call(functools.partial(restrict_kernel, upper=upper), out_shape...  10.2 us
    dot_general x3, matrix products, solve_blocks(): jnp.einsum('jerb,jebc->jrc', picked, inverse_blocks[edges[k]:edges[k + 1]...  9.14 us
    ppermute x12, waiting for transfers between devices, halve(): lax.ppermute(send.astype(wire), axis, pairs(axis, mask)).astype(x.dtype)  7.09 us
    unnamed x65, local copies, waits for them, and re-layouts  6.55 us
    gather x3, local copies, waits for them, and re-layouts, solve_blocks(): picked = jnp.take(extended, margin[edges[k]:edges[k + 1]], axis=0)  5.18 us
  transfers between devices with their start and end apart: 30, of which 13 were waited for; matrix products, arithmetic and copies ran while one was open for 25% of the time, Pallas kernels for 5%

profile of v21, /device:TPU:0, one launch (start us, length us, event | category | flops | bytes accessed | tf_op | source)
XLA Modules:
  0.0 109.1 jit_solution(7232426459423971633)
XLA Ops:
  1.5 5.1 %shard_map.83 = f32[12,256,128]{2,1,0:T(8,128)} custom-call(s32[8]{0:T(128)} %reshape.1808.links, s32[1]{0:T(128)} %bitcast.half, bf16[4,512,256]{2,1,0:T(8,128)(2,1)} %residual_ref.3, bf16[4,2,256,128]{3,2,1,0:T(8,128)(2,1)} %basis_ref.3), custom_call_target="tpu_custom_call" | custom-call | flops 134217728 | bytes 3145728 | tf_op jit(solution)/shard_map/pallas_call | solution.py:36
  7.1 2.0 %collective-permute-start = (bf16[1,512,256]{2,1,0:T(8,128)(2,1)S(1)}, bf16[1,512,256]{2,1,0:T(8,128)(2,1)S(1)}, u32[]{:S(2)}, u32[]{:S(2)}) collective-permute-start(bf16[1,512,256]{2,1,0:T(8,128)(2,1)S(1)} %get-tuple-element.62), channel_id=1, source_target_pairs={{0,1},{1,2},{2,3},{3,4},{4,5},{5,6},{6,7},{7,8},{8,9},{9,10},{10,1... | collective-permute-start | bytes 786440 | tf_op jit(solution)/shard_map/ppermute | solution.py:65
  9.1 1.3 %collective-permute-start.1 = (bf16[1,512,256]{2,1,0:T(8,128)(2,1)S(1)}, bf16[1,512,256]{2,1,0:T(8,128)(2,1)}, u32[]{:S(2)}, u32[]{:S(2)}) collective-permute-start(bf16[1,512,256]{2,1,0:T(8,128)(2,1)S(1)} %get-tuple-element.63), channel_id=1, source_target_pairs={{1,0},{2,1},{3,2},{4,3},{5,4},{6,5},{7,6},{8,7},{9,8},{10,9},{11,1... | collective-permute-start | bytes 786440 | tf_op jit(solution)/shard_map/ppermute | solution.py:67
  11.9 4.8 %collective-permute-start.3 = (bf16[3,4,136,128]{3,2,1,0:T(8,128)(2,1)}, bf16[3,4,136,128]{3,2,1,0:T(8,128)(2,1)S(1)}, u32[]{:S(2)}, u32[]{:S(2)}) collective-permute-start(bf16[3,4,136,128]{3,2,1,0:T(8,128)(2,1)} %pad_maximum_fusion.3), channel_id=1, source_target_pairs={{0,2},{1,3},{2,0},{3,1},{4,6},{5,7},{6,4},{7,5},{8,10},{9,11},{10,... | collective-permute-start | bytes 1253384 | tf_op jit(solution)/shard_map/ppermute | solution.py:142
  18.6 5.1 %shard_map.82 = f32[12,256,128]{2,1,0:T(8,128)} custom-call(s32[8]{0:T(128)} %reshape.1808.links, s32[1]{0:T(128)} %bitcast.half, bf16[4,512,256]{2,1,0:T(8,128)(2,1)} %residual_ref.3, bf16[4,2,256,128]{3,2,1,0:T(8,128)(2,1)} %basis_ref.3), custom_call_target="tpu_custom_call" | custom-call | flops 134217728 | bytes 3145728 | tf_op jit(solution)/shard_map/pallas_call | solution.py:36
  25.0 1.2 %pad_maximum_fusion = bf16[6,512,256]{2,1,0:T(8,128)(2,1)S(1)} fusion(bf16[1,512,256]{2,1,0:T(8,128)(2,1)} %collective-permute-done.1, bf16[4,512,256]{2,1,0:T(8,128)(2,1)S(1)} %copy-done.2, bf16[1,512,256]{2,1,0:T(8,128)(2,1)} %copy-done.18), kind=kLoop, calls=%fused_computation.15 | loop fusion | flops 1572864 | bytes 3145728 | tf_op jit(solution)/shard_map/concatenate | solution.py:63
  26.2 1.6 %add.236 = f32[12,256,128]{2,1,0:T(8,128)S(1)} add(f32[12,256,128]{2,1,0:T(8,128)S(1)} %copy-done.3, f32[12,256,128]{2,1,0:T(8,128)} %collective-permute-done.2) | non-fusion elementwise | flops 393216 | bytes 4718592 | tf_op jit(solution)/shard_map/add | solution.py:138
  30.2 2.5 %collective-permute-start.6 = (f32[4,1,2,2,1,2,16,128]{7,6,5,4,3,2,0,1:T(8,128)}, f32[4,1,2,2,1,2,16,128]{7,6,5,4,3,2,0,1:T(8,128)}, u32[]{:S(2)}, u32[]{:S(2)}) collective-permute-start(f32[4,1,2,2,1,2,16,128]{7,6,5,4,3,2,0,1:T(8,128)} %constant_dynamic-slice_fusion.9), channel_id=1, source_target_pairs={{0,8},{4,12},{8,0},{12,4},{16,24},{20,28},{24,16},{28,20},{1,9},{5... | collective-permute-start | bytes 786440 | tf_op jit(solution)/shard_map/ppermute | solution.py:98
  35.1 2.4 %collective-permute-start.4 = (f32[4,1,1,2,2,2,16,128]{7,6,5,4,3,2,0,1:T(8,128)}, f32[4,1,1,2,2,2,16,128]{7,6,5,4,3,2,0,1:T(8,128)}, u32[]{:S(2)}, u32[]{:S(2)}) collective-permute-start(f32[4,1,1,2,2,2,16,128]{7,6,5,4,3,2,0,1:T(8,128)} %constant_dynamic-slice_fusion.11), channel_id=1, source_target_pairs={{0,2},{1,3},{2,0},{3,1},{4,6},{5,7},{6,4},{7,5},{8,10},{9,11},{10,... | collective-permute-start | bytes 786440 | tf_op jit(solution)/shard_map/ppermute | solution.py:98
  37.4 2.0 %gather_fusion = bf16[8,512,256]{2,1,0:T(8,128)(2,1)} fusion(bf16[6,512,256]{2,1,0:T(8,128)(2,1)S(1)} %pad_maximum_fusion, s32[1024]{0:T(1024)S(1)} %pad_clamp_fusion.6), kind=kCustom, calls=%fused_computation.4 | custom fusion | bytes 4194336 | tf_op jit(solution)/shard_map/jit(_take)/gather | solution.py:154
  39.5 3.7 %fusion.6 = f32[2,512,256]{2,1,0:T(8,128)} fusion(bf16[2,4,512,256]{3,2,1,0:T(8,128)(2,1)} %bitcast.126, pred[2,4]{1,0:T(4,128)(4,1)S(1)} %copy-done.27, bf16[4,4,256,256]{3,2,1,0:T(8,128)(2,1)} %param.14), kind=kOutput, calls=%fused_computation.16 | convolution fusion | flops 537919488 | bytes 4194312 | tf_op jit(solution)/shard_map/jerb,jebc->jrc/dot_general | solution.py:155
  47.6 2.0 %collective-permute-start.8 = (f32[4,1,2,1,1,2,16,128]{7,6,5,4,3,2,0,1:T(8,128)S(1)}, f32[4,1,2,1,1,2,16,128]{7,6,5,4,3,2,0,1:T(8,128)S(1)}, u32[]{:S(2)}, u32[]{:S(2)}) collective-permute-start(f32[4,1,2,1,1,2,16,128]{7,6,5,4,3,2,0,1:T(8,128)S(1)} %constant_dynamic-slice_fusion.7), channel_id=1, source_target_pairs={{0,8},{4,12},{8,0},{12,4},{16,24},{20,28},{24,16},{28,20},{1,9},{5... | collective-permute-start | bytes 393224 | tf_op jit(solution)/shard_map/ppermute | solution.py:98
  49.9 1.6 %gather_fusion.4 = bf16[4,512,256]{2,1,0:T(8,128)(2,1)} fusion(bf16[6,512,256]{2,1,0:T(8,128)(2,1)S(1)} %pad_maximum_fusion, s32[1024]{0:T(1024)S(1)} %get-tuple-element.85), kind=kCustom, calls=%fused_computation.clone | custom fusion | bytes 2097168 | tf_op jit(solution)/shard_map/jit(_take)/gather | solution.py:154
  51.5 2.7 %convolution_bitcast_fusion.1 = f32[1,512,256]{2,1,0:T(8,128)} fusion(bf16[4,512,256]{2,1,0:T(8,128)(2,1)} %gather_fusion.4, pred[4]{0:T(512)(128)(4,1)S(1)} %copy-done.26, bf16[4,4,256,256]{3,2,1,0:T(8,128)(2,1)} %param.14), kind=kOutput, calls=%fused_computation.18 | convolution fusion | flops 268959744 | bytes 2097156 | tf_op jit(solution)/shard_map/jerb,jebc->jrc/dot_general | solution.py:155
  55.4 1.6 %gather_fusion.5 = bf16[4,512,256]{2,1,0:T(8,128)(2,1)} fusion(bf16[6,512,256]{2,1,0:T(8,128)(2,1)S(1)} %pad_maximum_fusion, s32[1024]{0:T(1024)S(1)} %get-tuple-element.84), kind=kCustom, calls=%fused_computation.2.clone | custom fusion | bytes 2097168 | tf_op jit(solution)/shard_map/jit(_take)/gather | solution.py:154
  57.0 2.8 %convolution_bitcast_fusion = f32[1,512,256]{2,1,0:T(8,128)} fusion(bf16[4,512,256]{2,1,0:T(8,128)(2,1)} %gather_fusion.5, pred[4]{0:T(512)(128)(4,1)S(1)} %copy-done.25, bf16[4,4,256,256]{3,2,1,0:T(8,128)(2,1)} %param.14), kind=kOutput, calls=%fused_computation.17 | convolution fusion | flops 268959744 | bytes 2097156 | tf_op jit(solution)/shard_map/jerb,jebc->jrc/dot_general | solution.py:155
  59.7 1.3 %constant_dynamic-update-slice_fusion = bf16[12,4,136,128]{3,2,1,0:T(8,128)(2,1)S(1)} fusion(bf16[12,4,136,128]{3,2,1,0:T(8,128)(2,1)S(1)} %copy-done.14, bf16[6,4,136,128]{3,2,1,0:T(8,128)(2,1)} %collective-permute-done.10), kind=kLoop, calls=%fused_computation.116 | loop fusion | bytes 1671168 | tf_op jit(solution)/shard_map/concatenate | solution.py:169
  63.1 1.9 %collective-permute-start.11 = (f32[4,1,1,1,1,2,16,128]{7,6,5,4,3,2,0,1:T(8,128)S(1)}, f32[4,1,1,1,1,2,16,128]{7,6,5,4,3,2,0,1:T(8,128)S(1)}, u32[]{:S(2)}, u32[]{:S(2)}) collective-permute-start(f32[4,1,1,1,1,2,16,128]{7,6,5,4,3,2,0,1:T(8,128)S(1)} %constant_dynamic-slice_fusion.5), channel_id=1, source_target_pairs={{0,8},{4,12},{8,0},{12,4},{16,24},{20,28},{24,16},{28,20},{1,9},{5... | collective-permute-start | bytes 196616 | tf_op jit(solution)/shard_map/ppermute | solution.py:98
  65.2 1.7 %collective-permute-done.13 = f32[4,1,1,2,1,1,16,128]{7,6,5,4,3,2,0,1:T(8,128)S(1)} collective-permute-done((f32[4,1,1,2,1,1,16,128]{7,6,5,4,3,2,0,1:T(8,128)S(1)}, f32[4,1,1,2,1,1,16,128]{7,6,5,4,3,2,0,1:T(8,128)S(1)}, u32[]{:S(2)}, u32[]{:S(2)}) %collective-permute-start.13) | collective-permute-done | bytes 65568 | tf_op jit(solution)/shard_map/ppermute | solution.py:98
  67.0 2.4 %collective-permute-done.12 = f32[4,1,2,1,1,1,16,128]{7,6,5,4,3,2,0,1:T(8,128)S(1)} collective-permute-done((f32[4,1,2,1,1,1,16,128]{7,6,5,4,3,2,0,1:T(8,128)S(1)}, f32[4,1,2,1,1,1,16,128]{7,6,5,4,3,2,0,1:T(8,128)S(1)}, u32[]{:S(2)}, u32[]{:S(2)}) %collective-permute-start.12) | collective-permute-done | bytes 65568 | tf_op jit(solution)/shard_map/ppermute | solution.py:98
  69.4 1.8 %collective-permute-start.14 = (f32[4,1,1,1,1,1,16,128]{7,6,5,4,3,2,0,1:T(8,128)S(1)}, f32[4,1,1,1,1,1,16,128]{7,6,5,4,3,2,0,1:T(8,128)S(1)}, u32[]{:S(2)}, u32[]{:S(2)}) collective-permute-start(f32[4,1,1,1,1,1,16,128]{7,6,5,4,3,2,0,1:T(8,128)S(1)} %constant_dynamic-slice_fusion.2), channel_id=1, source_target_pairs={{0,16},{4,20},{8,24},{12,28},{16,0},{20,4},{24,8},{28,12},{1,17},{... | collective-permute-start | bytes 98312 | tf_op jit(solution)/shard_map/ppermute | solution.py:98
  71.2 1.5 %collective-permute-start.15 = (f32[4,1,1,1,1,1,16,128]{7,6,5,4,3,2,0,1:T(8,128)S(1)}, f32[4,1,1,1,1,1,16,128]{7,6,5,4,3,2,0,1:T(8,128)S(1)}, u32[]{:S(2)}, u32[]{:S(2)}) collective-permute-start(f32[4,1,1,1,1,1,16,128]{7,6,5,4,3,2,0,1:T(8,128)S(1)} %constant_dynamic-slice_fusion.1), channel_id=1, source_target_pairs={{0,2},{1,3},{2,0},{3,1},{4,6},{5,7},{6,4},{7,5},{8,10},{9,11},{10,... | collective-permute-start | bytes 98312 | tf_op jit(solution)/shard_map/ppermute | solution.py:98
  75.2 1.5 %collective-permute-done.16 = f32[4,1,1,1,1,1,16,128]{7,6,5,4,3,2,0,1:T(8,128)S(1)} collective-permute-done((f32[4,1,1,1,1,1,16,128]{7,6,5,4,3,2,0,1:T(8,128)S(1)}, f32[4,1,1,1,1,1,16,128]{7,6,5,4,3,2,0,1:T(8,128)S(1)}, u32[]{:S(2)}, u32[]{:S(2)}) %collective-permute-start.16) | collective-permute-done | bytes 32800 | tf_op jit(solution)/shard_map/ppermute | solution.py:98
  77.3 1.8 %fusion.12 = bf16[12,16,128]{2,1,0:T(8,128)(2,1)S(1)} fusion(bf16[12,4,136,128]{3,2,1,0:T(8,128)(2,1)} %copy-done.15, bf16[12,4,16,128]{3,2,1,0:T(8,128)(2,1)S(1)} %bitcast.136, pred[12,4]{1,0:T(8,128)(4,1)S(1)} %copy.64), kind=kOutput, calls=%fused_computation.20 | convolution fusion | flops 25288704 | bytes 1818672 | tf_op jit(solution)/shard_map/nerc,necd->nrd/dot_general | solution.py:185
  81.6 1.8 %collective-permute-start.25 = (bf16[4,1,1,1,1,1,16,128]{7,6,0,5,4,3,2,1:T(8,128)(2,1)S(1)}, bf16[4,1,1,1,1,1,16,128]{7,6,0,5,4,3,2,1:T(8,128)(2,1)S(1)}, u32[]{:S(2)}, u32[]{:S(2)}) collective-permute-start(bf16[4,1,1,1,1,1,16,128]{7,6,0,5,4,3,2,1:T(8,128)(2,1)S(1)} %get-tuple-element.67), channel_id=1, source_target_pairs={{0,4},{4,0},{8,12},{12,8},{16,20},{20,16},{24,28},{28,24},{1,5},{5... | collective-permute-start | bytes 49160 | tf_op jit(solution)/shard_map/ppermute | solution.py:103
  84.5 1.7 %collective-permute-start.18 = (bf16[4,1,1,1,1,2,16,128]{7,6,0,5,4,3,2,1:T(8,128)(2,1)S(1)}, bf16[4,1,1,1,1,2,16,128]{7,6,0,5,4,3,2,1:T(8,128)(2,1)S(1)}, u32[]{:S(2)}, u32[]{:S(2)}) collective-permute-start(bf16[4,1,1,1,1,2,16,128]{7,6,0,5,4,3,2,1:T(8,128)(2,1)S(1)} %maximum_select_fusion.14), channel_id=1, source_target_pairs={{0,8},{4,12},{8,0},{12,4},{16,24},{20,28},{24,16},{28,20},{1,9},{5... | collective-permute-start | bytes 98312 | tf_op jit(solution)/shard_map/ppermute | solution.py:103
  89.4 2.1 %collective-permute-done.22 = bf16[4,1,2,1,1,1,16,128]{7,6,0,5,4,3,2,1:T(8,128)(2,1)S(1)} collective-permute-done((bf16[4,1,2,1,1,1,16,128]{7,6,0,5,4,3,2,1:T(8,128)(2,1)S(1)}, bf16[4,1,2,1,1,1,16,128]{7,6,0,5,4,3,2,1:T(8,128)(2,1)S(1)}, u32[]{:S(2)}, u32[]{:S(2)}) %collective-permute-start.22) | collective-permute-done | bytes 32800 | tf_op jit(solution)/shard_map/ppermute | solution.py:103
  91.7 1.8 %collective-permute-start.27 = (bf16[4,1,2,2,1,1,16,128]{7,6,0,5,4,3,2,1:T(8,128)(2,1)S(1)}, bf16[4,1,2,2,1,1,16,128]{7,6,0,5,4,3,2,1:T(8,128)(2,1)S(1)}, u32[]{:S(2)}, u32[]{:S(2)}) collective-permute-start(bf16[4,1,2,2,1,1,16,128]{7,6,0,5,4,3,2,1:T(8,128)(2,1)S(1)} %fusion.39), channel_id=1, source_target_pairs={{0,16},{4,20},{8,24},{12,28},{16,0},{20,4},{24,8},{28,12},{1,17},{... | collective-permute-start | bytes 196616 | tf_op jit(solution)/shard_map/ppermute | solution.py:103
  94.0 3.2 %collective-permute-done.23 = bf16[4,1,2,1,1,2,16,128]{7,6,0,5,4,3,2,1:T(8,128)(2,1)S(1)} collective-permute-done((bf16[4,1,2,1,1,2,16,128]{7,6,0,5,4,3,2,1:T(8,128)(2,1)S(1)}, bf16[4,1,2,1,1,2,16,128]{7,6,0,5,4,3,2,1:T(8,128)(2,1)S(1)}, u32[]{:S(2)}, u32[]{:S(2)}) %collective-permute-start.23) | collective-permute-done | bytes 65568 | tf_op jit(solution)/shard_map/ppermute | solution.py:103
  99.1 3.2 %collective-permute-done.24 = bf16[4,1,2,1,2,2,16,128]{7,6,0,5,4,3,2,1:T(8,128)(2,1)S(1)} collective-permute-done((bf16[4,1,2,1,2,2,16,128]{7,6,0,5,4,3,2,1:T(8,128)(2,1)S(1)}, bf16[4,1,2,1,2,2,16,128]{7,6,0,5,4,3,2,1:T(8,128)(2,1)S(1)}, u32[]{:S(2)}, u32[]{:S(2)}) %collective-permute-start.24) | collective-permute-done | bytes 131104 | tf_op jit(solution)/shard_map/ppermute | solution.py:103
  104.3 1.3 %collective-permute-done.29 = bf16[12,256,128]{2,1,0:T(8,128)(2,1)S(1)} collective-permute-done((bf16[12,256,128]{2,1,0:T(8,128)(2,1)S(1)}, bf16[12,256,128]{2,1,0:T(8,128)(2,1)S(1)}, u32[]{:S(2)}, u32[]{:S(2)}) %collective-permute-start.29) | collective-permute-done | bytes 786464 | tf_op jit(solution)/shard_map/ppermute | solution.py:194
  107.6 1.5 %fusion = bf16[4,512,256]{2,1,0:T(8,128)(2,1)} fusion(f32[1,512,256]{2,1,0:T(8,128)S(1)} %copy-done.29, f32[1,512,256]{2,1,0:T(8,128)S(1)} %copy-done.28, f32[2,512,256]{2,1,0:T(8,128)S(1)} %copy-done.30, bf16[4,2,256,128]{3,2,1,0:T(8,128)(2,1)S(1)} %copy-done.8, bf16[4,2,256,128]{3,2,1,0:T(8,128)(2,1)S(1)} %get-tuple-element.83, ...), kind=kOutput, calls=%fused_computation.9 | convolution fusion | flops 275251200 | bytes 4718593 | tf_op jit(solution)/shard_map/jqrc,jqbc->jrb/dot_general | solution.py:203
  (193 shorter events, 35.7 us)
Async XLA Ops:
  1.5 15.4 %copy-start = (s32[4]{0:T(128)S(1)}, s32[4]{0:T(128)}, u32[]{:S(2)}) copy-start(s32[4]{0:T(128)} %constant.322.clone) | copy-start | bytes 52
  6.6 19.6 %collective-permute-start.2 = (f32[12,256,128]{2,1,0:T(8,128)}, f32[12,256,128]{2,1,0:T(8,128)}, u32[]{:S(2)}, u32[]{:S(2)}) collective-permute-start(f32[12,256,128]{2,1,0:T(8,128)} %shard_map.83), channel_id=1, source_target_pairs={{0,1},{1,0},{2,3},{3,2},{4,5},{5,4},{6,7},{7,6},{8,9},{9,8},{10,11... | collective-permute-start | bytes 4718600 | tf_op jit(solution)/shard_map/ppermute | solution.py:137
  7.1 17.1 %collective-permute-start = (bf16[1,512,256]{2,1,0:T(8,128)(2,1)S(1)}, bf16[1,512,256]{2,1,0:T(8,128)(2,1)S(1)}, u32[]{:S(2)}, u32[]{:S(2)}) collective-permute-start(bf16[1,512,256]{2,1,0:T(8,128)(2,1)S(1)} %get-tuple-element.62), channel_id=1, source_target_pairs={{0,1},{1,2},{2,3},{3,4},{4,5},{5,6},{6,7},{7,8},{8,9},{9,10},{10,1... | collective-permute-start | bytes 786440 | tf_op jit(solution)/shard_map/ppermute | solution.py:65
  9.1 15.9 %collective-permute-start.1 = (bf16[1,512,256]{2,1,0:T(8,128)(2,1)S(1)}, bf16[1,512,256]{2,1,0:T(8,128)(2,1)}, u32[]{:S(2)}, u32[]{:S(2)}) collective-permute-start(bf16[1,512,256]{2,1,0:T(8,128)(2,1)S(1)} %get-tuple-element.63), channel_id=1, source_target_pairs={{1,0},{2,1},{3,2},{4,3},{5,4},{6,5},{7,6},{8,7},{9,8},{10,9},{11,1... | collective-permute-start | bytes 786440 | tf_op jit(solution)/shard_map/ppermute | solution.py:67
  11.9 16.6 %collective-permute-start.3 = (bf16[3,4,136,128]{3,2,1,0:T(8,128)(2,1)}, bf16[3,4,136,128]{3,2,1,0:T(8,128)(2,1)S(1)}, u32[]{:S(2)}, u32[]{:S(2)}) collective-permute-start(bf16[3,4,136,128]{3,2,1,0:T(8,128)(2,1)} %pad_maximum_fusion.3), channel_id=1, source_target_pairs={{0,2},{1,3},{2,0},{3,1},{4,6},{5,7},{6,4},{7,5},{8,10},{9,11},{10,... | collective-permute-start | bytes 1253384 | tf_op jit(solution)/shard_map/ppermute | solution.py:142
  30.2 13.0 %collective-permute-start.6 = (f32[4,1,2,2,1,2,16,128]{7,6,5,4,3,2,0,1:T(8,128)}, f32[4,1,2,2,1,2,16,128]{7,6,5,4,3,2,0,1:T(8,128)}, u32[]{:S(2)}, u32[]{:S(2)}) collective-permute-start(f32[4,1,2,2,1,2,16,128]{7,6,5,4,3,2,0,1:T(8,128)} %constant_dynamic-slice_fusion.9), channel_id=1, source_target_pairs={{0,8},{4,12},{8,0},{12,4},{16,24},{20,28},{24,16},{28,20},{1,9},{5... | collective-permute-start | bytes 786440 | tf_op jit(solution)/shard_map/ppermute | solution.py:98
  33.4 10.9 %collective-permute-start.5 = (f32[4,1,2,1,2,2,16,128]{7,6,5,4,3,2,0,1:T(8,128)}, f32[4,1,2,1,2,2,16,128]{7,6,5,4,3,2,0,1:T(8,128)}, u32[]{:S(2)}, u32[]{:S(2)}) collective-permute-start(f32[4,1,2,1,2,2,16,128]{7,6,5,4,3,2,0,1:T(8,128)} %constant_dynamic-slice_fusion.10), channel_id=1, source_target_pairs={{0,4},{4,0},{8,12},{12,8},{16,20},{20,16},{24,28},{28,24},{1,5},{5... | collective-permute-start | bytes 786440 | tf_op jit(solution)/shard_map/ppermute | solution.py:98
  35.1 10.3 %collective-permute-start.4 = (f32[4,1,1,2,2,2,16,128]{7,6,5,4,3,2,0,1:T(8,128)}, f32[4,1,1,2,2,2,16,128]{7,6,5,4,3,2,0,1:T(8,128)}, u32[]{:S(2)}, u32[]{:S(2)}) collective-permute-start(f32[4,1,1,2,2,2,16,128]{7,6,5,4,3,2,0,1:T(8,128)} %constant_dynamic-slice_fusion.11), channel_id=1, source_target_pairs={{0,2},{1,3},{2,0},{3,1},{4,6},{5,7},{6,4},{7,5},{8,10},{9,11},{10,... | collective-permute-start | bytes 786440 | tf_op jit(solution)/shard_map/ppermute | solution.py:98
  46.5 8.9 %collective-permute-start.9 = (f32[4,1,2,2,1,1,16,128]{7,6,5,4,3,2,0,1:T(8,128)S(1)}, f32[4,1,2,2,1,1,16,128]{7,6,5,4,3,2,0,1:T(8,128)S(1)}, u32[]{:S(2)}, u32[]{:S(2)}) collective-permute-start(f32[4,1,2,2,1,1,16,128]{7,6,5,4,3,2,0,1:T(8,128)S(1)} %constant_dynamic-slice_fusion.6), channel_id=1, source_target_pairs={{0,16},{4,20},{8,24},{12,28},{16,0},{20,4},{24,8},{28,12},{1,17},{... | collective-permute-start | bytes 393224 | tf_op jit(solution)/shard_map/ppermute | solution.py:98
  47.6 7.6 %collective-permute-start.8 = (f32[4,1,2,1,1,2,16,128]{7,6,5,4,3,2,0,1:T(8,128)S(1)}, f32[4,1,2,1,1,2,16,128]{7,6,5,4,3,2,0,1:T(8,128)S(1)}, u32[]{:S(2)}, u32[]{:S(2)}) collective-permute-start(f32[4,1,2,1,1,2,16,128]{7,6,5,4,3,2,0,1:T(8,128)S(1)} %constant_dynamic-slice_fusion.7), channel_id=1, source_target_pairs={{0,8},{4,12},{8,0},{12,4},{16,24},{20,28},{24,16},{28,20},{1,9},{5... | collective-permute-start | bytes 393224 | tf_op jit(solution)/shard_map/ppermute | solution.py:98
  49.7 5.6 %collective-permute-start.7 = (f32[4,1,1,1,2,2,16,128]{7,6,5,4,3,2,0,1:T(8,128)S(1)}, f32[4,1,1,1,2,2,16,128]{7,6,5,4,3,2,0,1:T(8,128)S(1)}, u32[]{:S(2)}, u32[]{:S(2)}) collective-permute-start(f32[4,1,1,1,2,2,16,128]{7,6,5,4,3,2,0,1:T(8,128)S(1)} %constant_dynamic-slice_fusion.8), channel_id=1, source_target_pairs={{0,4},{4,0},{8,12},{12,8},{16,20},{20,16},{24,28},{28,24},{1,5},{5... | collective-permute-start | bytes 393224 | tf_op jit(solution)/shard_map/ppermute | solution.py:98
  49.9 9.8 %collective-permute-start.10 = (bf16[6,4,136,128]{3,2,1,0:T(8,128)(2,1)S(1)}, bf16[6,4,136,128]{3,2,1,0:T(8,128)(2,1)}, u32[]{:S(2)}, u32[]{:S(2)}) collective-permute-start(bf16[6,4,136,128]{3,2,1,0:T(8,128)(2,1)S(1)} %pad_maximum_fusion.1), channel_id=1, source_target_pairs={{0,1},{1,0},{2,3},{3,2},{4,5},{5,4},{6,7},{7,6},{8,9},{9,8},{10,11... | collective-permute-start | bytes 2506760 | tf_op jit(solution)/shard_map/ppermute | solution.py:174
  62.2 17.4 %copy-start.24 = (pred[12]{0:T(512)(128)(4,1)S(1)}, pred[12]{0:T(512)(128)(4,1)}, u32[]{:S(2)}) copy-start(pred[12]{0:T(512)(128)(4,1)} %compare_and_fusion.2) | copy-start | bytes 40
  62.4 4.6 %collective-permute-start.13 = (f32[4,1,1,2,1,1,16,128]{7,6,5,4,3,2,0,1:T(8,128)S(1)}, f32[4,1,1,2,1,1,16,128]{7,6,5,4,3,2,0,1:T(8,128)S(1)}, u32[]{:S(2)}, u32[]{:S(2)}) collective-permute-start(f32[4,1,1,2,1,1,16,128]{7,6,5,4,3,2,0,1:T(8,128)S(1)} %constant_dynamic-slice_fusion.3), channel_id=1, source_target_pairs={{0,2},{1,3},{2,0},{3,1},{4,6},{5,7},{6,4},{7,5},{8,10},{9,11},{10,... | collective-permute-start | bytes 196616 | tf_op jit(solution)/shard_map/ppermute | solution.py:98
  63.0 6.3 %collective-permute-start.12 = (f32[4,1,2,1,1,1,16,128]{7,6,5,4,3,2,0,1:T(8,128)S(1)}, f32[4,1,2,1,1,1,16,128]{7,6,5,4,3,2,0,1:T(8,128)S(1)}, u32[]{:S(2)}, u32[]{:S(2)}) collective-permute-start(f32[4,1,2,1,1,1,16,128]{7,6,5,4,3,2,0,1:T(8,128)S(1)} %constant_dynamic-slice_fusion.4), channel_id=1, source_target_pairs={{0,16},{4,20},{8,24},{12,28},{16,0},{20,4},{24,8},{28,12},{1,17},{... | collective-permute-start | bytes 196616 | tf_op jit(solution)/shard_map/ppermute | solution.py:98
  63.1 6.3 %collective-permute-start.11 = (f32[4,1,1,1,1,2,16,128]{7,6,5,4,3,2,0,1:T(8,128)S(1)}, f32[4,1,1,1,1,2,16,128]{7,6,5,4,3,2,0,1:T(8,128)S(1)}, u32[]{:S(2)}, u32[]{:S(2)}) collective-permute-start(f32[4,1,1,1,1,2,16,128]{7,6,5,4,3,2,0,1:T(8,128)S(1)} %constant_dynamic-slice_fusion.5), channel_id=1, source_target_pairs={{0,8},{4,12},{8,0},{12,4},{16,24},{20,28},{24,16},{28,20},{1,9},{5... | collective-permute-start | bytes 196616 | tf_op jit(solution)/shard_map/ppermute | solution.py:98
  69.4 4.9 %collective-permute-start.14 = (f32[4,1,1,1,1,1,16,128]{7,6,5,4,3,2,0,1:T(8,128)S(1)}, f32[4,1,1,1,1,1,16,128]{7,6,5,4,3,2,0,1:T(8,128)S(1)}, u32[]{:S(2)}, u32[]{:S(2)}) collective-permute-start(f32[4,1,1,1,1,1,16,128]{7,6,5,4,3,2,0,1:T(8,128)S(1)} %constant_dynamic-slice_fusion.2), channel_id=1, source_target_pairs={{0,16},{4,20},{8,24},{12,28},{16,0},{20,4},{24,8},{28,12},{1,17},{... | collective-permute-start | bytes 98312 | tf_op jit(solution)/shard_map/ppermute | solution.py:98
  71.2 3.9 %collective-permute-start.15 = (f32[4,1,1,1,1,1,16,128]{7,6,5,4,3,2,0,1:T(8,128)S(1)}, f32[4,1,1,1,1,1,16,128]{7,6,5,4,3,2,0,1:T(8,128)S(1)}, u32[]{:S(2)}, u32[]{:S(2)}) collective-permute-start(f32[4,1,1,1,1,1,16,128]{7,6,5,4,3,2,0,1:T(8,128)S(1)} %constant_dynamic-slice_fusion.1), channel_id=1, source_target_pairs={{0,2},{1,3},{2,0},{3,1},{4,6},{5,7},{6,4},{7,5},{8,10},{9,11},{10,... | collective-permute-start | bytes 98312 | tf_op jit(solution)/shard_map/ppermute | solution.py:98
  72.7 3.9 %collective-permute-start.16 = (f32[4,1,1,1,1,1,16,128]{7,6,5,4,3,2,0,1:T(8,128)S(1)}, f32[4,1,1,1,1,1,16,128]{7,6,5,4,3,2,0,1:T(8,128)S(1)}, u32[]{:S(2)}, u32[]{:S(2)}) collective-permute-start(f32[4,1,1,1,1,1,16,128]{7,6,5,4,3,2,0,1:T(8,128)S(1)} %constant_dynamic-slice_fusion), channel_id=1, source_target_pairs={{0,4},{4,0},{8,12},{12,8},{16,20},{20,16},{24,28},{28,24},{1,5},{5... | collective-permute-start | bytes 98312 | tf_op jit(solution)/shard_map/ppermute | solution.py:98
  79.7 4.7 %collective-permute-start.17 = (bf16[4,1,1,1,1,1,16,128]{7,6,0,5,4,3,2,1:T(8,128)(2,1)S(1)}, bf16[4,1,1,1,1,1,16,128]{7,6,0,5,4,3,2,1:T(8,128)(2,1)S(1)}, u32[]{:S(2)}, u32[]{:S(2)}) collective-permute-start(bf16[4,1,1,1,1,1,16,128]{7,6,0,5,4,3,2,1:T(8,128)(2,1)S(1)} %get-tuple-element.65), channel_id=1, source_target_pairs={{0,16},{4,20},{8,24},{12,28},{16,0},{20,4},{24,8},{28,12},{1,17},{... | collective-permute-start | bytes 49160 | tf_op jit(solution)/shard_map/ppermute | solution.py:103
  80.9 5.2 %collective-permute-start.21 = (bf16[4,1,1,1,1,1,16,128]{7,6,0,5,4,3,2,1:T(8,128)(2,1)S(1)}, bf16[4,1,1,1,1,1,16,128]{7,6,0,5,4,3,2,1:T(8,128)(2,1)S(1)}, u32[]{:S(2)}, u32[]{:S(2)}) collective-permute-start(bf16[4,1,1,1,1,1,16,128]{7,6,0,5,4,3,2,1:T(8,128)(2,1)S(1)} %get-tuple-element.66), channel_id=1, source_target_pairs={{0,2},{1,3},{2,0},{3,1},{4,6},{5,7},{6,4},{7,5},{8,10},{9,11},{10,... | collective-permute-start | bytes 49160 | tf_op jit(solution)/shard_map/ppermute | solution.py:103
  81.6 5.4 %collective-permute-start.25 = (bf16[4,1,1,1,1,1,16,128]{7,6,0,5,4,3,2,1:T(8,128)(2,1)S(1)}, bf16[4,1,1,1,1,1,16,128]{7,6,0,5,4,3,2,1:T(8,128)(2,1)S(1)}, u32[]{:S(2)}, u32[]{:S(2)}) collective-permute-start(bf16[4,1,1,1,1,1,16,128]{7,6,0,5,4,3,2,1:T(8,128)(2,1)S(1)} %get-tuple-element.67), channel_id=1, source_target_pairs={{0,4},{4,0},{8,12},{12,8},{16,20},{20,16},{24,28},{28,24},{1,5},{5... | collective-permute-start | bytes 49160 | tf_op jit(solution)/shard_map/ppermute | solution.py:103
  84.5 4.0 %collective-permute-start.18 = (bf16[4,1,1,1,1,2,16,128]{7,6,0,5,4,3,2,1:T(8,128)(2,1)S(1)}, bf16[4,1,1,1,1,2,16,128]{7,6,0,5,4,3,2,1:T(8,128)(2,1)S(1)}, u32[]{:S(2)}, u32[]{:S(2)}) collective-permute-start(bf16[4,1,1,1,1,2,16,128]{7,6,0,5,4,3,2,1:T(8,128)(2,1)S(1)} %maximum_select_fusion.14), channel_id=1, source_target_pairs={{0,8},{4,12},{8,0},{12,4},{16,24},{20,28},{24,16},{28,20},{1,9},{5... | collective-permute-start | bytes 98312 | tf_op jit(solution)/shard_map/ppermute | solution.py:103
  86.1 5.4 %collective-permute-start.22 = (bf16[4,1,2,1,1,1,16,128]{7,6,0,5,4,3,2,1:T(8,128)(2,1)S(1)}, bf16[4,1,2,1,1,1,16,128]{7,6,0,5,4,3,2,1:T(8,128)(2,1)S(1)}, u32[]{:S(2)}, u32[]{:S(2)}) collective-permute-start(bf16[4,1,2,1,1,1,16,128]{7,6,0,5,4,3,2,1:T(8,128)(2,1)S(1)} %maximum_select_fusion.16), channel_id=1, source_target_pairs={{0,16},{4,20},{8,24},{12,28},{16,0},{20,4},{24,8},{28,12},{1,17},{... | collective-permute-start | bytes 98312 | tf_op jit(solution)/shard_map/ppermute | solution.py:103
  87.0 4.7 %collective-permute-start.26 = (bf16[4,1,1,2,1,1,16,128]{7,6,0,5,4,3,2,1:T(8,128)(2,1)S(1)}, bf16[4,1,1,2,1,1,16,128]{7,6,0,5,4,3,2,1:T(8,128)(2,1)S(1)}, u32[]{:S(2)}, u32[]{:S(2)}) collective-permute-start(bf16[4,1,1,2,1,1,16,128]{7,6,0,5,4,3,2,1:T(8,128)(2,1)S(1)} %maximum_select_fusion.18), channel_id=1, source_target_pairs={{0,2},{1,3},{2,0},{3,1},{4,6},{5,7},{6,4},{7,5},{8,10},{9,11},{10,... | collective-permute-start | bytes 98312 | tf_op jit(solution)/shard_map/ppermute | solution.py:103
  88.4 5.2 %collective-permute-start.19 = (bf16[4,1,1,1,2,2,16,128]{7,6,0,5,4,3,2,1:T(8,128)(2,1)S(1)}, bf16[4,1,1,1,2,2,16,128]{7,6,0,5,4,3,2,1:T(8,128)(2,1)S(1)}, u32[]{:S(2)}, u32[]{:S(2)}) collective-permute-start(bf16[4,1,1,1,2,2,16,128]{7,6,0,5,4,3,2,1:T(8,128)(2,1)S(1)} %maximum_select_fusion.9), channel_id=1, source_target_pairs={{0,4},{4,0},{8,12},{12,8},{16,20},{20,16},{24,28},{28,24},{1,5},{5... | collective-permute-start | bytes 196616 | tf_op jit(solution)/shard_map/ppermute | solution.py:103
  91.6 5.6 %collective-permute-start.23 = (bf16[4,1,2,1,1,2,16,128]{7,6,0,5,4,3,2,1:T(8,128)(2,1)S(1)}, bf16[4,1,2,1,1,2,16,128]{7,6,0,5,4,3,2,1:T(8,128)(2,1)S(1)}, u32[]{:S(2)}, u32[]{:S(2)}) collective-permute-start(bf16[4,1,2,1,1,2,16,128]{7,6,0,5,4,3,2,1:T(8,128)(2,1)S(1)} %maximum_select_fusion.11), channel_id=1, source_target_pairs={{0,8},{4,12},{8,0},{12,4},{16,24},{20,28},{24,16},{28,20},{1,9},{5... | collective-permute-start | bytes 196616 | tf_op jit(solution)/shard_map/ppermute | solution.py:103
  91.7 6.3 %collective-permute-start.27 = (bf16[4,1,2,2,1,1,16,128]{7,6,0,5,4,3,2,1:T(8,128)(2,1)S(1)}, bf16[4,1,2,2,1,1,16,128]{7,6,0,5,4,3,2,1:T(8,128)(2,1)S(1)}, u32[]{:S(2)}, u32[]{:S(2)}) collective-permute-start(bf16[4,1,2,2,1,1,16,128]{7,6,0,5,4,3,2,1:T(8,128)(2,1)S(1)} %fusion.39), channel_id=1, source_target_pairs={{0,16},{4,20},{8,24},{12,28},{16,0},{20,4},{24,8},{28,12},{1,17},{... | collective-permute-start | bytes 196616 | tf_op jit(solution)/shard_map/ppermute | solution.py:103
  93.6 5.4 %collective-permute-start.20 = (bf16[4,1,1,2,2,2,16,128]{7,6,0,5,4,3,2,1:T(8,128)(2,1)S(1)}, bf16[4,1,1,2,2,2,16,128]{7,6,0,5,4,3,2,1:T(8,128)(2,1)S(1)}, u32[]{:S(2)}, u32[]{:S(2)}) collective-permute-start(bf16[4,1,1,2,2,2,16,128]{7,6,0,5,4,3,2,1:T(8,128)(2,1)S(1)} %maximum_select_fusion.5), channel_id=1, source_target_pairs={{0,2},{1,3},{2,0},{3,1},{4,6},{5,7},{6,4},{7,5},{8,10},{9,11},{10,... | collective-permute-start | bytes 393224 | tf_op jit(solution)/shard_map/ppermute | solution.py:103
  97.3 5.0 %collective-permute-start.24 = (bf16[4,1,2,1,2,2,16,128]{7,6,0,5,4,3,2,1:T(8,128)(2,1)S(1)}, bf16[4,1,2,1,2,2,16,128]{7,6,0,5,4,3,2,1:T(8,128)(2,1)S(1)}, u32[]{:S(2)}, u32[]{:S(2)}) collective-permute-start(bf16[4,1,2,1,2,2,16,128]{7,6,0,5,4,3,2,1:T(8,128)(2,1)S(1)} %maximum_select_fusion.6), channel_id=1, source_target_pairs={{0,4},{4,0},{8,12},{12,8},{16,20},{20,16},{24,28},{28,24},{1,5},{5... | collective-permute-start | bytes 393224 | tf_op jit(solution)/shard_map/ppermute | solution.py:103
  98.0 5.0 %collective-permute-start.28 = (bf16[4,1,2,2,1,2,16,128]{7,6,0,5,4,3,2,1:T(8,128)(2,1)S(1)}, bf16[4,1,2,2,1,2,16,128]{7,6,0,5,4,3,2,1:T(8,128)(2,1)S(1)}, u32[]{:S(2)}, u32[]{:S(2)}) collective-permute-start(bf16[4,1,2,2,1,2,16,128]{7,6,0,5,4,3,2,1:T(8,128)(2,1)S(1)} %maximum_select_fusion.7), channel_id=1, source_target_pairs={{0,8},{4,12},{8,0},{12,4},{16,24},{20,28},{24,16},{28,20},{1,9},{5... | collective-permute-start | bytes 393224 | tf_op jit(solution)/shard_map/ppermute | solution.py:103
  103.2 2.4 %collective-permute-start.29 = (bf16[12,256,128]{2,1,0:T(8,128)(2,1)S(1)}, bf16[12,256,128]{2,1,0:T(8,128)(2,1)S(1)}, u32[]{:S(2)}, u32[]{:S(2)}) collective-permute-start(bf16[12,256,128]{2,1,0:T(8,128)(2,1)S(1)} %pad_maximum_fusion.2), channel_id=1, source_target_pairs={{0,1},{1,0},{2,3},{3,2},{4,5},{5,4},{6,7},{7,6},{8,9},{9,8},{10,11... | collective-permute-start | bytes 2359304 | tf_op jit(solution)/shard_map/ppermute | solution.py:194
  (29 other events, 124.1 us)

commit v22 on v20

--- a/solution.py
+++ b/solution.py
@@ -145,7 +145,7 @@
     packed = jnp.concatenate([packed, arriving], axis=0)
     arriving = None
     parts = [lax.slice_in_dim(whole, s * per, (s + 1) * per, axis=0) for s in range(streams)]
-    split_at = margin.shape[0] // 2
+    split_at = (3 * margin.shape[0]) // 4
     picked = jnp.take(extended, margin[:split_at], axis=0)
     local = [jnp.einsum("jerb,jebc->jrc", picked, inverse_blocks[:split_at], preferred_element_type=jnp.float32)]
     for step in range(1, nb):

time: 106 us -> 104 us (0.981)
  local copies, waits for them, and re-layouts: 19.7 us -> 18 us
  other arithmetic: 8.23 us -> 9.86 us
  matrix products: 10.6 us -> 9.19 us
    dot_general x1, matrix products: 1.78 us -> 0.37 us  [per_device(): jnp.einsum('nerc,necd->nrd', chosen, inverse_all, preferred_element_type=...]
    unnamed x55 -> x53, local copies, waits for them, and re-layouts: 4.88 us -> 4.71 us
  transfers between devices with their start and end apart: 30 -> 30, of which waited for: 14 -> 15; matrix products, arithmetic and copies ran while one was open for 22% -> 24% of each run, Pallas kernels for 5% -> 5%
where the time goes in v22:
time: 104 us; the launch traced here: 103 us
  starting transfers between devices  35.7 us (34%)
  waiting for transfers between devices  19.2 us (18%)
  local copies, waits for them, and re-layouts  18 us (17%)
  Pallas kernels  10.3 us (10%)
  other arithmetic  9.86 us (9%)
  matrix products  9.19 us (9%)
    ppermute x12, starting transfers between devices, halve(): lax.ppermute(send.astype(wire), axis, pairs(axis, mask)).astype(x.dtype)  14.6 us
    ppermute x12, starting transfers between devices, double(): recv = lax.ppermute(y, axis, pairs(axis, mask))  12.5 us
    pallas_call x2, Pallas kernels, restrict(): pl.pallas_call(functools.partial(restrict_kernel, upper=upper), out_shape...  10.3 us
    ppermute x12, waiting for transfers between devices, double(): recv = lax.ppermute(y, axis, pairs(axis, mask))  9.71 us
    ppermute x12, waiting for transfers between devices, halve(): lax.ppermute(send.astype(wire), axis, pairs(axis, mask)).astype(x.dtype)  7.06 us
    unnamed x53, local copies, waits for them, and re-layouts  4.71 us
    dot_general x1, matrix products, per_device(): jnp.einsum('jerb,jebc->jrc', picked, inverse_blocks[:split_at], preferred...  4.6 us
    ppermute x1, starting transfers between devices, per_device(): arriving = lax.ppermute(packed, exchanges[0][0], pairs(*exchanges[0]))  4.14 us
  transfers between devices with their start and end apart: 30, of which 15 were waited for; matrix products, arithmetic and copies ran while one was open for 24% of the time, Pallas kernels for 5%

profile of v22, /device:TPU:0, one launch (start us, length us, event | category | flops | bytes accessed | tf_op | source)
XLA Modules:
  0.0 102.9 jit_solution(2623860560475301691)
XLA Ops:
  1.5 5.1 %shard_map.83 = f32[12,256,128]{2,1,0:T(8,128)} custom-call(s32[8]{0:T(128)} %reshape.1794.links, s32[1]{0:T(128)} %bitcast.half, bf16[4,512,256]{2,1,0:T(8,128)(2,1)} %residual_ref.3, bf16[4,2,256,128]{3,2,1,0:T(8,128)(2,1)} %basis_ref.3), custom_call_target="tpu_custom_call" | custom-call | flops 134217728 | bytes 3145728 | tf_op jit(solution)/shard_map/pallas_call | solution.py:36
  7.1 2.7 %collective-permute-start = (bf16[1,512,256]{2,1,0:T(8,128)(2,1)S(1)}, bf16[1,512,256]{2,1,0:T(8,128)(2,1)}, u32[]{:S(2)}, u32[]{:S(2)}) collective-permute-start(bf16[1,512,256]{2,1,0:T(8,128)(2,1)S(1)} %get-tuple-element.51), channel_id=1, source_target_pairs={{0,1},{1,2},{2,3},{3,4},{4,5},{5,6},{6,7},{7,8},{8,9},{9,10},{10,1... | collective-permute-start | bytes 786440 | tf_op jit(solution)/shard_map/ppermute | solution.py:65
  9.8 1.3 %collective-permute-start.1 = (bf16[1,512,256]{2,1,0:T(8,128)(2,1)S(1)}, bf16[1,512,256]{2,1,0:T(8,128)(2,1)}, u32[]{:S(2)}, u32[]{:S(2)}) collective-permute-start(bf16[1,512,256]{2,1,0:T(8,128)(2,1)S(1)} %get-tuple-element.52), channel_id=1, source_target_pairs={{1,0},{2,1},{3,2},{4,3},{5,4},{6,5},{7,6},{8,7},{9,8},{10,9},{11,1... | collective-permute-start | bytes 786440 | tf_op jit(solution)/shard_map/ppermute | solution.py:67
  12.0 4.1 %collective-permute-start.3 = (bf16[3,4,136,128]{3,2,1,0:T(8,128)(2,1)}, bf16[3,4,136,128]{3,2,1,0:T(8,128)(2,1)S(1)}, u32[]{:S(2)}, u32[]{:S(2)}) collective-permute-start(bf16[3,4,136,128]{3,2,1,0:T(8,128)(2,1)} %pad_maximum_fusion.3), channel_id=1, source_target_pairs={{0,2},{1,3},{2,0},{3,1},{4,6},{5,7},{6,4},{7,5},{8,10},{9,11},{10,... | collective-permute-start | bytes 1253384 | tf_op jit(solution)/shard_map/ppermute | solution.py:142
  18.7 5.2 %shard_map.82 = f32[12,256,128]{2,1,0:T(8,128)} custom-call(s32[8]{0:T(128)} %reshape.1794.links, s32[1]{0:T(128)} %bitcast.half, bf16[4,512,256]{2,1,0:T(8,128)(2,1)} %residual_ref.3, bf16[4,2,256,128]{3,2,1,0:T(8,128)(2,1)} %basis_ref.3), custom_call_target="tpu_custom_call" | custom-call | flops 134217728 | bytes 3145728 | tf_op jit(solution)/shard_map/pallas_call | solution.py:36
  24.5 1.2 %pad_maximum_fusion = bf16[6,512,256]{2,1,0:T(8,128)(2,1)S(1)} fusion(bf16[1,512,256]{2,1,0:T(8,128)(2,1)} %collective-permute-done.1, bf16[4,512,256]{2,1,0:T(8,128)(2,1)S(1)} %copy-done.2, bf16[1,512,256]{2,1,0:T(8,128)(2,1)} %collective-permute-done), kind=kLoop, calls=%fused_computation.14 | loop fusion | flops 1572864 | bytes 3145728 | tf_op jit(solution)/shard_map/concatenate | solution.py:63
  25.7 1.6 %add.237 = f32[12,256,128]{2,1,0:T(8,128)S(1)} add(f32[12,256,128]{2,1,0:T(8,128)S(1)} %copy-done.3, f32[12,256,128]{2,1,0:T(8,128)} %collective-permute-done.2) | non-fusion elementwise | flops 393216 | bytes 4718592 | tf_op jit(solution)/shard_map/add | solution.py:138
  30.2 2.4 %collective-permute-start.6 = (f32[4,1,2,2,1,2,16,128]{7,6,5,4,3,2,0,1:T(8,128)}, f32[4,1,2,2,1,2,16,128]{7,6,5,4,3,2,0,1:T(8,128)}, u32[]{:S(2)}, u32[]{:S(2)}) collective-permute-start(f32[4,1,2,2,1,2,16,128]{7,6,5,4,3,2,0,1:T(8,128)} %constant_dynamic-slice_fusion.9), channel_id=1, source_target_pairs={{0,8},{4,12},{8,0},{12,4},{16,24},{20,28},{24,16},{28,20},{1,9},{5... | collective-permute-start | bytes 786440 | tf_op jit(solution)/shard_map/ppermute | solution.py:98
  34.8 2.1 %collective-permute-start.4 = (f32[4,1,1,2,2,2,16,128]{7,6,5,4,3,2,0,1:T(8,128)}, f32[4,1,1,2,2,2,16,128]{7,6,5,4,3,2,0,1:T(8,128)}, u32[]{:S(2)}, u32[]{:S(2)}) collective-permute-start(f32[4,1,1,2,2,2,16,128]{7,6,5,4,3,2,0,1:T(8,128)} %constant_dynamic-slice_fusion.11), channel_id=1, source_target_pairs={{0,2},{1,3},{2,0},{3,1},{4,6},{5,7},{6,4},{7,5},{8,10},{9,11},{10,... | collective-permute-start | bytes 786440 | tf_op jit(solution)/shard_map/ppermute | solution.py:98
  36.8 2.5 %gather_fusion = bf16[12,512,256]{2,1,0:T(8,128)(2,1)} fusion(bf16[6,512,256]{2,1,0:T(8,128)(2,1)S(1)} %pad_maximum_fusion, s32[1024]{0:T(1024)S(1)} %pad_clamp_fusion.5), kind=kCustom, calls=%fused_computation.2 | custom fusion | bytes 6291504 | tf_op jit(solution)/shard_map/jit(_take)/gather | solution.py:149
  39.3 4.6 %fusion.8 = f32[3,512,256]{2,1,0:T(8,128)} fusion(bf16[4,4,256,256]{3,2,1,0:T(8,128)(2,1)} %param.12, bf16[3,4,512,256]{3,2,1,0:T(8,128)(2,1)} %bitcast.100, pred[3,4]{1,0:T(4,128)(4,1)S(1)} %compare_and_fusion.3), kind=kOutput, calls=%fused_computation.17 | convolution fusion | flops 806879232 | bytes 6291468 | tf_op jit(solution)/shard_map/jerb,jebc->jrc/dot_general | solution.py:150
  49.2 2.0 %collective-permute-start.8 = (f32[4,1,2,1,1,2,16,128]{7,6,5,4,3,2,0,1:T(8,128)S(1)}, f32[4,1,2,1,1,2,16,128]{7,6,5,4,3,2,0,1:T(8,128)S(1)}, u32[]{:S(2)}, u32[]{:S(2)}) collective-permute-start(f32[4,1,2,1,1,2,16,128]{7,6,5,4,3,2,0,1:T(8,128)S(1)} %constant_dynamic-slice_fusion.7), channel_id=1, source_target_pairs={{0,8},{4,12},{8,0},{12,4},{16,24},{20,28},{24,16},{28,20},{1,9},{5... | collective-permute-start | bytes 393224 | tf_op jit(solution)/shard_map/ppermute | solution.py:98
  52.4 1.7 %gather_fusion.1 = bf16[4,512,256]{2,1,0:T(8,128)(2,1)} fusion(bf16[6,512,256]{2,1,0:T(8,128)(2,1)S(1)} %pad_maximum_fusion, s32[1024]{0:T(1024)} %pad_clamp_fusion.4), kind=kCustom, calls=%fused_computation.3 | custom fusion | bytes 2097168 | tf_op jit(solution)/shard_map/jit(_take)/gather | solution.py:155
  54.1 2.7 %convolution_bitcast_fusion = f32[1,512,256]{2,1,0:T(8,128)} fusion(bf16[4,512,256]{2,1,0:T(8,128)(2,1)} %gather_fusion.1, pred[4]{0:T(512)(128)(4,1)S(1)} %copy-done.22, bf16[4,4,256,256]{3,2,1,0:T(8,128)(2,1)} %param.12), kind=kOutput, calls=%fused_computation.18 | convolution fusion | flops 268959744 | bytes 2097156 | tf_op jit(solution)/shard_map/jerb,jebc->jrc/dot_general | solution.py:156
  57.9 1.3 %constant_dynamic-update-slice_fusion = bf16[12,4,136,128]{3,2,1,0:T(8,128)(2,1)S(1)} fusion(bf16[12,4,136,128]{3,2,1,0:T(8,128)(2,1)S(1)} %constant_dynamic-update-slice_fusion.1, bf16[6,4,136,128]{3,2,1,0:T(8,128)(2,1)} %collective-permute-done.10), kind=kLoop, calls=%fused_computation.107 | loop fusion | bytes 1671168 | tf_op jit(solution)/shard_map/concatenate | solution.py:162
  59.3 1.6 %collective-permute-start.11 = (f32[4,1,1,1,1,2,16,128]{7,6,5,4,3,2,0,1:T(8,128)S(1)}, f32[4,1,1,1,1,2,16,128]{7,6,5,4,3,2,0,1:T(8,128)S(1)}, u32[]{:S(2)}, u32[]{:S(2)}) collective-permute-start(f32[4,1,1,1,1,2,16,128]{7,6,5,4,3,2,0,1:T(8,128)S(1)} %constant_dynamic-slice_fusion.5), channel_id=1, source_target_pairs={{0,8},{4,12},{8,0},{12,4},{16,24},{20,28},{24,16},{28,20},{1,9},{5... | collective-permute-start | bytes 196616 | tf_op jit(solution)/shard_map/ppermute | solution.py:98
  62.5 1.4 %collective-permute-done.11 = f32[4,1,1,1,1,2,16,128]{7,6,5,4,3,2,0,1:T(8,128)S(1)} collective-permute-done((f32[4,1,1,1,1,2,16,128]{7,6,5,4,3,2,0,1:T(8,128)S(1)}, f32[4,1,1,1,1,2,16,128]{7,6,5,4,3,2,0,1:T(8,128)S(1)}, u32[]{:S(2)}, u32[]{:S(2)}) %collective-permute-start.11) | collective-permute-done | bytes 65568 | tf_op jit(solution)/shard_map/ppermute | solution.py:98
  63.9 1.3 %collective-permute-start.12 = (f32[4,1,1,1,1,1,16,128]{7,6,5,4,3,2,0,1:T(8,128)S(1)}, f32[4,1,1,1,1,1,16,128]{7,6,5,4,3,2,0,1:T(8,128)S(1)}, u32[]{:S(2)}, u32[]{:S(2)}) collective-permute-start(f32[4,1,1,1,1,1,16,128]{7,6,5,4,3,2,0,1:T(8,128)S(1)} %constant_dynamic-slice_fusion.4), channel_id=1, source_target_pairs={{0,16},{4,20},{8,24},{12,28},{16,0},{20,4},{24,8},{28,12},{1,17},{... | collective-permute-start | bytes 98312 | tf_op jit(solution)/shard_map/ppermute | solution.py:98
  65.2 2.2 %collective-permute-done.13 = f32[4,1,2,1,1,1,16,128]{7,6,5,4,3,2,0,1:T(8,128)S(1)} collective-permute-done((f32[4,1,2,1,1,1,16,128]{7,6,5,4,3,2,0,1:T(8,128)S(1)}, f32[4,1,2,1,1,1,16,128]{7,6,5,4,3,2,0,1:T(8,128)S(1)}, u32[]{:S(2)}, u32[]{:S(2)}) %collective-permute-start.13) | collective-permute-done | bytes 65568 | tf_op jit(solution)/shard_map/ppermute | solution.py:98
  69.2 2.2 %collective-permute-done.14 = f32[4,1,1,1,1,1,16,128]{7,6,5,4,3,2,0,1:T(8,128)S(1)} collective-permute-done((f32[4,1,1,1,1,1,16,128]{7,6,5,4,3,2,0,1:T(8,128)S(1)}, f32[4,1,1,1,1,1,16,128]{7,6,5,4,3,2,0,1:T(8,128)S(1)}, u32[]{:S(2)}, u32[]{:S(2)}) %collective-permute-start.14) | collective-permute-done | bytes 32800 | tf_op jit(solution)/shard_map/ppermute | solution.py:98
  75.8 1.9 %collective-permute-start.25 = (bf16[4,1,1,1,1,1,16,128]{7,6,0,5,4,3,2,1:T(8,128)(2,1)S(1)}, bf16[4,1,1,1,1,1,16,128]{7,6,0,5,4,3,2,1:T(8,128)(2,1)S(1)}, u32[]{:S(2)}, u32[]{:S(2)}) collective-permute-start(bf16[4,1,1,1,1,1,16,128]{7,6,0,5,4,3,2,1:T(8,128)(2,1)S(1)} %get-tuple-element.56), channel_id=1, source_target_pairs={{0,4},{4,0},{8,12},{12,8},{16,20},{20,16},{24,28},{28,24},{1,5},{5... | collective-permute-start | bytes 49160 | tf_op jit(solution)/shard_map/ppermute | solution.py:103
  77.7 1.3 %collective-permute-done.17 = bf16[4,1,1,1,1,1,16,128]{7,6,0,5,4,3,2,1:T(8,128)(2,1)S(1)} collective-permute-done((bf16[4,1,1,1,1,1,16,128]{7,6,0,5,4,3,2,1:T(8,128)(2,1)S(1)}, bf16[4,1,1,1,1,1,16,128]{7,6,0,5,4,3,2,1:T(8,128)(2,1)S(1)}, u32[]{:S(2)}, u32[]{:S(2)}) %collective-permute-start.17) | collective-permute-done | bytes 16416 | tf_op jit(solution)/shard_map/ppermute | solution.py:103
  79.1 2.0 %collective-permute-start.22 = (bf16[4,1,2,1,1,1,16,128]{7,6,0,5,4,3,2,1:T(8,128)(2,1)S(1)}, bf16[4,1,2,1,1,1,16,128]{7,6,0,5,4,3,2,1:T(8,128)(2,1)S(1)}, u32[]{:S(2)}, u32[]{:S(2)}) collective-permute-start(bf16[4,1,2,1,1,1,16,128]{7,6,0,5,4,3,2,1:T(8,128)(2,1)S(1)} %maximum_select_fusion.16), channel_id=1, source_target_pairs={{0,16},{4,20},{8,24},{12,28},{16,0},{20,4},{24,8},{28,12},{1,17},{... | collective-permute-start | bytes 98312 | tf_op jit(solution)/shard_map/ppermute | solution.py:103
  81.1 1.2 %collective-permute-start.26 = (bf16[4,1,1,2,1,1,16,128]{7,6,0,5,4,3,2,1:T(8,128)(2,1)S(1)}, bf16[4,1,1,2,1,1,16,128]{7,6,0,5,4,3,2,1:T(8,128)(2,1)S(1)}, u32[]{:S(2)}, u32[]{:S(2)}) collective-permute-start(bf16[4,1,1,2,1,1,16,128]{7,6,0,5,4,3,2,1:T(8,128)(2,1)S(1)} %maximum_select_fusion.18), channel_id=1, source_target_pairs={{0,2},{1,3},{2,0},{3,1},{4,6},{5,7},{6,4},{7,5},{8,10},{9,11},{10,... | collective-permute-start | bytes 98312 | tf_op jit(solution)/shard_map/ppermute | solution.py:103
  84.1 2.0 %collective-permute-start.23 = (bf16[4,1,2,1,1,2,16,128]{7,6,0,5,4,3,2,1:T(8,128)(2,1)S(1)}, bf16[4,1,2,1,1,2,16,128]{7,6,0,5,4,3,2,1:T(8,128)(2,1)S(1)}, u32[]{:S(2)}, u32[]{:S(2)}) collective-permute-start(bf16[4,1,2,1,1,2,16,128]{7,6,0,5,4,3,2,1:T(8,128)(2,1)S(1)} %maximum_select_fusion.11), channel_id=1, source_target_pairs={{0,8},{4,12},{8,0},{12,4},{16,24},{20,28},{24,16},{28,20},{1,9},{5... | collective-permute-start | bytes 196616 | tf_op jit(solution)/shard_map/ppermute | solution.py:103
  86.5 1.3 %collective-permute-done.19 = bf16[4,1,1,1,2,2,16,128]{7,6,0,5,4,3,2,1:T(8,128)(2,1)S(1)} collective-permute-done((bf16[4,1,1,1,2,2,16,128]{7,6,0,5,4,3,2,1:T(8,128)(2,1)S(1)}, bf16[4,1,1,1,2,2,16,128]{7,6,0,5,4,3,2,1:T(8,128)(2,1)S(1)}, u32[]{:S(2)}, u32[]{:S(2)}) %collective-permute-start.19) | collective-permute-done | bytes 65568 | tf_op jit(solution)/shard_map/ppermute | solution.py:103
  89.1 1.2 %collective-permute-start.24 = (bf16[4,1,2,1,2,2,16,128]{7,6,0,5,4,3,2,1:T(8,128)(2,1)S(1)}, bf16[4,1,2,1,2,2,16,128]{7,6,0,5,4,3,2,1:T(8,128)(2,1)S(1)}, u32[]{:S(2)}, u32[]{:S(2)}) collective-permute-start(bf16[4,1,2,1,2,2,16,128]{7,6,0,5,4,3,2,1:T(8,128)(2,1)S(1)} %maximum_select_fusion.6), channel_id=1, source_target_pairs={{0,4},{4,0},{8,12},{12,8},{16,20},{20,16},{24,28},{28,24},{1,5},{5... | collective-permute-start | bytes 393224 | tf_op jit(solution)/shard_map/ppermute | solution.py:103
  90.3 1.5 %collective-permute-done.27 = bf16[4,1,2,2,1,1,16,128]{7,6,0,5,4,3,2,1:T(8,128)(2,1)S(1)} collective-permute-done((bf16[4,1,2,2,1,1,16,128]{7,6,0,5,4,3,2,1:T(8,128)(2,1)S(1)}, bf16[4,1,2,2,1,1,16,128]{7,6,0,5,4,3,2,1:T(8,128)(2,1)S(1)}, u32[]{:S(2)}, u32[]{:S(2)}) %collective-permute-start.27) | collective-permute-done | bytes 65568 | tf_op jit(solution)/shard_map/ppermute | solution.py:103
  94.2 2.6 %collective-permute-done.28 = bf16[4,1,2,2,1,2,16,128]{7,6,0,5,4,3,2,1:T(8,128)(2,1)S(1)} collective-permute-done((bf16[4,1,2,2,1,2,16,128]{7,6,0,5,4,3,2,1:T(8,128)(2,1)S(1)}, bf16[4,1,2,2,1,2,16,128]{7,6,0,5,4,3,2,1:T(8,128)(2,1)S(1)}, u32[]{:S(2)}, u32[]{:S(2)}) %collective-permute-start.28) | collective-permute-done | bytes 131104 | tf_op jit(solution)/shard_map/ppermute | solution.py:103
  98.1 1.3 %collective-permute-done.29 = bf16[12,256,128]{2,1,0:T(8,128)(2,1)S(1)} collective-permute-done((bf16[12,256,128]{2,1,0:T(8,128)(2,1)S(1)}, bf16[12,256,128]{2,1,0:T(8,128)(2,1)S(1)}, u32[]{:S(2)}, u32[]{:S(2)}) %collective-permute-start.29) | collective-permute-done | bytes 786464 | tf_op jit(solution)/shard_map/ppermute | solution.py:187
  100.2 1.2 %copy-done.24 = f32[3,512,256]{2,1,0:T(8,128)S(1)} copy-done((f32[3,512,256]{2,1,0:T(8,128)S(1)}, f32[3,512,256]{2,1,0:T(8,128)}, u32[]{:S(2)}) %copy-start.24) | copy-done | bytes 1572888
  101.4 1.5 %fusion.3 = bf16[4,512,256]{2,1,0:T(8,128)(2,1)} fusion(f32[1,512,256]{2,1,0:T(8,128)S(1)} %copy-done.23, f32[3,512,256]{2,1,0:T(8,128)S(1)} %copy-done.24, bf16[4,2,256,128]{3,2,1,0:T(8,128)(2,1)S(1)} %copy-done.8, bf16[4,2,256,128]{3,2,1,0:T(8,128)(2,1)S(1)} %get-tuple-element.68, bf16[4,2,256,128]{3,2,1,0:T(8,128)(2,1)S(1)} %get-tuple-element.67, ...), kind=kOutput, calls=%fused_computation.11 | convolution fusion | flops 274726912 | bytes 4718593 | tf_op jit(solution)/shard_map/jqrc,jqbc->jrb/dot_general | solution.py:196
  (179 shorter events, 33.9 us)
Async XLA Ops:
  1.5 9.7 %copy-start.9 = (bf16[3,4,128,128]{3,2,1,0:T(8,128)(2,1)S(1)}, bf16[3,4,128,128]{3,2,1,0:T(8,128)(2,1)}, u32[]{:S(2)}) copy-start(bf16[3,4,128,128]{3,2,1,0:T(8,128)(2,1)} %param.16) | copy-start | bytes 1179652
  6.6 19.1 %collective-permute-start.2 = (f32[12,256,128]{2,1,0:T(8,128)}, f32[12,256,128]{2,1,0:T(8,128)}, u32[]{:S(2)}, u32[]{:S(2)}) collective-permute-start(f32[12,256,128]{2,1,0:T(8,128)} %shard_map.83), channel_id=1, source_target_pairs={{0,1},{1,0},{2,3},{3,2},{4,5},{5,4},{6,7},{7,6},{8,9},{9,8},{10,11... | collective-permute-start | bytes 4718600 | tf_op jit(solution)/shard_map/ppermute | solution.py:137
  7.1 17.3 %collective-permute-start = (bf16[1,512,256]{2,1,0:T(8,128)(2,1)S(1)}, bf16[1,512,256]{2,1,0:T(8,128)(2,1)}, u32[]{:S(2)}, u32[]{:S(2)}) collective-permute-start(bf16[1,512,256]{2,1,0:T(8,128)(2,1)S(1)} %get-tuple-element.51), channel_id=1, source_target_pairs={{0,1},{1,2},{2,3},{3,4},{4,5},{5,6},{6,7},{7,8},{8,9},{9,10},{10,1... | collective-permute-start | bytes 786440 | tf_op jit(solution)/shard_map/ppermute | solution.py:65
  9.8 14.7 %collective-permute-start.1 = (bf16[1,512,256]{2,1,0:T(8,128)(2,1)S(1)}, bf16[1,512,256]{2,1,0:T(8,128)(2,1)}, u32[]{:S(2)}, u32[]{:S(2)}) collective-permute-start(bf16[1,512,256]{2,1,0:T(8,128)(2,1)S(1)} %get-tuple-element.52), channel_id=1, source_target_pairs={{1,0},{2,1},{3,2},{4,3},{5,4},{6,5},{7,6},{8,7},{9,8},{10,9},{11,1... | collective-permute-start | bytes 786440 | tf_op jit(solution)/shard_map/ppermute | solution.py:67
  12.0 16.5 %collective-permute-start.3 = (bf16[3,4,136,128]{3,2,1,0:T(8,128)(2,1)}, bf16[3,4,136,128]{3,2,1,0:T(8,128)(2,1)S(1)}, u32[]{:S(2)}, u32[]{:S(2)}) collective-permute-start(bf16[3,4,136,128]{3,2,1,0:T(8,128)(2,1)} %pad_maximum_fusion.3), channel_id=1, source_target_pairs={{0,2},{1,3},{2,0},{3,1},{4,6},{5,7},{6,4},{7,5},{8,10},{9,11},{10,... | collective-permute-start | bytes 1253384 | tf_op jit(solution)/shard_map/ppermute | solution.py:142
  30.2 13.8 %collective-permute-start.6 = (f32[4,1,2,2,1,2,16,128]{7,6,5,4,3,2,0,1:T(8,128)}, f32[4,1,2,2,1,2,16,128]{7,6,5,4,3,2,0,1:T(8,128)}, u32[]{:S(2)}, u32[]{:S(2)}) collective-permute-start(f32[4,1,2,2,1,2,16,128]{7,6,5,4,3,2,0,1:T(8,128)} %constant_dynamic-slice_fusion.9), channel_id=1, source_target_pairs={{0,8},{4,12},{8,0},{12,4},{16,24},{20,28},{24,16},{28,20},{1,9},{5... | collective-permute-start | bytes 786440 | tf_op jit(solution)/shard_map/ppermute | solution.py:98
  33.4 12.5 %collective-permute-start.5 = (f32[4,1,2,1,2,2,16,128]{7,6,5,4,3,2,0,1:T(8,128)}, f32[4,1,2,1,2,2,16,128]{7,6,5,4,3,2,0,1:T(8,128)}, u32[]{:S(2)}, u32[]{:S(2)}) collective-permute-start(f32[4,1,2,1,2,2,16,128]{7,6,5,4,3,2,0,1:T(8,128)} %constant_dynamic-slice_fusion.10), channel_id=1, source_target_pairs={{0,4},{4,0},{8,12},{12,8},{16,20},{20,16},{24,28},{28,24},{1,5},{5... | collective-permute-start | bytes 786440 | tf_op jit(solution)/shard_map/ppermute | solution.py:98
  34.8 12.2 %collective-permute-start.4 = (f32[4,1,1,2,2,2,16,128]{7,6,5,4,3,2,0,1:T(8,128)}, f32[4,1,1,2,2,2,16,128]{7,6,5,4,3,2,0,1:T(8,128)}, u32[]{:S(2)}, u32[]{:S(2)}) collective-permute-start(f32[4,1,1,2,2,2,16,128]{7,6,5,4,3,2,0,1:T(8,128)} %constant_dynamic-slice_fusion.11), channel_id=1, source_target_pairs={{0,2},{1,3},{2,0},{3,1},{4,6},{5,7},{6,4},{7,5},{8,10},{9,11},{10,... | collective-permute-start | bytes 786440 | tf_op jit(solution)/shard_map/ppermute | solution.py:98
  48.1 9.7 %collective-permute-start.9 = (f32[4,1,2,2,1,1,16,128]{7,6,5,4,3,2,0,1:T(8,128)S(1)}, f32[4,1,2,2,1,1,16,128]{7,6,5,4,3,2,0,1:T(8,128)S(1)}, u32[]{:S(2)}, u32[]{:S(2)}) collective-permute-start(f32[4,1,2,2,1,1,16,128]{7,6,5,4,3,2,0,1:T(8,128)S(1)} %constant_dynamic-slice_fusion.6), channel_id=1, source_target_pairs={{0,16},{4,20},{8,24},{12,28},{16,0},{20,4},{24,8},{28,12},{1,17},{... | collective-permute-start | bytes 393224 | tf_op jit(solution)/shard_map/ppermute | solution.py:98
  49.2 7.7 %collective-permute-start.8 = (f32[4,1,2,1,1,2,16,128]{7,6,5,4,3,2,0,1:T(8,128)S(1)}, f32[4,1,2,1,1,2,16,128]{7,6,5,4,3,2,0,1:T(8,128)S(1)}, u32[]{:S(2)}, u32[]{:S(2)}) collective-permute-start(f32[4,1,2,1,1,2,16,128]{7,6,5,4,3,2,0,1:T(8,128)S(1)} %constant_dynamic-slice_fusion.7), channel_id=1, source_target_pairs={{0,8},{4,12},{8,0},{12,4},{16,24},{20,28},{24,16},{28,20},{1,9},{5... | collective-permute-start | bytes 393224 | tf_op jit(solution)/shard_map/ppermute | solution.py:98
  51.9 5.2 %collective-permute-start.7 = (f32[4,1,1,1,2,2,16,128]{7,6,5,4,3,2,0,1:T(8,128)}, f32[4,1,1,1,2,2,16,128]{7,6,5,4,3,2,0,1:T(8,128)S(1)}, u32[]{:S(2)}, u32[]{:S(2)}) collective-permute-start(f32[4,1,1,1,2,2,16,128]{7,6,5,4,3,2,0,1:T(8,128)} %constant_dynamic-slice_fusion.8), channel_id=1, source_target_pairs={{0,4},{4,0},{8,12},{12,8},{16,20},{20,16},{24,28},{28,24},{1,5},{5... | collective-permute-start | bytes 393224 | tf_op jit(solution)/shard_map/ppermute | solution.py:98
  52.4 5.4 %collective-permute-start.10 = (bf16[6,4,136,128]{3,2,1,0:T(8,128)(2,1)S(1)}, bf16[6,4,136,128]{3,2,1,0:T(8,128)(2,1)}, u32[]{:S(2)}, u32[]{:S(2)}) collective-permute-start(bf16[6,4,136,128]{3,2,1,0:T(8,128)(2,1)S(1)} %pad_maximum_fusion.1), channel_id=1, source_target_pairs={{0,1},{1,0},{2,3},{3,2},{4,5},{5,4},{6,7},{7,6},{8,9},{9,8},{10,11... | collective-permute-start | bytes 2506760 | tf_op jit(solution)/shard_map/ppermute | solution.py:167
  59.3 4.6 %collective-permute-start.11 = (f32[4,1,1,1,1,2,16,128]{7,6,5,4,3,2,0,1:T(8,128)S(1)}, f32[4,1,1,1,1,2,16,128]{7,6,5,4,3,2,0,1:T(8,128)S(1)}, u32[]{:S(2)}, u32[]{:S(2)}) collective-permute-start(f32[4,1,1,1,1,2,16,128]{7,6,5,4,3,2,0,1:T(8,128)S(1)} %constant_dynamic-slice_fusion.5), channel_id=1, source_target_pairs={{0,8},{4,12},{8,0},{12,4},{16,24},{20,28},{24,16},{28,20},{1,9},{5... | collective-permute-start | bytes 196616 | tf_op jit(solution)/shard_map/ppermute | solution.py:98
  61.0 6.5 %collective-permute-start.13 = (f32[4,1,2,1,1,1,16,128]{7,6,5,4,3,2,0,1:T(8,128)S(1)}, f32[4,1,2,1,1,1,16,128]{7,6,5,4,3,2,0,1:T(8,128)S(1)}, u32[]{:S(2)}, u32[]{:S(2)}) collective-permute-start(f32[4,1,2,1,1,1,16,128]{7,6,5,4,3,2,0,1:T(8,128)S(1)} %constant_dynamic-slice_fusion.3), channel_id=1, source_target_pairs={{0,16},{4,20},{8,24},{12,28},{16,0},{20,4},{24,8},{28,12},{1,17},{... | collective-permute-start | bytes 196616 | tf_op jit(solution)/shard_map/ppermute | solution.py:98
  61.3 7.2 %collective-permute-start.15 = (f32[4,1,1,2,1,1,16,128]{7,6,5,4,3,2,0,1:T(8,128)S(1)}, f32[4,1,1,2,1,1,16,128]{7,6,5,4,3,2,0,1:T(8,128)S(1)}, u32[]{:S(2)}, u32[]{:S(2)}) collective-permute-start(f32[4,1,1,2,1,1,16,128]{7,6,5,4,3,2,0,1:T(8,128)S(1)} %constant_dynamic-slice_fusion.1), channel_id=1, source_target_pairs={{0,2},{1,3},{2,0},{3,1},{4,6},{5,7},{6,4},{7,5},{8,10},{9,11},{10,... | collective-permute-start | bytes 196616 | tf_op jit(solution)/shard_map/ppermute | solution.py:98
  63.9 10.3 %copy-start.21 = (pred[12]{0:T(512)(128)(4,1)S(1)}, pred[12]{0:T(512)(128)(4,1)}, u32[]{:S(2)}) copy-start(pred[12]{0:T(512)(128)(4,1)} %compare_and_fusion.2) | copy-start | bytes 40
  63.9 5.3 %collective-permute-start.12 = (f32[4,1,1,1,1,1,16,128]{7,6,5,4,3,2,0,1:T(8,128)S(1)}, f32[4,1,1,1,1,1,16,128]{7,6,5,4,3,2,0,1:T(8,128)S(1)}, u32[]{:S(2)}, u32[]{:S(2)}) collective-permute-start(f32[4,1,1,1,1,1,16,128]{7,6,5,4,3,2,0,1:T(8,128)S(1)} %constant_dynamic-slice_fusion.4), channel_id=1, source_target_pairs={{0,16},{4,20},{8,24},{12,28},{16,0},{20,4},{24,8},{28,12},{1,17},{... | collective-permute-start | bytes 98312 | tf_op jit(solution)/shard_map/ppermute | solution.py:98
  67.5 4.0 %collective-permute-start.14 = (f32[4,1,1,1,1,1,16,128]{7,6,5,4,3,2,0,1:T(8,128)S(1)}, f32[4,1,1,1,1,1,16,128]{7,6,5,4,3,2,0,1:T(8,128)S(1)}, u32[]{:S(2)}, u32[]{:S(2)}) collective-permute-start(f32[4,1,1,1,1,1,16,128]{7,6,5,4,3,2,0,1:T(8,128)S(1)} %constant_dynamic-slice_fusion.2), channel_id=1, source_target_pairs={{0,2},{1,3},{2,0},{3,1},{4,6},{5,7},{6,4},{7,5},{8,10},{9,11},{10,... | collective-permute-start | bytes 98312 | tf_op jit(solution)/shard_map/ppermute | solution.py:98
  68.5 4.0 %collective-permute-start.16 = (f32[4,1,1,1,1,1,16,128]{7,6,5,4,3,2,0,1:T(8,128)S(1)}, f32[4,1,1,1,1,1,16,128]{7,6,5,4,3,2,0,1:T(8,128)S(1)}, u32[]{:S(2)}, u32[]{:S(2)}) collective-permute-start(f32[4,1,1,1,1,1,16,128]{7,6,5,4,3,2,0,1:T(8,128)S(1)} %constant_dynamic-slice_fusion), channel_id=1, source_target_pairs={{0,4},{4,0},{8,12},{12,8},{16,20},{20,16},{24,28},{28,24},{1,5},{5... | collective-permute-start | bytes 98312 | tf_op jit(solution)/shard_map/ppermute | solution.py:98
  74.3 4.7 %collective-permute-start.17 = (bf16[4,1,1,1,1,1,16,128]{7,6,0,5,4,3,2,1:T(8,128)(2,1)S(1)}, bf16[4,1,1,1,1,1,16,128]{7,6,0,5,4,3,2,1:T(8,128)(2,1)S(1)}, u32[]{:S(2)}, u32[]{:S(2)}) collective-permute-start(bf16[4,1,1,1,1,1,16,128]{7,6,0,5,4,3,2,1:T(8,128)(2,1)S(1)} %get-tuple-element.54), channel_id=1, source_target_pairs={{0,16},{4,20},{8,24},{12,28},{16,0},{20,4},{24,8},{28,12},{1,17},{... | collective-permute-start | bytes 49160 | tf_op jit(solution)/shard_map/ppermute | solution.py:103
  74.7 4.4 %collective-permute-start.21 = (bf16[4,1,1,1,1,1,16,128]{7,6,0,5,4,3,2,1:T(8,128)(2,1)S(1)}, bf16[4,1,1,1,1,1,16,128]{7,6,0,5,4,3,2,1:T(8,128)(2,1)S(1)}, u32[]{:S(2)}, u32[]{:S(2)}) collective-permute-start(bf16[4,1,1,1,1,1,16,128]{7,6,0,5,4,3,2,1:T(8,128)(2,1)S(1)} %get-tuple-element.55), channel_id=1, source_target_pairs={{0,2},{1,3},{2,0},{3,1},{4,6},{5,7},{6,4},{7,5},{8,10},{9,11},{10,... | collective-permute-start | bytes 49160 | tf_op jit(solution)/shard_map/ppermute | solution.py:103
  75.8 5.3 %collective-permute-start.25 = (bf16[4,1,1,1,1,1,16,128]{7,6,0,5,4,3,2,1:T(8,128)(2,1)S(1)}, bf16[4,1,1,1,1,1,16,128]{7,6,0,5,4,3,2,1:T(8,128)(2,1)S(1)}, u32[]{:S(2)}, u32[]{:S(2)}) collective-permute-start(bf16[4,1,1,1,1,1,16,128]{7,6,0,5,4,3,2,1:T(8,128)(2,1)S(1)} %get-tuple-element.56), channel_id=1, source_target_pairs={{0,4},{4,0},{8,12},{12,8},{16,20},{20,16},{24,28},{28,24},{1,5},{5... | collective-permute-start | bytes 49160 | tf_op jit(solution)/shard_map/ppermute | solution.py:103
  79.0 4.0 %collective-permute-start.18 = (bf16[4,1,1,1,1,2,16,128]{7,6,0,5,4,3,2,1:T(8,128)(2,1)S(1)}, bf16[4,1,1,1,1,2,16,128]{7,6,0,5,4,3,2,1:T(8,128)(2,1)S(1)}, u32[]{:S(2)}, u32[]{:S(2)}) collective-permute-start(bf16[4,1,1,1,1,2,16,128]{7,6,0,5,4,3,2,1:T(8,128)(2,1)S(1)} %maximum_select_fusion.14), channel_id=1, source_target_pairs={{0,8},{4,12},{8,0},{12,4},{16,24},{20,28},{24,16},{28,20},{1,9},{5... | collective-permute-start | bytes 98312 | tf_op jit(solution)/shard_map/ppermute | solution.py:103
  79.1 5.0 %collective-permute-start.22 = (bf16[4,1,2,1,1,1,16,128]{7,6,0,5,4,3,2,1:T(8,128)(2,1)S(1)}, bf16[4,1,2,1,1,1,16,128]{7,6,0,5,4,3,2,1:T(8,128)(2,1)S(1)}, u32[]{:S(2)}, u32[]{:S(2)}) collective-permute-start(bf16[4,1,2,1,1,1,16,128]{7,6,0,5,4,3,2,1:T(8,128)(2,1)S(1)} %maximum_select_fusion.16), channel_id=1, source_target_pairs={{0,16},{4,20},{8,24},{12,28},{16,0},{20,4},{24,8},{28,12},{1,17},{... | collective-permute-start | bytes 98312 | tf_op jit(solution)/shard_map/ppermute | solution.py:103
  81.1 5.0 %collective-permute-start.26 = (bf16[4,1,1,2,1,1,16,128]{7,6,0,5,4,3,2,1:T(8,128)(2,1)S(1)}, bf16[4,1,1,2,1,1,16,128]{7,6,0,5,4,3,2,1:T(8,128)(2,1)S(1)}, u32[]{:S(2)}, u32[]{:S(2)}) collective-permute-start(bf16[4,1,1,2,1,1,16,128]{7,6,0,5,4,3,2,1:T(8,128)(2,1)S(1)} %maximum_select_fusion.18), channel_id=1, source_target_pairs={{0,2},{1,3},{2,0},{3,1},{4,6},{5,7},{6,4},{7,5},{8,10},{9,11},{10,... | collective-permute-start | bytes 98312 | tf_op jit(solution)/shard_map/ppermute | solution.py:103
  83.0 4.9 %collective-permute-start.19 = (bf16[4,1,1,1,2,2,16,128]{7,6,0,5,4,3,2,1:T(8,128)(2,1)S(1)}, bf16[4,1,1,1,2,2,16,128]{7,6,0,5,4,3,2,1:T(8,128)(2,1)S(1)}, u32[]{:S(2)}, u32[]{:S(2)}) collective-permute-start(bf16[4,1,1,1,2,2,16,128]{7,6,0,5,4,3,2,1:T(8,128)(2,1)S(1)} %maximum_select_fusion.9), channel_id=1, source_target_pairs={{0,4},{4,0},{8,12},{12,8},{16,20},{20,16},{24,28},{28,24},{1,5},{5... | collective-permute-start | bytes 196616 | tf_op jit(solution)/shard_map/ppermute | solution.py:103
  84.1 5.0 %collective-permute-start.23 = (bf16[4,1,2,1,1,2,16,128]{7,6,0,5,4,3,2,1:T(8,128)(2,1)S(1)}, bf16[4,1,2,1,1,2,16,128]{7,6,0,5,4,3,2,1:T(8,128)(2,1)S(1)}, u32[]{:S(2)}, u32[]{:S(2)}) collective-permute-start(bf16[4,1,2,1,1,2,16,128]{7,6,0,5,4,3,2,1:T(8,128)(2,1)S(1)} %maximum_select_fusion.11), channel_id=1, source_target_pairs={{0,8},{4,12},{8,0},{12,4},{16,24},{20,28},{24,16},{28,20},{1,9},{5... | collective-permute-start | bytes 196616 | tf_op jit(solution)/shard_map/ppermute | solution.py:103
  86.1 5.7 %collective-permute-start.27 = (bf16[4,1,2,2,1,1,16,128]{7,6,0,5,4,3,2,1:T(8,128)(2,1)S(1)}, bf16[4,1,2,2,1,1,16,128]{7,6,0,5,4,3,2,1:T(8,128)(2,1)S(1)}, u32[]{:S(2)}, u32[]{:S(2)}) collective-permute-start(bf16[4,1,2,2,1,1,16,128]{7,6,0,5,4,3,2,1:T(8,128)(2,1)S(1)} %fusion.36), channel_id=1, source_target_pairs={{0,16},{4,20},{8,24},{12,28},{16,0},{20,4},{24,8},{28,12},{1,17},{... | collective-permute-start | bytes 196616 | tf_op jit(solution)/shard_map/ppermute | solution.py:103
  87.9 5.0 %collective-permute-start.20 = (bf16[4,1,1,2,2,2,16,128]{7,6,0,5,4,3,2,1:T(8,128)(2,1)S(1)}, bf16[4,1,1,2,2,2,16,128]{7,6,0,5,4,3,2,1:T(8,128)(2,1)S(1)}, u32[]{:S(2)}, u32[]{:S(2)}) collective-permute-start(bf16[4,1,1,2,2,2,16,128]{7,6,0,5,4,3,2,1:T(8,128)(2,1)S(1)} %maximum_select_fusion.5), channel_id=1, source_target_pairs={{0,2},{1,3},{2,0},{3,1},{4,6},{5,7},{6,4},{7,5},{8,10},{9,11},{10,... | collective-permute-start | bytes 393224 | tf_op jit(solution)/shard_map/ppermute | solution.py:103
  89.1 5.0 %collective-permute-start.24 = (bf16[4,1,2,1,2,2,16,128]{7,6,0,5,4,3,2,1:T(8,128)(2,1)S(1)}, bf16[4,1,2,1,2,2,16,128]{7,6,0,5,4,3,2,1:T(8,128)(2,1)S(1)}, u32[]{:S(2)}, u32[]{:S(2)}) collective-permute-start(bf16[4,1,2,1,2,2,16,128]{7,6,0,5,4,3,2,1:T(8,128)(2,1)S(1)} %maximum_select_fusion.6), channel_id=1, source_target_pairs={{0,4},{4,0},{8,12},{12,8},{16,20},{20,16},{24,28},{28,24},{1,5},{5... | collective-permute-start | bytes 393224 | tf_op jit(solution)/shard_map/ppermute | solution.py:103
  91.8 5.0 %collective-permute-start.28 = (bf16[4,1,2,2,1,2,16,128]{7,6,0,5,4,3,2,1:T(8,128)(2,1)S(1)}, bf16[4,1,2,2,1,2,16,128]{7,6,0,5,4,3,2,1:T(8,128)(2,1)S(1)}, u32[]{:S(2)}, u32[]{:S(2)}) collective-permute-start(bf16[4,1,2,2,1,2,16,128]{7,6,0,5,4,3,2,1:T(8,128)(2,1)S(1)} %maximum_select_fusion.7), channel_id=1, source_target_pairs={{0,8},{4,12},{8,0},{12,4},{16,24},{20,28},{24,16},{28,20},{1,9},{5... | collective-permute-start | bytes 393224 | tf_op jit(solution)/shard_map/ppermute | solution.py:103
  97.0 2.4 %collective-permute-start.29 = (bf16[12,256,128]{2,1,0:T(8,128)(2,1)S(1)}, bf16[12,256,128]{2,1,0:T(8,128)(2,1)S(1)}, u32[]{:S(2)}, u32[]{:S(2)}) collective-permute-start(bf16[12,256,128]{2,1,0:T(8,128)(2,1)S(1)} %pad_maximum_fusion.2), channel_id=1, source_target_pairs={{0,1},{1,0},{2,3},{3,2},{4,5},{5,4},{6,7},{7,6},{8,9},{9,8},{10,11... | collective-permute-start | bytes 2359304 | tf_op jit(solution)/shard_map/ppermute | solution.py:187
  (23 other events, 100.2 us)

commit v23 on v22

--- a/solution.py
+++ b/solution.py
@@ -154,8 +154,6 @@
             local[0], extended, parts = lax.optimization_barrier((local[0], extended, parts))
             picked = jnp.take(extended, margin[split_at:], axis=0)
             local.append(jnp.einsum("jerb,jebc->jrc", picked, inverse_blocks[split_at:], preferred_element_type=jnp.float32))
-        if step == 2:
-            local[1], parts = lax.optimization_barrier((local[1], parts))
         k = step
         if arriving is not None:
             arriving, parts = lax.optimization_barrier((arriving, parts))
@@ -183,6 +181,8 @@
     outs = [lax.slice_in_dim(solved, s * per, (s + 1) * per, axis=0) for s in range(streams)]
     for step in reversed(range(1, nb)):
         outs = [double(y, 1 + orders[s][step], *bits[orders[s][step]]) for s, y in enumerate(outs)]
+        if step == nb - 1:
+            local[1], outs = lax.optimization_barrier((local[1], outs))
     own = jnp.concatenate(outs, axis=0).reshape(total_blocks, rhs // 2, width)
     got = lax.ppermute(own, bits[0][0], pairs(*bits[0]))
     own_rows = jnp.take(own, interface, axis=0)

time: 104 us -> 110 us (1.058)
  waiting for transfers between devices: 19.2 us -> 27.1 us
  starting transfers between devices: 35.7 us -> 33.4 us
  matrix products: 9.19 us -> 8.02 us
    ppermute x12, waiting for transfers between devices: 9.71 us -> 14.4 us  [double(): recv = lax.ppermute(y, axis, pairs(axis, mask))]
    ppermute x12, starting transfers between devices: 12.5 us -> 10.2 us  [double(): recv = lax.ppermute(y, axis, pairs(axis, mask))]
    ppermute x12, waiting for transfers between devices: 7.06 us -> 9.23 us  [halve(): lax.ppermute(send.astype(wire), axis, pairs(axis, mask)).astype(x.dtype)]
    add x9, other arithmetic: 3.14 us -> 4.96 us  [halve(): keep + lax.ppermute(send.astype(wire), axis, pairs(axis, mask)).astype(x....]
    dot_general x1, matrix products: 2.71 us -> 1.53 us  [per_device(): jnp.einsum('jerb,jebc->jrc', picked, inverse_blocks[split_at:], preferred...]
    unnamed x53 -> x57, local copies, waits for them, and re-layouts: 4.71 us -> 5.22 us
  transfers between devices with their start and end apart: 30 -> 30, of which waited for: 15 -> 18; matrix products, arithmetic and copies ran while one was open for 24% -> 22% of each run, Pallas kernels for 5% -> 5%
where the time goes in v23:
time: 110 us; the launch traced here: 109 us
  starting transfers between devices  33.4 us (30%)
  waiting for transfers between devices  27.1 us (25%)
  local copies, waits for them, and re-layouts  19 us (17%)
  other arithmetic  10.5 us (10%)
  Pallas kernels  10.4 us (9%)
  matrix products  8.02 us (7%)
    ppermute x12, starting transfers between devices, halve(): lax.ppermute(send.astype(wire), axis, pairs(axis, mask)).astype(x.dtype)  14.5 us
    ppermute x12, waiting for transfers between devices, double(): recv = lax.ppermute(y, axis, pairs(axis, mask))  14.4 us
    pallas_call x2, Pallas kernels, restrict(): pl.pallas_call(functools.partial(restrict_kernel, upper=upper), out_shape...  10.4 us
    ppermute x12, starting transfers between devices, double(): recv = lax.ppermute(y, axis, pairs(axis, mask))  10.2 us
    ppermute x12, waiting for transfers between devices, halve(): lax.ppermute(send.astype(wire), axis, pairs(axis, mask)).astype(x.dtype)  9.23 us
    unnamed x57, local copies, waits for them, and re-layouts  5.22 us
    add x9, other arithmetic, halve(): keep + lax.ppermute(send.astype(wire), axis, pairs(axis, mask)).astype(x....  4.96 us
    dot_general x1, matrix products, per_device(): jnp.einsum('jerb,jebc->jrc', picked, inverse_blocks[:split_at], preferred...  4.61 us
  transfers between devices with their start and end apart: 30, of which 18 were waited for; matrix products, arithmetic and copies ran while one was open for 22% of the time, Pallas kernels for 5%

profile of v23, /device:TPU:0, one launch (start us, length us, event | category | flops | bytes accessed | tf_op | source)
XLA Modules:
  0.0 109.0 jit_solution(5035996958497878371)
XLA Ops:
  1.5 5.2 %shard_map.83 = f32[12,256,128]{2,1,0:T(8,128)} custom-call(s32[8]{0:T(128)} %reshape.1221.links, s32[1]{0:T(128)} %bitcast.half, bf16[4,512,256]{2,1,0:T(8,128)(2,1)} %residual_ref.3, bf16[4,2,256,128]{3,2,1,0:T(8,128)(2,1)} %basis_ref.3), custom_call_target="tpu_custom_call" | custom-call | flops 134217728 | bytes 3145728 | tf_op jit(solution)/shard_map/pallas_call | solution.py:36
  7.1 2.7 %collective-permute-start = (bf16[1,512,256]{2,1,0:T(8,128)(2,1)S(1)}, bf16[1,512,256]{2,1,0:T(8,128)(2,1)}, u32[]{:S(2)}, u32[]{:S(2)}) collective-permute-start(bf16[1,512,256]{2,1,0:T(8,128)(2,1)S(1)} %get-tuple-element.51), channel_id=1, source_target_pairs={{0,1},{1,2},{2,3},{3,4},{4,5},{5,6},{6,7},{7,8},{8,9},{9,10},{10,1... | collective-permute-start | bytes 786440 | tf_op jit(solution)/shard_map/ppermute | solution.py:65
  9.8 1.3 %collective-permute-start.1 = (bf16[1,512,256]{2,1,0:T(8,128)(2,1)S(1)}, bf16[1,512,256]{2,1,0:T(8,128)(2,1)}, u32[]{:S(2)}, u32[]{:S(2)}) collective-permute-start(bf16[1,512,256]{2,1,0:T(8,128)(2,1)S(1)} %get-tuple-element.52), channel_id=1, source_target_pairs={{1,0},{2,1},{3,2},{4,3},{5,4},{6,5},{7,6},{8,7},{9,8},{10,9},{11,1... | collective-permute-start | bytes 786440 | tf_op jit(solution)/shard_map/ppermute | solution.py:67
  12.0 4.1 %collective-permute-start.3 = (bf16[3,4,136,128]{3,2,1,0:T(8,128)(2,1)}, bf16[3,4,136,128]{3,2,1,0:T(8,128)(2,1)S(1)}, u32[]{:S(2)}, u32[]{:S(2)}) collective-permute-start(bf16[3,4,136,128]{3,2,1,0:T(8,128)(2,1)} %pad_maximum_fusion.3), channel_id=1, source_target_pairs={{0,2},{1,3},{2,0},{3,1},{4,6},{5,7},{6,4},{7,5},{8,10},{9,11},{10,... | collective-permute-start | bytes 1253384 | tf_op jit(solution)/shard_map/ppermute | solution.py:142
  17.7 5.2 %shard_map.82 = f32[12,256,128]{2,1,0:T(8,128)} custom-call(s32[8]{0:T(128)} %reshape.1221.links, s32[1]{0:T(128)} %bitcast.half, bf16[4,512,256]{2,1,0:T(8,128)(2,1)} %residual_ref.3, bf16[4,2,256,128]{3,2,1,0:T(8,128)(2,1)} %basis_ref.3), custom_call_target="tpu_custom_call" | custom-call | flops 134217728 | bytes 3145728 | tf_op jit(solution)/shard_map/pallas_call | solution.py:36
  24.7 1.6 %add.237 = f32[12,256,128]{2,1,0:T(8,128)S(1)} add(f32[12,256,128]{2,1,0:T(8,128)S(1)} %copy-done.3, f32[12,256,128]{2,1,0:T(8,128)} %collective-permute-done.2) | non-fusion elementwise | flops 393216 | bytes 4718592 | tf_op jit(solution)/shard_map/add | solution.py:138
  26.3 2.2 %collective-permute-done.3 = bf16[3,4,136,128]{3,2,1,0:T(8,128)(2,1)S(1)} collective-permute-done((bf16[3,4,136,128]{3,2,1,0:T(8,128)(2,1)}, bf16[3,4,136,128]{3,2,1,0:T(8,128)(2,1)S(1)}, u32[]{:S(2)}, u32[]{:S(2)}) %collective-permute-start.3) | collective-permute-done | bytes 417824 | tf_op jit(solution)/shard_map/ppermute | solution.py:142
  30.2 2.4 %collective-permute-start.6 = (f32[4,1,2,2,1,2,16,128]{7,6,5,4,3,2,0,1:T(8,128)}, f32[4,1,2,2,1,2,16,128]{7,6,5,4,3,2,0,1:T(8,128)}, u32[]{:S(2)}, u32[]{:S(2)}) collective-permute-start(f32[4,1,2,2,1,2,16,128]{7,6,5,4,3,2,0,1:T(8,128)} %constant_dynamic-slice_fusion.9), channel_id=1, source_target_pairs={{0,8},{4,12},{8,0},{12,4},{16,24},{20,28},{24,16},{28,20},{1,9},{5... | collective-permute-start | bytes 786440 | tf_op jit(solution)/shard_map/ppermute | solution.py:98
  34.7 2.1 %collective-permute-start.4 = (f32[4,1,1,2,2,2,16,128]{7,6,5,4,3,2,0,1:T(8,128)}, f32[4,1,1,2,2,2,16,128]{7,6,5,4,3,2,0,1:T(8,128)}, u32[]{:S(2)}, u32[]{:S(2)}) collective-permute-start(f32[4,1,1,2,2,2,16,128]{7,6,5,4,3,2,0,1:T(8,128)} %constant_dynamic-slice_fusion.11), channel_id=1, source_target_pairs={{0,2},{1,3},{2,0},{3,1},{4,6},{5,7},{6,4},{7,5},{8,10},{9,11},{10,... | collective-permute-start | bytes 786440 | tf_op jit(solution)/shard_map/ppermute | solution.py:98
  36.8 2.5 %gather_fusion = bf16[12,512,256]{2,1,0:T(8,128)(2,1)} fusion(bf16[6,512,256]{2,1,0:T(8,128)(2,1)S(1)} %pad_maximum_fusion, s32[1024]{0:T(1024)S(1)} %pad_clamp_fusion.5), kind=kCustom, calls=%fused_computation.2 | custom fusion | bytes 6291504 | tf_op jit(solution)/shard_map/jit(_take)/gather | solution.py:149
  39.3 4.6 %fusion.8 = f32[3,512,256]{2,1,0:T(8,128)} fusion(bf16[4,4,256,256]{3,2,1,0:T(8,128)(2,1)} %param.12, bf16[3,4,512,256]{3,2,1,0:T(8,128)(2,1)} %bitcast.80, pred[3,4]{1,0:T(4,128)(4,1)S(1)} %copy-done.24), kind=kOutput, calls=%fused_computation.17 | convolution fusion | flops 806879232 | bytes 6291468 | tf_op jit(solution)/shard_map/jerb,jebc->jrc/dot_general | solution.py:150
  50.0 2.0 %collective-permute-start.9 = (f32[4,1,2,1,1,2,16,128]{7,6,5,4,3,2,0,1:T(8,128)S(1)}, f32[4,1,2,1,1,2,16,128]{7,6,5,4,3,2,0,1:T(8,128)}, u32[]{:S(2)}, u32[]{:S(2)}) collective-permute-start(f32[4,1,2,1,1,2,16,128]{7,6,5,4,3,2,0,1:T(8,128)S(1)} %constant_dynamic-slice_fusion.7), channel_id=1, source_target_pairs={{0,8},{4,12},{8,0},{12,4},{16,24},{20,28},{24,16},{28,20},{1,9},{5... | collective-permute-start | bytes 393224 | tf_op jit(solution)/shard_map/ppermute | solution.py:98
  53.1 1.6 %gather_fusion.1 = bf16[4,512,256]{2,1,0:T(8,128)(2,1)} fusion(bf16[6,512,256]{2,1,0:T(8,128)(2,1)S(1)} %pad_maximum_fusion, s32[1024]{0:T(1024)S(1)} %pad_clamp_fusion.4), kind=kCustom, calls=%fused_computation.3 | custom fusion | bytes 2097168 | tf_op jit(solution)/shard_map/jit(_take)/gather | solution.py:155
  54.8 2.2 %collective-permute-done.9 = f32[4,1,2,1,1,2,16,128]{7,6,5,4,3,2,0,1:T(8,128)} collective-permute-done((f32[4,1,2,1,1,2,16,128]{7,6,5,4,3,2,0,1:T(8,128)S(1)}, f32[4,1,2,1,1,2,16,128]{7,6,5,4,3,2,0,1:T(8,128)}, u32[]{:S(2)}, u32[]{:S(2)}) %collective-permute-start.9) | collective-permute-done | bytes 131104 | tf_op jit(solution)/shard_map/ppermute | solution.py:98
  59.9 1.3 %constant_dynamic-update-slice_fusion = bf16[12,4,136,128]{3,2,1,0:T(8,128)(2,1)S(1)} fusion(bf16[12,4,136,128]{3,2,1,0:T(8,128)(2,1)S(1)} %constant_dynamic-update-slice_fusion.1, bf16[6,4,136,128]{3,2,1,0:T(8,128)(2,1)} %collective-permute-done.7), kind=kLoop, calls=%fused_computation.99 | loop fusion | bytes 1671168 | tf_op jit(solution)/shard_map/concatenate | solution.py:160
  62.9 1.6 %collective-permute-start.13 = (f32[4,1,2,1,1,1,16,128]{7,6,5,4,3,2,0,1:T(8,128)S(1)}, f32[4,1,2,1,1,1,16,128]{7,6,5,4,3,2,0,1:T(8,128)S(1)}, u32[]{:S(2)}, u32[]{:S(2)}) collective-permute-start(f32[4,1,2,1,1,1,16,128]{7,6,5,4,3,2,0,1:T(8,128)S(1)} %constant_dynamic-slice_fusion.3), channel_id=1, source_target_pairs={{0,16},{4,20},{8,24},{12,28},{16,0},{20,4},{24,8},{28,12},{1,17},{... | collective-permute-start | bytes 196616 | tf_op jit(solution)/shard_map/ppermute | solution.py:98
  64.8 2.5 %collective-permute-done.11 = f32[4,1,1,1,1,2,16,128]{7,6,5,4,3,2,0,1:T(8,128)S(1)} collective-permute-done((f32[4,1,1,1,1,2,16,128]{7,6,5,4,3,2,0,1:T(8,128)S(1)}, f32[4,1,1,1,1,2,16,128]{7,6,5,4,3,2,0,1:T(8,128)S(1)}, u32[]{:S(2)}, u32[]{:S(2)}) %collective-permute-start.11) | collective-permute-done | bytes 65568 | tf_op jit(solution)/shard_map/ppermute | solution.py:98
  68.4 2.3 %collective-permute-start.14 = (f32[4,1,1,1,1,1,16,128]{7,6,5,4,3,2,0,1:T(8,128)S(1)}, f32[4,1,1,1,1,1,16,128]{7,6,5,4,3,2,0,1:T(8,128)S(1)}, u32[]{:S(2)}, u32[]{:S(2)}) collective-permute-start(f32[4,1,1,1,1,1,16,128]{7,6,5,4,3,2,0,1:T(8,128)S(1)} %constant_dynamic-slice_fusion.2), channel_id=1, source_target_pairs={{0,2},{1,3},{2,0},{3,1},{4,6},{5,7},{6,4},{7,5},{8,10},{9,11},{10,... | collective-permute-start | bytes 98312 | tf_op jit(solution)/shard_map/ppermute | solution.py:98
  70.8 1.4 %collective-permute-start.16 = (f32[4,1,1,1,1,1,16,128]{7,6,5,4,3,2,0,1:T(8,128)S(1)}, f32[4,1,1,1,1,1,16,128]{7,6,5,4,3,2,0,1:T(8,128)S(1)}, u32[]{:S(2)}, u32[]{:S(2)}) collective-permute-start(f32[4,1,1,1,1,1,16,128]{7,6,5,4,3,2,0,1:T(8,128)S(1)} %constant_dynamic-slice_fusion), channel_id=1, source_target_pairs={{0,4},{4,0},{8,12},{12,8},{16,20},{20,16},{24,28},{28,24},{1,5},{5... | collective-permute-start | bytes 98312 | tf_op jit(solution)/shard_map/ppermute | solution.py:98
  72.6 2.1 %collective-permute-done.16 = f32[4,1,1,1,1,1,16,128]{7,6,5,4,3,2,0,1:T(8,128)S(1)} collective-permute-done((f32[4,1,1,1,1,1,16,128]{7,6,5,4,3,2,0,1:T(8,128)S(1)}, f32[4,1,1,1,1,1,16,128]{7,6,5,4,3,2,0,1:T(8,128)S(1)}, u32[]{:S(2)}, u32[]{:S(2)}) %collective-permute-start.16) | collective-permute-done | bytes 32800 | tf_op jit(solution)/shard_map/ppermute | solution.py:98
  76.4 1.4 %collective-permute-start.19 = (bf16[4,1,1,1,1,1,16,128]{7,6,0,5,4,3,2,1:T(8,128)(2,1)S(1)}, bf16[4,1,1,1,1,1,16,128]{7,6,0,5,4,3,2,1:T(8,128)(2,1)S(1)}, u32[]{:S(2)}, u32[]{:S(2)}) collective-permute-start(bf16[4,1,1,1,1,1,16,128]{7,6,0,5,4,3,2,1:T(8,128)(2,1)S(1)} %get-tuple-element.53), channel_id=1, source_target_pairs={{0,4},{4,0},{8,12},{12,8},{16,20},{20,16},{24,28},{28,24},{1,5},{5... | collective-permute-start | bytes 49160 | tf_op jit(solution)/shard_map/ppermute | solution.py:103
  77.9 1.5 %convolution_bitcast_fusion = f32[1,512,256]{2,1,0:T(8,128)S(1)} fusion(bf16[4,512,256]{2,1,0:T(8,128)(2,1)S(1)} %copy-done.10, pred[4]{0:T(512)(128)(4,1)S(1)} %copy-done.25, bf16[4,4,256,256]{3,2,1,0:T(8,128)(2,1)} %param.12), kind=kOutput, calls=%fused_computation.18 | convolution fusion | flops 268959744 | bytes 2097156 | tf_op jit(solution)/shard_map/jerb,jebc->jrc/dot_general | solution.py:156
  79.4 1.3 %collective-permute-start.18 = (bf16[4,1,1,1,1,1,16,128]{7,6,0,5,4,3,2,1:T(8,128)(2,1)S(1)}, bf16[4,1,1,1,1,1,16,128]{7,6,0,5,4,3,2,1:T(8,128)(2,1)S(1)}, u32[]{:S(2)}, u32[]{:S(2)}) collective-permute-start(bf16[4,1,1,1,1,1,16,128]{7,6,0,5,4,3,2,1:T(8,128)(2,1)S(1)} %get-tuple-element.54), channel_id=1, source_target_pairs={{0,2},{1,3},{2,0},{3,1},{4,6},{5,7},{6,4},{7,5},{8,10},{9,11},{10,... | collective-permute-start | bytes 49160 | tf_op jit(solution)/shard_map/ppermute | solution.py:103
  80.7 2.5 %collective-permute-done.18 = bf16[4,1,1,1,1,1,16,128]{7,6,0,5,4,3,2,1:T(8,128)(2,1)S(1)} collective-permute-done((bf16[4,1,1,1,1,1,16,128]{7,6,0,5,4,3,2,1:T(8,128)(2,1)S(1)}, bf16[4,1,1,1,1,1,16,128]{7,6,0,5,4,3,2,1:T(8,128)(2,1)S(1)}, u32[]{:S(2)}, u32[]{:S(2)}) %collective-permute-start.18) | collective-permute-done | bytes 16416 | tf_op jit(solution)/shard_map/ppermute | solution.py:103
  83.2 2.1 %collective-permute-done.17 = bf16[4,1,1,1,1,1,16,128]{7,6,0,5,4,3,2,1:T(8,128)(2,1)S(1)} collective-permute-done((bf16[4,1,1,1,1,1,16,128]{7,6,0,5,4,3,2,1:T(8,128)(2,1)S(1)}, bf16[4,1,1,1,1,1,16,128]{7,6,0,5,4,3,2,1:T(8,128)(2,1)S(1)}, u32[]{:S(2)}, u32[]{:S(2)}) %collective-permute-start.17) | collective-permute-done | bytes 16416 | tf_op jit(solution)/shard_map/ppermute | solution.py:103
  87.7 1.8 %collective-permute-done.20 = bf16[4,1,1,1,1,2,16,128]{7,6,0,5,4,3,2,1:T(8,128)(2,1)S(1)} collective-permute-done((bf16[4,1,1,1,1,2,16,128]{7,6,0,5,4,3,2,1:T(8,128)(2,1)S(1)}, bf16[4,1,1,1,1,2,16,128]{7,6,0,5,4,3,2,1:T(8,128)(2,1)S(1)}, u32[]{:S(2)}, u32[]{:S(2)}) %collective-permute-start.20) | collective-permute-done | bytes 32800 | tf_op jit(solution)/shard_map/ppermute | solution.py:103
  90.4 1.9 %collective-permute-start.24 = (bf16[4,1,2,1,1,2,16,128]{7,6,0,5,4,3,2,1:T(8,128)(2,1)S(1)}, bf16[4,1,2,1,1,2,16,128]{7,6,0,5,4,3,2,1:T(8,128)(2,1)S(1)}, u32[]{:S(2)}, u32[]{:S(2)}) collective-permute-start(bf16[4,1,2,1,1,2,16,128]{7,6,0,5,4,3,2,1:T(8,128)(2,1)S(1)} %maximum_select_fusion.11), channel_id=1, source_target_pairs={{0,8},{4,12},{8,0},{12,4},{16,24},{20,28},{24,16},{28,20},{1,9},{5... | collective-permute-start | bytes 196616 | tf_op jit(solution)/shard_map/ppermute | solution.py:103
  94.8 1.3 %collective-permute-start.25 = (bf16[4,1,2,1,2,2,16,128]{7,6,0,5,4,3,2,1:T(8,128)(2,1)S(1)}, bf16[4,1,2,1,2,2,16,128]{7,6,0,5,4,3,2,1:T(8,128)(2,1)S(1)}, u32[]{:S(2)}, u32[]{:S(2)}) collective-permute-start(bf16[4,1,2,1,2,2,16,128]{7,6,0,5,4,3,2,1:T(8,128)(2,1)S(1)} %maximum_select_fusion.6), channel_id=1, source_target_pairs={{0,4},{4,0},{8,12},{12,8},{16,20},{20,16},{24,28},{28,24},{1,5},{5... | collective-permute-start | bytes 393224 | tf_op jit(solution)/shard_map/ppermute | solution.py:103
  96.1 1.8 %collective-permute-done.27 = bf16[4,1,2,2,1,1,16,128]{7,6,0,5,4,3,2,1:T(8,128)(2,1)S(1)} collective-permute-done((bf16[4,1,2,2,1,1,16,128]{7,6,0,5,4,3,2,1:T(8,128)(2,1)S(1)}, bf16[4,1,2,2,1,1,16,128]{7,6,0,5,4,3,2,1:T(8,128)(2,1)S(1)}, u32[]{:S(2)}, u32[]{:S(2)}) %collective-permute-start.27) | collective-permute-done | bytes 65568 | tf_op jit(solution)/shard_map/ppermute | solution.py:103
  99.9 3.1 %collective-permute-done.28 = bf16[4,1,2,2,1,2,16,128]{7,6,0,5,4,3,2,1:T(8,128)(2,1)S(1)} collective-permute-done((bf16[4,1,2,2,1,2,16,128]{7,6,0,5,4,3,2,1:T(8,128)(2,1)S(1)}, bf16[4,1,2,2,1,2,16,128]{7,6,0,5,4,3,2,1:T(8,128)(2,1)S(1)}, u32[]{:S(2)}, u32[]{:S(2)}) %collective-permute-start.28) | collective-permute-done | bytes 131104 | tf_op jit(solution)/shard_map/ppermute | solution.py:103
  104.2 1.3 %collective-permute-done.29 = bf16[12,256,128]{2,1,0:T(8,128)(2,1)S(1)} collective-permute-done((bf16[12,256,128]{2,1,0:T(8,128)(2,1)S(1)}, bf16[12,256,128]{2,1,0:T(8,128)(2,1)S(1)}, u32[]{:S(2)}, u32[]{:S(2)}) %collective-permute-start.29) | collective-permute-done | bytes 786464 | tf_op jit(solution)/shard_map/ppermute | solution.py:187
  107.5 1.5 %fusion.3 = bf16[4,512,256]{2,1,0:T(8,128)(2,1)} fusion(f32[1,512,256]{2,1,0:T(8,128)S(1)} %convolution_bitcast_fusion, f32[3,512,256]{2,1,0:T(8,128)S(1)} %copy-done.26, bf16[4,2,256,128]{3,2,1,0:T(8,128)(2,1)S(1)} %copy-done.8, bf16[4,2,256,128]{3,2,1,0:T(8,128)(2,1)S(1)} %get-tuple-element.57, bf16[4,2,256,128]{3,2,1,0:T(8,128)(2,1)S(1)} %get-tuple-element.56, ...), kind=kOutput, calls=%fused_computation.11 | convolution fusion | flops 274726912 | bytes 4718593 | tf_op jit(solution)/shard_map/jqrc,jqbc->jrb/dot_general | solution.py:196
  (180 shorter events, 35.7 us)
Async XLA Ops:
  6.6 18.1 %collective-permute-start.2 = (f32[12,256,128]{2,1,0:T(8,128)}, f32[12,256,128]{2,1,0:T(8,128)}, u32[]{:S(2)}, u32[]{:S(2)}) collective-permute-start(f32[12,256,128]{2,1,0:T(8,128)} %shard_map.83), channel_id=1, source_target_pairs={{0,1},{1,0},{2,3},{3,2},{4,5},{5,4},{6,7},{7,6},{8,9},{9,8},{10,11... | collective-permute-start | bytes 4718600 | tf_op jit(solution)/shard_map/ppermute | solution.py:137
  7.1 16.3 %collective-permute-start = (bf16[1,512,256]{2,1,0:T(8,128)(2,1)S(1)}, bf16[1,512,256]{2,1,0:T(8,128)(2,1)}, u32[]{:S(2)}, u32[]{:S(2)}) collective-permute-start(bf16[1,512,256]{2,1,0:T(8,128)(2,1)S(1)} %get-tuple-element.51), channel_id=1, source_target_pairs={{0,1},{1,2},{2,3},{3,4},{4,5},{5,6},{6,7},{7,8},{8,9},{9,10},{10,1... | collective-permute-start | bytes 786440 | tf_op jit(solution)/shard_map/ppermute | solution.py:65
  9.8 13.7 %collective-permute-start.1 = (bf16[1,512,256]{2,1,0:T(8,128)(2,1)S(1)}, bf16[1,512,256]{2,1,0:T(8,128)(2,1)}, u32[]{:S(2)}, u32[]{:S(2)}) collective-permute-start(bf16[1,512,256]{2,1,0:T(8,128)(2,1)S(1)} %get-tuple-element.52), channel_id=1, source_target_pairs={{1,0},{2,1},{3,2},{4,3},{5,4},{6,5},{7,6},{8,7},{9,8},{10,9},{11,1... | collective-permute-start | bytes 786440 | tf_op jit(solution)/shard_map/ppermute | solution.py:67
  11.2 11.7 %copy-start.19 = (bf16[3,4,8,128]{3,2,1,0:T(8,128)(2,1)}, bf16[3,4,8,128]{3,2,1,0:T(8,128)(2,1)S(1)}, u32[]{:S(2)}) copy-start(bf16[3,4,8,128]{3,2,1,0:T(8,128)(2,1)S(1)} %broadcast_in_dim.61) | copy-start | bytes 73732
  12.0 16.5 %collective-permute-start.3 = (bf16[3,4,136,128]{3,2,1,0:T(8,128)(2,1)}, bf16[3,4,136,128]{3,2,1,0:T(8,128)(2,1)S(1)}, u32[]{:S(2)}, u32[]{:S(2)}) collective-permute-start(bf16[3,4,136,128]{3,2,1,0:T(8,128)(2,1)} %pad_maximum_fusion.3), channel_id=1, source_target_pairs={{0,2},{1,3},{2,0},{3,1},{4,6},{5,7},{6,4},{7,5},{8,10},{9,11},{10,... | collective-permute-start | bytes 1253384 | tf_op jit(solution)/shard_map/ppermute | solution.py:142
  30.2 13.8 %collective-permute-start.6 = (f32[4,1,2,2,1,2,16,128]{7,6,5,4,3,2,0,1:T(8,128)}, f32[4,1,2,2,1,2,16,128]{7,6,5,4,3,2,0,1:T(8,128)}, u32[]{:S(2)}, u32[]{:S(2)}) collective-permute-start(f32[4,1,2,2,1,2,16,128]{7,6,5,4,3,2,0,1:T(8,128)} %constant_dynamic-slice_fusion.9), channel_id=1, source_target_pairs={{0,8},{4,12},{8,0},{12,4},{16,24},{20,28},{24,16},{28,20},{1,9},{5... | collective-permute-start | bytes 786440 | tf_op jit(solution)/shard_map/ppermute | solution.py:98
  33.4 12.6 %collective-permute-start.5 = (f32[4,1,2,1,2,2,16,128]{7,6,5,4,3,2,0,1:T(8,128)}, f32[4,1,2,1,2,2,16,128]{7,6,5,4,3,2,0,1:T(8,128)}, u32[]{:S(2)}, u32[]{:S(2)}) collective-permute-start(f32[4,1,2,1,2,2,16,128]{7,6,5,4,3,2,0,1:T(8,128)} %constant_dynamic-slice_fusion.10), channel_id=1, source_target_pairs={{0,4},{4,0},{8,12},{12,8},{16,20},{20,16},{24,28},{28,24},{1,5},{5... | collective-permute-start | bytes 786440 | tf_op jit(solution)/shard_map/ppermute | solution.py:98
  34.7 12.3 %collective-permute-start.4 = (f32[4,1,1,2,2,2,16,128]{7,6,5,4,3,2,0,1:T(8,128)}, f32[4,1,1,2,2,2,16,128]{7,6,5,4,3,2,0,1:T(8,128)}, u32[]{:S(2)}, u32[]{:S(2)}) collective-permute-start(f32[4,1,1,2,2,2,16,128]{7,6,5,4,3,2,0,1:T(8,128)} %constant_dynamic-slice_fusion.11), channel_id=1, source_target_pairs={{0,2},{1,3},{2,0},{3,1},{4,6},{5,7},{6,4},{7,5},{8,10},{9,11},{10,... | collective-permute-start | bytes 786440 | tf_op jit(solution)/shard_map/ppermute | solution.py:98
  48.8 11.0 %collective-permute-start.10 = (f32[4,1,2,2,1,1,16,128]{7,6,5,4,3,2,0,1:T(8,128)}, f32[4,1,2,2,1,1,16,128]{7,6,5,4,3,2,0,1:T(8,128)S(1)}, u32[]{:S(2)}, u32[]{:S(2)}) collective-permute-start(f32[4,1,2,2,1,1,16,128]{7,6,5,4,3,2,0,1:T(8,128)} %constant_dynamic-slice_fusion.6), channel_id=1, source_target_pairs={{0,16},{4,20},{8,24},{12,28},{16,0},{20,4},{24,8},{28,12},{1,17},{... | collective-permute-start | bytes 393224 | tf_op jit(solution)/shard_map/ppermute | solution.py:98
  50.0 7.0 %collective-permute-start.9 = (f32[4,1,2,1,1,2,16,128]{7,6,5,4,3,2,0,1:T(8,128)S(1)}, f32[4,1,2,1,1,2,16,128]{7,6,5,4,3,2,0,1:T(8,128)}, u32[]{:S(2)}, u32[]{:S(2)}) collective-permute-start(f32[4,1,2,1,1,2,16,128]{7,6,5,4,3,2,0,1:T(8,128)S(1)} %constant_dynamic-slice_fusion.7), channel_id=1, source_target_pairs={{0,8},{4,12},{8,0},{12,4},{16,24},{20,28},{24,16},{28,20},{1,9},{5... | collective-permute-start | bytes 393224 | tf_op jit(solution)/shard_map/ppermute | solution.py:98
  52.0 7.9 %collective-permute-start.7 = (bf16[6,4,136,128]{3,2,1,0:T(8,128)(2,1)S(1)}, bf16[6,4,136,128]{3,2,1,0:T(8,128)(2,1)}, u32[]{:S(2)}, u32[]{:S(2)}) collective-permute-start(bf16[6,4,136,128]{3,2,1,0:T(8,128)(2,1)S(1)} %pad_maximum_fusion.1), channel_id=1, source_target_pairs={{0,1},{1,0},{2,3},{3,2},{4,5},{5,4},{6,7},{7,6},{8,9},{9,8},{10,11... | collective-permute-start | bytes 2506760 | tf_op jit(solution)/shard_map/ppermute | solution.py:165
  52.7 6.2 %collective-permute-start.8 = (f32[4,1,1,1,2,2,16,128]{7,6,5,4,3,2,0,1:T(8,128)}, f32[4,1,1,1,2,2,16,128]{7,6,5,4,3,2,0,1:T(8,128)}, u32[]{:S(2)}, u32[]{:S(2)}) collective-permute-start(f32[4,1,1,1,2,2,16,128]{7,6,5,4,3,2,0,1:T(8,128)} %constant_dynamic-slice_fusion.8), channel_id=1, source_target_pairs={{0,4},{4,0},{8,12},{12,8},{16,20},{20,16},{24,28},{28,24},{1,5},{5... | collective-permute-start | bytes 393224 | tf_op jit(solution)/shard_map/ppermute | solution.py:98
  62.3 13.1 %copy-start.16 = (bf16[12,4,136,128]{3,2,1,0:T(8,128)(2,1)S(1)}, bf16[12,4,136,128]{3,2,1,0:T(8,128)(2,1)}, u32[]{:S(2)}) copy-start(bf16[12,4,136,128]{3,2,1,0:T(8,128)(2,1)} %copy-done.15) | copy-start | bytes 5013508
  62.5 4.8 %collective-permute-start.11 = (f32[4,1,1,1,1,2,16,128]{7,6,5,4,3,2,0,1:T(8,128)S(1)}, f32[4,1,1,1,1,2,16,128]{7,6,5,4,3,2,0,1:T(8,128)S(1)}, u32[]{:S(2)}, u32[]{:S(2)}) collective-permute-start(f32[4,1,1,1,1,2,16,128]{7,6,5,4,3,2,0,1:T(8,128)S(1)} %constant_dynamic-slice_fusion.5), channel_id=1, source_target_pairs={{0,8},{4,12},{8,0},{12,4},{16,24},{20,28},{24,16},{28,20},{1,9},{5... | collective-permute-start | bytes 196616 | tf_op jit(solution)/shard_map/ppermute | solution.py:98
  62.9 5.5 %collective-permute-start.13 = (f32[4,1,2,1,1,1,16,128]{7,6,5,4,3,2,0,1:T(8,128)S(1)}, f32[4,1,2,1,1,1,16,128]{7,6,5,4,3,2,0,1:T(8,128)S(1)}, u32[]{:S(2)}, u32[]{:S(2)}) collective-permute-start(f32[4,1,2,1,1,1,16,128]{7,6,5,4,3,2,0,1:T(8,128)S(1)} %constant_dynamic-slice_fusion.3), channel_id=1, source_target_pairs={{0,16},{4,20},{8,24},{12,28},{16,0},{20,4},{24,8},{28,12},{1,17},{... | collective-permute-start | bytes 196616 | tf_op jit(solution)/shard_map/ppermute | solution.py:98
  64.5 6.3 %collective-permute-start.15 = (f32[4,1,1,2,1,1,16,128]{7,6,5,4,3,2,0,1:T(8,128)S(1)}, f32[4,1,1,2,1,1,16,128]{7,6,5,4,3,2,0,1:T(8,128)S(1)}, u32[]{:S(2)}, u32[]{:S(2)}) collective-permute-start(f32[4,1,1,2,1,1,16,128]{7,6,5,4,3,2,0,1:T(8,128)S(1)} %constant_dynamic-slice_fusion.1), channel_id=1, source_target_pairs={{0,2},{1,3},{2,0},{3,1},{4,6},{5,7},{6,4},{7,5},{8,10},{9,11},{10,... | collective-permute-start | bytes 196616 | tf_op jit(solution)/shard_map/ppermute | solution.py:98
  67.3 5.1 %collective-permute-start.12 = (f32[4,1,1,1,1,1,16,128]{7,6,5,4,3,2,0,1:T(8,128)S(1)}, f32[4,1,1,1,1,1,16,128]{7,6,5,4,3,2,0,1:T(8,128)S(1)}, u32[]{:S(2)}, u32[]{:S(2)}) collective-permute-start(f32[4,1,1,1,1,1,16,128]{7,6,5,4,3,2,0,1:T(8,128)S(1)} %constant_dynamic-slice_fusion.4), channel_id=1, source_target_pairs={{0,16},{4,20},{8,24},{12,28},{16,0},{20,4},{24,8},{28,12},{1,17},{... | collective-permute-start | bytes 98312 | tf_op jit(solution)/shard_map/ppermute | solution.py:98
  68.4 4.2 %collective-permute-start.14 = (f32[4,1,1,1,1,1,16,128]{7,6,5,4,3,2,0,1:T(8,128)S(1)}, f32[4,1,1,1,1,1,16,128]{7,6,5,4,3,2,0,1:T(8,128)S(1)}, u32[]{:S(2)}, u32[]{:S(2)}) collective-permute-start(f32[4,1,1,1,1,1,16,128]{7,6,5,4,3,2,0,1:T(8,128)S(1)} %constant_dynamic-slice_fusion.2), channel_id=1, source_target_pairs={{0,2},{1,3},{2,0},{3,1},{4,6},{5,7},{6,4},{7,5},{8,10},{9,11},{10,... | collective-permute-start | bytes 98312 | tf_op jit(solution)/shard_map/ppermute | solution.py:98
  70.8 4.0 %collective-permute-start.16 = (f32[4,1,1,1,1,1,16,128]{7,6,5,4,3,2,0,1:T(8,128)S(1)}, f32[4,1,1,1,1,1,16,128]{7,6,5,4,3,2,0,1:T(8,128)S(1)}, u32[]{:S(2)}, u32[]{:S(2)}) collective-permute-start(f32[4,1,1,1,1,1,16,128]{7,6,5,4,3,2,0,1:T(8,128)S(1)} %constant_dynamic-slice_fusion), channel_id=1, source_target_pairs={{0,4},{4,0},{8,12},{12,8},{16,20},{20,16},{24,28},{28,24},{1,5},{5... | collective-permute-start | bytes 98312 | tf_op jit(solution)/shard_map/ppermute | solution.py:98
  76.4 4.3 %collective-permute-start.19 = (bf16[4,1,1,1,1,1,16,128]{7,6,0,5,4,3,2,1:T(8,128)(2,1)S(1)}, bf16[4,1,1,1,1,1,16,128]{7,6,0,5,4,3,2,1:T(8,128)(2,1)S(1)}, u32[]{:S(2)}, u32[]{:S(2)}) collective-permute-start(bf16[4,1,1,1,1,1,16,128]{7,6,0,5,4,3,2,1:T(8,128)(2,1)S(1)} %get-tuple-element.53), channel_id=1, source_target_pairs={{0,4},{4,0},{8,12},{12,8},{16,20},{20,16},{24,28},{28,24},{1,5},{5... | collective-permute-start | bytes 49160 | tf_op jit(solution)/shard_map/ppermute | solution.py:103
  79.4 3.8 %collective-permute-start.18 = (bf16[4,1,1,1,1,1,16,128]{7,6,0,5,4,3,2,1:T(8,128)(2,1)S(1)}, bf16[4,1,1,1,1,1,16,128]{7,6,0,5,4,3,2,1:T(8,128)(2,1)S(1)}, u32[]{:S(2)}, u32[]{:S(2)}) collective-permute-start(bf16[4,1,1,1,1,1,16,128]{7,6,0,5,4,3,2,1:T(8,128)(2,1)S(1)} %get-tuple-element.54), channel_id=1, source_target_pairs={{0,2},{1,3},{2,0},{3,1},{4,6},{5,7},{6,4},{7,5},{8,10},{9,11},{10,... | collective-permute-start | bytes 49160 | tf_op jit(solution)/shard_map/ppermute | solution.py:103
  80.7 4.6 %collective-permute-start.17 = (bf16[4,1,1,1,1,1,16,128]{7,6,0,5,4,3,2,1:T(8,128)(2,1)S(1)}, bf16[4,1,1,1,1,1,16,128]{7,6,0,5,4,3,2,1:T(8,128)(2,1)S(1)}, u32[]{:S(2)}, u32[]{:S(2)}) collective-permute-start(bf16[4,1,1,1,1,1,16,128]{7,6,0,5,4,3,2,1:T(8,128)(2,1)S(1)} %get-tuple-element.55), channel_id=1, source_target_pairs={{0,16},{4,20},{8,24},{12,28},{16,0},{20,4},{24,8},{28,12},{1,17},{... | collective-permute-start | bytes 49160 | tf_op jit(solution)/shard_map/ppermute | solution.py:103
  85.4 4.1 %collective-permute-start.20 = (bf16[4,1,1,1,1,2,16,128]{7,6,0,5,4,3,2,1:T(8,128)(2,1)S(1)}, bf16[4,1,1,1,1,2,16,128]{7,6,0,5,4,3,2,1:T(8,128)(2,1)S(1)}, u32[]{:S(2)}, u32[]{:S(2)}) collective-permute-start(bf16[4,1,1,1,1,2,16,128]{7,6,0,5,4,3,2,1:T(8,128)(2,1)S(1)} %maximum_select_fusion.13), channel_id=1, source_target_pairs={{0,8},{4,12},{8,0},{12,4},{16,24},{20,28},{24,16},{28,20},{1,9},{5... | collective-permute-start | bytes 98312 | tf_op jit(solution)/shard_map/ppermute | solution.py:103
  85.4 4.9 %collective-permute-start.23 = (bf16[4,1,2,1,1,1,16,128]{7,6,0,2,5,4,3,1:T(8,128)(2,1)S(1)}, bf16[4,1,2,1,1,1,16,128]{7,6,0,2,5,4,3,1:T(8,128)(2,1)S(1)}, u32[]{:S(2)}, u32[]{:S(2)}) collective-permute-start(bf16[4,1,2,1,1,1,16,128]{7,6,0,2,5,4,3,1:T(8,128)(2,1)S(1)} %bitcast.89), channel_id=1, source_target_pairs={{0,16},{4,20},{8,24},{12,28},{16,0},{20,4},{24,8},{28,12},{1,17},{... | collective-permute-start | bytes 98312 | tf_op jit(solution)/shard_map/ppermute | solution.py:103
  86.6 5.8 %collective-permute-start.26 = (bf16[4,1,1,2,1,1,16,128]{7,6,0,3,5,4,2,1:T(8,128)(2,1)S(1)}, bf16[4,1,1,2,1,1,16,128]{7,6,0,3,5,4,2,1:T(8,128)(2,1)S(1)}, u32[]{:S(2)}, u32[]{:S(2)}) collective-permute-start(bf16[4,1,1,2,1,1,16,128]{7,6,0,3,5,4,2,1:T(8,128)(2,1)S(1)} %bitcast.86), channel_id=1, source_target_pairs={{0,2},{1,3},{2,0},{3,1},{4,6},{5,7},{6,4},{7,5},{8,10},{9,11},{10,... | collective-permute-start | bytes 98312 | tf_op jit(solution)/shard_map/ppermute | solution.py:103
  89.5 4.3 %collective-permute-start.21 = (bf16[4,1,1,1,2,2,16,128]{7,6,0,5,4,3,2,1:T(8,128)(2,1)S(1)}, bf16[4,1,1,1,2,2,16,128]{7,6,0,5,4,3,2,1:T(8,128)(2,1)S(1)}, u32[]{:S(2)}, u32[]{:S(2)}) collective-permute-start(bf16[4,1,1,1,2,2,16,128]{7,6,0,5,4,3,2,1:T(8,128)(2,1)S(1)} %maximum_select_fusion.9), channel_id=1, source_target_pairs={{0,4},{4,0},{8,12},{12,8},{16,20},{20,16},{24,28},{28,24},{1,5},{5... | collective-permute-start | bytes 196616 | tf_op jit(solution)/shard_map/ppermute | solution.py:103
  90.4 4.3 %collective-permute-start.24 = (bf16[4,1,2,1,1,2,16,128]{7,6,0,5,4,3,2,1:T(8,128)(2,1)S(1)}, bf16[4,1,2,1,1,2,16,128]{7,6,0,5,4,3,2,1:T(8,128)(2,1)S(1)}, u32[]{:S(2)}, u32[]{:S(2)}) collective-permute-start(bf16[4,1,2,1,1,2,16,128]{7,6,0,5,4,3,2,1:T(8,128)(2,1)S(1)} %maximum_select_fusion.11), channel_id=1, source_target_pairs={{0,8},{4,12},{8,0},{12,4},{16,24},{20,28},{24,16},{28,20},{1,9},{5... | collective-permute-start | bytes 196616 | tf_op jit(solution)/shard_map/ppermute | solution.py:103
  92.4 5.5 %collective-permute-start.27 = (bf16[4,1,2,2,1,1,16,128]{7,6,0,5,4,3,2,1:T(8,128)(2,1)S(1)}, bf16[4,1,2,2,1,1,16,128]{7,6,0,5,4,3,2,1:T(8,128)(2,1)S(1)}, u32[]{:S(2)}, u32[]{:S(2)}) collective-permute-start(bf16[4,1,2,2,1,1,16,128]{7,6,0,5,4,3,2,1:T(8,128)(2,1)S(1)} %fusion.36), channel_id=1, source_target_pairs={{0,16},{4,20},{8,24},{12,28},{16,0},{20,4},{24,8},{28,12},{1,17},{... | collective-permute-start | bytes 196616 | tf_op jit(solution)/shard_map/ppermute | solution.py:103
  93.9 5.0 %collective-permute-start.22 = (bf16[4,1,1,2,2,2,16,128]{7,6,0,5,4,3,2,1:T(8,128)(2,1)S(1)}, bf16[4,1,1,2,2,2,16,128]{7,6,0,5,4,3,2,1:T(8,128)(2,1)S(1)}, u32[]{:S(2)}, u32[]{:S(2)}) collective-permute-start(bf16[4,1,1,2,2,2,16,128]{7,6,0,5,4,3,2,1:T(8,128)(2,1)S(1)} %maximum_select_fusion.5), channel_id=1, source_target_pairs={{0,2},{1,3},{2,0},{3,1},{4,6},{5,7},{6,4},{7,5},{8,10},{9,11},{10,... | collective-permute-start | bytes 393224 | tf_op jit(solution)/shard_map/ppermute | solution.py:103
  94.8 5.0 %collective-permute-start.25 = (bf16[4,1,2,1,2,2,16,128]{7,6,0,5,4,3,2,1:T(8,128)(2,1)S(1)}, bf16[4,1,2,1,2,2,16,128]{7,6,0,5,4,3,2,1:T(8,128)(2,1)S(1)}, u32[]{:S(2)}, u32[]{:S(2)}) collective-permute-start(bf16[4,1,2,1,2,2,16,128]{7,6,0,5,4,3,2,1:T(8,128)(2,1)S(1)} %maximum_select_fusion.6), channel_id=1, source_target_pairs={{0,4},{4,0},{8,12},{12,8},{16,20},{20,16},{24,28},{28,24},{1,5},{5... | collective-permute-start | bytes 393224 | tf_op jit(solution)/shard_map/ppermute | solution.py:103
  97.9 5.0 %collective-permute-start.28 = (bf16[4,1,2,2,1,2,16,128]{7,6,0,5,4,3,2,1:T(8,128)(2,1)S(1)}, bf16[4,1,2,2,1,2,16,128]{7,6,0,5,4,3,2,1:T(8,128)(2,1)S(1)}, u32[]{:S(2)}, u32[]{:S(2)}) collective-permute-start(bf16[4,1,2,2,1,2,16,128]{7,6,0,5,4,3,2,1:T(8,128)(2,1)S(1)} %maximum_select_fusion.7), channel_id=1, source_target_pairs={{0,8},{4,12},{8,0},{12,4},{16,24},{20,28},{24,16},{28,20},{1,9},{5... | collective-permute-start | bytes 393224 | tf_op jit(solution)/shard_map/ppermute | solution.py:103
  103.1 2.4 %collective-permute-start.29 = (bf16[12,256,128]{2,1,0:T(8,128)(2,1)S(1)}, bf16[12,256,128]{2,1,0:T(8,128)(2,1)S(1)}, u32[]{:S(2)}, u32[]{:S(2)}) collective-permute-start(bf16[12,256,128]{2,1,0:T(8,128)(2,1)S(1)} %pad_maximum_fusion.2), channel_id=1, source_target_pairs={{0,1},{1,0},{2,3},{3,2},{4,5},{5,4},{6,7},{7,6},{8,9},{9,8},{10,11... | collective-permute-start | bytes 2359304 | tf_op jit(solution)/shard_map/ppermute | solution.py:187
  (25 other events, 122.7 us)

commit v24 on v22

--- a/solution.py
+++ b/solution.py
@@ -154,7 +154,7 @@
             local[0], extended, parts = lax.optimization_barrier((local[0], extended, parts))
             picked = jnp.take(extended, margin[split_at:], axis=0)
             local.append(jnp.einsum("jerb,jebc->jrc", picked, inverse_blocks[split_at:], preferred_element_type=jnp.float32))
-        if step == 2:
+        if step == 3:
             local[1], parts = lax.optimization_barrier((local[1], parts))
         k = step
         if arriving is not None:

time: 104 us -> 105 us (level)
  waiting for transfers between devices: 19.2 us -> 20.4 us
  transfers between devices with their start and end apart: 30 -> 30, of which waited for: 15 -> 13; matrix products, arithmetic and copies ran while one was open for 24% -> 23% of each run, Pallas kernels for 5% -> 5%
where the time goes in v24:
time: 105 us; the launch traced here: 104 us
  starting transfers between devices  35.6 us (34%)
  waiting for transfers between devices  20.4 us (19%)
  local copies, waits for them, and re-layouts  18.4 us (18%)
  Pallas kernels  10.3 us (10%)
  other arithmetic  9.86 us (9%)
  matrix products  9.2 us (9%)
    ppermute x12, starting transfers between devices, halve(): lax.ppermute(send.astype(wire), axis, pairs(axis, mask)).astype(x.dtype)  15.2 us
    ppermute x12, starting transfers between devices, double(): recv = lax.ppermute(y, axis, pairs(axis, mask))  11.7 us
    ppermute x12, waiting for transfers between devices, double(): recv = lax.ppermute(y, axis, pairs(axis, mask))  10.7 us
    pallas_call x2, Pallas kernels, restrict(): pl.pallas_call(functools.partial(restrict_kernel, upper=upper), out_shape...  10.3 us
    ppermute x12, waiting for transfers between devices, halve(): lax.ppermute(send.astype(wire), axis, pairs(axis, mask)).astype(x.dtype)  7.51 us
    unnamed x53, local copies, waits for them, and re-layouts  5.07 us
    dot_general x1, matrix products, per_device(): jnp.einsum('jerb,jebc->jrc', picked, inverse_blocks[:split_at], preferred...  4.6 us
    ppermute x1, starting transfers between devices, per_device(): arriving = lax.ppermute(packed, exchanges[0][0], pairs(*exchanges[0]))  4.14 us
  transfers between devices with their start and end apart: 30, of which 13 were waited for; matrix products, arithmetic and copies ran while one was open for 23% of the time, Pallas kernels for 5%

profile of v24, /device:TPU:0, one launch (start us, length us, event | category | flops | bytes accessed | tf_op | source)
XLA Modules:
  0.0 104.3 jit_solution(14432153233363470836)
XLA Ops:
  1.5 5.1 %shard_map.83 = f32[12,256,128]{2,1,0:T(8,128)} custom-call(s32[8]{0:T(128)} %reshape.1794.links, s32[1]{0:T(128)} %bitcast.half, bf16[4,512,256]{2,1,0:T(8,128)(2,1)} %residual_ref.3, bf16[4,2,256,128]{3,2,1,0:T(8,128)(2,1)} %basis_ref.3), custom_call_target="tpu_custom_call" | custom-call | flops 134217728 | bytes 3145728 | tf_op jit(solution)/shard_map/pallas_call | solution.py:36
  7.1 2.7 %collective-permute-start = (bf16[1,512,256]{2,1,0:T(8,128)(2,1)S(1)}, bf16[1,512,256]{2,1,0:T(8,128)(2,1)}, u32[]{:S(2)}, u32[]{:S(2)}) collective-permute-start(bf16[1,512,256]{2,1,0:T(8,128)(2,1)S(1)} %get-tuple-element.51), channel_id=1, source_target_pairs={{0,1},{1,2},{2,3},{3,4},{4,5},{5,6},{6,7},{7,8},{8,9},{9,10},{10,1... | collective-permute-start | bytes 786440 | tf_op jit(solution)/shard_map/ppermute | solution.py:65
  9.8 1.3 %collective-permute-start.1 = (bf16[1,512,256]{2,1,0:T(8,128)(2,1)S(1)}, bf16[1,512,256]{2,1,0:T(8,128)(2,1)}, u32[]{:S(2)}, u32[]{:S(2)}) collective-permute-start(bf16[1,512,256]{2,1,0:T(8,128)(2,1)S(1)} %get-tuple-element.52), channel_id=1, source_target_pairs={{1,0},{2,1},{3,2},{4,3},{5,4},{6,5},{7,6},{8,7},{9,8},{10,9},{11,1... | collective-permute-start | bytes 786440 | tf_op jit(solution)/shard_map/ppermute | solution.py:67
  12.0 4.1 %collective-permute-start.3 = (bf16[3,4,136,128]{3,2,1,0:T(8,128)(2,1)}, bf16[3,4,136,128]{3,2,1,0:T(8,128)(2,1)S(1)}, u32[]{:S(2)}, u32[]{:S(2)}) collective-permute-start(bf16[3,4,136,128]{3,2,1,0:T(8,128)(2,1)} %pad_maximum_fusion.3), channel_id=1, source_target_pairs={{0,2},{1,3},{2,0},{3,1},{4,6},{5,7},{6,4},{7,5},{8,10},{9,11},{10,... | collective-permute-start | bytes 1253384 | tf_op jit(solution)/shard_map/ppermute | solution.py:142
  18.7 5.2 %shard_map.82 = f32[12,256,128]{2,1,0:T(8,128)} custom-call(s32[8]{0:T(128)} %reshape.1794.links, s32[1]{0:T(128)} %bitcast.half, bf16[4,512,256]{2,1,0:T(8,128)(2,1)} %residual_ref.3, bf16[4,2,256,128]{3,2,1,0:T(8,128)(2,1)} %basis_ref.3), custom_call_target="tpu_custom_call" | custom-call | flops 134217728 | bytes 3145728 | tf_op jit(solution)/shard_map/pallas_call | solution.py:36
  24.5 1.2 %pad_maximum_fusion = bf16[6,512,256]{2,1,0:T(8,128)(2,1)S(1)} fusion(bf16[1,512,256]{2,1,0:T(8,128)(2,1)} %collective-permute-done.1, bf16[4,512,256]{2,1,0:T(8,128)(2,1)S(1)} %copy-done.2, bf16[1,512,256]{2,1,0:T(8,128)(2,1)} %collective-permute-done), kind=kLoop, calls=%fused_computation.14 | loop fusion | flops 1572864 | bytes 3145728 | tf_op jit(solution)/shard_map/concatenate | solution.py:63
  25.7 1.6 %add.237 = f32[12,256,128]{2,1,0:T(8,128)S(1)} add(f32[12,256,128]{2,1,0:T(8,128)S(1)} %copy-done.3, f32[12,256,128]{2,1,0:T(8,128)} %collective-permute-done.2) | non-fusion elementwise | flops 393216 | bytes 4718592 | tf_op jit(solution)/shard_map/add | solution.py:138
  27.3 1.2 %collective-permute-done.3 = bf16[3,4,136,128]{3,2,1,0:T(8,128)(2,1)S(1)} collective-permute-done((bf16[3,4,136,128]{3,2,1,0:T(8,128)(2,1)}, bf16[3,4,136,128]{3,2,1,0:T(8,128)(2,1)S(1)}, u32[]{:S(2)}, u32[]{:S(2)}) %collective-permute-start.3) | collective-permute-done | bytes 417824 | tf_op jit(solution)/shard_map/ppermute | solution.py:142
  30.2 2.4 %collective-permute-start.6 = (f32[4,1,2,2,1,2,16,128]{7,6,5,4,3,2,0,1:T(8,128)}, f32[4,1,2,2,1,2,16,128]{7,6,5,4,3,2,0,1:T(8,128)}, u32[]{:S(2)}, u32[]{:S(2)}) collective-permute-start(f32[4,1,2,2,1,2,16,128]{7,6,5,4,3,2,0,1:T(8,128)} %constant_dynamic-slice_fusion.9), channel_id=1, source_target_pairs={{0,8},{4,12},{8,0},{12,4},{16,24},{20,28},{24,16},{28,20},{1,9},{5... | collective-permute-start | bytes 786440 | tf_op jit(solution)/shard_map/ppermute | solution.py:98
  34.8 2.1 %collective-permute-start.4 = (f32[4,1,1,2,2,2,16,128]{7,6,5,4,3,2,0,1:T(8,128)}, f32[4,1,1,2,2,2,16,128]{7,6,5,4,3,2,0,1:T(8,128)}, u32[]{:S(2)}, u32[]{:S(2)}) collective-permute-start(f32[4,1,1,2,2,2,16,128]{7,6,5,4,3,2,0,1:T(8,128)} %constant_dynamic-slice_fusion.11), channel_id=1, source_target_pairs={{0,2},{1,3},{2,0},{3,1},{4,6},{5,7},{6,4},{7,5},{8,10},{9,11},{10,... | collective-permute-start | bytes 786440 | tf_op jit(solution)/shard_map/ppermute | solution.py:98
  36.8 2.5 %gather_fusion = bf16[12,512,256]{2,1,0:T(8,128)(2,1)} fusion(bf16[6,512,256]{2,1,0:T(8,128)(2,1)S(1)} %pad_maximum_fusion, s32[1024]{0:T(1024)S(1)} %pad_clamp_fusion.5), kind=kCustom, calls=%fused_computation.2 | custom fusion | bytes 6291504 | tf_op jit(solution)/shard_map/jit(_take)/gather | solution.py:149
  39.3 4.6 %fusion.8 = f32[3,512,256]{2,1,0:T(8,128)} fusion(bf16[4,4,256,256]{3,2,1,0:T(8,128)(2,1)} %param.12, bf16[3,4,512,256]{3,2,1,0:T(8,128)(2,1)} %bitcast.100, pred[3,4]{1,0:T(4,128)(4,1)S(1)} %compare_and_fusion.3), kind=kOutput, calls=%fused_computation.17 | convolution fusion | flops 806879232 | bytes 6291468 | tf_op jit(solution)/shard_map/jerb,jebc->jrc/dot_general | solution.py:150
  49.2 2.0 %collective-permute-start.9 = (f32[4,1,2,1,1,2,16,128]{7,6,5,4,3,2,0,1:T(8,128)S(1)}, f32[4,1,2,1,1,2,16,128]{7,6,5,4,3,2,0,1:T(8,128)S(1)}, u32[]{:S(2)}, u32[]{:S(2)}) collective-permute-start(f32[4,1,2,1,1,2,16,128]{7,6,5,4,3,2,0,1:T(8,128)S(1)} %constant_dynamic-slice_fusion.7), channel_id=1, source_target_pairs={{0,8},{4,12},{8,0},{12,4},{16,24},{20,28},{24,16},{28,20},{1,9},{5... | collective-permute-start | bytes 393224 | tf_op jit(solution)/shard_map/ppermute | solution.py:98
  52.4 1.7 %gather_fusion.1 = bf16[4,512,256]{2,1,0:T(8,128)(2,1)} fusion(bf16[6,512,256]{2,1,0:T(8,128)(2,1)S(1)} %pad_maximum_fusion, s32[1024]{0:T(1024)} %pad_clamp_fusion.4), kind=kCustom, calls=%fused_computation.3 | custom fusion | bytes 2097168 | tf_op jit(solution)/shard_map/jit(_take)/gather | solution.py:155
  54.1 2.7 %convolution_bitcast_fusion = f32[1,512,256]{2,1,0:T(8,128)} fusion(bf16[4,512,256]{2,1,0:T(8,128)(2,1)} %gather_fusion.1, pred[4]{0:T(512)(128)(4,1)S(1)} %copy-done.22, bf16[4,4,256,256]{3,2,1,0:T(8,128)(2,1)} %param.12), kind=kOutput, calls=%fused_computation.18 | convolution fusion | flops 268959744 | bytes 2097156 | tf_op jit(solution)/shard_map/jerb,jebc->jrc/dot_general | solution.py:156
  57.9 1.3 %constant_dynamic-update-slice_fusion = bf16[12,4,136,128]{3,2,1,0:T(8,128)(2,1)S(1)} fusion(bf16[12,4,136,128]{3,2,1,0:T(8,128)(2,1)S(1)} %constant_dynamic-update-slice_fusion.1, bf16[6,4,136,128]{3,2,1,0:T(8,128)(2,1)} %collective-permute-done.7), kind=kLoop, calls=%fused_computation.107 | loop fusion | bytes 1671168 | tf_op jit(solution)/shard_map/concatenate | solution.py:162
  60.3 1.9 %collective-permute-start.11 = (f32[4,1,1,1,1,2,16,128]{7,6,5,4,3,2,0,1:T(8,128)S(1)}, f32[4,1,1,1,1,2,16,128]{7,6,5,4,3,2,0,1:T(8,128)S(1)}, u32[]{:S(2)}, u32[]{:S(2)}) collective-permute-start(f32[4,1,1,1,1,2,16,128]{7,6,5,4,3,2,0,1:T(8,128)S(1)} %constant_dynamic-slice_fusion.5), channel_id=1, source_target_pairs={{0,8},{4,12},{8,0},{12,4},{16,24},{20,28},{24,16},{28,20},{1,9},{5... | collective-permute-start | bytes 196616 | tf_op jit(solution)/shard_map/ppermute | solution.py:98
  62.5 1.4 %collective-permute-done.13 = f32[4,1,1,2,1,1,16,128]{7,6,5,4,3,2,0,1:T(8,128)S(1)} collective-permute-done((f32[4,1,1,2,1,1,16,128]{7,6,5,4,3,2,0,1:T(8,128)S(1)}, f32[4,1,1,2,1,1,16,128]{7,6,5,4,3,2,0,1:T(8,128)S(1)}, u32[]{:S(2)}, u32[]{:S(2)}) %collective-permute-start.13) | collective-permute-done | bytes 65568 | tf_op jit(solution)/shard_map/ppermute | solution.py:98
  63.9 2.7 %collective-permute-done.12 = f32[4,1,2,1,1,1,16,128]{7,6,5,4,3,2,0,1:T(8,128)S(1)} collective-permute-done((f32[4,1,2,1,1,1,16,128]{7,6,5,4,3,2,0,1:T(8,128)S(1)}, f32[4,1,2,1,1,1,16,128]{7,6,5,4,3,2,0,1:T(8,128)S(1)}, u32[]{:S(2)}, u32[]{:S(2)}) %collective-permute-start.12) | collective-permute-done | bytes 65568 | tf_op jit(solution)/shard_map/ppermute | solution.py:98
  66.7 1.8 %collective-permute-start.14 = (f32[4,1,1,1,1,1,16,128]{7,6,5,4,3,2,0,1:T(8,128)S(1)}, f32[4,1,1,1,1,1,16,128]{7,6,5,4,3,2,0,1:T(8,128)S(1)}, u32[]{:S(2)}, u32[]{:S(2)}) collective-permute-start(f32[4,1,1,1,1,1,16,128]{7,6,5,4,3,2,0,1:T(8,128)S(1)} %constant_dynamic-slice_fusion.2), channel_id=1, source_target_pairs={{0,16},{4,20},{8,24},{12,28},{16,0},{20,4},{24,8},{28,12},{1,17},{... | collective-permute-start | bytes 98312 | tf_op jit(solution)/shard_map/ppermute | solution.py:98
  70.3 1.3 %collective-permute-done.14 = f32[4,1,1,1,1,1,16,128]{7,6,5,4,3,2,0,1:T(8,128)S(1)} collective-permute-done((f32[4,1,1,1,1,1,16,128]{7,6,5,4,3,2,0,1:T(8,128)S(1)}, f32[4,1,1,1,1,1,16,128]{7,6,5,4,3,2,0,1:T(8,128)S(1)}, u32[]{:S(2)}, u32[]{:S(2)}) %collective-permute-start.14) | collective-permute-done | bytes 32800 | tf_op jit(solution)/shard_map/ppermute | solution.py:98
  75.4 1.2 %collective-permute-start.17 = (bf16[4,1,1,1,1,1,16,128]{7,6,0,5,4,3,2,1:T(8,128)(2,1)S(1)}, bf16[4,1,1,1,1,1,16,128]{7,6,0,5,4,3,2,1:T(8,128)(2,1)S(1)}, u32[]{:S(2)}, u32[]{:S(2)}) collective-permute-start(bf16[4,1,1,1,1,1,16,128]{7,6,0,5,4,3,2,1:T(8,128)(2,1)S(1)} %get-tuple-element.54), channel_id=1, source_target_pairs={{0,16},{4,20},{8,24},{12,28},{16,0},{20,4},{24,8},{28,12},{1,17},{... | collective-permute-start | bytes 49160 | tf_op jit(solution)/shard_map/ppermute | solution.py:103
  77.5 1.2 %collective-permute-start.25 = (bf16[4,1,1,1,1,1,16,128]{7,6,0,5,4,3,2,1:T(8,128)(2,1)S(1)}, bf16[4,1,1,1,1,1,16,128]{7,6,0,5,4,3,2,1:T(8,128)(2,1)S(1)}, u32[]{:S(2)}, u32[]{:S(2)}) collective-permute-start(bf16[4,1,1,1,1,1,16,128]{7,6,0,5,4,3,2,1:T(8,128)(2,1)S(1)} %get-tuple-element.56), channel_id=1, source_target_pairs={{0,4},{4,0},{8,12},{12,8},{16,20},{20,16},{24,28},{28,24},{1,5},{5... | collective-permute-start | bytes 49160 | tf_op jit(solution)/shard_map/ppermute | solution.py:103
  78.8 1.4 %collective-permute-done.17 = bf16[4,1,1,1,1,1,16,128]{7,6,0,5,4,3,2,1:T(8,128)(2,1)S(1)} collective-permute-done((bf16[4,1,1,1,1,1,16,128]{7,6,0,5,4,3,2,1:T(8,128)(2,1)S(1)}, bf16[4,1,1,1,1,1,16,128]{7,6,0,5,4,3,2,1:T(8,128)(2,1)S(1)}, u32[]{:S(2)}, u32[]{:S(2)}) %collective-permute-start.17) | collective-permute-done | bytes 16416 | tf_op jit(solution)/shard_map/ppermute | solution.py:103
  80.2 1.5 %collective-permute-start.18 = (bf16[4,1,1,1,1,2,16,128]{7,6,0,5,4,3,2,1:T(8,128)(2,1)S(1)}, bf16[4,1,1,1,1,2,16,128]{7,6,0,5,4,3,2,1:T(8,128)(2,1)S(1)}, u32[]{:S(2)}, u32[]{:S(2)}) collective-permute-start(bf16[4,1,1,1,1,2,16,128]{7,6,0,5,4,3,2,1:T(8,128)(2,1)S(1)} %maximum_select_fusion.14), channel_id=1, source_target_pairs={{0,8},{4,12},{8,0},{12,4},{16,24},{20,28},{24,16},{28,20},{1,9},{5... | collective-permute-start | bytes 98312 | tf_op jit(solution)/shard_map/ppermute | solution.py:103
  84.8 2.5 %collective-permute-done.22 = bf16[4,1,2,1,1,1,16,128]{7,6,0,5,4,3,2,1:T(8,128)(2,1)S(1)} collective-permute-done((bf16[4,1,2,1,1,1,16,128]{7,6,0,5,4,3,2,1:T(8,128)(2,1)S(1)}, bf16[4,1,2,1,1,1,16,128]{7,6,0,5,4,3,2,1:T(8,128)(2,1)S(1)}, u32[]{:S(2)}, u32[]{:S(2)}) %collective-permute-start.22) | collective-permute-done | bytes 32800 | tf_op jit(solution)/shard_map/ppermute | solution.py:103
  87.5 1.8 %collective-permute-start.27 = (bf16[4,1,2,2,1,1,16,128]{7,6,0,5,4,3,2,1:T(8,128)(2,1)S(1)}, bf16[4,1,2,2,1,1,16,128]{7,6,0,5,4,3,2,1:T(8,128)(2,1)S(1)}, u32[]{:S(2)}, u32[]{:S(2)}) collective-permute-start(bf16[4,1,2,2,1,1,16,128]{7,6,0,5,4,3,2,1:T(8,128)(2,1)S(1)} %fusion.36), channel_id=1, source_target_pairs={{0,16},{4,20},{8,24},{12,28},{16,0},{20,4},{24,8},{28,12},{1,17},{... | collective-permute-start | bytes 196616 | tf_op jit(solution)/shard_map/ppermute | solution.py:103
  90.2 2.9 %collective-permute-done.23 = bf16[4,1,2,1,1,2,16,128]{7,6,0,5,4,3,2,1:T(8,128)(2,1)S(1)} collective-permute-done((bf16[4,1,2,1,1,2,16,128]{7,6,0,5,4,3,2,1:T(8,128)(2,1)S(1)}, bf16[4,1,2,1,1,2,16,128]{7,6,0,5,4,3,2,1:T(8,128)(2,1)S(1)}, u32[]{:S(2)}, u32[]{:S(2)}) %collective-permute-start.23) | collective-permute-done | bytes 65568 | tf_op jit(solution)/shard_map/ppermute | solution.py:103
  93.2 1.6 %collective-permute-start.28 = (bf16[4,1,2,2,1,2,16,128]{7,6,0,5,4,3,2,1:T(8,128)(2,1)S(1)}, bf16[4,1,2,2,1,2,16,128]{7,6,0,5,4,3,2,1:T(8,128)(2,1)S(1)}, u32[]{:S(2)}, u32[]{:S(2)}) collective-permute-start(bf16[4,1,2,2,1,2,16,128]{7,6,0,5,4,3,2,1:T(8,128)(2,1)S(1)} %maximum_select_fusion.7), channel_id=1, source_target_pairs={{0,8},{4,12},{8,0},{12,4},{16,24},{20,28},{24,16},{28,20},{1,9},{5... | collective-permute-start | bytes 393224 | tf_op jit(solution)/shard_map/ppermute | solution.py:103
  94.8 3.3 %collective-permute-done.24 = bf16[4,1,2,1,2,2,16,128]{7,6,0,5,4,3,2,1:T(8,128)(2,1)S(1)} collective-permute-done((bf16[4,1,2,1,2,2,16,128]{7,6,0,5,4,3,2,1:T(8,128)(2,1)S(1)}, bf16[4,1,2,1,2,2,16,128]{7,6,0,5,4,3,2,1:T(8,128)(2,1)S(1)}, u32[]{:S(2)}, u32[]{:S(2)}) %collective-permute-start.24) | collective-permute-done | bytes 131104 | tf_op jit(solution)/shard_map/ppermute | solution.py:103
  101.6 1.2 %copy-done.24 = f32[3,512,256]{2,1,0:T(8,128)S(1)} copy-done((f32[3,512,256]{2,1,0:T(8,128)S(1)}, f32[3,512,256]{2,1,0:T(8,128)}, u32[]{:S(2)}) %copy-start.24) | copy-done | bytes 1572888
  102.8 1.5 %fusion.3 = bf16[4,512,256]{2,1,0:T(8,128)(2,1)} fusion(f32[1,512,256]{2,1,0:T(8,128)S(1)} %copy-done.23, f32[3,512,256]{2,1,0:T(8,128)S(1)} %copy-done.24, bf16[4,2,256,128]{3,2,1,0:T(8,128)(2,1)S(1)} %copy-done.8, bf16[4,2,256,128]{3,2,1,0:T(8,128)(2,1)S(1)} %get-tuple-element.68, bf16[4,2,256,128]{3,2,1,0:T(8,128)(2,1)S(1)} %get-tuple-element.67, ...), kind=kOutput, calls=%fused_computation.11 | convolution fusion | flops 274726912 | bytes 4718593 | tf_op jit(solution)/shard_map/jqrc,jqbc->jrb/dot_general | solution.py:196
  (179 shorter events, 32.6 us)
Async XLA Ops:
  1.5 9.7 %copy-start.9 = (bf16[3,4,128,128]{3,2,1,0:T(8,128)(2,1)S(1)}, bf16[3,4,128,128]{3,2,1,0:T(8,128)(2,1)}, u32[]{:S(2)}) copy-start(bf16[3,4,128,128]{3,2,1,0:T(8,128)(2,1)} %param.16) | copy-start | bytes 1179652
  6.6 19.1 %collective-permute-start.2 = (f32[12,256,128]{2,1,0:T(8,128)}, f32[12,256,128]{2,1,0:T(8,128)}, u32[]{:S(2)}, u32[]{:S(2)}) collective-permute-start(f32[12,256,128]{2,1,0:T(8,128)} %shard_map.83), channel_id=1, source_target_pairs={{0,1},{1,0},{2,3},{3,2},{4,5},{5,4},{6,7},{7,6},{8,9},{9,8},{10,11... | collective-permute-start | bytes 4718600 | tf_op jit(solution)/shard_map/ppermute | solution.py:137
  7.1 17.3 %collective-permute-start = (bf16[1,512,256]{2,1,0:T(8,128)(2,1)S(1)}, bf16[1,512,256]{2,1,0:T(8,128)(2,1)}, u32[]{:S(2)}, u32[]{:S(2)}) collective-permute-start(bf16[1,512,256]{2,1,0:T(8,128)(2,1)S(1)} %get-tuple-element.51), channel_id=1, source_target_pairs={{0,1},{1,2},{2,3},{3,4},{4,5},{5,6},{6,7},{7,8},{8,9},{9,10},{10,1... | collective-permute-start | bytes 786440 | tf_op jit(solution)/shard_map/ppermute | solution.py:65
  9.8 14.7 %collective-permute-start.1 = (bf16[1,512,256]{2,1,0:T(8,128)(2,1)S(1)}, bf16[1,512,256]{2,1,0:T(8,128)(2,1)}, u32[]{:S(2)}, u32[]{:S(2)}) collective-permute-start(bf16[1,512,256]{2,1,0:T(8,128)(2,1)S(1)} %get-tuple-element.52), channel_id=1, source_target_pairs={{1,0},{2,1},{3,2},{4,3},{5,4},{6,5},{7,6},{8,7},{9,8},{10,9},{11,1... | collective-permute-start | bytes 786440 | tf_op jit(solution)/shard_map/ppermute | solution.py:67
  12.0 16.5 %collective-permute-start.3 = (bf16[3,4,136,128]{3,2,1,0:T(8,128)(2,1)}, bf16[3,4,136,128]{3,2,1,0:T(8,128)(2,1)S(1)}, u32[]{:S(2)}, u32[]{:S(2)}) collective-permute-start(bf16[3,4,136,128]{3,2,1,0:T(8,128)(2,1)} %pad_maximum_fusion.3), channel_id=1, source_target_pairs={{0,2},{1,3},{2,0},{3,1},{4,6},{5,7},{6,4},{7,5},{8,10},{9,11},{10,... | collective-permute-start | bytes 1253384 | tf_op jit(solution)/shard_map/ppermute | solution.py:142
  30.2 13.8 %collective-permute-start.6 = (f32[4,1,2,2,1,2,16,128]{7,6,5,4,3,2,0,1:T(8,128)}, f32[4,1,2,2,1,2,16,128]{7,6,5,4,3,2,0,1:T(8,128)}, u32[]{:S(2)}, u32[]{:S(2)}) collective-permute-start(f32[4,1,2,2,1,2,16,128]{7,6,5,4,3,2,0,1:T(8,128)} %constant_dynamic-slice_fusion.9), channel_id=1, source_target_pairs={{0,8},{4,12},{8,0},{12,4},{16,24},{20,28},{24,16},{28,20},{1,9},{5... | collective-permute-start | bytes 786440 | tf_op jit(solution)/shard_map/ppermute | solution.py:98
  33.4 12.5 %collective-permute-start.5 = (f32[4,1,2,1,2,2,16,128]{7,6,5,4,3,2,0,1:T(8,128)}, f32[4,1,2,1,2,2,16,128]{7,6,5,4,3,2,0,1:T(8,128)}, u32[]{:S(2)}, u32[]{:S(2)}) collective-permute-start(f32[4,1,2,1,2,2,16,128]{7,6,5,4,3,2,0,1:T(8,128)} %constant_dynamic-slice_fusion.10), channel_id=1, source_target_pairs={{0,4},{4,0},{8,12},{12,8},{16,20},{20,16},{24,28},{28,24},{1,5},{5... | collective-permute-start | bytes 786440 | tf_op jit(solution)/shard_map/ppermute | solution.py:98
  34.8 12.2 %collective-permute-start.4 = (f32[4,1,1,2,2,2,16,128]{7,6,5,4,3,2,0,1:T(8,128)}, f32[4,1,1,2,2,2,16,128]{7,6,5,4,3,2,0,1:T(8,128)}, u32[]{:S(2)}, u32[]{:S(2)}) collective-permute-start(f32[4,1,1,2,2,2,16,128]{7,6,5,4,3,2,0,1:T(8,128)} %constant_dynamic-slice_fusion.11), channel_id=1, source_target_pairs={{0,2},{1,3},{2,0},{3,1},{4,6},{5,7},{6,4},{7,5},{8,10},{9,11},{10,... | collective-permute-start | bytes 786440 | tf_op jit(solution)/shard_map/ppermute | solution.py:98
  48.1 9.7 %collective-permute-start.10 = (f32[4,1,2,2,1,1,16,128]{7,6,5,4,3,2,0,1:T(8,128)S(1)}, f32[4,1,2,2,1,1,16,128]{7,6,5,4,3,2,0,1:T(8,128)S(1)}, u32[]{:S(2)}, u32[]{:S(2)}) collective-permute-start(f32[4,1,2,2,1,1,16,128]{7,6,5,4,3,2,0,1:T(8,128)S(1)} %constant_dynamic-slice_fusion.6), channel_id=1, source_target_pairs={{0,16},{4,20},{8,24},{12,28},{16,0},{20,4},{24,8},{28,12},{1,17},{... | collective-permute-start | bytes 393224 | tf_op jit(solution)/shard_map/ppermute | solution.py:98
  49.2 7.7 %collective-permute-start.9 = (f32[4,1,2,1,1,2,16,128]{7,6,5,4,3,2,0,1:T(8,128)S(1)}, f32[4,1,2,1,1,2,16,128]{7,6,5,4,3,2,0,1:T(8,128)S(1)}, u32[]{:S(2)}, u32[]{:S(2)}) collective-permute-start(f32[4,1,2,1,1,2,16,128]{7,6,5,4,3,2,0,1:T(8,128)S(1)} %constant_dynamic-slice_fusion.7), channel_id=1, source_target_pairs={{0,8},{4,12},{8,0},{12,4},{16,24},{20,28},{24,16},{28,20},{1,9},{5... | collective-permute-start | bytes 393224 | tf_op jit(solution)/shard_map/ppermute | solution.py:98
  51.9 5.2 %collective-permute-start.8 = (f32[4,1,1,1,2,2,16,128]{7,6,5,4,3,2,0,1:T(8,128)}, f32[4,1,1,1,2,2,16,128]{7,6,5,4,3,2,0,1:T(8,128)S(1)}, u32[]{:S(2)}, u32[]{:S(2)}) collective-permute-start(f32[4,1,1,1,2,2,16,128]{7,6,5,4,3,2,0,1:T(8,128)} %constant_dynamic-slice_fusion.8), channel_id=1, source_target_pairs={{0,4},{4,0},{8,12},{12,8},{16,20},{20,16},{24,28},{28,24},{1,5},{5... | collective-permute-start | bytes 393224 | tf_op jit(solution)/shard_map/ppermute | solution.py:98
  52.4 5.4 %collective-permute-start.7 = (bf16[6,4,136,128]{3,2,1,0:T(8,128)(2,1)S(1)}, bf16[6,4,136,128]{3,2,1,0:T(8,128)(2,1)}, u32[]{:S(2)}, u32[]{:S(2)}) collective-permute-start(bf16[6,4,136,128]{3,2,1,0:T(8,128)(2,1)S(1)} %pad_maximum_fusion.1), channel_id=1, source_target_pairs={{0,1},{1,0},{2,3},{3,2},{4,5},{5,4},{6,7},{7,6},{8,9},{9,8},{10,11... | collective-permute-start | bytes 2506760 | tf_op jit(solution)/shard_map/ppermute | solution.py:167
  59.3 4.6 %collective-permute-start.13 = (f32[4,1,1,2,1,1,16,128]{7,6,5,4,3,2,0,1:T(8,128)S(1)}, f32[4,1,1,2,1,1,16,128]{7,6,5,4,3,2,0,1:T(8,128)S(1)}, u32[]{:S(2)}, u32[]{:S(2)}) collective-permute-start(f32[4,1,1,2,1,1,16,128]{7,6,5,4,3,2,0,1:T(8,128)S(1)} %constant_dynamic-slice_fusion.3), channel_id=1, source_target_pairs={{0,2},{1,3},{2,0},{3,1},{4,6},{5,7},{6,4},{7,5},{8,10},{9,11},{10,... | collective-permute-start | bytes 196616 | tf_op jit(solution)/shard_map/ppermute | solution.py:98
  60.3 6.3 %collective-permute-start.12 = (f32[4,1,2,1,1,1,16,128]{7,6,5,4,3,2,0,1:T(8,128)S(1)}, f32[4,1,2,1,1,1,16,128]{7,6,5,4,3,2,0,1:T(8,128)S(1)}, u32[]{:S(2)}, u32[]{:S(2)}) collective-permute-start(f32[4,1,2,1,1,1,16,128]{7,6,5,4,3,2,0,1:T(8,128)S(1)} %constant_dynamic-slice_fusion.4), channel_id=1, source_target_pairs={{0,16},{4,20},{8,24},{12,28},{16,0},{20,4},{24,8},{28,12},{1,17},{... | collective-permute-start | bytes 196616 | tf_op jit(solution)/shard_map/ppermute | solution.py:98
  60.3 6.3 %collective-permute-start.11 = (f32[4,1,1,1,1,2,16,128]{7,6,5,4,3,2,0,1:T(8,128)S(1)}, f32[4,1,1,1,1,2,16,128]{7,6,5,4,3,2,0,1:T(8,128)S(1)}, u32[]{:S(2)}, u32[]{:S(2)}) collective-permute-start(f32[4,1,1,1,1,2,16,128]{7,6,5,4,3,2,0,1:T(8,128)S(1)} %constant_dynamic-slice_fusion.5), channel_id=1, source_target_pairs={{0,8},{4,12},{8,0},{12,4},{16,24},{20,28},{24,16},{28,20},{1,9},{5... | collective-permute-start | bytes 196616 | tf_op jit(solution)/shard_map/ppermute | solution.py:98
  63.9 11.3 %copy-start.21 = (pred[12]{0:T(512)(128)(4,1)S(1)}, pred[12]{0:T(512)(128)(4,1)}, u32[]{:S(2)}) copy-start(pred[12]{0:T(512)(128)(4,1)} %compare_and_fusion.2) | copy-start | bytes 40
  66.7 4.9 %collective-permute-start.14 = (f32[4,1,1,1,1,1,16,128]{7,6,5,4,3,2,0,1:T(8,128)S(1)}, f32[4,1,1,1,1,1,16,128]{7,6,5,4,3,2,0,1:T(8,128)S(1)}, u32[]{:S(2)}, u32[]{:S(2)}) collective-permute-start(f32[4,1,1,1,1,1,16,128]{7,6,5,4,3,2,0,1:T(8,128)S(1)} %constant_dynamic-slice_fusion.2), channel_id=1, source_target_pairs={{0,16},{4,20},{8,24},{12,28},{16,0},{20,4},{24,8},{28,12},{1,17},{... | collective-permute-start | bytes 98312 | tf_op jit(solution)/shard_map/ppermute | solution.py:98
  68.5 3.9 %collective-permute-start.15 = (f32[4,1,1,1,1,1,16,128]{7,6,5,4,3,2,0,1:T(8,128)S(1)}, f32[4,1,1,1,1,1,16,128]{7,6,5,4,3,2,0,1:T(8,128)S(1)}, u32[]{:S(2)}, u32[]{:S(2)}) collective-permute-start(f32[4,1,1,1,1,1,16,128]{7,6,5,4,3,2,0,1:T(8,128)S(1)} %constant_dynamic-slice_fusion.1), channel_id=1, source_target_pairs={{0,2},{1,3},{2,0},{3,1},{4,6},{5,7},{6,4},{7,5},{8,10},{9,11},{10,... | collective-permute-start | bytes 98312 | tf_op jit(solution)/shard_map/ppermute | solution.py:98
  69.6 3.9 %collective-permute-start.16 = (f32[4,1,1,1,1,1,16,128]{7,6,5,4,3,2,0,1:T(8,128)S(1)}, f32[4,1,1,1,1,1,16,128]{7,6,5,4,3,2,0,1:T(8,128)S(1)}, u32[]{:S(2)}, u32[]{:S(2)}) collective-permute-start(f32[4,1,1,1,1,1,16,128]{7,6,5,4,3,2,0,1:T(8,128)S(1)} %constant_dynamic-slice_fusion), channel_id=1, source_target_pairs={{0,4},{4,0},{8,12},{12,8},{16,20},{20,16},{24,28},{28,24},{1,5},{5... | collective-permute-start | bytes 98312 | tf_op jit(solution)/shard_map/ppermute | solution.py:98
  75.4 4.8 %collective-permute-start.17 = (bf16[4,1,1,1,1,1,16,128]{7,6,0,5,4,3,2,1:T(8,128)(2,1)S(1)}, bf16[4,1,1,1,1,1,16,128]{7,6,0,5,4,3,2,1:T(8,128)(2,1)S(1)}, u32[]{:S(2)}, u32[]{:S(2)}) collective-permute-start(bf16[4,1,1,1,1,1,16,128]{7,6,0,5,4,3,2,1:T(8,128)(2,1)S(1)} %get-tuple-element.54), channel_id=1, source_target_pairs={{0,16},{4,20},{8,24},{12,28},{16,0},{20,4},{24,8},{28,12},{1,17},{... | collective-permute-start | bytes 49160 | tf_op jit(solution)/shard_map/ppermute | solution.py:103
  76.6 5.1 %collective-permute-start.21 = (bf16[4,1,1,1,1,1,16,128]{7,6,0,5,4,3,2,1:T(8,128)(2,1)S(1)}, bf16[4,1,1,1,1,1,16,128]{7,6,0,5,4,3,2,1:T(8,128)(2,1)S(1)}, u32[]{:S(2)}, u32[]{:S(2)}) collective-permute-start(bf16[4,1,1,1,1,1,16,128]{7,6,0,5,4,3,2,1:T(8,128)(2,1)S(1)} %get-tuple-element.55), channel_id=1, source_target_pairs={{0,2},{1,3},{2,0},{3,1},{4,6},{5,7},{6,4},{7,5},{8,10},{9,11},{10,... | collective-permute-start | bytes 49160 | tf_op jit(solution)/shard_map/ppermute | solution.py:103
  77.5 5.0 %collective-permute-start.25 = (bf16[4,1,1,1,1,1,16,128]{7,6,0,5,4,3,2,1:T(8,128)(2,1)S(1)}, bf16[4,1,1,1,1,1,16,128]{7,6,0,5,4,3,2,1:T(8,128)(2,1)S(1)}, u32[]{:S(2)}, u32[]{:S(2)}) collective-permute-start(bf16[4,1,1,1,1,1,16,128]{7,6,0,5,4,3,2,1:T(8,128)(2,1)S(1)} %get-tuple-element.56), channel_id=1, source_target_pairs={{0,4},{4,0},{8,12},{12,8},{16,20},{20,16},{24,28},{28,24},{1,5},{5... | collective-permute-start | bytes 49160 | tf_op jit(solution)/shard_map/ppermute | solution.py:103
  80.2 4.0 %collective-permute-start.18 = (bf16[4,1,1,1,1,2,16,128]{7,6,0,5,4,3,2,1:T(8,128)(2,1)S(1)}, bf16[4,1,1,1,1,2,16,128]{7,6,0,5,4,3,2,1:T(8,128)(2,1)S(1)}, u32[]{:S(2)}, u32[]{:S(2)}) collective-permute-start(bf16[4,1,1,1,1,2,16,128]{7,6,0,5,4,3,2,1:T(8,128)(2,1)S(1)} %maximum_select_fusion.14), channel_id=1, source_target_pairs={{0,8},{4,12},{8,0},{12,4},{16,24},{20,28},{24,16},{28,20},{1,9},{5... | collective-permute-start | bytes 98312 | tf_op jit(solution)/shard_map/ppermute | solution.py:103
  81.7 5.6 %collective-permute-start.22 = (bf16[4,1,2,1,1,1,16,128]{7,6,0,5,4,3,2,1:T(8,128)(2,1)S(1)}, bf16[4,1,2,1,1,1,16,128]{7,6,0,5,4,3,2,1:T(8,128)(2,1)S(1)}, u32[]{:S(2)}, u32[]{:S(2)}) collective-permute-start(bf16[4,1,2,1,1,1,16,128]{7,6,0,5,4,3,2,1:T(8,128)(2,1)S(1)} %maximum_select_fusion.16), channel_id=1, source_target_pairs={{0,16},{4,20},{8,24},{12,28},{16,0},{20,4},{24,8},{28,12},{1,17},{... | collective-permute-start | bytes 98312 | tf_op jit(solution)/shard_map/ppermute | solution.py:103
  82.6 4.9 %collective-permute-start.26 = (bf16[4,1,1,2,1,1,16,128]{7,6,0,5,4,3,2,1:T(8,128)(2,1)S(1)}, bf16[4,1,1,2,1,1,16,128]{7,6,0,5,4,3,2,1:T(8,128)(2,1)S(1)}, u32[]{:S(2)}, u32[]{:S(2)}) collective-permute-start(bf16[4,1,1,2,1,1,16,128]{7,6,0,5,4,3,2,1:T(8,128)(2,1)S(1)} %maximum_select_fusion.18), channel_id=1, source_target_pairs={{0,2},{1,3},{2,0},{3,1},{4,6},{5,7},{6,4},{7,5},{8,10},{9,11},{10,... | collective-permute-start | bytes 98312 | tf_op jit(solution)/shard_map/ppermute | solution.py:103
  84.2 5.2 %collective-permute-start.19 = (bf16[4,1,1,1,2,2,16,128]{7,6,0,5,4,3,2,1:T(8,128)(2,1)S(1)}, bf16[4,1,1,1,2,2,16,128]{7,6,0,5,4,3,2,1:T(8,128)(2,1)S(1)}, u32[]{:S(2)}, u32[]{:S(2)}) collective-permute-start(bf16[4,1,1,1,2,2,16,128]{7,6,0,5,4,3,2,1:T(8,128)(2,1)S(1)} %maximum_select_fusion.9), channel_id=1, source_target_pairs={{0,4},{4,0},{8,12},{12,8},{16,20},{20,16},{24,28},{28,24},{1,5},{5... | collective-permute-start | bytes 196616 | tf_op jit(solution)/shard_map/ppermute | solution.py:103
  87.3 5.7 %collective-permute-start.23 = (bf16[4,1,2,1,1,2,16,128]{7,6,0,5,4,3,2,1:T(8,128)(2,1)S(1)}, bf16[4,1,2,1,1,2,16,128]{7,6,0,5,4,3,2,1:T(8,128)(2,1)S(1)}, u32[]{:S(2)}, u32[]{:S(2)}) collective-permute-start(bf16[4,1,2,1,1,2,16,128]{7,6,0,5,4,3,2,1:T(8,128)(2,1)S(1)} %maximum_select_fusion.11), channel_id=1, source_target_pairs={{0,8},{4,12},{8,0},{12,4},{16,24},{20,28},{24,16},{28,20},{1,9},{5... | collective-permute-start | bytes 196616 | tf_op jit(solution)/shard_map/ppermute | solution.py:103
  87.5 5.7 %collective-permute-start.27 = (bf16[4,1,2,2,1,1,16,128]{7,6,0,5,4,3,2,1:T(8,128)(2,1)S(1)}, bf16[4,1,2,2,1,1,16,128]{7,6,0,5,4,3,2,1:T(8,128)(2,1)S(1)}, u32[]{:S(2)}, u32[]{:S(2)}) collective-permute-start(bf16[4,1,2,2,1,1,16,128]{7,6,0,5,4,3,2,1:T(8,128)(2,1)S(1)} %fusion.36), channel_id=1, source_target_pairs={{0,16},{4,20},{8,24},{12,28},{16,0},{20,4},{24,8},{28,12},{1,17},{... | collective-permute-start | bytes 196616 | tf_op jit(solution)/shard_map/ppermute | solution.py:103
  89.4 5.4 %collective-permute-start.20 = (bf16[4,1,1,2,2,2,16,128]{7,6,0,5,4,3,2,1:T(8,128)(2,1)S(1)}, bf16[4,1,1,2,2,2,16,128]{7,6,0,5,4,3,2,1:T(8,128)(2,1)S(1)}, u32[]{:S(2)}, u32[]{:S(2)}) collective-permute-start(bf16[4,1,1,2,2,2,16,128]{7,6,0,5,4,3,2,1:T(8,128)(2,1)S(1)} %maximum_select_fusion.5), channel_id=1, source_target_pairs={{0,2},{1,3},{2,0},{3,1},{4,6},{5,7},{6,4},{7,5},{8,10},{9,11},{10,... | collective-permute-start | bytes 393224 | tf_op jit(solution)/shard_map/ppermute | solution.py:103
  93.1 5.0 %collective-permute-start.24 = (bf16[4,1,2,1,2,2,16,128]{7,6,0,5,4,3,2,1:T(8,128)(2,1)S(1)}, bf16[4,1,2,1,2,2,16,128]{7,6,0,5,4,3,2,1:T(8,128)(2,1)S(1)}, u32[]{:S(2)}, u32[]{:S(2)}) collective-permute-start(bf16[4,1,2,1,2,2,16,128]{7,6,0,5,4,3,2,1:T(8,128)(2,1)S(1)} %maximum_select_fusion.6), channel_id=1, source_target_pairs={{0,4},{4,0},{8,12},{12,8},{16,20},{20,16},{24,28},{28,24},{1,5},{5... | collective-permute-start | bytes 393224 | tf_op jit(solution)/shard_map/ppermute | solution.py:103
  93.2 5.0 %collective-permute-start.28 = (bf16[4,1,2,2,1,2,16,128]{7,6,0,5,4,3,2,1:T(8,128)(2,1)S(1)}, bf16[4,1,2,2,1,2,16,128]{7,6,0,5,4,3,2,1:T(8,128)(2,1)S(1)}, u32[]{:S(2)}, u32[]{:S(2)}) collective-permute-start(bf16[4,1,2,2,1,2,16,128]{7,6,0,5,4,3,2,1:T(8,128)(2,1)S(1)} %maximum_select_fusion.7), channel_id=1, source_target_pairs={{0,8},{4,12},{8,0},{12,4},{16,24},{20,28},{24,16},{28,20},{1,9},{5... | collective-permute-start | bytes 393224 | tf_op jit(solution)/shard_map/ppermute | solution.py:103
  98.4 2.4 %collective-permute-start.29 = (bf16[12,256,128]{2,1,0:T(8,128)(2,1)S(1)}, bf16[12,256,128]{2,1,0:T(8,128)(2,1)S(1)}, u32[]{:S(2)}, u32[]{:S(2)}) collective-permute-start(bf16[12,256,128]{2,1,0:T(8,128)(2,1)S(1)} %pad_maximum_fusion.2), channel_id=1, source_target_pairs={{0,1},{1,0},{2,3},{3,2},{4,5},{5,4},{6,7},{7,6},{8,9},{9,8},{10,11... | collective-permute-start | bytes 2359304 | tf_op jit(solution)/shard_map/ppermute | solution.py:187
  (23 other events, 97.2 us)

commit v25 on v22

--- a/solution.py
+++ b/solution.py
@@ -18,7 +18,7 @@
         out_ref[...] = jnp.zeros_like(out_ref)
 
     for q in range(pairs_per):
-        n = links[j * pairs_per + q]
+        n = links[q * pl.num_programs(0) + j]
 
         @pl.when(half[0] == upper)
         def _():
@@ -124,7 +124,7 @@
     total_blocks = own_rows * lax.axis_size("coarse")
     bits = device_bits()
     own_half = bit_of(*bits[0])
-    links = interface.reshape(-1)
+    links = jnp.concatenate([interface[:, q] for q in range(interface.shape[1])])
     half = own_half.reshape(1).astype(jnp.int32)
     send = restrict(residual, basis, links, total_blocks, half, 1)
 

time: 104 us -> 103 us (level)
    unnamed x53 -> x52, local copies, waits for them, and re-layouts: 4.71 us -> 3.86 us
where the time goes in v25:
time: 103 us
  starting transfers between devices  35.7 us (35%)
  waiting for transfers between devices  19.2 us (19%)
  local copies, waits for them, and re-layouts  17.3 us (17%)
  other arithmetic  10.5 us (10%)
  Pallas kernels  10.3 us (10%)
  matrix products  9.18 us (9%)
    ppermute x12, starting transfers between devices, halve(): lax.ppermute(send.astype(wire), axis, pairs(axis, mask)).astype(x.dtype)  14.6 us
    ppermute x12, starting transfers between devices, double(): recv = lax.ppermute(y, axis, pairs(axis, mask))  12.5 us
    pallas_call x2, Pallas kernels, restrict(): pl.pallas_call(functools.partial(restrict_kernel, upper=upper), out_shape...  10.3 us
    ppermute x12, waiting for transfers between devices, double(): recv = lax.ppermute(y, axis, pairs(axis, mask))  9.7 us
    ppermute x12, waiting for transfers between devices, halve(): lax.ppermute(send.astype(wire), axis, pairs(axis, mask)).astype(x.dtype)  7.05 us
    dot_general x1, matrix products, per_device(): jnp.einsum('jerb,jebc->jrc', picked, inverse_blocks[:split_at], preferred...  4.59 us
    ppermute x1, starting transfers between devices, per_device(): arriving = lax.ppermute(packed, exchanges[0][0], pairs(*exchanges[0]))  4.14 us
    unnamed x52, local copies, waits for them, and re-layouts  3.86 us
  transfers between devices with their start and end apart: 30, of which 15 were waited for; matrix products, arithmetic and copies ran while one was open for 24% of the time, Pallas kernels for 5%

profile of v25, /device:TPU:0, one launch (start us, length us, event | category | flops | bytes accessed | tf_op | source)
XLA Modules:
  0.0 102.9 jit_solution(992201534921375266)
XLA Ops:
  1.4 5.1 %shard_map.83 = f32[12,256,128]{2,1,0:T(8,128)} custom-call(s32[8]{0:T(128)} %pad_add_fusion.links, s32[1]{0:T(128)} %bitcast.2.half, bf16[4,512,256]{2,1,0:T(8,128)(2,1)} %residual_ref.3, bf16[4,2,256,128]{3,2,1,0:T(8,128)(2,1)} %basis_ref.3), custom_call_target="tpu_custom_call" | custom-call | flops 134217728 | bytes 3145728 | tf_op jit(solution)/shard_map/pallas_call | solution.py:36
  7.1 2.7 %collective-permute-start = (bf16[1,512,256]{2,1,0:T(8,128)(2,1)S(1)}, bf16[1,512,256]{2,1,0:T(8,128)(2,1)}, u32[]{:S(2)}, u32[]{:S(2)}) collective-permute-start(bf16[1,512,256]{2,1,0:T(8,128)(2,1)S(1)} %get-tuple-element.51), channel_id=1, source_target_pairs={{0,1},{1,2},{2,3},{3,4},{4,5},{5,6},{6,7},{7,8},{8,9},{9,10},{10,1... | collective-permute-start | bytes 786440 | tf_op jit(solution)/shard_map/ppermute | solution.py:65
  9.8 1.3 %collective-permute-start.1 = (bf16[1,512,256]{2,1,0:T(8,128)(2,1)S(1)}, bf16[1,512,256]{2,1,0:T(8,128)(2,1)}, u32[]{:S(2)}, u32[]{:S(2)}) collective-permute-start(bf16[1,512,256]{2,1,0:T(8,128)(2,1)S(1)} %get-tuple-element.52), channel_id=1, source_target_pairs={{1,0},{2,1},{3,2},{4,3},{5,4},{6,5},{7,6},{8,7},{9,8},{10,9},{11,1... | collective-permute-start | bytes 786440 | tf_op jit(solution)/shard_map/ppermute | solution.py:67
  12.0 4.1 %collective-permute-start.3 = (bf16[3,4,136,128]{3,2,1,0:T(8,128)(2,1)}, bf16[3,4,136,128]{3,2,1,0:T(8,128)(2,1)S(1)}, u32[]{:S(2)}, u32[]{:S(2)}) collective-permute-start(bf16[3,4,136,128]{3,2,1,0:T(8,128)(2,1)} %pad_maximum_fusion.3), channel_id=1, source_target_pairs={{0,2},{1,3},{2,0},{3,1},{4,6},{5,7},{6,4},{7,5},{8,10},{9,11},{10,... | collective-permute-start | bytes 1253384 | tf_op jit(solution)/shard_map/ppermute | solution.py:142
  18.7 5.2 %shard_map.82 = f32[12,256,128]{2,1,0:T(8,128)} custom-call(s32[8]{0:T(128)} %pad_add_fusion.links, s32[1]{0:T(128)} %bitcast.2.half, bf16[4,512,256]{2,1,0:T(8,128)(2,1)} %residual_ref.3, bf16[4,2,256,128]{3,2,1,0:T(8,128)(2,1)} %basis_ref.3), custom_call_target="tpu_custom_call" | custom-call | flops 134217728 | bytes 3145728 | tf_op jit(solution)/shard_map/pallas_call | solution.py:36
  24.5 1.2 %pad_maximum_fusion = bf16[6,512,256]{2,1,0:T(8,128)(2,1)S(1)} fusion(bf16[1,512,256]{2,1,0:T(8,128)(2,1)} %collective-permute-done.1, bf16[4,512,256]{2,1,0:T(8,128)(2,1)S(1)} %copy-done.2, bf16[1,512,256]{2,1,0:T(8,128)(2,1)} %collective-permute-done), kind=kLoop, calls=%fused_computation.14 | loop fusion | flops 1572864 | bytes 3145728 | tf_op jit(solution)/shard_map/concatenate | solution.py:63
  25.7 1.6 %add.237 = f32[12,256,128]{2,1,0:T(8,128)S(1)} add(f32[12,256,128]{2,1,0:T(8,128)S(1)} %copy-done.3, f32[12,256,128]{2,1,0:T(8,128)} %collective-permute-done.2) | non-fusion elementwise | flops 393216 | bytes 4718592 | tf_op jit(solution)/shard_map/add | solution.py:138
  30.2 2.4 %collective-permute-start.6 = (f32[4,1,2,2,1,2,16,128]{7,6,5,4,3,2,0,1:T(8,128)}, f32[4,1,2,2,1,2,16,128]{7,6,5,4,3,2,0,1:T(8,128)}, u32[]{:S(2)}, u32[]{:S(2)}) collective-permute-start(f32[4,1,2,2,1,2,16,128]{7,6,5,4,3,2,0,1:T(8,128)} %constant_dynamic-slice_fusion.9), channel_id=1, source_target_pairs={{0,8},{4,12},{8,0},{12,4},{16,24},{20,28},{24,16},{28,20},{1,9},{5... | collective-permute-start | bytes 786440 | tf_op jit(solution)/shard_map/ppermute | solution.py:98
  34.7 2.1 %collective-permute-start.4 = (f32[4,1,1,2,2,2,16,128]{7,6,5,4,3,2,0,1:T(8,128)}, f32[4,1,1,2,2,2,16,128]{7,6,5,4,3,2,0,1:T(8,128)}, u32[]{:S(2)}, u32[]{:S(2)}) collective-permute-start(f32[4,1,1,2,2,2,16,128]{7,6,5,4,3,2,0,1:T(8,128)} %constant_dynamic-slice_fusion.11), channel_id=1, source_target_pairs={{0,2},{1,3},{2,0},{3,1},{4,6},{5,7},{6,4},{7,5},{8,10},{9,11},{10,... | collective-permute-start | bytes 786440 | tf_op jit(solution)/shard_map/ppermute | solution.py:98
  36.8 2.5 %gather_fusion = bf16[12,512,256]{2,1,0:T(8,128)(2,1)} fusion(bf16[6,512,256]{2,1,0:T(8,128)(2,1)S(1)} %pad_maximum_fusion, s32[1024]{0:T(1024)S(1)} %pad_clamp_fusion.5), kind=kCustom, calls=%fused_computation.2 | custom fusion | bytes 6291504 | tf_op jit(solution)/shard_map/jit(_take)/gather | solution.py:149
  39.3 4.6 %fusion.8 = f32[3,512,256]{2,1,0:T(8,128)} fusion(bf16[4,4,256,256]{3,2,1,0:T(8,128)(2,1)} %param.12, bf16[3,4,512,256]{3,2,1,0:T(8,128)(2,1)} %bitcast.104, pred[3,4]{1,0:T(4,128)(4,1)S(1)} %compare_and_fusion.3), kind=kOutput, calls=%fused_computation.17 | convolution fusion | flops 806879232 | bytes 6291468 | tf_op jit(solution)/shard_map/jerb,jebc->jrc/dot_general | solution.py:150
  49.2 2.0 %collective-permute-start.8 = (f32[4,1,2,1,1,2,16,128]{7,6,5,4,3,2,0,1:T(8,128)S(1)}, f32[4,1,2,1,1,2,16,128]{7,6,5,4,3,2,0,1:T(8,128)S(1)}, u32[]{:S(2)}, u32[]{:S(2)}) collective-permute-start(f32[4,1,2,1,1,2,16,128]{7,6,5,4,3,2,0,1:T(8,128)S(1)} %constant_dynamic-slice_fusion.7), channel_id=1, source_target_pairs={{0,8},{4,12},{8,0},{12,4},{16,24},{20,28},{24,16},{28,20},{1,9},{5... | collective-permute-start | bytes 393224 | tf_op jit(solution)/shard_map/ppermute | solution.py:98
  52.4 1.7 %gather_fusion.1 = bf16[4,512,256]{2,1,0:T(8,128)(2,1)} fusion(bf16[6,512,256]{2,1,0:T(8,128)(2,1)S(1)} %pad_maximum_fusion, s32[1024]{0:T(1024)} %pad_clamp_fusion.4), kind=kCustom, calls=%fused_computation.3 | custom fusion | bytes 2097168 | tf_op jit(solution)/shard_map/jit(_take)/gather | solution.py:155
  54.1 2.7 %convolution_bitcast_fusion = f32[1,512,256]{2,1,0:T(8,128)} fusion(bf16[4,512,256]{2,1,0:T(8,128)(2,1)} %gather_fusion.1, pred[4]{0:T(512)(128)(4,1)S(1)} %copy-done.22, bf16[4,4,256,256]{3,2,1,0:T(8,128)(2,1)} %param.12), kind=kOutput, calls=%fused_computation.18 | convolution fusion | flops 268959744 | bytes 2097156 | tf_op jit(solution)/shard_map/jerb,jebc->jrc/dot_general | solution.py:156
  57.8 1.3 %constant_dynamic-update-slice_fusion = bf16[12,4,136,128]{3,2,1,0:T(8,128)(2,1)S(1)} fusion(bf16[12,4,136,128]{3,2,1,0:T(8,128)(2,1)S(1)} %constant_dynamic-update-slice_fusion.1, bf16[6,4,136,128]{3,2,1,0:T(8,128)(2,1)} %collective-permute-done.10), kind=kLoop, calls=%fused_computation.107 | loop fusion | bytes 1671168 | tf_op jit(solution)/shard_map/concatenate | solution.py:162
  59.3 1.6 %collective-permute-start.11 = (f32[4,1,1,1,1,2,16,128]{7,6,5,4,3,2,0,1:T(8,128)S(1)}, f32[4,1,1,1,1,2,16,128]{7,6,5,4,3,2,0,1:T(8,128)S(1)}, u32[]{:S(2)}, u32[]{:S(2)}) collective-permute-start(f32[4,1,1,1,1,2,16,128]{7,6,5,4,3,2,0,1:T(8,128)S(1)} %constant_dynamic-slice_fusion.5), channel_id=1, source_target_pairs={{0,8},{4,12},{8,0},{12,4},{16,24},{20,28},{24,16},{28,20},{1,9},{5... | collective-permute-start | bytes 196616 | tf_op jit(solution)/shard_map/ppermute | solution.py:98
  62.4 1.4 %collective-permute-done.11 = f32[4,1,1,1,1,2,16,128]{7,6,5,4,3,2,0,1:T(8,128)S(1)} collective-permute-done((f32[4,1,1,1,1,2,16,128]{7,6,5,4,3,2,0,1:T(8,128)S(1)}, f32[4,1,1,1,1,2,16,128]{7,6,5,4,3,2,0,1:T(8,128)S(1)}, u32[]{:S(2)}, u32[]{:S(2)}) %collective-permute-start.11) | collective-permute-done | bytes 65568 | tf_op jit(solution)/shard_map/ppermute | solution.py:98
  63.9 1.3 %collective-permute-start.12 = (f32[4,1,1,1,1,1,16,128]{7,6,5,4,3,2,0,1:T(8,128)S(1)}, f32[4,1,1,1,1,1,16,128]{7,6,5,4,3,2,0,1:T(8,128)S(1)}, u32[]{:S(2)}, u32[]{:S(2)}) collective-permute-start(f32[4,1,1,1,1,1,16,128]{7,6,5,4,3,2,0,1:T(8,128)S(1)} %constant_dynamic-slice_fusion.4), channel_id=1, source_target_pairs={{0,16},{4,20},{8,24},{12,28},{16,0},{20,4},{24,8},{28,12},{1,17},{... | collective-permute-start | bytes 98312 | tf_op jit(solution)/shard_map/ppermute | solution.py:98
  65.1 2.2 %collective-permute-done.13 = f32[4,1,2,1,1,1,16,128]{7,6,5,4,3,2,0,1:T(8,128)S(1)} collective-permute-done((f32[4,1,2,1,1,1,16,128]{7,6,5,4,3,2,0,1:T(8,128)S(1)}, f32[4,1,2,1,1,1,16,128]{7,6,5,4,3,2,0,1:T(8,128)S(1)}, u32[]{:S(2)}, u32[]{:S(2)}) %collective-permute-start.13) | collective-permute-done | bytes 65568 | tf_op jit(solution)/shard_map/ppermute | solution.py:98
  69.2 2.2 %collective-permute-done.14 = f32[4,1,1,1,1,1,16,128]{7,6,5,4,3,2,0,1:T(8,128)S(1)} collective-permute-done((f32[4,1,1,1,1,1,16,128]{7,6,5,4,3,2,0,1:T(8,128)S(1)}, f32[4,1,1,1,1,1,16,128]{7,6,5,4,3,2,0,1:T(8,128)S(1)}, u32[]{:S(2)}, u32[]{:S(2)}) %collective-permute-start.14) | collective-permute-done | bytes 32800 | tf_op jit(solution)/shard_map/ppermute | solution.py:98
  75.8 1.9 %collective-permute-start.25 = (bf16[4,1,1,1,1,1,16,128]{7,6,0,5,4,3,2,1:T(8,128)(2,1)S(1)}, bf16[4,1,1,1,1,1,16,128]{7,6,0,5,4,3,2,1:T(8,128)(2,1)S(1)}, u32[]{:S(2)}, u32[]{:S(2)}) collective-permute-start(bf16[4,1,1,1,1,1,16,128]{7,6,0,5,4,3,2,1:T(8,128)(2,1)S(1)} %get-tuple-element.56), channel_id=1, source_target_pairs={{0,4},{4,0},{8,12},{12,8},{16,20},{20,16},{24,28},{28,24},{1,5},{5... | collective-permute-start | bytes 49160 | tf_op jit(solution)/shard_map/ppermute | solution.py:103
  77.6 1.3 %collective-permute-done.17 = bf16[4,1,1,1,1,1,16,128]{7,6,0,5,4,3,2,1:T(8,128)(2,1)S(1)} collective-permute-done((bf16[4,1,1,1,1,1,16,128]{7,6,0,5,4,3,2,1:T(8,128)(2,1)S(1)}, bf16[4,1,1,1,1,1,16,128]{7,6,0,5,4,3,2,1:T(8,128)(2,1)S(1)}, u32[]{:S(2)}, u32[]{:S(2)}) %collective-permute-start.17) | collective-permute-done | bytes 16416 | tf_op jit(solution)/shard_map/ppermute | solution.py:103
  79.0 2.0 %collective-permute-start.22 = (bf16[4,1,2,1,1,1,16,128]{7,6,0,5,4,3,2,1:T(8,128)(2,1)S(1)}, bf16[4,1,2,1,1,1,16,128]{7,6,0,5,4,3,2,1:T(8,128)(2,1)S(1)}, u32[]{:S(2)}, u32[]{:S(2)}) collective-permute-start(bf16[4,1,2,1,1,1,16,128]{7,6,0,5,4,3,2,1:T(8,128)(2,1)S(1)} %maximum_select_fusion.16), channel_id=1, source_target_pairs={{0,16},{4,20},{8,24},{12,28},{16,0},{20,4},{24,8},{28,12},{1,17},{... | collective-permute-start | bytes 98312 | tf_op jit(solution)/shard_map/ppermute | solution.py:103
  81.0 1.2 %collective-permute-start.26 = (bf16[4,1,1,2,1,1,16,128]{7,6,0,5,4,3,2,1:T(8,128)(2,1)S(1)}, bf16[4,1,1,2,1,1,16,128]{7,6,0,5,4,3,2,1:T(8,128)(2,1)S(1)}, u32[]{:S(2)}, u32[]{:S(2)}) collective-permute-start(bf16[4,1,1,2,1,1,16,128]{7,6,0,5,4,3,2,1:T(8,128)(2,1)S(1)} %maximum_select_fusion.18), channel_id=1, source_target_pairs={{0,2},{1,3},{2,0},{3,1},{4,6},{5,7},{6,4},{7,5},{8,10},{9,11},{10,... | collective-permute-start | bytes 98312 | tf_op jit(solution)/shard_map/ppermute | solution.py:103
  84.1 2.0 %collective-permute-start.23 = (bf16[4,1,2,1,1,2,16,128]{7,6,0,5,4,3,2,1:T(8,128)(2,1)S(1)}, bf16[4,1,2,1,1,2,16,128]{7,6,0,5,4,3,2,1:T(8,128)(2,1)S(1)}, u32[]{:S(2)}, u32[]{:S(2)}) collective-permute-start(bf16[4,1,2,1,1,2,16,128]{7,6,0,5,4,3,2,1:T(8,128)(2,1)S(1)} %maximum_select_fusion.11), channel_id=1, source_target_pairs={{0,8},{4,12},{8,0},{12,4},{16,24},{20,28},{24,16},{28,20},{1,9},{5... | collective-permute-start | bytes 196616 | tf_op jit(solution)/shard_map/ppermute | solution.py:103
  86.5 1.3 %collective-permute-done.19 = bf16[4,1,1,1,2,2,16,128]{7,6,0,5,4,3,2,1:T(8,128)(2,1)S(1)} collective-permute-done((bf16[4,1,1,1,2,2,16,128]{7,6,0,5,4,3,2,1:T(8,128)(2,1)S(1)}, bf16[4,1,1,1,2,2,16,128]{7,6,0,5,4,3,2,1:T(8,128)(2,1)S(1)}, u32[]{:S(2)}, u32[]{:S(2)}) %collective-permute-start.19) | collective-permute-done | bytes 65568 | tf_op jit(solution)/shard_map/ppermute | solution.py:103
  89.0 1.2 %collective-permute-start.24 = (bf16[4,1,2,1,2,2,16,128]{7,6,0,5,4,3,2,1:T(8,128)(2,1)S(1)}, bf16[4,1,2,1,2,2,16,128]{7,6,0,5,4,3,2,1:T(8,128)(2,1)S(1)}, u32[]{:S(2)}, u32[]{:S(2)}) collective-permute-start(bf16[4,1,2,1,2,2,16,128]{7,6,0,5,4,3,2,1:T(8,128)(2,1)S(1)} %maximum_select_fusion.6), channel_id=1, source_target_pairs={{0,4},{4,0},{8,12},{12,8},{16,20},{20,16},{24,28},{28,24},{1,5},{5... | collective-permute-start | bytes 393224 | tf_op jit(solution)/shard_map/ppermute | solution.py:103
  90.2 1.5 %collective-permute-done.27 = bf16[4,1,2,2,1,1,16,128]{7,6,0,5,4,3,2,1:T(8,128)(2,1)S(1)} collective-permute-done((bf16[4,1,2,2,1,1,16,128]{7,6,0,5,4,3,2,1:T(8,128)(2,1)S(1)}, bf16[4,1,2,2,1,1,16,128]{7,6,0,5,4,3,2,1:T(8,128)(2,1)S(1)}, u32[]{:S(2)}, u32[]{:S(2)}) %collective-permute-start.27) | collective-permute-done | bytes 65568 | tf_op jit(solution)/shard_map/ppermute | solution.py:103
  94.1 2.7 %collective-permute-done.28 = bf16[4,1,2,2,1,2,16,128]{7,6,0,5,4,3,2,1:T(8,128)(2,1)S(1)} collective-permute-done((bf16[4,1,2,2,1,2,16,128]{7,6,0,5,4,3,2,1:T(8,128)(2,1)S(1)}, bf16[4,1,2,2,1,2,16,128]{7,6,0,5,4,3,2,1:T(8,128)(2,1)S(1)}, u32[]{:S(2)}, u32[]{:S(2)}) %collective-permute-start.28) | collective-permute-done | bytes 131104 | tf_op jit(solution)/shard_map/ppermute | solution.py:103
  98.0 1.3 %collective-permute-done.29 = bf16[12,256,128]{2,1,0:T(8,128)(2,1)S(1)} collective-permute-done((bf16[12,256,128]{2,1,0:T(8,128)(2,1)S(1)}, bf16[12,256,128]{2,1,0:T(8,128)(2,1)S(1)}, u32[]{:S(2)}, u32[]{:S(2)}) %collective-permute-start.29) | collective-permute-done | bytes 786464 | tf_op jit(solution)/shard_map/ppermute | solution.py:187
  100.2 1.2 %copy-done.24 = f32[3,512,256]{2,1,0:T(8,128)S(1)} copy-done((f32[3,512,256]{2,1,0:T(8,128)S(1)}, f32[3,512,256]{2,1,0:T(8,128)}, u32[]{:S(2)}) %copy-start.24) | copy-done | bytes 1572888
  101.4 1.5 %fusion.3 = bf16[4,512,256]{2,1,0:T(8,128)(2,1)} fusion(f32[1,512,256]{2,1,0:T(8,128)S(1)} %copy-done.23, f32[3,512,256]{2,1,0:T(8,128)S(1)} %copy-done.24, bf16[4,2,256,128]{3,2,1,0:T(8,128)(2,1)S(1)} %copy-done.8, bf16[4,2,256,128]{3,2,1,0:T(8,128)(2,1)S(1)} %get-tuple-element.70, bf16[4,2,256,128]{3,2,1,0:T(8,128)(2,1)S(1)} %get-tuple-element.69, ...), kind=kOutput, calls=%fused_computation.11 | convolution fusion | flops 274726912 | bytes 4718593 | tf_op jit(solution)/shard_map/jqrc,jqbc->jrb/dot_general | solution.py:196
  (179 shorter events, 33.9 us)
Async XLA Ops:
  1.4 9.7 %copy-start.9 = (bf16[3,4,128,128]{3,2,1,0:T(8,128)(2,1)S(1)}, bf16[3,4,128,128]{3,2,1,0:T(8,128)(2,1)}, u32[]{:S(2)}) copy-start(bf16[3,4,128,128]{3,2,1,0:T(8,128)(2,1)} %param.16) | copy-start | bytes 1179652
  6.6 19.1 %collective-permute-start.2 = (f32[12,256,128]{2,1,0:T(8,128)}, f32[12,256,128]{2,1,0:T(8,128)}, u32[]{:S(2)}, u32[]{:S(2)}) collective-permute-start(f32[12,256,128]{2,1,0:T(8,128)} %shard_map.83), channel_id=1, source_target_pairs={{0,1},{1,0},{2,3},{3,2},{4,5},{5,4},{6,7},{7,6},{8,9},{9,8},{10,11... | collective-permute-start | bytes 4718600 | tf_op jit(solution)/shard_map/ppermute | solution.py:137
  7.1 17.4 %collective-permute-start = (bf16[1,512,256]{2,1,0:T(8,128)(2,1)S(1)}, bf16[1,512,256]{2,1,0:T(8,128)(2,1)}, u32[]{:S(2)}, u32[]{:S(2)}) collective-permute-start(bf16[1,512,256]{2,1,0:T(8,128)(2,1)S(1)} %get-tuple-element.51), channel_id=1, source_target_pairs={{0,1},{1,2},{2,3},{3,4},{4,5},{5,6},{6,7},{7,8},{8,9},{9,10},{10,1... | collective-permute-start | bytes 786440 | tf_op jit(solution)/shard_map/ppermute | solution.py:65
  9.8 14.7 %collective-permute-start.1 = (bf16[1,512,256]{2,1,0:T(8,128)(2,1)S(1)}, bf16[1,512,256]{2,1,0:T(8,128)(2,1)}, u32[]{:S(2)}, u32[]{:S(2)}) collective-permute-start(bf16[1,512,256]{2,1,0:T(8,128)(2,1)S(1)} %get-tuple-element.52), channel_id=1, source_target_pairs={{1,0},{2,1},{3,2},{4,3},{5,4},{6,5},{7,6},{8,7},{9,8},{10,9},{11,1... | collective-permute-start | bytes 786440 | tf_op jit(solution)/shard_map/ppermute | solution.py:67
  12.0 16.5 %collective-permute-start.3 = (bf16[3,4,136,128]{3,2,1,0:T(8,128)(2,1)}, bf16[3,4,136,128]{3,2,1,0:T(8,128)(2,1)S(1)}, u32[]{:S(2)}, u32[]{:S(2)}) collective-permute-start(bf16[3,4,136,128]{3,2,1,0:T(8,128)(2,1)} %pad_maximum_fusion.3), channel_id=1, source_target_pairs={{0,2},{1,3},{2,0},{3,1},{4,6},{5,7},{6,4},{7,5},{8,10},{9,11},{10,... | collective-permute-start | bytes 1253384 | tf_op jit(solution)/shard_map/ppermute | solution.py:142
  30.2 13.7 %collective-permute-start.6 = (f32[4,1,2,2,1,2,16,128]{7,6,5,4,3,2,0,1:T(8,128)}, f32[4,1,2,2,1,2,16,128]{7,6,5,4,3,2,0,1:T(8,128)}, u32[]{:S(2)}, u32[]{:S(2)}) collective-permute-start(f32[4,1,2,2,1,2,16,128]{7,6,5,4,3,2,0,1:T(8,128)} %constant_dynamic-slice_fusion.9), channel_id=1, source_target_pairs={{0,8},{4,12},{8,0},{12,4},{16,24},{20,28},{24,16},{28,20},{1,9},{5... | collective-permute-start | bytes 786440 | tf_op jit(solution)/shard_map/ppermute | solution.py:98
  33.4 12.5 %collective-permute-start.5 = (f32[4,1,2,1,2,2,16,128]{7,6,5,4,3,2,0,1:T(8,128)}, f32[4,1,2,1,2,2,16,128]{7,6,5,4,3,2,0,1:T(8,128)}, u32[]{:S(2)}, u32[]{:S(2)}) collective-permute-start(f32[4,1,2,1,2,2,16,128]{7,6,5,4,3,2,0,1:T(8,128)} %constant_dynamic-slice_fusion.10), channel_id=1, source_target_pairs={{0,4},{4,0},{8,12},{12,8},{16,20},{20,16},{24,28},{28,24},{1,5},{5... | collective-permute-start | bytes 786440 | tf_op jit(solution)/shard_map/ppermute | solution.py:98
  34.7 12.2 %collective-permute-start.4 = (f32[4,1,1,2,2,2,16,128]{7,6,5,4,3,2,0,1:T(8,128)}, f32[4,1,1,2,2,2,16,128]{7,6,5,4,3,2,0,1:T(8,128)}, u32[]{:S(2)}, u32[]{:S(2)}) collective-permute-start(f32[4,1,1,2,2,2,16,128]{7,6,5,4,3,2,0,1:T(8,128)} %constant_dynamic-slice_fusion.11), channel_id=1, source_target_pairs={{0,2},{1,3},{2,0},{3,1},{4,6},{5,7},{6,4},{7,5},{8,10},{9,11},{10,... | collective-permute-start | bytes 786440 | tf_op jit(solution)/shard_map/ppermute | solution.py:98
  48.0 9.7 %collective-permute-start.9 = (f32[4,1,2,2,1,1,16,128]{7,6,5,4,3,2,0,1:T(8,128)S(1)}, f32[4,1,2,2,1,1,16,128]{7,6,5,4,3,2,0,1:T(8,128)S(1)}, u32[]{:S(2)}, u32[]{:S(2)}) collective-permute-start(f32[4,1,2,2,1,1,16,128]{7,6,5,4,3,2,0,1:T(8,128)S(1)} %constant_dynamic-slice_fusion.6), channel_id=1, source_target_pairs={{0,16},{4,20},{8,24},{12,28},{16,0},{20,4},{24,8},{28,12},{1,17},{... | collective-permute-start | bytes 393224 | tf_op jit(solution)/shard_map/ppermute | solution.py:98
  49.2 7.6 %collective-permute-start.8 = (f32[4,1,2,1,1,2,16,128]{7,6,5,4,3,2,0,1:T(8,128)S(1)}, f32[4,1,2,1,1,2,16,128]{7,6,5,4,3,2,0,1:T(8,128)S(1)}, u32[]{:S(2)}, u32[]{:S(2)}) collective-permute-start(f32[4,1,2,1,1,2,16,128]{7,6,5,4,3,2,0,1:T(8,128)S(1)} %constant_dynamic-slice_fusion.7), channel_id=1, source_target_pairs={{0,8},{4,12},{8,0},{12,4},{16,24},{20,28},{24,16},{28,20},{1,9},{5... | collective-permute-start | bytes 393224 | tf_op jit(solution)/shard_map/ppermute | solution.py:98
  51.9 5.2 %collective-permute-start.7 = (f32[4,1,1,1,2,2,16,128]{7,6,5,4,3,2,0,1:T(8,128)}, f32[4,1,1,1,2,2,16,128]{7,6,5,4,3,2,0,1:T(8,128)S(1)}, u32[]{:S(2)}, u32[]{:S(2)}) collective-permute-start(f32[4,1,1,1,2,2,16,128]{7,6,5,4,3,2,0,1:T(8,128)} %constant_dynamic-slice_fusion.8), channel_id=1, source_target_pairs={{0,4},{4,0},{8,12},{12,8},{16,20},{20,16},{24,28},{28,24},{1,5},{5... | collective-permute-start | bytes 393224 | tf_op jit(solution)/shard_map/ppermute | solution.py:98
  52.4 5.4 %collective-permute-start.10 = (bf16[6,4,136,128]{3,2,1,0:T(8,128)(2,1)S(1)}, bf16[6,4,136,128]{3,2,1,0:T(8,128)(2,1)}, u32[]{:S(2)}, u32[]{:S(2)}) collective-permute-start(bf16[6,4,136,128]{3,2,1,0:T(8,128)(2,1)S(1)} %pad_maximum_fusion.1), channel_id=1, source_target_pairs={{0,1},{1,0},{2,3},{3,2},{4,5},{5,4},{6,7},{7,6},{8,9},{9,8},{10,11... | collective-permute-start | bytes 2506760 | tf_op jit(solution)/shard_map/ppermute | solution.py:167
  59.3 4.6 %collective-permute-start.11 = (f32[4,1,1,1,1,2,16,128]{7,6,5,4,3,2,0,1:T(8,128)S(1)}, f32[4,1,1,1,1,2,16,128]{7,6,5,4,3,2,0,1:T(8,128)S(1)}, u32[]{:S(2)}, u32[]{:S(2)}) collective-permute-start(f32[4,1,1,1,1,2,16,128]{7,6,5,4,3,2,0,1:T(8,128)S(1)} %constant_dynamic-slice_fusion.5), channel_id=1, source_target_pairs={{0,8},{4,12},{8,0},{12,4},{16,24},{20,28},{24,16},{28,20},{1,9},{5... | collective-permute-start | bytes 196616 | tf_op jit(solution)/shard_map/ppermute | solution.py:98
  60.9 6.5 %collective-permute-start.13 = (f32[4,1,2,1,1,1,16,128]{7,6,5,4,3,2,0,1:T(8,128)S(1)}, f32[4,1,2,1,1,1,16,128]{7,6,5,4,3,2,0,1:T(8,128)S(1)}, u32[]{:S(2)}, u32[]{:S(2)}) collective-permute-start(f32[4,1,2,1,1,1,16,128]{7,6,5,4,3,2,0,1:T(8,128)S(1)} %constant_dynamic-slice_fusion.3), channel_id=1, source_target_pairs={{0,16},{4,20},{8,24},{12,28},{16,0},{20,4},{24,8},{28,12},{1,17},{... | collective-permute-start | bytes 196616 | tf_op jit(solution)/shard_map/ppermute | solution.py:98
  61.2 7.1 %collective-permute-start.15 = (f32[4,1,1,2,1,1,16,128]{7,6,5,4,3,2,0,1:T(8,128)S(1)}, f32[4,1,1,2,1,1,16,128]{7,6,5,4,3,2,0,1:T(8,128)S(1)}, u32[]{:S(2)}, u32[]{:S(2)}) collective-permute-start(f32[4,1,1,2,1,1,16,128]{7,6,5,4,3,2,0,1:T(8,128)S(1)} %constant_dynamic-slice_fusion.1), channel_id=1, source_target_pairs={{0,2},{1,3},{2,0},{3,1},{4,6},{5,7},{6,4},{7,5},{8,10},{9,11},{10,... | collective-permute-start | bytes 196616 | tf_op jit(solution)/shard_map/ppermute | solution.py:98
  63.9 10.3 %copy-start.21 = (pred[12]{0:T(512)(128)(4,1)S(1)}, pred[12]{0:T(512)(128)(4,1)}, u32[]{:S(2)}) copy-start(pred[12]{0:T(512)(128)(4,1)} %compare_and_fusion.2) | copy-start | bytes 40
  63.9 5.3 %collective-permute-start.12 = (f32[4,1,1,1,1,1,16,128]{7,6,5,4,3,2,0,1:T(8,128)S(1)}, f32[4,1,1,1,1,1,16,128]{7,6,5,4,3,2,0,1:T(8,128)S(1)}, u32[]{:S(2)}, u32[]{:S(2)}) collective-permute-start(f32[4,1,1,1,1,1,16,128]{7,6,5,4,3,2,0,1:T(8,128)S(1)} %constant_dynamic-slice_fusion.4), channel_id=1, source_target_pairs={{0,16},{4,20},{8,24},{12,28},{16,0},{20,4},{24,8},{28,12},{1,17},{... | collective-permute-start | bytes 98312 | tf_op jit(solution)/shard_map/ppermute | solution.py:98
  67.4 4.0 %collective-permute-start.14 = (f32[4,1,1,1,1,1,16,128]{7,6,5,4,3,2,0,1:T(8,128)S(1)}, f32[4,1,1,1,1,1,16,128]{7,6,5,4,3,2,0,1:T(8,128)S(1)}, u32[]{:S(2)}, u32[]{:S(2)}) collective-permute-start(f32[4,1,1,1,1,1,16,128]{7,6,5,4,3,2,0,1:T(8,128)S(1)} %constant_dynamic-slice_fusion.2), channel_id=1, source_target_pairs={{0,2},{1,3},{2,0},{3,1},{4,6},{5,7},{6,4},{7,5},{8,10},{9,11},{10,... | collective-permute-start | bytes 98312 | tf_op jit(solution)/shard_map/ppermute | solution.py:98
  68.4 4.0 %collective-permute-start.16 = (f32[4,1,1,1,1,1,16,128]{7,6,5,4,3,2,0,1:T(8,128)S(1)}, f32[4,1,1,1,1,1,16,128]{7,6,5,4,3,2,0,1:T(8,128)S(1)}, u32[]{:S(2)}, u32[]{:S(2)}) collective-permute-start(f32[4,1,1,1,1,1,16,128]{7,6,5,4,3,2,0,1:T(8,128)S(1)} %constant_dynamic-slice_fusion), channel_id=1, source_target_pairs={{0,4},{4,0},{8,12},{12,8},{16,20},{20,16},{24,28},{28,24},{1,5},{5... | collective-permute-start | bytes 98312 | tf_op jit(solution)/shard_map/ppermute | solution.py:98
  74.2 4.7 %collective-permute-start.17 = (bf16[4,1,1,1,1,1,16,128]{7,6,0,5,4,3,2,1:T(8,128)(2,1)S(1)}, bf16[4,1,1,1,1,1,16,128]{7,6,0,5,4,3,2,1:T(8,128)(2,1)S(1)}, u32[]{:S(2)}, u32[]{:S(2)}) collective-permute-start(bf16[4,1,1,1,1,1,16,128]{7,6,0,5,4,3,2,1:T(8,128)(2,1)S(1)} %get-tuple-element.54), channel_id=1, source_target_pairs={{0,16},{4,20},{8,24},{12,28},{16,0},{20,4},{24,8},{28,12},{1,17},{... | collective-permute-start | bytes 49160 | tf_op jit(solution)/shard_map/ppermute | solution.py:103
  74.6 4.4 %collective-permute-start.21 = (bf16[4,1,1,1,1,1,16,128]{7,6,0,5,4,3,2,1:T(8,128)(2,1)S(1)}, bf16[4,1,1,1,1,1,16,128]{7,6,0,5,4,3,2,1:T(8,128)(2,1)S(1)}, u32[]{:S(2)}, u32[]{:S(2)}) collective-permute-start(bf16[4,1,1,1,1,1,16,128]{7,6,0,5,4,3,2,1:T(8,128)(2,1)S(1)} %get-tuple-element.55), channel_id=1, source_target_pairs={{0,2},{1,3},{2,0},{3,1},{4,6},{5,7},{6,4},{7,5},{8,10},{9,11},{10,... | collective-permute-start | bytes 49160 | tf_op jit(solution)/shard_map/ppermute | solution.py:103
  75.8 5.3 %collective-permute-start.25 = (bf16[4,1,1,1,1,1,16,128]{7,6,0,5,4,3,2,1:T(8,128)(2,1)S(1)}, bf16[4,1,1,1,1,1,16,128]{7,6,0,5,4,3,2,1:T(8,128)(2,1)S(1)}, u32[]{:S(2)}, u32[]{:S(2)}) collective-permute-start(bf16[4,1,1,1,1,1,16,128]{7,6,0,5,4,3,2,1:T(8,128)(2,1)S(1)} %get-tuple-element.56), channel_id=1, source_target_pairs={{0,4},{4,0},{8,12},{12,8},{16,20},{20,16},{24,28},{28,24},{1,5},{5... | collective-permute-start | bytes 49160 | tf_op jit(solution)/shard_map/ppermute | solution.py:103
  78.9 4.0 %collective-permute-start.18 = (bf16[4,1,1,1,1,2,16,128]{7,6,0,5,4,3,2,1:T(8,128)(2,1)S(1)}, bf16[4,1,1,1,1,2,16,128]{7,6,0,5,4,3,2,1:T(8,128)(2,1)S(1)}, u32[]{:S(2)}, u32[]{:S(2)}) collective-permute-start(bf16[4,1,1,1,1,2,16,128]{7,6,0,5,4,3,2,1:T(8,128)(2,1)S(1)} %maximum_select_fusion.14), channel_id=1, source_target_pairs={{0,8},{4,12},{8,0},{12,4},{16,24},{20,28},{24,16},{28,20},{1,9},{5... | collective-permute-start | bytes 98312 | tf_op jit(solution)/shard_map/ppermute | solution.py:103
  79.0 5.0 %collective-permute-start.22 = (bf16[4,1,2,1,1,1,16,128]{7,6,0,5,4,3,2,1:T(8,128)(2,1)S(1)}, bf16[4,1,2,1,1,1,16,128]{7,6,0,5,4,3,2,1:T(8,128)(2,1)S(1)}, u32[]{:S(2)}, u32[]{:S(2)}) collective-permute-start(bf16[4,1,2,1,1,1,16,128]{7,6,0,5,4,3,2,1:T(8,128)(2,1)S(1)} %maximum_select_fusion.16), channel_id=1, source_target_pairs={{0,16},{4,20},{8,24},{12,28},{16,0},{20,4},{24,8},{28,12},{1,17},{... | collective-permute-start | bytes 98312 | tf_op jit(solution)/shard_map/ppermute | solution.py:103
  81.0 5.0 %collective-permute-start.26 = (bf16[4,1,1,2,1,1,16,128]{7,6,0,5,4,3,2,1:T(8,128)(2,1)S(1)}, bf16[4,1,1,2,1,1,16,128]{7,6,0,5,4,3,2,1:T(8,128)(2,1)S(1)}, u32[]{:S(2)}, u32[]{:S(2)}) collective-permute-start(bf16[4,1,1,2,1,1,16,128]{7,6,0,5,4,3,2,1:T(8,128)(2,1)S(1)} %maximum_select_fusion.18), channel_id=1, source_target_pairs={{0,2},{1,3},{2,0},{3,1},{4,6},{5,7},{6,4},{7,5},{8,10},{9,11},{10,... | collective-permute-start | bytes 98312 | tf_op jit(solution)/shard_map/ppermute | solution.py:103
  82.9 4.9 %collective-permute-start.19 = (bf16[4,1,1,1,2,2,16,128]{7,6,0,5,4,3,2,1:T(8,128)(2,1)S(1)}, bf16[4,1,1,1,2,2,16,128]{7,6,0,5,4,3,2,1:T(8,128)(2,1)S(1)}, u32[]{:S(2)}, u32[]{:S(2)}) collective-permute-start(bf16[4,1,1,1,2,2,16,128]{7,6,0,5,4,3,2,1:T(8,128)(2,1)S(1)} %maximum_select_fusion.9), channel_id=1, source_target_pairs={{0,4},{4,0},{8,12},{12,8},{16,20},{20,16},{24,28},{28,24},{1,5},{5... | collective-permute-start | bytes 196616 | tf_op jit(solution)/shard_map/ppermute | solution.py:103
  84.1 5.0 %collective-permute-start.23 = (bf16[4,1,2,1,1,2,16,128]{7,6,0,5,4,3,2,1:T(8,128)(2,1)S(1)}, bf16[4,1,2,1,1,2,16,128]{7,6,0,5,4,3,2,1:T(8,128)(2,1)S(1)}, u32[]{:S(2)}, u32[]{:S(2)}) collective-permute-start(bf16[4,1,2,1,1,2,16,128]{7,6,0,5,4,3,2,1:T(8,128)(2,1)S(1)} %maximum_select_fusion.11), channel_id=1, source_target_pairs={{0,8},{4,12},{8,0},{12,4},{16,24},{20,28},{24,16},{28,20},{1,9},{5... | collective-permute-start | bytes 196616 | tf_op jit(solution)/shard_map/ppermute | solution.py:103
  86.1 5.7 %collective-permute-start.27 = (bf16[4,1,2,2,1,1,16,128]{7,6,0,5,4,3,2,1:T(8,128)(2,1)S(1)}, bf16[4,1,2,2,1,1,16,128]{7,6,0,5,4,3,2,1:T(8,128)(2,1)S(1)}, u32[]{:S(2)}, u32[]{:S(2)}) collective-permute-start(bf16[4,1,2,2,1,1,16,128]{7,6,0,5,4,3,2,1:T(8,128)(2,1)S(1)} %fusion.36), channel_id=1, source_target_pairs={{0,16},{4,20},{8,24},{12,28},{16,0},{20,4},{24,8},{28,12},{1,17},{... | collective-permute-start | bytes 196616 | tf_op jit(solution)/shard_map/ppermute | solution.py:103
  87.8 5.0 %collective-permute-start.20 = (bf16[4,1,1,2,2,2,16,128]{7,6,0,5,4,3,2,1:T(8,128)(2,1)S(1)}, bf16[4,1,1,2,2,2,16,128]{7,6,0,5,4,3,2,1:T(8,128)(2,1)S(1)}, u32[]{:S(2)}, u32[]{:S(2)}) collective-permute-start(bf16[4,1,1,2,2,2,16,128]{7,6,0,5,4,3,2,1:T(8,128)(2,1)S(1)} %maximum_select_fusion.5), channel_id=1, source_target_pairs={{0,2},{1,3},{2,0},{3,1},{4,6},{5,7},{6,4},{7,5},{8,10},{9,11},{10,... | collective-permute-start | bytes 393224 | tf_op jit(solution)/shard_map/ppermute | solution.py:103
  89.0 5.0 %collective-permute-start.24 = (bf16[4,1,2,1,2,2,16,128]{7,6,0,5,4,3,2,1:T(8,128)(2,1)S(1)}, bf16[4,1,2,1,2,2,16,128]{7,6,0,5,4,3,2,1:T(8,128)(2,1)S(1)}, u32[]{:S(2)}, u32[]{:S(2)}) collective-permute-start(bf16[4,1,2,1,2,2,16,128]{7,6,0,5,4,3,2,1:T(8,128)(2,1)S(1)} %maximum_select_fusion.6), channel_id=1, source_target_pairs={{0,4},{4,0},{8,12},{12,8},{16,20},{20,16},{24,28},{28,24},{1,5},{5... | collective-permute-start | bytes 393224 | tf_op jit(solution)/shard_map/ppermute | solution.py:103
  91.8 5.0 %collective-permute-start.28 = (bf16[4,1,2,2,1,2,16,128]{7,6,0,5,4,3,2,1:T(8,128)(2,1)S(1)}, bf16[4,1,2,2,1,2,16,128]{7,6,0,5,4,3,2,1:T(8,128)(2,1)S(1)}, u32[]{:S(2)}, u32[]{:S(2)}) collective-permute-start(bf16[4,1,2,2,1,2,16,128]{7,6,0,5,4,3,2,1:T(8,128)(2,1)S(1)} %maximum_select_fusion.7), channel_id=1, source_target_pairs={{0,8},{4,12},{8,0},{12,4},{16,24},{20,28},{24,16},{28,20},{1,9},{5... | collective-permute-start | bytes 393224 | tf_op jit(solution)/shard_map/ppermute | solution.py:103
  97.0 2.4 %collective-permute-start.29 = (bf16[12,256,128]{2,1,0:T(8,128)(2,1)S(1)}, bf16[12,256,128]{2,1,0:T(8,128)(2,1)S(1)}, u32[]{:S(2)}, u32[]{:S(2)}) collective-permute-start(bf16[12,256,128]{2,1,0:T(8,128)(2,1)S(1)} %pad_maximum_fusion.2), channel_id=1, source_target_pairs={{0,1},{1,0},{2,3},{3,2},{4,5},{5,4},{6,7},{7,6},{8,9},{9,8},{10,11... | collective-permute-start | bytes 2359304 | tf_op jit(solution)/shard_map/ppermute | solution.py:187
  (23 other events, 100.1 us)
